TPU v7x, 32 devices: a whole 2x2x4 slice. The times are simulated.
32 devices in a mesh: ep: 8 (over z, y), rep: 4 (over x, core).
Axes of the slice: x: 2, y: 2, z: 4, core: 2. Of those that a mesh axis runs over, the one named last changes fastest.
Arguments:
- residual: bfloat16 [4096, 2048], P(('rep', 'ep')), parts along dimension 0, may hold values from -6 to 6
- attn_out: bfloat16 [4096, 4096], P(('rep', 'ep')), parts along dimension 0, may hold values from -6 to 6
- out_weight: bfloat16 [4096, 2048], P('ep'), may hold values from -0.09375 to 0.09375
- post_gain: float32 [2048], replicated, may hold values from 0.1 to 1.9
- gate_up: bfloat16 [16, 2048, 1536], P('ep'), may hold values from -0.125 to 0.125
- down: bfloat16 [16, 768, 2048], P('ep'), may hold values from -0.21875 to 0.21875
- route_ids: int32 [4096, 8], P(('rep', 'ep')), parts along dimension 0, may hold values from 0 to 15, all different within a row; in each aligned block of 64 rows (0 to 63, 64 to 127, ...) at most 48 rows name the same one
- route_weight: float32 [4096, 8], P(('rep', 'ep')), parts along dimension 0, may hold values from 0.05 to 1
- final_gain: float32 [2048], replicated, may hold values from 0.1 to 1.9
Outputs:
- stream: bfloat16 [4096, 2048], P(('rep', 'ep')), parts along dimension 0
- next_input: bfloat16 [4096, 2048], P(('rep', 'ep')), parts along dimension 0
There are 4 independent parts, one for each index of `rep`. A program takes and returns all parts, laid end to end along the dimension named above; an argument that names none is the same for every part. Nothing has to cross between parts.
Inputs may be any that keep to these rules, and one draw needn't show every extreme that they name: `route_ids`: each row names 8 different experts. In each aligned block of 64 rows of one device no expert is named by more than 48 rows, a bound that some block reaches.
All inputs are finite; a program needn't handle non-finite values.
Results may differ from a plain program's by a relative error of at most 0.014.
Values may be sent and summed in bfloat16 or wider, within the bound.
No kernel may reach another device: no remote copies, remote signals or barrier semaphores. Data moves between devices by JAX's collectives and lax.ppermute only.
A program may use at most 128 MiB of HBM per device.

v0:
```python
import jax
import jax.numpy as jnp
from jax import lax
from jax.sharding import PartitionSpec as P


def rms_scale(values, scale_gain):
    mean_square = jnp.mean(values * values, axis=-1, keepdims=True)
    return values * lax.rsqrt(mean_square + 1e-06) * scale_gain


def body(
    residual, attn_out, out_weight, post_gain, gate_up, down, route_ids, route_weight, final_gain
):
    row_count, model_width = residual.shape
    ep_size = lax.axis_size("ep")
    local_experts = gate_up.shape[0]
    hidden_width = down.shape[1]
    experts = local_experts * ep_size
    top_count = route_ids.shape[1]
    half_rows = row_count // 2
    capacity = 3 * half_rows * top_count // (2 * experts)
    projected = jnp.dot(
        attn_out,
        lax.all_gather(out_weight, "ep", axis=0, tiled=True),
        preferred_element_type=jnp.float32,
    )
    middle = (residual.astype(jnp.float32) + projected).astype(jnp.bfloat16)
    normed = rms_scale(middle.astype(jnp.float32), post_gain).astype(jnp.bfloat16)
    targets = route_ids.reshape(2, half_rows * top_count)
    onehot = (targets[:, :, None] == jnp.arange(experts, dtype=jnp.int32)).astype(jnp.int32)
    slot_rank = jnp.sum(jnp.cumsum(onehot, axis=1) * onehot, axis=2) - 1
    source = jnp.repeat(normed, top_count, axis=0).reshape(2, half_rows * top_count, model_width)
    position = jnp.arange(2, dtype=jnp.int32)[:, None] * capacity + slot_rank
    flat_index = (targets * (2 * capacity) + position).reshape(-1)
    buffer = (
        jnp.zeros((experts * 2 * capacity, model_width), jnp.bfloat16)
        .at[flat_index]
        .set(source.reshape(-1, model_width))
    )
    buffer = buffer.reshape(ep_size, local_experts, 2 * capacity, model_width)
    projected_up = jnp.einsum(
        "nesd,edf->nesf",
        lax.all_to_all(buffer, "ep", split_axis=0, concat_axis=0, tiled=True),
        gate_up,
        preferred_element_type=jnp.float32,
    )
    activated = (
        jax.nn.silu(projected_up[..., :hidden_width]) * projected_up[..., hidden_width:]
    ).astype(jnp.bfloat16)
    returned = lax.all_to_all(
        jnp.einsum("nesf,efd->nesd", activated, down, preferred_element_type=jnp.float32).astype(
            jnp.bfloat16
        ),
        "ep",
        split_axis=0,
        concat_axis=0,
        tiled=True,
    )
    picked = returned.reshape(experts * 2 * capacity, model_width)[flat_index]
    picked = picked.reshape(row_count, top_count, model_width)
    combined = jnp.sum(picked.astype(jnp.float32) * route_weight[:, :, None], axis=1)
    updated = middle.astype(jnp.float32) + combined
    return (updated.astype(jnp.bfloat16), rms_scale(updated, final_gain).astype(jnp.bfloat16))


def solution(mesh):
    in_specs = (
        P(("rep", "ep"), None),
        P(("rep", "ep"), None),
        P("ep", None),
        P(),
        P("ep", None, None),
        P("ep", None, None),
        P(("rep", "ep"), None),
        P(("rep", "ep"), None),
        P(),
    )
    out_specs = (P(("rep", "ep"), None), P(("rep", "ep"), None))
    return jax.shard_map(body, mesh=mesh, in_specs=in_specs, out_specs=out_specs, check_vma=False)
```

profile of v0, /device:TPU:0, one launch (start us, length us, event | category | flops | bytes accessed | tf_op | source)
XLA Modules:
  0.0 598.1 jit_solution(7272418808549959246)
XLA Ops:
  7.2 0.0 copy-start
  7.2 0.0 all-gather.2.cloned.1.call-start
  7.2 0.7 all-gather.2.cloned.1.call-update
  7.9 0.8 copy.20
  8.7 0.1 eq.29
  8.8 0.1 eq.25
  8.9 0.7 broadcast_multiply_fusion
  9.6 0.1 copy.19
  9.7 0.1 mul.83
  9.8 2.3 reduce-window.6
  12.1 0.3 slice_reduce_fusion
  12.4 0.1 fusion.23
  12.5 0.1 add_bitcast_fusion.1
  12.6 0.0 copy-start.2
  12.7 227.8 %all-gather.2.cloned.1.call-done = bf16[4096,2048]{1,0:T(8,128)(2,1)} async-done(((bf16[512,2048]{1,0:T(8,128)(2,1)}), bf16[4096,2048]{1,0:T(8,128)(2,1)}) %all-gather.2.cloned.1.call-update) | async-done | bytes 16777232 | tf_op jit(solution)/shard_map/all_gather | solution.py:25
  240.5 0.0 copy-done
  240.5 8.3 %multiply_reduce_fusion.1 = (f32[128]{0:T(128)S(1)}, f32[128,2048]{1,0:T(8,128)S(1)}) fusion(bf16[128,4096]{1,0:T(8,128)(2,1)S(1)} %copy-done, bf16[4096,2048]{1,0:T(8,128)(2,1)} %all-gather.2.cloned.1.call-done, bf16[128,2048]{1,0:T(8,128)(2,1)} %param.9), kind=kOutput, calls=%fused_computation.24 | convolution fusion | flops 2149056512 | bytes 19399168 | tf_op jit(solution)/shard_map/dot_general | solution.py:23
  248.8 0.0 copy-done.2
  248.8 0.2 multiply_convert_fusion.1
  249.0 10.2 %scatter_custom_fusion = bf16[1536,2048]{1,0:T(8,128)(2,1)} fusion(s32[1024]{0:T(1024)S(1)} %bitcast.51, bf16[]{:T(256)} %constant.10.clone.1, bf16[128,2048]{1,0:T(8,128)(2,1)S(1)} %multiply_convert_fusion.1), kind=kCustom, calls=%fused_computation.13 | custom fusion | bytes 6815746 | tf_op jit(solution)/shard_map/scatter | solution.py:39
  259.2 141.7 %all_to_all.10 = bf16[8,2,96,2048]{3,2,1,0:T(8,128)(2,1)S(1)} all-to-all(bf16[8,2,96,2048]{3,2,1,0:T(8,128)(2,1)} %bitcast.50), channel_id=1, replica_groups=mesh['ep'=8,'rep'=4] {'ep'}, dimensions={0} | all-to-all | bytes 12582912 | tf_op jit(solution)/shard_map/all_to_all | solution.py:44
  400.9 15.0 %fusion.6 = f32[8,2,96,1536]{3,2,0,1:T(8,128)} fusion(bf16[2,2048,1536]{2,1,0:T(8,128)(2,1)} %param.13, bf16[8,2,96,2048]{3,2,1,0:T(8,128)(2,1)S(1)} %all_to_all.10), kind=kOutput, calls=%fused_computation.10 | convolution fusion | flops 9663676416 | bytes 28311552 | tf_op jit(solution)/shard_map/nesd,edf->nesf/dot_general | solution.py:42
  415.9 9.6 %convert_bitcast_fusion = bf16[8,2,96,2048]{3,2,0,1:T(8,128)(2,1)S(1)} fusion(bf16[2,768,2048]{2,1,0:T(8,128)(2,1)} %param.14, f32[8,2,96,1536]{3,2,0,1:T(8,128)} %fusion.6), kind=kOutput, calls=%fused_computation.9 | convolution fusion | flops 4842061824 | bytes 22020096 | tf_op jit(solution)/shard_map/nesf,efd->nesd/dot_general | solution.py:52
  425.5 3.2 copy.24
  428.7 0.0 copy-start.4
  428.7 5.1 all-to-all-start.1
  433.8 0.0 copy-done.4
  433.8 0.1 copy.25
  433.9 136.9 %all-to-all-done.1 = bf16[8,2,96,2048]{3,2,1,0:T(8,128)(2,1)} async-done(((bf16[8,2,96,2048]{3,2,1,0:T(8,128)(2,1)}), bf16[8,2,96,2048]{3,2,1,0:T(8,128)(2,1)}, u32[]{:S(2)}, u32[]{:S(2)}) %all-to-all-start.1) | async-done | bytes 6291488 | tf_op jit(solution)/shard_map/all_to_all | solution.py:51
  570.8 0.0 copy-start.1
  570.8 12.5 %gather_fusion = bf16[1024,2048]{1,0:T(8,128)(2,1)} fusion(bf16[1536,2048]{1,0:T(8,128)(2,1)} %bitcast.10, s32[1024]{0:T(1024)S(1)} %broadcast_clamp_fusion), kind=kCustom, calls=%fused_computation | custom fusion | bytes 8392704 | tf_op jit(solution)/shard_map/gather | solution.py:60
  583.3 0.0 copy-start.3
  583.3 6.5 %fusion.2 = f32[128,2048]{1,0:T(8,128)S(1)} fusion(bf16[1024,2048]{1,0:T(8,128)(2,1)} %gather_fusion, f32[128,8]{1,0:T(8,128)S(1)} %copy.25), kind=kLoop, calls=%fused_computation.5 | loop fusion | flops 6029312 | bytes 5246976 | tf_op jit(solution)/shard_map/reduce_sum | solution.py:62
  589.8 0.3 multiply_reduce_fusion
  590.1 0.0 copy-done.3
  590.1 1.1 multiply_convert_fusion
  591.3 0.0 copy-done.1
  (9 shorter events, 0.1 us)
Async XLA Ops:
  7.2 233.3 %copy-start = (bf16[128,4096]{1,0:T(8,128)(2,1)S(1)}, bf16[128,4096]{1,0:T(8,128)(2,1)}, u32[]{:S(2)}) copy-start(bf16[128,4096]{1,0:T(8,128)(2,1)} %param.10) | copy-start | bytes 3145732
  7.2 233.3 %all-gather.2.cloned.1.call-start = ((), (), s32[]{:S(2)}) async-start(), calls=%async_computation.2 | async-start | bytes 18874368 | tf_op jit(solution)/shard_map/all_gather | solution.py:25
  12.6 236.2 %copy-start.2 = (f32[2048]{0:T(1024)S(1)}, f32[2048]{0:T(1024)}, u32[]{:S(2)}) copy-start(f32[2048]{0:T(1024)} %param.12) | copy-start | bytes 24580
  428.7 5.1 copy-start.4
  428.7 142.1 %all-to-all-start.1 = ((bf16[8,2,96,2048]{3,2,1,0:T(8,128)(2,1)}), bf16[8,2,96,2048]{3,2,1,0:T(8,128)(2,1)}, u32[]{:S(2)}, u32[]{:S(2)}) async-start(bf16[8,2,96,2048]{3,2,1,0:T(8,128)(2,1)} %copy.24), calls=%async_computation.1 | async-start | bytes 12582912 | tf_op jit(solution)/shard_map/all_to_all | solution.py:51
  570.8 20.4 %copy-start.1 = (bf16[128,4096]{1,0:T(8,128)(2,1)S(1)}, bf16[128,4096]{1,0:T(8,128)(2,1)}, u32[]{:S(2)}) copy-start(bf16[128,4096]{1,0:T(8,128)(2,1)} %param.10) | copy-start | bytes 3145732
  583.3 6.8 %copy-start.3 = (f32[2048]{0:T(1024)S(1)}, f32[2048]{0:T(1024)}, u32[]{:S(2)}) copy-start(f32[2048]{0:T(1024)} %param.17) | copy-start | bytes 24580
Sparse Core Ops, SparseCore 0:
  10.1 230.3 all-gather.1
where the time goes:
time: 598 us
  waiting for transfers between devices  365 us (61%)
  blocking collectives  142 us (24%)
  matrix products  32.9 us (6%)
  local copies, waits for them, and re-layouts  27.6 us (5%)
  between operations  14.1 us (2%)
  other arithmetic  11.3 us (2%)
    all_gather x1, waiting for transfers between devices, body(): lax.all_gather(out_weight, 'ep', axis=0, tiled=True)  228 us
    all_to_all x1, blocking collectives, body(): lax.all_to_all(buffer, 'ep', split_axis=0, concat_axis=0, tiled=True)  142 us
    all_to_all x1, waiting for transfers between devices, body(): lax.all_to_all(jnp.einsum('nesf,efd->nesd', activated, down, preferred_el...  137 us
    dot_general x1, matrix products, body(): jnp.einsum('nesd,edf->nesf', lax.all_to_all(buffer, 'ep', split_axis=0, c...  15 us
    gather x1, local copies, waits for them, and re-layouts, body(): picked = returned.reshape(experts * 2 * capacity, model_width)[flat_index]  12.5 us
  transfers between devices with their start and end apart: 2, of which 2 were waited for; matrix products, arithmetic and copies ran while one was open for 1% of the time, Pallas kernels for 0%

commit v1 on v0

v1 whole, which is shorter than its diff:
```python
import jax
import jax.numpy as jnp
from jax import lax
from jax.sharding import PartitionSpec as P


def rms_scale(values, scale_gain):
    mean_square = jnp.mean(values * values, axis=-1, keepdims=True)
    return values * lax.rsqrt(mean_square + 1e-06) * scale_gain


def body(
    residual, attn_out, out_weight, post_gain, gate_up, down, route_ids, route_weight, final_gain
):
    row_count, model_width = residual.shape
    ep_size = lax.axis_size("ep")
    me = lax.axis_index("ep")
    local_experts = gate_up.shape[0]
    hidden_width = down.shape[1]
    slice_width = out_weight.shape[0]
    group_rows = row_count * ep_size

    with jax.named_scope("out_projection"):
        columns = attn_out.reshape(row_count, ep_size, slice_width).transpose(1, 0, 2)
        columns = lax.all_to_all(columns, "ep", split_axis=0, concat_axis=0, tiled=True)
        partial = jnp.dot(
            columns.reshape(group_rows, slice_width), out_weight, preferred_element_type=jnp.float32
        )
        owner = (lax.broadcasted_iota(jnp.int32, (group_rows, 1), 0) // row_count) == me
        padded_residual = jnp.tile(residual.astype(jnp.float32), (ep_size, 1))
        partial = partial + jnp.where(owner, padded_residual, 0.0)
        middle_all = lax.psum(partial.astype(jnp.bfloat16), "ep")

    normed_all = rms_scale(middle_all.astype(jnp.float32), post_gain).astype(jnp.bfloat16)
    ids_all = lax.all_gather(route_ids, "ep", axis=0, tiled=True)
    weights_all = lax.all_gather(route_weight, "ep", axis=0, tiled=True)

    with jax.named_scope("local_experts"):
        combined_part = jnp.zeros((group_rows, model_width), jnp.float32)
        for e in range(local_experts):
            expert_id = me * local_experts + e
            row_weight = jnp.sum(jnp.where(ids_all == expert_id, weights_all, 0.0), axis=1)
            projected_up = jnp.dot(normed_all, gate_up[e], preferred_element_type=jnp.float32)
            activated = (
                jax.nn.silu(projected_up[:, :hidden_width]) * projected_up[:, hidden_width:]
            ).astype(jnp.bfloat16)
            expert_out = jnp.dot(activated, down[e], preferred_element_type=jnp.float32).astype(
                jnp.bfloat16
            )
            combined_part = combined_part + row_weight[:, None] * expert_out.astype(jnp.float32)

    with jax.named_scope("combine_return"):
        combined = lax.psum_scatter(
            combined_part.astype(jnp.bfloat16), "ep", scatter_dimension=0, tiled=True
        )
    middle = lax.dynamic_slice_in_dim(middle_all, me * row_count, row_count, axis=0)
    updated = middle.astype(jnp.float32) + combined.astype(jnp.float32)
    return (updated.astype(jnp.bfloat16), rms_scale(updated, final_gain).astype(jnp.bfloat16))


def solution(mesh):
    in_specs = (
        P(("rep", "ep"), None),
        P(("rep", "ep"), None),
        P("ep", None),
        P(),
        P("ep", None, None),
        P("ep", None, None),
        P(("rep", "ep"), None),
        P(("rep", "ep"), None),
        P(),
    )
    out_specs = (P(("rep", "ep"), None), P(("rep", "ep"), None))
    return jax.shard_map(body, mesh=mesh, in_specs=in_specs, out_specs=out_specs, check_vma=False)
```

time: 598 us -> 346 us (0.58)
  waiting for transfers between devices: 365 us -> 204 us
  blocking collectives: 142 us -> 63.1 us
  local copies, waits for them, and re-layouts: 27.6 us -> 5.54 us
  matrix products: 32.9 us -> 43.2 us
    all_gather x1 -> x0, waiting for transfers between devices: 228 us -> none  [body(): lax.all_gather(out_weight, 'ep', axis=0, tiled=True)]
    all_to_all x1 -> x0, blocking collectives: 142 us -> none  [body(): lax.all_to_all(buffer, 'ep', split_axis=0, concat_axis=0, tiled=True)]
    all_to_all x1, waiting for transfers between devices: 137 us -> 24.7 us  [body(): lax.all_to_all(columns, 'ep', split_axis=0, concat_axis=0, tiled=True)]
    psum x0 -> x1, waiting for transfers between devices: none -> 92.1 us  [body(): middle_all = lax.psum(partial.astype(jnp.bfloat16), 'ep')]
    reduce_scatter x0 -> x1, waiting for transfers between devices: none -> 87.1 us  [body(): lax.psum_scatter(combined_part.astype(jnp.bfloat16), 'ep', scatter_dimens...]
    all_gather x0 -> x2, blocking collectives: none -> 63.1 us  [the longest x1 31.8 us: body(): ids_all = lax.all_gather(route_ids, 'ep', axis=0, tiled=True)]
    gather x1 -> x0, local copies, waits for them, and re-layouts: 12.5 us -> none  [body(): picked = returned.reshape(experts * 2 * capacity, model_width)[flat_index]]
    dot_general x3 -> x5, matrix products: 32.9 us -> 43.2 us  [the longest x2 19.6 us: body(): jnp.dot(normed_all, gate_up[e], preferred_element_type=jnp.float32)]
  transfers between devices with their start and end apart: 2 -> 3, of which waited for: 2 -> 3; matrix products, arithmetic and copies ran while one was open for 1% -> 0% of each run, Pallas kernels for 0% -> 0%
where the time goes in v1:
time: 346 us; the launch traced here: 345 us
  waiting for transfers between devices  204 us (59%)
  blocking collectives  63.1 us (18%)
  matrix products  43.2 us (12%)
  between operations  14.1 us (4%)
  other arithmetic  8.29 us (2%)
  starting transfers between devices  7.36 us (2%)
  local copies, waits for them, and re-layouts  5.54 us (2%)
    psum x1, waiting for transfers between devices, body(): middle_all = lax.psum(partial.astype(jnp.bfloat16), 'ep')  92.1 us
    reduce_scatter x1, waiting for transfers between devices, body(): lax.psum_scatter(combined_part.astype(jnp.bfloat16), 'ep', scatter_dimens...  87.1 us
    all_gather x1, blocking collectives, body(): ids_all = lax.all_gather(route_ids, 'ep', axis=0, tiled=True)  31.8 us
    all_gather x1, blocking collectives, body(): weights_all = lax.all_gather(route_weight, 'ep', axis=0, tiled=True)  31.3 us
    all_to_all x1, waiting for transfers between devices, body(): lax.all_to_all(columns, 'ep', split_axis=0, concat_axis=0, tiled=True)  24.7 us
    dot_general x2, matrix products, body(): jnp.dot(normed_all, gate_up[e], preferred_element_type=jnp.float32)  19.6 us
    dot_general x2, matrix products, body(): jnp.dot(activated, down[e], preferred_element_type=jnp.float32)  18 us
    all_to_all x1, starting transfers between devices, body(): lax.all_to_all(columns, 'ep', split_axis=0, concat_axis=0, tiled=True)  7.28 us
  transfers between devices with their start and end apart: 3, of which 3 were waited for; matrix products, arithmetic and copies ran while one was open for 0% of the time, Pallas kernels for 0%

profile of v1, /device:TPU:0, one launch (start us, length us, event | category | flops | bytes accessed | tf_op | source)
XLA Modules:
  0.0 345.4 jit_solution(18292304097757044108)
XLA Ops:
  7.2 0.0 copy-start
  7.2 2.4 copy.11
  9.6 7.3 %all-to-all-start = ((bf16[8,128,512]{1,2,0:T(8,128)(2,1)}), bf16[8,128,512]{1,2,0:T(8,128)(2,1)}, u32[]{:S(2)}, u32[]{:S(2)}) async-start(bf16[8,128,512]{1,2,0:T(8,128)(2,1)} %bitcast.1), calls=%async_computation | async-start | bytes 2097152 | tf_op jit(solution)/shard_map/out_projection/all_to_all | solution.py:25
  16.9 0.0 all-reduce.2.cloned.1.call-start
  16.9 1.1 convert_element_type.45
  18.1 24.7 %all-to-all-done = bf16[8,128,512]{1,2,0:T(8,128)(2,1)} async-done(((bf16[8,128,512]{1,2,0:T(8,128)(2,1)}), bf16[8,128,512]{1,2,0:T(8,128)(2,1)}, u32[]{:S(2)}, u32[]{:S(2)}) %all-to-all-start) | async-done | bytes 1048608 | tf_op jit(solution)/shard_map/out_projection/all_to_all | solution.py:25
  42.8 2.3 copy.12
  45.0 0.0 copy-done
  45.0 5.5 %fusion.4 = bf16[1024,2048]{1,0:T(8,128)(2,1)} fusion(f32[128,2048]{1,0:T(8,128)S(1)} %convert_element_type.45, pred[1024]{0:T(1024)(128)(4,1)S(1)} %fusion.25, bf16[1024,512]{1,0:T(8,128)(2,1)} %bitcast.24, bf16[512,2048]{1,0:T(8,128)(2,1)S(1)} %copy-done), kind=kOutput, calls=%fused_computation.7 | convolution fusion | flops 2153775104 | bytes 8389632 | tf_op jit(solution)/shard_map/out_projection/dot_general | solution.py:26
  50.5 0.0 copy-start.3
  50.6 0.0 copy-start.4
  50.6 0.0 copy-start.5
  50.6 0.0 all-reduce.2.cloned.1.call-update
  50.6 0.0 reduce-scatter.2.cloned.1.call-start
  50.6 0.6 copy-done.3
  51.2 31.3 %all_gather.7 = f32[1024,8]{0,1:T(8,128)S(1)} all-gather(f32[128,8]{0,1:T(8,128)S(1)} %copy-done.3), channel_id=1, replica_groups=mesh['ep'=8,'rep'=4] {'ep'}, dimensions={0}, use_global_device_ids=true | all-gather | bytes 36864 | tf_op jit(solution)/shard_map/all_gather | solution.py:36
  82.5 0.0 copy-done.4
  82.5 31.8 %all_gather.6 = s32[1024,8]{0,1:T(8,128)S(1)} all-gather(s32[128,8]{0,1:T(8,128)S(1)} %copy-done.4), channel_id=1, replica_groups=mesh['ep'=8,'rep'=4] {'ep'}, dimensions={0}, use_global_device_ids=true | all-gather | bytes 36864 | tf_op jit(solution)/shard_map/all_gather | solution.py:35
  114.3 92.1 %all-reduce.2.cloned.1.call-done = bf16[1024,2048]{1,0:T(8,128)(2,1)} async-done(((bf16[1024,2048]{1,0:T(8,128)(2,1)}), bf16[1024,2048]{1,0:T(8,128)(2,1)}) %all-reduce.2.cloned.1.call-update) | async-done | bytes 4194320 | tf_op jit(solution)/shard_map/out_projection/psum | solution.py:32
  206.4 0.0 copy-start.1
  206.4 0.0 slice-start.3
  206.4 3.2 fusion
  209.6 0.0 copy-done.5
  209.6 0.2 copy-done.1
  209.8 0.0 slice-start.4
  209.8 0.0 slice-start
  209.8 0.0 slice-start.1
  209.8 10.9 %fusion.7 = f32[1024,1536]{1,0:T(8,128)} fusion(bf16[2,2048,1536]{2,1,0:T(8,128)(2,1)} %param.13, bf16[1024,2048]{1,0:T(8,128)(2,1)S(1)} %copy-done.1, f32[2048]{0:T(1024)S(1)} %copy-done.5, f32[1024]{0:T(1024)S(1)} %add_rsqrt_fusion), kind=kOutput, calls=%fused_computation.11 | convolution fusion | flops 6450839552 | bytes 16789504 | tf_op jit(solution)/shard_map/local_experts/dot_general | solution.py:43
  220.8 0.0 slice-done.3
  220.8 0.0 slice-done.4
  220.8 0.0 slice-start.2
  220.8 8.2 %fusion.14 = bf16[1024,2048]{1,0:T(8,128)(2,1)} fusion(bf16[2,768,2048]{2,1,0:T(8,128)(2,1)S(1)} %bitcast.28, f32[1024,1536]{1,0:T(8,128)} %fusion.7), kind=kOutput, calls=%fused_computation.20 | convolution fusion | flops 3225944064 | bytes 13631488 | tf_op jit(solution)/shard_map/local_experts/dot_general | solution.py:47
  229.0 0.0 slice-done
  229.0 0.0 slice-done.1
  229.0 0.0 slice-done.2
  229.0 8.7 %fusion.5 = f32[1024,1536]{1,0:T(8,128)} fusion(bf16[2,2048,1536]{2,1,0:T(8,128)(2,1)S(1)} %bitcast.26, bf16[1024,2048]{1,0:T(8,128)(2,1)S(1)} %copy-done.1, f32[2048]{0:T(1024)S(1)} %copy-done.5, f32[1024]{0:T(1024)S(1)} %add_rsqrt_fusion), kind=kOutput, calls=%fused_computation.9 | convolution fusion | flops 6450839552 | bytes 16789504 | tf_op jit(solution)/shard_map/local_experts/dot_general | solution.py:43
  237.7 9.9 %add_convert_fusion = bf16[1024,2048]{1,0:T(8,128)(2,1)} fusion(f32[1024]{0:T(1024)S(1)} %get-tuple-element.3, bf16[1024,2048]{1,0:T(8,128)(2,1)} %fusion.14, f32[1024]{0:T(1024)S(1)} %get-tuple-element.2, bf16[2,768,2048]{2,1,0:T(8,128)(2,1)S(1)} %bitcast.28, f32[1024,1536]{1,0:T(8,128)} %fusion.5), kind=kOutput, calls=%fused_computation.8 | convolution fusion | flops 3240624128 | bytes 17833984 | tf_op jit(solution)/shard_map/local_experts/dot_general | solution.py:47
  247.6 0.0 copy-start.2
  247.6 0.0 reduce-scatter.2.cloned.1.call-update
  247.6 87.1 %reduce-scatter.2.cloned.1.call-done = bf16[128,2048]{1,0:T(8,128)(2,1)} async-done(((bf16[1024,2048]{1,0:T(8,128)(2,1)}), bf16[128,2048]{1,0:T(8,128)(2,1)}) %reduce-scatter.2.cloned.1.call-update) | async-done | bytes 524304 | tf_op jit(solution)/shard_map/combine_return/reduce_scatter | solution.py:53
  334.7 1.5 multiply_reduce_fusion
  336.1 0.0 copy-done.2
  336.1 2.4 multiply_convert_fusion
  (6 shorter events, 0.0 us)
Async XLA Ops:
  7.2 37.9 %copy-start = (bf16[512,2048]{1,0:T(8,128)(2,1)S(1)}, bf16[512,2048]{1,0:T(8,128)(2,1)}, u32[]{:S(2)}) copy-start(bf16[512,2048]{1,0:T(8,128)(2,1)} %param.11) | copy-start | bytes 6291460
  9.6 33.2 %all-to-all-start = ((bf16[8,128,512]{1,2,0:T(8,128)(2,1)}), bf16[8,128,512]{1,2,0:T(8,128)(2,1)}, u32[]{:S(2)}, u32[]{:S(2)}) async-start(bf16[8,128,512]{1,2,0:T(8,128)(2,1)} %bitcast.1), calls=%async_computation | async-start | bytes 2097152 | tf_op jit(solution)/shard_map/out_projection/all_to_all | solution.py:25
  16.9 189.5 %all-reduce.2.cloned.1.call-start = ((), (), s32[]{:S(2)}) async-start(), calls=%async_computation.2 | async-start | bytes 8388608 | tf_op jit(solution)/shard_map/out_projection/psum | solution.py:32
  50.5 0.7 copy-start.3
  50.6 32.0 %copy-start.4 = (s32[128,8]{0,1:T(8,128)S(1)}, s32[128,8]{0,1:T(8,128)}, u32[]{:S(2)}) copy-start(s32[128,8]{0,1:T(8,128)} %param.15) | copy-start | bytes 12292
  50.6 159.1 %copy-start.5 = (f32[2048]{0:T(1024)S(1)}, f32[2048]{0:T(1024)}, u32[]{:S(2)}) copy-start(f32[2048]{0:T(1024)} %param.12) | copy-start | bytes 24580
  50.6 284.1 %reduce-scatter.2.cloned.1.call-start = ((), (), s32[]{:S(2)}) async-start(), calls=%async_computation.3 | async-start | bytes 4718592 | tf_op jit(solution)/shard_map/combine_return/reduce_scatter | solution.py:53
  206.4 3.4 copy-start.1
  206.4 14.4 %slice-start.3 = ((s8[6291456]{0:T(1024)(128)(4,1)}), s8[4194304]{0:T(1024)(128)(4,1)S(1)}, s32[]{:S(2)}) async-start(s8[6291456]{0:T(1024)(128)(4,1)} %bitcast.27), calls=%async_computation.7 | async-start | bytes 8388608
  209.8 10.9 %slice-start.4 = ((s8[6291456]{0:T(1024)(128)(4,1)}), s8[2097152]{0:T(1024)(128)(4,1)S(1)}, s32[]{:S(2)}) async-start(s8[6291456]{0:T(1024)(128)(4,1)} %bitcast.27), calls=%async_computation.8 | async-start | bytes 4194304
  209.8 19.1 %slice-start = ((s8[12582912]{0:T(1024)(128)(4,1)}), s8[4194304]{0:T(1024)(128)(4,1)S(1)}, s32[]{:S(2)}) async-start(s8[12582912]{0:T(1024)(128)(4,1)} %bitcast.25), calls=%async_computation.4 | async-start | bytes 8388608
  209.8 19.1 %slice-start.1 = ((s8[12582912]{0:T(1024)(128)(4,1)}), s8[4194304]{0:T(1024)(128)(4,1)S(1)}, s32[]{:S(2)}) async-start(s8[12582912]{0:T(1024)(128)(4,1)} %bitcast.25), calls=%async_computation.5 | async-start | bytes 8388608
  220.8 8.2 %slice-start.2 = ((s8[12582912]{0:T(1024)(128)(4,1)}), s8[4194304]{0:T(1024)(128)(4,1)S(1)}, s32[]{:S(2)}) async-start(s8[12582912]{0:T(1024)(128)(4,1)} %bitcast.25), calls=%async_computation.6 | async-start | bytes 8388608
  247.6 88.6 %copy-start.2 = (f32[2048]{0:T(1024)S(1)}, f32[2048]{0:T(1024)}, u32[]{:S(2)}) copy-start(f32[2048]{0:T(1024)} %param.17) | copy-start | bytes 24580
Sparse Core Ops, SparseCore 0:
  50.7 155.6 all-reduce.1
  247.7 86.9 reduce-scatter.1

commit v2 on v1

--- a/solution.py
+++ b/solution.py
@@ -20,6 +20,15 @@
     slice_width = out_weight.shape[0]
     group_rows = row_count * ep_size
 
+    with jax.named_scope("route_weights"):
+        expert_ids = jnp.arange(local_experts * ep_size, dtype=jnp.int32)
+        dense_weight = jnp.sum(
+            jnp.where(route_ids[:, :, None] == expert_ids, route_weight[:, :, None], 0.0), axis=1
+        )
+        dense_weight = dense_weight.reshape(row_count, ep_size, local_experts).transpose(1, 0, 2)
+        row_weights = lax.all_to_all(dense_weight, "ep", split_axis=0, concat_axis=0, tiled=True)
+        row_weights = row_weights.reshape(group_rows, local_experts)
+
     with jax.named_scope("out_projection"):
         columns = attn_out.reshape(row_count, ep_size, slice_width).transpose(1, 0, 2)
         columns = lax.all_to_all(columns, "ep", split_axis=0, concat_axis=0, tiled=True)
@@ -32,14 +41,10 @@
         middle_all = lax.psum(partial.astype(jnp.bfloat16), "ep")
 
     normed_all = rms_scale(middle_all.astype(jnp.float32), post_gain).astype(jnp.bfloat16)
-    ids_all = lax.all_gather(route_ids, "ep", axis=0, tiled=True)
-    weights_all = lax.all_gather(route_weight, "ep", axis=0, tiled=True)
-
     with jax.named_scope("local_experts"):
         combined_part = jnp.zeros((group_rows, model_width), jnp.float32)
         for e in range(local_experts):
-            expert_id = me * local_experts + e
-            row_weight = jnp.sum(jnp.where(ids_all == expert_id, weights_all, 0.0), axis=1)
+            row_weight = row_weights[:, e]
             projected_up = jnp.dot(normed_all, gate_up[e], preferred_element_type=jnp.float32)
             activated = (
                 jax.nn.silu(projected_up[:, :hidden_width]) * projected_up[:, hidden_width:]

time: 346 us -> 346 us (level)
  blocking collectives: 63.1 us -> 10.6 us
  waiting for transfers between devices: 204 us -> 256 us
    all_gather x2 -> x0, blocking collectives: 63.1 us -> none  [the longest x1 31.8 us: body(): ids_all = lax.all_gather(route_ids, 'ep', axis=0, tiled=True)]
    psum x1, waiting for transfers between devices: 92.1 us -> 144 us  [body(): middle_all = lax.psum(partial.astype(jnp.bfloat16), 'ep')]
    all_to_all x0 -> x1, blocking collectives: none -> 10.6 us  [body(): lax.all_to_all(dense_weight, 'ep', split_axis=0, concat_axis=0, tiled=True)]
where the time goes in v2:
time: 346 us; the launch traced here: 345 us
  waiting for transfers between devices  256 us (74%)
  matrix products  43.2 us (12%)
  between operations  14.1 us (4%)
  blocking collectives  10.6 us (3%)
  other arithmetic  8.28 us (2%)
  starting transfers between devices  7.36 us (2%)
  local copies, waits for them, and re-layouts  5.55 us (2%)
    psum x1, waiting for transfers between devices, body(): middle_all = lax.psum(partial.astype(jnp.bfloat16), 'ep')  144 us
    reduce_scatter x1, waiting for transfers between devices, body(): lax.psum_scatter(combined_part.astype(jnp.bfloat16), 'ep', scatter_dimens...  87.1 us
    all_to_all x1, waiting for transfers between devices, body(): lax.all_to_all(columns, 'ep', split_axis=0, concat_axis=0, tiled=True)  24.7 us
    dot_general x2, matrix products, body(): jnp.dot(normed_all, gate_up[e], preferred_element_type=jnp.float32)  19.7 us
    dot_general x2, matrix products, body(): jnp.dot(activated, down[e], preferred_element_type=jnp.float32)  18 us
    all_to_all x1, blocking collectives, body(): lax.all_to_all(dense_weight, 'ep', split_axis=0, concat_axis=0, tiled=True)  10.6 us
    all_to_all x1, starting transfers between devices, body(): lax.all_to_all(columns, 'ep', split_axis=0, concat_axis=0, tiled=True)  7.28 us
  transfers between devices with their start and end apart: 3, of which 3 were waited for; matrix products, arithmetic and copies ran while one was open for 0% of the time, Pallas kernels for 0%

profile of v2, /device:TPU:0, one launch (start us, length us, event | category | flops | bytes accessed | tf_op | source)
XLA Modules:
  0.0 345.1 jit_solution(9347439068771346674)
XLA Ops:
  7.2 0.0 copy-start
  7.2 2.4 copy.19
  9.6 7.3 %all-to-all-start = ((bf16[8,128,512]{1,2,0:T(8,128)(2,1)}), bf16[8,128,512]{1,2,0:T(8,128)(2,1)}, u32[]{:S(2)}, u32[]{:S(2)}) async-start(bf16[8,128,512]{1,2,0:T(8,128)(2,1)} %bitcast.1), calls=%async_computation | async-start | bytes 2097152 | tf_op jit(solution)/shard_map/out_projection/all_to_all | solution.py:34
  16.9 0.0 all-reduce.2.cloned.1.call-start
  16.9 1.1 convert_element_type.45
  18.1 24.7 %all-to-all-done = bf16[8,128,512]{1,2,0:T(8,128)(2,1)} async-done(((bf16[8,128,512]{1,2,0:T(8,128)(2,1)}), bf16[8,128,512]{1,2,0:T(8,128)(2,1)}, u32[]{:S(2)}, u32[]{:S(2)}) %all-to-all-start) | async-done | bytes 1048608 | tf_op jit(solution)/shard_map/out_projection/all_to_all | solution.py:34
  42.7 2.3 copy.20
  45.0 0.0 copy-done
  45.0 5.5 %fusion.4 = bf16[1024,2048]{1,0:T(8,128)(2,1)} fusion(f32[128,2048]{1,0:T(8,128)S(1)} %convert_element_type.45, pred[1024]{0:T(1024)(128)(4,1)S(1)} %fusion.25, bf16[1024,512]{1,0:T(8,128)(2,1)} %bitcast.30, bf16[512,2048]{1,0:T(8,128)(2,1)S(1)} %copy-done), kind=kOutput, calls=%fused_computation.7 | convolution fusion | flops 2153775104 | bytes 8389632 | tf_op jit(solution)/shard_map/out_projection/dot_general | solution.py:35
  50.6 0.0 copy-start.3
  50.6 0.0 copy-start.4
  50.6 0.0 copy-start.5
  50.6 0.0 all-reduce.2.cloned.1.call-update
  50.6 0.0 reduce-scatter.2.cloned.1.call-start
  50.6 0.6 copy-done.3
  51.2 0.0 copy-done.4
  51.3 10.6 %all_to_all.10 = f32[8,128,2]{1,2,0:T(2,128)S(1)} all-to-all(f32[8,128,2]{1,2,0:T(2,128)S(1)} %bitcast.32), channel_id=1, replica_groups=mesh['ep'=8,'rep'=4] {'ep'}, dimensions={0} | all-to-all | bytes 16384 | tf_op jit(solution)/shard_map/route_weights/all_to_all | solution.py:29
  61.8 144.3 %all-reduce.2.cloned.1.call-done = bf16[1024,2048]{1,0:T(8,128)(2,1)} async-done(((bf16[1024,2048]{1,0:T(8,128)(2,1)}), bf16[1024,2048]{1,0:T(8,128)(2,1)}) %all-reduce.2.cloned.1.call-update) | async-done | bytes 4194320 | tf_op jit(solution)/shard_map/out_projection/psum | solution.py:41
  206.2 0.0 copy-start.1
  206.2 0.0 slice-start.3
  206.2 3.2 fusion
  209.4 0.0 copy-done.5
  209.4 0.2 copy-done.1
  209.6 0.0 slice-start.4
  209.6 0.0 slice-start
  209.6 0.0 slice-start.1
  209.6 10.9 %fusion.7 = f32[1024,1536]{1,0:T(8,128)} fusion(bf16[2,2048,1536]{2,1,0:T(8,128)(2,1)} %param.13, bf16[1024,2048]{1,0:T(8,128)(2,1)S(1)} %copy-done.1, f32[2048]{0:T(1024)S(1)} %copy-done.5, f32[1024]{0:T(1024)S(1)} %add_rsqrt_fusion), kind=kOutput, calls=%fused_computation.11 | convolution fusion | flops 6450839552 | bytes 16789504 | tf_op jit(solution)/shard_map/local_experts/dot_general | solution.py:48
  220.6 0.0 slice-done.3
  220.6 0.0 slice-done.4
  220.6 0.0 slice-start.2
  220.6 8.1 %fusion.14 = bf16[1024,2048]{1,0:T(8,128)(2,1)} fusion(bf16[2,768,2048]{2,1,0:T(8,128)(2,1)S(1)} %bitcast.38, f32[1024,1536]{1,0:T(8,128)} %fusion.7), kind=kOutput, calls=%fused_computation.20 | convolution fusion | flops 3225944064 | bytes 13631488 | tf_op jit(solution)/shard_map/local_experts/dot_general | solution.py:52
  228.7 0.0 slice-done
  228.7 0.0 slice-done.1
  228.7 0.0 slice-done.2
  228.7 8.7 %fusion.5 = f32[1024,1536]{1,0:T(8,128)} fusion(bf16[2,2048,1536]{2,1,0:T(8,128)(2,1)S(1)} %bitcast.36, bf16[1024,2048]{1,0:T(8,128)(2,1)S(1)} %copy-done.1, f32[2048]{0:T(1024)S(1)} %copy-done.5, f32[1024]{0:T(1024)S(1)} %add_rsqrt_fusion), kind=kOutput, calls=%fused_computation.9 | convolution fusion | flops 6450839552 | bytes 16789504 | tf_op jit(solution)/shard_map/local_experts/dot_general | solution.py:48
  237.5 9.8 %add_convert_fusion = bf16[1024,2048]{1,0:T(8,128)(2,1)} fusion(f32[1024]{0:T(1024)S(1)} %bitcast.34, bf16[1024,2048]{1,0:T(8,128)(2,1)} %fusion.14, f32[1024]{0:T(1024)S(1)} %bitcast.33, bf16[2,768,2048]{2,1,0:T(8,128)(2,1)S(1)} %bitcast.38, f32[1024,1536]{1,0:T(8,128)} %fusion.5), kind=kOutput, calls=%fused_computation.8 | convolution fusion | flops 3240624128 | bytes 17833984 | tf_op jit(solution)/shard_map/local_experts/dot_general | solution.py:52
  247.3 0.0 copy-start.2
  247.3 0.0 reduce-scatter.2.cloned.1.call-update
  247.3 87.1 %reduce-scatter.2.cloned.1.call-done = bf16[128,2048]{1,0:T(8,128)(2,1)} async-done(((bf16[1024,2048]{1,0:T(8,128)(2,1)}), bf16[128,2048]{1,0:T(8,128)(2,1)}) %reduce-scatter.2.cloned.1.call-update) | async-done | bytes 524304 | tf_op jit(solution)/shard_map/combine_return/reduce_scatter | solution.py:58
  334.4 1.5 multiply_reduce_fusion
  335.9 0.0 copy-done.2
  335.9 2.4 multiply_convert_fusion
  (7 shorter events, 0.0 us)
Async XLA Ops:
  7.2 37.9 %copy-start = (bf16[512,2048]{1,0:T(8,128)(2,1)S(1)}, bf16[512,2048]{1,0:T(8,128)(2,1)}, u32[]{:S(2)}) copy-start(bf16[512,2048]{1,0:T(8,128)(2,1)} %param.11) | copy-start | bytes 6291460
  9.6 33.2 %all-to-all-start = ((bf16[8,128,512]{1,2,0:T(8,128)(2,1)}), bf16[8,128,512]{1,2,0:T(8,128)(2,1)}, u32[]{:S(2)}, u32[]{:S(2)}) async-start(bf16[8,128,512]{1,2,0:T(8,128)(2,1)} %bitcast.1), calls=%async_computation | async-start | bytes 2097152 | tf_op jit(solution)/shard_map/out_projection/all_to_all | solution.py:34
  16.9 189.3 %all-reduce.2.cloned.1.call-start = ((), (), s32[]{:S(2)}) async-start(), calls=%async_computation.3 | async-start | bytes 8388608 | tf_op jit(solution)/shard_map/out_projection/psum | solution.py:41
  50.6 0.7 copy-start.3
  50.6 0.7 copy-start.4
  50.6 158.9 %copy-start.5 = (f32[2048]{0:T(1024)S(1)}, f32[2048]{0:T(1024)}, u32[]{:S(2)}) copy-start(f32[2048]{0:T(1024)} %param.12) | copy-start | bytes 24580
  50.6 283.8 %reduce-scatter.2.cloned.1.call-start = ((), (), s32[]{:S(2)}) async-start(), calls=%async_computation.4 | async-start | bytes 4718592 | tf_op jit(solution)/shard_map/combine_return/reduce_scatter | solution.py:58
  206.2 3.4 copy-start.1
  206.2 14.4 %slice-start.3 = ((s8[6291456]{0:T(1024)(128)(4,1)}), s8[4194304]{0:T(1024)(128)(4,1)S(1)}, s32[]{:S(2)}) async-start(s8[6291456]{0:T(1024)(128)(4,1)} %bitcast.37), calls=%async_computation.8 | async-start | bytes 8388608
  209.6 10.9 %slice-start.4 = ((s8[6291456]{0:T(1024)(128)(4,1)}), s8[2097152]{0:T(1024)(128)(4,1)S(1)}, s32[]{:S(2)}) async-start(s8[6291456]{0:T(1024)(128)(4,1)} %bitcast.37), calls=%async_computation.9 | async-start | bytes 4194304
  209.6 19.1 %slice-start = ((s8[12582912]{0:T(1024)(128)(4,1)}), s8[4194304]{0:T(1024)(128)(4,1)S(1)}, s32[]{:S(2)}) async-start(s8[12582912]{0:T(1024)(128)(4,1)} %bitcast.35), calls=%async_computation.5 | async-start | bytes 8388608
  209.6 19.1 %slice-start.1 = ((s8[12582912]{0:T(1024)(128)(4,1)}), s8[4194304]{0:T(1024)(128)(4,1)S(1)}, s32[]{:S(2)}) async-start(s8[12582912]{0:T(1024)(128)(4,1)} %bitcast.35), calls=%async_computation.6 | async-start | bytes 8388608
  220.6 8.2 %slice-start.2 = ((s8[12582912]{0:T(1024)(128)(4,1)}), s8[4194304]{0:T(1024)(128)(4,1)S(1)}, s32[]{:S(2)}) async-start(s8[12582912]{0:T(1024)(128)(4,1)} %bitcast.35), calls=%async_computation.7 | async-start | bytes 8388608
  247.3 88.5 %copy-start.2 = (f32[2048]{0:T(1024)S(1)}, f32[2048]{0:T(1024)}, u32[]{:S(2)}) copy-start(f32[2048]{0:T(1024)} %param.17) | copy-start | bytes 24580
Sparse Core Ops, SparseCore 0:
  50.7 155.4 all-reduce.1
  247.5 86.8 reduce-scatter.1

commit v3 on v2

--- a/solution.py
+++ b/solution.py
@@ -7,6 +7,54 @@
 def rms_scale(values, scale_gain):
     mean_square = jnp.mean(values * values, axis=-1, keepdims=True)
     return values * lax.rsqrt(mean_square + 1e-06) * scale_gain
+
+
+def ring_order(n):
+    if n % 2:
+        return list(range(n))
+    return list(range(0, n, 2)) + list(range(n - 1, 0, -2))
+
+
+def ring_reduce_scatter(blocks, ring, pos):
+    n, rows, _ = blocks.shape
+    half = rows // 2
+    ring_index = jnp.array(ring, dtype=jnp.int32)
+    forward = [(ring[q], ring[(q + 1) % n]) for q in range(n)]
+    backward = [(ring[q], ring[(q - 1) % n]) for q in range(n)]
+    got_fwd = got_bwd = None
+    for step in range(n - 1):
+        owner_fwd = ring_index[(pos - 1 - step) % n]
+        owner_bwd = ring_index[(pos + 1 + step) % n]
+        send_fwd = lax.dynamic_index_in_dim(blocks, owner_fwd, 0, keepdims=False)[:half]
+        send_bwd = lax.dynamic_index_in_dim(blocks, owner_bwd, 0, keepdims=False)[half:]
+        if step:
+            send_fwd = send_fwd + got_fwd
+            send_bwd = send_bwd + got_bwd
+        got_fwd = lax.ppermute(send_fwd.astype(jnp.bfloat16), "ep", forward).astype(jnp.float32)
+        got_bwd = lax.ppermute(send_bwd.astype(jnp.bfloat16), "ep", backward).astype(jnp.float32)
+    me = ring_index[pos]
+    own = lax.dynamic_index_in_dim(blocks, me, 0, keepdims=False)
+    return jnp.concatenate([own[:half] + got_fwd, own[half:] + got_bwd], axis=0)
+
+
+def ring_all_gather(block, ring, pos):
+    n = len(ring)
+    rows = block.shape[0]
+    half = rows // 2
+    ring_index = jnp.array(ring, dtype=jnp.int32)
+    forward = [(ring[q], ring[(q + 1) % n]) for q in range(n)]
+    backward = [(ring[q], ring[(q - 1) % n]) for q in range(n)]
+    out = jnp.zeros((n,) + block.shape, block.dtype)
+    out = lax.dynamic_update_index_in_dim(out, block, ring_index[pos], 0)
+    got_fwd, got_bwd = block[:half], block[half:]
+    for step in range(n - 1):
+        got_fwd = lax.ppermute(got_fwd, "ep", forward)
+        got_bwd = lax.ppermute(got_bwd, "ep", backward)
+        src_fwd = ring_index[(pos - 1 - step) % n]
+        src_bwd = ring_index[(pos + 1 + step) % n]
+        out = lax.dynamic_update_slice(out, got_fwd[None], (src_fwd, 0, 0))
+        out = lax.dynamic_update_slice(out, got_bwd[None], (src_bwd, half, 0))
+    return out
 
 
 def body(
@@ -19,6 +67,8 @@
     hidden_width = down.shape[1]
     slice_width = out_weight.shape[0]
     group_rows = row_count * ep_size
+    ring = ring_order(ep_size)
+    pos = jnp.array([ring.index(p) for p in range(ep_size)], dtype=jnp.int32)[me]
 
     with jax.named_scope("route_weights"):
         expert_ids = jnp.arange(local_experts * ep_size, dtype=jnp.int32)
@@ -35,12 +85,13 @@
         partial = jnp.dot(
             columns.reshape(group_rows, slice_width), out_weight, preferred_element_type=jnp.float32
         )
-        owner = (lax.broadcasted_iota(jnp.int32, (group_rows, 1), 0) // row_count) == me
-        padded_residual = jnp.tile(residual.astype(jnp.float32), (ep_size, 1))
-        partial = partial + jnp.where(owner, padded_residual, 0.0)
-        middle_all = lax.psum(partial.astype(jnp.bfloat16), "ep")
+        projected = ring_reduce_scatter(partial.reshape(ep_size, row_count, model_width), ring, pos)
+        middle = (residual.astype(jnp.float32) + projected).astype(jnp.bfloat16)
 
-    normed_all = rms_scale(middle_all.astype(jnp.float32), post_gain).astype(jnp.bfloat16)
+    normed = rms_scale(middle.astype(jnp.float32), post_gain).astype(jnp.bfloat16)
+    with jax.named_scope("dispatch_gather"):
+        normed_all = ring_all_gather(normed, ring, pos).reshape(group_rows, model_width)
+
     with jax.named_scope("local_experts"):
         combined_part = jnp.zeros((group_rows, model_width), jnp.float32)
         for e in range(local_experts):
@@ -55,11 +106,10 @@
             combined_part = combined_part + row_weight[:, None] * expert_out.astype(jnp.float32)
 
     with jax.named_scope("combine_return"):
-        combined = lax.psum_scatter(
-            combined_part.astype(jnp.bfloat16), "ep", scatter_dimension=0, tiled=True
+        combined = ring_reduce_scatter(
+            combined_part.reshape(ep_size, row_count, model_width), ring, pos
         )
-    middle = lax.dynamic_slice_in_dim(middle_all, me * row_count, row_count, axis=0)
-    updated = middle.astype(jnp.float32) + combined.astype(jnp.float32)
+    updated = middle.astype(jnp.float32) + combined
     return (updated.astype(jnp.bfloat16), rms_scale(updated, final_gain).astype(jnp.bfloat16))
 
 

time: 346 us -> 330 us (0.954)
  waiting for transfers between devices: 256 us -> 178 us
  starting transfers between devices: 7.36 us -> 40.4 us
  between operations: 14.1 us -> 41 us
  matrix products: 43.2 us -> 29.3 us
  other arithmetic: 8.28 us -> 17 us
    ppermute x0 -> x42, waiting for transfers between devices: none -> 168 us  [the longest x14 75 us: ring_reduce_scatter(): lax.ppermute(send_fwd.astype(jnp.bfloat16), 'ep', forward)]
    psum x1 -> x0, waiting for transfers between devices: 144 us -> none  [body(): middle_all = lax.psum(partial.astype(jnp.bfloat16), 'ep')]
    reduce_scatter x1 -> x0, waiting for transfers between devices: 87.1 us -> none  [body(): lax.psum_scatter(combined_part.astype(jnp.bfloat16), 'ep', scatter_dimens...]
    ppermute x0 -> x42, starting transfers between devices: none -> 33.1 us  [the longest x14 17.8 us: ring_reduce_scatter(): lax.ppermute(send_bwd.astype(jnp.bfloat16), 'ep', backward)]
    all_to_all x1, waiting for transfers between devices: 24.7 us -> 9.33 us  [body(): lax.all_to_all(columns, 'ep', split_axis=0, concat_axis=0, tiled=True)]
    convert_element_type x1 -> x22, other arithmetic: 1.14 us -> 12.6 us  [the longest x12 6.89 us: ring_reduce_scatter(): send_fwd.astype(jnp.bfloat16)]
    dot_general x2, matrix products: 18 us -> 9.64 us  [body(): jnp.dot(activated, down[e], preferred_element_type=jnp.float32)]
    reduce_sum x2, other arithmetic: 4.67 us -> 0.48 us  [rms_scale(): mean_square = jnp.mean(values * values, axis=-1, keepdims=True)]
  transfers between devices with their start and end apart: 3 -> 43, of which waited for: 3 -> 38; matrix products, arithmetic and copies ran while one was open for 0% -> 1% of each run, Pallas kernels for 0% -> 0%
where the time goes in v3:
time: 330 us; the launch traced here: 328 us
  waiting for transfers between devices  178 us (54%)
  between operations  41 us (12%)
  starting transfers between devices  40.4 us (12%)
  matrix products  29.3 us (9%)
  other arithmetic  17 us (5%)
  blocking collectives  14 us (4%)
  local copies, waits for them, and re-layouts  8.87 us (3%)
    ppermute x14, waiting for transfers between devices, ring_reduce_scatter(): lax.ppermute(send_fwd.astype(jnp.bfloat16), 'ep', forward)  75 us
    ppermute x14, waiting for transfers between devices, ring_reduce_scatter(): lax.ppermute(send_bwd.astype(jnp.bfloat16), 'ep', backward)  61.8 us
    ppermute x7, waiting for transfers between devices, ring_all_gather(): got_bwd = lax.ppermute(got_bwd, 'ep', backward)  23.4 us
    ppermute x14, starting transfers between devices, ring_reduce_scatter(): lax.ppermute(send_bwd.astype(jnp.bfloat16), 'ep', backward)  17.8 us
    dot_general x2, matrix products, body(): jnp.dot(normed_all, gate_up[e], preferred_element_type=jnp.float32)  17.3 us
    all_to_all x1, blocking collectives, body(): lax.all_to_all(dense_weight, 'ep', split_axis=0, concat_axis=0, tiled=True)  14 us
    dot_general x2, matrix products, body(): jnp.dot(activated, down[e], preferred_element_type=jnp.float32)  9.64 us
    all_to_all x1, waiting for transfers between devices, body(): lax.all_to_all(columns, 'ep', split_axis=0, concat_axis=0, tiled=True)  9.33 us
  transfers between devices with their start and end apart: 43, of which 38 were waited for; matrix products, arithmetic and copies ran while one was open for 1% of the time, Pallas kernels for 0%

profile of v3, /device:TPU:0, one launch (start us, length us, event | category | flops | bytes accessed | tf_op | source)
XLA Modules:
  0.0 328.2 jit_solution(4672074723467558836)
XLA Ops:
  0.7 1.8 copy.21
  2.5 1.3 copy.22
  3.8 7.3 %all-to-all-start = ((bf16[8,128,512]{2,1,0:T(8,128)(2,1)}), bf16[8,128,512]{2,1,0:T(8,128)(2,1)S(1)}, u32[]{:S(2)}, u32[]{:S(2)}) async-start(bf16[8,128,512]{2,1,0:T(8,128)(2,1)} %bitcast.1), calls=%async_computation | async-start | bytes 2097152 | tf_op jit(solution)/shard_map/out_projection/all_to_all | solution.py:84
  27.5 9.3 %all-to-all-done = bf16[8,128,512]{2,1,0:T(8,128)(2,1)S(1)} async-done(((bf16[8,128,512]{2,1,0:T(8,128)(2,1)}), bf16[8,128,512]{2,1,0:T(8,128)(2,1)S(1)}, u32[]{:S(2)}, u32[]{:S(2)}) %all-to-all-start) | async-done | bytes 1048608 | tf_op jit(solution)/shard_map/out_projection/all_to_all | solution.py:84
  36.8 2.4 fusion.13
  39.2 3.3 %copy-done.2 = f32[8,128,2048]{2,1,0:T(8,128)} copy-done((f32[8,128,2048]{2,1,0:T(8,128)}, f32[8,128,2048]{2,1,0:T(8,128)S(1)}, u32[]{:S(2)}) %copy-start.2) | copy-done | bytes 8388632
  44.3 5.2 %collective-permute-done = bf16[64,2048]{1,0:T(8,128)(2,1)S(1)} collective-permute-done((bf16[64,2048]{1,0:T(8,128)(2,1)S(1)}, bf16[64,2048]{1,0:T(8,128)(2,1)S(1)}, u32[]{:S(2)}, u32[]{:S(2)}) %collective-permute-start) | collective-permute-done | bytes 262176 | tf_op jit(solution)/shard_map/out_projection/ppermute | solution.py:33
  49.6 1.1 fusion.63
  52.8 4.3 %collective-permute-done.1 = bf16[64,2048]{1,0:T(8,128)(2,1)S(1)} collective-permute-done((bf16[64,2048]{1,0:T(8,128)(2,1)S(1)}, bf16[64,2048]{1,0:T(8,128)(2,1)S(1)}, u32[]{:S(2)}, u32[]{:S(2)}) %collective-permute-start.1) | collective-permute-done | bytes 262176 | tf_op jit(solution)/shard_map/out_projection/ppermute | solution.py:33
  60.3 4.3 %collective-permute-done.2 = bf16[64,2048]{1,0:T(8,128)(2,1)S(1)} collective-permute-done((bf16[64,2048]{1,0:T(8,128)(2,1)S(1)}, bf16[64,2048]{1,0:T(8,128)(2,1)S(1)}, u32[]{:S(2)}, u32[]{:S(2)}) %collective-permute-start.2) | collective-permute-done | bytes 262176 | tf_op jit(solution)/shard_map/out_projection/ppermute | solution.py:33
  67.6 4.6 %collective-permute-done.3 = bf16[64,2048]{1,0:T(8,128)(2,1)S(1)} collective-permute-done((bf16[64,2048]{1,0:T(8,128)(2,1)S(1)}, bf16[64,2048]{1,0:T(8,128)(2,1)S(1)}, u32[]{:S(2)}, u32[]{:S(2)}) %collective-permute-start.3) | collective-permute-done | bytes 262176 | tf_op jit(solution)/shard_map/out_projection/ppermute | solution.py:33
  75.3 4.7 %collective-permute-done.4 = bf16[64,2048]{1,0:T(8,128)(2,1)S(1)} collective-permute-done((bf16[64,2048]{1,0:T(8,128)(2,1)S(1)}, bf16[64,2048]{1,0:T(8,128)(2,1)S(1)}, u32[]{:S(2)}, u32[]{:S(2)}) %collective-permute-start.4) | collective-permute-done | bytes 262176 | tf_op jit(solution)/shard_map/out_projection/ppermute | solution.py:33
  82.9 2.2 collective-permute-start.7
  85.2 4.0 %collective-permute-done.5 = bf16[64,2048]{1,0:T(8,128)(2,1)S(1)} collective-permute-done((bf16[64,2048]{1,0:T(8,128)(2,1)S(1)}, bf16[64,2048]{1,0:T(8,128)(2,1)S(1)}, u32[]{:S(2)}, u32[]{:S(2)}) %collective-permute-start.5) | collective-permute-done | bytes 262176 | tf_op jit(solution)/shard_map/out_projection/ppermute | solution.py:33
  89.1 1.1 fusion.73
  95.0 2.0 collective-permute-done.6
  97.0 1.3 fusion.74
  98.3 2.1 collective-permute-start.8
  102.3 4.2 %collective-permute-done.8 = bf16[64,2048]{1,0:T(8,128)(2,1)S(1)} collective-permute-done((bf16[64,2048]{1,0:T(8,128)(2,1)S(1)}, bf16[64,2048]{1,0:T(8,128)(2,1)S(1)}, u32[]{:S(2)}, u32[]{:S(2)}) %collective-permute-start.8) | collective-permute-done | bytes 262176 | tf_op jit(solution)/shard_map/out_projection/ppermute | solution.py:34
  107.5 2.1 collective-permute-start.9
  111.5 4.0 %collective-permute-done.9 = bf16[64,2048]{1,0:T(8,128)(2,1)S(1)} collective-permute-done((bf16[64,2048]{1,0:T(8,128)(2,1)S(1)}, bf16[64,2048]{1,0:T(8,128)(2,1)S(1)}, u32[]{:S(2)}, u32[]{:S(2)}) %collective-permute-start.9) | collective-permute-done | bytes 262176 | tf_op jit(solution)/shard_map/out_projection/ppermute | solution.py:34
  115.5 1.1 fusion.54
  116.6 1.4 collective-permute-start.10
  120.0 3.6 %collective-permute-done.10 = bf16[64,2048]{1,0:T(8,128)(2,1)S(1)} collective-permute-done((bf16[64,2048]{1,0:T(8,128)(2,1)S(1)}, bf16[64,2048]{1,0:T(8,128)(2,1)S(1)}, u32[]{:S(2)}, u32[]{:S(2)}) %collective-permute-start.10) | collective-permute-done | bytes 262176 | tf_op jit(solution)/shard_map/out_projection/ppermute | solution.py:34
  123.7 1.1 fusion.56
  127.4 3.8 %collective-permute-done.11 = bf16[64,2048]{1,0:T(8,128)(2,1)S(1)} collective-permute-done((bf16[64,2048]{1,0:T(8,128)(2,1)S(1)}, bf16[64,2048]{1,0:T(8,128)(2,1)S(1)}, u32[]{:S(2)}, u32[]{:S(2)}) %collective-permute-start.11) | collective-permute-done | bytes 262176 | tf_op jit(solution)/shard_map/out_projection/ppermute | solution.py:34
  131.2 1.1 fusion.58
  134.9 3.8 %collective-permute-done.12 = bf16[64,2048]{1,0:T(8,128)(2,1)S(1)} collective-permute-done((bf16[64,2048]{1,0:T(8,128)(2,1)S(1)}, bf16[64,2048]{1,0:T(8,128)(2,1)S(1)}, u32[]{:S(2)}, u32[]{:S(2)}) %collective-permute-start.12) | collective-permute-done | bytes 262176 | tf_op jit(solution)/shard_map/out_projection/ppermute | solution.py:34
  138.7 1.1 fusion.60
  140.6 5.6 %collective-permute-done.13 = bf16[64,2048]{1,0:T(8,128)(2,1)S(1)} collective-permute-done((bf16[64,2048]{1,0:T(8,128)(2,1)S(1)}, bf16[64,2048]{1,0:T(8,128)(2,1)S(1)}, u32[]{:S(2)}, u32[]{:S(2)}) %collective-permute-start.13) | collective-permute-done | bytes 262176 | tf_op jit(solution)/shard_map/out_projection/ppermute | solution.py:34
  149.3 1.2 collective-permute-start.14
  150.5 14.0 %all_to_all.10 = f32[8,128,2]{1,2,0:T(2,128)S(1)} all-to-all(f32[8,128,2]{1,2,0:T(2,128)S(1)} %bitcast.260), channel_id=1, replica_groups=mesh['ep'=8,'rep'=4] {'ep'}, dimensions={0} | all-to-all | bytes 16384 | tf_op jit(solution)/shard_map/route_weights/all_to_all | solution.py:79
  165.1 1.6 collective-permute-start.16
  166.7 5.7 %collective-permute-done.17 = bf16[64,2048]{1,0:T(8,128)(2,1)S(1)} collective-permute-done((bf16[64,2048]{1,0:T(8,128)(2,1)S(1)}, bf16[64,2048]{1,0:T(8,128)(2,1)S(1)}, u32[]{:S(2)}, u32[]{:S(2)}) %collective-permute-start.17) | collective-permute-done | bytes 262176 | tf_op jit(solution)/shard_map/dispatch_gather/ppermute | solution.py:52
  173.0 1.5 collective-permute-start.18
  174.6 4.8 %collective-permute-done.19 = bf16[64,2048]{1,0:T(8,128)(2,1)S(1)} collective-permute-done((bf16[64,2048]{1,0:T(8,128)(2,1)S(1)}, bf16[64,2048]{1,0:T(8,128)(2,1)S(1)}, u32[]{:S(2)}, u32[]{:S(2)}) %collective-permute-start.19) | collective-permute-done | bytes 262176 | tf_op jit(solution)/shard_map/dispatch_gather/ppermute | solution.py:52
  181.5 4.3 %collective-permute-done.21 = bf16[64,2048]{1,0:T(8,128)(2,1)S(1)} collective-permute-done((bf16[64,2048]{1,0:T(8,128)(2,1)S(1)}, bf16[64,2048]{1,0:T(8,128)(2,1)S(1)}, u32[]{:S(2)}, u32[]{:S(2)}) %collective-permute-start.21) | collective-permute-done | bytes 262176 | tf_op jit(solution)/shard_map/dispatch_gather/ppermute | solution.py:52
  185.8 1.5 collective-permute-start.23
  187.9 4.3 %collective-permute-done.23 = bf16[64,2048]{1,0:T(8,128)(2,1)S(1)} collective-permute-done((bf16[64,2048]{1,0:T(8,128)(2,1)S(1)}, bf16[64,2048]{1,0:T(8,128)(2,1)S(1)}, u32[]{:S(2)}, u32[]{:S(2)}) %collective-permute-start.23) | collective-permute-done | bytes 262176 | tf_op jit(solution)/shard_map/dispatch_gather/ppermute | solution.py:52
  192.1 1.5 collective-permute-start.25
  194.2 4.3 %collective-permute-done.25 = bf16[64,2048]{1,0:T(8,128)(2,1)S(1)} collective-permute-done((bf16[64,2048]{1,0:T(8,128)(2,1)S(1)}, bf16[64,2048]{1,0:T(8,128)(2,1)S(1)}, u32[]{:S(2)}, u32[]{:S(2)}) %collective-permute-start.25) | collective-permute-done | bytes 262176 | tf_op jit(solution)/shard_map/dispatch_gather/ppermute | solution.py:52
  198.5 1.5 collective-permute-start.27
  200.6 6.3 %collective-permute-done.26 = bf16[64,2048]{1,0:T(8,128)(2,1)S(1)} collective-permute-done((bf16[64,2048]{1,0:T(8,128)(2,1)S(1)}, bf16[64,2048]{1,0:T(8,128)(2,1)S(1)}, u32[]{:S(2)}, u32[]{:S(2)}) %collective-permute-start.26) | collective-permute-done | bytes 262176 | tf_op jit(solution)/shard_map/dispatch_gather/ppermute | solution.py:51
  207.0 10.6 %fusion = f32[1024,1536]{1,0:T(8,128)} fusion(bf16[1024,2048]{1,0:T(8,128)(2,1)S(1)} %bitcast.256, bf16[2,2048,1536]{2,1,0:T(8,128)(2,1)} %param.17), kind=kOutput, calls=%fused_computation.1 | convolution fusion | flops 6442450944 | bytes 16777216 | tf_op jit(solution)/shard_map/local_experts/dot_general | solution.py:99
  217.6 6.7 %fusion.2 = f32[1024,1536]{1,0:T(8,128)S(1)} fusion(bf16[1024,2048]{1,0:T(8,128)(2,1)S(1)} %bitcast.257, bf16[2,2048,1536]{2,1,0:T(8,128)(2,1)S(1)} %bitcast.264), kind=kOutput, calls=%fused_computation.3 | convolution fusion | flops 6442450944 | bytes 16777216 | tf_op jit(solution)/shard_map/local_experts/dot_general | solution.py:99
  224.3 3.7 %fusion.9 = bf16[1024,2048]{1,0:T(8,128)(2,1)S(1)} fusion(bf16[2,768,2048]{2,1,0:T(8,128)(2,1)S(1)} %bitcast.266, f32[1024,1536]{1,0:T(8,128)S(1)} %fusion.2), kind=kOutput, calls=%fused_computation.12 | convolution fusion | flops 3225944064 | bytes 13631488 | tf_op jit(solution)/shard_map/local_experts/dot_general | solution.py:103
  228.0 6.0 %multiply_add_fusion = f32[1024,2048]{1,0:T(8,128)S(1)} fusion(f32[1024]{0:T(1024)S(1)} %bitcast.262, bf16[1024,2048]{1,0:T(8,128)(2,1)S(1)} %fusion.9, f32[1024]{0:T(1024)S(1)} %bitcast.261, bf16[2,768,2048]{2,1,0:T(8,128)(2,1)S(1)} %bitcast.266, f32[1024,1536]{1,0:T(8,128)} %fusion), kind=kOutput, calls=%fused_computation | convolution fusion | flops 3238526976 | bytes 22028288 | tf_op jit(solution)/shard_map/local_experts/dot_general | solution.py:103
  234.1 8.9 %collective-permute-done.28 = bf16[64,2048]{1,0:T(8,128)(2,1)S(1)} collective-permute-done((bf16[64,2048]{1,0:T(8,128)(2,1)S(1)}, bf16[64,2048]{1,0:T(8,128)(2,1)S(1)}, u32[]{:S(2)}, u32[]{:S(2)}) %collective-permute-start.28) | collective-permute-done | bytes 262176 | tf_op jit(solution)/shard_map/combine_return/ppermute | solution.py:33
  243.2 8.7 %collective-permute-done.29 = bf16[64,2048]{1,0:T(8,128)(2,1)S(1)} collective-permute-done((bf16[64,2048]{1,0:T(8,128)(2,1)S(1)}, bf16[64,2048]{1,0:T(8,128)(2,1)S(1)}, u32[]{:S(2)}, u32[]{:S(2)}) %collective-permute-start.29) | collective-permute-done | bytes 262176 | tf_op jit(solution)/shard_map/combine_return/ppermute | solution.py:33
  252.0 7.7 %collective-permute-done.30 = bf16[64,2048]{1,0:T(8,128)(2,1)S(1)} collective-permute-done((bf16[64,2048]{1,0:T(8,128)(2,1)S(1)}, bf16[64,2048]{1,0:T(8,128)(2,1)S(1)}, u32[]{:S(2)}, u32[]{:S(2)}) %collective-permute-start.30) | collective-permute-done | bytes 262176 | tf_op jit(solution)/shard_map/combine_return/ppermute | solution.py:33
  260.1 6.1 %collective-permute-done.31 = bf16[64,2048]{1,0:T(8,128)(2,1)S(1)} collective-permute-done((bf16[64,2048]{1,0:T(8,128)(2,1)S(1)}, bf16[64,2048]{1,0:T(8,128)(2,1)S(1)}, u32[]{:S(2)}, u32[]{:S(2)}) %collective-permute-start.31) | collective-permute-done | bytes 262176 | tf_op jit(solution)/shard_map/combine_return/ppermute | solution.py:33
  266.6 6.1 %collective-permute-done.32 = bf16[64,2048]{1,0:T(8,128)(2,1)S(1)} collective-permute-done((bf16[64,2048]{1,0:T(8,128)(2,1)S(1)}, bf16[64,2048]{1,0:T(8,128)(2,1)S(1)}, u32[]{:S(2)}, u32[]{:S(2)}) %collective-permute-start.32) | collective-permute-done | bytes 262176 | tf_op jit(solution)/shard_map/combine_return/ppermute | solution.py:33
  273.1 1.7 collective-permute-start.35
  274.8 4.3 %collective-permute-done.33 = bf16[64,2048]{1,0:T(8,128)(2,1)S(1)} collective-permute-done((bf16[64,2048]{1,0:T(8,128)(2,1)S(1)}, bf16[64,2048]{1,0:T(8,128)(2,1)S(1)}, u32[]{:S(2)}, u32[]{:S(2)}) %collective-permute-start.33) | collective-permute-done | bytes 262176 | tf_op jit(solution)/shard_map/combine_return/ppermute | solution.py:33
  279.5 2.0 collective-permute-done.35
  281.5 4.1 %collective-permute-done.34 = bf16[64,2048]{1,0:T(8,128)(2,1)S(1)} collective-permute-done((bf16[64,2048]{1,0:T(8,128)(2,1)S(1)}, bf16[64,2048]{1,0:T(8,128)(2,1)S(1)}, u32[]{:S(2)}, u32[]{:S(2)}) %collective-permute-start.34) | collective-permute-done | bytes 262176 | tf_op jit(solution)/shard_map/combine_return/ppermute | solution.py:33
  285.8 1.5 collective-permute-start.36
  287.2 7.1 %collective-permute-done.36 = bf16[64,2048]{1,0:T(8,128)(2,1)S(1)} collective-permute-done((bf16[64,2048]{1,0:T(8,128)(2,1)S(1)}, bf16[64,2048]{1,0:T(8,128)(2,1)S(1)}, u32[]{:S(2)}, u32[]{:S(2)}) %collective-permute-start.36) | collective-permute-done | bytes 262176 | tf_op jit(solution)/shard_map/combine_return/ppermute | solution.py:34
  295.3 5.5 %collective-permute-done.37 = bf16[64,2048]{1,0:T(8,128)(2,1)S(1)} collective-permute-done((bf16[64,2048]{1,0:T(8,128)(2,1)S(1)}, bf16[64,2048]{1,0:T(8,128)(2,1)S(1)}, u32[]{:S(2)}, u32[]{:S(2)}) %collective-permute-start.37) | collective-permute-done | bytes 262176 | tf_op jit(solution)/shard_map/combine_return/ppermute | solution.py:34
  301.8 5.5 %collective-permute-done.38 = bf16[64,2048]{1,0:T(8,128)(2,1)S(1)} collective-permute-done((bf16[64,2048]{1,0:T(8,128)(2,1)S(1)}, bf16[64,2048]{1,0:T(8,128)(2,1)S(1)}, u32[]{:S(2)}, u32[]{:S(2)}) %collective-permute-start.38) | collective-permute-done | bytes 262176 | tf_op jit(solution)/shard_map/combine_return/ppermute | solution.py:34
  308.3 5.5 %collective-permute-done.39 = bf16[64,2048]{1,0:T(8,128)(2,1)S(1)} collective-permute-done((bf16[64,2048]{1,0:T(8,128)(2,1)S(1)}, bf16[64,2048]{1,0:T(8,128)(2,1)S(1)}, u32[]{:S(2)}, u32[]{:S(2)}) %collective-permute-start.39) | collective-permute-done | bytes 262176 | tf_op jit(solution)/shard_map/combine_return/ppermute | solution.py:34
  314.7 5.5 %collective-permute-done.40 = bf16[64,2048]{1,0:T(8,128)(2,1)S(1)} collective-permute-done((bf16[64,2048]{1,0:T(8,128)(2,1)S(1)}, bf16[64,2048]{1,0:T(8,128)(2,1)S(1)}, u32[]{:S(2)}, u32[]{:S(2)}) %collective-permute-start.40) | collective-permute-done | bytes 262176 | tf_op jit(solution)/shard_map/combine_return/ppermute | solution.py:34
  321.2 5.5 %collective-permute-done.41 = bf16[64,2048]{1,0:T(8,128)(2,1)S(1)} collective-permute-done((bf16[64,2048]{1,0:T(8,128)(2,1)S(1)}, bf16[64,2048]{1,0:T(8,128)(2,1)S(1)}, u32[]{:S(2)}, u32[]{:S(2)}) %collective-permute-start.41) | collective-permute-done | bytes 262176 | tf_op jit(solution)/shard_map/combine_return/ppermute | solution.py:34
  327.1 1.2 multiply_convert_fusion
  (116 shorter events, 25.6 us)
Async XLA Ops:
  0.6 36.2 %copy-start = (bf16[512,2048]{1,0:T(8,128)(2,1)S(1)}, bf16[512,2048]{1,0:T(8,128)(2,1)}, u32[]{:S(2)}) copy-start(bf16[512,2048]{1,0:T(8,128)(2,1)} %param.15) | copy-start | bytes 6291460
  0.6 10.4 %copy-start.9 = (s32[8]{0:T(128)S(1)}, s32[8]{0:T(128)}, u32[]{:S(2)}) copy-start(s32[8]{0:T(128)} %constant.252.clone) | copy-start | bytes 100
  0.7 22.3 %copy-start.4 = (s32[8]{0:T(128)S(1)}, s32[8]{0:T(128)}, u32[]{:S(2)}) copy-start(s32[8]{0:T(128)} %constant.253.clone) | copy-start | bytes 100
  3.8 33.0 %all-to-all-start = ((bf16[8,128,512]{2,1,0:T(8,128)(2,1)}), bf16[8,128,512]{2,1,0:T(8,128)(2,1)S(1)}, u32[]{:S(2)}, u32[]{:S(2)}) async-start(bf16[8,128,512]{2,1,0:T(8,128)(2,1)} %bitcast.1), calls=%async_computation | async-start | bytes 2097152 | tf_op jit(solution)/shard_map/out_projection/all_to_all | solution.py:84
  39.2 3.3 %copy-start.2 = (f32[8,128,2048]{2,1,0:T(8,128)}, f32[8,128,2048]{2,1,0:T(8,128)S(1)}, u32[]{:S(2)}) copy-start(f32[8,128,2048]{2,1,0:T(8,128)S(1)} %fusion.13) | copy-start | bytes 25165828
  42.6 7.0 %collective-permute-start = (bf16[64,2048]{1,0:T(8,128)(2,1)S(1)}, bf16[64,2048]{1,0:T(8,128)(2,1)S(1)}, u32[]{:S(2)}, u32[]{:S(2)}) collective-permute-start(bf16[64,2048]{1,0:T(8,128)(2,1)S(1)} %get-tuple-element.12), channel_id=1, source_target_pairs={{0,8},{8,16},{16,24},{24,28},{28,20},{20,12},{12,4},{4,0},{1,9},{9... | collective-permute-start | bytes 786440 | tf_op jit(solution)/shard_map/out_projection/ppermute | solution.py:33
  50.7 6.4 %collective-permute-start.1 = (bf16[64,2048]{1,0:T(8,128)(2,1)S(1)}, bf16[64,2048]{1,0:T(8,128)(2,1)S(1)}, u32[]{:S(2)}, u32[]{:S(2)}) collective-permute-start(bf16[64,2048]{1,0:T(8,128)(2,1)S(1)} %fusion.63), channel_id=1, source_target_pairs={{0,8},{8,16},{16,24},{24,28},{28,20},{20,12},{12,4},{4,0},{1,9},{9... | collective-permute-start | bytes 786440 | tf_op jit(solution)/shard_map/out_projection/ppermute | solution.py:33
  58.2 6.4 %collective-permute-start.2 = (bf16[64,2048]{1,0:T(8,128)(2,1)S(1)}, bf16[64,2048]{1,0:T(8,128)(2,1)S(1)}, u32[]{:S(2)}, u32[]{:S(2)}) collective-permute-start(bf16[64,2048]{1,0:T(8,128)(2,1)S(1)} %fusion.65), channel_id=1, source_target_pairs={{0,8},{8,16},{16,24},{24,28},{28,20},{20,12},{12,4},{4,0},{1,9},{9... | collective-permute-start | bytes 786440 | tf_op jit(solution)/shard_map/out_projection/ppermute | solution.py:33
  65.7 6.5 %collective-permute-start.3 = (bf16[64,2048]{1,0:T(8,128)(2,1)S(1)}, bf16[64,2048]{1,0:T(8,128)(2,1)S(1)}, u32[]{:S(2)}, u32[]{:S(2)}) collective-permute-start(bf16[64,2048]{1,0:T(8,128)(2,1)S(1)} %fusion.67), channel_id=1, source_target_pairs={{0,8},{8,16},{16,24},{24,28},{28,20},{20,12},{12,4},{4,0},{1,9},{9... | collective-permute-start | bytes 786440 | tf_op jit(solution)/shard_map/out_projection/ppermute | solution.py:33
  73.3 6.7 %collective-permute-start.4 = (bf16[64,2048]{1,0:T(8,128)(2,1)S(1)}, bf16[64,2048]{1,0:T(8,128)(2,1)S(1)}, u32[]{:S(2)}, u32[]{:S(2)}) collective-permute-start(bf16[64,2048]{1,0:T(8,128)(2,1)S(1)} %fusion.69), channel_id=1, source_target_pairs={{0,8},{8,16},{16,24},{24,28},{28,20},{20,12},{12,4},{4,0},{1,9},{9... | collective-permute-start | bytes 786440 | tf_op jit(solution)/shard_map/out_projection/ppermute | solution.py:33
  81.1 8.0 %collective-permute-start.5 = (bf16[64,2048]{1,0:T(8,128)(2,1)S(1)}, bf16[64,2048]{1,0:T(8,128)(2,1)S(1)}, u32[]{:S(2)}, u32[]{:S(2)}) collective-permute-start(bf16[64,2048]{1,0:T(8,128)(2,1)S(1)} %fusion.71), channel_id=1, source_target_pairs={{0,8},{8,16},{16,24},{24,28},{28,20},{20,12},{12,4},{4,0},{1,9},{9... | collective-permute-start | bytes 786440 | tf_op jit(solution)/shard_map/out_projection/ppermute | solution.py:33
  82.9 12.0 %collective-permute-start.7 = (bf16[64,2048]{1,0:T(8,128)(2,1)S(1)}, bf16[64,2048]{1,0:T(8,128)(2,1)S(1)}, u32[]{:S(2)}, u32[]{:S(2)}) collective-permute-start(bf16[64,2048]{1,0:T(8,128)(2,1)S(1)} %get-tuple-element.13), channel_id=1, source_target_pairs={{0,4},{8,0},{16,8},{24,16},{28,24},{20,28},{12,20},{4,12},{1,5},{9... | collective-permute-start | bytes 786440 | tf_op jit(solution)/shard_map/out_projection/ppermute | solution.py:34
  90.2 6.7 %collective-permute-start.6 = (bf16[64,2048]{1,0:T(8,128)(2,1)S(1)}, bf16[64,2048]{1,0:T(8,128)(2,1)S(1)}, u32[]{:S(2)}, u32[]{:S(2)}) collective-permute-start(bf16[64,2048]{1,0:T(8,128)(2,1)S(1)} %fusion.73), channel_id=1, source_target_pairs={{0,8},{8,16},{16,24},{24,28},{28,20},{20,12},{12,4},{4,0},{1,9},{9... | collective-permute-start | bytes 786440 | tf_op jit(solution)/shard_map/out_projection/ppermute | solution.py:33
  95.0 52.4 %copy-start.3 = (bf16[128,2048]{1,0:T(8,128)(2,1)S(1)}, bf16[128,2048]{1,0:T(8,128)(2,1)}, u32[]{:S(2)}) copy-start(bf16[128,2048]{1,0:T(8,128)(2,1)} %param.13) | copy-start | bytes 1572868
  98.3 8.2 %collective-permute-start.8 = (bf16[64,2048]{1,0:T(8,128)(2,1)S(1)}, bf16[64,2048]{1,0:T(8,128)(2,1)S(1)}, u32[]{:S(2)}, u32[]{:S(2)}) collective-permute-start(bf16[64,2048]{1,0:T(8,128)(2,1)S(1)} %get-tuple-element.11), channel_id=1, source_target_pairs={{0,4},{8,0},{16,8},{24,16},{28,24},{20,28},{12,20},{4,12},{1,5},{9... | collective-permute-start | bytes 786440 | tf_op jit(solution)/shard_map/out_projection/ppermute | solution.py:34
  107.5 8.0 %collective-permute-start.9 = (bf16[64,2048]{1,0:T(8,128)(2,1)S(1)}, bf16[64,2048]{1,0:T(8,128)(2,1)S(1)}, u32[]{:S(2)}, u32[]{:S(2)}) collective-permute-start(bf16[64,2048]{1,0:T(8,128)(2,1)S(1)} %fusion.52), channel_id=1, source_target_pairs={{0,4},{8,0},{16,8},{24,16},{28,24},{20,28},{12,20},{4,12},{1,5},{9... | collective-permute-start | bytes 786440 | tf_op jit(solution)/shard_map/out_projection/ppermute | solution.py:34
  116.6 7.1 %collective-permute-start.10 = (bf16[64,2048]{1,0:T(8,128)(2,1)S(1)}, bf16[64,2048]{1,0:T(8,128)(2,1)S(1)}, u32[]{:S(2)}, u32[]{:S(2)}) collective-permute-start(bf16[64,2048]{1,0:T(8,128)(2,1)S(1)} %fusion.54), channel_id=1, source_target_pairs={{0,4},{8,0},{16,8},{24,16},{28,24},{20,28},{12,20},{4,12},{1,5},{9... | collective-permute-start | bytes 786440 | tf_op jit(solution)/shard_map/out_projection/ppermute | solution.py:34
  124.8 6.4 %collective-permute-start.11 = (bf16[64,2048]{1,0:T(8,128)(2,1)S(1)}, bf16[64,2048]{1,0:T(8,128)(2,1)S(1)}, u32[]{:S(2)}, u32[]{:S(2)}) collective-permute-start(bf16[64,2048]{1,0:T(8,128)(2,1)S(1)} %fusion.56), channel_id=1, source_target_pairs={{0,4},{8,0},{16,8},{24,16},{28,24},{20,28},{12,20},{4,12},{1,5},{9... | collective-permute-start | bytes 786440 | tf_op jit(solution)/shard_map/out_projection/ppermute | solution.py:34
  132.3 6.4 %collective-permute-start.12 = (bf16[64,2048]{1,0:T(8,128)(2,1)S(1)}, bf16[64,2048]{1,0:T(8,128)(2,1)S(1)}, u32[]{:S(2)}, u32[]{:S(2)}) collective-permute-start(bf16[64,2048]{1,0:T(8,128)(2,1)S(1)} %fusion.58), channel_id=1, source_target_pairs={{0,4},{8,0},{16,8},{24,16},{28,24},{20,28},{12,20},{4,12},{1,5},{9... | collective-permute-start | bytes 786440 | tf_op jit(solution)/shard_map/out_projection/ppermute | solution.py:34
  134.9 13.3 %copy-start.5 = (f32[2048]{0:T(1024)S(1)}, f32[2048]{0:T(1024)}, u32[]{:S(2)}) copy-start(f32[2048]{0:T(1024)} %param.16) | copy-start | bytes 24580
  139.8 6.5 %collective-permute-start.13 = (bf16[64,2048]{1,0:T(8,128)(2,1)S(1)}, bf16[64,2048]{1,0:T(8,128)(2,1)S(1)}, u32[]{:S(2)}, u32[]{:S(2)}) collective-permute-start(bf16[64,2048]{1,0:T(8,128)(2,1)S(1)} %fusion.60), channel_id=1, source_target_pairs={{0,4},{8,0},{16,8},{24,16},{28,24},{20,28},{12,20},{4,12},{1,5},{9... | collective-permute-start | bytes 786440 | tf_op jit(solution)/shard_map/out_projection/ppermute | solution.py:34
  147.4 3.1 copy-start.7
  147.4 3.1 copy-start.8
  148.4 16.2 %collective-permute-start.15 = (bf16[64,2048]{1,0:T(8,128)(2,1)S(1)}, bf16[64,2048]{1,0:T(8,128)(2,1)S(1)}, u32[]{:S(2)}, u32[]{:S(2)}) collective-permute-start(bf16[64,2048]{1,0:T(8,128)(2,1)S(1)} %get-tuple-element.16), channel_id=1, source_target_pairs={{0,4},{8,0},{16,8},{24,16},{28,24},{20,28},{12,20},{4,12},{1,5},{9... | collective-permute-start | bytes 786440 | tf_op jit(solution)/shard_map/dispatch_gather/ppermute | solution.py:52
  149.3 15.8 %collective-permute-start.14 = (bf16[64,2048]{1,0:T(8,128)(2,1)S(1)}, bf16[64,2048]{1,0:T(8,128)(2,1)S(1)}, u32[]{:S(2)}, u32[]{:S(2)}) collective-permute-start(bf16[64,2048]{1,0:T(8,128)(2,1)S(1)} %get-tuple-element.17), channel_id=1, source_target_pairs={{0,8},{8,16},{16,24},{24,28},{28,20},{20,12},{12,4},{4,0},{1,9},{9... | collective-permute-start | bytes 786440 | tf_op jit(solution)/shard_map/dispatch_gather/ppermute | solution.py:51
  164.6 7.9 %collective-permute-start.17 = (bf16[64,2048]{1,0:T(8,128)(2,1)S(1)}, bf16[64,2048]{1,0:T(8,128)(2,1)S(1)}, u32[]{:S(2)}, u32[]{:S(2)}) collective-permute-start(bf16[64,2048]{1,0:T(8,128)(2,1)S(1)} %collective-permute-done.15), channel_id=1, source_target_pairs={{0,4},{8,0},{16,8},{24,16},{28,24},{20,28},{12,20},{4,12},{1,5},{9... | collective-permute-start | bytes 786440 | tf_op jit(solution)/shard_map/dispatch_gather/ppermute | solution.py:52
  165.1 7.9 %collective-permute-start.16 = (bf16[64,2048]{1,0:T(8,128)(2,1)S(1)}, bf16[64,2048]{1,0:T(8,128)(2,1)S(1)}, u32[]{:S(2)}, u32[]{:S(2)}) collective-permute-start(bf16[64,2048]{1,0:T(8,128)(2,1)S(1)} %collective-permute-done.14), channel_id=1, source_target_pairs={{0,8},{8,16},{16,24},{24,28},{28,20},{20,12},{12,4},{4,0},{1,9},{9... | collective-permute-start | bytes 786440 | tf_op jit(solution)/shard_map/dispatch_gather/ppermute | solution.py:51
  172.5 6.9 %collective-permute-start.19 = (bf16[64,2048]{1,0:T(8,128)(2,1)S(1)}, bf16[64,2048]{1,0:T(8,128)(2,1)S(1)}, u32[]{:S(2)}, u32[]{:S(2)}) collective-permute-start(bf16[64,2048]{1,0:T(8,128)(2,1)S(1)} %collective-permute-done.17), channel_id=1, source_target_pairs={{0,4},{8,0},{16,8},{24,16},{28,24},{20,28},{12,20},{4,12},{1,5},{9... | collective-permute-start | bytes 786440 | tf_op jit(solution)/shard_map/dispatch_gather/ppermute | solution.py:52
  173.0 7.6 %collective-permute-start.18 = (bf16[64,2048]{1,0:T(8,128)(2,1)S(1)}, bf16[64,2048]{1,0:T(8,128)(2,1)S(1)}, u32[]{:S(2)}, u32[]{:S(2)}) collective-permute-start(bf16[64,2048]{1,0:T(8,128)(2,1)S(1)} %collective-permute-done.16), channel_id=1, source_target_pairs={{0,8},{8,16},{16,24},{24,28},{28,20},{20,12},{12,4},{4,0},{1,9},{9... | collective-permute-start | bytes 786440 | tf_op jit(solution)/shard_map/dispatch_gather/ppermute | solution.py:51
  179.4 6.4 %collective-permute-start.21 = (bf16[64,2048]{1,0:T(8,128)(2,1)S(1)}, bf16[64,2048]{1,0:T(8,128)(2,1)S(1)}, u32[]{:S(2)}, u32[]{:S(2)}) collective-permute-start(bf16[64,2048]{1,0:T(8,128)(2,1)S(1)} %collective-permute-done.19), channel_id=1, source_target_pairs={{0,4},{8,0},{16,8},{24,16},{28,24},{20,28},{12,20},{4,12},{1,5},{9... | collective-permute-start | bytes 786440 | tf_op jit(solution)/shard_map/dispatch_gather/ppermute | solution.py:52
  180.6 7.1 %collective-permute-start.20 = (bf16[64,2048]{1,0:T(8,128)(2,1)S(1)}, bf16[64,2048]{1,0:T(8,128)(2,1)S(1)}, u32[]{:S(2)}, u32[]{:S(2)}) collective-permute-start(bf16[64,2048]{1,0:T(8,128)(2,1)S(1)} %collective-permute-done.18), channel_id=1, source_target_pairs={{0,8},{8,16},{16,24},{24,28},{28,20},{20,12},{12,4},{4,0},{1,9},{9... | collective-permute-start | bytes 786440 | tf_op jit(solution)/shard_map/dispatch_gather/ppermute | solution.py:51
  185.8 6.4 %collective-permute-start.23 = (bf16[64,2048]{1,0:T(8,128)(2,1)S(1)}, bf16[64,2048]{1,0:T(8,128)(2,1)S(1)}, u32[]{:S(2)}, u32[]{:S(2)}) collective-permute-start(bf16[64,2048]{1,0:T(8,128)(2,1)S(1)} %collective-permute-done.21), channel_id=1, source_target_pairs={{0,4},{8,0},{16,8},{24,16},{28,24},{20,28},{12,20},{4,12},{1,5},{9... | collective-permute-start | bytes 786440 | tf_op jit(solution)/shard_map/dispatch_gather/ppermute | solution.py:52
  187.7 6.4 %collective-permute-start.22 = (bf16[64,2048]{1,0:T(8,128)(2,1)S(1)}, bf16[64,2048]{1,0:T(8,128)(2,1)S(1)}, u32[]{:S(2)}, u32[]{:S(2)}) collective-permute-start(bf16[64,2048]{1,0:T(8,128)(2,1)S(1)} %collective-permute-done.20), channel_id=1, source_target_pairs={{0,8},{8,16},{16,24},{24,28},{28,20},{20,12},{12,4},{4,0},{1,9},{9... | collective-permute-start | bytes 786440 | tf_op jit(solution)/shard_map/dispatch_gather/ppermute | solution.py:51
  192.1 6.4 %collective-permute-start.25 = (bf16[64,2048]{1,0:T(8,128)(2,1)S(1)}, bf16[64,2048]{1,0:T(8,128)(2,1)S(1)}, u32[]{:S(2)}, u32[]{:S(2)}) collective-permute-start(bf16[64,2048]{1,0:T(8,128)(2,1)S(1)} %collective-permute-done.23), channel_id=1, source_target_pairs={{0,4},{8,0},{16,8},{24,16},{28,24},{20,28},{12,20},{4,12},{1,5},{9... | collective-permute-start | bytes 786440 | tf_op jit(solution)/shard_map/dispatch_gather/ppermute | solution.py:52
  194.1 6.4 %collective-permute-start.24 = (bf16[64,2048]{1,0:T(8,128)(2,1)S(1)}, bf16[64,2048]{1,0:T(8,128)(2,1)S(1)}, u32[]{:S(2)}, u32[]{:S(2)}) collective-permute-start(bf16[64,2048]{1,0:T(8,128)(2,1)S(1)} %collective-permute-done.22), channel_id=1, source_target_pairs={{0,8},{8,16},{16,24},{24,28},{28,20},{20,12},{12,4},{4,0},{1,9},{9... | collective-permute-start | bytes 786440 | tf_op jit(solution)/shard_map/dispatch_gather/ppermute | solution.py:51
  198.5 8.4 %collective-permute-start.27 = (bf16[64,2048]{1,0:T(8,128)(2,1)S(1)}, bf16[64,2048]{1,0:T(8,128)(2,1)S(1)}, u32[]{:S(2)}, u32[]{:S(2)}) collective-permute-start(bf16[64,2048]{1,0:T(8,128)(2,1)S(1)} %collective-permute-done.25), channel_id=1, source_target_pairs={{0,4},{8,0},{16,8},{24,16},{28,24},{20,28},{12,20},{4,12},{1,5},{9... | collective-permute-start | bytes 786440 | tf_op jit(solution)/shard_map/dispatch_gather/ppermute | solution.py:52
  200.5 6.4 %collective-permute-start.26 = (bf16[64,2048]{1,0:T(8,128)(2,1)S(1)}, bf16[64,2048]{1,0:T(8,128)(2,1)S(1)}, u32[]{:S(2)}, u32[]{:S(2)}) collective-permute-start(bf16[64,2048]{1,0:T(8,128)(2,1)S(1)} %collective-permute-done.24), channel_id=1, source_target_pairs={{0,8},{8,16},{16,24},{24,28},{28,20},{20,12},{12,4},{4,0},{1,9},{9... | collective-permute-start | bytes 786440 | tf_op jit(solution)/shard_map/dispatch_gather/ppermute | solution.py:51
  206.9 10.7 %slice-start = ((s8[12582912]{0:T(1024)(128)(4,1)}), s8[4194304]{0:T(1024)(128)(4,1)S(1)}, s32[]{:S(2)}) async-start(s8[12582912]{0:T(1024)(128)(4,1)} %bitcast.263), calls=%async_computation.2 | async-start | bytes 8388608
  206.9 10.7 %slice-start.1 = ((s8[12582912]{0:T(1024)(128)(4,1)}), s8[4194304]{0:T(1024)(128)(4,1)S(1)}, s32[]{:S(2)}) async-start(s8[12582912]{0:T(1024)(128)(4,1)} %bitcast.263), calls=%async_computation.3 | async-start | bytes 8388608
  206.9 10.6 %slice-start.2 = ((s8[12582912]{0:T(1024)(128)(4,1)}), s8[4194304]{0:T(1024)(128)(4,1)S(1)}, s32[]{:S(2)}) async-start(s8[12582912]{0:T(1024)(128)(4,1)} %bitcast.263), calls=%async_computation.4 | async-start | bytes 8388608
  207.0 17.3 %slice-start.3 = ((s8[6291456]{0:T(1024)(128)(4,1)}), s8[4194304]{0:T(1024)(128)(4,1)S(1)}, s32[]{:S(2)}) async-start(s8[6291456]{0:T(1024)(128)(4,1)} %bitcast.265), calls=%async_computation.5 | async-start | bytes 8388608
  217.6 6.7 %slice-start.4 = ((s8[6291456]{0:T(1024)(128)(4,1)}), s8[2097152]{0:T(1024)(128)(4,1)S(1)}, s32[]{:S(2)}) async-start(s8[6291456]{0:T(1024)(128)(4,1)} %bitcast.265), calls=%async_computation.6 | async-start | bytes 4194304
  234.0 9.0 %collective-permute-start.28 = (bf16[64,2048]{1,0:T(8,128)(2,1)S(1)}, bf16[64,2048]{1,0:T(8,128)(2,1)S(1)}, u32[]{:S(2)}, u32[]{:S(2)}) collective-permute-start(bf16[64,2048]{1,0:T(8,128)(2,1)S(1)} %get-tuple-element.8), channel_id=1, source_target_pairs={{0,8},{8,16},{16,24},{24,28},{28,20},{20,12},{12,4},{4,0},{1,9},{9... | collective-permute-start | bytes 786440 | tf_op jit(solution)/shard_map/combine_return/ppermute | solution.py:33
  243.1 8.7 %collective-permute-start.29 = (bf16[64,2048]{1,0:T(8,128)(2,1)S(1)}, bf16[64,2048]{1,0:T(8,128)(2,1)S(1)}, u32[]{:S(2)}, u32[]{:S(2)}) collective-permute-start(bf16[64,2048]{1,0:T(8,128)(2,1)S(1)} %fusion.37), channel_id=1, source_target_pairs={{0,8},{8,16},{16,24},{24,28},{28,20},{20,12},{12,4},{4,0},{1,9},{9... | collective-permute-start | bytes 786440 | tf_op jit(solution)/shard_map/combine_return/ppermute | solution.py:33
  251.9 7.8 %collective-permute-start.30 = (bf16[64,2048]{1,0:T(8,128)(2,1)S(1)}, bf16[64,2048]{1,0:T(8,128)(2,1)S(1)}, u32[]{:S(2)}, u32[]{:S(2)}) collective-permute-start(bf16[64,2048]{1,0:T(8,128)(2,1)S(1)} %fusion.39), channel_id=1, source_target_pairs={{0,8},{8,16},{16,24},{24,28},{28,20},{20,12},{12,4},{4,0},{1,9},{9... | collective-permute-start | bytes 786440 | tf_op jit(solution)/shard_map/combine_return/ppermute | solution.py:33
  259.8 6.4 %collective-permute-start.31 = (bf16[64,2048]{1,0:T(8,128)(2,1)S(1)}, bf16[64,2048]{1,0:T(8,128)(2,1)S(1)}, u32[]{:S(2)}, u32[]{:S(2)}) collective-permute-start(bf16[64,2048]{1,0:T(8,128)(2,1)S(1)} %fusion.41), channel_id=1, source_target_pairs={{0,8},{8,16},{16,24},{24,28},{28,20},{20,12},{12,4},{4,0},{1,9},{9... | collective-permute-start | bytes 786440 | tf_op jit(solution)/shard_map/combine_return/ppermute | solution.py:33
  266.2 6.4 %collective-permute-start.32 = (bf16[64,2048]{1,0:T(8,128)(2,1)S(1)}, bf16[64,2048]{1,0:T(8,128)(2,1)S(1)}, u32[]{:S(2)}, u32[]{:S(2)}) collective-permute-start(bf16[64,2048]{1,0:T(8,128)(2,1)S(1)} %fusion.43), channel_id=1, source_target_pairs={{0,8},{8,16},{16,24},{24,28},{28,20},{20,12},{12,4},{4,0},{1,9},{9... | collective-permute-start | bytes 786440 | tf_op jit(solution)/shard_map/combine_return/ppermute | solution.py:33
  272.7 6.4 %collective-permute-start.33 = (bf16[64,2048]{1,0:T(8,128)(2,1)S(1)}, bf16[64,2048]{1,0:T(8,128)(2,1)S(1)}, u32[]{:S(2)}, u32[]{:S(2)}) collective-permute-start(bf16[64,2048]{1,0:T(8,128)(2,1)S(1)} %fusion.45), channel_id=1, source_target_pairs={{0,8},{8,16},{16,24},{24,28},{28,20},{20,12},{12,4},{4,0},{1,9},{9... | collective-permute-start | bytes 786440 | tf_op jit(solution)/shard_map/combine_return/ppermute | solution.py:33
  273.1 8.5 %collective-permute-start.35 = (bf16[64,2048]{1,0:T(8,128)(2,1)S(1)}, bf16[64,2048]{1,0:T(8,128)(2,1)S(1)}, u32[]{:S(2)}, u32[]{:S(2)}) collective-permute-start(bf16[64,2048]{1,0:T(8,128)(2,1)S(1)} %get-tuple-element.9), channel_id=1, source_target_pairs={{0,4},{8,0},{16,8},{24,16},{28,24},{20,28},{12,20},{4,12},{1,5},{9... | collective-permute-start | bytes 786440 | tf_op jit(solution)/shard_map/combine_return/ppermute | solution.py:34
  279.2 6.4 %collective-permute-start.34 = (bf16[64,2048]{1,0:T(8,128)(2,1)S(1)}, bf16[64,2048]{1,0:T(8,128)(2,1)S(1)}, u32[]{:S(2)}, u32[]{:S(2)}) collective-permute-start(bf16[64,2048]{1,0:T(8,128)(2,1)S(1)} %fusion.47), channel_id=1, source_target_pairs={{0,8},{8,16},{16,24},{24,28},{28,20},{20,12},{12,4},{4,0},{1,9},{9... | collective-permute-start | bytes 786440 | tf_op jit(solution)/shard_map/combine_return/ppermute | solution.py:33
  285.8 41.3 %copy-start.6 = (f32[2048]{0:T(1024)S(1)}, f32[2048]{0:T(1024)}, u32[]{:S(2)}) copy-start(f32[2048]{0:T(1024)} %param.21) | copy-start | bytes 24580
  285.8 8.6 %collective-permute-start.36 = (bf16[64,2048]{1,0:T(8,128)(2,1)S(1)}, bf16[64,2048]{1,0:T(8,128)(2,1)S(1)}, u32[]{:S(2)}, u32[]{:S(2)}) collective-permute-start(bf16[64,2048]{1,0:T(8,128)(2,1)S(1)} %get-tuple-element.7), channel_id=1, source_target_pairs={{0,4},{8,0},{16,8},{24,16},{28,24},{20,28},{12,20},{4,12},{1,5},{9... | collective-permute-start | bytes 786440 | tf_op jit(solution)/shard_map/combine_return/ppermute | solution.py:34
  294.4 6.4 %collective-permute-start.37 = (bf16[64,2048]{1,0:T(8,128)(2,1)S(1)}, bf16[64,2048]{1,0:T(8,128)(2,1)S(1)}, u32[]{:S(2)}, u32[]{:S(2)}) collective-permute-start(bf16[64,2048]{1,0:T(8,128)(2,1)S(1)} %fusion.26), channel_id=1, source_target_pairs={{0,4},{8,0},{16,8},{24,16},{28,24},{20,28},{12,20},{4,12},{1,5},{9... | collective-permute-start | bytes 786440 | tf_op jit(solution)/shard_map/combine_return/ppermute | solution.py:34
  300.8 27.4 %copy-start.1 = (bf16[512,2048]{1,0:T(8,128)(2,1)S(1)}, bf16[512,2048]{1,0:T(8,128)(2,1)}, u32[]{:S(2)}) copy-start(bf16[512,2048]{1,0:T(8,128)(2,1)} %param.15) | copy-start | bytes 6291460
  300.9 6.4 %collective-permute-start.38 = (bf16[64,2048]{1,0:T(8,128)(2,1)S(1)}, bf16[64,2048]{1,0:T(8,128)(2,1)S(1)}, u32[]{:S(2)}, u32[]{:S(2)}) collective-permute-start(bf16[64,2048]{1,0:T(8,128)(2,1)S(1)} %fusion.28), channel_id=1, source_target_pairs={{0,4},{8,0},{16,8},{24,16},{28,24},{20,28},{12,20},{4,12},{1,5},{9... | collective-permute-start | bytes 786440 | tf_op jit(solution)/shard_map/combine_return/ppermute | solution.py:34
  307.4 6.4 %collective-permute-start.39 = (bf16[64,2048]{1,0:T(8,128)(2,1)S(1)}, bf16[64,2048]{1,0:T(8,128)(2,1)S(1)}, u32[]{:S(2)}, u32[]{:S(2)}) collective-permute-start(bf16[64,2048]{1,0:T(8,128)(2,1)S(1)} %fusion.30), channel_id=1, source_target_pairs={{0,4},{8,0},{16,8},{24,16},{28,24},{20,28},{12,20},{4,12},{1,5},{9... | collective-permute-start | bytes 786440 | tf_op jit(solution)/shard_map/combine_return/ppermute | solution.py:34
  313.8 6.4 %collective-permute-start.40 = (bf16[64,2048]{1,0:T(8,128)(2,1)S(1)}, bf16[64,2048]{1,0:T(8,128)(2,1)S(1)}, u32[]{:S(2)}, u32[]{:S(2)}) collective-permute-start(bf16[64,2048]{1,0:T(8,128)(2,1)S(1)} %fusion.32), channel_id=1, source_target_pairs={{0,4},{8,0},{16,8},{24,16},{28,24},{20,28},{12,20},{4,12},{1,5},{9... | collective-permute-start | bytes 786440 | tf_op jit(solution)/shard_map/combine_return/ppermute | solution.py:34
  320.3 6.4 %collective-permute-start.41 = (bf16[64,2048]{1,0:T(8,128)(2,1)S(1)}, bf16[64,2048]{1,0:T(8,128)(2,1)S(1)}, u32[]{:S(2)}, u32[]{:S(2)}) collective-permute-start(bf16[64,2048]{1,0:T(8,128)(2,1)S(1)} %fusion.34), channel_id=1, source_target_pairs={{0,4},{8,0},{16,8},{24,16},{28,24},{20,28},{12,20},{4,12},{1,5},{9... | collective-permute-start | bytes 786440 | tf_op jit(solution)/shard_map/combine_return/ppermute | solution.py:34

commit v4 on v3

--- a/solution.py
+++ b/solution.py
@@ -30,8 +30,14 @@
         if step:
             send_fwd = send_fwd + got_fwd
             send_bwd = send_bwd + got_bwd
-        got_fwd = lax.ppermute(send_fwd.astype(jnp.bfloat16), "ep", forward).astype(jnp.float32)
-        got_bwd = lax.ppermute(send_bwd.astype(jnp.bfloat16), "ep", backward).astype(jnp.float32)
+        send_fwd, send_bwd = lax.optimization_barrier(
+            (send_fwd.astype(jnp.bfloat16), send_bwd.astype(jnp.bfloat16))
+        )
+        got_fwd, got_bwd = lax.optimization_barrier(
+            (lax.ppermute(send_fwd, "ep", forward), lax.ppermute(send_bwd, "ep", backward))
+        )
+        got_fwd = got_fwd.astype(jnp.float32)
+        got_bwd = got_bwd.astype(jnp.float32)
     me = ring_index[pos]
     own = lax.dynamic_index_in_dim(blocks, me, 0, keepdims=False)
     return jnp.concatenate([own[:half] + got_fwd, own[half:] + got_bwd], axis=0)
@@ -48,8 +54,9 @@
     out = lax.dynamic_update_index_in_dim(out, block, ring_index[pos], 0)
     got_fwd, got_bwd = block[:half], block[half:]
     for step in range(n - 1):
-        got_fwd = lax.ppermute(got_fwd, "ep", forward)
-        got_bwd = lax.ppermute(got_bwd, "ep", backward)
+        got_fwd, got_bwd = lax.optimization_barrier(
+            (lax.ppermute(got_fwd, "ep", forward), lax.ppermute(got_bwd, "ep", backward))
+        )
         src_fwd = ring_index[(pos - 1 - step) % n]
         src_bwd = ring_index[(pos + 1 + step) % n]
         out = lax.dynamic_update_slice(out, got_fwd[None], (src_fwd, 0, 0))
@@ -82,6 +89,7 @@
     with jax.named_scope("out_projection"):
         columns = attn_out.reshape(row_count, ep_size, slice_width).transpose(1, 0, 2)
         columns = lax.all_to_all(columns, "ep", split_axis=0, concat_axis=0, tiled=True)
+        columns, row_weights = lax.optimization_barrier((columns, row_weights))
         partial = jnp.dot(
             columns.reshape(group_rows, slice_width), out_weight, preferred_element_type=jnp.float32
         )

time: 330 us -> 264 us (0.80)
  waiting for transfers between devices: 178 us -> 117 us
  starting transfers between devices: 40.4 us -> 54.7 us
  blocking collectives: 14 us -> 0 us
  other arithmetic: 17 us -> 13.3 us
    ppermute x42, waiting for transfers between devices: 168 us -> 105 us  [the longest x14 44.9 us: ring_reduce_scatter(): lax.ppermute(send_fwd, 'ep', forward)]
    all_to_all x1 -> x0, blocking collectives: 14 us -> none  [body(): lax.all_to_all(dense_weight, 'ep', split_axis=0, concat_axis=0, tiled=True)]
    ppermute x42, starting transfers between devices: 33.1 us -> 43.9 us  [the longest x14 14.8 us: ring_reduce_scatter(): lax.ppermute(send_bwd, 'ep', backward)]
    all_to_all x0 -> x1, starting transfers between devices: none -> 7.28 us  [body(): lax.all_to_all(dense_weight, 'ep', split_axis=0, concat_axis=0, tiled=True)]
    convert_element_type x12 -> x0, other arithmetic: 6.89 us -> none  [ring_reduce_scatter(): send_fwd.astype(jnp.bfloat16)]
    all_to_all x0 -> x1, waiting for transfers between devices: none -> 4.19 us  [body(): lax.all_to_all(dense_weight, 'ep', split_axis=0, concat_axis=0, tiled=True)]
    all_to_all x1, starting transfers between devices: 7.28 us -> 3.56 us  [body(): lax.all_to_all(columns, 'ep', split_axis=0, concat_axis=0, tiled=True)]
    convert_element_type x10 -> x12, other arithmetic: 5.72 us -> 8.5 us  [ring_reduce_scatter(): send_bwd.astype(jnp.bfloat16)]
  transfers between devices with their start and end apart: 43 -> 44, of which waited for: 38 -> 43; matrix products, arithmetic and copies ran while one was open for 1% -> 1% of each run, Pallas kernels for 0% -> 0%
where the time goes in v4:
time: 264 us; the launch traced here: 263 us
  waiting for transfers between devices  117 us (44%)
  starting transfers between devices  54.7 us (21%)
  between operations  40.4 us (15%)
  matrix products  29.3 us (11%)
  other arithmetic  13.3 us (5%)
  local copies, waits for them, and re-layouts  8.07 us (3%)
    ppermute x14, waiting for transfers between devices, ring_reduce_scatter(): lax.ppermute(send_fwd, 'ep', forward)  44.9 us
    ppermute x7, waiting for transfers between devices, ring_all_gather(): lax.ppermute(got_fwd, 'ep', forward)  32.4 us
    dot_general x2, matrix products, body(): jnp.dot(normed_all, gate_up[e], preferred_element_type=jnp.float32)  17.3 us
    ppermute x14, waiting for transfers between devices, ring_reduce_scatter(): lax.ppermute(send_bwd, 'ep', backward)  15.6 us
    ppermute x14, starting transfers between devices, ring_reduce_scatter(): lax.ppermute(send_bwd, 'ep', backward)  14.8 us
    ppermute x14, starting transfers between devices, ring_reduce_scatter(): lax.ppermute(send_fwd, 'ep', forward)  14.3 us
    ppermute x7, waiting for transfers between devices, ring_all_gather(): lax.ppermute(got_bwd, 'ep', backward)  11.7 us
    dot_general x2, matrix products, body(): jnp.dot(activated, down[e], preferred_element_type=jnp.float32)  9.63 us
  transfers between devices with their start and end apart: 44, of which 43 were waited for; matrix products, arithmetic and copies ran while one was open for 1% of the time, Pallas kernels for 0%

profile of v4, /device:TPU:0, one launch (start us, length us, event | category | flops | bytes accessed | tf_op | source)
XLA Modules:
  0.0 263.0 jit_solution(3448895327336251970)
XLA Ops:
  0.7 1.5 select_reduce_fusion
  2.1 7.3 %all-to-all-start.1 = ((f32[8,128,2]{1,2,0:T(2,128)}), f32[8,128,2]{1,2,0:T(2,128)S(1)}, u32[]{:S(2)}, u32[]{:S(2)}) async-start(f32[8,128,2]{1,2,0:T(2,128)} %bitcast.2), calls=%async_computation.1 | async-start | bytes 16384 | tf_op jit(solution)/shard_map/route_weights/all_to_all | solution.py:86
  9.4 2.3 copy.24
  11.7 4.2 %all-to-all-done.1 = f32[8,128,2]{1,2,0:T(2,128)S(1)} async-done(((f32[8,128,2]{1,2,0:T(2,128)}), f32[8,128,2]{1,2,0:T(2,128)S(1)}, u32[]{:S(2)}, u32[]{:S(2)}) %all-to-all-start.1) | async-done | bytes 8224 | tf_op jit(solution)/shard_map/route_weights/all_to_all | solution.py:86
  15.9 3.6 %all-to-all-start = ((bf16[8,128,512]{2,1,0:T(8,128)(2,1)}), bf16[8,128,512]{2,1,0:T(8,128)(2,1)S(1)}, u32[]{:S(2)}, u32[]{:S(2)}) async-start(bf16[8,128,512]{2,1,0:T(8,128)(2,1)} %bitcast.246), calls=%async_computation | async-start | bytes 2097152 | tf_op jit(solution)/shard_map/out_projection/all_to_all | solution.py:91
  35.8 8.4 %all-to-all-done = bf16[8,128,512]{2,1,0:T(8,128)(2,1)S(1)} async-done(((bf16[8,128,512]{2,1,0:T(8,128)(2,1)}), bf16[8,128,512]{2,1,0:T(8,128)(2,1)S(1)}, u32[]{:S(2)}, u32[]{:S(2)}) %all-to-all-start) | async-done | bytes 1048608 | tf_op jit(solution)/shard_map/out_projection/all_to_all | solution.py:91
  44.2 2.4 fusion.13
  46.6 3.3 %copy-done.2 = f32[8,128,2048]{2,1,0:T(8,128)} copy-done((f32[8,128,2048]{2,1,0:T(8,128)}, f32[8,128,2048]{2,1,0:T(8,128)S(1)}, u32[]{:S(2)}) %copy-start.2) | copy-done | bytes 8388632
  50.1 2.0 collective-permute-start.1
  56.6 1.3 fusion.61
  58.5 1.5 collective-permute-start.3
  64.4 2.1 collective-permute-done.3
  66.5 1.3 fusion.59
  67.8 1.8 collective-permute-start.4
  74.2 1.8 collective-permute-done.5
  76.0 1.3 fusion.57
  77.3 1.8 collective-permute-start.6
  83.7 1.9 collective-permute-done.7
  85.6 1.3 fusion.55
  87.5 1.5 collective-permute-start.9
  92.4 2.2 collective-permute-done.8
  95.2 1.3 fusion.53
  97.1 1.5 collective-permute-start.11
  102.4 3.1 %collective-permute-done.10 = bf16[64,2048]{1,0:T(8,128)(2,1)S(1)} collective-permute-done((bf16[64,2048]{1,0:T(8,128)(2,1)S(1)}, bf16[64,2048]{1,0:T(8,128)(2,1)S(1)}, u32[]{:S(2)}, u32[]{:S(2)}) %collective-permute-start.10) | collective-permute-done | bytes 262176 | tf_op jit(solution)/shard_map/out_projection/ppermute | solution.py:37
  111.5 3.8 %collective-permute-done.12 = bf16[64,2048]{1,0:T(8,128)(2,1)S(1)} collective-permute-done((bf16[64,2048]{1,0:T(8,128)(2,1)S(1)}, bf16[64,2048]{1,0:T(8,128)(2,1)S(1)}, u32[]{:S(2)}, u32[]{:S(2)}) %collective-permute-start.12) | collective-permute-done | bytes 262176 | tf_op jit(solution)/shard_map/out_projection/ppermute | solution.py:37
  115.3 1.7 collective-permute-done.13
  117.0 1.3 fusion.74
  119.4 1.5 collective-permute-start.15
  121.5 4.6 %collective-permute-done.15 = bf16[64,2048]{1,0:T(8,128)(2,1)S(1)} collective-permute-done((bf16[64,2048]{1,0:T(8,128)(2,1)S(1)}, bf16[64,2048]{1,0:T(8,128)(2,1)S(1)}, u32[]{:S(2)}, u32[]{:S(2)}) %collective-permute-start.15) | collective-permute-done | bytes 262176 | tf_op jit(solution)/shard_map/dispatch_gather/ppermute | solution.py:58
  126.1 3.1 %collective-permute-done.14 = bf16[64,2048]{1,0:T(8,128)(2,1)S(1)} collective-permute-done((bf16[64,2048]{1,0:T(8,128)(2,1)S(1)}, bf16[64,2048]{1,0:T(8,128)(2,1)S(1)}, u32[]{:S(2)}, u32[]{:S(2)}) %collective-permute-start.14) | collective-permute-done | bytes 262176 | tf_op jit(solution)/shard_map/dispatch_gather/ppermute | solution.py:58
  131.4 6.7 %collective-permute-done.16 = bf16[64,2048]{1,0:T(8,128)(2,1)S(1)} collective-permute-done((bf16[64,2048]{1,0:T(8,128)(2,1)S(1)}, bf16[64,2048]{1,0:T(8,128)(2,1)S(1)}, u32[]{:S(2)}, u32[]{:S(2)}) %collective-permute-start.16) | collective-permute-done | bytes 262176 | tf_op jit(solution)/shard_map/dispatch_gather/ppermute | solution.py:58
  138.5 1.3 collective-permute-start.18
  140.6 5.6 %collective-permute-done.18 = bf16[64,2048]{1,0:T(8,128)(2,1)S(1)} collective-permute-done((bf16[64,2048]{1,0:T(8,128)(2,1)S(1)}, bf16[64,2048]{1,0:T(8,128)(2,1)S(1)}, u32[]{:S(2)}, u32[]{:S(2)}) %collective-permute-start.18) | collective-permute-done | bytes 262176 | tf_op jit(solution)/shard_map/dispatch_gather/ppermute | solution.py:58
  149.4 4.4 %collective-permute-done.20 = bf16[64,2048]{1,0:T(8,128)(2,1)S(1)} collective-permute-done((bf16[64,2048]{1,0:T(8,128)(2,1)S(1)}, bf16[64,2048]{1,0:T(8,128)(2,1)S(1)}, u32[]{:S(2)}, u32[]{:S(2)}) %collective-permute-start.20) | collective-permute-done | bytes 262176 | tf_op jit(solution)/shard_map/dispatch_gather/ppermute | solution.py:58
  153.8 1.6 collective-permute-done.21
  156.1 1.4 collective-permute-start.23
  157.6 4.2 %collective-permute-done.22 = bf16[64,2048]{1,0:T(8,128)(2,1)S(1)} collective-permute-done((bf16[64,2048]{1,0:T(8,128)(2,1)S(1)}, bf16[64,2048]{1,0:T(8,128)(2,1)S(1)}, u32[]{:S(2)}, u32[]{:S(2)}) %collective-permute-start.22) | collective-permute-done | bytes 262176 | tf_op jit(solution)/shard_map/dispatch_gather/ppermute | solution.py:58
  162.6 1.5 collective-permute-start.24
  164.7 4.2 %collective-permute-done.24 = bf16[64,2048]{1,0:T(8,128)(2,1)S(1)} collective-permute-done((bf16[64,2048]{1,0:T(8,128)(2,1)S(1)}, bf16[64,2048]{1,0:T(8,128)(2,1)S(1)}, u32[]{:S(2)}, u32[]{:S(2)}) %collective-permute-start.24) | collective-permute-done | bytes 262176 | tf_op jit(solution)/shard_map/dispatch_gather/ppermute | solution.py:58
  168.9 1.5 collective-permute-done.25
  170.5 1.4 collective-permute-start.26
  172.8 4.1 %collective-permute-done.26 = bf16[64,2048]{1,0:T(8,128)(2,1)S(1)} collective-permute-done((bf16[64,2048]{1,0:T(8,128)(2,1)S(1)}, bf16[64,2048]{1,0:T(8,128)(2,1)S(1)}, u32[]{:S(2)}, u32[]{:S(2)}) %collective-permute-start.26) | collective-permute-done | bytes 262176 | tf_op jit(solution)/shard_map/dispatch_gather/ppermute | solution.py:58
  176.9 1.7 collective-permute-done.27
  178.6 10.6 %fusion = f32[1024,1536]{1,0:T(8,128)} fusion(bf16[1024,2048]{1,0:T(8,128)(2,1)S(1)} %bitcast.255, bf16[2,2048,1536]{2,1,0:T(8,128)(2,1)} %param.17), kind=kOutput, calls=%fused_computation.1 | convolution fusion | flops 6442450944 | bytes 16777216 | tf_op jit(solution)/shard_map/local_experts/dot_general | solution.py:107
  189.3 6.7 %fusion.2 = f32[1024,1536]{1,0:T(8,128)S(1)} fusion(bf16[1024,2048]{1,0:T(8,128)(2,1)S(1)} %bitcast.256, bf16[2,2048,1536]{2,1,0:T(8,128)(2,1)S(1)} %bitcast.262), kind=kOutput, calls=%fused_computation.3 | convolution fusion | flops 6442450944 | bytes 16777216 | tf_op jit(solution)/shard_map/local_experts/dot_general | solution.py:107
  196.0 3.7 %fusion.9 = bf16[1024,2048]{1,0:T(8,128)(2,1)S(1)} fusion(bf16[2,768,2048]{2,1,0:T(8,128)(2,1)S(1)} %bitcast.264, f32[1024,1536]{1,0:T(8,128)S(1)} %fusion.2), kind=kOutput, calls=%fused_computation.12 | convolution fusion | flops 3225944064 | bytes 13631488 | tf_op jit(solution)/shard_map/local_experts/dot_general | solution.py:111
  199.7 5.9 %multiply_add_fusion = f32[1024,2048]{1,0:T(8,128)S(1)} fusion(f32[1024]{0:T(1024)S(1)} %bitcast.260, bf16[1024,2048]{1,0:T(8,128)(2,1)S(1)} %fusion.9, f32[1024]{0:T(1024)S(1)} %bitcast.259, bf16[2,768,2048]{2,1,0:T(8,128)(2,1)S(1)} %bitcast.264, f32[1024,1536]{1,0:T(8,128)} %fusion), kind=kOutput, calls=%fused_computation | convolution fusion | flops 3238526976 | bytes 22028288 | tf_op jit(solution)/shard_map/local_experts/dot_general | solution.py:111
  206.3 1.5 collective-permute-start.29
  207.8 5.8 %collective-permute-done.28 = bf16[64,2048]{1,0:T(8,128)(2,1)S(1)} collective-permute-done((bf16[64,2048]{1,0:T(8,128)(2,1)S(1)}, bf16[64,2048]{1,0:T(8,128)(2,1)S(1)}, u32[]{:S(2)}, u32[]{:S(2)}) %collective-permute-start.28) | collective-permute-done | bytes 262176 | tf_op jit(solution)/shard_map/combine_return/ppermute | solution.py:37
  214.2 1.6 collective-permute-start.31
  215.8 5.7 %collective-permute-done.30 = bf16[64,2048]{1,0:T(8,128)(2,1)S(1)} collective-permute-done((bf16[64,2048]{1,0:T(8,128)(2,1)S(1)}, bf16[64,2048]{1,0:T(8,128)(2,1)S(1)}, u32[]{:S(2)}, u32[]{:S(2)}) %collective-permute-start.30) | collective-permute-done | bytes 262176 | tf_op jit(solution)/shard_map/combine_return/ppermute | solution.py:37
  221.7 2.1 collective-permute-start.32
  223.9 4.7 %collective-permute-done.32 = bf16[64,2048]{1,0:T(8,128)(2,1)S(1)} collective-permute-done((bf16[64,2048]{1,0:T(8,128)(2,1)S(1)}, bf16[64,2048]{1,0:T(8,128)(2,1)S(1)}, u32[]{:S(2)}, u32[]{:S(2)}) %collective-permute-start.32) | collective-permute-done | bytes 262176 | tf_op jit(solution)/shard_map/combine_return/ppermute | solution.py:37
  228.6 1.9 collective-permute-done.33
  230.6 1.8 collective-permute-start.34
  232.7 4.3 %collective-permute-done.34 = bf16[64,2048]{1,0:T(8,128)(2,1)S(1)} collective-permute-done((bf16[64,2048]{1,0:T(8,128)(2,1)S(1)}, bf16[64,2048]{1,0:T(8,128)(2,1)S(1)}, u32[]{:S(2)}, u32[]{:S(2)}) %collective-permute-start.34) | collective-permute-done | bytes 262176 | tf_op jit(solution)/shard_map/combine_return/ppermute | solution.py:37
  237.0 1.7 collective-permute-done.35
  239.5 1.4 collective-permute-start.37
  241.0 4.3 %collective-permute-done.36 = bf16[64,2048]{1,0:T(8,128)(2,1)S(1)} collective-permute-done((bf16[64,2048]{1,0:T(8,128)(2,1)S(1)}, bf16[64,2048]{1,0:T(8,128)(2,1)S(1)}, u32[]{:S(2)}, u32[]{:S(2)}) %collective-permute-start.36) | collective-permute-done | bytes 262176 | tf_op jit(solution)/shard_map/combine_return/ppermute | solution.py:37
  246.1 1.8 collective-permute-start.38
  248.1 4.3 %collective-permute-done.38 = bf16[64,2048]{1,0:T(8,128)(2,1)S(1)} collective-permute-done((bf16[64,2048]{1,0:T(8,128)(2,1)S(1)}, bf16[64,2048]{1,0:T(8,128)(2,1)S(1)}, u32[]{:S(2)}, u32[]{:S(2)}) %collective-permute-start.38) | collective-permute-done | bytes 262176 | tf_op jit(solution)/shard_map/combine_return/ppermute | solution.py:37
  252.5 1.7 collective-permute-done.39
  255.0 1.4 collective-permute-start.41
  256.4 4.3 %collective-permute-done.40 = bf16[64,2048]{1,0:T(8,128)(2,1)S(1)} collective-permute-done((bf16[64,2048]{1,0:T(8,128)(2,1)S(1)}, bf16[64,2048]{1,0:T(8,128)(2,1)S(1)}, u32[]{:S(2)}, u32[]{:S(2)}) %collective-permute-start.40) | collective-permute-done | bytes 262176 | tf_op jit(solution)/shard_map/combine_return/ppermute | solution.py:37
  (100 shorter events, 28.7 us)
Async XLA Ops:
  0.6 43.6 %copy-start = (bf16[512,2048]{1,0:T(8,128)(2,1)S(1)}, bf16[512,2048]{1,0:T(8,128)(2,1)}, u32[]{:S(2)}) copy-start(bf16[512,2048]{1,0:T(8,128)(2,1)} %param.15) | copy-start | bytes 6291460
  0.6 18.9 %copy-start.7 = (s32[8]{0:T(128)S(1)}, s32[8]{0:T(128)}, u32[]{:S(2)}) copy-start(s32[8]{0:T(128)} %constant.252.clone) | copy-start | bytes 100
  0.7 30.7 %copy-start.4 = (s32[8]{0:T(128)S(1)}, s32[8]{0:T(128)}, u32[]{:S(2)}) copy-start(s32[8]{0:T(128)} %constant.253.clone) | copy-start | bytes 100
  2.1 13.8 %all-to-all-start.1 = ((f32[8,128,2]{1,2,0:T(2,128)}), f32[8,128,2]{1,2,0:T(2,128)S(1)}, u32[]{:S(2)}, u32[]{:S(2)}) async-start(f32[8,128,2]{1,2,0:T(2,128)} %bitcast.2), calls=%async_computation.1 | async-start | bytes 16384 | tf_op jit(solution)/shard_map/route_weights/all_to_all | solution.py:86
  15.9 28.3 %all-to-all-start = ((bf16[8,128,512]{2,1,0:T(8,128)(2,1)}), bf16[8,128,512]{2,1,0:T(8,128)(2,1)S(1)}, u32[]{:S(2)}, u32[]{:S(2)}) async-start(bf16[8,128,512]{2,1,0:T(8,128)(2,1)} %bitcast.246), calls=%async_computation | async-start | bytes 2097152 | tf_op jit(solution)/shard_map/out_projection/all_to_all | solution.py:91
  46.6 3.3 %copy-start.2 = (f32[8,128,2048]{2,1,0:T(8,128)}, f32[8,128,2048]{2,1,0:T(8,128)S(1)}, u32[]{:S(2)}) copy-start(f32[8,128,2048]{2,1,0:T(8,128)S(1)} %fusion.13) | copy-start | bytes 25165828
  50.0 6.6 %collective-permute-start = (bf16[64,2048]{1,0:T(8,128)(2,1)S(1)}, bf16[64,2048]{1,0:T(8,128)(2,1)S(1)}, u32[]{:S(2)}, u32[]{:S(2)}) collective-permute-start(bf16[64,2048]{1,0:T(8,128)(2,1)S(1)} %get-tuple-element.75), channel_id=1, source_target_pairs={{0,8},{8,16},{16,24},{24,28},{28,20},{20,12},{12,4},{4,0},{1,9},{9... | collective-permute-start | bytes 786440 | tf_op jit(solution)/shard_map/out_projection/ppermute | solution.py:37
  50.1 6.6 %collective-permute-start.1 = (bf16[64,2048]{1,0:T(8,128)(2,1)S(1)}, bf16[64,2048]{1,0:T(8,128)(2,1)S(1)}, u32[]{:S(2)}, u32[]{:S(2)}) collective-permute-start(bf16[64,2048]{1,0:T(8,128)(2,1)S(1)} %get-tuple-element.76), channel_id=1, source_target_pairs={{0,4},{8,0},{16,8},{24,16},{28,24},{20,28},{12,20},{4,12},{1,5},{9... | collective-permute-start | bytes 786440 | tf_op jit(solution)/shard_map/out_projection/ppermute | solution.py:37
  57.9 6.4 %collective-permute-start.2 = (bf16[64,2048]{1,0:T(8,128)(2,1)S(1)}, bf16[64,2048]{1,0:T(8,128)(2,1)S(1)}, u32[]{:S(2)}, u32[]{:S(2)}) collective-permute-start(bf16[64,2048]{1,0:T(8,128)(2,1)S(1)} %get-tuple-element.79), channel_id=1, source_target_pairs={{0,8},{8,16},{16,24},{24,28},{28,20},{20,12},{12,4},{4,0},{1,9},{9... | collective-permute-start | bytes 786440 | tf_op jit(solution)/shard_map/out_projection/ppermute | solution.py:37
  58.5 7.9 %collective-permute-start.3 = (bf16[64,2048]{1,0:T(8,128)(2,1)S(1)}, bf16[64,2048]{1,0:T(8,128)(2,1)S(1)}, u32[]{:S(2)}, u32[]{:S(2)}) collective-permute-start(bf16[64,2048]{1,0:T(8,128)(2,1)S(1)} %get-tuple-element.80), channel_id=1, source_target_pairs={{0,4},{8,0},{16,8},{24,16},{28,24},{20,28},{12,20},{4,12},{1,5},{9... | collective-permute-start | bytes 786440 | tf_op jit(solution)/shard_map/out_projection/ppermute | solution.py:37
  67.8 6.4 %collective-permute-start.4 = (bf16[64,2048]{1,0:T(8,128)(2,1)S(1)}, bf16[64,2048]{1,0:T(8,128)(2,1)S(1)}, u32[]{:S(2)}, u32[]{:S(2)}) collective-permute-start(bf16[64,2048]{1,0:T(8,128)(2,1)S(1)} %get-tuple-element.83), channel_id=1, source_target_pairs={{0,8},{8,16},{16,24},{24,28},{28,20},{20,12},{12,4},{4,0},{1,9},{9... | collective-permute-start | bytes 786440 | tf_op jit(solution)/shard_map/out_projection/ppermute | solution.py:37
  69.6 6.4 %collective-permute-start.5 = (bf16[64,2048]{1,0:T(8,128)(2,1)S(1)}, bf16[64,2048]{1,0:T(8,128)(2,1)S(1)}, u32[]{:S(2)}, u32[]{:S(2)}) collective-permute-start(bf16[64,2048]{1,0:T(8,128)(2,1)S(1)} %get-tuple-element.84), channel_id=1, source_target_pairs={{0,4},{8,0},{16,8},{24,16},{28,24},{20,28},{12,20},{4,12},{1,5},{9... | collective-permute-start | bytes 786440 | tf_op jit(solution)/shard_map/out_projection/ppermute | solution.py:37
  77.3 6.4 %collective-permute-start.6 = (bf16[64,2048]{1,0:T(8,128)(2,1)S(1)}, bf16[64,2048]{1,0:T(8,128)(2,1)S(1)}, u32[]{:S(2)}, u32[]{:S(2)}) collective-permute-start(bf16[64,2048]{1,0:T(8,128)(2,1)S(1)} %get-tuple-element.87), channel_id=1, source_target_pairs={{0,8},{8,16},{16,24},{24,28},{28,20},{20,12},{12,4},{4,0},{1,9},{9... | collective-permute-start | bytes 786440 | tf_op jit(solution)/shard_map/out_projection/ppermute | solution.py:37
  79.0 6.6 %collective-permute-start.7 = (bf16[64,2048]{1,0:T(8,128)(2,1)S(1)}, bf16[64,2048]{1,0:T(8,128)(2,1)S(1)}, u32[]{:S(2)}, u32[]{:S(2)}) collective-permute-start(bf16[64,2048]{1,0:T(8,128)(2,1)S(1)} %get-tuple-element.88), channel_id=1, source_target_pairs={{0,4},{8,0},{16,8},{24,16},{28,24},{20,28},{12,20},{4,12},{1,5},{9... | collective-permute-start | bytes 786440 | tf_op jit(solution)/shard_map/out_projection/ppermute | solution.py:37
  83.3 35.0 %copy-start.3 = (bf16[128,2048]{1,0:T(8,128)(2,1)S(1)}, bf16[128,2048]{1,0:T(8,128)(2,1)}, u32[]{:S(2)}) copy-start(bf16[128,2048]{1,0:T(8,128)(2,1)} %param.13) | copy-start | bytes 1572868
  86.9 7.7 %collective-permute-start.8 = (bf16[64,2048]{1,0:T(8,128)(2,1)S(1)}, bf16[64,2048]{1,0:T(8,128)(2,1)S(1)}, u32[]{:S(2)}, u32[]{:S(2)}) collective-permute-start(bf16[64,2048]{1,0:T(8,128)(2,1)S(1)} %get-tuple-element.91), channel_id=1, source_target_pairs={{0,8},{8,16},{16,24},{24,28},{28,20},{20,12},{12,4},{4,0},{1,9},{9... | collective-permute-start | bytes 786440 | tf_op jit(solution)/shard_map/out_projection/ppermute | solution.py:37
  87.5 7.8 %collective-permute-start.9 = (bf16[64,2048]{1,0:T(8,128)(2,1)S(1)}, bf16[64,2048]{1,0:T(8,128)(2,1)S(1)}, u32[]{:S(2)}, u32[]{:S(2)}) collective-permute-start(bf16[64,2048]{1,0:T(8,128)(2,1)S(1)} %get-tuple-element.92), channel_id=1, source_target_pairs={{0,4},{8,0},{16,8},{24,16},{28,24},{20,28},{12,20},{4,12},{1,5},{9... | collective-permute-start | bytes 786440 | tf_op jit(solution)/shard_map/out_projection/ppermute | solution.py:37
  96.5 9.0 %collective-permute-start.10 = (bf16[64,2048]{1,0:T(8,128)(2,1)S(1)}, bf16[64,2048]{1,0:T(8,128)(2,1)S(1)}, u32[]{:S(2)}, u32[]{:S(2)}) collective-permute-start(bf16[64,2048]{1,0:T(8,128)(2,1)S(1)} %get-tuple-element.95), channel_id=1, source_target_pairs={{0,8},{8,16},{16,24},{24,28},{28,20},{20,12},{12,4},{4,0},{1,9},{9... | collective-permute-start | bytes 786440 | tf_op jit(solution)/shard_map/out_projection/ppermute | solution.py:37
  97.1 9.2 %collective-permute-start.11 = (bf16[64,2048]{1,0:T(8,128)(2,1)S(1)}, bf16[64,2048]{1,0:T(8,128)(2,1)S(1)}, u32[]{:S(2)}, u32[]{:S(2)}) collective-permute-start(bf16[64,2048]{1,0:T(8,128)(2,1)S(1)} %get-tuple-element.96), channel_id=1, source_target_pairs={{0,4},{8,0},{16,8},{24,16},{28,24},{20,28},{12,20},{4,12},{1,5},{9... | collective-permute-start | bytes 786440 | tf_op jit(solution)/shard_map/out_projection/ppermute | solution.py:37
  107.6 7.8 %collective-permute-start.12 = (bf16[64,2048]{1,0:T(8,128)(2,1)S(1)}, bf16[64,2048]{1,0:T(8,128)(2,1)S(1)}, u32[]{:S(2)}, u32[]{:S(2)}) collective-permute-start(bf16[64,2048]{1,0:T(8,128)(2,1)S(1)} %get-tuple-element.99), channel_id=1, source_target_pairs={{0,8},{8,16},{16,24},{24,28},{28,20},{20,12},{12,4},{4,0},{1,9},{9... | collective-permute-start | bytes 786440 | tf_op jit(solution)/shard_map/out_projection/ppermute | solution.py:37
  108.5 8.6 %collective-permute-start.13 = (bf16[64,2048]{1,0:T(8,128)(2,1)S(1)}, bf16[64,2048]{1,0:T(8,128)(2,1)S(1)}, u32[]{:S(2)}, u32[]{:S(2)}) collective-permute-start(bf16[64,2048]{1,0:T(8,128)(2,1)S(1)} %get-tuple-element.100), channel_id=1, source_target_pairs={{0,4},{8,0},{16,8},{24,16},{28,24},{20,28},{12,20},{4,12},{1,5},{9... | collective-permute-start | bytes 786440 | tf_op jit(solution)/shard_map/out_projection/ppermute | solution.py:37
  111.5 7.6 %copy-start.5 = (f32[2048]{0:T(1024)S(1)}, f32[2048]{0:T(1024)}, u32[]{:S(2)}) copy-start(f32[2048]{0:T(1024)} %param.16) | copy-start | bytes 24580
  119.4 6.7 %collective-permute-start.15 = (bf16[64,2048]{1,0:T(8,128)(2,1)S(1)}, bf16[64,2048]{1,0:T(8,128)(2,1)S(1)}, u32[]{:S(2)}, u32[]{:S(2)}) collective-permute-start(bf16[64,2048]{1,0:T(8,128)(2,1)S(1)} %get-tuple-element.184), channel_id=1, source_target_pairs={{0,4},{8,0},{16,8},{24,16},{28,24},{20,28},{12,20},{4,12},{1,5},{9... | collective-permute-start | bytes 786440 | tf_op jit(solution)/shard_map/dispatch_gather/ppermute | solution.py:58
  120.9 8.3 %collective-permute-start.14 = (bf16[64,2048]{1,0:T(8,128)(2,1)S(1)}, bf16[64,2048]{1,0:T(8,128)(2,1)S(1)}, u32[]{:S(2)}, u32[]{:S(2)}) collective-permute-start(bf16[64,2048]{1,0:T(8,128)(2,1)S(1)} %get-tuple-element.185), channel_id=1, source_target_pairs={{0,8},{8,16},{16,24},{24,28},{28,20},{20,12},{12,4},{4,0},{1,9},{9... | collective-permute-start | bytes 786440 | tf_op jit(solution)/shard_map/dispatch_gather/ppermute | solution.py:58
  129.3 8.9 %collective-permute-start.16 = (bf16[64,2048]{1,0:T(8,128)(2,1)S(1)}, bf16[64,2048]{1,0:T(8,128)(2,1)S(1)}, u32[]{:S(2)}, u32[]{:S(2)}) collective-permute-start(bf16[64,2048]{1,0:T(8,128)(2,1)S(1)} %collective-permute-done.14), channel_id=1, source_target_pairs={{0,8},{8,16},{16,24},{24,28},{28,20},{20,12},{12,4},{4,0},{1,9},{9... | collective-permute-start | bytes 786440 | tf_op jit(solution)/shard_map/dispatch_gather/ppermute | solution.py:58
  130.1 8.3 %collective-permute-start.17 = (bf16[64,2048]{1,0:T(8,128)(2,1)S(1)}, bf16[64,2048]{1,0:T(8,128)(2,1)S(1)}, u32[]{:S(2)}, u32[]{:S(2)}) collective-permute-start(bf16[64,2048]{1,0:T(8,128)(2,1)S(1)} %collective-permute-done.15), channel_id=1, source_target_pairs={{0,4},{8,0},{16,8},{24,16},{28,24},{20,28},{12,20},{4,12},{1,5},{9... | collective-permute-start | bytes 786440 | tf_op jit(solution)/shard_map/dispatch_gather/ppermute | solution.py:58
  138.5 7.7 %collective-permute-start.18 = (bf16[64,2048]{1,0:T(8,128)(2,1)S(1)}, bf16[64,2048]{1,0:T(8,128)(2,1)S(1)}, u32[]{:S(2)}, u32[]{:S(2)}) collective-permute-start(bf16[64,2048]{1,0:T(8,128)(2,1)S(1)} %collective-permute-done.16), channel_id=1, source_target_pairs={{0,8},{8,16},{16,24},{24,28},{28,20},{20,12},{12,4},{4,0},{1,9},{9... | collective-permute-start | bytes 786440 | tf_op jit(solution)/shard_map/dispatch_gather/ppermute | solution.py:58
  139.8 7.5 %collective-permute-start.19 = (bf16[64,2048]{1,0:T(8,128)(2,1)S(1)}, bf16[64,2048]{1,0:T(8,128)(2,1)S(1)}, u32[]{:S(2)}, u32[]{:S(2)}) collective-permute-start(bf16[64,2048]{1,0:T(8,128)(2,1)S(1)} %collective-permute-done.17), channel_id=1, source_target_pairs={{0,4},{8,0},{16,8},{24,16},{28,24},{20,28},{12,20},{4,12},{1,5},{9... | collective-permute-start | bytes 786440 | tf_op jit(solution)/shard_map/dispatch_gather/ppermute | solution.py:58
  147.3 6.5 %collective-permute-start.20 = (bf16[64,2048]{1,0:T(8,128)(2,1)S(1)}, bf16[64,2048]{1,0:T(8,128)(2,1)S(1)}, u32[]{:S(2)}, u32[]{:S(2)}) collective-permute-start(bf16[64,2048]{1,0:T(8,128)(2,1)S(1)} %collective-permute-done.18), channel_id=1, source_target_pairs={{0,8},{8,16},{16,24},{24,28},{28,20},{20,12},{12,4},{4,0},{1,9},{9... | collective-permute-start | bytes 786440 | tf_op jit(solution)/shard_map/dispatch_gather/ppermute | solution.py:58
  148.3 7.1 %collective-permute-start.21 = (bf16[64,2048]{1,0:T(8,128)(2,1)S(1)}, bf16[64,2048]{1,0:T(8,128)(2,1)S(1)}, u32[]{:S(2)}, u32[]{:S(2)}) collective-permute-start(bf16[64,2048]{1,0:T(8,128)(2,1)S(1)} %collective-permute-done.19), channel_id=1, source_target_pairs={{0,4},{8,0},{16,8},{24,16},{28,24},{20,28},{12,20},{4,12},{1,5},{9... | collective-permute-start | bytes 786440 | tf_op jit(solution)/shard_map/dispatch_gather/ppermute | solution.py:58
  155.4 6.4 %collective-permute-start.22 = (bf16[64,2048]{1,0:T(8,128)(2,1)S(1)}, bf16[64,2048]{1,0:T(8,128)(2,1)S(1)}, u32[]{:S(2)}, u32[]{:S(2)}) collective-permute-start(bf16[64,2048]{1,0:T(8,128)(2,1)S(1)} %collective-permute-done.20), channel_id=1, source_target_pairs={{0,8},{8,16},{16,24},{24,28},{28,20},{20,12},{12,4},{4,0},{1,9},{9... | collective-permute-start | bytes 786440 | tf_op jit(solution)/shard_map/dispatch_gather/ppermute | solution.py:58
  156.1 6.5 %collective-permute-start.23 = (bf16[64,2048]{1,0:T(8,128)(2,1)S(1)}, bf16[64,2048]{1,0:T(8,128)(2,1)S(1)}, u32[]{:S(2)}, u32[]{:S(2)}) collective-permute-start(bf16[64,2048]{1,0:T(8,128)(2,1)S(1)} %collective-permute-done.21), channel_id=1, source_target_pairs={{0,4},{8,0},{16,8},{24,16},{28,24},{20,28},{12,20},{4,12},{1,5},{9... | collective-permute-start | bytes 786440 | tf_op jit(solution)/shard_map/dispatch_gather/ppermute | solution.py:58
  162.6 6.4 %collective-permute-start.24 = (bf16[64,2048]{1,0:T(8,128)(2,1)S(1)}, bf16[64,2048]{1,0:T(8,128)(2,1)S(1)}, u32[]{:S(2)}, u32[]{:S(2)}) collective-permute-start(bf16[64,2048]{1,0:T(8,128)(2,1)S(1)} %collective-permute-done.22), channel_id=1, source_target_pairs={{0,8},{8,16},{16,24},{24,28},{28,20},{20,12},{12,4},{4,0},{1,9},{9... | collective-permute-start | bytes 786440 | tf_op jit(solution)/shard_map/dispatch_gather/ppermute | solution.py:58
  164.1 6.4 %collective-permute-start.25 = (bf16[64,2048]{1,0:T(8,128)(2,1)S(1)}, bf16[64,2048]{1,0:T(8,128)(2,1)S(1)}, u32[]{:S(2)}, u32[]{:S(2)}) collective-permute-start(bf16[64,2048]{1,0:T(8,128)(2,1)S(1)} %collective-permute-done.23), channel_id=1, source_target_pairs={{0,4},{8,0},{16,8},{24,16},{28,24},{20,28},{12,20},{4,12},{1,5},{9... | collective-permute-start | bytes 786440 | tf_op jit(solution)/shard_map/dispatch_gather/ppermute | solution.py:58
  170.5 6.4 %collective-permute-start.26 = (bf16[64,2048]{1,0:T(8,128)(2,1)S(1)}, bf16[64,2048]{1,0:T(8,128)(2,1)S(1)}, u32[]{:S(2)}, u32[]{:S(2)}) collective-permute-start(bf16[64,2048]{1,0:T(8,128)(2,1)S(1)} %collective-permute-done.24), channel_id=1, source_target_pairs={{0,8},{8,16},{16,24},{24,28},{28,20},{20,12},{12,4},{4,0},{1,9},{9... | collective-permute-start | bytes 786440 | tf_op jit(solution)/shard_map/dispatch_gather/ppermute | solution.py:58
  171.9 6.6 %collective-permute-start.27 = (bf16[64,2048]{1,0:T(8,128)(2,1)S(1)}, bf16[64,2048]{1,0:T(8,128)(2,1)S(1)}, u32[]{:S(2)}, u32[]{:S(2)}) collective-permute-start(bf16[64,2048]{1,0:T(8,128)(2,1)S(1)} %collective-permute-done.25), channel_id=1, source_target_pairs={{0,4},{8,0},{16,8},{24,16},{28,24},{20,28},{12,20},{4,12},{1,5},{9... | collective-permute-start | bytes 786440 | tf_op jit(solution)/shard_map/dispatch_gather/ppermute | solution.py:58
  178.5 10.7 %slice-start = ((s8[12582912]{0:T(1024)(128)(4,1)}), s8[4194304]{0:T(1024)(128)(4,1)S(1)}, s32[]{:S(2)}) async-start(s8[12582912]{0:T(1024)(128)(4,1)} %bitcast.261), calls=%async_computation.2 | async-start | bytes 8388608
  178.6 10.7 %slice-start.1 = ((s8[12582912]{0:T(1024)(128)(4,1)}), s8[4194304]{0:T(1024)(128)(4,1)S(1)}, s32[]{:S(2)}) async-start(s8[12582912]{0:T(1024)(128)(4,1)} %bitcast.261), calls=%async_computation.3 | async-start | bytes 8388608
  178.6 10.7 %slice-start.2 = ((s8[12582912]{0:T(1024)(128)(4,1)}), s8[4194304]{0:T(1024)(128)(4,1)S(1)}, s32[]{:S(2)}) async-start(s8[12582912]{0:T(1024)(128)(4,1)} %bitcast.261), calls=%async_computation.4 | async-start | bytes 8388608
  178.6 17.3 %slice-start.3 = ((s8[6291456]{0:T(1024)(128)(4,1)}), s8[4194304]{0:T(1024)(128)(4,1)S(1)}, s32[]{:S(2)}) async-start(s8[6291456]{0:T(1024)(128)(4,1)} %bitcast.263), calls=%async_computation.5 | async-start | bytes 8388608
  189.3 6.7 %slice-start.4 = ((s8[6291456]{0:T(1024)(128)(4,1)}), s8[2097152]{0:T(1024)(128)(4,1)S(1)}, s32[]{:S(2)}) async-start(s8[6291456]{0:T(1024)(128)(4,1)} %bitcast.263), calls=%async_computation.6 | async-start | bytes 4194304
  205.7 7.8 %collective-permute-start.28 = (bf16[64,2048]{1,0:T(8,128)(2,1)S(1)}, bf16[64,2048]{1,0:T(8,128)(2,1)S(1)}, u32[]{:S(2)}, u32[]{:S(2)}) collective-permute-start(bf16[64,2048]{1,0:T(8,128)(2,1)S(1)} %get-tuple-element.118), channel_id=1, source_target_pairs={{0,8},{8,16},{16,24},{24,28},{28,20},{20,12},{12,4},{4,0},{1,9},{9... | collective-permute-start | bytes 786440 | tf_op jit(solution)/shard_map/combine_return/ppermute | solution.py:37
  206.3 7.3 %collective-permute-start.29 = (bf16[64,2048]{1,0:T(8,128)(2,1)S(1)}, bf16[64,2048]{1,0:T(8,128)(2,1)S(1)}, u32[]{:S(2)}, u32[]{:S(2)}) collective-permute-start(bf16[64,2048]{1,0:T(8,128)(2,1)S(1)} %get-tuple-element.119), channel_id=1, source_target_pairs={{0,4},{8,0},{16,8},{24,16},{28,24},{20,28},{12,20},{4,12},{1,5},{9... | collective-permute-start | bytes 786440 | tf_op jit(solution)/shard_map/combine_return/ppermute | solution.py:37
  213.8 7.7 %collective-permute-start.30 = (bf16[64,2048]{1,0:T(8,128)(2,1)S(1)}, bf16[64,2048]{1,0:T(8,128)(2,1)S(1)}, u32[]{:S(2)}, u32[]{:S(2)}) collective-permute-start(bf16[64,2048]{1,0:T(8,128)(2,1)S(1)} %get-tuple-element.122), channel_id=1, source_target_pairs={{0,8},{8,16},{16,24},{24,28},{28,20},{20,12},{12,4},{4,0},{1,9},{9... | collective-permute-start | bytes 786440 | tf_op jit(solution)/shard_map/combine_return/ppermute | solution.py:37
  214.2 7.4 %collective-permute-start.31 = (bf16[64,2048]{1,0:T(8,128)(2,1)S(1)}, bf16[64,2048]{1,0:T(8,128)(2,1)S(1)}, u32[]{:S(2)}, u32[]{:S(2)}) collective-permute-start(bf16[64,2048]{1,0:T(8,128)(2,1)S(1)} %get-tuple-element.123), channel_id=1, source_target_pairs={{0,4},{8,0},{16,8},{24,16},{28,24},{20,28},{12,20},{4,12},{1,5},{9... | collective-permute-start | bytes 786440 | tf_op jit(solution)/shard_map/combine_return/ppermute | solution.py:37
  221.7 6.8 %collective-permute-start.32 = (bf16[64,2048]{1,0:T(8,128)(2,1)S(1)}, bf16[64,2048]{1,0:T(8,128)(2,1)S(1)}, u32[]{:S(2)}, u32[]{:S(2)}) collective-permute-start(bf16[64,2048]{1,0:T(8,128)(2,1)S(1)} %get-tuple-element.126), channel_id=1, source_target_pairs={{0,8},{8,16},{16,24},{24,28},{28,20},{20,12},{12,4},{4,0},{1,9},{9... | collective-permute-start | bytes 786440 | tf_op jit(solution)/shard_map/combine_return/ppermute | solution.py:37
  223.9 6.6 %collective-permute-start.33 = (bf16[64,2048]{1,0:T(8,128)(2,1)S(1)}, bf16[64,2048]{1,0:T(8,128)(2,1)S(1)}, u32[]{:S(2)}, u32[]{:S(2)}) collective-permute-start(bf16[64,2048]{1,0:T(8,128)(2,1)S(1)} %get-tuple-element.127), channel_id=1, source_target_pairs={{0,4},{8,0},{16,8},{24,16},{28,24},{20,28},{12,20},{4,12},{1,5},{9... | collective-permute-start | bytes 786440 | tf_op jit(solution)/shard_map/combine_return/ppermute | solution.py:37
  230.6 6.4 %collective-permute-start.34 = (bf16[64,2048]{1,0:T(8,128)(2,1)S(1)}, bf16[64,2048]{1,0:T(8,128)(2,1)S(1)}, u32[]{:S(2)}, u32[]{:S(2)}) collective-permute-start(bf16[64,2048]{1,0:T(8,128)(2,1)S(1)} %get-tuple-element.130), channel_id=1, source_target_pairs={{0,8},{8,16},{16,24},{24,28},{28,20},{20,12},{12,4},{4,0},{1,9},{9... | collective-permute-start | bytes 786440 | tf_op jit(solution)/shard_map/combine_return/ppermute | solution.py:37
  232.4 6.4 %collective-permute-start.35 = (bf16[64,2048]{1,0:T(8,128)(2,1)S(1)}, bf16[64,2048]{1,0:T(8,128)(2,1)S(1)}, u32[]{:S(2)}, u32[]{:S(2)}) collective-permute-start(bf16[64,2048]{1,0:T(8,128)(2,1)S(1)} %get-tuple-element.131), channel_id=1, source_target_pairs={{0,4},{8,0},{16,8},{24,16},{28,24},{20,28},{12,20},{4,12},{1,5},{9... | collective-permute-start | bytes 786440 | tf_op jit(solution)/shard_map/combine_return/ppermute | solution.py:37
  238.9 22.9 %copy-start.6 = (f32[2048]{0:T(1024)S(1)}, f32[2048]{0:T(1024)}, u32[]{:S(2)}) copy-start(f32[2048]{0:T(1024)} %param.21) | copy-start | bytes 24580
  238.9 6.4 %collective-permute-start.36 = (bf16[64,2048]{1,0:T(8,128)(2,1)S(1)}, bf16[64,2048]{1,0:T(8,128)(2,1)S(1)}, u32[]{:S(2)}, u32[]{:S(2)}) collective-permute-start(bf16[64,2048]{1,0:T(8,128)(2,1)S(1)} %get-tuple-element.134), channel_id=1, source_target_pairs={{0,8},{8,16},{16,24},{24,28},{28,20},{20,12},{12,4},{4,0},{1,9},{9... | collective-permute-start | bytes 786440 | tf_op jit(solution)/shard_map/combine_return/ppermute | solution.py:37
  239.5 6.4 %collective-permute-start.37 = (bf16[64,2048]{1,0:T(8,128)(2,1)S(1)}, bf16[64,2048]{1,0:T(8,128)(2,1)S(1)}, u32[]{:S(2)}, u32[]{:S(2)}) collective-permute-start(bf16[64,2048]{1,0:T(8,128)(2,1)S(1)} %get-tuple-element.135), channel_id=1, source_target_pairs={{0,4},{8,0},{16,8},{24,16},{28,24},{20,28},{12,20},{4,12},{1,5},{9... | collective-permute-start | bytes 786440 | tf_op jit(solution)/shard_map/combine_return/ppermute | solution.py:37
  246.1 16.9 %copy-start.1 = (bf16[512,2048]{1,0:T(8,128)(2,1)S(1)}, bf16[512,2048]{1,0:T(8,128)(2,1)}, u32[]{:S(2)}) copy-start(bf16[512,2048]{1,0:T(8,128)(2,1)} %param.15) | copy-start | bytes 6291460
  246.1 6.4 %collective-permute-start.38 = (bf16[64,2048]{1,0:T(8,128)(2,1)S(1)}, bf16[64,2048]{1,0:T(8,128)(2,1)S(1)}, u32[]{:S(2)}, u32[]{:S(2)}) collective-permute-start(bf16[64,2048]{1,0:T(8,128)(2,1)S(1)} %get-tuple-element.138), channel_id=1, source_target_pairs={{0,8},{8,16},{16,24},{24,28},{28,20},{20,12},{12,4},{4,0},{1,9},{9... | collective-permute-start | bytes 786440 | tf_op jit(solution)/shard_map/combine_return/ppermute | solution.py:37
  247.9 6.4 %collective-permute-start.39 = (bf16[64,2048]{1,0:T(8,128)(2,1)S(1)}, bf16[64,2048]{1,0:T(8,128)(2,1)S(1)}, u32[]{:S(2)}, u32[]{:S(2)}) collective-permute-start(bf16[64,2048]{1,0:T(8,128)(2,1)S(1)} %get-tuple-element.139), channel_id=1, source_target_pairs={{0,4},{8,0},{16,8},{24,16},{28,24},{20,28},{12,20},{4,12},{1,5},{9... | collective-permute-start | bytes 786440 | tf_op jit(solution)/shard_map/combine_return/ppermute | solution.py:37
  254.4 6.4 %collective-permute-start.40 = (bf16[64,2048]{1,0:T(8,128)(2,1)S(1)}, bf16[64,2048]{1,0:T(8,128)(2,1)S(1)}, u32[]{:S(2)}, u32[]{:S(2)}) collective-permute-start(bf16[64,2048]{1,0:T(8,128)(2,1)S(1)} %get-tuple-element.142), channel_id=1, source_target_pairs={{0,8},{8,16},{16,24},{24,28},{28,20},{20,12},{12,4},{4,0},{1,9},{9... | collective-permute-start | bytes 786440 | tf_op jit(solution)/shard_map/combine_return/ppermute | solution.py:37
  255.0 6.4 %collective-permute-start.41 = (bf16[64,2048]{1,0:T(8,128)(2,1)S(1)}, bf16[64,2048]{1,0:T(8,128)(2,1)S(1)}, u32[]{:S(2)}, u32[]{:S(2)}) collective-permute-start(bf16[64,2048]{1,0:T(8,128)(2,1)S(1)} %get-tuple-element.143), channel_id=1, source_target_pairs={{0,4},{8,0},{16,8},{24,16},{28,24},{20,28},{12,20},{4,12},{1,5},{9... | collective-permute-start | bytes 786440 | tf_op jit(solution)/shard_map/combine_return/ppermute | solution.py:37

commit v5 on v4

--- a/solution.py
+++ b/solution.py
@@ -45,23 +45,55 @@
 
 def ring_all_gather(block, ring, pos):
     n = len(ring)
-    rows = block.shape[0]
-    half = rows // 2
-    ring_index = jnp.array(ring, dtype=jnp.int32)
+    half = block.shape[0] // 2
     forward = [(ring[q], ring[(q + 1) % n]) for q in range(n)]
     backward = [(ring[q], ring[(q - 1) % n]) for q in range(n)]
-    out = jnp.zeros((n,) + block.shape, block.dtype)
-    out = lax.dynamic_update_index_in_dim(out, block, ring_index[pos], 0)
     got_fwd, got_bwd = block[:half], block[half:]
+    arrived = []
     for step in range(n - 1):
         got_fwd, got_bwd = lax.optimization_barrier(
             (lax.ppermute(got_fwd, "ep", forward), lax.ppermute(got_bwd, "ep", backward))
         )
-        src_fwd = ring_index[(pos - 1 - step) % n]
-        src_bwd = ring_index[(pos + 1 + step) % n]
-        out = lax.dynamic_update_slice(out, got_fwd[None], (src_fwd, 0, 0))
-        out = lax.dynamic_update_slice(out, got_bwd[None], (src_bwd, half, 0))
-    return out
+        arrived.append((got_fwd, got_bwd))
+    return arrived
+
+
+def ring_reduce_scatter_steps(pieces, own, ring):
+    n = len(ring)
+    forward = [(ring[q], ring[(q + 1) % n]) for q in range(n)]
+    backward = [(ring[q], ring[(q - 1) % n]) for q in range(n)]
+    got_fwd = got_bwd = None
+    for step in range(n - 1):
+        send_fwd, send_bwd = pieces[step]
+        if step:
+            send_fwd = send_fwd + got_fwd
+            send_bwd = send_bwd + got_bwd
+        send_fwd, send_bwd = lax.optimization_barrier(
+            (send_fwd.astype(jnp.bfloat16), send_bwd.astype(jnp.bfloat16))
+        )
+        got_fwd, got_bwd = lax.optimization_barrier(
+            (lax.ppermute(send_fwd, "ep", forward), lax.ppermute(send_bwd, "ep", backward))
+        )
+        got_fwd = got_fwd.astype(jnp.float32)
+        got_bwd = got_bwd.astype(jnp.float32)
+    half = own.shape[0] // 2
+    return jnp.concatenate([own[:half] + got_fwd, own[half:] + got_bwd], axis=0)
+
+
+def expert_mix(rows, weights, gate_up, down):
+    hidden_width = down.shape[1]
+    total = None
+    for e in range(gate_up.shape[0]):
+        projected_up = jnp.dot(rows, gate_up[e], preferred_element_type=jnp.float32)
+        activated = (
+            jax.nn.silu(projected_up[:, :hidden_width]) * projected_up[:, hidden_width:]
+        ).astype(jnp.bfloat16)
+        expert_out = jnp.dot(activated, down[e], preferred_element_type=jnp.float32).astype(
+            jnp.bfloat16
+        )
+        term = weights[:, e : e + 1] * expert_out.astype(jnp.float32)
+        total = term if total is None else total + term
+    return total
 
 
 def body(
@@ -98,25 +130,44 @@
 
     normed = rms_scale(middle.astype(jnp.float32), post_gain).astype(jnp.bfloat16)
     with jax.named_scope("dispatch_gather"):
-        normed_all = ring_all_gather(normed, ring, pos).reshape(group_rows, model_width)
+        arrived = ring_all_gather(normed, ring, pos)
+
+    ring_index = jnp.array(ring, dtype=jnp.int32)
+    weight_blocks = row_weights.reshape(ep_size, row_count, local_experts)
+    half = row_count // 2
+
+    def step_weights(step):
+        owner_fwd = ring_index[(pos - 1 - step) % ep_size]
+        owner_bwd = ring_index[(pos + 1 + step) % ep_size]
+        w_fwd = lax.dynamic_index_in_dim(weight_blocks, owner_fwd, 0, keepdims=False)[:half]
+        w_bwd = lax.dynamic_index_in_dim(weight_blocks, owner_bwd, 0, keepdims=False)[half:]
+        return w_fwd, w_bwd
 
     with jax.named_scope("local_experts"):
-        combined_part = jnp.zeros((group_rows, model_width), jnp.float32)
-        for e in range(local_experts):
-            row_weight = row_weights[:, e]
-            projected_up = jnp.dot(normed_all, gate_up[e], preferred_element_type=jnp.float32)
-            activated = (
-                jax.nn.silu(projected_up[:, :hidden_width]) * projected_up[:, hidden_width:]
-            ).astype(jnp.bfloat16)
-            expert_out = jnp.dot(activated, down[e], preferred_element_type=jnp.float32).astype(
-                jnp.bfloat16
+        first = (ep_size - 1 + 1) // 2
+        chunks = [list(range(first)), list(range(first, ep_size - 1))]
+        pieces = [None] * (ep_size - 1)
+        own_part = None
+        for c, steps in enumerate(chunks):
+            rows_in = []
+            weights_in = []
+            for step in steps:
+                rows_in += list(arrived[step])
+                weights_in += list(step_weights(step))
+            if c == len(chunks) - 1:
+                rows_in.append(normed)
+                weights_in.append(lax.dynamic_index_in_dim(weight_blocks, me, 0, keepdims=False))
+            mixed = expert_mix(
+                jnp.concatenate(rows_in, axis=0), jnp.concatenate(weights_in, axis=0), gate_up, down
             )
-            combined_part = combined_part + row_weight[:, None] * expert_out.astype(jnp.float32)
+            for i, step in enumerate(steps):
+                pieces[step] = (mixed[(2 * i) * half : (2 * i + 1) * half],
+                                mixed[(2 * i + 1) * half : (2 * i + 2) * half])
+            if c == len(chunks) - 1:
+                own_part = mixed[2 * len(steps) * half :]
 
     with jax.named_scope("combine_return"):
-        combined = ring_reduce_scatter(
-            combined_part.reshape(ep_size, row_count, model_width), ring, pos
-        )
+        combined = ring_reduce_scatter_steps(pieces, own_part, ring)
     updated = middle.astype(jnp.float32) + combined
     return (updated.astype(jnp.bfloat16), rms_scale(updated, final_gain).astype(jnp.bfloat16))
 

time: 264 us -> 246 us (0.932)
  waiting for transfers between devices: 117 us -> 92.7 us
  other arithmetic: 13.3 us -> 17.1 us
    ppermute x14 -> x7, waiting for transfers between devices: 44.9 us -> 12.3 us  [ring_reduce_scatter(): lax.ppermute(send_fwd, 'ep', forward)]
    ppermute x0 -> x14, waiting for transfers between devices: none -> 28.3 us  [the longest x7 21.6 us: ring_reduce_scatter_steps(): lax.ppermute(send_fwd, 'ep', forward)]
    ppermute x0 -> x14, starting transfers between devices: none -> 14.6 us  [the longest x7 7.57 us: ring_reduce_scatter_steps(): lax.ppermute(send_fwd, 'ep', forward)]
    ppermute x14 -> x7, waiting for transfers between devices: 15.6 us -> 7.75 us  [ring_reduce_scatter(): lax.ppermute(send_bwd, 'ep', backward)]
    ppermute x14 -> x7, starting transfers between devices: 14.3 us -> 6.59 us  [ring_reduce_scatter(): lax.ppermute(send_fwd, 'ep', forward)]
    ppermute x14 -> x7, starting transfers between devices: 14.8 us -> 7.96 us  [ring_reduce_scatter(): lax.ppermute(send_bwd, 'ep', backward)]
    ppermute x7, waiting for transfers between devices: 32.4 us -> 26.1 us  [ring_all_gather(): lax.ppermute(got_fwd, 'ep', forward)]
    ppermute x7, waiting for transfers between devices: 11.7 us -> 5.83 us  [ring_all_gather(): lax.ppermute(got_bwd, 'ep', backward)]
  transfers between devices with their start and end apart: 44 -> 44, of which waited for: 43 -> 37; matrix products, arithmetic and copies ran while one was open for 1% -> 8% of each run, Pallas kernels for 0% -> 0%
where the time goes in v5:
time: 246 us; the launch traced here: 245 us
  waiting for transfers between devices  92.7 us (38%)
  starting transfers between devices  55.4 us (23%)
  between operations  40.8 us (17%)
  matrix products  30 us (12%)
  other arithmetic  17.1 us (7%)
  local copies, waits for them, and re-layouts  9.08 us (4%)
    ppermute x7, waiting for transfers between devices, ring_all_gather(): lax.ppermute(got_fwd, 'ep', forward)  26.1 us
    ppermute x7, waiting for transfers between devices, ring_reduce_scatter_steps(): lax.ppermute(send_fwd, 'ep', forward)  21.6 us
    dot_general x4, matrix products, expert_mix(): projected_up = jnp.dot(rows, gate_up[e], preferred_element_type=jnp.float32)  18.1 us
    ppermute x7, waiting for transfers between devices, ring_reduce_scatter(): lax.ppermute(send_fwd, 'ep', forward)  12.3 us
    dot_general x4, matrix products, expert_mix(): jnp.dot(activated, down[e], preferred_element_type=jnp.float32)  9.52 us
    all_to_all x1, waiting for transfers between devices, body(): lax.all_to_all(columns, 'ep', split_axis=0, concat_axis=0, tiled=True)  8.28 us
    ppermute x7, starting transfers between devices, ring_all_gather(): lax.ppermute(got_bwd, 'ep', backward)  8.18 us
    ppermute x7, starting transfers between devices, ring_reduce_scatter(): lax.ppermute(send_bwd, 'ep', backward)  7.96 us
  transfers between devices with their start and end apart: 44, of which 37 were waited for; matrix products, arithmetic and copies ran while one was open for 8% of the time, Pallas kernels for 0%

profile of v5, /device:TPU:0, one launch (start us, length us, event | category | flops | bytes accessed | tf_op | source)
XLA Modules:
  0.0 245.1 jit_solution(14893545526126461075)
XLA Ops:
  0.6 1.5 select_reduce_fusion
  2.1 7.3 %all-to-all-start.1 = ((f32[8,128,2]{1,2,0:T(2,128)}), f32[8,128,2]{1,2,0:T(2,128)S(1)}, u32[]{:S(2)}, u32[]{:S(2)}) async-start(f32[8,128,2]{1,2,0:T(2,128)} %bitcast.2), calls=%async_computation.1 | async-start | bytes 16384 | tf_op jit(solution)/shard_map/route_weights/all_to_all | solution.py:118
  9.4 2.3 copy.25
  11.7 4.2 %all-to-all-done.1 = f32[8,128,2]{1,2,0:T(2,128)S(1)} async-done(((f32[8,128,2]{1,2,0:T(2,128)}), f32[8,128,2]{1,2,0:T(2,128)S(1)}, u32[]{:S(2)}, u32[]{:S(2)}) %all-to-all-start.1) | async-done | bytes 8224 | tf_op jit(solution)/shard_map/route_weights/all_to_all | solution.py:118
  15.9 3.6 %all-to-all-start = ((bf16[8,128,512]{2,1,0:T(8,128)(2,1)}), bf16[8,128,512]{2,1,0:T(8,128)(2,1)S(1)}, u32[]{:S(2)}, u32[]{:S(2)}) async-start(bf16[8,128,512]{2,1,0:T(8,128)(2,1)} %bitcast.176), calls=%async_computation | async-start | bytes 2097152 | tf_op jit(solution)/shard_map/out_projection/all_to_all | solution.py:123
  35.9 8.3 %all-to-all-done = bf16[8,128,512]{2,1,0:T(8,128)(2,1)S(1)} async-done(((bf16[8,128,512]{2,1,0:T(8,128)(2,1)}), bf16[8,128,512]{2,1,0:T(8,128)(2,1)S(1)}, u32[]{:S(2)}, u32[]{:S(2)}) %all-to-all-start) | async-done | bytes 1048608 | tf_op jit(solution)/shard_map/out_projection/all_to_all | solution.py:123
  44.2 2.3 fusion.40
  46.6 3.4 %copy-done.2 = f32[8,128,2048]{2,1,0:T(8,128)} copy-done((f32[8,128,2048]{2,1,0:T(8,128)}, f32[8,128,2048]{2,1,0:T(8,128)S(1)}, u32[]{:S(2)}) %copy-start.2) | copy-done | bytes 8388632
  50.0 2.0 collective-permute-start.1
  56.6 1.3 fusion.82
  58.5 1.5 collective-permute-start.3
  64.4 2.1 collective-permute-done.3
  66.5 1.3 fusion.80
  67.8 1.8 collective-permute-start.4
  74.2 1.8 collective-permute-done.5
  76.0 1.3 fusion.78
  77.3 1.8 collective-permute-start.6
  83.7 1.9 collective-permute-done.7
  85.6 1.3 fusion.76
  87.5 1.5 collective-permute-start.9
  92.7 1.8 collective-permute-done.8
  95.2 1.3 fusion.74
  97.1 1.5 collective-permute-start.11
  102.7 2.8 %collective-permute-done.10 = bf16[64,2048]{1,0:T(8,128)(2,1)S(1)} collective-permute-done((bf16[64,2048]{1,0:T(8,128)(2,1)S(1)}, bf16[64,2048]{1,0:T(8,128)(2,1)S(1)}, u32[]{:S(2)}, u32[]{:S(2)}) %collective-permute-start.10) | collective-permute-done | bytes 262176 | tf_op jit(solution)/shard_map/out_projection/ppermute | solution.py:37
  106.3 1.3 fusion.72
  111.4 5.1 %collective-permute-done.12 = bf16[64,2048]{1,0:T(8,128)(2,1)S(1)} collective-permute-done((bf16[64,2048]{1,0:T(8,128)(2,1)S(1)}, bf16[64,2048]{1,0:T(8,128)(2,1)S(1)}, u32[]{:S(2)}, u32[]{:S(2)}) %collective-permute-start.12) | collective-permute-done | bytes 262176 | tf_op jit(solution)/shard_map/out_projection/ppermute | solution.py:37
  117.0 1.3 fusion.95
  119.5 1.5 collective-permute-start.15
  121.2 4.9 %collective-permute-done.14 = bf16[64,2048]{1,0:T(8,128)(2,1)S(1)} collective-permute-done((bf16[64,2048]{1,0:T(8,128)(2,1)S(1)}, bf16[64,2048]{1,0:T(8,128)(2,1)S(1)}, u32[]{:S(2)}, u32[]{:S(2)}) %collective-permute-start.14) | collective-permute-done | bytes 262176 | tf_op jit(solution)/shard_map/dispatch_gather/ppermute | solution.py:55
  126.4 2.0 collective-permute-start.17
  128.5 6.0 %collective-permute-done.16 = bf16[64,2048]{1,0:T(8,128)(2,1)S(1)} collective-permute-done((bf16[64,2048]{1,0:T(8,128)(2,1)S(1)}, bf16[64,2048]{1,0:T(8,128)(2,1)S(1)}, u32[]{:S(2)}, u32[]{:S(2)}) %collective-permute-start.16) | collective-permute-done | bytes 262176 | tf_op jit(solution)/shard_map/dispatch_gather/ppermute | solution.py:55
  135.0 1.9 collective-permute-start.19
  137.0 4.3 %collective-permute-done.18 = bf16[64,2048]{1,0:T(8,128)(2,1)S(1)} collective-permute-done((bf16[64,2048]{1,0:T(8,128)(2,1)S(1)}, bf16[64,2048]{1,0:T(8,128)(2,1)S(1)}, u32[]{:S(2)}, u32[]{:S(2)}) %collective-permute-start.18) | collective-permute-done | bytes 262176 | tf_op jit(solution)/shard_map/dispatch_gather/ppermute | solution.py:55
  142.3 2.8 %collective-permute-start.20 = (bf16[64,2048]{1,0:T(8,128)(2,1)S(1)}, bf16[64,2048]{1,0:T(8,128)(2,1)S(1)}, u32[]{:S(2)}, u32[]{:S(2)}) collective-permute-start(bf16[64,2048]{1,0:T(8,128)(2,1)S(1)} %collective-permute-done.18), channel_id=1, source_target_pairs={{0,8},{8,16},{16,24},{24,28},{28,20},{20,12},{12,4},{4,0},{1,9},{9... | collective-permute-start | bytes 786440 | tf_op jit(solution)/shard_map/dispatch_gather/ppermute | solution.py:55
  145.2 3.8 %collective-permute-done.20 = bf16[64,2048]{1,0:T(8,128)(2,1)S(1)} collective-permute-done((bf16[64,2048]{1,0:T(8,128)(2,1)S(1)}, bf16[64,2048]{1,0:T(8,128)(2,1)S(1)}, u32[]{:S(2)}, u32[]{:S(2)}) %collective-permute-start.20) | collective-permute-done | bytes 262176 | tf_op jit(solution)/shard_map/dispatch_gather/ppermute | solution.py:55
  149.0 2.5 %collective-permute-done.21 = bf16[64,2048]{1,0:T(8,128)(2,1)S(1)} collective-permute-done((bf16[64,2048]{1,0:T(8,128)(2,1)S(1)}, bf16[64,2048]{1,0:T(8,128)(2,1)S(1)}, u32[]{:S(2)}, u32[]{:S(2)}) %collective-permute-start.21) | collective-permute-done | bytes 262176 | tf_op jit(solution)/shard_map/dispatch_gather/ppermute | solution.py:55
  151.6 5.7 %fusion.4 = f32[512,1536]{1,0:T(8,128)S(1)} fusion(bf16[512,2048]{1,0:T(8,128)(2,1)S(1)} %constant_dynamic-update-slice_fusion.7, bf16[2,2048,1536]{2,1,0:T(8,128)(2,1)} %param.16), kind=kOutput, calls=%fused_computation.4 | convolution fusion | flops 3221225472 | bytes 11534336 | tf_op jit(solution)/shard_map/local_experts/dot_general | solution.py:87
  158.0 3.4 %fusion = f32[512,1536]{1,0:T(8,128)S(1)} fusion(bf16[512,2048]{1,0:T(8,128)(2,1)S(1)} %constant_dynamic-update-slice_fusion.7, bf16[2,2048,1536]{2,1,0:T(8,128)(2,1)S(1)} %bitcast.202), kind=kOutput, calls=%fused_computation | convolution fusion | flops 3221225472 | bytes 11534336 | tf_op jit(solution)/shard_map/local_experts/dot_general | solution.py:87
  161.5 1.8 fusion.23
  163.3 4.0 %fusion.109 = (bf16[512,2048]{1,0:T(8,128)(2,1)S(1)}, f32[512,2048]{1,0:T(8,128)}) fusion(bf16[2,768,2048]{2,1,0:T(8,128)(2,1)S(1)} %bitcast.206, f32[512,1536]{1,0:T(8,128)S(1)} %fusion, f32[512]{0:T(512)S(1)} %bitcast.200, bf16[512,2048]{1,0:T(8,128)(2,1)S(1)} %fusion.23, f32[512]{0:T(512)S(1)} %bitcast.199), kind=kOutput, calls=%fused_computation.170 | convolution fusion | flops 1620312064 | bytes 14684160 | tf_op jit(solution)/shard_map/local_experts/dot_general | solution.py:91
  167.3 2.1 collective-permute-start.28
  169.5 2.1 collective-permute-start.22
  171.6 4.9 %collective-permute-done.28 = bf16[64,2048]{1,0:T(8,128)(2,1)S(1)} collective-permute-done((bf16[64,2048]{1,0:T(8,128)(2,1)S(1)}, bf16[64,2048]{1,0:T(8,128)(2,1)S(1)}, u32[]{:S(2)}, u32[]{:S(2)}) %collective-permute-start.28) | collective-permute-done | bytes 262176 | tf_op jit(solution)/shard_map/combine_return/ppermute | solution.py:75
  176.5 2.1 collective-permute-done.29
  178.6 1.3 fusion.63
  187.3 1.3 fusion.62
  189.1 1.5 collective-permute-start.33
  191.2 1.5 collective-permute-start.27
  192.8 7.1 %collective-permute-done.26 = bf16[64,2048]{1,0:T(8,128)(2,1)S(1)} collective-permute-done((bf16[64,2048]{1,0:T(8,128)(2,1)S(1)}, bf16[64,2048]{1,0:T(8,128)(2,1)S(1)}, u32[]{:S(2)}, u32[]{:S(2)}) %collective-permute-start.26) | collective-permute-done | bytes 262176 | tf_op jit(solution)/shard_map/dispatch_gather/ppermute | solution.py:55
  200.8 5.7 %fusion.6 = f32[512,1536]{1,0:T(8,128)S(1)} fusion(bf16[512,2048]{1,0:T(8,128)(2,1)S(1)} %constant_dynamic-update-slice_fusion, bf16[2,2048,1536]{2,1,0:T(8,128)(2,1)} %param.16), kind=kOutput, calls=%fused_computation.6 | convolution fusion | flops 3221225472 | bytes 11534336 | tf_op jit(solution)/shard_map/local_experts/dot_general | solution.py:87
  206.5 3.4 %fusion.2 = f32[512,1536]{1,0:T(8,128)S(1)} fusion(bf16[512,2048]{1,0:T(8,128)(2,1)S(1)} %constant_dynamic-update-slice_fusion, bf16[2,2048,1536]{2,1,0:T(8,128)(2,1)S(1)} %bitcast.204), kind=kOutput, calls=%fused_computation.2 | convolution fusion | flops 3221225472 | bytes 11534336 | tf_op jit(solution)/shard_map/local_experts/dot_general | solution.py:87
  209.9 1.3 fusion.61
  211.2 1.7 collective-permute-start.34
  213.3 1.8 fusion.20
  215.2 1.9 multiply_add_fusion.1
  217.1 2.7 %collective-permute-done.34 = bf16[64,2048]{1,0:T(8,128)(2,1)S(1)} collective-permute-done((bf16[64,2048]{1,0:T(8,128)(2,1)S(1)}, bf16[64,2048]{1,0:T(8,128)(2,1)S(1)}, u32[]{:S(2)}, u32[]{:S(2)}) %collective-permute-start.34) | collective-permute-done | bytes 262176 | tf_op jit(solution)/shard_map/combine_return/ppermute | solution.py:75
  219.8 1.5 collective-permute-done.35
  222.0 1.5 collective-permute-start.37
  223.5 4.3 %collective-permute-done.36 = bf16[64,2048]{1,0:T(8,128)(2,1)S(1)} collective-permute-done((bf16[64,2048]{1,0:T(8,128)(2,1)S(1)}, bf16[64,2048]{1,0:T(8,128)(2,1)S(1)}, u32[]{:S(2)}, u32[]{:S(2)}) %collective-permute-start.36) | collective-permute-done | bytes 262176 | tf_op jit(solution)/shard_map/combine_return/ppermute | solution.py:75
  228.6 2.0 collective-permute-start.39
  230.6 4.3 %collective-permute-done.38 = bf16[64,2048]{1,0:T(8,128)(2,1)S(1)} collective-permute-done((bf16[64,2048]{1,0:T(8,128)(2,1)S(1)}, bf16[64,2048]{1,0:T(8,128)(2,1)S(1)}, u32[]{:S(2)}, u32[]{:S(2)}) %collective-permute-start.38) | collective-permute-done | bytes 262176 | tf_op jit(solution)/shard_map/combine_return/ppermute | solution.py:75
  235.1 1.5 collective-permute-start.40
  237.2 4.3 %collective-permute-done.40 = bf16[64,2048]{1,0:T(8,128)(2,1)S(1)} collective-permute-done((bf16[64,2048]{1,0:T(8,128)(2,1)S(1)}, bf16[64,2048]{1,0:T(8,128)(2,1)S(1)}, u32[]{:S(2)}, u32[]{:S(2)}) %collective-permute-start.40) | collective-permute-done | bytes 262176 | tf_op jit(solution)/shard_map/combine_return/ppermute | solution.py:75
  241.5 1.5 collective-permute-done.41
  (122 shorter events, 28.8 us)
Async XLA Ops:
  0.6 43.6 %copy-start = (bf16[512,2048]{1,0:T(8,128)(2,1)S(1)}, bf16[512,2048]{1,0:T(8,128)(2,1)}, u32[]{:S(2)}) copy-start(bf16[512,2048]{1,0:T(8,128)(2,1)} %param.14) | copy-start | bytes 6291460
  2.1 13.8 %all-to-all-start.1 = ((f32[8,128,2]{1,2,0:T(2,128)}), f32[8,128,2]{1,2,0:T(2,128)S(1)}, u32[]{:S(2)}, u32[]{:S(2)}) async-start(f32[8,128,2]{1,2,0:T(2,128)} %bitcast.2), calls=%async_computation.1 | async-start | bytes 16384 | tf_op jit(solution)/shard_map/route_weights/all_to_all | solution.py:118
  9.4 10.1 %copy-start.7 = (s32[8]{0:T(128)S(1)}, s32[8]{0:T(128)}, u32[]{:S(2)}) copy-start(s32[8]{0:T(128)} %constant.220.clone) | copy-start | bytes 100
  9.4 21.9 %copy-start.4 = (s32[8]{0:T(128)S(1)}, s32[8]{0:T(128)}, u32[]{:S(2)}) copy-start(s32[8]{0:T(128)} %constant.221.clone) | copy-start | bytes 100
  15.9 28.3 %all-to-all-start = ((bf16[8,128,512]{2,1,0:T(8,128)(2,1)}), bf16[8,128,512]{2,1,0:T(8,128)(2,1)S(1)}, u32[]{:S(2)}, u32[]{:S(2)}) async-start(bf16[8,128,512]{2,1,0:T(8,128)(2,1)} %bitcast.176), calls=%async_computation | async-start | bytes 2097152 | tf_op jit(solution)/shard_map/out_projection/all_to_all | solution.py:123
  46.5 3.4 %copy-start.2 = (f32[8,128,2048]{2,1,0:T(8,128)}, f32[8,128,2048]{2,1,0:T(8,128)S(1)}, u32[]{:S(2)}) copy-start(f32[8,128,2048]{2,1,0:T(8,128)S(1)} %fusion.40) | copy-start | bytes 25165828
  50.0 6.6 %collective-permute-start = (bf16[64,2048]{1,0:T(8,128)(2,1)S(1)}, bf16[64,2048]{1,0:T(8,128)(2,1)S(1)}, u32[]{:S(2)}, u32[]{:S(2)}) collective-permute-start(bf16[64,2048]{1,0:T(8,128)(2,1)S(1)} %get-tuple-element.75), channel_id=1, source_target_pairs={{0,8},{8,16},{16,24},{24,28},{28,20},{20,12},{12,4},{4,0},{1,9},{9... | collective-permute-start | bytes 786440 | tf_op jit(solution)/shard_map/out_projection/ppermute | solution.py:37
  50.0 6.6 %collective-permute-start.1 = (bf16[64,2048]{1,0:T(8,128)(2,1)S(1)}, bf16[64,2048]{1,0:T(8,128)(2,1)S(1)}, u32[]{:S(2)}, u32[]{:S(2)}) collective-permute-start(bf16[64,2048]{1,0:T(8,128)(2,1)S(1)} %get-tuple-element.76), channel_id=1, source_target_pairs={{0,4},{8,0},{16,8},{24,16},{28,24},{20,28},{12,20},{4,12},{1,5},{9... | collective-permute-start | bytes 786440 | tf_op jit(solution)/shard_map/out_projection/ppermute | solution.py:37
  57.9 6.4 %collective-permute-start.2 = (bf16[64,2048]{1,0:T(8,128)(2,1)S(1)}, bf16[64,2048]{1,0:T(8,128)(2,1)S(1)}, u32[]{:S(2)}, u32[]{:S(2)}) collective-permute-start(bf16[64,2048]{1,0:T(8,128)(2,1)S(1)} %get-tuple-element.79), channel_id=1, source_target_pairs={{0,8},{8,16},{16,24},{24,28},{28,20},{20,12},{12,4},{4,0},{1,9},{9... | collective-permute-start | bytes 786440 | tf_op jit(solution)/shard_map/out_projection/ppermute | solution.py:37
  58.5 7.9 %collective-permute-start.3 = (bf16[64,2048]{1,0:T(8,128)(2,1)S(1)}, bf16[64,2048]{1,0:T(8,128)(2,1)S(1)}, u32[]{:S(2)}, u32[]{:S(2)}) collective-permute-start(bf16[64,2048]{1,0:T(8,128)(2,1)S(1)} %get-tuple-element.80), channel_id=1, source_target_pairs={{0,4},{8,0},{16,8},{24,16},{28,24},{20,28},{12,20},{4,12},{1,5},{9... | collective-permute-start | bytes 786440 | tf_op jit(solution)/shard_map/out_projection/ppermute | solution.py:37
  67.8 6.4 %collective-permute-start.4 = (bf16[64,2048]{1,0:T(8,128)(2,1)S(1)}, bf16[64,2048]{1,0:T(8,128)(2,1)S(1)}, u32[]{:S(2)}, u32[]{:S(2)}) collective-permute-start(bf16[64,2048]{1,0:T(8,128)(2,1)S(1)} %get-tuple-element.83), channel_id=1, source_target_pairs={{0,8},{8,16},{16,24},{24,28},{28,20},{20,12},{12,4},{4,0},{1,9},{9... | collective-permute-start | bytes 786440 | tf_op jit(solution)/shard_map/out_projection/ppermute | solution.py:37
  69.6 6.4 %collective-permute-start.5 = (bf16[64,2048]{1,0:T(8,128)(2,1)S(1)}, bf16[64,2048]{1,0:T(8,128)(2,1)S(1)}, u32[]{:S(2)}, u32[]{:S(2)}) collective-permute-start(bf16[64,2048]{1,0:T(8,128)(2,1)S(1)} %get-tuple-element.84), channel_id=1, source_target_pairs={{0,4},{8,0},{16,8},{24,16},{28,24},{20,28},{12,20},{4,12},{1,5},{9... | collective-permute-start | bytes 786440 | tf_op jit(solution)/shard_map/out_projection/ppermute | solution.py:37
  77.3 6.4 %collective-permute-start.6 = (bf16[64,2048]{1,0:T(8,128)(2,1)S(1)}, bf16[64,2048]{1,0:T(8,128)(2,1)S(1)}, u32[]{:S(2)}, u32[]{:S(2)}) collective-permute-start(bf16[64,2048]{1,0:T(8,128)(2,1)S(1)} %get-tuple-element.87), channel_id=1, source_target_pairs={{0,8},{8,16},{16,24},{24,28},{28,20},{20,12},{12,4},{4,0},{1,9},{9... | collective-permute-start | bytes 786440 | tf_op jit(solution)/shard_map/out_projection/ppermute | solution.py:37
  79.1 6.6 %collective-permute-start.7 = (bf16[64,2048]{1,0:T(8,128)(2,1)S(1)}, bf16[64,2048]{1,0:T(8,128)(2,1)S(1)}, u32[]{:S(2)}, u32[]{:S(2)}) collective-permute-start(bf16[64,2048]{1,0:T(8,128)(2,1)S(1)} %get-tuple-element.88), channel_id=1, source_target_pairs={{0,4},{8,0},{16,8},{24,16},{28,24},{20,28},{12,20},{4,12},{1,5},{9... | collective-permute-start | bytes 786440 | tf_op jit(solution)/shard_map/out_projection/ppermute | solution.py:37
  86.9 7.7 %collective-permute-start.8 = (bf16[64,2048]{1,0:T(8,128)(2,1)S(1)}, bf16[64,2048]{1,0:T(8,128)(2,1)S(1)}, u32[]{:S(2)}, u32[]{:S(2)}) collective-permute-start(bf16[64,2048]{1,0:T(8,128)(2,1)S(1)} %get-tuple-element.91), channel_id=1, source_target_pairs={{0,8},{8,16},{16,24},{24,28},{28,20},{20,12},{12,4},{4,0},{1,9},{9... | collective-permute-start | bytes 786440 | tf_op jit(solution)/shard_map/out_projection/ppermute | solution.py:37
  87.5 7.7 %collective-permute-start.9 = (bf16[64,2048]{1,0:T(8,128)(2,1)S(1)}, bf16[64,2048]{1,0:T(8,128)(2,1)S(1)}, u32[]{:S(2)}, u32[]{:S(2)}) collective-permute-start(bf16[64,2048]{1,0:T(8,128)(2,1)S(1)} %get-tuple-element.92), channel_id=1, source_target_pairs={{0,4},{8,0},{16,8},{24,16},{28,24},{20,28},{12,20},{4,12},{1,5},{9... | collective-permute-start | bytes 786440 | tf_op jit(solution)/shard_map/out_projection/ppermute | solution.py:37
  96.5 8.9 %collective-permute-start.10 = (bf16[64,2048]{1,0:T(8,128)(2,1)S(1)}, bf16[64,2048]{1,0:T(8,128)(2,1)S(1)}, u32[]{:S(2)}, u32[]{:S(2)}) collective-permute-start(bf16[64,2048]{1,0:T(8,128)(2,1)S(1)} %get-tuple-element.95), channel_id=1, source_target_pairs={{0,8},{8,16},{16,24},{24,28},{28,20},{20,12},{12,4},{4,0},{1,9},{9... | collective-permute-start | bytes 786440 | tf_op jit(solution)/shard_map/out_projection/ppermute | solution.py:37
  97.1 9.1 %collective-permute-start.11 = (bf16[64,2048]{1,0:T(8,128)(2,1)S(1)}, bf16[64,2048]{1,0:T(8,128)(2,1)S(1)}, u32[]{:S(2)}, u32[]{:S(2)}) collective-permute-start(bf16[64,2048]{1,0:T(8,128)(2,1)S(1)} %get-tuple-element.96), channel_id=1, source_target_pairs={{0,4},{8,0},{16,8},{24,16},{28,24},{20,28},{12,20},{4,12},{1,5},{9... | collective-permute-start | bytes 786440 | tf_op jit(solution)/shard_map/out_projection/ppermute | solution.py:37
  102.6 15.7 %copy-start.3 = (bf16[128,2048]{1,0:T(8,128)(2,1)S(1)}, bf16[128,2048]{1,0:T(8,128)(2,1)}, u32[]{:S(2)}) copy-start(bf16[128,2048]{1,0:T(8,128)(2,1)} %param.12) | copy-start | bytes 1572868
  107.6 8.9 %collective-permute-start.12 = (bf16[64,2048]{1,0:T(8,128)(2,1)S(1)}, bf16[64,2048]{1,0:T(8,128)(2,1)S(1)}, u32[]{:S(2)}, u32[]{:S(2)}) collective-permute-start(bf16[64,2048]{1,0:T(8,128)(2,1)S(1)} %get-tuple-element.99), channel_id=1, source_target_pairs={{0,8},{8,16},{16,24},{24,28},{28,20},{20,12},{12,4},{4,0},{1,9},{9... | collective-permute-start | bytes 786440 | tf_op jit(solution)/shard_map/out_projection/ppermute | solution.py:37
  108.8 8.3 %collective-permute-start.13 = (bf16[64,2048]{1,0:T(8,128)(2,1)S(1)}, bf16[64,2048]{1,0:T(8,128)(2,1)S(1)}, u32[]{:S(2)}, u32[]{:S(2)}) collective-permute-start(bf16[64,2048]{1,0:T(8,128)(2,1)S(1)} %get-tuple-element.100), channel_id=1, source_target_pairs={{0,4},{8,0},{16,8},{24,16},{28,24},{20,28},{12,20},{4,12},{1,5},{9... | collective-permute-start | bytes 786440 | tf_op jit(solution)/shard_map/out_projection/ppermute | solution.py:37
  111.4 7.3 %copy-start.5 = (f32[2048]{0:T(1024)S(1)}, f32[2048]{0:T(1024)}, u32[]{:S(2)}) copy-start(f32[2048]{0:T(1024)} %param.15) | copy-start | bytes 24580
  118.9 7.1 %collective-permute-start.14 = (bf16[64,2048]{1,0:T(8,128)(2,1)S(1)}, bf16[64,2048]{1,0:T(8,128)(2,1)S(1)}, u32[]{:S(2)}, u32[]{:S(2)}) collective-permute-start(bf16[64,2048]{1,0:T(8,128)(2,1)S(1)} %get-tuple-element.183), channel_id=1, source_target_pairs={{0,8},{8,16},{16,24},{24,28},{28,20},{20,12},{12,4},{4,0},{1,9},{9... | collective-permute-start | bytes 786440 | tf_op jit(solution)/shard_map/dispatch_gather/ppermute | solution.py:55
  119.5 6.9 %collective-permute-start.15 = (bf16[64,2048]{1,0:T(8,128)(2,1)S(1)}, bf16[64,2048]{1,0:T(8,128)(2,1)S(1)}, u32[]{:S(2)}, u32[]{:S(2)}) collective-permute-start(bf16[64,2048]{1,0:T(8,128)(2,1)S(1)} %get-tuple-element.182), channel_id=1, source_target_pairs={{0,4},{8,0},{16,8},{24,16},{28,24},{20,28},{12,20},{4,12},{1,5},{9... | collective-permute-start | bytes 786440 | tf_op jit(solution)/shard_map/dispatch_gather/ppermute | solution.py:55
  126.4 8.1 %collective-permute-start.16 = (bf16[64,2048]{1,0:T(8,128)(2,1)S(1)}, bf16[64,2048]{1,0:T(8,128)(2,1)S(1)}, u32[]{:S(2)}, u32[]{:S(2)}) collective-permute-start(bf16[64,2048]{1,0:T(8,128)(2,1)S(1)} %collective-permute-done.14), channel_id=1, source_target_pairs={{0,8},{8,16},{16,24},{24,28},{28,20},{20,12},{12,4},{4,0},{1,9},{9... | collective-permute-start | bytes 786440 | tf_op jit(solution)/shard_map/dispatch_gather/ppermute | solution.py:55
  126.4 8.1 %collective-permute-start.17 = (bf16[64,2048]{1,0:T(8,128)(2,1)S(1)}, bf16[64,2048]{1,0:T(8,128)(2,1)S(1)}, u32[]{:S(2)}, u32[]{:S(2)}) collective-permute-start(bf16[64,2048]{1,0:T(8,128)(2,1)S(1)} %collective-permute-done.15), channel_id=1, source_target_pairs={{0,4},{8,0},{16,8},{24,16},{28,24},{20,28},{12,20},{4,12},{1,5},{9... | collective-permute-start | bytes 786440 | tf_op jit(solution)/shard_map/dispatch_gather/ppermute | solution.py:55
  134.5 6.8 %collective-permute-start.18 = (bf16[64,2048]{1,0:T(8,128)(2,1)S(1)}, bf16[64,2048]{1,0:T(8,128)(2,1)S(1)}, u32[]{:S(2)}, u32[]{:S(2)}) collective-permute-start(bf16[64,2048]{1,0:T(8,128)(2,1)S(1)} %collective-permute-done.16), channel_id=1, source_target_pairs={{0,8},{8,16},{16,24},{24,28},{28,20},{20,12},{12,4},{4,0},{1,9},{9... | collective-permute-start | bytes 786440 | tf_op jit(solution)/shard_map/dispatch_gather/ppermute | solution.py:55
  135.0 7.3 %collective-permute-start.19 = (bf16[64,2048]{1,0:T(8,128)(2,1)S(1)}, bf16[64,2048]{1,0:T(8,128)(2,1)S(1)}, u32[]{:S(2)}, u32[]{:S(2)}) collective-permute-start(bf16[64,2048]{1,0:T(8,128)(2,1)S(1)} %collective-permute-done.17), channel_id=1, source_target_pairs={{0,4},{8,0},{16,8},{24,16},{28,24},{20,28},{12,20},{4,12},{1,5},{9... | collective-permute-start | bytes 786440 | tf_op jit(solution)/shard_map/dispatch_gather/ppermute | solution.py:55
  142.3 6.7 %collective-permute-start.20 = (bf16[64,2048]{1,0:T(8,128)(2,1)S(1)}, bf16[64,2048]{1,0:T(8,128)(2,1)S(1)}, u32[]{:S(2)}, u32[]{:S(2)}) collective-permute-start(bf16[64,2048]{1,0:T(8,128)(2,1)S(1)} %collective-permute-done.18), channel_id=1, source_target_pairs={{0,8},{8,16},{16,24},{24,28},{28,20},{20,12},{12,4},{4,0},{1,9},{9... | collective-permute-start | bytes 786440 | tf_op jit(solution)/shard_map/dispatch_gather/ppermute | solution.py:55
  145.1 6.4 %collective-permute-start.21 = (bf16[64,2048]{1,0:T(8,128)(2,1)S(1)}, bf16[64,2048]{1,0:T(8,128)(2,1)S(1)}, u32[]{:S(2)}, u32[]{:S(2)}) collective-permute-start(bf16[64,2048]{1,0:T(8,128)(2,1)S(1)} %collective-permute-done.19), channel_id=1, source_target_pairs={{0,4},{8,0},{16,8},{24,16},{28,24},{20,28},{12,20},{4,12},{1,5},{9... | collective-permute-start | bytes 786440 | tf_op jit(solution)/shard_map/dispatch_gather/ppermute | solution.py:55
  151.5 5.8 %slice-start = ((s8[12582912]{0:T(1024)(128)(4,1)}), s8[4194304]{0:T(1024)(128)(4,1)S(1)}, s32[]{:S(2)}) async-start(s8[12582912]{0:T(1024)(128)(4,1)} %bitcast.201), calls=%async_computation.2 | async-start | bytes 8388608
  151.5 5.7 %slice-start.1 = ((s8[12582912]{0:T(1024)(128)(4,1)}), s8[4194304]{0:T(1024)(128)(4,1)S(1)}, s32[]{:S(2)}) async-start(s8[12582912]{0:T(1024)(128)(4,1)} %bitcast.201), calls=%async_computation.3 | async-start | bytes 8388608
  151.6 6.5 %slice-start.2 = ((s8[12582912]{0:T(1024)(128)(4,1)}), s8[4194304]{0:T(1024)(128)(4,1)S(1)}, s32[]{:S(2)}) async-start(s8[12582912]{0:T(1024)(128)(4,1)} %bitcast.201), calls=%async_computation.4 | async-start | bytes 8388608
  151.6 9.9 %slice-start.6 = ((s8[6291456]{0:T(1024)(128)(4,1)}), s8[4194304]{0:T(1024)(128)(4,1)S(1)}, s32[]{:S(2)}) async-start(s8[6291456]{0:T(1024)(128)(4,1)} %bitcast.205), calls=%async_computation.8 | async-start | bytes 8388608
  158.0 3.4 %slice-start.7 = ((s8[6291456]{0:T(1024)(128)(4,1)}), s8[2097152]{0:T(1024)(128)(4,1)S(1)}, s32[]{:S(2)}) async-start(s8[6291456]{0:T(1024)(128)(4,1)} %bitcast.205), calls=%async_computation.9 | async-start | bytes 4194304
  167.3 9.2 %collective-permute-start.28 = (bf16[64,2048]{1,0:T(8,128)(2,1)S(1)}, bf16[64,2048]{1,0:T(8,128)(2,1)S(1)}, u32[]{:S(2)}, u32[]{:S(2)}) collective-permute-start(bf16[64,2048]{1,0:T(8,128)(2,1)S(1)} %get-tuple-element.118), channel_id=1, source_target_pairs={{0,8},{8,16},{16,24},{24,28},{28,20},{20,12},{12,4},{4,0},{1,9},{9... | collective-permute-start | bytes 786440 | tf_op jit(solution)/shard_map/combine_return/ppermute | solution.py:75
  169.4 9.2 %collective-permute-start.29 = (bf16[64,2048]{1,0:T(8,128)(2,1)S(1)}, bf16[64,2048]{1,0:T(8,128)(2,1)S(1)}, u32[]{:S(2)}, u32[]{:S(2)}) collective-permute-start(bf16[64,2048]{1,0:T(8,128)(2,1)S(1)} %get-tuple-element.119), channel_id=1, source_target_pairs={{0,4},{8,0},{16,8},{24,16},{28,24},{20,28},{12,20},{4,12},{1,5},{9... | collective-permute-start | bytes 786440 | tf_op jit(solution)/shard_map/combine_return/ppermute | solution.py:75
  169.5 12.4 %collective-permute-start.22 = (bf16[64,2048]{1,0:T(8,128)(2,1)S(1)}, bf16[64,2048]{1,0:T(8,128)(2,1)S(1)}, u32[]{:S(2)}, u32[]{:S(2)}) collective-permute-start(bf16[64,2048]{1,0:T(8,128)(2,1)S(1)} %collective-permute-done.20), channel_id=1, source_target_pairs={{0,8},{8,16},{16,24},{24,28},{28,20},{20,12},{12,4},{4,0},{1,9},{9... | collective-permute-start | bytes 786440 | tf_op jit(solution)/shard_map/dispatch_gather/ppermute | solution.py:55
  171.6 11.6 %collective-permute-start.23 = (bf16[64,2048]{1,0:T(8,128)(2,1)S(1)}, bf16[64,2048]{1,0:T(8,128)(2,1)S(1)}, u32[]{:S(2)}, u32[]{:S(2)}) collective-permute-start(bf16[64,2048]{1,0:T(8,128)(2,1)S(1)} %collective-permute-done.21), channel_id=1, source_target_pairs={{0,4},{8,0},{16,8},{24,16},{28,24},{20,28},{12,20},{4,12},{1,5},{9... | collective-permute-start | bytes 786440 | tf_op jit(solution)/shard_map/dispatch_gather/ppermute | solution.py:55
  179.9 6.4 %collective-permute-start.30 = (bf16[64,2048]{1,0:T(8,128)(2,1)S(1)}, bf16[64,2048]{1,0:T(8,128)(2,1)S(1)}, u32[]{:S(2)}, u32[]{:S(2)}) collective-permute-start(bf16[64,2048]{1,0:T(8,128)(2,1)S(1)} %get-tuple-element.122), channel_id=1, source_target_pairs={{0,8},{8,16},{16,24},{24,28},{28,20},{20,12},{12,4},{4,0},{1,9},{9... | collective-permute-start | bytes 786440 | tf_op jit(solution)/shard_map/combine_return/ppermute | solution.py:75
  180.9 6.4 %collective-permute-start.31 = (bf16[64,2048]{1,0:T(8,128)(2,1)S(1)}, bf16[64,2048]{1,0:T(8,128)(2,1)S(1)}, u32[]{:S(2)}, u32[]{:S(2)}) collective-permute-start(bf16[64,2048]{1,0:T(8,128)(2,1)S(1)} %get-tuple-element.123), channel_id=1, source_target_pairs={{0,4},{8,0},{16,8},{24,16},{28,24},{20,28},{12,20},{4,12},{1,5},{9... | collective-permute-start | bytes 786440 | tf_op jit(solution)/shard_map/combine_return/ppermute | solution.py:75
  183.2 7.5 %collective-permute-start.24 = (bf16[64,2048]{1,0:T(8,128)(2,1)S(1)}, bf16[64,2048]{1,0:T(8,128)(2,1)S(1)}, u32[]{:S(2)}, u32[]{:S(2)}) collective-permute-start(bf16[64,2048]{1,0:T(8,128)(2,1)S(1)} %collective-permute-done.22), channel_id=1, source_target_pairs={{0,8},{8,16},{16,24},{24,28},{28,20},{20,12},{12,4},{4,0},{1,9},{9... | collective-permute-start | bytes 786440 | tf_op jit(solution)/shard_map/dispatch_gather/ppermute | solution.py:55
  184.0 6.6 %collective-permute-start.25 = (bf16[64,2048]{1,0:T(8,128)(2,1)S(1)}, bf16[64,2048]{1,0:T(8,128)(2,1)S(1)}, u32[]{:S(2)}, u32[]{:S(2)}) collective-permute-start(bf16[64,2048]{1,0:T(8,128)(2,1)S(1)} %collective-permute-done.23), channel_id=1, source_target_pairs={{0,4},{8,0},{16,8},{24,16},{28,24},{20,28},{12,20},{4,12},{1,5},{9... | collective-permute-start | bytes 786440 | tf_op jit(solution)/shard_map/dispatch_gather/ppermute | solution.py:55
  188.6 21.3 %collective-permute-start.32 = (bf16[64,2048]{1,0:T(8,128)(2,1)S(1)}, bf16[64,2048]{1,0:T(8,128)(2,1)S(1)}, u32[]{:S(2)}, u32[]{:S(2)}) collective-permute-start(bf16[64,2048]{1,0:T(8,128)(2,1)S(1)} %get-tuple-element.126), channel_id=1, source_target_pairs={{0,8},{8,16},{16,24},{24,28},{28,20},{20,12},{12,4},{4,0},{1,9},{9... | collective-permute-start | bytes 786440 | tf_op jit(solution)/shard_map/combine_return/ppermute | solution.py:75
  189.1 20.8 %collective-permute-start.33 = (bf16[64,2048]{1,0:T(8,128)(2,1)S(1)}, bf16[64,2048]{1,0:T(8,128)(2,1)S(1)}, u32[]{:S(2)}, u32[]{:S(2)}) collective-permute-start(bf16[64,2048]{1,0:T(8,128)(2,1)S(1)} %get-tuple-element.127), channel_id=1, source_target_pairs={{0,4},{8,0},{16,8},{24,16},{28,24},{20,28},{12,20},{4,12},{1,5},{9... | collective-permute-start | bytes 786440 | tf_op jit(solution)/shard_map/combine_return/ppermute | solution.py:75
  190.7 9.2 %collective-permute-start.26 = (bf16[64,2048]{1,0:T(8,128)(2,1)S(1)}, bf16[64,2048]{1,0:T(8,128)(2,1)S(1)}, u32[]{:S(2)}, u32[]{:S(2)}) collective-permute-start(bf16[64,2048]{1,0:T(8,128)(2,1)S(1)} %collective-permute-done.24), channel_id=1, source_target_pairs={{0,8},{8,16},{16,24},{24,28},{28,20},{20,12},{12,4},{4,0},{1,9},{9... | collective-permute-start | bytes 786440 | tf_op jit(solution)/shard_map/dispatch_gather/ppermute | solution.py:55
  191.2 9.3 %collective-permute-start.27 = (bf16[64,2048]{1,0:T(8,128)(2,1)S(1)}, bf16[64,2048]{1,0:T(8,128)(2,1)S(1)}, u32[]{:S(2)}, u32[]{:S(2)}) collective-permute-start(bf16[64,2048]{1,0:T(8,128)(2,1)S(1)} %collective-permute-done.25), channel_id=1, source_target_pairs={{0,4},{8,0},{16,8},{24,16},{28,24},{20,28},{12,20},{4,12},{1,5},{9... | collective-permute-start | bytes 786440 | tf_op jit(solution)/shard_map/dispatch_gather/ppermute | solution.py:55
  192.7 13.7 %slice-start.3 = ((s8[12582912]{0:T(1024)(128)(4,1)}), s8[4194304]{0:T(1024)(128)(4,1)S(1)}, s32[]{:S(2)}) async-start(s8[12582912]{0:T(1024)(128)(4,1)} %bitcast.203), calls=%async_computation.5 | async-start | bytes 8388608
  200.7 5.7 %slice-start.4 = ((s8[12582912]{0:T(1024)(128)(4,1)}), s8[4194304]{0:T(1024)(128)(4,1)S(1)}, s32[]{:S(2)}) async-start(s8[12582912]{0:T(1024)(128)(4,1)} %bitcast.203), calls=%async_computation.6 | async-start | bytes 8388608
  200.8 5.7 %slice-start.5 = ((s8[12582912]{0:T(1024)(128)(4,1)}), s8[4194304]{0:T(1024)(128)(4,1)S(1)}, s32[]{:S(2)}) async-start(s8[12582912]{0:T(1024)(128)(4,1)} %bitcast.203), calls=%async_computation.7 | async-start | bytes 8388608
  200.8 12.6 %slice-start.8 = ((s8[6291456]{0:T(1024)(128)(4,1)}), s8[4194304]{0:T(1024)(128)(4,1)S(1)}, s32[]{:S(2)}) async-start(s8[6291456]{0:T(1024)(128)(4,1)} %bitcast.207), calls=%async_computation.10 | async-start | bytes 8388608
  206.5 6.8 %slice-start.9 = ((s8[6291456]{0:T(1024)(128)(4,1)}), s8[2097152]{0:T(1024)(128)(4,1)S(1)}, s32[]{:S(2)}) async-start(s8[6291456]{0:T(1024)(128)(4,1)} %bitcast.207), calls=%async_computation.11 | async-start | bytes 4194304
  211.2 8.6 %collective-permute-start.34 = (bf16[64,2048]{1,0:T(8,128)(2,1)S(1)}, bf16[64,2048]{1,0:T(8,128)(2,1)S(1)}, u32[]{:S(2)}, u32[]{:S(2)}) collective-permute-start(bf16[64,2048]{1,0:T(8,128)(2,1)S(1)} %get-tuple-element.130), channel_id=1, source_target_pairs={{0,8},{8,16},{16,24},{24,28},{28,20},{20,12},{12,4},{4,0},{1,9},{9... | collective-permute-start | bytes 786440 | tf_op jit(solution)/shard_map/combine_return/ppermute | solution.py:75
  212.9 8.4 %collective-permute-start.35 = (bf16[64,2048]{1,0:T(8,128)(2,1)S(1)}, bf16[64,2048]{1,0:T(8,128)(2,1)S(1)}, u32[]{:S(2)}, u32[]{:S(2)}) collective-permute-start(bf16[64,2048]{1,0:T(8,128)(2,1)S(1)} %get-tuple-element.131), channel_id=1, source_target_pairs={{0,4},{8,0},{16,8},{24,16},{28,24},{20,28},{12,20},{4,12},{1,5},{9... | collective-permute-start | bytes 786440 | tf_op jit(solution)/shard_map/combine_return/ppermute | solution.py:75
  221.4 6.4 %collective-permute-start.36 = (bf16[64,2048]{1,0:T(8,128)(2,1)S(1)}, bf16[64,2048]{1,0:T(8,128)(2,1)S(1)}, u32[]{:S(2)}, u32[]{:S(2)}) collective-permute-start(bf16[64,2048]{1,0:T(8,128)(2,1)S(1)} %get-tuple-element.134), channel_id=1, source_target_pairs={{0,8},{8,16},{16,24},{24,28},{28,20},{20,12},{12,4},{4,0},{1,9},{9... | collective-permute-start | bytes 786440 | tf_op jit(solution)/shard_map/combine_return/ppermute | solution.py:75
  222.0 6.4 %collective-permute-start.37 = (bf16[64,2048]{1,0:T(8,128)(2,1)S(1)}, bf16[64,2048]{1,0:T(8,128)(2,1)S(1)}, u32[]{:S(2)}, u32[]{:S(2)}) collective-permute-start(bf16[64,2048]{1,0:T(8,128)(2,1)S(1)} %get-tuple-element.135), channel_id=1, source_target_pairs={{0,4},{8,0},{16,8},{24,16},{28,24},{20,28},{12,20},{4,12},{1,5},{9... | collective-permute-start | bytes 786440 | tf_op jit(solution)/shard_map/combine_return/ppermute | solution.py:75
  228.5 6.4 %collective-permute-start.38 = (bf16[64,2048]{1,0:T(8,128)(2,1)S(1)}, bf16[64,2048]{1,0:T(8,128)(2,1)S(1)}, u32[]{:S(2)}, u32[]{:S(2)}) collective-permute-start(bf16[64,2048]{1,0:T(8,128)(2,1)S(1)} %get-tuple-element.138), channel_id=1, source_target_pairs={{0,8},{8,16},{16,24},{24,28},{28,20},{20,12},{12,4},{4,0},{1,9},{9... | collective-permute-start | bytes 786440 | tf_op jit(solution)/shard_map/combine_return/ppermute | solution.py:75
  228.6 6.4 %collective-permute-start.39 = (bf16[64,2048]{1,0:T(8,128)(2,1)S(1)}, bf16[64,2048]{1,0:T(8,128)(2,1)S(1)}, u32[]{:S(2)}, u32[]{:S(2)}) collective-permute-start(bf16[64,2048]{1,0:T(8,128)(2,1)S(1)} %get-tuple-element.139), channel_id=1, source_target_pairs={{0,4},{8,0},{16,8},{24,16},{28,24},{20,28},{12,20},{4,12},{1,5},{9... | collective-permute-start | bytes 786440 | tf_op jit(solution)/shard_map/combine_return/ppermute | solution.py:75
  235.1 8.3 %copy-start.6 = (f32[2048]{0:T(1024)S(1)}, f32[2048]{0:T(1024)}, u32[]{:S(2)}) copy-start(f32[2048]{0:T(1024)} %param.20) | copy-start | bytes 24580
  235.1 6.4 %collective-permute-start.40 = (bf16[64,2048]{1,0:T(8,128)(2,1)S(1)}, bf16[64,2048]{1,0:T(8,128)(2,1)S(1)}, u32[]{:S(2)}, u32[]{:S(2)}) collective-permute-start(bf16[64,2048]{1,0:T(8,128)(2,1)S(1)} %get-tuple-element.142), channel_id=1, source_target_pairs={{0,8},{8,16},{16,24},{24,28},{28,20},{20,12},{12,4},{4,0},{1,9},{9... | collective-permute-start | bytes 786440 | tf_op jit(solution)/shard_map/combine_return/ppermute | solution.py:75
  236.7 6.4 %collective-permute-start.41 = (bf16[64,2048]{1,0:T(8,128)(2,1)S(1)}, bf16[64,2048]{1,0:T(8,128)(2,1)S(1)}, u32[]{:S(2)}, u32[]{:S(2)}) collective-permute-start(bf16[64,2048]{1,0:T(8,128)(2,1)S(1)} %get-tuple-element.143), channel_id=1, source_target_pairs={{0,4},{8,0},{16,8},{24,16},{28,24},{20,28},{12,20},{4,12},{1,5},{9... | collective-permute-start | bytes 786440 | tf_op jit(solution)/shard_map/combine_return/ppermute | solution.py:75
  243.1 1.9 copy-start.1

commit v6 on v5

v6 whole, which is shorter than its diff:
```python
import jax
import jax.numpy as jnp
from jax import lax
from jax.sharding import PartitionSpec as P


def rms_scale(values, scale_gain):
    mean_square = jnp.mean(values * values, axis=-1, keepdims=True)
    return values * lax.rsqrt(mean_square + 1e-06) * scale_gain


def ring_order(n):
    if n % 2:
        return list(range(n))
    return list(range(0, n, 2)) + list(range(n - 1, 0, -2))


def ring_all_gather(block, ring, pos):
    n = len(ring)
    half = block.shape[0] // 2
    forward = [(ring[q], ring[(q + 1) % n]) for q in range(n)]
    backward = [(ring[q], ring[(q - 1) % n]) for q in range(n)]
    got_fwd, got_bwd = block[:half], block[half:]
    arrived = []
    for step in range(n - 1):
        got_fwd, got_bwd = lax.optimization_barrier(
            (lax.ppermute(got_fwd, "ep", forward), lax.ppermute(got_bwd, "ep", backward))
        )
        arrived.append((got_fwd, got_bwd))
    return arrived


def ring_reduce_scatter_steps(pieces, own, ring):
    n = len(ring)
    forward = [(ring[q], ring[(q + 1) % n]) for q in range(n)]
    backward = [(ring[q], ring[(q - 1) % n]) for q in range(n)]
    got_fwd = got_bwd = None
    for step in range(n - 1):
        send_fwd, send_bwd = pieces[step]
        if step:
            send_fwd = send_fwd + got_fwd
            send_bwd = send_bwd + got_bwd
        send_fwd, send_bwd = lax.optimization_barrier(
            (send_fwd.astype(jnp.bfloat16), send_bwd.astype(jnp.bfloat16))
        )
        got_fwd, got_bwd = lax.optimization_barrier(
            (lax.ppermute(send_fwd, "ep", forward), lax.ppermute(send_bwd, "ep", backward))
        )
        got_fwd = got_fwd.astype(jnp.float32)
        got_bwd = got_bwd.astype(jnp.float32)
    half = own.shape[0] // 2
    return jnp.concatenate([own[:half] + got_fwd, own[half:] + got_bwd], axis=0)


def expert_mix(rows, weights, gate_up, down):
    hidden_width = down.shape[1]
    total = None
    for e in range(gate_up.shape[0]):
        projected_up = jnp.dot(rows, gate_up[e], preferred_element_type=jnp.float32)
        activated = (
            jax.nn.silu(projected_up[:, :hidden_width]) * projected_up[:, hidden_width:]
        ).astype(jnp.bfloat16)
        expert_out = jnp.dot(activated, down[e], preferred_element_type=jnp.float32).astype(
            jnp.bfloat16
        )
        term = weights[:, e : e + 1] * expert_out.astype(jnp.float32)
        total = term if total is None else total + term
    return total


def split_exact(values):
    first = lax.reduce_precision(values, exponent_bits=8, mantissa_bits=7)
    rest = values - first
    second = lax.reduce_precision(rest, exponent_bits=8, mantissa_bits=7)
    third = rest - second
    return jnp.concatenate([first, second, third], axis=-1).astype(jnp.bfloat16)


def join_exact(parts, count):
    parts = parts.astype(jnp.float32)
    return (parts[:, :count] + parts[:, count : 2 * count]) + parts[:, 2 * count : 3 * count]


def body(
    residual, attn_out, out_weight, post_gain, gate_up, down, route_ids, route_weight, final_gain
):
    row_count, model_width = residual.shape
    ep_size = lax.axis_size("ep")
    me = lax.axis_index("ep")
    local_experts = gate_up.shape[0]
    slice_width = out_weight.shape[0]
    half = row_count // 2
    ring = ring_order(ep_size)
    ring_index = jnp.array(ring, dtype=jnp.int32)
    pos = jnp.array([ring.index(p) for p in range(ep_size)], dtype=jnp.int32)[me]

    with jax.named_scope("route_weights"):
        expert_ids = jnp.arange(local_experts * ep_size, dtype=jnp.int32)
        dense_weight = jnp.sum(
            jnp.where(route_ids[:, :, None] == expert_ids, route_weight[:, :, None], 0.0), axis=1
        )
        dense_weight = dense_weight.reshape(row_count, ep_size, local_experts)
        own_weight = lax.dynamic_index_in_dim(dense_weight, me, 1, keepdims=False)

    with jax.named_scope("column_exchange"):
        columns = attn_out.reshape(row_count, ep_size, slice_width)
        pad = (-3 * local_experts) % 128
        by_shift = {}
        shifts = []
        for k in range(1, ep_size):
            for shift in (k, ep_size - k):
                if shift not in shifts:
                    shifts.append(shift)
        for shift in shifts:
            target = ring_index[(pos + shift) % ep_size]
            payload = jnp.concatenate(
                [
                    lax.dynamic_index_in_dim(columns, target, 1, keepdims=False),
                    split_exact(lax.dynamic_index_in_dim(dense_weight, target, 1, keepdims=False)),
                    jnp.zeros((row_count, pad), jnp.bfloat16),
                ],
                axis=1,
            )
            pairs = [(ring[q], ring[(q + shift) % ep_size]) for q in range(ep_size)]
            by_shift[shift] = lax.ppermute(payload, "ep", pairs)

    def shift_rows(shift, rows):
        got = by_shift[shift][rows]
        return got[:, :slice_width], join_exact(got[:, slice_width:], local_experts)

    with jax.named_scope("out_projection"):
        pieces = []
        step_weights = []
        for step in range(ep_size - 1):
            cols_fwd, w_fwd = shift_rows(step + 1, slice(0, half))
            cols_bwd, w_bwd = shift_rows(ep_size - 1 - step, slice(half, row_count))
            part = jnp.dot(
                jnp.concatenate([cols_fwd, cols_bwd], axis=0),
                out_weight,
                preferred_element_type=jnp.float32,
            )
            pieces.append((part[:half], part[half:]))
            step_weights.append((w_fwd, w_bwd))
        own_columns = lax.dynamic_index_in_dim(columns, me, 1, keepdims=False)
        own_part = jnp.dot(own_columns, out_weight, preferred_element_type=jnp.float32)
        projected = ring_reduce_scatter_steps(pieces, own_part, ring)
        middle = (residual.astype(jnp.float32) + projected).astype(jnp.bfloat16)

    normed = rms_scale(middle.astype(jnp.float32), post_gain).astype(jnp.bfloat16)
    with jax.named_scope("dispatch_gather"):
        arrived = ring_all_gather(normed, ring, pos)

    with jax.named_scope("local_experts"):
        first = ep_size // 2
        chunks = [list(range(first)), list(range(first, ep_size - 1))]
        pieces = [None] * (ep_size - 1)
        own_mix = None
        for c, steps in enumerate(chunks):
            rows_in = []
            weights_in = []
            for step in steps:
                rows_in += list(arrived[step])
                weights_in += list(step_weights[step])
            if c == len(chunks) - 1:
                rows_in.append(normed)
                weights_in.append(own_weight)
            mixed = expert_mix(
                jnp.concatenate(rows_in, axis=0), jnp.concatenate(weights_in, axis=0), gate_up, down
            )
            for i, step in enumerate(steps):
                pieces[step] = (mixed[(2 * i) * half : (2 * i + 1) * half],
                                mixed[(2 * i + 1) * half : (2 * i + 2) * half])
            if c == len(chunks) - 1:
                own_mix = mixed[2 * len(steps) * half :]

    with jax.named_scope("combine_return"):
        combined = ring_reduce_scatter_steps(pieces, own_mix, ring)
    updated = middle.astype(jnp.float32) + combined
    return (updated.astype(jnp.bfloat16), rms_scale(updated, final_gain).astype(jnp.bfloat16))


def solution(mesh):
    in_specs = (
        P(("rep", "ep"), None),
        P(("rep", "ep"), None),
        P("ep", None),
        P(),
        P("ep", None, None),
        P("ep", None, None),
        P(("rep", "ep"), None),
        P(("rep", "ep"), None),
        P(),
    )
    out_specs = (P(("rep", "ep"), None), P(("rep", "ep"), None))
    return jax.shard_map(body, mesh=mesh, in_specs=in_specs, out_specs=out_specs, check_vma=False)
```

time: 246 us -> 274 us (1.11)
  local copies, waits for them, and re-layouts: 9.08 us -> 48.9 us
  between operations: 40.8 us -> 19.6 us
  starting transfers between devices: 55.4 us -> 62.4 us
  waiting for transfers between devices: 92.7 us -> 97.6 us
  other arithmetic: 17.1 us -> 12.9 us
    ppermute x7 -> x14, waiting for transfers between devices: 21.6 us -> 44.7 us  [ring_reduce_scatter_steps(): lax.ppermute(send_fwd, 'ep', forward)]
    ppermute x14 -> x7, waiting for transfers between devices: 20 us -> 2.14 us  [body(): by_shift[shift] = lax.ppermute(payload, 'ep', pairs)]
    another operation x0 -> x22, local copies, waits for them, and re-layouts: none -> 14.7 us
    ppermute x7 -> x14, waiting for transfers between devices: 6.67 us -> 19.7 us  [ring_reduce_scatter_steps(): lax.ppermute(send_bwd, 'ep', backward)]
    all_to_all x2 -> x0, waiting for transfers between devices: 12.5 us -> none  [the longest x1 8.28 us: body(): lax.all_to_all(columns, 'ep', split_axis=0, concat_axis=0, tiled=True)]
    concatenate x0 -> x7, local copies, waits for them, and re-layouts: none -> 11.6 us  [body(): jnp.concatenate([lax.dynamic_index_in_dim(columns, target, 1, keepdims=Fa...]
    dynamic_slice x2 -> x9, local copies, waits for them, and re-layouts: 0.78 us -> 11.6 us  [the longest x8 10 us: body(): lax.dynamic_index_in_dim(columns, target, 1, keepdims=False)]
    all_to_all x2 -> x0, starting transfers between devices: 10.8 us -> none  [the longest x1 7.28 us: body(): lax.all_to_all(dense_weight, 'ep', split_axis=0, concat_axis=0, tiled=True)]
  transfers between devices with their start and end apart: 44 -> 49, of which waited for: 37 -> 37; matrix products, arithmetic and copies ran while one was open for 8% -> 23% of each run, Pallas kernels for 0% -> 0%
where the time goes in v6:
time: 274 us; the launch traced here: 273 us
  waiting for transfers between devices  97.6 us (36%)
  starting transfers between devices  62.4 us (23%)
  local copies, waits for them, and re-layouts  48.9 us (18%)
  matrix products  31.2 us (11%)
  between operations  19.6 us (7%)
  other arithmetic  12.9 us (5%)
    ppermute x14, waiting for transfers between devices, ring_reduce_scatter_steps(): lax.ppermute(send_fwd, 'ep', forward)  44.7 us
    ppermute x7, waiting for transfers between devices, ring_all_gather(): lax.ppermute(got_fwd, 'ep', forward)  25.9 us
    ppermute x14, waiting for transfers between devices, ring_reduce_scatter_steps(): lax.ppermute(send_bwd, 'ep', backward)  19.7 us
    dot_general x4, matrix products, expert_mix(): projected_up = jnp.dot(rows, gate_up[e], preferred_element_type=jnp.float32)  18.1 us
    ppermute x14, starting transfers between devices, ring_reduce_scatter_steps(): lax.ppermute(send_fwd, 'ep', forward)  17.8 us
    ppermute x14, starting transfers between devices, ring_reduce_scatter_steps(): lax.ppermute(send_bwd, 'ep', backward)  15.4 us
    ppermute x7, starting transfers between devices, body(): by_shift[shift] = lax.ppermute(payload, 'ep', pairs)  14.8 us
    another operation x22, local copies, waits for them, and re-layouts  14.7 us
  transfers between devices with their start and end apart: 49, of which 37 were waited for; matrix products, arithmetic and copies ran while one was open for 23% of the time, Pallas kernels for 0%

profile of v6, /device:TPU:0, one launch (start us, length us, event | category | flops | bytes accessed | tf_op | source)
XLA Modules:
  0.0 272.5 jit_solution(7073622712411176853)
XLA Ops:
  6.7 1.6 fusion.147
  23.7 1.6 copy.153
  26.1 1.7 copy.155
  27.8 1.7 concatenate.81
  29.5 3.0 %collective-permute-start = (bf16[128,640]{1,0:T(8,128)(2,1)}, bf16[128,640]{1,0:T(8,128)(2,1)}, u32[]{:S(2)}, u32[]{:S(2)}) collective-permute-start(bf16[128,640]{1,0:T(8,128)(2,1)} %concatenate.81), channel_id=1, source_target_pairs={{0,4},{8,0},{16,8},{24,16},{28,24},{20,28},{12,20},{4,12},{1,5},{9... | collective-permute-start | bytes 491528 | tf_op jit(solution)/shard_map/column_exchange/ppermute | solution.py:125
  34.7 1.7 copy.159
  36.3 1.7 concatenate.82
  40.3 1.7 copy.163
  42.0 1.7 concatenate.84
  43.7 3.0 %collective-permute-start.2 = (bf16[128,640]{1,0:T(8,128)(2,1)}, bf16[128,640]{1,0:T(8,128)(2,1)}, u32[]{:S(2)}, u32[]{:S(2)}) collective-permute-start(bf16[128,640]{1,0:T(8,128)(2,1)} %concatenate.84), channel_id=1, source_target_pairs={{0,12},{8,4},{16,0},{24,8},{28,16},{20,24},{12,28},{4,20},{1,13},{... | collective-permute-start | bytes 491528 | tf_op jit(solution)/shard_map/column_exchange/ppermute | solution.py:125
  48.9 1.7 copy.167
  50.6 1.7 concatenate.85
  54.7 1.7 copy.171
  56.4 1.7 concatenate.87
  58.1 3.9 %collective-permute-start.4 = (bf16[128,640]{1,0:T(8,128)(2,1)}, bf16[128,640]{1,0:T(8,128)(2,1)}, u32[]{:S(2)}, u32[]{:S(2)}) collective-permute-start(bf16[128,640]{1,0:T(8,128)(2,1)} %concatenate.87), channel_id=1, source_target_pairs={{0,20},{8,12},{16,4},{24,0},{28,8},{20,16},{12,24},{4,28},{1,21},{... | collective-permute-start | bytes 491528 | tf_op jit(solution)/shard_map/column_exchange/ppermute | solution.py:125
  68.0 1.7 concatenate.88
  73.1 4.8 %collective-permute-start.6 = (bf16[128,640]{1,0:T(8,128)(2,1)S(1)}, bf16[128,640]{1,0:T(8,128)(2,1)S(1)}, u32[]{:S(2)}, u32[]{:S(2)}) collective-permute-start(bf16[128,640]{1,0:T(8,128)(2,1)S(1)} %copy-done.3), channel_id=1, source_target_pairs={{0,28},{8,20},{16,12},{24,4},{28,0},{20,8},{12,16},{4,24},{1,29},{... | collective-permute-start | bytes 491528 | tf_op jit(solution)/shard_map/column_exchange/ppermute | solution.py:125
  80.3 2.1 collective-permute-start.8
  84.6 2.1 collective-permute-done.5
  90.1 1.8 collective-permute-start.10
  93.3 5.1 %collective-permute-done.10 = bf16[64,2048]{1,0:T(8,128)(2,1)S(1)} collective-permute-done((bf16[64,2048]{1,0:T(8,128)(2,1)S(1)}, bf16[64,2048]{1,0:T(8,128)(2,1)S(1)}, u32[]{:S(2)}, u32[]{:S(2)}) %collective-permute-start.10) | collective-permute-done | bytes 262176 | tf_op jit(solution)/shard_map/out_projection/ppermute | solution.py:47
  98.4 2.7 collective-permute-done.9
  101.3 2.0 collective-permute-start.12
  103.4 4.2 %collective-permute-done.11 = bf16[64,2048]{1,0:T(8,128)(2,1)S(1)} collective-permute-done((bf16[64,2048]{1,0:T(8,128)(2,1)S(1)}, bf16[64,2048]{1,0:T(8,128)(2,1)S(1)}, u32[]{:S(2)}, u32[]{:S(2)}) %collective-permute-start.11) | collective-permute-done | bytes 262176 | tf_op jit(solution)/shard_map/out_projection/ppermute | solution.py:47
  110.9 3.5 %collective-permute-done.13 = bf16[64,2048]{1,0:T(8,128)(2,1)S(1)} collective-permute-done((bf16[64,2048]{1,0:T(8,128)(2,1)S(1)}, bf16[64,2048]{1,0:T(8,128)(2,1)S(1)}, u32[]{:S(2)}, u32[]{:S(2)}) %collective-permute-start.13) | collective-permute-done | bytes 262176 | tf_op jit(solution)/shard_map/out_projection/ppermute | solution.py:47
  116.0 2.5 collective-permute-start.15
  119.4 5.2 %collective-permute-done.15 = bf16[64,2048]{1,0:T(8,128)(2,1)S(1)} collective-permute-done((bf16[64,2048]{1,0:T(8,128)(2,1)S(1)}, bf16[64,2048]{1,0:T(8,128)(2,1)S(1)}, u32[]{:S(2)}, u32[]{:S(2)}) %collective-permute-start.15) | collective-permute-done | bytes 262176 | tf_op jit(solution)/shard_map/out_projection/ppermute | solution.py:47
  124.6 2.8 %collective-permute-done.16 = bf16[64,2048]{1,0:T(8,128)(2,1)S(1)} collective-permute-done((bf16[64,2048]{1,0:T(8,128)(2,1)S(1)}, bf16[64,2048]{1,0:T(8,128)(2,1)S(1)}, u32[]{:S(2)}, u32[]{:S(2)}) %collective-permute-start.16) | collective-permute-done | bytes 262176 | tf_op jit(solution)/shard_map/out_projection/ppermute | solution.py:47
  127.9 1.7 collective-permute-start.18
  130.5 5.4 %collective-permute-done.17 = bf16[64,2048]{1,0:T(8,128)(2,1)S(1)} collective-permute-done((bf16[64,2048]{1,0:T(8,128)(2,1)S(1)}, bf16[64,2048]{1,0:T(8,128)(2,1)S(1)}, u32[]{:S(2)}, u32[]{:S(2)}) %collective-permute-start.17) | collective-permute-done | bytes 262176 | tf_op jit(solution)/shard_map/out_projection/ppermute | solution.py:47
  136.1 1.6 collective-permute-start.19
  139.1 5.0 %collective-permute-done.19 = bf16[64,2048]{1,0:T(8,128)(2,1)S(1)} collective-permute-done((bf16[64,2048]{1,0:T(8,128)(2,1)S(1)}, bf16[64,2048]{1,0:T(8,128)(2,1)S(1)}, u32[]{:S(2)}, u32[]{:S(2)}) %collective-permute-start.19) | collective-permute-done | bytes 262176 | tf_op jit(solution)/shard_map/out_projection/ppermute | solution.py:47
  148.7 3.5 %collective-permute-done.21 = bf16[64,2048]{1,0:T(8,128)(2,1)S(1)} collective-permute-done((bf16[64,2048]{1,0:T(8,128)(2,1)S(1)}, bf16[64,2048]{1,0:T(8,128)(2,1)S(1)}, u32[]{:S(2)}, u32[]{:S(2)}) %collective-permute-start.21) | collective-permute-done | bytes 262176 | tf_op jit(solution)/shard_map/dispatch_gather/ppermute | solution.py:27
  152.2 2.2 collective-permute-done.22
  156.5 6.3 %collective-permute-done.23 = bf16[64,2048]{1,0:T(8,128)(2,1)S(1)} collective-permute-done((bf16[64,2048]{1,0:T(8,128)(2,1)S(1)}, bf16[64,2048]{1,0:T(8,128)(2,1)S(1)}, u32[]{:S(2)}, u32[]{:S(2)}) %collective-permute-start.23) | collective-permute-done | bytes 262176 | tf_op jit(solution)/shard_map/dispatch_gather/ppermute | solution.py:27
  162.8 1.8 collective-permute-done.24
  164.9 1.8 collective-permute-start.26
  166.7 4.3 %collective-permute-done.25 = bf16[64,2048]{1,0:T(8,128)(2,1)S(1)} collective-permute-done((bf16[64,2048]{1,0:T(8,128)(2,1)S(1)}, bf16[64,2048]{1,0:T(8,128)(2,1)S(1)}, u32[]{:S(2)}, u32[]{:S(2)}) %collective-permute-start.25) | collective-permute-done | bytes 262176 | tf_op jit(solution)/shard_map/dispatch_gather/ppermute | solution.py:27
  171.3 2.0 collective-permute-start.28
  173.3 4.3 %collective-permute-done.27 = bf16[64,2048]{1,0:T(8,128)(2,1)S(1)} collective-permute-done((bf16[64,2048]{1,0:T(8,128)(2,1)S(1)}, bf16[64,2048]{1,0:T(8,128)(2,1)S(1)}, u32[]{:S(2)}, u32[]{:S(2)}) %collective-permute-start.27) | collective-permute-done | bytes 262176 | tf_op jit(solution)/shard_map/dispatch_gather/ppermute | solution.py:27
  177.7 5.7 %fusion.4 = f32[512,1536]{1,0:T(8,128)S(1)} fusion(bf16[512,2048]{1,0:T(8,128)(2,1)S(1)} %constant_dynamic-update-slice_fusion.7, bf16[2,2048,1536]{2,1,0:T(8,128)(2,1)} %param.15), kind=kOutput, calls=%fused_computation.4 | convolution fusion | flops 3221225472 | bytes 11534336 | tf_op jit(solution)/shard_map/local_experts/dot_general | solution.py:59
  184.2 3.4 %fusion = f32[512,1536]{1,0:T(8,128)S(1)} fusion(bf16[512,2048]{1,0:T(8,128)(2,1)S(1)} %constant_dynamic-update-slice_fusion.7, bf16[2,2048,1536]{2,1,0:T(8,128)(2,1)S(1)} %bitcast.151), kind=kOutput, calls=%fused_computation | convolution fusion | flops 3221225472 | bytes 11534336 | tf_op jit(solution)/shard_map/local_experts/dot_general | solution.py:59
  187.6 1.8 fusion.23
  189.4 4.0 %fusion.148 = (bf16[512,2048]{1,0:T(8,128)(2,1)S(1)}, f32[512,2048]{1,0:T(8,128)}) fusion(bf16[2,768,2048]{2,1,0:T(8,128)(2,1)S(1)} %bitcast.155, f32[512,1536]{1,0:T(8,128)S(1)} %fusion, f32[512]{0:T(512)S(1)} %bitcast.149, bf16[512,2048]{1,0:T(8,128)(2,1)S(1)} %fusion.23, f32[512]{0:T(512)S(1)} %bitcast.148), kind=kOutput, calls=%fused_computation.276 | convolution fusion | flops 1620312064 | bytes 14684160 | tf_op jit(solution)/shard_map/local_experts/dot_general | solution.py:63
  193.6 2.0 collective-permute-start.36
  196.2 2.0 collective-permute-start.30
  198.2 4.4 %collective-permute-done.35 = bf16[64,2048]{1,0:T(8,128)(2,1)S(1)} collective-permute-done((bf16[64,2048]{1,0:T(8,128)(2,1)S(1)}, bf16[64,2048]{1,0:T(8,128)(2,1)S(1)}, u32[]{:S(2)}, u32[]{:S(2)}) %collective-permute-start.35) | collective-permute-done | bytes 262176 | tf_op jit(solution)/shard_map/combine_return/ppermute | solution.py:47
  204.1 1.8 collective-permute-start.37
  206.1 1.9 collective-permute-done.29
  214.0 1.6 collective-permute-start.40
  216.5 1.6 collective-permute-start.34
  218.2 5.7 %collective-permute-done.33 = bf16[64,2048]{1,0:T(8,128)(2,1)S(1)} collective-permute-done((bf16[64,2048]{1,0:T(8,128)(2,1)S(1)}, bf16[64,2048]{1,0:T(8,128)(2,1)S(1)}, u32[]{:S(2)}, u32[]{:S(2)}) %collective-permute-start.33) | collective-permute-done | bytes 262176 | tf_op jit(solution)/shard_map/dispatch_gather/ppermute | solution.py:27
  224.2 5.7 %fusion.6 = f32[512,1536]{1,0:T(8,128)S(1)} fusion(bf16[512,2048]{1,0:T(8,128)(2,1)S(1)} %constant_dynamic-update-slice_fusion, bf16[2,2048,1536]{2,1,0:T(8,128)(2,1)} %param.15), kind=kOutput, calls=%fused_computation.6 | convolution fusion | flops 3221225472 | bytes 11534336 | tf_op jit(solution)/shard_map/local_experts/dot_general | solution.py:59
  229.9 3.4 %fusion.2 = f32[512,1536]{1,0:T(8,128)S(1)} fusion(bf16[512,2048]{1,0:T(8,128)(2,1)S(1)} %constant_dynamic-update-slice_fusion, bf16[2,2048,1536]{2,1,0:T(8,128)(2,1)S(1)} %bitcast.153), kind=kOutput, calls=%fused_computation.2 | convolution fusion | flops 3221225472 | bytes 11534336 | tf_op jit(solution)/shard_map/local_experts/dot_general | solution.py:59
  234.7 3.5 %collective-permute-start.41 = (bf16[64,2048]{1,0:T(8,128)(2,1)S(1)}, bf16[64,2048]{1,0:T(8,128)(2,1)S(1)}, u32[]{:S(2)}, u32[]{:S(2)}) collective-permute-start(bf16[64,2048]{1,0:T(8,128)(2,1)S(1)} %get-tuple-element.126), channel_id=1, source_target_pairs={{0,8},{8,16},{16,24},{24,28},{28,20},{20,12},{12,4},{4,0},{1,9},{9... | collective-permute-start | bytes 786440 | tf_op jit(solution)/shard_map/combine_return/ppermute | solution.py:47
  238.2 1.8 fusion.20
  240.1 1.9 multiply_add_fusion.1
  242.1 3.8 %collective-permute-done.42 = bf16[64,2048]{1,0:T(8,128)(2,1)S(1)} collective-permute-done((bf16[64,2048]{1,0:T(8,128)(2,1)S(1)}, bf16[64,2048]{1,0:T(8,128)(2,1)S(1)}, u32[]{:S(2)}, u32[]{:S(2)}) %collective-permute-start.42) | collective-permute-done | bytes 262176 | tf_op jit(solution)/shard_map/combine_return/ppermute | solution.py:47
  246.0 3.9 %collective-permute-start.43 = (bf16[64,2048]{1,0:T(8,128)(2,1)S(1)}, bf16[64,2048]{1,0:T(8,128)(2,1)S(1)}, u32[]{:S(2)}, u32[]{:S(2)}) collective-permute-start(bf16[64,2048]{1,0:T(8,128)(2,1)S(1)} %get-tuple-element.130), channel_id=1, source_target_pairs={{0,8},{8,16},{16,24},{24,28},{28,20},{20,12},{12,4},{4,0},{1,9},{9... | collective-permute-start | bytes 786440 | tf_op jit(solution)/shard_map/combine_return/ppermute | solution.py:47
  249.9 3.9 %collective-permute-done.43 = bf16[64,2048]{1,0:T(8,128)(2,1)S(1)} collective-permute-done((bf16[64,2048]{1,0:T(8,128)(2,1)S(1)}, bf16[64,2048]{1,0:T(8,128)(2,1)S(1)}, u32[]{:S(2)}, u32[]{:S(2)}) %collective-permute-start.43) | collective-permute-done | bytes 262176 | tf_op jit(solution)/shard_map/combine_return/ppermute | solution.py:47
  253.8 2.5 collective-permute-done.44
  258.5 4.3 %collective-permute-done.45 = bf16[64,2048]{1,0:T(8,128)(2,1)S(1)} collective-permute-done((bf16[64,2048]{1,0:T(8,128)(2,1)S(1)}, bf16[64,2048]{1,0:T(8,128)(2,1)S(1)}, u32[]{:S(2)}, u32[]{:S(2)}) %collective-permute-start.45) | collective-permute-done | bytes 262176 | tf_op jit(solution)/shard_map/combine_return/ppermute | solution.py:47
  264.1 1.7 collective-permute-start.48
  265.8 4.3 %collective-permute-done.47 = bf16[64,2048]{1,0:T(8,128)(2,1)S(1)} collective-permute-done((bf16[64,2048]{1,0:T(8,128)(2,1)S(1)}, bf16[64,2048]{1,0:T(8,128)(2,1)S(1)}, u32[]{:S(2)}, u32[]{:S(2)}) %collective-permute-start.47) | collective-permute-done | bytes 262176 | tf_op jit(solution)/shard_map/combine_return/ppermute | solution.py:47
  (207 shorter events, 65.8 us)
Async XLA Ops:
  0.6 70.6 %copy-start = (bf16[512,2048]{1,0:T(8,128)(2,1)S(1)}, bf16[512,2048]{1,0:T(8,128)(2,1)}, u32[]{:S(2)}) copy-start(bf16[512,2048]{1,0:T(8,128)(2,1)} %param.13) | copy-start | bytes 6291460
  29.5 42.2 %collective-permute-start = (bf16[128,640]{1,0:T(8,128)(2,1)}, bf16[128,640]{1,0:T(8,128)(2,1)}, u32[]{:S(2)}, u32[]{:S(2)}) collective-permute-start(bf16[128,640]{1,0:T(8,128)(2,1)} %concatenate.81), channel_id=1, source_target_pairs={{0,4},{8,0},{16,8},{24,16},{28,24},{20,28},{12,20},{4,12},{1,5},{9... | collective-permute-start | bytes 491528 | tf_op jit(solution)/shard_map/column_exchange/ppermute | solution.py:125
  38.0 35.1 %collective-permute-start.1 = (bf16[128,640]{1,0:T(8,128)(2,1)}, bf16[128,640]{1,0:T(8,128)(2,1)}, u32[]{:S(2)}, u32[]{:S(2)}) collective-permute-start(bf16[128,640]{1,0:T(8,128)(2,1)} %concatenate.82), channel_id=1, source_target_pairs={{0,8},{8,16},{16,24},{24,28},{28,20},{20,12},{12,4},{4,0},{1,9},{9... | collective-permute-start | bytes 491528 | tf_op jit(solution)/shard_map/column_exchange/ppermute | solution.py:125
  43.7 35.7 %collective-permute-start.2 = (bf16[128,640]{1,0:T(8,128)(2,1)}, bf16[128,640]{1,0:T(8,128)(2,1)}, u32[]{:S(2)}, u32[]{:S(2)}) collective-permute-start(bf16[128,640]{1,0:T(8,128)(2,1)} %concatenate.84), channel_id=1, source_target_pairs={{0,12},{8,4},{16,0},{24,8},{28,16},{20,24},{12,28},{4,20},{1,13},{... | collective-permute-start | bytes 491528 | tf_op jit(solution)/shard_map/column_exchange/ppermute | solution.py:125
  52.2 28.0 %collective-permute-start.3 = (bf16[128,640]{1,0:T(8,128)(2,1)}, bf16[128,640]{1,0:T(8,128)(2,1)}, u32[]{:S(2)}, u32[]{:S(2)}) collective-permute-start(bf16[128,640]{1,0:T(8,128)(2,1)} %concatenate.85), channel_id=1, source_target_pairs={{0,16},{8,24},{16,28},{24,20},{28,12},{20,4},{12,0},{4,8},{1,17},{... | collective-permute-start | bytes 491528 | tf_op jit(solution)/shard_map/column_exchange/ppermute | solution.py:125
  58.1 25.6 %collective-permute-start.4 = (bf16[128,640]{1,0:T(8,128)(2,1)}, bf16[128,640]{1,0:T(8,128)(2,1)}, u32[]{:S(2)}, u32[]{:S(2)}) collective-permute-start(bf16[128,640]{1,0:T(8,128)(2,1)} %concatenate.87), channel_id=1, source_target_pairs={{0,20},{8,12},{16,4},{24,0},{28,8},{20,16},{12,24},{4,28},{1,21},{... | collective-permute-start | bytes 491528 | tf_op jit(solution)/shard_map/column_exchange/ppermute | solution.py:125
  72.1 14.6 %collective-permute-start.5 = (bf16[128,640]{1,0:T(8,128)(2,1)S(1)}, bf16[128,640]{1,0:T(8,128)(2,1)S(1)}, u32[]{:S(2)}, u32[]{:S(2)}) collective-permute-start(bf16[128,640]{1,0:T(8,128)(2,1)S(1)} %copy-done.4), channel_id=1, source_target_pairs={{0,24},{8,28},{16,20},{24,12},{28,4},{20,0},{12,8},{4,16},{1,25},{... | collective-permute-start | bytes 491528 | tf_op jit(solution)/shard_map/column_exchange/ppermute | solution.py:125
  73.1 15.0 %collective-permute-start.6 = (bf16[128,640]{1,0:T(8,128)(2,1)S(1)}, bf16[128,640]{1,0:T(8,128)(2,1)S(1)}, u32[]{:S(2)}, u32[]{:S(2)}) collective-permute-start(bf16[128,640]{1,0:T(8,128)(2,1)S(1)} %copy-done.3), channel_id=1, source_target_pairs={{0,28},{8,20},{16,12},{24,4},{28,0},{20,8},{12,16},{4,24},{1,29},{... | collective-permute-start | bytes 491528 | tf_op jit(solution)/shard_map/column_exchange/ppermute | solution.py:125
  79.3 10.6 %collective-permute-start.7 = (bf16[64,2048]{1,0:T(8,128)(2,1)S(1)}, bf16[64,2048]{1,0:T(8,128)(2,1)S(1)}, u32[]{:S(2)}, u32[]{:S(2)}) collective-permute-start(bf16[64,2048]{1,0:T(8,128)(2,1)S(1)} %get-tuple-element.72), channel_id=1, source_target_pairs={{0,8},{8,16},{16,24},{24,28},{28,20},{20,12},{12,4},{4,0},{1,9},{9... | collective-permute-start | bytes 786440 | tf_op jit(solution)/shard_map/out_projection/ppermute | solution.py:47
  80.3 9.7 %collective-permute-start.8 = (bf16[64,2048]{1,0:T(8,128)(2,1)S(1)}, bf16[64,2048]{1,0:T(8,128)(2,1)S(1)}, u32[]{:S(2)}, u32[]{:S(2)}) collective-permute-start(bf16[64,2048]{1,0:T(8,128)(2,1)S(1)} %get-tuple-element.73), channel_id=1, source_target_pairs={{0,4},{8,0},{16,8},{24,16},{28,24},{20,28},{12,20},{4,12},{1,5},{9... | collective-permute-start | bytes 786440 | tf_op jit(solution)/shard_map/out_projection/ppermute | solution.py:47
  90.1 8.3 %collective-permute-start.10 = (bf16[64,2048]{1,0:T(8,128)(2,1)S(1)}, bf16[64,2048]{1,0:T(8,128)(2,1)S(1)}, u32[]{:S(2)}, u32[]{:S(2)}) collective-permute-start(bf16[64,2048]{1,0:T(8,128)(2,1)S(1)} %get-tuple-element.77), channel_id=1, source_target_pairs={{0,4},{8,0},{16,8},{24,16},{28,24},{20,28},{12,20},{4,12},{1,5},{9... | collective-permute-start | bytes 786440 | tf_op jit(solution)/shard_map/out_projection/ppermute | solution.py:47
  91.8 9.2 %collective-permute-start.9 = (bf16[64,2048]{1,0:T(8,128)(2,1)S(1)}, bf16[64,2048]{1,0:T(8,128)(2,1)S(1)}, u32[]{:S(2)}, u32[]{:S(2)}) collective-permute-start(bf16[64,2048]{1,0:T(8,128)(2,1)S(1)} %get-tuple-element.76), channel_id=1, source_target_pairs={{0,8},{8,16},{16,24},{24,28},{28,20},{20,12},{12,4},{4,0},{1,9},{9... | collective-permute-start | bytes 786440 | tf_op jit(solution)/shard_map/out_projection/ppermute | solution.py:47
  101.2 6.4 %collective-permute-start.11 = (bf16[64,2048]{1,0:T(8,128)(2,1)S(1)}, bf16[64,2048]{1,0:T(8,128)(2,1)S(1)}, u32[]{:S(2)}, u32[]{:S(2)}) collective-permute-start(bf16[64,2048]{1,0:T(8,128)(2,1)S(1)} %get-tuple-element.80), channel_id=1, source_target_pairs={{0,8},{8,16},{16,24},{24,28},{28,20},{20,12},{12,4},{4,0},{1,9},{9... | collective-permute-start | bytes 786440 | tf_op jit(solution)/shard_map/out_projection/ppermute | solution.py:47
  101.3 6.6 %collective-permute-start.12 = (bf16[64,2048]{1,0:T(8,128)(2,1)S(1)}, bf16[64,2048]{1,0:T(8,128)(2,1)S(1)}, u32[]{:S(2)}, u32[]{:S(2)}) collective-permute-start(bf16[64,2048]{1,0:T(8,128)(2,1)S(1)} %get-tuple-element.81), channel_id=1, source_target_pairs={{0,4},{8,0},{16,8},{24,16},{28,24},{20,28},{12,20},{4,12},{1,5},{9... | collective-permute-start | bytes 786440 | tf_op jit(solution)/shard_map/out_projection/ppermute | solution.py:47
  108.0 6.4 %collective-permute-start.13 = (bf16[64,2048]{1,0:T(8,128)(2,1)S(1)}, bf16[64,2048]{1,0:T(8,128)(2,1)S(1)}, u32[]{:S(2)}, u32[]{:S(2)}) collective-permute-start(bf16[64,2048]{1,0:T(8,128)(2,1)S(1)} %get-tuple-element.84), channel_id=1, source_target_pairs={{0,8},{8,16},{16,24},{24,28},{28,20},{20,12},{12,4},{4,0},{1,9},{9... | collective-permute-start | bytes 786440 | tf_op jit(solution)/shard_map/out_projection/ppermute | solution.py:47
  109.5 6.4 %collective-permute-start.14 = (bf16[64,2048]{1,0:T(8,128)(2,1)S(1)}, bf16[64,2048]{1,0:T(8,128)(2,1)S(1)}, u32[]{:S(2)}, u32[]{:S(2)}) collective-permute-start(bf16[64,2048]{1,0:T(8,128)(2,1)S(1)} %get-tuple-element.85), channel_id=1, source_target_pairs={{0,4},{8,0},{16,8},{24,16},{28,24},{20,28},{12,20},{4,12},{1,5},{9... | collective-permute-start | bytes 786440 | tf_op jit(solution)/shard_map/out_projection/ppermute | solution.py:47
  116.0 8.6 %collective-permute-start.15 = (bf16[64,2048]{1,0:T(8,128)(2,1)S(1)}, bf16[64,2048]{1,0:T(8,128)(2,1)S(1)}, u32[]{:S(2)}, u32[]{:S(2)}) collective-permute-start(bf16[64,2048]{1,0:T(8,128)(2,1)S(1)} %get-tuple-element.88), channel_id=1, source_target_pairs={{0,8},{8,16},{16,24},{24,28},{28,20},{20,12},{12,4},{4,0},{1,9},{9... | collective-permute-start | bytes 786440 | tf_op jit(solution)/shard_map/out_projection/ppermute | solution.py:47
  118.5 8.9 %collective-permute-start.16 = (bf16[64,2048]{1,0:T(8,128)(2,1)S(1)}, bf16[64,2048]{1,0:T(8,128)(2,1)S(1)}, u32[]{:S(2)}, u32[]{:S(2)}) collective-permute-start(bf16[64,2048]{1,0:T(8,128)(2,1)S(1)} %get-tuple-element.89), channel_id=1, source_target_pairs={{0,4},{8,0},{16,8},{24,16},{28,24},{20,28},{12,20},{4,12},{1,5},{9... | collective-permute-start | bytes 786440 | tf_op jit(solution)/shard_map/out_projection/ppermute | solution.py:47
  127.5 8.4 %collective-permute-start.17 = (bf16[64,2048]{1,0:T(8,128)(2,1)S(1)}, bf16[64,2048]{1,0:T(8,128)(2,1)S(1)}, u32[]{:S(2)}, u32[]{:S(2)}) collective-permute-start(bf16[64,2048]{1,0:T(8,128)(2,1)S(1)} %get-tuple-element.92), channel_id=1, source_target_pairs={{0,8},{8,16},{16,24},{24,28},{28,20},{20,12},{12,4},{4,0},{1,9},{9... | collective-permute-start | bytes 786440 | tf_op jit(solution)/shard_map/out_projection/ppermute | solution.py:47
  127.9 8.2 %collective-permute-start.18 = (bf16[64,2048]{1,0:T(8,128)(2,1)S(1)}, bf16[64,2048]{1,0:T(8,128)(2,1)S(1)}, u32[]{:S(2)}, u32[]{:S(2)}) collective-permute-start(bf16[64,2048]{1,0:T(8,128)(2,1)S(1)} %get-tuple-element.93), channel_id=1, source_target_pairs={{0,4},{8,0},{16,8},{24,16},{28,24},{20,28},{12,20},{4,12},{1,5},{9... | collective-permute-start | bytes 786440 | tf_op jit(solution)/shard_map/out_projection/ppermute | solution.py:47
  130.5 14.8 %copy-start.2 = (bf16[128,2048]{1,0:T(8,128)(2,1)S(1)}, bf16[128,2048]{1,0:T(8,128)(2,1)}, u32[]{:S(2)}) copy-start(bf16[128,2048]{1,0:T(8,128)(2,1)} %param.11) | copy-start | bytes 1572868
  136.1 8.0 %collective-permute-start.19 = (bf16[64,2048]{1,0:T(8,128)(2,1)S(1)}, bf16[64,2048]{1,0:T(8,128)(2,1)S(1)}, u32[]{:S(2)}, u32[]{:S(2)}) collective-permute-start(bf16[64,2048]{1,0:T(8,128)(2,1)S(1)} %get-tuple-element.96), channel_id=1, source_target_pairs={{0,8},{8,16},{16,24},{24,28},{28,20},{20,12},{12,4},{4,0},{1,9},{9... | collective-permute-start | bytes 786440 | tf_op jit(solution)/shard_map/out_projection/ppermute | solution.py:47
  137.8 7.4 %collective-permute-start.20 = (bf16[64,2048]{1,0:T(8,128)(2,1)S(1)}, bf16[64,2048]{1,0:T(8,128)(2,1)S(1)}, u32[]{:S(2)}, u32[]{:S(2)}) collective-permute-start(bf16[64,2048]{1,0:T(8,128)(2,1)S(1)} %get-tuple-element.97), channel_id=1, source_target_pairs={{0,4},{8,0},{16,8},{24,16},{28,24},{20,28},{12,20},{4,12},{1,5},{9... | collective-permute-start | bytes 786440 | tf_op jit(solution)/shard_map/out_projection/ppermute | solution.py:47
  139.1 6.5 %copy-start.5 = (f32[2048]{0:T(1024)S(1)}, f32[2048]{0:T(1024)}, u32[]{:S(2)}) copy-start(f32[2048]{0:T(1024)} %param.14) | copy-start | bytes 24580
  145.8 6.4 %collective-permute-start.21 = (bf16[64,2048]{1,0:T(8,128)(2,1)S(1)}, bf16[64,2048]{1,0:T(8,128)(2,1)S(1)}, u32[]{:S(2)}, u32[]{:S(2)}) collective-permute-start(bf16[64,2048]{1,0:T(8,128)(2,1)S(1)} %get-tuple-element.184), channel_id=1, source_target_pairs={{0,8},{8,16},{16,24},{24,28},{28,20},{20,12},{12,4},{4,0},{1,9},{9... | collective-permute-start | bytes 786440 | tf_op jit(solution)/shard_map/dispatch_gather/ppermute | solution.py:27
  147.3 7.2 %collective-permute-start.22 = (bf16[64,2048]{1,0:T(8,128)(2,1)S(1)}, bf16[64,2048]{1,0:T(8,128)(2,1)S(1)}, u32[]{:S(2)}, u32[]{:S(2)}) collective-permute-start(bf16[64,2048]{1,0:T(8,128)(2,1)S(1)} %get-tuple-element.183), channel_id=1, source_target_pairs={{0,4},{8,0},{16,8},{24,16},{28,24},{20,28},{12,20},{4,12},{1,5},{9... | collective-permute-start | bytes 786440 | tf_op jit(solution)/shard_map/dispatch_gather/ppermute | solution.py:27
  154.5 8.4 %collective-permute-start.23 = (bf16[64,2048]{1,0:T(8,128)(2,1)S(1)}, bf16[64,2048]{1,0:T(8,128)(2,1)S(1)}, u32[]{:S(2)}, u32[]{:S(2)}) collective-permute-start(bf16[64,2048]{1,0:T(8,128)(2,1)S(1)} %collective-permute-done.21), channel_id=1, source_target_pairs={{0,8},{8,16},{16,24},{24,28},{28,20},{20,12},{12,4},{4,0},{1,9},{9... | collective-permute-start | bytes 786440 | tf_op jit(solution)/shard_map/dispatch_gather/ppermute | solution.py:27
  155.8 8.8 %collective-permute-start.24 = (bf16[64,2048]{1,0:T(8,128)(2,1)S(1)}, bf16[64,2048]{1,0:T(8,128)(2,1)S(1)}, u32[]{:S(2)}, u32[]{:S(2)}) collective-permute-start(bf16[64,2048]{1,0:T(8,128)(2,1)S(1)} %collective-permute-done.22), channel_id=1, source_target_pairs={{0,4},{8,0},{16,8},{24,16},{28,24},{20,28},{12,20},{4,12},{1,5},{9... | collective-permute-start | bytes 786440 | tf_op jit(solution)/shard_map/dispatch_gather/ppermute | solution.py:27
  164.6 6.4 %collective-permute-start.25 = (bf16[64,2048]{1,0:T(8,128)(2,1)S(1)}, bf16[64,2048]{1,0:T(8,128)(2,1)S(1)}, u32[]{:S(2)}, u32[]{:S(2)}) collective-permute-start(bf16[64,2048]{1,0:T(8,128)(2,1)S(1)} %collective-permute-done.23), channel_id=1, source_target_pairs={{0,8},{8,16},{16,24},{24,28},{28,20},{20,12},{12,4},{4,0},{1,9},{9... | collective-permute-start | bytes 786440 | tf_op jit(solution)/shard_map/dispatch_gather/ppermute | solution.py:27
  164.9 6.4 %collective-permute-start.26 = (bf16[64,2048]{1,0:T(8,128)(2,1)S(1)}, bf16[64,2048]{1,0:T(8,128)(2,1)S(1)}, u32[]{:S(2)}, u32[]{:S(2)}) collective-permute-start(bf16[64,2048]{1,0:T(8,128)(2,1)S(1)} %collective-permute-done.24), channel_id=1, source_target_pairs={{0,4},{8,0},{16,8},{24,16},{28,24},{20,28},{12,20},{4,12},{1,5},{9... | collective-permute-start | bytes 786440 | tf_op jit(solution)/shard_map/dispatch_gather/ppermute | solution.py:27
  171.3 6.4 %collective-permute-start.27 = (bf16[64,2048]{1,0:T(8,128)(2,1)S(1)}, bf16[64,2048]{1,0:T(8,128)(2,1)S(1)}, u32[]{:S(2)}, u32[]{:S(2)}) collective-permute-start(bf16[64,2048]{1,0:T(8,128)(2,1)S(1)} %collective-permute-done.25), channel_id=1, source_target_pairs={{0,8},{8,16},{16,24},{24,28},{28,20},{20,12},{12,4},{4,0},{1,9},{9... | collective-permute-start | bytes 786440 | tf_op jit(solution)/shard_map/dispatch_gather/ppermute | solution.py:27
  171.3 6.4 %collective-permute-start.28 = (bf16[64,2048]{1,0:T(8,128)(2,1)S(1)}, bf16[64,2048]{1,0:T(8,128)(2,1)S(1)}, u32[]{:S(2)}, u32[]{:S(2)}) collective-permute-start(bf16[64,2048]{1,0:T(8,128)(2,1)S(1)} %collective-permute-done.26), channel_id=1, source_target_pairs={{0,4},{8,0},{16,8},{24,16},{28,24},{20,28},{12,20},{4,12},{1,5},{9... | collective-permute-start | bytes 786440 | tf_op jit(solution)/shard_map/dispatch_gather/ppermute | solution.py:27
  177.6 5.8 %slice-start = ((s8[12582912]{0:T(1024)(128)(4,1)}), s8[4194304]{0:T(1024)(128)(4,1)S(1)}, s32[]{:S(2)}) async-start(s8[12582912]{0:T(1024)(128)(4,1)} %bitcast.150), calls=%async_computation | async-start | bytes 8388608
  177.7 5.7 %slice-start.1 = ((s8[12582912]{0:T(1024)(128)(4,1)}), s8[4194304]{0:T(1024)(128)(4,1)S(1)}, s32[]{:S(2)}) async-start(s8[12582912]{0:T(1024)(128)(4,1)} %bitcast.150), calls=%async_computation.1 | async-start | bytes 8388608
  177.7 6.5 %slice-start.2 = ((s8[12582912]{0:T(1024)(128)(4,1)}), s8[4194304]{0:T(1024)(128)(4,1)S(1)}, s32[]{:S(2)}) async-start(s8[12582912]{0:T(1024)(128)(4,1)} %bitcast.150), calls=%async_computation.2 | async-start | bytes 8388608
  177.7 9.9 %slice-start.6 = ((s8[6291456]{0:T(1024)(128)(4,1)}), s8[4194304]{0:T(1024)(128)(4,1)S(1)}, s32[]{:S(2)}) async-start(s8[6291456]{0:T(1024)(128)(4,1)} %bitcast.154), calls=%async_computation.6 | async-start | bytes 8388608
  184.2 3.4 %slice-start.7 = ((s8[6291456]{0:T(1024)(128)(4,1)}), s8[2097152]{0:T(1024)(128)(4,1)S(1)}, s32[]{:S(2)}) async-start(s8[6291456]{0:T(1024)(128)(4,1)} %bitcast.154), calls=%async_computation.7 | async-start | bytes 4194304
  193.4 9.2 %collective-permute-start.35 = (bf16[64,2048]{1,0:T(8,128)(2,1)S(1)}, bf16[64,2048]{1,0:T(8,128)(2,1)S(1)}, u32[]{:S(2)}, u32[]{:S(2)}) collective-permute-start(bf16[64,2048]{1,0:T(8,128)(2,1)S(1)} %get-tuple-element.114), channel_id=1, source_target_pairs={{0,8},{8,16},{16,24},{24,28},{28,20},{20,12},{12,4},{4,0},{1,9},{9... | collective-permute-start | bytes 786440 | tf_op jit(solution)/shard_map/combine_return/ppermute | solution.py:47
  193.6 9.2 %collective-permute-start.36 = (bf16[64,2048]{1,0:T(8,128)(2,1)S(1)}, bf16[64,2048]{1,0:T(8,128)(2,1)S(1)}, u32[]{:S(2)}, u32[]{:S(2)}) collective-permute-start(bf16[64,2048]{1,0:T(8,128)(2,1)S(1)} %get-tuple-element.115), channel_id=1, source_target_pairs={{0,4},{8,0},{16,8},{24,16},{28,24},{20,28},{12,20},{4,12},{1,5},{9... | collective-permute-start | bytes 786440 | tf_op jit(solution)/shard_map/combine_return/ppermute | solution.py:47
  196.2 11.9 %collective-permute-start.29 = (bf16[64,2048]{1,0:T(8,128)(2,1)S(1)}, bf16[64,2048]{1,0:T(8,128)(2,1)S(1)}, u32[]{:S(2)}, u32[]{:S(2)}) collective-permute-start(bf16[64,2048]{1,0:T(8,128)(2,1)S(1)} %collective-permute-done.27), channel_id=1, source_target_pairs={{0,8},{8,16},{16,24},{24,28},{28,20},{20,12},{12,4},{4,0},{1,9},{9... | collective-permute-start | bytes 786440 | tf_op jit(solution)/shard_map/dispatch_gather/ppermute | solution.py:27
  196.2 12.0 %collective-permute-start.30 = (bf16[64,2048]{1,0:T(8,128)(2,1)S(1)}, bf16[64,2048]{1,0:T(8,128)(2,1)S(1)}, u32[]{:S(2)}, u32[]{:S(2)}) collective-permute-start(bf16[64,2048]{1,0:T(8,128)(2,1)S(1)} %collective-permute-done.28), channel_id=1, source_target_pairs={{0,4},{8,0},{16,8},{24,16},{28,24},{20,28},{12,20},{4,12},{1,5},{9... | collective-permute-start | bytes 786440 | tf_op jit(solution)/shard_map/dispatch_gather/ppermute | solution.py:27
  204.1 6.8 %collective-permute-start.37 = (bf16[64,2048]{1,0:T(8,128)(2,1)S(1)}, bf16[64,2048]{1,0:T(8,128)(2,1)S(1)}, u32[]{:S(2)}, u32[]{:S(2)}) collective-permute-start(bf16[64,2048]{1,0:T(8,128)(2,1)S(1)} %get-tuple-element.118), channel_id=1, source_target_pairs={{0,8},{8,16},{16,24},{24,28},{28,20},{20,12},{12,4},{4,0},{1,9},{9... | collective-permute-start | bytes 786440 | tf_op jit(solution)/shard_map/combine_return/ppermute | solution.py:47
  205.9 6.4 %collective-permute-start.38 = (bf16[64,2048]{1,0:T(8,128)(2,1)S(1)}, bf16[64,2048]{1,0:T(8,128)(2,1)S(1)}, u32[]{:S(2)}, u32[]{:S(2)}) collective-permute-start(bf16[64,2048]{1,0:T(8,128)(2,1)S(1)} %get-tuple-element.119), channel_id=1, source_target_pairs={{0,4},{8,0},{16,8},{24,16},{28,24},{20,28},{12,20},{4,12},{1,5},{9... | collective-permute-start | bytes 786440 | tf_op jit(solution)/shard_map/combine_return/ppermute | solution.py:47
  208.2 7.4 %collective-permute-start.31 = (bf16[64,2048]{1,0:T(8,128)(2,1)S(1)}, bf16[64,2048]{1,0:T(8,128)(2,1)S(1)}, u32[]{:S(2)}, u32[]{:S(2)}) collective-permute-start(bf16[64,2048]{1,0:T(8,128)(2,1)S(1)} %collective-permute-done.29), channel_id=1, source_target_pairs={{0,8},{8,16},{16,24},{24,28},{28,20},{20,12},{12,4},{4,0},{1,9},{9... | collective-permute-start | bytes 786440 | tf_op jit(solution)/shard_map/dispatch_gather/ppermute | solution.py:27
  209.7 6.4 %collective-permute-start.32 = (bf16[64,2048]{1,0:T(8,128)(2,1)S(1)}, bf16[64,2048]{1,0:T(8,128)(2,1)S(1)}, u32[]{:S(2)}, u32[]{:S(2)}) collective-permute-start(bf16[64,2048]{1,0:T(8,128)(2,1)S(1)} %collective-permute-done.30), channel_id=1, source_target_pairs={{0,4},{8,0},{16,8},{24,16},{28,24},{20,28},{12,20},{4,12},{1,5},{9... | collective-permute-start | bytes 786440 | tf_op jit(solution)/shard_map/dispatch_gather/ppermute | solution.py:27
  213.5 19.8 %collective-permute-start.39 = (bf16[64,2048]{1,0:T(8,128)(2,1)S(1)}, bf16[64,2048]{1,0:T(8,128)(2,1)S(1)}, u32[]{:S(2)}, u32[]{:S(2)}) collective-permute-start(bf16[64,2048]{1,0:T(8,128)(2,1)S(1)} %get-tuple-element.122), channel_id=1, source_target_pairs={{0,8},{8,16},{16,24},{24,28},{28,20},{20,12},{12,4},{4,0},{1,9},{9... | collective-permute-start | bytes 786440 | tf_op jit(solution)/shard_map/combine_return/ppermute | solution.py:47
  214.0 19.3 %collective-permute-start.40 = (bf16[64,2048]{1,0:T(8,128)(2,1)S(1)}, bf16[64,2048]{1,0:T(8,128)(2,1)S(1)}, u32[]{:S(2)}, u32[]{:S(2)}) collective-permute-start(bf16[64,2048]{1,0:T(8,128)(2,1)S(1)} %get-tuple-element.123), channel_id=1, source_target_pairs={{0,4},{8,0},{16,8},{24,16},{28,24},{20,28},{12,20},{4,12},{1,5},{9... | collective-permute-start | bytes 786440 | tf_op jit(solution)/shard_map/combine_return/ppermute | solution.py:47
  216.2 7.8 %collective-permute-start.33 = (bf16[64,2048]{1,0:T(8,128)(2,1)S(1)}, bf16[64,2048]{1,0:T(8,128)(2,1)S(1)}, u32[]{:S(2)}, u32[]{:S(2)}) collective-permute-start(bf16[64,2048]{1,0:T(8,128)(2,1)S(1)} %collective-permute-done.31), channel_id=1, source_target_pairs={{0,8},{8,16},{16,24},{24,28},{28,20},{20,12},{12,4},{4,0},{1,9},{9... | collective-permute-start | bytes 786440 | tf_op jit(solution)/shard_map/dispatch_gather/ppermute | solution.py:27
  216.5 7.4 %collective-permute-start.34 = (bf16[64,2048]{1,0:T(8,128)(2,1)S(1)}, bf16[64,2048]{1,0:T(8,128)(2,1)S(1)}, u32[]{:S(2)}, u32[]{:S(2)}) collective-permute-start(bf16[64,2048]{1,0:T(8,128)(2,1)S(1)} %collective-permute-done.32), channel_id=1, source_target_pairs={{0,4},{8,0},{16,8},{24,16},{28,24},{20,28},{12,20},{4,12},{1,5},{9... | collective-permute-start | bytes 786440 | tf_op jit(solution)/shard_map/dispatch_gather/ppermute | solution.py:27
  218.2 11.7 %slice-start.3 = ((s8[12582912]{0:T(1024)(128)(4,1)}), s8[4194304]{0:T(1024)(128)(4,1)S(1)}, s32[]{:S(2)}) async-start(s8[12582912]{0:T(1024)(128)(4,1)} %bitcast.152), calls=%async_computation.3 | async-start | bytes 8388608
  224.2 5.7 %slice-start.4 = ((s8[12582912]{0:T(1024)(128)(4,1)}), s8[4194304]{0:T(1024)(128)(4,1)S(1)}, s32[]{:S(2)}) async-start(s8[12582912]{0:T(1024)(128)(4,1)} %bitcast.152), calls=%async_computation.4 | async-start | bytes 8388608
  224.2 5.7 %slice-start.5 = ((s8[12582912]{0:T(1024)(128)(4,1)}), s8[4194304]{0:T(1024)(128)(4,1)S(1)}, s32[]{:S(2)}) async-start(s8[12582912]{0:T(1024)(128)(4,1)} %bitcast.152), calls=%async_computation.5 | async-start | bytes 8388608
  224.2 14.0 %slice-start.8 = ((s8[6291456]{0:T(1024)(128)(4,1)}), s8[4194304]{0:T(1024)(128)(4,1)S(1)}, s32[]{:S(2)}) async-start(s8[6291456]{0:T(1024)(128)(4,1)} %bitcast.156), calls=%async_computation.8 | async-start | bytes 8388608
  229.9 8.3 %slice-start.9 = ((s8[6291456]{0:T(1024)(128)(4,1)}), s8[2097152]{0:T(1024)(128)(4,1)S(1)}, s32[]{:S(2)}) async-start(s8[6291456]{0:T(1024)(128)(4,1)} %bitcast.156), calls=%async_computation.9 | async-start | bytes 4194304
  234.7 7.4 %collective-permute-start.41 = (bf16[64,2048]{1,0:T(8,128)(2,1)S(1)}, bf16[64,2048]{1,0:T(8,128)(2,1)S(1)}, u32[]{:S(2)}, u32[]{:S(2)}) collective-permute-start(bf16[64,2048]{1,0:T(8,128)(2,1)S(1)} %get-tuple-element.126), channel_id=1, source_target_pairs={{0,8},{8,16},{16,24},{24,28},{28,20},{20,12},{12,4},{4,0},{1,9},{9... | collective-permute-start | bytes 786440 | tf_op jit(solution)/shard_map/combine_return/ppermute | solution.py:47
  238.2 7.7 %collective-permute-start.42 = (bf16[64,2048]{1,0:T(8,128)(2,1)S(1)}, bf16[64,2048]{1,0:T(8,128)(2,1)S(1)}, u32[]{:S(2)}, u32[]{:S(2)}) collective-permute-start(bf16[64,2048]{1,0:T(8,128)(2,1)S(1)} %get-tuple-element.127), channel_id=1, source_target_pairs={{0,4},{8,0},{16,8},{24,16},{28,24},{20,28},{12,20},{4,12},{1,5},{9... | collective-permute-start | bytes 786440 | tf_op jit(solution)/shard_map/combine_return/ppermute | solution.py:47
  246.0 7.8 %collective-permute-start.43 = (bf16[64,2048]{1,0:T(8,128)(2,1)S(1)}, bf16[64,2048]{1,0:T(8,128)(2,1)S(1)}, u32[]{:S(2)}, u32[]{:S(2)}) collective-permute-start(bf16[64,2048]{1,0:T(8,128)(2,1)S(1)} %get-tuple-element.130), channel_id=1, source_target_pairs={{0,8},{8,16},{16,24},{24,28},{28,20},{20,12},{12,4},{4,0},{1,9},{9... | collective-permute-start | bytes 786440 | tf_op jit(solution)/shard_map/combine_return/ppermute | solution.py:47
  249.9 6.4 %collective-permute-start.44 = (bf16[64,2048]{1,0:T(8,128)(2,1)S(1)}, bf16[64,2048]{1,0:T(8,128)(2,1)S(1)}, u32[]{:S(2)}, u32[]{:S(2)}) collective-permute-start(bf16[64,2048]{1,0:T(8,128)(2,1)S(1)} %get-tuple-element.131), channel_id=1, source_target_pairs={{0,4},{8,0},{16,8},{24,16},{28,24},{20,28},{12,20},{4,12},{1,5},{9... | collective-permute-start | bytes 786440 | tf_op jit(solution)/shard_map/combine_return/ppermute | solution.py:47
  256.4 6.4 %collective-permute-start.45 = (bf16[64,2048]{1,0:T(8,128)(2,1)S(1)}, bf16[64,2048]{1,0:T(8,128)(2,1)S(1)}, u32[]{:S(2)}, u32[]{:S(2)}) collective-permute-start(bf16[64,2048]{1,0:T(8,128)(2,1)S(1)} %get-tuple-element.134), channel_id=1, source_target_pairs={{0,8},{8,16},{16,24},{24,28},{28,20},{20,12},{12,4},{4,0},{1,9},{9... | collective-permute-start | bytes 786440 | tf_op jit(solution)/shard_map/combine_return/ppermute | solution.py:47
  257.2 6.4 %collective-permute-start.46 = (bf16[64,2048]{1,0:T(8,128)(2,1)S(1)}, bf16[64,2048]{1,0:T(8,128)(2,1)S(1)}, u32[]{:S(2)}, u32[]{:S(2)}) collective-permute-start(bf16[64,2048]{1,0:T(8,128)(2,1)S(1)} %get-tuple-element.135), channel_id=1, source_target_pairs={{0,4},{8,0},{16,8},{24,16},{28,24},{20,28},{12,20},{4,12},{1,5},{9... | collective-permute-start | bytes 786440 | tf_op jit(solution)/shard_map/combine_return/ppermute | solution.py:47
  263.7 7.2 %copy-start.6 = (f32[2048]{0:T(1024)S(1)}, f32[2048]{0:T(1024)}, u32[]{:S(2)}) copy-start(f32[2048]{0:T(1024)} %param.19) | copy-start | bytes 24580
  263.7 6.4 %collective-permute-start.47 = (bf16[64,2048]{1,0:T(8,128)(2,1)S(1)}, bf16[64,2048]{1,0:T(8,128)(2,1)S(1)}, u32[]{:S(2)}, u32[]{:S(2)}) collective-permute-start(bf16[64,2048]{1,0:T(8,128)(2,1)S(1)} %get-tuple-element.138), channel_id=1, source_target_pairs={{0,8},{8,16},{16,24},{24,28},{28,20},{20,12},{12,4},{4,0},{1,9},{9... | collective-permute-start | bytes 786440 | tf_op jit(solution)/shard_map/combine_return/ppermute | solution.py:47
  264.1 6.4 %collective-permute-start.48 = (bf16[64,2048]{1,0:T(8,128)(2,1)S(1)}, bf16[64,2048]{1,0:T(8,128)(2,1)S(1)}, u32[]{:S(2)}, u32[]{:S(2)}) collective-permute-start(bf16[64,2048]{1,0:T(8,128)(2,1)S(1)} %get-tuple-element.139), channel_id=1, source_target_pairs={{0,4},{8,0},{16,8},{24,16},{28,24},{20,28},{12,20},{4,12},{1,5},{9... | collective-permute-start | bytes 786440 | tf_op jit(solution)/shard_map/combine_return/ppermute | solution.py:47
  270.6 1.9 copy-start.1
  (2 other events, 2.8 us)

commit v7 on v6

--- a/solution.py
+++ b/solution.py
@@ -105,6 +105,14 @@
     with jax.named_scope("column_exchange"):
         columns = attn_out.reshape(row_count, ep_size, slice_width)
         pad = (-3 * local_experts) % 128
+        payloads = jnp.concatenate(
+            [
+                columns.transpose(1, 0, 2),
+                split_exact(dense_weight).transpose(1, 0, 2),
+                jnp.zeros((ep_size, row_count, pad), jnp.bfloat16),
+            ],
+            axis=2,
+        )
         by_shift = {}
         shifts = []
         for k in range(1, ep_size):
@@ -113,14 +121,7 @@
                     shifts.append(shift)
         for shift in shifts:
             target = ring_index[(pos + shift) % ep_size]
-            payload = jnp.concatenate(
-                [
-                    lax.dynamic_index_in_dim(columns, target, 1, keepdims=False),
-                    split_exact(lax.dynamic_index_in_dim(dense_weight, target, 1, keepdims=False)),
-                    jnp.zeros((row_count, pad), jnp.bfloat16),
-                ],
-                axis=1,
-            )
+            payload = lax.dynamic_index_in_dim(payloads, target, 0, keepdims=False)
             pairs = [(ring[q], ring[(q + shift) % ep_size]) for q in range(ep_size)]
             by_shift[shift] = lax.ppermute(payload, "ep", pairs)
 

time: 274 us -> 251 us (0.916)
  local copies, waits for them, and re-layouts: 48.9 us -> 23.1 us
  waiting for transfers between devices: 97.6 us -> 103 us
    another operation x22 -> x0, local copies, waits for them, and re-layouts: 14.7 us -> none
    concatenate x7 -> x1, local copies, waits for them, and re-layouts: 11.6 us -> 0.08 us  [body(): jnp.concatenate([columns.transpose(1, 0, 2), split_exact(dense_weight).tr...]
    ppermute x7, waiting for transfers between devices: 2.14 us -> 6.04 us  [body(): by_shift[shift] = lax.ppermute(payload, 'ep', pairs)]
  transfers between devices with their start and end apart: 49 -> 49, of which waited for: 37 -> 34; matrix products, arithmetic and copies ran while one was open for 23% -> 15% of each run, Pallas kernels for 0% -> 0%
where the time goes in v7:
time: 251 us; the launch traced here: 250 us
  waiting for transfers between devices  103 us (41%)
  starting transfers between devices  59.9 us (24%)
  matrix products  31.2 us (12%)
  local copies, waits for them, and re-layouts  23.1 us (9%)
  between operations  19.8 us (8%)
  other arithmetic  12.6 us (5%)
    ppermute x14, waiting for transfers between devices, ring_reduce_scatter_steps(): lax.ppermute(send_fwd, 'ep', forward)  45.3 us
    ppermute x7, waiting for transfers between devices, ring_all_gather(): lax.ppermute(got_fwd, 'ep', forward)  25.2 us
    ppermute x14, waiting for transfers between devices, ring_reduce_scatter_steps(): lax.ppermute(send_bwd, 'ep', backward)  20.8 us
    dot_general x4, matrix products, expert_mix(): projected_up = jnp.dot(rows, gate_up[e], preferred_element_type=jnp.float32)  18.1 us
    ppermute x14, starting transfers between devices, ring_reduce_scatter_steps(): lax.ppermute(send_fwd, 'ep', forward)  17.2 us
    ppermute x7, starting transfers between devices, body(): by_shift[shift] = lax.ppermute(payload, 'ep', pairs)  14.8 us
    ppermute x14, starting transfers between devices, ring_reduce_scatter_steps(): lax.ppermute(send_bwd, 'ep', backward)  13.5 us
    dynamic_slice x8, local copies, waits for them, and re-layouts, body(): payload = lax.dynamic_index_in_dim(payloads, target, 0, keepdims=False)  10.5 us
  transfers between devices with their start and end apart: 49, of which 34 were waited for; matrix products, arithmetic and copies ran while one was open for 15% of the time, Pallas kernels for 0%

profile of v7, /device:TPU:0, one launch (start us, length us, event | category | flops | bytes accessed | tf_op | source)
XLA Modules:
  0.0 249.6 jit_solution(14418357397861946648)
XLA Ops:
  0.7 1.4 dynamic_slice.55
  6.7 1.6 fusion.134
  18.2 1.6 copy.90
  25.7 1.7 copy.96
  27.4 3.0 %collective-permute-start.1 = (bf16[128,640]{1,0:T(8,128)(2,1)}, bf16[128,640]{1,0:T(8,128)(2,1)}, u32[]{:S(2)}, u32[]{:S(2)}) collective-permute-start(bf16[128,640]{1,0:T(8,128)(2,1)} %bitcast.91), channel_id=1, source_target_pairs={{0,8},{8,16},{16,24},{24,28},{28,20},{20,12},{12,4},{4,0},{1,9},{9... | collective-permute-start | bytes 491528 | tf_op jit(solution)/shard_map/column_exchange/ppermute | solution.py:126
  30.4 1.7 copy.95
  32.1 1.7 copy.98
  33.9 3.0 %collective-permute-start.3 = (bf16[128,640]{1,0:T(8,128)(2,1)}, bf16[128,640]{1,0:T(8,128)(2,1)}, u32[]{:S(2)}, u32[]{:S(2)}) collective-permute-start(bf16[128,640]{1,0:T(8,128)(2,1)} %bitcast.89), channel_id=1, source_target_pairs={{0,16},{8,24},{16,28},{24,20},{28,12},{20,4},{12,0},{4,8},{1,17},{... | collective-permute-start | bytes 491528 | tf_op jit(solution)/shard_map/column_exchange/ppermute | solution.py:126
  36.9 1.7 copy.97
  38.6 1.7 copy.100
  40.3 3.9 %collective-permute-start.5 = (bf16[128,640]{1,0:T(8,128)(2,1)}, bf16[128,640]{1,0:T(8,128)(2,1)}, u32[]{:S(2)}, u32[]{:S(2)}) collective-permute-start(bf16[128,640]{1,0:T(8,128)(2,1)} %bitcast.87), channel_id=1, source_target_pairs={{0,24},{8,28},{16,20},{24,12},{28,4},{20,0},{12,8},{4,16},{1,25},{... | collective-permute-start | bytes 491528 | tf_op jit(solution)/shard_map/column_exchange/ppermute | solution.py:126
  47.1 4.8 %collective-permute-start.6 = (bf16[128,640]{1,0:T(8,128)(2,1)S(1)}, bf16[128,640]{1,0:T(8,128)(2,1)S(1)}, u32[]{:S(2)}, u32[]{:S(2)}) collective-permute-start(bf16[128,640]{1,0:T(8,128)(2,1)S(1)} %bitcast.85), channel_id=1, source_target_pairs={{0,28},{8,20},{16,12},{24,4},{28,0},{20,8},{12,16},{4,24},{1,29},{... | collective-permute-start | bytes 491528 | tf_op jit(solution)/shard_map/column_exchange/ppermute | solution.py:126
  54.3 6.0 %collective-permute-done.2 = bf16[128,640]{1,0:T(8,128)(2,1)} collective-permute-done((bf16[128,640]{1,0:T(8,128)(2,1)}, bf16[128,640]{1,0:T(8,128)(2,1)}, u32[]{:S(2)}, u32[]{:S(2)}) %collective-permute-start.2) | collective-permute-done | bytes 163872 | tf_op jit(solution)/shard_map/column_exchange/ppermute | solution.py:126
  65.6 2.5 collective-permute-done.8
  68.4 4.0 %collective-permute-start.9 = (bf16[64,2048]{1,0:T(8,128)(2,1)S(1)}, bf16[64,2048]{1,0:T(8,128)(2,1)S(1)}, u32[]{:S(2)}, u32[]{:S(2)}) collective-permute-start(bf16[64,2048]{1,0:T(8,128)(2,1)S(1)} %get-tuple-element.76), channel_id=1, source_target_pairs={{0,8},{8,16},{16,24},{24,28},{28,20},{20,12},{12,4},{4,0},{1,9},{9... | collective-permute-start | bytes 786440 | tf_op jit(solution)/shard_map/out_projection/ppermute | solution.py:47
  73.2 4.5 %collective-permute-done.10 = bf16[64,2048]{1,0:T(8,128)(2,1)S(1)} collective-permute-done((bf16[64,2048]{1,0:T(8,128)(2,1)S(1)}, bf16[64,2048]{1,0:T(8,128)(2,1)S(1)}, u32[]{:S(2)}, u32[]{:S(2)}) %collective-permute-start.10) | collective-permute-done | bytes 262176 | tf_op jit(solution)/shard_map/out_projection/ppermute | solution.py:47
  77.9 1.9 collective-permute-start.11
  80.8 3.6 %collective-permute-done.11 = bf16[64,2048]{1,0:T(8,128)(2,1)S(1)} collective-permute-done((bf16[64,2048]{1,0:T(8,128)(2,1)S(1)}, bf16[64,2048]{1,0:T(8,128)(2,1)S(1)}, u32[]{:S(2)}, u32[]{:S(2)}) %collective-permute-start.11) | collective-permute-done | bytes 262176 | tf_op jit(solution)/shard_map/out_projection/ppermute | solution.py:47
  84.4 1.7 collective-permute-done.12
  86.2 2.2 collective-permute-start.13
  89.3 4.7 %collective-permute-done.13 = bf16[64,2048]{1,0:T(8,128)(2,1)S(1)} collective-permute-done((bf16[64,2048]{1,0:T(8,128)(2,1)S(1)}, bf16[64,2048]{1,0:T(8,128)(2,1)S(1)}, u32[]{:S(2)}, u32[]{:S(2)}) %collective-permute-start.13) | collective-permute-done | bytes 262176 | tf_op jit(solution)/shard_map/out_projection/ppermute | solution.py:47
  93.9 2.8 %collective-permute-done.14 = bf16[64,2048]{1,0:T(8,128)(2,1)S(1)} collective-permute-done((bf16[64,2048]{1,0:T(8,128)(2,1)S(1)}, bf16[64,2048]{1,0:T(8,128)(2,1)S(1)}, u32[]{:S(2)}, u32[]{:S(2)}) %collective-permute-start.14) | collective-permute-done | bytes 262176 | tf_op jit(solution)/shard_map/out_projection/ppermute | solution.py:47
  96.9 2.0 collective-permute-start.16
  99.8 6.0 %collective-permute-done.15 = bf16[64,2048]{1,0:T(8,128)(2,1)S(1)} collective-permute-done((bf16[64,2048]{1,0:T(8,128)(2,1)S(1)}, bf16[64,2048]{1,0:T(8,128)(2,1)S(1)}, u32[]{:S(2)}, u32[]{:S(2)}) %collective-permute-start.15) | collective-permute-done | bytes 262176 | tf_op jit(solution)/shard_map/out_projection/ppermute | solution.py:47
  106.2 1.8 collective-permute-start.18
  108.2 5.9 %collective-permute-done.17 = bf16[64,2048]{1,0:T(8,128)(2,1)S(1)} collective-permute-done((bf16[64,2048]{1,0:T(8,128)(2,1)S(1)}, bf16[64,2048]{1,0:T(8,128)(2,1)S(1)}, u32[]{:S(2)}, u32[]{:S(2)}) %collective-permute-start.17) | collective-permute-done | bytes 262176 | tf_op jit(solution)/shard_map/out_projection/ppermute | solution.py:47
  114.4 1.4 collective-permute-start.19
  116.6 5.5 %collective-permute-done.19 = bf16[64,2048]{1,0:T(8,128)(2,1)S(1)} collective-permute-done((bf16[64,2048]{1,0:T(8,128)(2,1)S(1)}, bf16[64,2048]{1,0:T(8,128)(2,1)S(1)}, u32[]{:S(2)}, u32[]{:S(2)}) %collective-permute-start.19) | collective-permute-done | bytes 262176 | tf_op jit(solution)/shard_map/out_projection/ppermute | solution.py:47
  123.7 1.4 collective-permute-start.21
  126.7 3.5 %collective-permute-done.21 = bf16[64,2048]{1,0:T(8,128)(2,1)S(1)} collective-permute-done((bf16[64,2048]{1,0:T(8,128)(2,1)S(1)}, bf16[64,2048]{1,0:T(8,128)(2,1)S(1)}, u32[]{:S(2)}, u32[]{:S(2)}) %collective-permute-start.21) | collective-permute-done | bytes 262176 | tf_op jit(solution)/shard_map/dispatch_gather/ppermute | solution.py:27
  130.2 2.2 collective-permute-done.22
  133.0 1.4 collective-permute-start.24
  134.4 6.3 %collective-permute-done.23 = bf16[64,2048]{1,0:T(8,128)(2,1)S(1)} collective-permute-done((bf16[64,2048]{1,0:T(8,128)(2,1)S(1)}, bf16[64,2048]{1,0:T(8,128)(2,1)S(1)}, u32[]{:S(2)}, u32[]{:S(2)}) %collective-permute-start.23) | collective-permute-done | bytes 262176 | tf_op jit(solution)/shard_map/dispatch_gather/ppermute | solution.py:27
  141.7 2.0 collective-permute-start.26
  143.7 4.3 %collective-permute-done.25 = bf16[64,2048]{1,0:T(8,128)(2,1)S(1)} collective-permute-done((bf16[64,2048]{1,0:T(8,128)(2,1)S(1)}, bf16[64,2048]{1,0:T(8,128)(2,1)S(1)}, u32[]{:S(2)}, u32[]{:S(2)}) %collective-permute-start.25) | collective-permute-done | bytes 262176 | tf_op jit(solution)/shard_map/dispatch_gather/ppermute | solution.py:27
  148.0 1.7 collective-permute-start.27
  150.1 4.3 %collective-permute-done.27 = bf16[64,2048]{1,0:T(8,128)(2,1)S(1)} collective-permute-done((bf16[64,2048]{1,0:T(8,128)(2,1)S(1)}, bf16[64,2048]{1,0:T(8,128)(2,1)S(1)}, u32[]{:S(2)}, u32[]{:S(2)}) %collective-permute-start.27) | collective-permute-done | bytes 262176 | tf_op jit(solution)/shard_map/dispatch_gather/ppermute | solution.py:27
  154.4 1.7 collective-permute-done.28
  156.2 5.7 %fusion.4 = f32[512,1536]{1,0:T(8,128)S(1)} fusion(bf16[512,2048]{1,0:T(8,128)(2,1)S(1)} %constant_dynamic-update-slice_fusion.7, bf16[2,2048,1536]{2,1,0:T(8,128)(2,1)} %param.15), kind=kOutput, calls=%fused_computation.4 | convolution fusion | flops 3221225472 | bytes 11534336 | tf_op jit(solution)/shard_map/local_experts/dot_general | solution.py:59
  162.7 3.4 %fusion = f32[512,1536]{1,0:T(8,128)S(1)} fusion(bf16[512,2048]{1,0:T(8,128)(2,1)S(1)} %constant_dynamic-update-slice_fusion.7, bf16[2,2048,1536]{2,1,0:T(8,128)(2,1)S(1)} %bitcast.99), kind=kOutput, calls=%fused_computation | convolution fusion | flops 3221225472 | bytes 11534336 | tf_op jit(solution)/shard_map/local_experts/dot_general | solution.py:59
  166.1 1.8 fusion.23
  168.0 4.0 %fusion.135 = (bf16[512,2048]{1,0:T(8,128)(2,1)S(1)}, f32[512,2048]{1,0:T(8,128)}) fusion(bf16[2,768,2048]{2,1,0:T(8,128)(2,1)S(1)} %bitcast.103, f32[512,1536]{1,0:T(8,128)S(1)} %fusion, f32[512]{0:T(512)S(1)} %bitcast.97, bf16[512,2048]{1,0:T(8,128)(2,1)S(1)} %fusion.23, f32[512]{0:T(512)S(1)} %bitcast.96), kind=kOutput, calls=%fused_computation.234 | convolution fusion | flops 1620312064 | bytes 14684160 | tf_op jit(solution)/shard_map/local_experts/dot_general | solution.py:63
  172.0 2.1 collective-permute-start.35
  174.6 2.1 collective-permute-start.29
  176.7 4.4 %collective-permute-done.35 = bf16[64,2048]{1,0:T(8,128)(2,1)S(1)} collective-permute-done((bf16[64,2048]{1,0:T(8,128)(2,1)S(1)}, bf16[64,2048]{1,0:T(8,128)(2,1)S(1)}, u32[]{:S(2)}, u32[]{:S(2)}) %collective-permute-start.35) | collective-permute-done | bytes 262176 | tf_op jit(solution)/shard_map/combine_return/ppermute | solution.py:47
  181.2 2.1 collective-permute-done.36
  184.6 2.0 collective-permute-start.38
  188.0 1.7 collective-permute-start.32
  192.4 2.0 collective-permute-start.40
  194.7 1.7 collective-permute-start.34
  196.5 6.8 %collective-permute-done.33 = bf16[64,2048]{1,0:T(8,128)(2,1)S(1)} collective-permute-done((bf16[64,2048]{1,0:T(8,128)(2,1)S(1)}, bf16[64,2048]{1,0:T(8,128)(2,1)S(1)}, u32[]{:S(2)}, u32[]{:S(2)}) %collective-permute-start.33) | collective-permute-done | bytes 262176 | tf_op jit(solution)/shard_map/dispatch_gather/ppermute | solution.py:27
  203.6 5.7 %fusion.6 = f32[512,1536]{1,0:T(8,128)S(1)} fusion(bf16[512,2048]{1,0:T(8,128)(2,1)S(1)} %constant_dynamic-update-slice_fusion, bf16[2,2048,1536]{2,1,0:T(8,128)(2,1)} %param.15), kind=kOutput, calls=%fused_computation.6 | convolution fusion | flops 3221225472 | bytes 11534336 | tf_op jit(solution)/shard_map/local_experts/dot_general | solution.py:59
  209.3 3.4 %fusion.2 = f32[512,1536]{1,0:T(8,128)S(1)} fusion(bf16[512,2048]{1,0:T(8,128)(2,1)S(1)} %constant_dynamic-update-slice_fusion, bf16[2,2048,1536]{2,1,0:T(8,128)(2,1)S(1)} %bitcast.101), kind=kOutput, calls=%fused_computation.2 | convolution fusion | flops 3221225472 | bytes 11534336 | tf_op jit(solution)/shard_map/local_experts/dot_general | solution.py:59
  212.7 1.3 fusion.59
  214.0 2.3 collective-permute-start.41
  217.4 1.8 fusion.20
  219.3 1.9 multiply_add_fusion.1
  222.0 3.4 %collective-permute-done.42 = bf16[64,2048]{1,0:T(8,128)(2,1)S(1)} collective-permute-done((bf16[64,2048]{1,0:T(8,128)(2,1)S(1)}, bf16[64,2048]{1,0:T(8,128)(2,1)S(1)}, u32[]{:S(2)}, u32[]{:S(2)}) %collective-permute-start.42) | collective-permute-done | bytes 262176 | tf_op jit(solution)/shard_map/combine_return/ppermute | solution.py:47
  225.4 1.8 collective-permute-start.43
  227.5 4.3 %collective-permute-done.43 = bf16[64,2048]{1,0:T(8,128)(2,1)S(1)} collective-permute-done((bf16[64,2048]{1,0:T(8,128)(2,1)S(1)}, bf16[64,2048]{1,0:T(8,128)(2,1)S(1)}, u32[]{:S(2)}, u32[]{:S(2)}) %collective-permute-start.43) | collective-permute-done | bytes 262176 | tf_op jit(solution)/shard_map/combine_return/ppermute | solution.py:47
  231.9 1.8 collective-permute-done.44
  235.8 4.3 %collective-permute-done.45 = bf16[64,2048]{1,0:T(8,128)(2,1)S(1)} collective-permute-done((bf16[64,2048]{1,0:T(8,128)(2,1)S(1)}, bf16[64,2048]{1,0:T(8,128)(2,1)S(1)}, u32[]{:S(2)}, u32[]{:S(2)}) %collective-permute-start.45) | collective-permute-done | bytes 262176 | tf_op jit(solution)/shard_map/combine_return/ppermute | solution.py:47
  241.2 2.0 collective-permute-start.48
  243.1 4.3 %collective-permute-done.47 = bf16[64,2048]{1,0:T(8,128)(2,1)S(1)} collective-permute-done((bf16[64,2048]{1,0:T(8,128)(2,1)S(1)}, bf16[64,2048]{1,0:T(8,128)(2,1)S(1)}, u32[]{:S(2)}, u32[]{:S(2)}) %collective-permute-start.47) | collective-permute-done | bytes 262176 | tf_op jit(solution)/shard_map/combine_return/ppermute | solution.py:47
  (181 shorter events, 38.2 us)
Async XLA Ops:
  0.6 44.6 %copy-start = (bf16[512,2048]{1,0:T(8,128)(2,1)S(1)}, bf16[512,2048]{1,0:T(8,128)(2,1)}, u32[]{:S(2)}) copy-start(bf16[512,2048]{1,0:T(8,128)(2,1)} %param.13) | copy-start | bytes 6291460
  27.4 18.4 %collective-permute-start.1 = (bf16[128,640]{1,0:T(8,128)(2,1)}, bf16[128,640]{1,0:T(8,128)(2,1)}, u32[]{:S(2)}, u32[]{:S(2)}) collective-permute-start(bf16[128,640]{1,0:T(8,128)(2,1)} %bitcast.91), channel_id=1, source_target_pairs={{0,8},{8,16},{16,24},{24,28},{28,20},{20,12},{12,4},{4,0},{1,9},{9... | collective-permute-start | bytes 491528 | tf_op jit(solution)/shard_map/column_exchange/ppermute | solution.py:126
  32.1 14.9 %collective-permute-start = (bf16[128,640]{1,0:T(8,128)(2,1)}, bf16[128,640]{1,0:T(8,128)(2,1)}, u32[]{:S(2)}, u32[]{:S(2)}) collective-permute-start(bf16[128,640]{1,0:T(8,128)(2,1)} %bitcast.90), channel_id=1, source_target_pairs={{0,4},{8,0},{16,8},{24,16},{28,24},{20,28},{12,20},{4,12},{1,5},{9... | collective-permute-start | bytes 491528 | tf_op jit(solution)/shard_map/column_exchange/ppermute | solution.py:126
  33.9 19.4 %collective-permute-start.3 = (bf16[128,640]{1,0:T(8,128)(2,1)}, bf16[128,640]{1,0:T(8,128)(2,1)}, u32[]{:S(2)}, u32[]{:S(2)}) collective-permute-start(bf16[128,640]{1,0:T(8,128)(2,1)} %bitcast.89), channel_id=1, source_target_pairs={{0,16},{8,24},{16,28},{24,20},{28,12},{20,4},{12,0},{4,8},{1,17},{... | collective-permute-start | bytes 491528 | tf_op jit(solution)/shard_map/column_exchange/ppermute | solution.py:126
  38.6 21.7 %collective-permute-start.2 = (bf16[128,640]{1,0:T(8,128)(2,1)}, bf16[128,640]{1,0:T(8,128)(2,1)}, u32[]{:S(2)}, u32[]{:S(2)}) collective-permute-start(bf16[128,640]{1,0:T(8,128)(2,1)} %bitcast.88), channel_id=1, source_target_pairs={{0,12},{8,4},{16,0},{24,8},{28,16},{20,24},{12,28},{4,20},{1,13},{... | collective-permute-start | bytes 491528 | tf_op jit(solution)/shard_map/column_exchange/ppermute | solution.py:126
  40.3 21.3 %collective-permute-start.5 = (bf16[128,640]{1,0:T(8,128)(2,1)}, bf16[128,640]{1,0:T(8,128)(2,1)}, u32[]{:S(2)}, u32[]{:S(2)}) collective-permute-start(bf16[128,640]{1,0:T(8,128)(2,1)} %bitcast.87), channel_id=1, source_target_pairs={{0,24},{8,28},{16,20},{24,12},{28,4},{20,0},{12,8},{4,16},{1,25},{... | collective-permute-start | bytes 491528 | tf_op jit(solution)/shard_map/column_exchange/ppermute | solution.py:126
  46.2 16.4 %collective-permute-start.4 = (bf16[128,640]{1,0:T(8,128)(2,1)S(1)}, bf16[128,640]{1,0:T(8,128)(2,1)S(1)}, u32[]{:S(2)}, u32[]{:S(2)}) collective-permute-start(bf16[128,640]{1,0:T(8,128)(2,1)S(1)} %bitcast.86), channel_id=1, source_target_pairs={{0,20},{8,12},{16,4},{24,0},{28,8},{20,16},{12,24},{4,28},{1,21},{... | collective-permute-start | bytes 491528 | tf_op jit(solution)/shard_map/column_exchange/ppermute | solution.py:126
  47.1 16.8 %collective-permute-start.6 = (bf16[128,640]{1,0:T(8,128)(2,1)S(1)}, bf16[128,640]{1,0:T(8,128)(2,1)S(1)}, u32[]{:S(2)}, u32[]{:S(2)}) collective-permute-start(bf16[128,640]{1,0:T(8,128)(2,1)S(1)} %bitcast.85), channel_id=1, source_target_pairs={{0,28},{8,20},{16,12},{24,4},{28,0},{20,8},{12,16},{4,24},{1,29},{... | collective-permute-start | bytes 491528 | tf_op jit(solution)/shard_map/column_exchange/ppermute | solution.py:126
  53.3 12.3 %collective-permute-start.7 = (bf16[64,2048]{1,0:T(8,128)(2,1)S(1)}, bf16[64,2048]{1,0:T(8,128)(2,1)S(1)}, u32[]{:S(2)}, u32[]{:S(2)}) collective-permute-start(bf16[64,2048]{1,0:T(8,128)(2,1)S(1)} %get-tuple-element.72), channel_id=1, source_target_pairs={{0,8},{8,16},{16,24},{24,28},{28,20},{20,12},{12,4},{4,0},{1,9},{9... | collective-permute-start | bytes 786440 | tf_op jit(solution)/shard_map/out_projection/ppermute | solution.py:47
  60.3 7.8 %collective-permute-start.8 = (bf16[64,2048]{1,0:T(8,128)(2,1)S(1)}, bf16[64,2048]{1,0:T(8,128)(2,1)S(1)}, u32[]{:S(2)}, u32[]{:S(2)}) collective-permute-start(bf16[64,2048]{1,0:T(8,128)(2,1)S(1)} %get-tuple-element.73), channel_id=1, source_target_pairs={{0,4},{8,0},{16,8},{24,16},{28,24},{20,28},{12,20},{4,12},{1,5},{9... | collective-permute-start | bytes 786440 | tf_op jit(solution)/shard_map/out_projection/ppermute | solution.py:47
  68.2 9.6 %collective-permute-start.10 = (bf16[64,2048]{1,0:T(8,128)(2,1)S(1)}, bf16[64,2048]{1,0:T(8,128)(2,1)S(1)}, u32[]{:S(2)}, u32[]{:S(2)}) collective-permute-start(bf16[64,2048]{1,0:T(8,128)(2,1)S(1)} %get-tuple-element.77), channel_id=1, source_target_pairs={{0,4},{8,0},{16,8},{24,16},{28,24},{20,28},{12,20},{4,12},{1,5},{9... | collective-permute-start | bytes 786440 | tf_op jit(solution)/shard_map/out_projection/ppermute | solution.py:47
  68.4 9.4 %collective-permute-start.9 = (bf16[64,2048]{1,0:T(8,128)(2,1)S(1)}, bf16[64,2048]{1,0:T(8,128)(2,1)S(1)}, u32[]{:S(2)}, u32[]{:S(2)}) collective-permute-start(bf16[64,2048]{1,0:T(8,128)(2,1)S(1)} %get-tuple-element.76), channel_id=1, source_target_pairs={{0,8},{8,16},{16,24},{24,28},{28,20},{20,12},{12,4},{4,0},{1,9},{9... | collective-permute-start | bytes 786440 | tf_op jit(solution)/shard_map/out_projection/ppermute | solution.py:47
  77.9 6.6 %collective-permute-start.11 = (bf16[64,2048]{1,0:T(8,128)(2,1)S(1)}, bf16[64,2048]{1,0:T(8,128)(2,1)S(1)}, u32[]{:S(2)}, u32[]{:S(2)}) collective-permute-start(bf16[64,2048]{1,0:T(8,128)(2,1)S(1)} %get-tuple-element.80), channel_id=1, source_target_pairs={{0,8},{8,16},{16,24},{24,28},{28,20},{20,12},{12,4},{4,0},{1,9},{9... | collective-permute-start | bytes 786440 | tf_op jit(solution)/shard_map/out_projection/ppermute | solution.py:47
  79.7 6.4 %collective-permute-start.12 = (bf16[64,2048]{1,0:T(8,128)(2,1)S(1)}, bf16[64,2048]{1,0:T(8,128)(2,1)S(1)}, u32[]{:S(2)}, u32[]{:S(2)}) collective-permute-start(bf16[64,2048]{1,0:T(8,128)(2,1)S(1)} %get-tuple-element.81), channel_id=1, source_target_pairs={{0,4},{8,0},{16,8},{24,16},{28,24},{20,28},{12,20},{4,12},{1,5},{9... | collective-permute-start | bytes 786440 | tf_op jit(solution)/shard_map/out_projection/ppermute | solution.py:47
  86.2 7.7 %collective-permute-start.13 = (bf16[64,2048]{1,0:T(8,128)(2,1)S(1)}, bf16[64,2048]{1,0:T(8,128)(2,1)S(1)}, u32[]{:S(2)}, u32[]{:S(2)}) collective-permute-start(bf16[64,2048]{1,0:T(8,128)(2,1)S(1)} %get-tuple-element.84), channel_id=1, source_target_pairs={{0,8},{8,16},{16,24},{24,28},{28,20},{20,12},{12,4},{4,0},{1,9},{9... | collective-permute-start | bytes 786440 | tf_op jit(solution)/shard_map/out_projection/ppermute | solution.py:47
  88.4 8.3 %collective-permute-start.14 = (bf16[64,2048]{1,0:T(8,128)(2,1)S(1)}, bf16[64,2048]{1,0:T(8,128)(2,1)S(1)}, u32[]{:S(2)}, u32[]{:S(2)}) collective-permute-start(bf16[64,2048]{1,0:T(8,128)(2,1)S(1)} %get-tuple-element.85), channel_id=1, source_target_pairs={{0,4},{8,0},{16,8},{24,16},{28,24},{20,28},{12,20},{4,12},{1,5},{9... | collective-permute-start | bytes 786440 | tf_op jit(solution)/shard_map/out_projection/ppermute | solution.py:47
  96.8 9.0 %collective-permute-start.15 = (bf16[64,2048]{1,0:T(8,128)(2,1)S(1)}, bf16[64,2048]{1,0:T(8,128)(2,1)S(1)}, u32[]{:S(2)}, u32[]{:S(2)}) collective-permute-start(bf16[64,2048]{1,0:T(8,128)(2,1)S(1)} %get-tuple-element.88), channel_id=1, source_target_pairs={{0,8},{8,16},{16,24},{24,28},{28,20},{20,12},{12,4},{4,0},{1,9},{9... | collective-permute-start | bytes 786440 | tf_op jit(solution)/shard_map/out_projection/ppermute | solution.py:47
  96.9 9.0 %collective-permute-start.16 = (bf16[64,2048]{1,0:T(8,128)(2,1)S(1)}, bf16[64,2048]{1,0:T(8,128)(2,1)S(1)}, u32[]{:S(2)}, u32[]{:S(2)}) collective-permute-start(bf16[64,2048]{1,0:T(8,128)(2,1)S(1)} %get-tuple-element.89), channel_id=1, source_target_pairs={{0,4},{8,0},{16,8},{24,16},{28,24},{20,28},{12,20},{4,12},{1,5},{9... | collective-permute-start | bytes 786440 | tf_op jit(solution)/shard_map/out_projection/ppermute | solution.py:47
  106.0 8.1 %collective-permute-start.17 = (bf16[64,2048]{1,0:T(8,128)(2,1)S(1)}, bf16[64,2048]{1,0:T(8,128)(2,1)S(1)}, u32[]{:S(2)}, u32[]{:S(2)}) collective-permute-start(bf16[64,2048]{1,0:T(8,128)(2,1)S(1)} %get-tuple-element.92), channel_id=1, source_target_pairs={{0,8},{8,16},{16,24},{24,28},{28,20},{20,12},{12,4},{4,0},{1,9},{9... | collective-permute-start | bytes 786440 | tf_op jit(solution)/shard_map/out_projection/ppermute | solution.py:47
  106.2 8.1 %collective-permute-start.18 = (bf16[64,2048]{1,0:T(8,128)(2,1)S(1)}, bf16[64,2048]{1,0:T(8,128)(2,1)S(1)}, u32[]{:S(2)}, u32[]{:S(2)}) collective-permute-start(bf16[64,2048]{1,0:T(8,128)(2,1)S(1)} %get-tuple-element.93), channel_id=1, source_target_pairs={{0,4},{8,0},{16,8},{24,16},{28,24},{20,28},{12,20},{4,12},{1,5},{9... | collective-permute-start | bytes 786440 | tf_op jit(solution)/shard_map/out_projection/ppermute | solution.py:47
  108.2 15.1 %copy-start.2 = (bf16[128,2048]{1,0:T(8,128)(2,1)S(1)}, bf16[128,2048]{1,0:T(8,128)(2,1)}, u32[]{:S(2)}) copy-start(bf16[128,2048]{1,0:T(8,128)(2,1)} %param.11) | copy-start | bytes 1572868
  114.4 7.8 %collective-permute-start.19 = (bf16[64,2048]{1,0:T(8,128)(2,1)S(1)}, bf16[64,2048]{1,0:T(8,128)(2,1)S(1)}, u32[]{:S(2)}, u32[]{:S(2)}) collective-permute-start(bf16[64,2048]{1,0:T(8,128)(2,1)S(1)} %get-tuple-element.96), channel_id=1, source_target_pairs={{0,8},{8,16},{16,24},{24,28},{28,20},{20,12},{12,4},{4,0},{1,9},{9... | collective-permute-start | bytes 786440 | tf_op jit(solution)/shard_map/out_projection/ppermute | solution.py:47
  115.9 7.2 %collective-permute-start.20 = (bf16[64,2048]{1,0:T(8,128)(2,1)S(1)}, bf16[64,2048]{1,0:T(8,128)(2,1)S(1)}, u32[]{:S(2)}, u32[]{:S(2)}) collective-permute-start(bf16[64,2048]{1,0:T(8,128)(2,1)S(1)} %get-tuple-element.97), channel_id=1, source_target_pairs={{0,4},{8,0},{16,8},{24,16},{28,24},{20,28},{12,20},{4,12},{1,5},{9... | collective-permute-start | bytes 786440 | tf_op jit(solution)/shard_map/out_projection/ppermute | solution.py:47
  116.6 6.9 %copy-start.4 = (f32[2048]{0:T(1024)S(1)}, f32[2048]{0:T(1024)}, u32[]{:S(2)}) copy-start(f32[2048]{0:T(1024)} %param.14) | copy-start | bytes 24580
  123.7 6.4 %collective-permute-start.21 = (bf16[64,2048]{1,0:T(8,128)(2,1)S(1)}, bf16[64,2048]{1,0:T(8,128)(2,1)S(1)}, u32[]{:S(2)}, u32[]{:S(2)}) collective-permute-start(bf16[64,2048]{1,0:T(8,128)(2,1)S(1)} %get-tuple-element.184), channel_id=1, source_target_pairs={{0,8},{8,16},{16,24},{24,28},{28,20},{20,12},{12,4},{4,0},{1,9},{9... | collective-permute-start | bytes 786440 | tf_op jit(solution)/shard_map/dispatch_gather/ppermute | solution.py:27
  125.1 7.2 %collective-permute-start.22 = (bf16[64,2048]{1,0:T(8,128)(2,1)S(1)}, bf16[64,2048]{1,0:T(8,128)(2,1)S(1)}, u32[]{:S(2)}, u32[]{:S(2)}) collective-permute-start(bf16[64,2048]{1,0:T(8,128)(2,1)S(1)} %get-tuple-element.183), channel_id=1, source_target_pairs={{0,4},{8,0},{16,8},{24,16},{28,24},{20,28},{12,20},{4,12},{1,5},{9... | collective-permute-start | bytes 786440 | tf_op jit(solution)/shard_map/dispatch_gather/ppermute | solution.py:27
  132.4 8.4 %collective-permute-start.23 = (bf16[64,2048]{1,0:T(8,128)(2,1)S(1)}, bf16[64,2048]{1,0:T(8,128)(2,1)S(1)}, u32[]{:S(2)}, u32[]{:S(2)}) collective-permute-start(bf16[64,2048]{1,0:T(8,128)(2,1)S(1)} %collective-permute-done.21), channel_id=1, source_target_pairs={{0,8},{8,16},{16,24},{24,28},{28,20},{20,12},{12,4},{4,0},{1,9},{9... | collective-permute-start | bytes 786440 | tf_op jit(solution)/shard_map/dispatch_gather/ppermute | solution.py:27
  133.0 8.6 %collective-permute-start.24 = (bf16[64,2048]{1,0:T(8,128)(2,1)S(1)}, bf16[64,2048]{1,0:T(8,128)(2,1)S(1)}, u32[]{:S(2)}, u32[]{:S(2)}) collective-permute-start(bf16[64,2048]{1,0:T(8,128)(2,1)S(1)} %collective-permute-done.22), channel_id=1, source_target_pairs={{0,4},{8,0},{16,8},{24,16},{28,24},{20,28},{12,20},{4,12},{1,5},{9... | collective-permute-start | bytes 786440 | tf_op jit(solution)/shard_map/dispatch_gather/ppermute | solution.py:27
  141.7 6.4 %collective-permute-start.25 = (bf16[64,2048]{1,0:T(8,128)(2,1)S(1)}, bf16[64,2048]{1,0:T(8,128)(2,1)S(1)}, u32[]{:S(2)}, u32[]{:S(2)}) collective-permute-start(bf16[64,2048]{1,0:T(8,128)(2,1)S(1)} %collective-permute-done.23), channel_id=1, source_target_pairs={{0,8},{8,16},{16,24},{24,28},{28,20},{20,12},{12,4},{4,0},{1,9},{9... | collective-permute-start | bytes 786440 | tf_op jit(solution)/shard_map/dispatch_gather/ppermute | solution.py:27
  141.7 6.4 %collective-permute-start.26 = (bf16[64,2048]{1,0:T(8,128)(2,1)S(1)}, bf16[64,2048]{1,0:T(8,128)(2,1)S(1)}, u32[]{:S(2)}, u32[]{:S(2)}) collective-permute-start(bf16[64,2048]{1,0:T(8,128)(2,1)S(1)} %collective-permute-done.24), channel_id=1, source_target_pairs={{0,4},{8,0},{16,8},{24,16},{28,24},{20,28},{12,20},{4,12},{1,5},{9... | collective-permute-start | bytes 786440 | tf_op jit(solution)/shard_map/dispatch_gather/ppermute | solution.py:27
  148.0 6.4 %collective-permute-start.27 = (bf16[64,2048]{1,0:T(8,128)(2,1)S(1)}, bf16[64,2048]{1,0:T(8,128)(2,1)S(1)}, u32[]{:S(2)}, u32[]{:S(2)}) collective-permute-start(bf16[64,2048]{1,0:T(8,128)(2,1)S(1)} %collective-permute-done.25), channel_id=1, source_target_pairs={{0,8},{8,16},{16,24},{24,28},{28,20},{20,12},{12,4},{4,0},{1,9},{9... | collective-permute-start | bytes 786440 | tf_op jit(solution)/shard_map/dispatch_gather/ppermute | solution.py:27
  149.8 6.4 %collective-permute-start.28 = (bf16[64,2048]{1,0:T(8,128)(2,1)S(1)}, bf16[64,2048]{1,0:T(8,128)(2,1)S(1)}, u32[]{:S(2)}, u32[]{:S(2)}) collective-permute-start(bf16[64,2048]{1,0:T(8,128)(2,1)S(1)} %collective-permute-done.26), channel_id=1, source_target_pairs={{0,4},{8,0},{16,8},{24,16},{28,24},{20,28},{12,20},{4,12},{1,5},{9... | collective-permute-start | bytes 786440 | tf_op jit(solution)/shard_map/dispatch_gather/ppermute | solution.py:27
  150.1 16.0 %slice-start.6 = ((s8[6291456]{0:T(1024)(128)(4,1)}), s8[4194304]{0:T(1024)(128)(4,1)S(1)}, s32[]{:S(2)}) async-start(s8[6291456]{0:T(1024)(128)(4,1)} %bitcast.102), calls=%async_computation.6 | async-start | bytes 8388608
  156.2 5.8 %slice-start = ((s8[12582912]{0:T(1024)(128)(4,1)}), s8[4194304]{0:T(1024)(128)(4,1)S(1)}, s32[]{:S(2)}) async-start(s8[12582912]{0:T(1024)(128)(4,1)} %bitcast.98), calls=%async_computation | async-start | bytes 8388608
  156.2 5.7 %slice-start.1 = ((s8[12582912]{0:T(1024)(128)(4,1)}), s8[4194304]{0:T(1024)(128)(4,1)S(1)}, s32[]{:S(2)}) async-start(s8[12582912]{0:T(1024)(128)(4,1)} %bitcast.98), calls=%async_computation.1 | async-start | bytes 8388608
  156.2 6.5 %slice-start.2 = ((s8[12582912]{0:T(1024)(128)(4,1)}), s8[4194304]{0:T(1024)(128)(4,1)S(1)}, s32[]{:S(2)}) async-start(s8[12582912]{0:T(1024)(128)(4,1)} %bitcast.98), calls=%async_computation.2 | async-start | bytes 8388608
  156.2 9.9 %slice-start.7 = ((s8[6291456]{0:T(1024)(128)(4,1)}), s8[2097152]{0:T(1024)(128)(4,1)S(1)}, s32[]{:S(2)}) async-start(s8[6291456]{0:T(1024)(128)(4,1)} %bitcast.102), calls=%async_computation.7 | async-start | bytes 4194304
  172.0 9.2 %collective-permute-start.35 = (bf16[64,2048]{1,0:T(8,128)(2,1)S(1)}, bf16[64,2048]{1,0:T(8,128)(2,1)S(1)}, u32[]{:S(2)}, u32[]{:S(2)}) collective-permute-start(bf16[64,2048]{1,0:T(8,128)(2,1)S(1)} %get-tuple-element.114), channel_id=1, source_target_pairs={{0,8},{8,16},{16,24},{24,28},{28,20},{20,12},{12,4},{4,0},{1,9},{9... | collective-permute-start | bytes 786440 | tf_op jit(solution)/shard_map/combine_return/ppermute | solution.py:47
  174.0 9.2 %collective-permute-start.36 = (bf16[64,2048]{1,0:T(8,128)(2,1)S(1)}, bf16[64,2048]{1,0:T(8,128)(2,1)S(1)}, u32[]{:S(2)}, u32[]{:S(2)}) collective-permute-start(bf16[64,2048]{1,0:T(8,128)(2,1)S(1)} %get-tuple-element.115), channel_id=1, source_target_pairs={{0,4},{8,0},{16,8},{24,16},{28,24},{20,28},{12,20},{4,12},{1,5},{9... | collective-permute-start | bytes 786440 | tf_op jit(solution)/shard_map/combine_return/ppermute | solution.py:47
  174.6 12.0 %collective-permute-start.29 = (bf16[64,2048]{1,0:T(8,128)(2,1)S(1)}, bf16[64,2048]{1,0:T(8,128)(2,1)S(1)}, u32[]{:S(2)}, u32[]{:S(2)}) collective-permute-start(bf16[64,2048]{1,0:T(8,128)(2,1)S(1)} %collective-permute-done.27), channel_id=1, source_target_pairs={{0,8},{8,16},{16,24},{24,28},{28,20},{20,12},{12,4},{4,0},{1,9},{9... | collective-permute-start | bytes 786440 | tf_op jit(solution)/shard_map/dispatch_gather/ppermute | solution.py:27
  176.7 10.9 %collective-permute-start.30 = (bf16[64,2048]{1,0:T(8,128)(2,1)S(1)}, bf16[64,2048]{1,0:T(8,128)(2,1)S(1)}, u32[]{:S(2)}, u32[]{:S(2)}) collective-permute-start(bf16[64,2048]{1,0:T(8,128)(2,1)S(1)} %collective-permute-done.28), channel_id=1, source_target_pairs={{0,4},{8,0},{16,8},{24,16},{28,24},{20,28},{12,20},{4,12},{1,5},{9... | collective-permute-start | bytes 786440 | tf_op jit(solution)/shard_map/dispatch_gather/ppermute | solution.py:27
  184.6 6.4 %collective-permute-start.37 = (bf16[64,2048]{1,0:T(8,128)(2,1)S(1)}, bf16[64,2048]{1,0:T(8,128)(2,1)S(1)}, u32[]{:S(2)}, u32[]{:S(2)}) collective-permute-start(bf16[64,2048]{1,0:T(8,128)(2,1)S(1)} %get-tuple-element.118), channel_id=1, source_target_pairs={{0,8},{8,16},{16,24},{24,28},{28,20},{20,12},{12,4},{4,0},{1,9},{9... | collective-permute-start | bytes 786440 | tf_op jit(solution)/shard_map/combine_return/ppermute | solution.py:47
  184.6 6.4 %collective-permute-start.38 = (bf16[64,2048]{1,0:T(8,128)(2,1)S(1)}, bf16[64,2048]{1,0:T(8,128)(2,1)S(1)}, u32[]{:S(2)}, u32[]{:S(2)}) collective-permute-start(bf16[64,2048]{1,0:T(8,128)(2,1)S(1)} %get-tuple-element.119), channel_id=1, source_target_pairs={{0,4},{8,0},{16,8},{24,16},{28,24},{20,28},{12,20},{4,12},{1,5},{9... | collective-permute-start | bytes 786440 | tf_op jit(solution)/shard_map/combine_return/ppermute | solution.py:47
  187.6 6.8 %collective-permute-start.31 = (bf16[64,2048]{1,0:T(8,128)(2,1)S(1)}, bf16[64,2048]{1,0:T(8,128)(2,1)S(1)}, u32[]{:S(2)}, u32[]{:S(2)}) collective-permute-start(bf16[64,2048]{1,0:T(8,128)(2,1)S(1)} %collective-permute-done.29), channel_id=1, source_target_pairs={{0,8},{8,16},{16,24},{24,28},{28,20},{20,12},{12,4},{4,0},{1,9},{9... | collective-permute-start | bytes 786440 | tf_op jit(solution)/shard_map/dispatch_gather/ppermute | solution.py:27
  188.0 6.5 %collective-permute-start.32 = (bf16[64,2048]{1,0:T(8,128)(2,1)S(1)}, bf16[64,2048]{1,0:T(8,128)(2,1)S(1)}, u32[]{:S(2)}, u32[]{:S(2)}) collective-permute-start(bf16[64,2048]{1,0:T(8,128)(2,1)S(1)} %collective-permute-done.30), channel_id=1, source_target_pairs={{0,4},{8,0},{16,8},{24,16},{28,24},{20,28},{12,20},{4,12},{1,5},{9... | collective-permute-start | bytes 786440 | tf_op jit(solution)/shard_map/dispatch_gather/ppermute | solution.py:27
  192.4 20.3 %collective-permute-start.39 = (bf16[64,2048]{1,0:T(8,128)(2,1)S(1)}, bf16[64,2048]{1,0:T(8,128)(2,1)S(1)}, u32[]{:S(2)}, u32[]{:S(2)}) collective-permute-start(bf16[64,2048]{1,0:T(8,128)(2,1)S(1)} %get-tuple-element.122), channel_id=1, source_target_pairs={{0,8},{8,16},{16,24},{24,28},{28,20},{20,12},{12,4},{4,0},{1,9},{9... | collective-permute-start | bytes 786440 | tf_op jit(solution)/shard_map/combine_return/ppermute | solution.py:47
  192.4 20.3 %collective-permute-start.40 = (bf16[64,2048]{1,0:T(8,128)(2,1)S(1)}, bf16[64,2048]{1,0:T(8,128)(2,1)S(1)}, u32[]{:S(2)}, u32[]{:S(2)}) collective-permute-start(bf16[64,2048]{1,0:T(8,128)(2,1)S(1)} %get-tuple-element.123), channel_id=1, source_target_pairs={{0,4},{8,0},{16,8},{24,16},{28,24},{20,28},{12,20},{4,12},{1,5},{9... | collective-permute-start | bytes 786440 | tf_op jit(solution)/shard_map/combine_return/ppermute | solution.py:47
  194.4 8.8 %collective-permute-start.33 = (bf16[64,2048]{1,0:T(8,128)(2,1)S(1)}, bf16[64,2048]{1,0:T(8,128)(2,1)S(1)}, u32[]{:S(2)}, u32[]{:S(2)}) collective-permute-start(bf16[64,2048]{1,0:T(8,128)(2,1)S(1)} %collective-permute-done.31), channel_id=1, source_target_pairs={{0,8},{8,16},{16,24},{24,28},{28,20},{20,12},{12,4},{4,0},{1,9},{9... | collective-permute-start | bytes 786440 | tf_op jit(solution)/shard_map/dispatch_gather/ppermute | solution.py:27
  194.7 8.5 %collective-permute-start.34 = (bf16[64,2048]{1,0:T(8,128)(2,1)S(1)}, bf16[64,2048]{1,0:T(8,128)(2,1)S(1)}, u32[]{:S(2)}, u32[]{:S(2)}) collective-permute-start(bf16[64,2048]{1,0:T(8,128)(2,1)S(1)} %collective-permute-done.32), channel_id=1, source_target_pairs={{0,4},{8,0},{16,8},{24,16},{28,24},{20,28},{12,20},{4,12},{1,5},{9... | collective-permute-start | bytes 786440 | tf_op jit(solution)/shard_map/dispatch_gather/ppermute | solution.py:27
  196.5 12.7 %slice-start.3 = ((s8[12582912]{0:T(1024)(128)(4,1)}), s8[4194304]{0:T(1024)(128)(4,1)S(1)}, s32[]{:S(2)}) async-start(s8[12582912]{0:T(1024)(128)(4,1)} %bitcast.100), calls=%async_computation.3 | async-start | bytes 8388608
  203.5 5.7 %slice-start.4 = ((s8[12582912]{0:T(1024)(128)(4,1)}), s8[4194304]{0:T(1024)(128)(4,1)S(1)}, s32[]{:S(2)}) async-start(s8[12582912]{0:T(1024)(128)(4,1)} %bitcast.100), calls=%async_computation.4 | async-start | bytes 8388608
  203.5 5.7 %slice-start.5 = ((s8[12582912]{0:T(1024)(128)(4,1)}), s8[4194304]{0:T(1024)(128)(4,1)S(1)}, s32[]{:S(2)}) async-start(s8[12582912]{0:T(1024)(128)(4,1)} %bitcast.100), calls=%async_computation.5 | async-start | bytes 8388608
  203.6 13.9 %slice-start.8 = ((s8[6291456]{0:T(1024)(128)(4,1)}), s8[4194304]{0:T(1024)(128)(4,1)S(1)}, s32[]{:S(2)}) async-start(s8[6291456]{0:T(1024)(128)(4,1)} %bitcast.104), calls=%async_computation.8 | async-start | bytes 8388608
  209.3 8.2 %slice-start.9 = ((s8[6291456]{0:T(1024)(128)(4,1)}), s8[2097152]{0:T(1024)(128)(4,1)S(1)}, s32[]{:S(2)}) async-start(s8[6291456]{0:T(1024)(128)(4,1)} %bitcast.104), calls=%async_computation.9 | async-start | bytes 4194304
  214.0 8.0 %collective-permute-start.41 = (bf16[64,2048]{1,0:T(8,128)(2,1)S(1)}, bf16[64,2048]{1,0:T(8,128)(2,1)S(1)}, u32[]{:S(2)}, u32[]{:S(2)}) collective-permute-start(bf16[64,2048]{1,0:T(8,128)(2,1)S(1)} %get-tuple-element.126), channel_id=1, source_target_pairs={{0,8},{8,16},{16,24},{24,28},{28,20},{20,12},{12,4},{4,0},{1,9},{9... | collective-permute-start | bytes 786440 | tf_op jit(solution)/shard_map/combine_return/ppermute | solution.py:47
  216.3 9.0 %collective-permute-start.42 = (bf16[64,2048]{1,0:T(8,128)(2,1)S(1)}, bf16[64,2048]{1,0:T(8,128)(2,1)S(1)}, u32[]{:S(2)}, u32[]{:S(2)}) collective-permute-start(bf16[64,2048]{1,0:T(8,128)(2,1)S(1)} %get-tuple-element.127), channel_id=1, source_target_pairs={{0,4},{8,0},{16,8},{24,16},{28,24},{20,28},{12,20},{4,12},{1,5},{9... | collective-permute-start | bytes 786440 | tf_op jit(solution)/shard_map/combine_return/ppermute | solution.py:47
  225.4 6.4 %collective-permute-start.43 = (bf16[64,2048]{1,0:T(8,128)(2,1)S(1)}, bf16[64,2048]{1,0:T(8,128)(2,1)S(1)}, u32[]{:S(2)}, u32[]{:S(2)}) collective-permute-start(bf16[64,2048]{1,0:T(8,128)(2,1)S(1)} %get-tuple-element.130), channel_id=1, source_target_pairs={{0,8},{8,16},{16,24},{24,28},{28,20},{20,12},{12,4},{4,0},{1,9},{9... | collective-permute-start | bytes 786440 | tf_op jit(solution)/shard_map/combine_return/ppermute | solution.py:47
  227.3 6.4 %collective-permute-start.44 = (bf16[64,2048]{1,0:T(8,128)(2,1)S(1)}, bf16[64,2048]{1,0:T(8,128)(2,1)S(1)}, u32[]{:S(2)}, u32[]{:S(2)}) collective-permute-start(bf16[64,2048]{1,0:T(8,128)(2,1)S(1)} %get-tuple-element.131), channel_id=1, source_target_pairs={{0,4},{8,0},{16,8},{24,16},{28,24},{20,28},{12,20},{4,12},{1,5},{9... | collective-permute-start | bytes 786440 | tf_op jit(solution)/shard_map/combine_return/ppermute | solution.py:47
  233.8 6.4 %collective-permute-start.45 = (bf16[64,2048]{1,0:T(8,128)(2,1)S(1)}, bf16[64,2048]{1,0:T(8,128)(2,1)S(1)}, u32[]{:S(2)}, u32[]{:S(2)}) collective-permute-start(bf16[64,2048]{1,0:T(8,128)(2,1)S(1)} %get-tuple-element.134), channel_id=1, source_target_pairs={{0,8},{8,16},{16,24},{24,28},{28,20},{20,12},{12,4},{4,0},{1,9},{9... | collective-permute-start | bytes 786440 | tf_op jit(solution)/shard_map/combine_return/ppermute | solution.py:47
  234.6 6.4 %collective-permute-start.46 = (bf16[64,2048]{1,0:T(8,128)(2,1)S(1)}, bf16[64,2048]{1,0:T(8,128)(2,1)S(1)}, u32[]{:S(2)}, u32[]{:S(2)}) collective-permute-start(bf16[64,2048]{1,0:T(8,128)(2,1)S(1)} %get-tuple-element.135), channel_id=1, source_target_pairs={{0,4},{8,0},{16,8},{24,16},{28,24},{20,28},{12,20},{4,12},{1,5},{9... | collective-permute-start | bytes 786440 | tf_op jit(solution)/shard_map/combine_return/ppermute | solution.py:47
  241.0 6.9 %copy-start.5 = (f32[2048]{0:T(1024)S(1)}, f32[2048]{0:T(1024)}, u32[]{:S(2)}) copy-start(f32[2048]{0:T(1024)} %param.19) | copy-start | bytes 24580
  241.1 6.4 %collective-permute-start.47 = (bf16[64,2048]{1,0:T(8,128)(2,1)S(1)}, bf16[64,2048]{1,0:T(8,128)(2,1)S(1)}, u32[]{:S(2)}, u32[]{:S(2)}) collective-permute-start(bf16[64,2048]{1,0:T(8,128)(2,1)S(1)} %get-tuple-element.138), channel_id=1, source_target_pairs={{0,8},{8,16},{16,24},{24,28},{28,20},{20,12},{12,4},{4,0},{1,9},{9... | collective-permute-start | bytes 786440 | tf_op jit(solution)/shard_map/combine_return/ppermute | solution.py:47
  241.2 6.4 %collective-permute-start.48 = (bf16[64,2048]{1,0:T(8,128)(2,1)S(1)}, bf16[64,2048]{1,0:T(8,128)(2,1)S(1)}, u32[]{:S(2)}, u32[]{:S(2)}) collective-permute-start(bf16[64,2048]{1,0:T(8,128)(2,1)S(1)} %get-tuple-element.139), channel_id=1, source_target_pairs={{0,4},{8,0},{16,8},{24,16},{28,24},{20,28},{12,20},{4,12},{1,5},{9... | collective-permute-start | bytes 786440 | tf_op jit(solution)/shard_map/combine_return/ppermute | solution.py:47
  247.7 1.9 copy-start.1
  (1 other events, 0.9 us)

commit v8 on v5

--- a/solution.py
+++ b/solution.py
@@ -96,6 +96,19 @@
     return total
 
 
+def split_exact(values):
+    first = lax.reduce_precision(values, exponent_bits=8, mantissa_bits=7)
+    rest = values - first
+    second = lax.reduce_precision(rest, exponent_bits=8, mantissa_bits=7)
+    third = rest - second
+    return jnp.concatenate([first, second, third], axis=-1).astype(jnp.bfloat16)
+
+
+def join_exact(parts, count):
+    parts = parts.astype(jnp.float32)
+    return (parts[..., :count] + parts[..., count : 2 * count]) + parts[..., 2 * count : 3 * count]
+
+
 def body(
     residual, attn_out, out_weight, post_gain, gate_up, down, route_ids, route_weight, final_gain
 ):
@@ -114,14 +127,22 @@
         dense_weight = jnp.sum(
             jnp.where(route_ids[:, :, None] == expert_ids, route_weight[:, :, None], 0.0), axis=1
         )
-        dense_weight = dense_weight.reshape(row_count, ep_size, local_experts).transpose(1, 0, 2)
-        row_weights = lax.all_to_all(dense_weight, "ep", split_axis=0, concat_axis=0, tiled=True)
-        row_weights = row_weights.reshape(group_rows, local_experts)
+        dense_weight = dense_weight.reshape(row_count, ep_size, local_experts)
 
     with jax.named_scope("out_projection"):
-        columns = attn_out.reshape(row_count, ep_size, slice_width).transpose(1, 0, 2)
-        columns = lax.all_to_all(columns, "ep", split_axis=0, concat_axis=0, tiled=True)
-        columns, row_weights = lax.optimization_barrier((columns, row_weights))
+        pad = (-3 * local_experts) % 128
+        payloads = jnp.concatenate(
+            [
+                attn_out.reshape(row_count, ep_size, slice_width).transpose(1, 0, 2),
+                split_exact(dense_weight).transpose(1, 0, 2),
+                jnp.zeros((ep_size, row_count, pad), jnp.bfloat16),
+            ],
+            axis=2,
+        )
+        payloads = lax.all_to_all(payloads, "ep", split_axis=0, concat_axis=0, tiled=True)
+        columns = payloads[:, :, :slice_width]
+        row_weights = join_exact(payloads[:, :, slice_width : slice_width + 3 * local_experts],
+                                 local_experts).reshape(group_rows, local_experts)
         partial = jnp.dot(
             columns.reshape(group_rows, slice_width), out_weight, preferred_element_type=jnp.float32
         )

time: 246 us -> 248 us (level)
  starting transfers between devices: 55.4 us -> 52.2 us
  local copies, waits for them, and re-layouts: 9.08 us -> 11.9 us
    all_to_all x2 -> x1, starting transfers between devices: 10.8 us -> 7.41 us  [body(): lax.all_to_all(payloads, 'ep', split_axis=0, concat_axis=0, tiled=True)]
    all_to_all x2 -> x1, waiting for transfers between devices: 12.5 us -> 15 us  [body(): lax.all_to_all(payloads, 'ep', split_axis=0, concat_axis=0, tiled=True)]
  transfers between devices with their start and end apart: 44 -> 43, of which waited for: 37 -> 37; matrix products, arithmetic and copies ran while one was open for 8% -> 8% of each run, Pallas kernels for 0% -> 0%
where the time goes in v8:
time: 248 us; the launch traced here: 247 us
  waiting for transfers between devices  94 us (38%)
  starting transfers between devices  52.2 us (21%)
  between operations  40.7 us (16%)
  matrix products  30 us (12%)
  other arithmetic  18.1 us (7%)
  local copies, waits for them, and re-layouts  11.9 us (5%)
    ppermute x7, waiting for transfers between devices, ring_all_gather(): lax.ppermute(got_fwd, 'ep', forward)  25 us
    ppermute x7, waiting for transfers between devices, ring_reduce_scatter_steps(): lax.ppermute(send_fwd, 'ep', forward)  21.6 us
    dot_general x4, matrix products, expert_mix(): projected_up = jnp.dot(rows, gate_up[e], preferred_element_type=jnp.float32)  18.1 us
    all_to_all x1, waiting for transfers between devices, body(): lax.all_to_all(payloads, 'ep', split_axis=0, concat_axis=0, tiled=True)  15 us
    ppermute x7, waiting for transfers between devices, ring_reduce_scatter(): lax.ppermute(send_fwd, 'ep', forward)  13.1 us
    dot_general x4, matrix products, expert_mix(): jnp.dot(activated, down[e], preferred_element_type=jnp.float32)  9.54 us
    ppermute x7, starting transfers between devices, ring_all_gather(): lax.ppermute(got_fwd, 'ep', forward)  8.25 us
    convert_element_type x6, other arithmetic, ring_reduce_scatter(): send_bwd.astype(jnp.bfloat16)  7.79 us
  transfers between devices with their start and end apart: 43, of which 37 were waited for; matrix products, arithmetic and copies ran while one was open for 8% of the time, Pallas kernels for 0%

profile of v8, /device:TPU:0, one launch (start us, length us, event | category | flops | bytes accessed | tf_op | source)
XLA Modules:
  0.0 247.0 jit_solution(12708240229990200579)
XLA Ops:
  1.8 2.3 copy.119
  4.0 1.5 copy.120
  5.6 1.3 maximum_maximum_fusion
  7.0 7.4 %all-to-all-start = ((bf16[8,128,640]{2,1,0:T(8,128)(2,1)}), bf16[8,128,640]{2,1,0:T(8,128)(2,1)S(1)}, u32[]{:S(2)}, u32[]{:S(2)}) async-start(bf16[8,128,640]{2,1,0:T(8,128)(2,1)} %maximum_maximum_fusion), calls=%async_computation | async-start | bytes 2621440 | tf_op jit(solution)/shard_map/out_projection/all_to_all | solution.py:142
  30.8 15.0 %all-to-all-done = bf16[8,128,640]{2,1,0:T(8,128)(2,1)S(1)} async-done(((bf16[8,128,640]{2,1,0:T(8,128)(2,1)}), bf16[8,128,640]{2,1,0:T(8,128)(2,1)S(1)}, u32[]{:S(2)}, u32[]{:S(2)}) %all-to-all-start) | async-done | bytes 1310752 | tf_op jit(solution)/shard_map/out_projection/all_to_all | solution.py:142
  45.8 2.3 fusion.40
  48.1 3.4 %copy-done.2 = f32[8,128,2048]{2,1,0:T(8,128)} copy-done((f32[8,128,2048]{2,1,0:T(8,128)}, f32[8,128,2048]{2,1,0:T(8,128)S(1)}, u32[]{:S(2)}) %copy-start.2) | copy-done | bytes 8388632
  51.6 2.0 collective-permute-start.1
  58.6 1.3 fusion.83
  59.9 2.1 collective-permute-start.2
  66.8 2.2 collective-permute-done.3
  69.0 1.3 fusion.81
  70.3 1.5 collective-permute-start.4
  76.8 1.4 collective-permute-done.5
  78.2 1.3 fusion.79
  79.5 1.3 collective-permute-start.6
  85.9 1.5 collective-permute-done.7
  87.4 1.3 fusion.77
  89.4 1.4 collective-permute-start.9
  94.1 2.3 collective-permute-done.8
  97.3 1.3 fusion.75
  99.2 1.5 collective-permute-start.11
  106.5 1.3 collective-permute-done.10
  108.3 1.3 fusion.73
  109.6 1.3 collective-permute-start.12
  112.1 6.4 %collective-permute-done.12 = bf16[64,2048]{1,0:T(8,128)(2,1)S(1)} collective-permute-done((bf16[64,2048]{1,0:T(8,128)(2,1)S(1)}, bf16[64,2048]{1,0:T(8,128)(2,1)S(1)}, u32[]{:S(2)}, u32[]{:S(2)}) %collective-permute-start.12) | collective-permute-done | bytes 262176 | tf_op jit(solution)/shard_map/out_projection/ppermute | solution.py:37
  118.8 1.3 fusion.96
  121.4 1.4 collective-permute-start.15
  123.5 4.4 %collective-permute-done.14 = bf16[64,2048]{1,0:T(8,128)(2,1)S(1)} collective-permute-done((bf16[64,2048]{1,0:T(8,128)(2,1)S(1)}, bf16[64,2048]{1,0:T(8,128)(2,1)S(1)}, u32[]{:S(2)}, u32[]{:S(2)}) %collective-permute-start.14) | collective-permute-done | bytes 262176 | tf_op jit(solution)/shard_map/dispatch_gather/ppermute | solution.py:55
  128.3 2.0 collective-permute-start.17
  130.3 5.9 %collective-permute-done.16 = bf16[64,2048]{1,0:T(8,128)(2,1)S(1)} collective-permute-done((bf16[64,2048]{1,0:T(8,128)(2,1)S(1)}, bf16[64,2048]{1,0:T(8,128)(2,1)S(1)}, u32[]{:S(2)}, u32[]{:S(2)}) %collective-permute-start.16) | collective-permute-done | bytes 262176 | tf_op jit(solution)/shard_map/dispatch_gather/ppermute | solution.py:55
  137.2 1.7 collective-permute-start.19
  138.9 4.3 %collective-permute-done.18 = bf16[64,2048]{1,0:T(8,128)(2,1)S(1)} collective-permute-done((bf16[64,2048]{1,0:T(8,128)(2,1)S(1)}, bf16[64,2048]{1,0:T(8,128)(2,1)S(1)}, u32[]{:S(2)}, u32[]{:S(2)}) %collective-permute-start.18) | collective-permute-done | bytes 262176 | tf_op jit(solution)/shard_map/dispatch_gather/ppermute | solution.py:55
  144.2 2.8 %collective-permute-start.20 = (bf16[64,2048]{1,0:T(8,128)(2,1)S(1)}, bf16[64,2048]{1,0:T(8,128)(2,1)S(1)}, u32[]{:S(2)}, u32[]{:S(2)}) collective-permute-start(bf16[64,2048]{1,0:T(8,128)(2,1)S(1)} %collective-permute-done.18), channel_id=1, source_target_pairs={{0,8},{8,16},{16,24},{24,28},{28,20},{20,12},{12,4},{4,0},{1,9},{9... | collective-permute-start | bytes 786440 | tf_op jit(solution)/shard_map/dispatch_gather/ppermute | solution.py:55
  147.0 3.8 %collective-permute-done.20 = bf16[64,2048]{1,0:T(8,128)(2,1)S(1)} collective-permute-done((bf16[64,2048]{1,0:T(8,128)(2,1)S(1)}, bf16[64,2048]{1,0:T(8,128)(2,1)S(1)}, u32[]{:S(2)}, u32[]{:S(2)}) %collective-permute-start.20) | collective-permute-done | bytes 262176 | tf_op jit(solution)/shard_map/dispatch_gather/ppermute | solution.py:55
  150.9 2.5 %collective-permute-done.21 = bf16[64,2048]{1,0:T(8,128)(2,1)S(1)} collective-permute-done((bf16[64,2048]{1,0:T(8,128)(2,1)S(1)}, bf16[64,2048]{1,0:T(8,128)(2,1)S(1)}, u32[]{:S(2)}, u32[]{:S(2)}) %collective-permute-start.21) | collective-permute-done | bytes 262176 | tf_op jit(solution)/shard_map/dispatch_gather/ppermute | solution.py:55
  153.4 5.7 %fusion.4 = f32[512,1536]{1,0:T(8,128)S(1)} fusion(bf16[512,2048]{1,0:T(8,128)(2,1)S(1)} %constant_dynamic-update-slice_fusion.7, bf16[2,2048,1536]{2,1,0:T(8,128)(2,1)} %param.16), kind=kOutput, calls=%fused_computation.4 | convolution fusion | flops 3221225472 | bytes 11534336 | tf_op jit(solution)/shard_map/local_experts/dot_general | solution.py:87
  159.9 3.4 %fusion = f32[512,1536]{1,0:T(8,128)S(1)} fusion(bf16[512,2048]{1,0:T(8,128)(2,1)S(1)} %constant_dynamic-update-slice_fusion.7, bf16[2,2048,1536]{2,1,0:T(8,128)(2,1)S(1)} %bitcast.188), kind=kOutput, calls=%fused_computation | convolution fusion | flops 3221225472 | bytes 11534336 | tf_op jit(solution)/shard_map/local_experts/dot_general | solution.py:87
  163.3 1.8 fusion.23
  165.1 4.0 %fusion.111 = (bf16[512,2048]{1,0:T(8,128)(2,1)S(1)}, f32[512,2048]{1,0:T(8,128)}) fusion(bf16[2,768,2048]{2,1,0:T(8,128)(2,1)S(1)} %bitcast.192, f32[512,1536]{1,0:T(8,128)S(1)} %fusion, f32[512]{0:T(512)S(1)} %bitcast.186, bf16[512,2048]{1,0:T(8,128)(2,1)S(1)} %fusion.23, f32[512]{0:T(512)S(1)} %bitcast.185), kind=kOutput, calls=%fused_computation.179 | convolution fusion | flops 1620312064 | bytes 14684160 | tf_op jit(solution)/shard_map/local_experts/dot_general | solution.py:91
  169.2 2.1 collective-permute-start.28
  171.9 2.1 collective-permute-start.22
  174.0 4.3 %collective-permute-done.28 = bf16[64,2048]{1,0:T(8,128)(2,1)S(1)} collective-permute-done((bf16[64,2048]{1,0:T(8,128)(2,1)S(1)}, bf16[64,2048]{1,0:T(8,128)(2,1)S(1)}, u32[]{:S(2)}, u32[]{:S(2)}) %collective-permute-start.28) | collective-permute-done | bytes 262176 | tf_op jit(solution)/shard_map/combine_return/ppermute | solution.py:75
  178.3 2.1 collective-permute-done.29
  180.4 1.3 fusion.64
  182.2 1.6 collective-permute-start.31
  185.6 1.5 collective-permute-start.25
  188.6 1.3 fusion.63
  194.1 6.6 %collective-permute-done.26 = bf16[64,2048]{1,0:T(8,128)(2,1)S(1)} collective-permute-done((bf16[64,2048]{1,0:T(8,128)(2,1)S(1)}, bf16[64,2048]{1,0:T(8,128)(2,1)S(1)}, u32[]{:S(2)}, u32[]{:S(2)}) %collective-permute-start.26) | collective-permute-done | bytes 262176 | tf_op jit(solution)/shard_map/dispatch_gather/ppermute | solution.py:55
  200.7 1.9 collective-permute-done.27
  202.9 5.7 %fusion.6 = f32[512,1536]{1,0:T(8,128)S(1)} fusion(bf16[512,2048]{1,0:T(8,128)(2,1)S(1)} %constant_dynamic-update-slice_fusion, bf16[2,2048,1536]{2,1,0:T(8,128)(2,1)} %param.16), kind=kOutput, calls=%fused_computation.6 | convolution fusion | flops 3221225472 | bytes 11534336 | tf_op jit(solution)/shard_map/local_experts/dot_general | solution.py:87
  208.6 3.4 %fusion.2 = f32[512,1536]{1,0:T(8,128)S(1)} fusion(bf16[512,2048]{1,0:T(8,128)(2,1)S(1)} %constant_dynamic-update-slice_fusion, bf16[2,2048,1536]{2,1,0:T(8,128)(2,1)S(1)} %bitcast.190), kind=kOutput, calls=%fused_computation.2 | convolution fusion | flops 3221225472 | bytes 11534336 | tf_op jit(solution)/shard_map/local_experts/dot_general | solution.py:87
  212.1 1.3 fusion.62
  213.4 1.3 collective-permute-start.34
  215.5 1.8 fusion.20
  217.3 1.9 multiply_add_fusion.1
  219.2 3.1 %collective-permute-done.34 = bf16[64,2048]{1,0:T(8,128)(2,1)S(1)} collective-permute-done((bf16[64,2048]{1,0:T(8,128)(2,1)S(1)}, bf16[64,2048]{1,0:T(8,128)(2,1)S(1)}, u32[]{:S(2)}, u32[]{:S(2)}) %collective-permute-start.34) | collective-permute-done | bytes 262176 | tf_op jit(solution)/shard_map/combine_return/ppermute | solution.py:75
  223.8 1.5 collective-permute-start.37
  225.3 4.3 %collective-permute-done.36 = bf16[64,2048]{1,0:T(8,128)(2,1)S(1)} collective-permute-done((bf16[64,2048]{1,0:T(8,128)(2,1)S(1)}, bf16[64,2048]{1,0:T(8,128)(2,1)S(1)}, u32[]{:S(2)}, u32[]{:S(2)}) %collective-permute-start.36) | collective-permute-done | bytes 262176 | tf_op jit(solution)/shard_map/combine_return/ppermute | solution.py:75
  230.4 2.0 collective-permute-start.39
  232.4 4.3 %collective-permute-done.38 = bf16[64,2048]{1,0:T(8,128)(2,1)S(1)} collective-permute-done((bf16[64,2048]{1,0:T(8,128)(2,1)S(1)}, bf16[64,2048]{1,0:T(8,128)(2,1)S(1)}, u32[]{:S(2)}, u32[]{:S(2)}) %collective-permute-start.38) | collective-permute-done | bytes 262176 | tf_op jit(solution)/shard_map/combine_return/ppermute | solution.py:75
  236.9 1.7 collective-permute-start.40
  239.0 4.3 %collective-permute-done.40 = bf16[64,2048]{1,0:T(8,128)(2,1)S(1)} collective-permute-done((bf16[64,2048]{1,0:T(8,128)(2,1)S(1)}, bf16[64,2048]{1,0:T(8,128)(2,1)S(1)}, u32[]{:S(2)}, u32[]{:S(2)}) %collective-permute-start.40) | collective-permute-done | bytes 262176 | tf_op jit(solution)/shard_map/combine_return/ppermute | solution.py:75
  243.3 1.7 collective-permute-done.41
  (143 shorter events, 31.0 us)
Async XLA Ops:
  0.6 45.1 %copy-start = (bf16[512,2048]{1,0:T(8,128)(2,1)S(1)}, bf16[512,2048]{1,0:T(8,128)(2,1)}, u32[]{:S(2)}) copy-start(bf16[512,2048]{1,0:T(8,128)(2,1)} %param.14) | copy-start | bytes 6291460
  5.6 8.8 %copy-start.7 = (s32[8]{0:T(128)S(1)}, s32[8]{0:T(128)}, u32[]{:S(2)}) copy-start(s32[8]{0:T(128)} %constant.222.clone) | copy-start | bytes 100
  7.0 19.3 %copy-start.4 = (s32[8]{0:T(128)S(1)}, s32[8]{0:T(128)}, u32[]{:S(2)}) copy-start(s32[8]{0:T(128)} %constant.223.clone) | copy-start | bytes 100
  7.0 38.8 %all-to-all-start = ((bf16[8,128,640]{2,1,0:T(8,128)(2,1)}), bf16[8,128,640]{2,1,0:T(8,128)(2,1)S(1)}, u32[]{:S(2)}, u32[]{:S(2)}) async-start(bf16[8,128,640]{2,1,0:T(8,128)(2,1)} %maximum_maximum_fusion), calls=%async_computation | async-start | bytes 2621440 | tf_op jit(solution)/shard_map/out_projection/all_to_all | solution.py:142
  48.1 3.4 %copy-start.2 = (f32[8,128,2048]{2,1,0:T(8,128)}, f32[8,128,2048]{2,1,0:T(8,128)S(1)}, u32[]{:S(2)}) copy-start(f32[8,128,2048]{2,1,0:T(8,128)S(1)} %fusion.40) | copy-start | bytes 25165828
  51.6 7.0 %collective-permute-start = (bf16[64,2048]{1,0:T(8,128)(2,1)S(1)}, bf16[64,2048]{1,0:T(8,128)(2,1)S(1)}, u32[]{:S(2)}, u32[]{:S(2)}) collective-permute-start(bf16[64,2048]{1,0:T(8,128)(2,1)S(1)} %get-tuple-element.72), channel_id=1, source_target_pairs={{0,8},{8,16},{16,24},{24,28},{28,20},{20,12},{12,4},{4,0},{1,9},{9... | collective-permute-start | bytes 786440 | tf_op jit(solution)/shard_map/out_projection/ppermute | solution.py:37
  51.6 7.0 %collective-permute-start.1 = (bf16[64,2048]{1,0:T(8,128)(2,1)S(1)}, bf16[64,2048]{1,0:T(8,128)(2,1)S(1)}, u32[]{:S(2)}, u32[]{:S(2)}) collective-permute-start(bf16[64,2048]{1,0:T(8,128)(2,1)S(1)} %get-tuple-element.73), channel_id=1, source_target_pairs={{0,4},{8,0},{16,8},{24,16},{28,24},{20,28},{12,20},{4,12},{1,5},{9... | collective-permute-start | bytes 786440 | tf_op jit(solution)/shard_map/out_projection/ppermute | solution.py:37
  59.9 7.0 %collective-permute-start.2 = (bf16[64,2048]{1,0:T(8,128)(2,1)S(1)}, bf16[64,2048]{1,0:T(8,128)(2,1)S(1)}, u32[]{:S(2)}, u32[]{:S(2)}) collective-permute-start(bf16[64,2048]{1,0:T(8,128)(2,1)S(1)} %get-tuple-element.76), channel_id=1, source_target_pairs={{0,8},{8,16},{16,24},{24,28},{28,20},{20,12},{12,4},{4,0},{1,9},{9... | collective-permute-start | bytes 786440 | tf_op jit(solution)/shard_map/out_projection/ppermute | solution.py:37
  61.9 7.1 %collective-permute-start.3 = (bf16[64,2048]{1,0:T(8,128)(2,1)S(1)}, bf16[64,2048]{1,0:T(8,128)(2,1)S(1)}, u32[]{:S(2)}, u32[]{:S(2)}) collective-permute-start(bf16[64,2048]{1,0:T(8,128)(2,1)S(1)} %get-tuple-element.77), channel_id=1, source_target_pairs={{0,4},{8,0},{16,8},{24,16},{28,24},{20,28},{12,20},{4,12},{1,5},{9... | collective-permute-start | bytes 786440 | tf_op jit(solution)/shard_map/out_projection/ppermute | solution.py:37
  70.3 6.4 %collective-permute-start.4 = (bf16[64,2048]{1,0:T(8,128)(2,1)S(1)}, bf16[64,2048]{1,0:T(8,128)(2,1)S(1)}, u32[]{:S(2)}, u32[]{:S(2)}) collective-permute-start(bf16[64,2048]{1,0:T(8,128)(2,1)S(1)} %get-tuple-element.80), channel_id=1, source_target_pairs={{0,8},{8,16},{16,24},{24,28},{28,20},{20,12},{12,4},{4,0},{1,9},{9... | collective-permute-start | bytes 786440 | tf_op jit(solution)/shard_map/out_projection/ppermute | solution.py:37
  71.8 6.4 %collective-permute-start.5 = (bf16[64,2048]{1,0:T(8,128)(2,1)S(1)}, bf16[64,2048]{1,0:T(8,128)(2,1)S(1)}, u32[]{:S(2)}, u32[]{:S(2)}) collective-permute-start(bf16[64,2048]{1,0:T(8,128)(2,1)S(1)} %get-tuple-element.81), channel_id=1, source_target_pairs={{0,4},{8,0},{16,8},{24,16},{28,24},{20,28},{12,20},{4,12},{1,5},{9... | collective-permute-start | bytes 786440 | tf_op jit(solution)/shard_map/out_projection/ppermute | solution.py:37
  79.5 6.4 %collective-permute-start.6 = (bf16[64,2048]{1,0:T(8,128)(2,1)S(1)}, bf16[64,2048]{1,0:T(8,128)(2,1)S(1)}, u32[]{:S(2)}, u32[]{:S(2)}) collective-permute-start(bf16[64,2048]{1,0:T(8,128)(2,1)S(1)} %get-tuple-element.84), channel_id=1, source_target_pairs={{0,8},{8,16},{16,24},{24,28},{28,20},{20,12},{12,4},{4,0},{1,9},{9... | collective-permute-start | bytes 786440 | tf_op jit(solution)/shard_map/out_projection/ppermute | solution.py:37
  80.8 6.6 %collective-permute-start.7 = (bf16[64,2048]{1,0:T(8,128)(2,1)S(1)}, bf16[64,2048]{1,0:T(8,128)(2,1)S(1)}, u32[]{:S(2)}, u32[]{:S(2)}) collective-permute-start(bf16[64,2048]{1,0:T(8,128)(2,1)S(1)} %get-tuple-element.85), channel_id=1, source_target_pairs={{0,4},{8,0},{16,8},{24,16},{28,24},{20,28},{12,20},{4,12},{1,5},{9... | collective-permute-start | bytes 786440 | tf_op jit(solution)/shard_map/out_projection/ppermute | solution.py:37
  88.7 7.7 %collective-permute-start.8 = (bf16[64,2048]{1,0:T(8,128)(2,1)S(1)}, bf16[64,2048]{1,0:T(8,128)(2,1)S(1)}, u32[]{:S(2)}, u32[]{:S(2)}) collective-permute-start(bf16[64,2048]{1,0:T(8,128)(2,1)S(1)} %get-tuple-element.88), channel_id=1, source_target_pairs={{0,8},{8,16},{16,24},{24,28},{28,20},{20,12},{12,4},{4,0},{1,9},{9... | collective-permute-start | bytes 786440 | tf_op jit(solution)/shard_map/out_projection/ppermute | solution.py:37
  89.4 7.9 %collective-permute-start.9 = (bf16[64,2048]{1,0:T(8,128)(2,1)S(1)}, bf16[64,2048]{1,0:T(8,128)(2,1)S(1)}, u32[]{:S(2)}, u32[]{:S(2)}) collective-permute-start(bf16[64,2048]{1,0:T(8,128)(2,1)S(1)} %get-tuple-element.89), channel_id=1, source_target_pairs={{0,4},{8,0},{16,8},{24,16},{28,24},{20,28},{12,20},{4,12},{1,5},{9... | collective-permute-start | bytes 786440 | tf_op jit(solution)/shard_map/out_projection/ppermute | solution.py:37
  98.6 9.1 %collective-permute-start.10 = (bf16[64,2048]{1,0:T(8,128)(2,1)S(1)}, bf16[64,2048]{1,0:T(8,128)(2,1)S(1)}, u32[]{:S(2)}, u32[]{:S(2)}) collective-permute-start(bf16[64,2048]{1,0:T(8,128)(2,1)S(1)} %get-tuple-element.92), channel_id=1, source_target_pairs={{0,8},{8,16},{16,24},{24,28},{28,20},{20,12},{12,4},{4,0},{1,9},{9... | collective-permute-start | bytes 786440 | tf_op jit(solution)/shard_map/out_projection/ppermute | solution.py:37
  99.2 9.1 %collective-permute-start.11 = (bf16[64,2048]{1,0:T(8,128)(2,1)S(1)}, bf16[64,2048]{1,0:T(8,128)(2,1)S(1)}, u32[]{:S(2)}, u32[]{:S(2)}) collective-permute-start(bf16[64,2048]{1,0:T(8,128)(2,1)S(1)} %get-tuple-element.93), channel_id=1, source_target_pairs={{0,4},{8,0},{16,8},{24,16},{28,24},{20,28},{12,20},{4,12},{1,5},{9... | collective-permute-start | bytes 786440 | tf_op jit(solution)/shard_map/out_projection/ppermute | solution.py:37
  109.6 8.9 %collective-permute-start.12 = (bf16[64,2048]{1,0:T(8,128)(2,1)S(1)}, bf16[64,2048]{1,0:T(8,128)(2,1)S(1)}, u32[]{:S(2)}, u32[]{:S(2)}) collective-permute-start(bf16[64,2048]{1,0:T(8,128)(2,1)S(1)} %get-tuple-element.96), channel_id=1, source_target_pairs={{0,8},{8,16},{16,24},{24,28},{28,20},{20,12},{12,4},{4,0},{1,9},{9... | collective-permute-start | bytes 786440 | tf_op jit(solution)/shard_map/out_projection/ppermute | solution.py:37
  110.9 7.9 %collective-permute-start.13 = (bf16[64,2048]{1,0:T(8,128)(2,1)S(1)}, bf16[64,2048]{1,0:T(8,128)(2,1)S(1)}, u32[]{:S(2)}, u32[]{:S(2)}) collective-permute-start(bf16[64,2048]{1,0:T(8,128)(2,1)S(1)} %get-tuple-element.97), channel_id=1, source_target_pairs={{0,4},{8,0},{16,8},{24,16},{28,24},{20,28},{12,20},{4,12},{1,5},{9... | collective-permute-start | bytes 786440 | tf_op jit(solution)/shard_map/out_projection/ppermute | solution.py:37
  111.8 8.4 %copy-start.3 = (bf16[128,2048]{1,0:T(8,128)(2,1)S(1)}, bf16[128,2048]{1,0:T(8,128)(2,1)}, u32[]{:S(2)}) copy-start(bf16[128,2048]{1,0:T(8,128)(2,1)} %param.12) | copy-start | bytes 1572868
  112.1 8.3 %copy-start.5 = (f32[2048]{0:T(1024)S(1)}, f32[2048]{0:T(1024)}, u32[]{:S(2)}) copy-start(f32[2048]{0:T(1024)} %param.15) | copy-start | bytes 24580
  120.7 7.2 %collective-permute-start.14 = (bf16[64,2048]{1,0:T(8,128)(2,1)S(1)}, bf16[64,2048]{1,0:T(8,128)(2,1)S(1)}, u32[]{:S(2)}, u32[]{:S(2)}) collective-permute-start(bf16[64,2048]{1,0:T(8,128)(2,1)S(1)} %get-tuple-element.193), channel_id=1, source_target_pairs={{0,8},{8,16},{16,24},{24,28},{28,20},{20,12},{12,4},{4,0},{1,9},{9... | collective-permute-start | bytes 786440 | tf_op jit(solution)/shard_map/dispatch_gather/ppermute | solution.py:55
  121.4 6.8 %collective-permute-start.15 = (bf16[64,2048]{1,0:T(8,128)(2,1)S(1)}, bf16[64,2048]{1,0:T(8,128)(2,1)S(1)}, u32[]{:S(2)}, u32[]{:S(2)}) collective-permute-start(bf16[64,2048]{1,0:T(8,128)(2,1)S(1)} %get-tuple-element.192), channel_id=1, source_target_pairs={{0,4},{8,0},{16,8},{24,16},{28,24},{20,28},{12,20},{4,12},{1,5},{9... | collective-permute-start | bytes 786440 | tf_op jit(solution)/shard_map/dispatch_gather/ppermute | solution.py:55
  128.2 8.0 %collective-permute-start.16 = (bf16[64,2048]{1,0:T(8,128)(2,1)S(1)}, bf16[64,2048]{1,0:T(8,128)(2,1)S(1)}, u32[]{:S(2)}, u32[]{:S(2)}) collective-permute-start(bf16[64,2048]{1,0:T(8,128)(2,1)S(1)} %collective-permute-done.14), channel_id=1, source_target_pairs={{0,8},{8,16},{16,24},{24,28},{28,20},{20,12},{12,4},{4,0},{1,9},{9... | collective-permute-start | bytes 786440 | tf_op jit(solution)/shard_map/dispatch_gather/ppermute | solution.py:55
  128.3 8.0 %collective-permute-start.17 = (bf16[64,2048]{1,0:T(8,128)(2,1)S(1)}, bf16[64,2048]{1,0:T(8,128)(2,1)S(1)}, u32[]{:S(2)}, u32[]{:S(2)}) collective-permute-start(bf16[64,2048]{1,0:T(8,128)(2,1)S(1)} %collective-permute-done.15), channel_id=1, source_target_pairs={{0,4},{8,0},{16,8},{24,16},{28,24},{20,28},{12,20},{4,12},{1,5},{9... | collective-permute-start | bytes 786440 | tf_op jit(solution)/shard_map/dispatch_gather/ppermute | solution.py:55
  136.2 7.0 %collective-permute-start.18 = (bf16[64,2048]{1,0:T(8,128)(2,1)S(1)}, bf16[64,2048]{1,0:T(8,128)(2,1)S(1)}, u32[]{:S(2)}, u32[]{:S(2)}) collective-permute-start(bf16[64,2048]{1,0:T(8,128)(2,1)S(1)} %collective-permute-done.16), channel_id=1, source_target_pairs={{0,8},{8,16},{16,24},{24,28},{28,20},{20,12},{12,4},{4,0},{1,9},{9... | collective-permute-start | bytes 786440 | tf_op jit(solution)/shard_map/dispatch_gather/ppermute | solution.py:55
  137.2 7.0 %collective-permute-start.19 = (bf16[64,2048]{1,0:T(8,128)(2,1)S(1)}, bf16[64,2048]{1,0:T(8,128)(2,1)S(1)}, u32[]{:S(2)}, u32[]{:S(2)}) collective-permute-start(bf16[64,2048]{1,0:T(8,128)(2,1)S(1)} %collective-permute-done.17), channel_id=1, source_target_pairs={{0,4},{8,0},{16,8},{24,16},{28,24},{20,28},{12,20},{4,12},{1,5},{9... | collective-permute-start | bytes 786440 | tf_op jit(solution)/shard_map/dispatch_gather/ppermute | solution.py:55
  144.2 6.6 %collective-permute-start.20 = (bf16[64,2048]{1,0:T(8,128)(2,1)S(1)}, bf16[64,2048]{1,0:T(8,128)(2,1)S(1)}, u32[]{:S(2)}, u32[]{:S(2)}) collective-permute-start(bf16[64,2048]{1,0:T(8,128)(2,1)S(1)} %collective-permute-done.18), channel_id=1, source_target_pairs={{0,8},{8,16},{16,24},{24,28},{28,20},{20,12},{12,4},{4,0},{1,9},{9... | collective-permute-start | bytes 786440 | tf_op jit(solution)/shard_map/dispatch_gather/ppermute | solution.py:55
  147.0 6.4 %collective-permute-start.21 = (bf16[64,2048]{1,0:T(8,128)(2,1)S(1)}, bf16[64,2048]{1,0:T(8,128)(2,1)S(1)}, u32[]{:S(2)}, u32[]{:S(2)}) collective-permute-start(bf16[64,2048]{1,0:T(8,128)(2,1)S(1)} %collective-permute-done.19), channel_id=1, source_target_pairs={{0,4},{8,0},{16,8},{24,16},{28,24},{20,28},{12,20},{4,12},{1,5},{9... | collective-permute-start | bytes 786440 | tf_op jit(solution)/shard_map/dispatch_gather/ppermute | solution.py:55
  147.0 16.3 %slice-start.6 = ((s8[6291456]{0:T(1024)(128)(4,1)}), s8[4194304]{0:T(1024)(128)(4,1)S(1)}, s32[]{:S(2)}) async-start(s8[6291456]{0:T(1024)(128)(4,1)} %bitcast.191), calls=%async_computation.7 | async-start | bytes 8388608
  153.3 5.8 %slice-start = ((s8[12582912]{0:T(1024)(128)(4,1)}), s8[4194304]{0:T(1024)(128)(4,1)S(1)}, s32[]{:S(2)}) async-start(s8[12582912]{0:T(1024)(128)(4,1)} %bitcast.187), calls=%async_computation.1 | async-start | bytes 8388608
  153.4 5.7 %slice-start.1 = ((s8[12582912]{0:T(1024)(128)(4,1)}), s8[4194304]{0:T(1024)(128)(4,1)S(1)}, s32[]{:S(2)}) async-start(s8[12582912]{0:T(1024)(128)(4,1)} %bitcast.187), calls=%async_computation.2 | async-start | bytes 8388608
  153.4 6.5 %slice-start.2 = ((s8[12582912]{0:T(1024)(128)(4,1)}), s8[4194304]{0:T(1024)(128)(4,1)S(1)}, s32[]{:S(2)}) async-start(s8[12582912]{0:T(1024)(128)(4,1)} %bitcast.187), calls=%async_computation.3 | async-start | bytes 8388608
  153.4 9.9 %slice-start.7 = ((s8[6291456]{0:T(1024)(128)(4,1)}), s8[2097152]{0:T(1024)(128)(4,1)S(1)}, s32[]{:S(2)}) async-start(s8[6291456]{0:T(1024)(128)(4,1)} %bitcast.191), calls=%async_computation.8 | async-start | bytes 4194304
  169.2 9.2 %collective-permute-start.28 = (bf16[64,2048]{1,0:T(8,128)(2,1)S(1)}, bf16[64,2048]{1,0:T(8,128)(2,1)S(1)}, u32[]{:S(2)}, u32[]{:S(2)}) collective-permute-start(bf16[64,2048]{1,0:T(8,128)(2,1)S(1)} %get-tuple-element.114), channel_id=1, source_target_pairs={{0,8},{8,16},{16,24},{24,28},{28,20},{20,12},{12,4},{4,0},{1,9},{9... | collective-permute-start | bytes 786440 | tf_op jit(solution)/shard_map/combine_return/ppermute | solution.py:75
  171.3 9.2 %collective-permute-start.29 = (bf16[64,2048]{1,0:T(8,128)(2,1)S(1)}, bf16[64,2048]{1,0:T(8,128)(2,1)S(1)}, u32[]{:S(2)}, u32[]{:S(2)}) collective-permute-start(bf16[64,2048]{1,0:T(8,128)(2,1)S(1)} %get-tuple-element.115), channel_id=1, source_target_pairs={{0,4},{8,0},{16,8},{24,16},{28,24},{20,28},{12,20},{4,12},{1,5},{9... | collective-permute-start | bytes 786440 | tf_op jit(solution)/shard_map/combine_return/ppermute | solution.py:75
  171.9 11.9 %collective-permute-start.22 = (bf16[64,2048]{1,0:T(8,128)(2,1)S(1)}, bf16[64,2048]{1,0:T(8,128)(2,1)S(1)}, u32[]{:S(2)}, u32[]{:S(2)}) collective-permute-start(bf16[64,2048]{1,0:T(8,128)(2,1)S(1)} %collective-permute-done.20), channel_id=1, source_target_pairs={{0,8},{8,16},{16,24},{24,28},{28,20},{20,12},{12,4},{4,0},{1,9},{9... | collective-permute-start | bytes 786440 | tf_op jit(solution)/shard_map/dispatch_gather/ppermute | solution.py:55
  174.0 11.0 %collective-permute-start.23 = (bf16[64,2048]{1,0:T(8,128)(2,1)S(1)}, bf16[64,2048]{1,0:T(8,128)(2,1)S(1)}, u32[]{:S(2)}, u32[]{:S(2)}) collective-permute-start(bf16[64,2048]{1,0:T(8,128)(2,1)S(1)} %collective-permute-done.21), channel_id=1, source_target_pairs={{0,4},{8,0},{16,8},{24,16},{28,24},{20,28},{12,20},{4,12},{1,5},{9... | collective-permute-start | bytes 786440 | tf_op jit(solution)/shard_map/dispatch_gather/ppermute | solution.py:55
  181.8 6.4 %collective-permute-start.30 = (bf16[64,2048]{1,0:T(8,128)(2,1)S(1)}, bf16[64,2048]{1,0:T(8,128)(2,1)S(1)}, u32[]{:S(2)}, u32[]{:S(2)}) collective-permute-start(bf16[64,2048]{1,0:T(8,128)(2,1)S(1)} %get-tuple-element.118), channel_id=1, source_target_pairs={{0,8},{8,16},{16,24},{24,28},{28,20},{20,12},{12,4},{4,0},{1,9},{9... | collective-permute-start | bytes 786440 | tf_op jit(solution)/shard_map/combine_return/ppermute | solution.py:75
  182.2 6.4 %collective-permute-start.31 = (bf16[64,2048]{1,0:T(8,128)(2,1)S(1)}, bf16[64,2048]{1,0:T(8,128)(2,1)S(1)}, u32[]{:S(2)}, u32[]{:S(2)}) collective-permute-start(bf16[64,2048]{1,0:T(8,128)(2,1)S(1)} %get-tuple-element.119), channel_id=1, source_target_pairs={{0,4},{8,0},{16,8},{24,16},{28,24},{20,28},{12,20},{4,12},{1,5},{9... | collective-permute-start | bytes 786440 | tf_op jit(solution)/shard_map/combine_return/ppermute | solution.py:75
  185.0 7.0 %collective-permute-start.24 = (bf16[64,2048]{1,0:T(8,128)(2,1)S(1)}, bf16[64,2048]{1,0:T(8,128)(2,1)S(1)}, u32[]{:S(2)}, u32[]{:S(2)}) collective-permute-start(bf16[64,2048]{1,0:T(8,128)(2,1)S(1)} %collective-permute-done.22), channel_id=1, source_target_pairs={{0,8},{8,16},{16,24},{24,28},{28,20},{20,12},{12,4},{4,0},{1,9},{9... | collective-permute-start | bytes 786440 | tf_op jit(solution)/shard_map/dispatch_gather/ppermute | solution.py:55
  185.6 6.4 %collective-permute-start.25 = (bf16[64,2048]{1,0:T(8,128)(2,1)S(1)}, bf16[64,2048]{1,0:T(8,128)(2,1)S(1)}, u32[]{:S(2)}, u32[]{:S(2)}) collective-permute-start(bf16[64,2048]{1,0:T(8,128)(2,1)S(1)} %collective-permute-done.23), channel_id=1, source_target_pairs={{0,4},{8,0},{16,8},{24,16},{28,24},{20,28},{12,20},{4,12},{1,5},{9... | collective-permute-start | bytes 786440 | tf_op jit(solution)/shard_map/dispatch_gather/ppermute | solution.py:55
  189.9 22.2 %collective-permute-start.32 = (bf16[64,2048]{1,0:T(8,128)(2,1)S(1)}, bf16[64,2048]{1,0:T(8,128)(2,1)S(1)}, u32[]{:S(2)}, u32[]{:S(2)}) collective-permute-start(bf16[64,2048]{1,0:T(8,128)(2,1)S(1)} %get-tuple-element.122), channel_id=1, source_target_pairs={{0,8},{8,16},{16,24},{24,28},{28,20},{20,12},{12,4},{4,0},{1,9},{9... | collective-permute-start | bytes 786440 | tf_op jit(solution)/shard_map/combine_return/ppermute | solution.py:75
  191.2 20.9 %collective-permute-start.33 = (bf16[64,2048]{1,0:T(8,128)(2,1)S(1)}, bf16[64,2048]{1,0:T(8,128)(2,1)S(1)}, u32[]{:S(2)}, u32[]{:S(2)}) collective-permute-start(bf16[64,2048]{1,0:T(8,128)(2,1)S(1)} %get-tuple-element.123), channel_id=1, source_target_pairs={{0,4},{8,0},{16,8},{24,16},{28,24},{20,28},{12,20},{4,12},{1,5},{9... | collective-permute-start | bytes 786440 | tf_op jit(solution)/shard_map/combine_return/ppermute | solution.py:75
  192.0 8.7 %collective-permute-start.26 = (bf16[64,2048]{1,0:T(8,128)(2,1)S(1)}, bf16[64,2048]{1,0:T(8,128)(2,1)S(1)}, u32[]{:S(2)}, u32[]{:S(2)}) collective-permute-start(bf16[64,2048]{1,0:T(8,128)(2,1)S(1)} %collective-permute-done.24), channel_id=1, source_target_pairs={{0,8},{8,16},{16,24},{24,28},{28,20},{20,12},{12,4},{4,0},{1,9},{9... | collective-permute-start | bytes 786440 | tf_op jit(solution)/shard_map/dispatch_gather/ppermute | solution.py:55
  193.2 9.5 %collective-permute-start.27 = (bf16[64,2048]{1,0:T(8,128)(2,1)S(1)}, bf16[64,2048]{1,0:T(8,128)(2,1)S(1)}, u32[]{:S(2)}, u32[]{:S(2)}) collective-permute-start(bf16[64,2048]{1,0:T(8,128)(2,1)S(1)} %collective-permute-done.25), channel_id=1, source_target_pairs={{0,4},{8,0},{16,8},{24,16},{28,24},{20,28},{12,20},{4,12},{1,5},{9... | collective-permute-start | bytes 786440 | tf_op jit(solution)/shard_map/dispatch_gather/ppermute | solution.py:55
  194.1 14.5 %slice-start.3 = ((s8[12582912]{0:T(1024)(128)(4,1)}), s8[4194304]{0:T(1024)(128)(4,1)S(1)}, s32[]{:S(2)}) async-start(s8[12582912]{0:T(1024)(128)(4,1)} %bitcast.189), calls=%async_computation.4 | async-start | bytes 8388608
  202.9 5.7 %slice-start.4 = ((s8[12582912]{0:T(1024)(128)(4,1)}), s8[4194304]{0:T(1024)(128)(4,1)S(1)}, s32[]{:S(2)}) async-start(s8[12582912]{0:T(1024)(128)(4,1)} %bitcast.189), calls=%async_computation.5 | async-start | bytes 8388608
  202.9 5.7 %slice-start.5 = ((s8[12582912]{0:T(1024)(128)(4,1)}), s8[4194304]{0:T(1024)(128)(4,1)S(1)}, s32[]{:S(2)}) async-start(s8[12582912]{0:T(1024)(128)(4,1)} %bitcast.189), calls=%async_computation.6 | async-start | bytes 8388608
  202.9 12.6 %slice-start.8 = ((s8[6291456]{0:T(1024)(128)(4,1)}), s8[4194304]{0:T(1024)(128)(4,1)S(1)}, s32[]{:S(2)}) async-start(s8[6291456]{0:T(1024)(128)(4,1)} %bitcast.193), calls=%async_computation.9 | async-start | bytes 8388608
  208.6 6.8 %slice-start.9 = ((s8[6291456]{0:T(1024)(128)(4,1)}), s8[2097152]{0:T(1024)(128)(4,1)S(1)}, s32[]{:S(2)}) async-start(s8[6291456]{0:T(1024)(128)(4,1)} %bitcast.193), calls=%async_computation.10 | async-start | bytes 4194304
  213.4 9.0 %collective-permute-start.34 = (bf16[64,2048]{1,0:T(8,128)(2,1)S(1)}, bf16[64,2048]{1,0:T(8,128)(2,1)S(1)}, u32[]{:S(2)}, u32[]{:S(2)}) collective-permute-start(bf16[64,2048]{1,0:T(8,128)(2,1)S(1)} %get-tuple-element.126), channel_id=1, source_target_pairs={{0,8},{8,16},{16,24},{24,28},{28,20},{20,12},{12,4},{4,0},{1,9},{9... | collective-permute-start | bytes 786440 | tf_op jit(solution)/shard_map/combine_return/ppermute | solution.py:75
  214.7 8.4 %collective-permute-start.35 = (bf16[64,2048]{1,0:T(8,128)(2,1)S(1)}, bf16[64,2048]{1,0:T(8,128)(2,1)S(1)}, u32[]{:S(2)}, u32[]{:S(2)}) collective-permute-start(bf16[64,2048]{1,0:T(8,128)(2,1)S(1)} %get-tuple-element.127), channel_id=1, source_target_pairs={{0,4},{8,0},{16,8},{24,16},{28,24},{20,28},{12,20},{4,12},{1,5},{9... | collective-permute-start | bytes 786440 | tf_op jit(solution)/shard_map/combine_return/ppermute | solution.py:75
  223.2 6.4 %collective-permute-start.36 = (bf16[64,2048]{1,0:T(8,128)(2,1)S(1)}, bf16[64,2048]{1,0:T(8,128)(2,1)S(1)}, u32[]{:S(2)}, u32[]{:S(2)}) collective-permute-start(bf16[64,2048]{1,0:T(8,128)(2,1)S(1)} %get-tuple-element.130), channel_id=1, source_target_pairs={{0,8},{8,16},{16,24},{24,28},{28,20},{20,12},{12,4},{4,0},{1,9},{9... | collective-permute-start | bytes 786440 | tf_op jit(solution)/shard_map/combine_return/ppermute | solution.py:75
  223.8 6.4 %collective-permute-start.37 = (bf16[64,2048]{1,0:T(8,128)(2,1)S(1)}, bf16[64,2048]{1,0:T(8,128)(2,1)S(1)}, u32[]{:S(2)}, u32[]{:S(2)}) collective-permute-start(bf16[64,2048]{1,0:T(8,128)(2,1)S(1)} %get-tuple-element.131), channel_id=1, source_target_pairs={{0,4},{8,0},{16,8},{24,16},{28,24},{20,28},{12,20},{4,12},{1,5},{9... | collective-permute-start | bytes 786440 | tf_op jit(solution)/shard_map/combine_return/ppermute | solution.py:75
  230.3 6.4 %collective-permute-start.38 = (bf16[64,2048]{1,0:T(8,128)(2,1)S(1)}, bf16[64,2048]{1,0:T(8,128)(2,1)S(1)}, u32[]{:S(2)}, u32[]{:S(2)}) collective-permute-start(bf16[64,2048]{1,0:T(8,128)(2,1)S(1)} %get-tuple-element.134), channel_id=1, source_target_pairs={{0,8},{8,16},{16,24},{24,28},{28,20},{20,12},{12,4},{4,0},{1,9},{9... | collective-permute-start | bytes 786440 | tf_op jit(solution)/shard_map/combine_return/ppermute | solution.py:75
  230.4 6.4 %collective-permute-start.39 = (bf16[64,2048]{1,0:T(8,128)(2,1)S(1)}, bf16[64,2048]{1,0:T(8,128)(2,1)S(1)}, u32[]{:S(2)}, u32[]{:S(2)}) collective-permute-start(bf16[64,2048]{1,0:T(8,128)(2,1)S(1)} %get-tuple-element.135), channel_id=1, source_target_pairs={{0,4},{8,0},{16,8},{24,16},{28,24},{20,28},{12,20},{4,12},{1,5},{9... | collective-permute-start | bytes 786440 | tf_op jit(solution)/shard_map/combine_return/ppermute | solution.py:75
  236.9 8.5 %copy-start.6 = (f32[2048]{0:T(1024)S(1)}, f32[2048]{0:T(1024)}, u32[]{:S(2)}) copy-start(f32[2048]{0:T(1024)} %param.20) | copy-start | bytes 24580
  236.9 6.4 %collective-permute-start.40 = (bf16[64,2048]{1,0:T(8,128)(2,1)S(1)}, bf16[64,2048]{1,0:T(8,128)(2,1)S(1)}, u32[]{:S(2)}, u32[]{:S(2)}) collective-permute-start(bf16[64,2048]{1,0:T(8,128)(2,1)S(1)} %get-tuple-element.138), channel_id=1, source_target_pairs={{0,8},{8,16},{16,24},{24,28},{28,20},{20,12},{12,4},{4,0},{1,9},{9... | collective-permute-start | bytes 786440 | tf_op jit(solution)/shard_map/combine_return/ppermute | solution.py:75
  238.6 6.4 %collective-permute-start.41 = (bf16[64,2048]{1,0:T(8,128)(2,1)S(1)}, bf16[64,2048]{1,0:T(8,128)(2,1)S(1)}, u32[]{:S(2)}, u32[]{:S(2)}) collective-permute-start(bf16[64,2048]{1,0:T(8,128)(2,1)S(1)} %get-tuple-element.139), channel_id=1, source_target_pairs={{0,4},{8,0},{16,8},{24,16},{28,24},{20,28},{12,20},{4,12},{1,5},{9... | collective-permute-start | bytes 786440 | tf_op jit(solution)/shard_map/combine_return/ppermute | solution.py:75
  245.1 1.9 copy-start.1

commit v9 on v5

--- a/solution.py
+++ b/solution.py
@@ -144,8 +144,8 @@
         return w_fwd, w_bwd
 
     with jax.named_scope("local_experts"):
-        first = (ep_size - 1 + 1) // 2
-        chunks = [list(range(first)), list(range(first, ep_size - 1))]
+        steps_all = list(range(ep_size - 1))
+        chunks = [steps_all[i : i + 2] for i in range(0, ep_size - 1, 2)]
         pieces = [None] * (ep_size - 1)
         own_part = None
         for c, steps in enumerate(chunks):

time: 246 us -> 220 us (0.89)
  waiting for transfers between devices: 92.7 us -> 69.3 us
  other arithmetic: 17.1 us -> 13.6 us
    ppermute x7, waiting for transfers between devices: 26.1 us -> 9.08 us  [ring_all_gather(): lax.ppermute(got_fwd, 'ep', forward)]
    ppermute x7, waiting for transfers between devices: 21.6 us -> 17.1 us  [ring_reduce_scatter_steps(): lax.ppermute(send_fwd, 'ep', forward)]
    convert_element_type x6, other arithmetic: 4.27 us -> 0.68 us  [ring_reduce_scatter_steps(): send_bwd.astype(jnp.bfloat16)]
    ppermute x7, waiting for transfers between devices: 6.67 us -> 3.89 us  [ring_reduce_scatter_steps(): lax.ppermute(send_bwd, 'ep', backward)]
    dot_general x4 -> x8, matrix products: 18.1 us -> 20.1 us  [expert_mix(): projected_up = jnp.dot(rows, gate_up[e], preferred_element_type=jnp.float32)]
    dot_general x4 -> x8, matrix products: 9.52 us -> 8.31 us  [expert_mix(): jnp.dot(activated, down[e], preferred_element_type=jnp.float32)]
    unnamed x50 -> x36, local copies, waits for them, and re-layouts: 4.94 us -> 4.14 us
  transfers between devices with their start and end apart: 44 -> 44, of which waited for: 37 -> 34; matrix products, arithmetic and copies ran while one was open for 8% -> 15% of each run, Pallas kernels for 0% -> 0%
where the time goes in v9:
time: 220 us; the launch traced here: 219 us
  waiting for transfers between devices  69.3 us (32%)
  starting transfers between devices  56.3 us (26%)
  between operations  40.4 us (18%)
  matrix products  30.8 us (14%)
  other arithmetic  13.6 us (6%)
  local copies, waits for them, and re-layouts  8.18 us (4%)
    dot_general x8, matrix products, expert_mix(): projected_up = jnp.dot(rows, gate_up[e], preferred_element_type=jnp.float32)  20.1 us
    ppermute x7, waiting for transfers between devices, ring_reduce_scatter_steps(): lax.ppermute(send_fwd, 'ep', forward)  17.1 us
    ppermute x7, waiting for transfers between devices, ring_reduce_scatter(): lax.ppermute(send_fwd, 'ep', forward)  11.6 us
    ppermute x7, starting transfers between devices, ring_reduce_scatter_steps(): lax.ppermute(send_bwd, 'ep', backward)  9.27 us
    ppermute x7, waiting for transfers between devices, ring_all_gather(): lax.ppermute(got_fwd, 'ep', forward)  9.08 us
    ppermute x7, starting transfers between devices, ring_all_gather(): lax.ppermute(got_bwd, 'ep', backward)  8.58 us
    all_to_all x1, waiting for transfers between devices, body(): lax.all_to_all(columns, 'ep', split_axis=0, concat_axis=0, tiled=True)  8.34 us
    dot_general x8, matrix products, expert_mix(): jnp.dot(activated, down[e], preferred_element_type=jnp.float32)  8.31 us
  transfers between devices with their start and end apart: 44, of which 34 were waited for; matrix products, arithmetic and copies ran while one was open for 15% of the time, Pallas kernels for 0%

profile of v9, /device:TPU:0, one launch (start us, length us, event | category | flops | bytes accessed | tf_op | source)
XLA Modules:
  0.0 218.6 jit_solution(2730049927843850142)
XLA Ops:
  0.6 1.5 select_reduce_fusion
  2.1 7.3 %all-to-all-start.1 = ((f32[8,128,2]{1,2,0:T(2,128)}), f32[8,128,2]{1,2,0:T(2,128)S(1)}, u32[]{:S(2)}, u32[]{:S(2)}) async-start(f32[8,128,2]{1,2,0:T(2,128)} %bitcast.2), calls=%async_computation.1 | async-start | bytes 16384 | tf_op jit(solution)/shard_map/route_weights/all_to_all | solution.py:118
  9.4 2.3 %copy.25 = bf16[16,8,8,512]{3,2,0,1:T(8,128)(2,1)} copy(bf16[16,8,8,512]{3,2,1,0:T(8,128)(2,1)} %bitcast.244) | data formatting | bytes 2097152 | tf_op jit(solution)/shard_map/out_projection/reshape | solution.py:122
  11.7 4.2 %all-to-all-done.1 = f32[8,128,2]{1,2,0:T(2,128)S(1)} async-done(((f32[8,128,2]{1,2,0:T(2,128)}), f32[8,128,2]{1,2,0:T(2,128)S(1)}, u32[]{:S(2)}, u32[]{:S(2)}) %all-to-all-start.1) | async-done | bytes 8224 | tf_op jit(solution)/shard_map/route_weights/all_to_all | solution.py:118
  15.9 3.6 %all-to-all-start = ((bf16[8,128,512]{2,1,0:T(8,128)(2,1)}), bf16[8,128,512]{2,1,0:T(8,128)(2,1)S(1)}, u32[]{:S(2)}, u32[]{:S(2)}) async-start(bf16[8,128,512]{2,1,0:T(8,128)(2,1)} %bitcast.242), calls=%async_computation | async-start | bytes 2097152 | tf_op jit(solution)/shard_map/out_projection/all_to_all | solution.py:123
  35.9 8.3 %all-to-all-done = bf16[8,128,512]{2,1,0:T(8,128)(2,1)S(1)} async-done(((bf16[8,128,512]{2,1,0:T(8,128)(2,1)}), bf16[8,128,512]{2,1,0:T(8,128)(2,1)S(1)}, u32[]{:S(2)}, u32[]{:S(2)}) %all-to-all-start) | async-done | bytes 1048608 | tf_op jit(solution)/shard_map/out_projection/all_to_all | solution.py:123
  44.2 2.3 %fusion.124 = f32[8,128,2048]{2,1,0:T(8,128)S(1)} fusion(bf16[8,128,512]{2,1,0:T(8,128)(2,1)S(1)} %all-to-all-done, bf16[512,2048]{1,0:T(8,128)(2,1)S(1)} %copy-done), kind=kOutput, calls=%fused_computation.68 | convolution fusion | flops 2147483648 | bytes 11534336 | tf_op jit(solution)/shard_map/out_projection/dot_general | solution.py:125
  46.6 3.3 %copy-done.2 = f32[8,128,2048]{2,1,0:T(8,128)} copy-done((f32[8,128,2048]{2,1,0:T(8,128)}, f32[8,128,2048]{2,1,0:T(8,128)S(1)}, u32[]{:S(2)}) %copy-start.2) | copy-done | bytes 8388632
  50.0 2.0 collective-permute-start.1
  56.6 1.3 fusion.170
  58.5 1.5 collective-permute-start.3
  64.3 2.1 collective-permute-done.3
  66.4 1.3 fusion.168
  67.7 1.8 collective-permute-start.4
  74.2 1.8 collective-permute-done.5
  75.9 1.3 fusion.166
  77.2 1.8 collective-permute-start.6
  83.7 1.9 collective-permute-done.7
  85.6 1.3 fusion.164
  87.4 1.5 collective-permute-start.9
  92.8 1.7 collective-permute-done.8
  95.2 1.3 fusion.162
  97.1 1.5 collective-permute-start.11
  105.7 1.3 fusion.160
  107.1 1.7 collective-permute-start.12
  109.2 6.3 %collective-permute-done.12 = bf16[64,2048]{1,0:T(8,128)(2,1)S(1)} collective-permute-done((bf16[64,2048]{1,0:T(8,128)(2,1)S(1)}, bf16[64,2048]{1,0:T(8,128)(2,1)S(1)}, u32[]{:S(2)}, u32[]{:S(2)}) %collective-permute-start.12) | collective-permute-done | bytes 262176 | tf_op jit(solution)/shard_map/out_projection/ppermute | solution.py:37
  116.2 1.3 fusion.183
  118.0 1.6 collective-permute-start.15
  120.2 5.7 %collective-permute-done.15 = bf16[64,2048]{1,0:T(8,128)(2,1)S(1)} collective-permute-done((bf16[64,2048]{1,0:T(8,128)(2,1)S(1)}, bf16[64,2048]{1,0:T(8,128)(2,1)S(1)}, u32[]{:S(2)}, u32[]{:S(2)}) %collective-permute-start.15) | collective-permute-done | bytes 262176 | tf_op jit(solution)/shard_map/dispatch_gather/ppermute | solution.py:55
  126.9 2.1 collective-permute-start.17
  129.0 4.3 %collective-permute-done.16 = bf16[64,2048]{1,0:T(8,128)(2,1)S(1)} collective-permute-done((bf16[64,2048]{1,0:T(8,128)(2,1)S(1)}, bf16[64,2048]{1,0:T(8,128)(2,1)S(1)}, u32[]{:S(2)}, u32[]{:S(2)}) %collective-permute-start.16) | collective-permute-done | bytes 262176 | tf_op jit(solution)/shard_map/dispatch_gather/ppermute | solution.py:55
  133.7 2.0 collective-permute-start.18
  135.8 4.7 %fusion = f32[256,1536]{1,0:T(8,128)S(1)} fusion(bf16[256,2048]{1,0:T(8,128)(2,1)S(1)} %constant_dynamic-update-slice_fusion.8, bf16[2,2048,1536]{2,1,0:T(8,128)(2,1)} %param.16), kind=kOutput, calls=%fused_computation | convolution fusion | flops 1610612736 | bytes 8912896 | tf_op jit(solution)/shard_map/local_experts/dot_general | solution.py:87
  140.6 4.7 %fusion.8 = f32[256,1536]{1,0:T(8,128)S(1)} fusion(bf16[256,2048]{1,0:T(8,128)(2,1)S(1)} %constant_dynamic-update-slice_fusion.8, bf16[2,2048,1536]{2,1,0:T(8,128)(2,1)} %param.16), kind=kOutput, calls=%fused_computation.8 | convolution fusion | flops 1610612736 | bytes 8912896 | tf_op jit(solution)/shard_map/local_experts/dot_general | solution.py:87
  146.4 1.0 fusion.221
  147.5 2.1 collective-permute-start.28
  149.7 2.1 collective-permute-start.20
  151.7 4.2 %collective-permute-done.28 = bf16[64,2048]{1,0:T(8,128)(2,1)S(1)} collective-permute-done((bf16[64,2048]{1,0:T(8,128)(2,1)S(1)}, bf16[64,2048]{1,0:T(8,128)(2,1)S(1)}, u32[]{:S(2)}, u32[]{:S(2)}) %collective-permute-start.28) | collective-permute-done | bytes 262176 | tf_op jit(solution)/shard_map/combine_return/ppermute | solution.py:75
  156.4 1.9 collective-permute-start.31
  158.4 1.5 collective-permute-done.20
  160.2 2.0 collective-permute-start.23
  162.4 1.8 fusion.2
  164.1 1.8 fusion.10
  168.2 1.1 collective-permute-start.32
  171.5 1.2 collective-permute-start.24
  173.5 4.0 %collective-permute-done.32 = bf16[64,2048]{1,0:T(8,128)(2,1)S(1)} collective-permute-done((bf16[64,2048]{1,0:T(8,128)(2,1)S(1)}, bf16[64,2048]{1,0:T(8,128)(2,1)S(1)}, u32[]{:S(2)}, u32[]{:S(2)}) %collective-permute-start.32) | collective-permute-done | bytes 262176 | tf_op jit(solution)/shard_map/combine_return/ppermute | solution.py:75
  177.5 1.1 collective-permute-done.33
  178.8 1.9 collective-permute-start.35
  180.8 2.3 %collective-permute-done.24 = bf16[64,2048]{1,0:T(8,128)(2,1)S(1)} collective-permute-done((bf16[64,2048]{1,0:T(8,128)(2,1)S(1)}, bf16[64,2048]{1,0:T(8,128)(2,1)S(1)}, u32[]{:S(2)}, u32[]{:S(2)}) %collective-permute-start.24) | collective-permute-done | bytes 262176 | tf_op jit(solution)/shard_map/dispatch_gather/ppermute | solution.py:55
  183.7 2.0 collective-permute-start.27
  185.8 1.8 fusion.4
  187.6 1.8 fusion.12
  190.4 1.1 fusion.61
  191.7 2.0 collective-permute-start.37
  193.7 1.8 fusion.6
  195.5 1.8 fusion.14
  197.3 3.1 %collective-permute-done.36 = bf16[64,2048]{1,0:T(8,128)(2,1)S(1)} collective-permute-done((bf16[64,2048]{1,0:T(8,128)(2,1)S(1)}, bf16[64,2048]{1,0:T(8,128)(2,1)S(1)}, u32[]{:S(2)}, u32[]{:S(2)}) %collective-permute-start.36) | collective-permute-done | bytes 262176 | tf_op jit(solution)/shard_map/combine_return/ppermute | solution.py:75
  200.6 2.4 %collective-permute-start.39 = (bf16[64,2048]{1,0:T(8,128)(2,1)S(1)}, bf16[64,2048]{1,0:T(8,128)(2,1)S(1)}, u32[]{:S(2)}, u32[]{:S(2)}) collective-permute-start(bf16[64,2048]{1,0:T(8,128)(2,1)S(1)} %get-tuple-element.139), channel_id=1, source_target_pairs={{0,4},{8,0},{16,8},{24,16},{28,24},{20,28},{12,20},{4,12},{1,5},{9... | collective-permute-start | bytes 786440 | tf_op jit(solution)/shard_map/combine_return/ppermute | solution.py:75
  204.0 1.1 fusion.49
  205.1 2.0 collective-permute-done.38
  207.3 2.8 %collective-permute-start.40 = (bf16[64,2048]{1,0:T(8,128)(2,1)S(1)}, bf16[64,2048]{1,0:T(8,128)(2,1)S(1)}, u32[]{:S(2)}, u32[]{:S(2)}) collective-permute-start(bf16[64,2048]{1,0:T(8,128)(2,1)S(1)} %get-tuple-element.142), channel_id=1, source_target_pairs={{0,8},{8,16},{16,24},{24,28},{28,20},{20,12},{12,4},{4,0},{1,9},{9... | collective-permute-start | bytes 786440 | tf_op jit(solution)/shard_map/combine_return/ppermute | solution.py:75
  210.1 3.9 %collective-permute-done.40 = bf16[64,2048]{1,0:T(8,128)(2,1)S(1)} collective-permute-done((bf16[64,2048]{1,0:T(8,128)(2,1)S(1)}, bf16[64,2048]{1,0:T(8,128)(2,1)S(1)}, u32[]{:S(2)}, u32[]{:S(2)}) %collective-permute-start.40) | collective-permute-done | bytes 262176 | tf_op jit(solution)/shard_map/combine_return/ppermute | solution.py:75
  214.0 2.5 %collective-permute-done.41 = bf16[64,2048]{1,0:T(8,128)(2,1)S(1)} collective-permute-done((bf16[64,2048]{1,0:T(8,128)(2,1)S(1)}, bf16[64,2048]{1,0:T(8,128)(2,1)S(1)}, u32[]{:S(2)}, u32[]{:S(2)}) %collective-permute-start.41) | collective-permute-done | bytes 262176 | tf_op jit(solution)/shard_map/combine_return/ppermute | solution.py:75
  216.9 1.2 multiply_convert_fusion
  (119 shorter events, 24.3 us)
Async XLA Ops:
  0.6 43.6 %copy-start = (bf16[512,2048]{1,0:T(8,128)(2,1)S(1)}, bf16[512,2048]{1,0:T(8,128)(2,1)}, u32[]{:S(2)}) copy-start(bf16[512,2048]{1,0:T(8,128)(2,1)} %param.14) | copy-start | bytes 6291460
  2.1 13.8 %all-to-all-start.1 = ((f32[8,128,2]{1,2,0:T(2,128)}), f32[8,128,2]{1,2,0:T(2,128)S(1)}, u32[]{:S(2)}, u32[]{:S(2)}) async-start(f32[8,128,2]{1,2,0:T(2,128)} %bitcast.2), calls=%async_computation.1 | async-start | bytes 16384 | tf_op jit(solution)/shard_map/route_weights/all_to_all | solution.py:118
  9.4 10.1 %copy-start.7 = (s32[8]{0:T(128)S(1)}, s32[8]{0:T(128)}, u32[]{:S(2)}) copy-start(s32[8]{0:T(128)} %constant.224.clone) | copy-start | bytes 100
  9.4 21.9 %copy-start.4 = (s32[8]{0:T(128)S(1)}, s32[8]{0:T(128)}, u32[]{:S(2)}) copy-start(s32[8]{0:T(128)} %constant.225.clone) | copy-start | bytes 100
  15.9 28.3 %all-to-all-start = ((bf16[8,128,512]{2,1,0:T(8,128)(2,1)}), bf16[8,128,512]{2,1,0:T(8,128)(2,1)S(1)}, u32[]{:S(2)}, u32[]{:S(2)}) async-start(bf16[8,128,512]{2,1,0:T(8,128)(2,1)} %bitcast.242), calls=%async_computation | async-start | bytes 2097152 | tf_op jit(solution)/shard_map/out_projection/all_to_all | solution.py:123
  46.5 3.3 %copy-start.2 = (f32[8,128,2048]{2,1,0:T(8,128)}, f32[8,128,2048]{2,1,0:T(8,128)S(1)}, u32[]{:S(2)}) copy-start(f32[8,128,2048]{2,1,0:T(8,128)S(1)} %fusion.124) | copy-start | bytes 25165828
  49.9 6.6 %collective-permute-start = (bf16[64,2048]{1,0:T(8,128)(2,1)S(1)}, bf16[64,2048]{1,0:T(8,128)(2,1)S(1)}, u32[]{:S(2)}, u32[]{:S(2)}) collective-permute-start(bf16[64,2048]{1,0:T(8,128)(2,1)S(1)} %get-tuple-element.75), channel_id=1, source_target_pairs={{0,8},{8,16},{16,24},{24,28},{28,20},{20,12},{12,4},{4,0},{1,9},{9... | collective-permute-start | bytes 786440 | tf_op jit(solution)/shard_map/out_projection/ppermute | solution.py:37
  50.0 6.6 %collective-permute-start.1 = (bf16[64,2048]{1,0:T(8,128)(2,1)S(1)}, bf16[64,2048]{1,0:T(8,128)(2,1)S(1)}, u32[]{:S(2)}, u32[]{:S(2)}) collective-permute-start(bf16[64,2048]{1,0:T(8,128)(2,1)S(1)} %get-tuple-element.76), channel_id=1, source_target_pairs={{0,4},{8,0},{16,8},{24,16},{28,24},{20,28},{12,20},{4,12},{1,5},{9... | collective-permute-start | bytes 786440 | tf_op jit(solution)/shard_map/out_projection/ppermute | solution.py:37
  57.9 6.4 %collective-permute-start.2 = (bf16[64,2048]{1,0:T(8,128)(2,1)S(1)}, bf16[64,2048]{1,0:T(8,128)(2,1)S(1)}, u32[]{:S(2)}, u32[]{:S(2)}) collective-permute-start(bf16[64,2048]{1,0:T(8,128)(2,1)S(1)} %get-tuple-element.79), channel_id=1, source_target_pairs={{0,8},{8,16},{16,24},{24,28},{28,20},{20,12},{12,4},{4,0},{1,9},{9... | collective-permute-start | bytes 786440 | tf_op jit(solution)/shard_map/out_projection/ppermute | solution.py:37
  58.5 7.9 %collective-permute-start.3 = (bf16[64,2048]{1,0:T(8,128)(2,1)S(1)}, bf16[64,2048]{1,0:T(8,128)(2,1)S(1)}, u32[]{:S(2)}, u32[]{:S(2)}) collective-permute-start(bf16[64,2048]{1,0:T(8,128)(2,1)S(1)} %get-tuple-element.80), channel_id=1, source_target_pairs={{0,4},{8,0},{16,8},{24,16},{28,24},{20,28},{12,20},{4,12},{1,5},{9... | collective-permute-start | bytes 786440 | tf_op jit(solution)/shard_map/out_projection/ppermute | solution.py:37
  67.7 6.4 %collective-permute-start.4 = (bf16[64,2048]{1,0:T(8,128)(2,1)S(1)}, bf16[64,2048]{1,0:T(8,128)(2,1)S(1)}, u32[]{:S(2)}, u32[]{:S(2)}) collective-permute-start(bf16[64,2048]{1,0:T(8,128)(2,1)S(1)} %get-tuple-element.83), channel_id=1, source_target_pairs={{0,8},{8,16},{16,24},{24,28},{28,20},{20,12},{12,4},{4,0},{1,9},{9... | collective-permute-start | bytes 786440 | tf_op jit(solution)/shard_map/out_projection/ppermute | solution.py:37
  69.5 6.4 %collective-permute-start.5 = (bf16[64,2048]{1,0:T(8,128)(2,1)S(1)}, bf16[64,2048]{1,0:T(8,128)(2,1)S(1)}, u32[]{:S(2)}, u32[]{:S(2)}) collective-permute-start(bf16[64,2048]{1,0:T(8,128)(2,1)S(1)} %get-tuple-element.84), channel_id=1, source_target_pairs={{0,4},{8,0},{16,8},{24,16},{28,24},{20,28},{12,20},{4,12},{1,5},{9... | collective-permute-start | bytes 786440 | tf_op jit(solution)/shard_map/out_projection/ppermute | solution.py:37
  77.2 6.4 %collective-permute-start.6 = (bf16[64,2048]{1,0:T(8,128)(2,1)S(1)}, bf16[64,2048]{1,0:T(8,128)(2,1)S(1)}, u32[]{:S(2)}, u32[]{:S(2)}) collective-permute-start(bf16[64,2048]{1,0:T(8,128)(2,1)S(1)} %get-tuple-element.87), channel_id=1, source_target_pairs={{0,8},{8,16},{16,24},{24,28},{28,20},{20,12},{12,4},{4,0},{1,9},{9... | collective-permute-start | bytes 786440 | tf_op jit(solution)/shard_map/out_projection/ppermute | solution.py:37
  79.0 6.6 %collective-permute-start.7 = (bf16[64,2048]{1,0:T(8,128)(2,1)S(1)}, bf16[64,2048]{1,0:T(8,128)(2,1)S(1)}, u32[]{:S(2)}, u32[]{:S(2)}) collective-permute-start(bf16[64,2048]{1,0:T(8,128)(2,1)S(1)} %get-tuple-element.88), channel_id=1, source_target_pairs={{0,4},{8,0},{16,8},{24,16},{28,24},{20,28},{12,20},{4,12},{1,5},{9... | collective-permute-start | bytes 786440 | tf_op jit(solution)/shard_map/out_projection/ppermute | solution.py:37
  86.9 7.7 %collective-permute-start.8 = (bf16[64,2048]{1,0:T(8,128)(2,1)S(1)}, bf16[64,2048]{1,0:T(8,128)(2,1)S(1)}, u32[]{:S(2)}, u32[]{:S(2)}) collective-permute-start(bf16[64,2048]{1,0:T(8,128)(2,1)S(1)} %get-tuple-element.91), channel_id=1, source_target_pairs={{0,8},{8,16},{16,24},{24,28},{28,20},{20,12},{12,4},{4,0},{1,9},{9... | collective-permute-start | bytes 786440 | tf_op jit(solution)/shard_map/out_projection/ppermute | solution.py:37
  87.4 7.7 %collective-permute-start.9 = (bf16[64,2048]{1,0:T(8,128)(2,1)S(1)}, bf16[64,2048]{1,0:T(8,128)(2,1)S(1)}, u32[]{:S(2)}, u32[]{:S(2)}) collective-permute-start(bf16[64,2048]{1,0:T(8,128)(2,1)S(1)} %get-tuple-element.92), channel_id=1, source_target_pairs={{0,4},{8,0},{16,8},{24,16},{28,24},{20,28},{12,20},{4,12},{1,5},{9... | collective-permute-start | bytes 786440 | tf_op jit(solution)/shard_map/out_projection/ppermute | solution.py:37
  96.5 8.6 %collective-permute-start.10 = (bf16[64,2048]{1,0:T(8,128)(2,1)S(1)}, bf16[64,2048]{1,0:T(8,128)(2,1)S(1)}, u32[]{:S(2)}, u32[]{:S(2)}) collective-permute-start(bf16[64,2048]{1,0:T(8,128)(2,1)S(1)} %get-tuple-element.95), channel_id=1, source_target_pairs={{0,8},{8,16},{16,24},{24,28},{28,20},{20,12},{12,4},{4,0},{1,9},{9... | collective-permute-start | bytes 786440 | tf_op jit(solution)/shard_map/out_projection/ppermute | solution.py:37
  97.1 8.7 %collective-permute-start.11 = (bf16[64,2048]{1,0:T(8,128)(2,1)S(1)}, bf16[64,2048]{1,0:T(8,128)(2,1)S(1)}, u32[]{:S(2)}, u32[]{:S(2)}) collective-permute-start(bf16[64,2048]{1,0:T(8,128)(2,1)S(1)} %get-tuple-element.96), channel_id=1, source_target_pairs={{0,4},{8,0},{16,8},{24,16},{28,24},{20,28},{12,20},{4,12},{1,5},{9... | collective-permute-start | bytes 786440 | tf_op jit(solution)/shard_map/out_projection/ppermute | solution.py:37
  104.5 13.0 %copy-start.3 = (bf16[128,2048]{1,0:T(8,128)(2,1)S(1)}, bf16[128,2048]{1,0:T(8,128)(2,1)}, u32[]{:S(2)}) copy-start(bf16[128,2048]{1,0:T(8,128)(2,1)} %param.12) | copy-start | bytes 1572868
  107.1 8.4 %collective-permute-start.12 = (bf16[64,2048]{1,0:T(8,128)(2,1)S(1)}, bf16[64,2048]{1,0:T(8,128)(2,1)S(1)}, u32[]{:S(2)}, u32[]{:S(2)}) collective-permute-start(bf16[64,2048]{1,0:T(8,128)(2,1)S(1)} %get-tuple-element.99), channel_id=1, source_target_pairs={{0,8},{8,16},{16,24},{24,28},{28,20},{20,12},{12,4},{4,0},{1,9},{9... | collective-permute-start | bytes 786440 | tf_op jit(solution)/shard_map/out_projection/ppermute | solution.py:37
  108.8 7.4 %collective-permute-start.13 = (bf16[64,2048]{1,0:T(8,128)(2,1)S(1)}, bf16[64,2048]{1,0:T(8,128)(2,1)S(1)}, u32[]{:S(2)}, u32[]{:S(2)}) collective-permute-start(bf16[64,2048]{1,0:T(8,128)(2,1)S(1)} %get-tuple-element.100), channel_id=1, source_target_pairs={{0,4},{8,0},{16,8},{24,16},{28,24},{20,28},{12,20},{4,12},{1,5},{9... | collective-permute-start | bytes 786440 | tf_op jit(solution)/shard_map/out_projection/ppermute | solution.py:37
  109.2 8.6 %copy-start.5 = (f32[2048]{0:T(1024)S(1)}, f32[2048]{0:T(1024)}, u32[]{:S(2)}) copy-start(f32[2048]{0:T(1024)} %param.15) | copy-start | bytes 24580
  118.0 7.9 %collective-permute-start.15 = (bf16[64,2048]{1,0:T(8,128)(2,1)S(1)}, bf16[64,2048]{1,0:T(8,128)(2,1)S(1)}, u32[]{:S(2)}, u32[]{:S(2)}) collective-permute-start(bf16[64,2048]{1,0:T(8,128)(2,1)S(1)} %get-tuple-element.182), channel_id=1, source_target_pairs={{0,4},{8,0},{16,8},{24,16},{28,24},{20,28},{12,20},{4,12},{1,5},{9... | collective-permute-start | bytes 786440 | tf_op jit(solution)/shard_map/dispatch_gather/ppermute | solution.py:55
  119.6 6.4 %collective-permute-start.14 = (bf16[64,2048]{1,0:T(8,128)(2,1)S(1)}, bf16[64,2048]{1,0:T(8,128)(2,1)S(1)}, u32[]{:S(2)}, u32[]{:S(2)}) collective-permute-start(bf16[64,2048]{1,0:T(8,128)(2,1)S(1)} %get-tuple-element.183), channel_id=1, source_target_pairs={{0,8},{8,16},{16,24},{24,28},{28,20},{20,12},{12,4},{4,0},{1,9},{9... | collective-permute-start | bytes 786440 | tf_op jit(solution)/shard_map/dispatch_gather/ppermute | solution.py:55
  126.0 7.3 %collective-permute-start.16 = (bf16[64,2048]{1,0:T(8,128)(2,1)S(1)}, bf16[64,2048]{1,0:T(8,128)(2,1)S(1)}, u32[]{:S(2)}, u32[]{:S(2)}) collective-permute-start(bf16[64,2048]{1,0:T(8,128)(2,1)S(1)} %collective-permute-done.14), channel_id=1, source_target_pairs={{0,8},{8,16},{16,24},{24,28},{28,20},{20,12},{12,4},{4,0},{1,9},{9... | collective-permute-start | bytes 786440 | tf_op jit(solution)/shard_map/dispatch_gather/ppermute | solution.py:55
  126.9 6.8 %collective-permute-start.17 = (bf16[64,2048]{1,0:T(8,128)(2,1)S(1)}, bf16[64,2048]{1,0:T(8,128)(2,1)S(1)}, u32[]{:S(2)}, u32[]{:S(2)}) collective-permute-start(bf16[64,2048]{1,0:T(8,128)(2,1)S(1)} %collective-permute-done.15), channel_id=1, source_target_pairs={{0,4},{8,0},{16,8},{24,16},{28,24},{20,28},{12,20},{4,12},{1,5},{9... | collective-permute-start | bytes 786440 | tf_op jit(solution)/shard_map/dispatch_gather/ppermute | solution.py:55
  133.7 15.9 %collective-permute-start.18 = (bf16[64,2048]{1,0:T(8,128)(2,1)S(1)}, bf16[64,2048]{1,0:T(8,128)(2,1)S(1)}, u32[]{:S(2)}, u32[]{:S(2)}) collective-permute-start(bf16[64,2048]{1,0:T(8,128)(2,1)S(1)} %collective-permute-done.16), channel_id=1, source_target_pairs={{0,8},{8,16},{16,24},{24,28},{28,20},{20,12},{12,4},{4,0},{1,9},{9... | collective-permute-start | bytes 786440 | tf_op jit(solution)/shard_map/dispatch_gather/ppermute | solution.py:55
  135.7 13.9 %collective-permute-start.19 = (bf16[64,2048]{1,0:T(8,128)(2,1)S(1)}, bf16[64,2048]{1,0:T(8,128)(2,1)S(1)}, u32[]{:S(2)}, u32[]{:S(2)}) collective-permute-start(bf16[64,2048]{1,0:T(8,128)(2,1)S(1)} %collective-permute-done.17), channel_id=1, source_target_pairs={{0,4},{8,0},{16,8},{24,16},{28,24},{20,28},{12,20},{4,12},{1,5},{9... | collective-permute-start | bytes 786440 | tf_op jit(solution)/shard_map/dispatch_gather/ppermute | solution.py:55
  135.8 9.5 %slice-start.3 = ((s8[6291456]{0:T(1024)(128)(4,1)}), s8[4194304]{0:T(1024)(128)(4,1)S(1)}, s32[]{:S(2)}) async-start(s8[6291456]{0:T(1024)(128)(4,1)} %bitcast.273), calls=%async_computation.5 | async-start | bytes 8388608
  140.5 4.8 %slice-start.4 = ((s8[6291456]{0:T(1024)(128)(4,1)}), s8[2097152]{0:T(1024)(128)(4,1)S(1)}, s32[]{:S(2)}) async-start(s8[6291456]{0:T(1024)(128)(4,1)} %bitcast.273), calls=%async_computation.6 | async-start | bytes 4194304
  145.3 17.0 %slice-start = ((s8[12582912]{0:T(1024)(128)(4,1)}), s8[4194304]{0:T(1024)(128)(4,1)S(1)}, s32[]{:S(2)}) async-start(s8[12582912]{0:T(1024)(128)(4,1)} %bitcast.271), calls=%async_computation.2 | async-start | bytes 8388608
  145.3 17.0 %slice-start.1 = ((s8[12582912]{0:T(1024)(128)(4,1)}), s8[4194304]{0:T(1024)(128)(4,1)S(1)}, s32[]{:S(2)}) async-start(s8[12582912]{0:T(1024)(128)(4,1)} %bitcast.271), calls=%async_computation.3 | async-start | bytes 8388608
  146.4 16.0 %slice-start.2 = ((s8[12582912]{0:T(1024)(128)(4,1)}), s8[4194304]{0:T(1024)(128)(4,1)S(1)}, s32[]{:S(2)}) async-start(s8[12582912]{0:T(1024)(128)(4,1)} %bitcast.271), calls=%async_computation.4 | async-start | bytes 8388608
  147.5 8.5 %collective-permute-start.28 = (bf16[64,2048]{1,0:T(8,128)(2,1)S(1)}, bf16[64,2048]{1,0:T(8,128)(2,1)S(1)}, u32[]{:S(2)}, u32[]{:S(2)}) collective-permute-start(bf16[64,2048]{1,0:T(8,128)(2,1)S(1)} %get-tuple-element.118), channel_id=1, source_target_pairs={{0,8},{8,16},{16,24},{24,28},{28,20},{20,12},{12,4},{4,0},{1,9},{9... | collective-permute-start | bytes 786440 | tf_op jit(solution)/shard_map/combine_return/ppermute | solution.py:75
  149.6 6.6 %collective-permute-start.29 = (bf16[64,2048]{1,0:T(8,128)(2,1)S(1)}, bf16[64,2048]{1,0:T(8,128)(2,1)S(1)}, u32[]{:S(2)}, u32[]{:S(2)}) collective-permute-start(bf16[64,2048]{1,0:T(8,128)(2,1)S(1)} %get-tuple-element.119), channel_id=1, source_target_pairs={{0,4},{8,0},{16,8},{24,16},{28,24},{20,28},{12,20},{4,12},{1,5},{9... | collective-permute-start | bytes 786440 | tf_op jit(solution)/shard_map/combine_return/ppermute | solution.py:75
  149.7 10.2 %collective-permute-start.20 = (bf16[64,2048]{1,0:T(8,128)(2,1)S(1)}, bf16[64,2048]{1,0:T(8,128)(2,1)S(1)}, u32[]{:S(2)}, u32[]{:S(2)}) collective-permute-start(bf16[64,2048]{1,0:T(8,128)(2,1)S(1)} %collective-permute-done.18), channel_id=1, source_target_pairs={{0,8},{8,16},{16,24},{24,28},{28,20},{20,12},{12,4},{4,0},{1,9},{9... | collective-permute-start | bytes 786440 | tf_op jit(solution)/shard_map/dispatch_gather/ppermute | solution.py:55
  151.7 8.5 %collective-permute-start.21 = (bf16[64,2048]{1,0:T(8,128)(2,1)S(1)}, bf16[64,2048]{1,0:T(8,128)(2,1)S(1)}, u32[]{:S(2)}, u32[]{:S(2)}) collective-permute-start(bf16[64,2048]{1,0:T(8,128)(2,1)S(1)} %collective-permute-done.19), channel_id=1, source_target_pairs={{0,4},{8,0},{16,8},{24,16},{28,24},{20,28},{12,20},{4,12},{1,5},{9... | collective-permute-start | bytes 786440 | tf_op jit(solution)/shard_map/dispatch_gather/ppermute | solution.py:55
  156.3 9.6 %collective-permute-start.30 = (bf16[64,2048]{1,0:T(8,128)(2,1)S(1)}, bf16[64,2048]{1,0:T(8,128)(2,1)S(1)}, u32[]{:S(2)}, u32[]{:S(2)}) collective-permute-start(bf16[64,2048]{1,0:T(8,128)(2,1)S(1)} %get-tuple-element.122), channel_id=1, source_target_pairs={{0,8},{8,16},{16,24},{24,28},{28,20},{20,12},{12,4},{4,0},{1,9},{9... | collective-permute-start | bytes 786440 | tf_op jit(solution)/shard_map/combine_return/ppermute | solution.py:75
  156.4 9.5 %collective-permute-start.31 = (bf16[64,2048]{1,0:T(8,128)(2,1)S(1)}, bf16[64,2048]{1,0:T(8,128)(2,1)S(1)}, u32[]{:S(2)}, u32[]{:S(2)}) collective-permute-start(bf16[64,2048]{1,0:T(8,128)(2,1)S(1)} %get-tuple-element.123), channel_id=1, source_target_pairs={{0,4},{8,0},{16,8},{24,16},{28,24},{20,28},{12,20},{4,12},{1,5},{9... | collective-permute-start | bytes 786440 | tf_op jit(solution)/shard_map/combine_return/ppermute | solution.py:75
  160.2 11.0 %collective-permute-start.22 = (bf16[64,2048]{1,0:T(8,128)(2,1)S(1)}, bf16[64,2048]{1,0:T(8,128)(2,1)S(1)}, u32[]{:S(2)}, u32[]{:S(2)}) collective-permute-start(bf16[64,2048]{1,0:T(8,128)(2,1)S(1)} %collective-permute-done.20), channel_id=1, source_target_pairs={{0,8},{8,16},{16,24},{24,28},{28,20},{20,12},{12,4},{4,0},{1,9},{9... | collective-permute-start | bytes 786440 | tf_op jit(solution)/shard_map/dispatch_gather/ppermute | solution.py:55
  160.2 11.2 %collective-permute-start.23 = (bf16[64,2048]{1,0:T(8,128)(2,1)S(1)}, bf16[64,2048]{1,0:T(8,128)(2,1)S(1)}, u32[]{:S(2)}, u32[]{:S(2)}) collective-permute-start(bf16[64,2048]{1,0:T(8,128)(2,1)S(1)} %collective-permute-done.21), channel_id=1, source_target_pairs={{0,4},{8,0},{16,8},{24,16},{28,24},{20,28},{12,20},{4,12},{1,5},{9... | collective-permute-start | bytes 786440 | tf_op jit(solution)/shard_map/dispatch_gather/ppermute | solution.py:55
  168.2 9.3 %collective-permute-start.32 = (bf16[64,2048]{1,0:T(8,128)(2,1)S(1)}, bf16[64,2048]{1,0:T(8,128)(2,1)S(1)}, u32[]{:S(2)}, u32[]{:S(2)}) collective-permute-start(bf16[64,2048]{1,0:T(8,128)(2,1)S(1)} %get-tuple-element.126), channel_id=1, source_target_pairs={{0,8},{8,16},{16,24},{24,28},{28,20},{20,12},{12,4},{4,0},{1,9},{9... | collective-permute-start | bytes 786440 | tf_op jit(solution)/shard_map/combine_return/ppermute | solution.py:75
  169.3 9.2 %collective-permute-start.33 = (bf16[64,2048]{1,0:T(8,128)(2,1)S(1)}, bf16[64,2048]{1,0:T(8,128)(2,1)S(1)}, u32[]{:S(2)}, u32[]{:S(2)}) collective-permute-start(bf16[64,2048]{1,0:T(8,128)(2,1)S(1)} %get-tuple-element.127), channel_id=1, source_target_pairs={{0,4},{8,0},{16,8},{24,16},{28,24},{20,28},{12,20},{4,12},{1,5},{9... | collective-permute-start | bytes 786440 | tf_op jit(solution)/shard_map/combine_return/ppermute | solution.py:75
  171.5 11.6 %collective-permute-start.24 = (bf16[64,2048]{1,0:T(8,128)(2,1)S(1)}, bf16[64,2048]{1,0:T(8,128)(2,1)S(1)}, u32[]{:S(2)}, u32[]{:S(2)}) collective-permute-start(bf16[64,2048]{1,0:T(8,128)(2,1)S(1)} %collective-permute-done.22), channel_id=1, source_target_pairs={{0,8},{8,16},{16,24},{24,28},{28,20},{20,12},{12,4},{4,0},{1,9},{9... | collective-permute-start | bytes 786440 | tf_op jit(solution)/shard_map/dispatch_gather/ppermute | solution.py:55
  172.6 11.1 %collective-permute-start.25 = (bf16[64,2048]{1,0:T(8,128)(2,1)S(1)}, bf16[64,2048]{1,0:T(8,128)(2,1)S(1)}, u32[]{:S(2)}, u32[]{:S(2)}) collective-permute-start(bf16[64,2048]{1,0:T(8,128)(2,1)S(1)} %collective-permute-done.23), channel_id=1, source_target_pairs={{0,4},{8,0},{16,8},{24,16},{28,24},{20,28},{12,20},{4,12},{1,5},{9... | collective-permute-start | bytes 786440 | tf_op jit(solution)/shard_map/dispatch_gather/ppermute | solution.py:55
  178.7 10.7 %collective-permute-start.34 = (bf16[64,2048]{1,0:T(8,128)(2,1)S(1)}, bf16[64,2048]{1,0:T(8,128)(2,1)S(1)}, u32[]{:S(2)}, u32[]{:S(2)}) collective-permute-start(bf16[64,2048]{1,0:T(8,128)(2,1)S(1)} %get-tuple-element.130), channel_id=1, source_target_pairs={{0,8},{8,16},{16,24},{24,28},{28,20},{20,12},{12,4},{4,0},{1,9},{9... | collective-permute-start | bytes 786440 | tf_op jit(solution)/shard_map/combine_return/ppermute | solution.py:75
  178.8 10.5 %collective-permute-start.35 = (bf16[64,2048]{1,0:T(8,128)(2,1)S(1)}, bf16[64,2048]{1,0:T(8,128)(2,1)S(1)}, u32[]{:S(2)}, u32[]{:S(2)}) collective-permute-start(bf16[64,2048]{1,0:T(8,128)(2,1)S(1)} %get-tuple-element.131), channel_id=1, source_target_pairs={{0,4},{8,0},{16,8},{24,16},{28,24},{20,28},{12,20},{4,12},{1,5},{9... | collective-permute-start | bytes 786440 | tf_op jit(solution)/shard_map/combine_return/ppermute | solution.py:75
  183.7 10.0 %collective-permute-start.26 = (bf16[64,2048]{1,0:T(8,128)(2,1)S(1)}, bf16[64,2048]{1,0:T(8,128)(2,1)S(1)}, u32[]{:S(2)}, u32[]{:S(2)}) collective-permute-start(bf16[64,2048]{1,0:T(8,128)(2,1)S(1)} %collective-permute-done.24), channel_id=1, source_target_pairs={{0,8},{8,16},{16,24},{24,28},{28,20},{20,12},{12,4},{4,0},{1,9},{9... | collective-permute-start | bytes 786440 | tf_op jit(solution)/shard_map/dispatch_gather/ppermute | solution.py:55
  183.7 10.0 %collective-permute-start.27 = (bf16[64,2048]{1,0:T(8,128)(2,1)S(1)}, bf16[64,2048]{1,0:T(8,128)(2,1)S(1)}, u32[]{:S(2)}, u32[]{:S(2)}) collective-permute-start(bf16[64,2048]{1,0:T(8,128)(2,1)S(1)} %collective-permute-done.25), channel_id=1, source_target_pairs={{0,4},{8,0},{16,8},{24,16},{28,24},{20,28},{12,20},{4,12},{1,5},{9... | collective-permute-start | bytes 786440 | tf_op jit(solution)/shard_map/dispatch_gather/ppermute | solution.py:55
  191.6 8.7 %collective-permute-start.36 = (bf16[64,2048]{1,0:T(8,128)(2,1)S(1)}, bf16[64,2048]{1,0:T(8,128)(2,1)S(1)}, u32[]{:S(2)}, u32[]{:S(2)}) collective-permute-start(bf16[64,2048]{1,0:T(8,128)(2,1)S(1)} %get-tuple-element.134), channel_id=1, source_target_pairs={{0,8},{8,16},{16,24},{24,28},{28,20},{20,12},{12,4},{4,0},{1,9},{9... | collective-permute-start | bytes 786440 | tf_op jit(solution)/shard_map/combine_return/ppermute | solution.py:75
  191.7 8.7 %collective-permute-start.37 = (bf16[64,2048]{1,0:T(8,128)(2,1)S(1)}, bf16[64,2048]{1,0:T(8,128)(2,1)S(1)}, u32[]{:S(2)}, u32[]{:S(2)}) collective-permute-start(bf16[64,2048]{1,0:T(8,128)(2,1)S(1)} %get-tuple-element.135), channel_id=1, source_target_pairs={{0,4},{8,0},{16,8},{24,16},{28,24},{20,28},{12,20},{4,12},{1,5},{9... | collective-permute-start | bytes 786440 | tf_op jit(solution)/shard_map/combine_return/ppermute | solution.py:75
  200.5 6.6 %collective-permute-start.38 = (bf16[64,2048]{1,0:T(8,128)(2,1)S(1)}, bf16[64,2048]{1,0:T(8,128)(2,1)S(1)}, u32[]{:S(2)}, u32[]{:S(2)}) collective-permute-start(bf16[64,2048]{1,0:T(8,128)(2,1)S(1)} %get-tuple-element.138), channel_id=1, source_target_pairs={{0,8},{8,16},{16,24},{24,28},{28,20},{20,12},{12,4},{4,0},{1,9},{9... | collective-permute-start | bytes 786440 | tf_op jit(solution)/shard_map/combine_return/ppermute | solution.py:75
  200.6 6.6 %collective-permute-start.39 = (bf16[64,2048]{1,0:T(8,128)(2,1)S(1)}, bf16[64,2048]{1,0:T(8,128)(2,1)S(1)}, u32[]{:S(2)}, u32[]{:S(2)}) collective-permute-start(bf16[64,2048]{1,0:T(8,128)(2,1)S(1)} %get-tuple-element.139), channel_id=1, source_target_pairs={{0,4},{8,0},{16,8},{24,16},{28,24},{20,28},{12,20},{4,12},{1,5},{9... | collective-permute-start | bytes 786440 | tf_op jit(solution)/shard_map/combine_return/ppermute | solution.py:75
  207.3 9.6 %copy-start.6 = (f32[2048]{0:T(1024)S(1)}, f32[2048]{0:T(1024)}, u32[]{:S(2)}) copy-start(f32[2048]{0:T(1024)} %param.20) | copy-start | bytes 24580
  207.3 6.7 %collective-permute-start.40 = (bf16[64,2048]{1,0:T(8,128)(2,1)S(1)}, bf16[64,2048]{1,0:T(8,128)(2,1)S(1)}, u32[]{:S(2)}, u32[]{:S(2)}) collective-permute-start(bf16[64,2048]{1,0:T(8,128)(2,1)S(1)} %get-tuple-element.142), channel_id=1, source_target_pairs={{0,8},{8,16},{16,24},{24,28},{28,20},{20,12},{12,4},{4,0},{1,9},{9... | collective-permute-start | bytes 786440 | tf_op jit(solution)/shard_map/combine_return/ppermute | solution.py:75
  210.1 6.4 %collective-permute-start.41 = (bf16[64,2048]{1,0:T(8,128)(2,1)S(1)}, bf16[64,2048]{1,0:T(8,128)(2,1)S(1)}, u32[]{:S(2)}, u32[]{:S(2)}) collective-permute-start(bf16[64,2048]{1,0:T(8,128)(2,1)S(1)} %get-tuple-element.143), channel_id=1, source_target_pairs={{0,4},{8,0},{16,8},{24,16},{28,24},{20,28},{12,20},{4,12},{1,5},{9... | collective-permute-start | bytes 786440 | tf_op jit(solution)/shard_map/combine_return/ppermute | solution.py:75
  216.7 2.0 copy-start.1

commit v10 on v9

--- a/solution.py
+++ b/solution.py
@@ -96,6 +96,19 @@
     return total
 
 
+def split_exact(values):
+    first = lax.reduce_precision(values, exponent_bits=8, mantissa_bits=7)
+    rest = values - first
+    second = lax.reduce_precision(rest, exponent_bits=8, mantissa_bits=7)
+    third = rest - second
+    return jnp.concatenate([first, second, third], axis=-1).astype(jnp.bfloat16)
+
+
+def join_exact(parts, count):
+    parts = parts.astype(jnp.float32)
+    return (parts[..., :count] + parts[..., count : 2 * count]) + parts[..., 2 * count : 3 * count]
+
+
 def body(
     residual, attn_out, out_weight, post_gain, gate_up, down, route_ids, route_weight, final_gain
 ):
@@ -110,18 +123,18 @@
     pos = jnp.array([ring.index(p) for p in range(ep_size)], dtype=jnp.int32)[me]
 
     with jax.named_scope("route_weights"):
-        expert_ids = jnp.arange(local_experts * ep_size, dtype=jnp.int32)
+        experts = local_experts * ep_size
+        expert_ids = jnp.arange(experts, dtype=jnp.int32)
         dense_weight = jnp.sum(
             jnp.where(route_ids[:, :, None] == expert_ids, route_weight[:, :, None], 0.0), axis=1
         )
-        dense_weight = dense_weight.reshape(row_count, ep_size, local_experts).transpose(1, 0, 2)
-        row_weights = lax.all_to_all(dense_weight, "ep", split_axis=0, concat_axis=0, tiled=True)
-        row_weights = row_weights.reshape(group_rows, local_experts)
+        own_weight = lax.dynamic_index_in_dim(
+            dense_weight.reshape(row_count, ep_size, local_experts), me, 1, keepdims=False
+        )
 
     with jax.named_scope("out_projection"):
         columns = attn_out.reshape(row_count, ep_size, slice_width).transpose(1, 0, 2)
         columns = lax.all_to_all(columns, "ep", split_axis=0, concat_axis=0, tiled=True)
-        columns, row_weights = lax.optimization_barrier((columns, row_weights))
         partial = jnp.dot(
             columns.reshape(group_rows, slice_width), out_weight, preferred_element_type=jnp.float32
         )
@@ -130,18 +143,20 @@
 
     normed = rms_scale(middle.astype(jnp.float32), post_gain).astype(jnp.bfloat16)
     with jax.named_scope("dispatch_gather"):
-        arrived = ring_all_gather(normed, ring, pos)
-
-    ring_index = jnp.array(ring, dtype=jnp.int32)
-    weight_blocks = row_weights.reshape(ep_size, row_count, local_experts)
+        pad = (-3 * experts) % 128
+        payload = jnp.concatenate(
+            [normed, split_exact(dense_weight), jnp.zeros((row_count, pad), jnp.bfloat16)], axis=1
+        )
+        arrived = ring_all_gather(payload, ring, pos)
+
+    def unpack(piece):
+        weights = join_exact(piece[:, model_width : model_width + 3 * experts], experts)
+        weights = lax.dynamic_index_in_dim(
+            weights.reshape(-1, ep_size, local_experts), me, 1, keepdims=False
+        )
+        return piece[:, :model_width], weights
+
     half = row_count // 2
-
-    def step_weights(step):
-        owner_fwd = ring_index[(pos - 1 - step) % ep_size]
-        owner_bwd = ring_index[(pos + 1 + step) % ep_size]
-        w_fwd = lax.dynamic_index_in_dim(weight_blocks, owner_fwd, 0, keepdims=False)[:half]
-        w_bwd = lax.dynamic_index_in_dim(weight_blocks, owner_bwd, 0, keepdims=False)[half:]
-        return w_fwd, w_bwd
 
     with jax.named_scope("local_experts"):
         steps_all = list(range(ep_size - 1))
@@ -152,11 +167,13 @@
             rows_in = []
             weights_in = []
             for step in steps:
-                rows_in += list(arrived[step])
-                weights_in += list(step_weights(step))
+                for piece in arrived[step]:
+                    piece_rows, piece_weights = unpack(piece)
+                    rows_in.append(piece_rows)
+                    weights_in.append(piece_weights)
             if c == len(chunks) - 1:
                 rows_in.append(normed)
-                weights_in.append(lax.dynamic_index_in_dim(weight_blocks, me, 0, keepdims=False))
+                weights_in.append(own_weight)
             mixed = expert_mix(
                 jnp.concatenate(rows_in, axis=0), jnp.concatenate(weights_in, axis=0), gate_up, down
             )

time: 220 us -> 258 us (1.17)
  matrix products: 30.8 us -> 69.4 us
  starting transfers between devices: 56.3 us -> 50.8 us
    dot_general x8, matrix products: 20.1 us -> 40.2 us  [expert_mix(): projected_up = jnp.dot(rows, gate_up[e], preferred_element_type=jnp.float32)]
    dot_general x8, matrix products: 8.31 us -> 26.8 us  [expert_mix(): jnp.dot(activated, down[e], preferred_element_type=jnp.float32)]
    all_to_all x1 -> x0, starting transfers between devices: 7.28 us -> none  [body(): lax.all_to_all(dense_weight, 'ep', split_axis=0, concat_axis=0, tiled=True)]
    all_to_all x1 -> x0, waiting for transfers between devices: 4.16 us -> none  [body(): lax.all_to_all(dense_weight, 'ep', split_axis=0, concat_axis=0, tiled=True)]
    ppermute x7, waiting for transfers between devices: 9.08 us -> 13 us  [ring_all_gather(): lax.ppermute(got_fwd, 'ep', forward)]
    all_to_all x1, starting transfers between devices: 3.56 us -> 7.28 us  [body(): lax.all_to_all(columns, 'ep', split_axis=0, concat_axis=0, tiled=True)]
    ppermute x7, waiting for transfers between devices: 7.35 us -> 4.01 us  [ring_all_gather(): lax.ppermute(got_bwd, 'ep', backward)]
    unnamed x36 -> x35, local copies, waits for them, and re-layouts: 4.14 us -> 5.7 us
  transfers between devices with their start and end apart: 44 -> 43, of which waited for: 34 -> 37; matrix products, arithmetic and copies ran while one was open for 15% -> 7% of each run, Pallas kernels for 0% -> 0%
where the time goes in v10:
time: 258 us; the launch traced here: 256 us
  matrix products  69.4 us (27%)
  waiting for transfers between devices  68.9 us (27%)
  starting transfers between devices  50.8 us (20%)
  between operations  41 us (16%)
  other arithmetic  15.9 us (6%)
  local copies, waits for them, and re-layouts  10.3 us (4%)
    dot_general x8, matrix products, expert_mix(): projected_up = jnp.dot(rows, gate_up[e], preferred_element_type=jnp.float32)  40.2 us
    dot_general x8, matrix products, expert_mix(): jnp.dot(activated, down[e], preferred_element_type=jnp.float32)  26.8 us
    ppermute x7, waiting for transfers between devices, ring_reduce_scatter_steps(): lax.ppermute(send_fwd, 'ep', forward)  16 us
    ppermute x7, waiting for transfers between devices, ring_all_gather(): lax.ppermute(got_fwd, 'ep', forward)  13 us
    ppermute x7, waiting for transfers between devices, ring_reduce_scatter(): lax.ppermute(send_fwd, 'ep', forward)  12.9 us
    all_to_all x1, waiting for transfers between devices, body(): lax.all_to_all(columns, 'ep', split_axis=0, concat_axis=0, tiled=True)  9.17 us
    convert_element_type x6, other arithmetic, ring_reduce_scatter(): send_bwd.astype(jnp.bfloat16)  7.8 us
    ppermute x7, starting transfers between devices, ring_all_gather(): lax.ppermute(got_bwd, 'ep', backward)  7.71 us
  transfers between devices with their start and end apart: 43, of which 37 were waited for; matrix products, arithmetic and copies ran while one was open for 7% of the time, Pallas kernels for 0%

profile of v10, /device:TPU:0, one launch (start us, length us, event | category | flops | bytes accessed | tf_op | source)
XLA Modules:
  0.0 256.4 jit_solution(10735485374677465289)
XLA Ops:
  0.6 1.8 copy.68
  2.4 1.3 copy.69
  3.8 7.3 %all-to-all-start = ((bf16[8,128,512]{2,1,0:T(8,128)(2,1)}), bf16[8,128,512]{2,1,0:T(8,128)(2,1)S(1)}, u32[]{:S(2)}, u32[]{:S(2)}) async-start(bf16[8,128,512]{2,1,0:T(8,128)(2,1)} %bitcast.1), calls=%async_computation | async-start | bytes 2097152 | tf_op jit(solution)/shard_map/out_projection/all_to_all | solution.py:137
  27.6 9.2 %all-to-all-done = bf16[8,128,512]{2,1,0:T(8,128)(2,1)S(1)} async-done(((bf16[8,128,512]{2,1,0:T(8,128)(2,1)}), bf16[8,128,512]{2,1,0:T(8,128)(2,1)S(1)}, u32[]{:S(2)}, u32[]{:S(2)}) %all-to-all-start) | async-done | bytes 1048608 | tf_op jit(solution)/shard_map/out_projection/all_to_all | solution.py:137
  36.8 2.3 fusion.124
  39.2 3.4 %copy-done.2 = f32[8,128,2048]{2,1,0:T(8,128)} copy-done((f32[8,128,2048]{2,1,0:T(8,128)}, f32[8,128,2048]{2,1,0:T(8,128)S(1)}, u32[]{:S(2)}) %copy-start.2) | copy-done | bytes 8388632
  42.7 2.0 collective-permute-start.1
  50.9 1.6 collective-permute-start.2
  57.4 2.2 collective-permute-done.3
  60.9 1.5 collective-permute-start.4
  67.3 1.4 collective-permute-done.5
  70.0 1.8 collective-permute-start.6
  76.5 1.9 collective-permute-done.7
  80.5 1.3 collective-permute-start.9
  85.1 2.3 collective-permute-done.8
  88.4 1.3 fusion.162
  90.3 1.5 collective-permute-start.11
  95.5 3.4 %collective-permute-done.10 = bf16[64,2048]{1,0:T(8,128)(2,1)S(1)} collective-permute-done((bf16[64,2048]{1,0:T(8,128)(2,1)S(1)}, bf16[64,2048]{1,0:T(8,128)(2,1)S(1)}, u32[]{:S(2)}, u32[]{:S(2)}) %collective-permute-start.10) | collective-permute-done | bytes 262176 | tf_op jit(solution)/shard_map/out_projection/ppermute | solution.py:37
  100.6 1.5 collective-permute-start.12
  105.2 4.6 %collective-permute-done.12 = bf16[64,2048]{1,0:T(8,128)(2,1)S(1)} collective-permute-done((bf16[64,2048]{1,0:T(8,128)(2,1)S(1)}, bf16[64,2048]{1,0:T(8,128)(2,1)S(1)}, u32[]{:S(2)}, u32[]{:S(2)}) %collective-permute-start.12) | collective-permute-done | bytes 262176 | tf_op jit(solution)/shard_map/out_projection/ppermute | solution.py:37
  113.2 1.4 collective-permute-start.15
  114.6 4.5 %collective-permute-done.14 = bf16[64,2176]{1,0:T(8,128)(2,1)S(1)} collective-permute-done((bf16[64,2176]{1,0:T(8,128)(2,1)S(1)}, bf16[64,2176]{1,0:T(8,128)(2,1)S(1)}, u32[]{:S(2)}, u32[]{:S(2)}) %collective-permute-start.14) | collective-permute-done | bytes 278560 | tf_op jit(solution)/shard_map/dispatch_gather/ppermute | solution.py:55
  120.2 1.6 collective-permute-start.17
  122.2 4.1 %collective-permute-done.16 = bf16[64,2176]{1,0:T(8,128)(2,1)S(1)} collective-permute-done((bf16[64,2176]{1,0:T(8,128)(2,1)S(1)}, bf16[64,2176]{1,0:T(8,128)(2,1)S(1)}, u32[]{:S(2)}, u32[]{:S(2)}) %collective-permute-start.16) | collective-permute-done | bytes 278560 | tf_op jit(solution)/shard_map/dispatch_gather/ppermute | solution.py:55
  126.9 5.7 %fusion.8 = f32[256,1536]{1,0:T(8,128)} fusion(bf16[2,2048,1536]{2,1,0:T(8,128)(2,1)} %param.15, bf16[64,2048]{1,0:T(8,128)(2,1)S(1)} %slice.589, bf16[64,2048]{1,0:T(8,128)(2,1)S(1)} %slice.588, bf16[64,2048]{1,0:T(8,128)(2,1)S(1)} %slice.587, bf16[64,2048]{1,0:T(8,128)(2,1)S(1)} %slice.586), kind=kOutput, calls=%fused_computation.8 | convolution fusion | flops 1614807040 | bytes 8912896 | tf_op jit(solution)/shard_map/local_experts/dot_general | solution.py:87
  132.6 5.7 %fusion = f32[256,1536]{1,0:T(8,128)} fusion(bf16[2,2048,1536]{2,1,0:T(8,128)(2,1)} %param.15, bf16[64,2048]{1,0:T(8,128)(2,1)S(1)} %slice.589, bf16[64,2048]{1,0:T(8,128)(2,1)S(1)} %slice.588, bf16[64,2048]{1,0:T(8,128)(2,1)S(1)} %slice.587, bf16[64,2048]{1,0:T(8,128)(2,1)S(1)} %slice.586), kind=kOutput, calls=%fused_computation | convolution fusion | flops 1614807040 | bytes 8912896 | tf_op jit(solution)/shard_map/local_experts/dot_general | solution.py:87
  138.7 3.5 %fusion.121 = f32[256,2048]{1,0:T(8,128)S(1)} fusion(bf16[2,768,2048]{2,1,0:T(8,128)(2,1)} %param.16, f32[256]{0:T(256)S(1)} %bitcast.273, f32[256,1536]{1,0:T(8,128)} %fusion), kind=kOutput, calls=%fused_computation.67 | convolution fusion | flops 808058880 | bytes 6816768 | tf_op jit(solution)/shard_map/local_experts/dot_general | solution.py:91
  142.3 3.0 %fusion.243 = (bf16[256,2048]{1,0:T(8,128)(2,1)S(1)}, f32[256,2048]{1,0:T(8,128)S(1)}) fusion(f32[256,2048]{1,0:T(8,128)S(1)} %fusion.121, bf16[2,768,2048]{2,1,0:T(8,128)(2,1)} %param.16, f32[256,1536]{1,0:T(8,128)S(1)} %copy-done.10, f32[256]{0:T(256)S(1)} %bitcast.269), kind=kOutput, calls=%fused_computation.295 | convolution fusion | flops 809107456 | bytes 9962496 | tf_op jit(solution)/shard_map/local_experts/dot_general | solution.py:91
  145.3 1.5 collective-permute-start.28
  147.4 1.5 collective-permute-start.18
  149.4 3.1 %collective-permute-done.28 = bf16[64,2048]{1,0:T(8,128)(2,1)S(1)} collective-permute-done((bf16[64,2048]{1,0:T(8,128)(2,1)S(1)}, bf16[64,2048]{1,0:T(8,128)(2,1)S(1)}, u32[]{:S(2)}, u32[]{:S(2)}) %collective-permute-start.28) | collective-permute-done | bytes 262176 | tf_op jit(solution)/shard_map/combine_return/ppermute | solution.py:75
  152.5 1.5 collective-permute-done.29
  154.9 1.7 collective-permute-start.30
  157.0 1.7 collective-permute-start.20
  159.6 1.9 collective-permute-done.30
  161.5 1.7 collective-permute-done.31
  163.2 1.3 collective-permute-done.20
  164.5 1.7 collective-permute-done.21
  166.2 5.7 %fusion.10 = f32[256,1536]{1,0:T(8,128)} fusion(bf16[2,2048,1536]{2,1,0:T(8,128)(2,1)} %param.15, bf16[64,2048]{1,0:T(8,128)(2,1)S(1)} %slice.561, bf16[64,2048]{1,0:T(8,128)(2,1)S(1)} %slice.560, bf16[64,2048]{1,0:T(8,128)(2,1)S(1)} %slice.559, bf16[64,2048]{1,0:T(8,128)(2,1)S(1)} %slice.558), kind=kOutput, calls=%fused_computation.10 | convolution fusion | flops 1614807040 | bytes 8912896 | tf_op jit(solution)/shard_map/local_experts/dot_general | solution.py:87
  171.9 5.7 %fusion.2 = f32[256,1536]{1,0:T(8,128)} fusion(bf16[2,2048,1536]{2,1,0:T(8,128)(2,1)} %param.15, bf16[64,2048]{1,0:T(8,128)(2,1)S(1)} %slice.561, bf16[64,2048]{1,0:T(8,128)(2,1)S(1)} %slice.560, bf16[64,2048]{1,0:T(8,128)(2,1)S(1)} %slice.559, bf16[64,2048]{1,0:T(8,128)(2,1)S(1)} %slice.558), kind=kOutput, calls=%fused_computation.2 | convolution fusion | flops 1614807040 | bytes 8912896 | tf_op jit(solution)/shard_map/local_experts/dot_general | solution.py:87
  178.1 3.5 %fusion.112 = f32[256,2048]{1,0:T(8,128)S(1)} fusion(bf16[2,768,2048]{2,1,0:T(8,128)(2,1)} %param.16, f32[256]{0:T(256)S(1)} %bitcast.274, f32[256,1536]{1,0:T(8,128)} %fusion.2), kind=kOutput, calls=%fused_computation.64 | convolution fusion | flops 808058880 | bytes 6816768 | tf_op jit(solution)/shard_map/local_experts/dot_general | solution.py:91
  181.6 3.0 %fusion.73 = f32[256,2048]{1,0:T(8,128)S(1)} fusion(f32[256,2048]{1,0:T(8,128)S(1)} %fusion.112, bf16[2,768,2048]{2,1,0:T(8,128)(2,1)} %param.16, f32[256]{0:T(256)S(1)} %bitcast.270, f32[256,1536]{1,0:T(8,128)S(1)} %copy-done.11), kind=kOutput, calls=%fused_computation.51 | convolution fusion | flops 808583168 | bytes 8913920 | tf_op jit(solution)/shard_map/local_experts/dot_general | solution.py:91
  184.7 1.6 collective-permute-start.32
  186.8 1.6 collective-permute-start.22
  188.8 2.3 collective-permute-done.32
  191.2 1.6 collective-permute-done.33
  194.3 1.4 collective-permute-start.35
  196.4 1.4 collective-permute-start.25
  198.2 2.0 collective-permute-done.34
  200.8 2.3 collective-permute-done.24
  203.9 5.7 %fusion.12 = f32[256,1536]{1,0:T(8,128)} fusion(bf16[2,2048,1536]{2,1,0:T(8,128)(2,1)} %param.15, bf16[64,2048]{1,0:T(8,128)(2,1)S(1)} %slice.533, bf16[64,2048]{1,0:T(8,128)(2,1)S(1)} %slice.532, bf16[64,2048]{1,0:T(8,128)(2,1)S(1)} %slice.531, bf16[64,2048]{1,0:T(8,128)(2,1)S(1)} %slice.530), kind=kOutput, calls=%fused_computation.12 | convolution fusion | flops 1614807040 | bytes 8912896 | tf_op jit(solution)/shard_map/local_experts/dot_general | solution.py:87
  209.6 5.7 %fusion.4 = f32[256,1536]{1,0:T(8,128)} fusion(bf16[2,2048,1536]{2,1,0:T(8,128)(2,1)} %param.15, bf16[64,2048]{1,0:T(8,128)(2,1)S(1)} %slice.533, bf16[64,2048]{1,0:T(8,128)(2,1)S(1)} %slice.532, bf16[64,2048]{1,0:T(8,128)(2,1)S(1)} %slice.531, bf16[64,2048]{1,0:T(8,128)(2,1)S(1)} %slice.530), kind=kOutput, calls=%fused_computation.4 | convolution fusion | flops 1614807040 | bytes 8912896 | tf_op jit(solution)/shard_map/local_experts/dot_general | solution.py:87
  215.8 3.5 %fusion.103 = f32[256,2048]{1,0:T(8,128)S(1)} fusion(bf16[2,768,2048]{2,1,0:T(8,128)(2,1)} %param.16, f32[256]{0:T(256)S(1)} %bitcast.275, f32[256,1536]{1,0:T(8,128)} %fusion.4), kind=kOutput, calls=%fused_computation.61 | convolution fusion | flops 808058880 | bytes 6816768 | tf_op jit(solution)/shard_map/local_experts/dot_general | solution.py:91
  219.3 3.7 %fusion.61 = f32[256,2048]{1,0:T(8,128)S(1)} fusion(f32[256,2048]{1,0:T(8,128)S(1)} %fusion.103, bf16[2,768,2048]{2,1,0:T(8,128)(2,1)} %param.16, f32[256]{0:T(256)S(1)} %bitcast.271, f32[256,1536]{1,0:T(8,128)S(1)} %copy-done.12), kind=kOutput, calls=%fused_computation.47 | convolution fusion | flops 808583168 | bytes 8913920 | tf_op jit(solution)/shard_map/local_experts/dot_general | solution.py:91
  223.6 1.7 collective-permute-start.37
  225.6 1.7 collective-permute-start.27
  227.3 2.3 collective-permute-done.36
  230.6 1.5 collective-permute-start.39
  233.3 2.9 %fusion.14 = f32[256,1536]{1,0:T(8,128)} fusion(bf16[2,2048,1536]{2,1,0:T(8,128)(2,1)S(1)} %bitcast.278, bf16[128,2048]{1,0:T(8,128)(2,1)S(1)} %fusion.136, bf16[64,2048]{1,0:T(8,128)(2,1)S(1)} %slice.501, bf16[64,2048]{1,0:T(8,128)(2,1)S(1)} %slice.500), kind=kOutput, calls=%fused_computation.14 | convolution fusion | flops 1613758464 | bytes 8912896 | tf_op jit(solution)/shard_map/local_experts/dot_general | solution.py:87
  236.2 2.9 %fusion.6 = f32[256,1536]{1,0:T(8,128)} fusion(bf16[2,2048,1536]{2,1,0:T(8,128)(2,1)S(1)} %bitcast.278, bf16[128,2048]{1,0:T(8,128)(2,1)S(1)} %fusion.136, bf16[64,2048]{1,0:T(8,128)(2,1)S(1)} %slice.501, bf16[64,2048]{1,0:T(8,128)(2,1)S(1)} %slice.500), kind=kOutput, calls=%fused_computation.6 | convolution fusion | flops 1613758464 | bytes 8912896 | tf_op jit(solution)/shard_map/local_experts/dot_general | solution.py:87
  239.6 3.5 %fusion.94 = f32[256,2048]{1,0:T(8,128)S(1)} fusion(bf16[2,768,2048]{2,1,0:T(8,128)(2,1)} %param.16, f32[256]{0:T(256)S(1)} %bitcast.276, f32[256,1536]{1,0:T(8,128)} %fusion.6), kind=kOutput, calls=%fused_computation.58 | convolution fusion | flops 808058880 | bytes 6816768 | tf_op jit(solution)/shard_map/local_experts/dot_general | solution.py:91
  243.1 3.0 %fusion.49 = f32[256,2048]{1,0:T(8,128)S(1)} fusion(f32[256,2048]{1,0:T(8,128)S(1)} %fusion.94, bf16[2,768,2048]{2,1,0:T(8,128)(2,1)} %param.16, f32[256]{0:T(256)S(1)} %bitcast.272, f32[256,1536]{1,0:T(8,128)S(1)} %copy-done.13), kind=kOutput, calls=%fused_computation.43 | convolution fusion | flops 808583168 | bytes 8913920 | tf_op jit(solution)/shard_map/local_experts/dot_general | solution.py:91
  247.9 1.4 collective-permute-start.41
  249.3 4.3 %collective-permute-done.40 = bf16[64,2048]{1,0:T(8,128)(2,1)S(1)} collective-permute-done((bf16[64,2048]{1,0:T(8,128)(2,1)S(1)}, bf16[64,2048]{1,0:T(8,128)(2,1)S(1)}, u32[]{:S(2)}, u32[]{:S(2)}) %collective-permute-start.40) | collective-permute-done | bytes 262176 | tf_op jit(solution)/shard_map/combine_return/ppermute | solution.py:75
  (180 shorter events, 38.6 us)
Async XLA Ops:
  0.6 36.2 %copy-start = (bf16[512,2048]{1,0:T(8,128)(2,1)S(1)}, bf16[512,2048]{1,0:T(8,128)(2,1)}, u32[]{:S(2)}) copy-start(bf16[512,2048]{1,0:T(8,128)(2,1)} %param.13) | copy-start | bytes 6291460
  2.4 8.6 %copy-start.9 = (s32[8]{0:T(128)S(1)}, s32[8]{0:T(128)}, u32[]{:S(2)}) copy-start(s32[8]{0:T(128)} %constant.200.clone) | copy-start | bytes 100
  2.4 20.5 %copy-start.4 = (s32[8]{0:T(128)S(1)}, s32[8]{0:T(128)}, u32[]{:S(2)}) copy-start(s32[8]{0:T(128)} %constant.201.clone) | copy-start | bytes 100
  3.8 33.0 %all-to-all-start = ((bf16[8,128,512]{2,1,0:T(8,128)(2,1)}), bf16[8,128,512]{2,1,0:T(8,128)(2,1)S(1)}, u32[]{:S(2)}, u32[]{:S(2)}) async-start(bf16[8,128,512]{2,1,0:T(8,128)(2,1)} %bitcast.1), calls=%async_computation | async-start | bytes 2097152 | tf_op jit(solution)/shard_map/out_projection/all_to_all | solution.py:137
  39.2 3.4 %copy-start.2 = (f32[8,128,2048]{2,1,0:T(8,128)}, f32[8,128,2048]{2,1,0:T(8,128)S(1)}, u32[]{:S(2)}) copy-start(f32[8,128,2048]{2,1,0:T(8,128)S(1)} %fusion.124) | copy-start | bytes 25165828
  42.6 7.0 %collective-permute-start = (bf16[64,2048]{1,0:T(8,128)(2,1)S(1)}, bf16[64,2048]{1,0:T(8,128)(2,1)S(1)}, u32[]{:S(2)}, u32[]{:S(2)}) collective-permute-start(bf16[64,2048]{1,0:T(8,128)(2,1)S(1)} %get-tuple-element.72), channel_id=1, source_target_pairs={{0,8},{8,16},{16,24},{24,28},{28,20},{20,12},{12,4},{4,0},{1,9},{9... | collective-permute-start | bytes 786440 | tf_op jit(solution)/shard_map/out_projection/ppermute | solution.py:37
  42.7 6.9 %collective-permute-start.1 = (bf16[64,2048]{1,0:T(8,128)(2,1)S(1)}, bf16[64,2048]{1,0:T(8,128)(2,1)S(1)}, u32[]{:S(2)}, u32[]{:S(2)}) collective-permute-start(bf16[64,2048]{1,0:T(8,128)(2,1)S(1)} %get-tuple-element.73), channel_id=1, source_target_pairs={{0,4},{8,0},{16,8},{24,16},{28,24},{20,28},{12,20},{4,12},{1,5},{9... | collective-permute-start | bytes 786440 | tf_op jit(solution)/shard_map/out_projection/ppermute | solution.py:37
  50.9 6.5 %collective-permute-start.2 = (bf16[64,2048]{1,0:T(8,128)(2,1)S(1)}, bf16[64,2048]{1,0:T(8,128)(2,1)S(1)}, u32[]{:S(2)}, u32[]{:S(2)}) collective-permute-start(bf16[64,2048]{1,0:T(8,128)(2,1)S(1)} %get-tuple-element.76), channel_id=1, source_target_pairs={{0,8},{8,16},{16,24},{24,28},{28,20},{20,12},{12,4},{4,0},{1,9},{9... | collective-permute-start | bytes 786440 | tf_op jit(solution)/shard_map/out_projection/ppermute | solution.py:37
  52.5 7.1 %collective-permute-start.3 = (bf16[64,2048]{1,0:T(8,128)(2,1)S(1)}, bf16[64,2048]{1,0:T(8,128)(2,1)S(1)}, u32[]{:S(2)}, u32[]{:S(2)}) collective-permute-start(bf16[64,2048]{1,0:T(8,128)(2,1)S(1)} %get-tuple-element.77), channel_id=1, source_target_pairs={{0,4},{8,0},{16,8},{24,16},{28,24},{20,28},{12,20},{4,12},{1,5},{9... | collective-permute-start | bytes 786440 | tf_op jit(solution)/shard_map/out_projection/ppermute | solution.py:37
  60.9 6.4 %collective-permute-start.4 = (bf16[64,2048]{1,0:T(8,128)(2,1)S(1)}, bf16[64,2048]{1,0:T(8,128)(2,1)S(1)}, u32[]{:S(2)}, u32[]{:S(2)}) collective-permute-start(bf16[64,2048]{1,0:T(8,128)(2,1)S(1)} %get-tuple-element.80), channel_id=1, source_target_pairs={{0,8},{8,16},{16,24},{24,28},{28,20},{20,12},{12,4},{4,0},{1,9},{9... | collective-permute-start | bytes 786440 | tf_op jit(solution)/shard_map/out_projection/ppermute | solution.py:37
  62.4 6.4 %collective-permute-start.5 = (bf16[64,2048]{1,0:T(8,128)(2,1)S(1)}, bf16[64,2048]{1,0:T(8,128)(2,1)S(1)}, u32[]{:S(2)}, u32[]{:S(2)}) collective-permute-start(bf16[64,2048]{1,0:T(8,128)(2,1)S(1)} %get-tuple-element.81), channel_id=1, source_target_pairs={{0,4},{8,0},{16,8},{24,16},{28,24},{20,28},{12,20},{4,12},{1,5},{9... | collective-permute-start | bytes 786440 | tf_op jit(solution)/shard_map/out_projection/ppermute | solution.py:37
  70.0 6.4 %collective-permute-start.6 = (bf16[64,2048]{1,0:T(8,128)(2,1)S(1)}, bf16[64,2048]{1,0:T(8,128)(2,1)S(1)}, u32[]{:S(2)}, u32[]{:S(2)}) collective-permute-start(bf16[64,2048]{1,0:T(8,128)(2,1)S(1)} %get-tuple-element.84), channel_id=1, source_target_pairs={{0,8},{8,16},{16,24},{24,28},{28,20},{20,12},{12,4},{4,0},{1,9},{9... | collective-permute-start | bytes 786440 | tf_op jit(solution)/shard_map/out_projection/ppermute | solution.py:37
  71.8 6.6 %collective-permute-start.7 = (bf16[64,2048]{1,0:T(8,128)(2,1)S(1)}, bf16[64,2048]{1,0:T(8,128)(2,1)S(1)}, u32[]{:S(2)}, u32[]{:S(2)}) collective-permute-start(bf16[64,2048]{1,0:T(8,128)(2,1)S(1)} %get-tuple-element.85), channel_id=1, source_target_pairs={{0,4},{8,0},{16,8},{24,16},{28,24},{20,28},{12,20},{4,12},{1,5},{9... | collective-permute-start | bytes 786440 | tf_op jit(solution)/shard_map/out_projection/ppermute | solution.py:37
  79.7 7.7 %collective-permute-start.8 = (bf16[64,2048]{1,0:T(8,128)(2,1)S(1)}, bf16[64,2048]{1,0:T(8,128)(2,1)S(1)}, u32[]{:S(2)}, u32[]{:S(2)}) collective-permute-start(bf16[64,2048]{1,0:T(8,128)(2,1)S(1)} %get-tuple-element.88), channel_id=1, source_target_pairs={{0,8},{8,16},{16,24},{24,28},{28,20},{20,12},{12,4},{4,0},{1,9},{9... | collective-permute-start | bytes 786440 | tf_op jit(solution)/shard_map/out_projection/ppermute | solution.py:37
  80.5 8.0 %collective-permute-start.9 = (bf16[64,2048]{1,0:T(8,128)(2,1)S(1)}, bf16[64,2048]{1,0:T(8,128)(2,1)S(1)}, u32[]{:S(2)}, u32[]{:S(2)}) collective-permute-start(bf16[64,2048]{1,0:T(8,128)(2,1)S(1)} %get-tuple-element.89), channel_id=1, source_target_pairs={{0,4},{8,0},{16,8},{24,16},{28,24},{20,28},{12,20},{4,12},{1,5},{9... | collective-permute-start | bytes 786440 | tf_op jit(solution)/shard_map/out_projection/ppermute | solution.py:37
  85.1 17.6 %copy-start.7 = (f32[128,8]{0,1:T(8,128)S(1)}, f32[128,8]{0,1:T(8,128)}, u32[]{:S(2)}) copy-start(f32[128,8]{0,1:T(8,128)} %param.18) | copy-start | bytes 12292
  85.1 17.5 %copy-start.8 = (s32[128,8]{0,1:T(8,128)S(1)}, s32[128,8]{0,1:T(8,128)}, u32[]{:S(2)}) copy-start(s32[128,8]{0,1:T(8,128)} %param.17) | copy-start | bytes 12292
  89.7 9.2 %collective-permute-start.10 = (bf16[64,2048]{1,0:T(8,128)(2,1)S(1)}, bf16[64,2048]{1,0:T(8,128)(2,1)S(1)}, u32[]{:S(2)}, u32[]{:S(2)}) collective-permute-start(bf16[64,2048]{1,0:T(8,128)(2,1)S(1)} %get-tuple-element.92), channel_id=1, source_target_pairs={{0,8},{8,16},{16,24},{24,28},{28,20},{20,12},{12,4},{4,0},{1,9},{9... | collective-permute-start | bytes 786440 | tf_op jit(solution)/shard_map/out_projection/ppermute | solution.py:37
  90.3 9.0 %collective-permute-start.11 = (bf16[64,2048]{1,0:T(8,128)(2,1)S(1)}, bf16[64,2048]{1,0:T(8,128)(2,1)S(1)}, u32[]{:S(2)}, u32[]{:S(2)}) collective-permute-start(bf16[64,2048]{1,0:T(8,128)(2,1)S(1)} %get-tuple-element.93), channel_id=1, source_target_pairs={{0,4},{8,0},{16,8},{24,16},{28,24},{20,28},{12,20},{4,12},{1,5},{9... | collective-permute-start | bytes 786440 | tf_op jit(solution)/shard_map/out_projection/ppermute | solution.py:37
  95.5 16.1 %copy-start.3 = (bf16[128,2048]{1,0:T(8,128)(2,1)S(1)}, bf16[128,2048]{1,0:T(8,128)(2,1)}, u32[]{:S(2)}) copy-start(bf16[128,2048]{1,0:T(8,128)(2,1)} %param.11) | copy-start | bytes 1572868
  100.6 9.2 %collective-permute-start.12 = (bf16[64,2048]{1,0:T(8,128)(2,1)S(1)}, bf16[64,2048]{1,0:T(8,128)(2,1)S(1)}, u32[]{:S(2)}, u32[]{:S(2)}) collective-permute-start(bf16[64,2048]{1,0:T(8,128)(2,1)S(1)} %get-tuple-element.96), channel_id=1, source_target_pairs={{0,8},{8,16},{16,24},{24,28},{28,20},{20,12},{12,4},{4,0},{1,9},{9... | collective-permute-start | bytes 786440 | tf_op jit(solution)/shard_map/out_projection/ppermute | solution.py:37
  102.1 8.3 %collective-permute-start.13 = (bf16[64,2048]{1,0:T(8,128)(2,1)S(1)}, bf16[64,2048]{1,0:T(8,128)(2,1)S(1)}, u32[]{:S(2)}, u32[]{:S(2)}) collective-permute-start(bf16[64,2048]{1,0:T(8,128)(2,1)S(1)} %get-tuple-element.97), channel_id=1, source_target_pairs={{0,4},{8,0},{16,8},{24,16},{28,24},{20,28},{12,20},{4,12},{1,5},{9... | collective-permute-start | bytes 786440 | tf_op jit(solution)/shard_map/out_projection/ppermute | solution.py:37
  105.2 6.8 %copy-start.5 = (f32[2048]{0:T(1024)S(1)}, f32[2048]{0:T(1024)}, u32[]{:S(2)}) copy-start(f32[2048]{0:T(1024)} %param.14) | copy-start | bytes 24580
  112.5 6.6 %collective-permute-start.14 = (bf16[64,2176]{1,0:T(8,128)(2,1)S(1)}, bf16[64,2176]{1,0:T(8,128)(2,1)S(1)}, u32[]{:S(2)}, u32[]{:S(2)}) collective-permute-start(bf16[64,2176]{1,0:T(8,128)(2,1)S(1)} %get-tuple-element.179), channel_id=1, source_target_pairs={{0,8},{8,16},{16,24},{24,28},{28,20},{20,12},{12,4},{4,0},{1,9},{9... | collective-permute-start | bytes 835592 | tf_op jit(solution)/shard_map/dispatch_gather/ppermute | solution.py:55
  113.2 6.5 %collective-permute-start.15 = (bf16[64,2176]{1,0:T(8,128)(2,1)S(1)}, bf16[64,2176]{1,0:T(8,128)(2,1)S(1)}, u32[]{:S(2)}, u32[]{:S(2)}) collective-permute-start(bf16[64,2176]{1,0:T(8,128)(2,1)S(1)} %get-tuple-element.178), channel_id=1, source_target_pairs={{0,4},{8,0},{16,8},{24,16},{28,24},{20,28},{12,20},{4,12},{1,5},{9... | collective-permute-start | bytes 835592 | tf_op jit(solution)/shard_map/dispatch_gather/ppermute | solution.py:55
  119.7 6.5 %collective-permute-start.16 = (bf16[64,2176]{1,0:T(8,128)(2,1)S(1)}, bf16[64,2176]{1,0:T(8,128)(2,1)S(1)}, u32[]{:S(2)}, u32[]{:S(2)}) collective-permute-start(bf16[64,2176]{1,0:T(8,128)(2,1)S(1)} %collective-permute-done.14), channel_id=1, source_target_pairs={{0,8},{8,16},{16,24},{24,28},{28,20},{20,12},{12,4},{4,0},{1,9},{9... | collective-permute-start | bytes 835592 | tf_op jit(solution)/shard_map/dispatch_gather/ppermute | solution.py:55
  120.2 6.6 %collective-permute-start.17 = (bf16[64,2176]{1,0:T(8,128)(2,1)S(1)}, bf16[64,2176]{1,0:T(8,128)(2,1)S(1)}, u32[]{:S(2)}, u32[]{:S(2)}) collective-permute-start(bf16[64,2176]{1,0:T(8,128)(2,1)S(1)} %collective-permute-done.15), channel_id=1, source_target_pairs={{0,4},{8,0},{16,8},{24,16},{28,24},{20,28},{12,20},{4,12},{1,5},{9... | collective-permute-start | bytes 835592 | tf_op jit(solution)/shard_map/dispatch_gather/ppermute | solution.py:55
  138.7 3.5 %copy-start.10 = (f32[256,1536]{1,0:T(8,128)S(1)}, f32[256,1536]{1,0:T(8,128)}, u32[]{:S(2)}) copy-start(f32[256,1536]{1,0:T(8,128)} %fusion.8) | copy-start | bytes 4718596
  145.3 7.2 %collective-permute-start.28 = (bf16[64,2048]{1,0:T(8,128)(2,1)S(1)}, bf16[64,2048]{1,0:T(8,128)(2,1)S(1)}, u32[]{:S(2)}, u32[]{:S(2)}) collective-permute-start(bf16[64,2048]{1,0:T(8,128)(2,1)S(1)} %get-tuple-element.114), channel_id=1, source_target_pairs={{0,8},{8,16},{16,24},{24,28},{28,20},{20,12},{12,4},{4,0},{1,9},{9... | collective-permute-start | bytes 786440 | tf_op jit(solution)/shard_map/combine_return/ppermute | solution.py:75
  146.8 7.2 %collective-permute-start.29 = (bf16[64,2048]{1,0:T(8,128)(2,1)S(1)}, bf16[64,2048]{1,0:T(8,128)(2,1)S(1)}, u32[]{:S(2)}, u32[]{:S(2)}) collective-permute-start(bf16[64,2048]{1,0:T(8,128)(2,1)S(1)} %get-tuple-element.115), channel_id=1, source_target_pairs={{0,4},{8,0},{16,8},{24,16},{28,24},{20,28},{12,20},{4,12},{1,5},{9... | collective-permute-start | bytes 786440 | tf_op jit(solution)/shard_map/combine_return/ppermute | solution.py:75
  147.4 9.6 %collective-permute-start.18 = (bf16[64,2176]{1,0:T(8,128)(2,1)S(1)}, bf16[64,2176]{1,0:T(8,128)(2,1)S(1)}, u32[]{:S(2)}, u32[]{:S(2)}) collective-permute-start(bf16[64,2176]{1,0:T(8,128)(2,1)S(1)} %collective-permute-done.16), channel_id=1, source_target_pairs={{0,8},{8,16},{16,24},{24,28},{28,20},{20,12},{12,4},{4,0},{1,9},{9... | collective-permute-start | bytes 835592 | tf_op jit(solution)/shard_map/dispatch_gather/ppermute | solution.py:55
  148.9 8.1 %collective-permute-start.19 = (bf16[64,2176]{1,0:T(8,128)(2,1)S(1)}, bf16[64,2176]{1,0:T(8,128)(2,1)S(1)}, u32[]{:S(2)}, u32[]{:S(2)}) collective-permute-start(bf16[64,2176]{1,0:T(8,128)(2,1)S(1)} %collective-permute-done.17), channel_id=1, source_target_pairs={{0,4},{8,0},{16,8},{24,16},{28,24},{20,28},{12,20},{4,12},{1,5},{9... | collective-permute-start | bytes 835592 | tf_op jit(solution)/shard_map/dispatch_gather/ppermute | solution.py:55
  154.9 6.6 %collective-permute-start.30 = (bf16[64,2048]{1,0:T(8,128)(2,1)}, bf16[64,2048]{1,0:T(8,128)(2,1)S(1)}, u32[]{:S(2)}, u32[]{:S(2)}) collective-permute-start(bf16[64,2048]{1,0:T(8,128)(2,1)} %get-tuple-element.118), channel_id=1, source_target_pairs={{0,8},{8,16},{16,24},{24,28},{28,20},{20,12},{12,4},{4,0},{1,9},{9... | collective-permute-start | bytes 786440 | tf_op jit(solution)/shard_map/combine_return/ppermute | solution.py:75
  156.6 6.6 %collective-permute-start.31 = (bf16[64,2048]{1,0:T(8,128)(2,1)}, bf16[64,2048]{1,0:T(8,128)(2,1)S(1)}, u32[]{:S(2)}, u32[]{:S(2)}) collective-permute-start(bf16[64,2048]{1,0:T(8,128)(2,1)} %get-tuple-element.119), channel_id=1, source_target_pairs={{0,4},{8,0},{16,8},{24,16},{28,24},{20,28},{12,20},{4,12},{1,5},{9... | collective-permute-start | bytes 786440 | tf_op jit(solution)/shard_map/combine_return/ppermute | solution.py:75
  157.0 7.5 %collective-permute-start.20 = (bf16[64,2176]{1,0:T(8,128)(2,1)S(1)}, bf16[64,2176]{1,0:T(8,128)(2,1)S(1)}, u32[]{:S(2)}, u32[]{:S(2)}) collective-permute-start(bf16[64,2176]{1,0:T(8,128)(2,1)S(1)} %collective-permute-done.18), channel_id=1, source_target_pairs={{0,8},{8,16},{16,24},{24,28},{28,20},{20,12},{12,4},{4,0},{1,9},{9... | collective-permute-start | bytes 835592 | tf_op jit(solution)/shard_map/dispatch_gather/ppermute | solution.py:55
  158.7 7.5 %collective-permute-start.21 = (bf16[64,2176]{1,0:T(8,128)(2,1)S(1)}, bf16[64,2176]{1,0:T(8,128)(2,1)S(1)}, u32[]{:S(2)}, u32[]{:S(2)}) collective-permute-start(bf16[64,2176]{1,0:T(8,128)(2,1)S(1)} %collective-permute-done.19), channel_id=1, source_target_pairs={{0,4},{8,0},{16,8},{24,16},{28,24},{20,28},{12,20},{4,12},{1,5},{9... | collective-permute-start | bytes 835592 | tf_op jit(solution)/shard_map/dispatch_gather/ppermute | solution.py:55
  178.1 3.5 %copy-start.11 = (f32[256,1536]{1,0:T(8,128)S(1)}, f32[256,1536]{1,0:T(8,128)}, u32[]{:S(2)}) copy-start(f32[256,1536]{1,0:T(8,128)} %fusion.10) | copy-start | bytes 4718596
  184.7 6.4 %collective-permute-start.32 = (bf16[64,2048]{1,0:T(8,128)(2,1)S(1)}, bf16[64,2048]{1,0:T(8,128)(2,1)S(1)}, u32[]{:S(2)}, u32[]{:S(2)}) collective-permute-start(bf16[64,2048]{1,0:T(8,128)(2,1)S(1)} %get-tuple-element.122), channel_id=1, source_target_pairs={{0,8},{8,16},{16,24},{24,28},{28,20},{20,12},{12,4},{4,0},{1,9},{9... | collective-permute-start | bytes 786440 | tf_op jit(solution)/shard_map/combine_return/ppermute | solution.py:75
  186.3 6.4 %collective-permute-start.33 = (bf16[64,2048]{1,0:T(8,128)(2,1)S(1)}, bf16[64,2048]{1,0:T(8,128)(2,1)S(1)}, u32[]{:S(2)}, u32[]{:S(2)}) collective-permute-start(bf16[64,2048]{1,0:T(8,128)(2,1)S(1)} %get-tuple-element.123), channel_id=1, source_target_pairs={{0,4},{8,0},{16,8},{24,16},{28,24},{20,28},{12,20},{4,12},{1,5},{9... | collective-permute-start | bytes 786440 | tf_op jit(solution)/shard_map/combine_return/ppermute | solution.py:75
  186.8 8.8 %collective-permute-start.22 = (bf16[64,2176]{1,0:T(8,128)(2,1)S(1)}, bf16[64,2176]{1,0:T(8,128)(2,1)S(1)}, u32[]{:S(2)}, u32[]{:S(2)}) collective-permute-start(bf16[64,2176]{1,0:T(8,128)(2,1)S(1)} %collective-permute-done.20), channel_id=1, source_target_pairs={{0,8},{8,16},{16,24},{24,28},{28,20},{20,12},{12,4},{4,0},{1,9},{9... | collective-permute-start | bytes 835592 | tf_op jit(solution)/shard_map/dispatch_gather/ppermute | solution.py:55
  188.4 7.3 %collective-permute-start.23 = (bf16[64,2176]{1,0:T(8,128)(2,1)S(1)}, bf16[64,2176]{1,0:T(8,128)(2,1)S(1)}, u32[]{:S(2)}, u32[]{:S(2)}) collective-permute-start(bf16[64,2176]{1,0:T(8,128)(2,1)S(1)} %collective-permute-done.21), channel_id=1, source_target_pairs={{0,4},{8,0},{16,8},{24,16},{28,24},{20,28},{12,20},{4,12},{1,5},{9... | collective-permute-start | bytes 835592 | tf_op jit(solution)/shard_map/dispatch_gather/ppermute | solution.py:55
  193.6 6.6 %collective-permute-start.34 = (bf16[64,2048]{1,0:T(8,128)(2,1)}, bf16[64,2048]{1,0:T(8,128)(2,1)S(1)}, u32[]{:S(2)}, u32[]{:S(2)}) collective-permute-start(bf16[64,2048]{1,0:T(8,128)(2,1)} %get-tuple-element.126), channel_id=1, source_target_pairs={{0,8},{8,16},{16,24},{24,28},{28,20},{20,12},{12,4},{4,0},{1,9},{9... | collective-permute-start | bytes 786440 | tf_op jit(solution)/shard_map/combine_return/ppermute | solution.py:75
  194.3 6.6 %collective-permute-start.35 = (bf16[64,2048]{1,0:T(8,128)(2,1)}, bf16[64,2048]{1,0:T(8,128)(2,1)S(1)}, u32[]{:S(2)}, u32[]{:S(2)}) collective-permute-start(bf16[64,2048]{1,0:T(8,128)(2,1)} %get-tuple-element.127), channel_id=1, source_target_pairs={{0,4},{8,0},{16,8},{24,16},{28,24},{20,28},{12,20},{4,12},{1,5},{9... | collective-permute-start | bytes 786440 | tf_op jit(solution)/shard_map/combine_return/ppermute | solution.py:75
  195.7 7.5 %collective-permute-start.24 = (bf16[64,2176]{1,0:T(8,128)(2,1)S(1)}, bf16[64,2176]{1,0:T(8,128)(2,1)S(1)}, u32[]{:S(2)}, u32[]{:S(2)}) collective-permute-start(bf16[64,2176]{1,0:T(8,128)(2,1)S(1)} %collective-permute-done.22), channel_id=1, source_target_pairs={{0,8},{8,16},{16,24},{24,28},{28,20},{20,12},{12,4},{4,0},{1,9},{9... | collective-permute-start | bytes 835592 | tf_op jit(solution)/shard_map/dispatch_gather/ppermute | solution.py:55
  196.4 7.5 %collective-permute-start.25 = (bf16[64,2176]{1,0:T(8,128)(2,1)S(1)}, bf16[64,2176]{1,0:T(8,128)(2,1)S(1)}, u32[]{:S(2)}, u32[]{:S(2)}) collective-permute-start(bf16[64,2176]{1,0:T(8,128)(2,1)S(1)} %collective-permute-done.23), channel_id=1, source_target_pairs={{0,4},{8,0},{16,8},{24,16},{28,24},{20,28},{12,20},{4,12},{1,5},{9... | collective-permute-start | bytes 835592 | tf_op jit(solution)/shard_map/dispatch_gather/ppermute | solution.py:55
  215.8 3.6 %copy-start.12 = (f32[256,1536]{1,0:T(8,128)S(1)}, f32[256,1536]{1,0:T(8,128)}, u32[]{:S(2)}) copy-start(f32[256,1536]{1,0:T(8,128)} %fusion.12) | copy-start | bytes 4718596
  215.8 17.5 %slice-start = ((s8[12582912]{0:T(1024)(128)(4,1)}), s8[4194304]{0:T(1024)(128)(4,1)S(1)}, s32[]{:S(2)}) async-start(s8[12582912]{0:T(1024)(128)(4,1)} %bitcast.277), calls=%async_computation.1 | async-start | bytes 8388608
  215.8 17.5 %slice-start.1 = ((s8[12582912]{0:T(1024)(128)(4,1)}), s8[4194304]{0:T(1024)(128)(4,1)S(1)}, s32[]{:S(2)}) async-start(s8[12582912]{0:T(1024)(128)(4,1)} %bitcast.277), calls=%async_computation.2 | async-start | bytes 8388608
  219.3 14.0 %slice-start.2 = ((s8[12582912]{0:T(1024)(128)(4,1)}), s8[4194304]{0:T(1024)(128)(4,1)S(1)}, s32[]{:S(2)}) async-start(s8[12582912]{0:T(1024)(128)(4,1)} %bitcast.277), calls=%async_computation.3 | async-start | bytes 8388608
  223.2 6.4 %collective-permute-start.36 = (bf16[64,2048]{1,0:T(8,128)(2,1)S(1)}, bf16[64,2048]{1,0:T(8,128)(2,1)S(1)}, u32[]{:S(2)}, u32[]{:S(2)}) collective-permute-start(bf16[64,2048]{1,0:T(8,128)(2,1)S(1)} %get-tuple-element.130), channel_id=1, source_target_pairs={{0,8},{8,16},{16,24},{24,28},{28,20},{20,12},{12,4},{4,0},{1,9},{9... | collective-permute-start | bytes 786440 | tf_op jit(solution)/shard_map/combine_return/ppermute | solution.py:75
  223.6 6.4 %collective-permute-start.37 = (bf16[64,2048]{1,0:T(8,128)(2,1)S(1)}, bf16[64,2048]{1,0:T(8,128)(2,1)S(1)}, u32[]{:S(2)}, u32[]{:S(2)}) collective-permute-start(bf16[64,2048]{1,0:T(8,128)(2,1)S(1)} %get-tuple-element.131), channel_id=1, source_target_pairs={{0,4},{8,0},{16,8},{24,16},{28,24},{20,28},{12,20},{4,12},{1,5},{9... | collective-permute-start | bytes 786440 | tf_op jit(solution)/shard_map/combine_return/ppermute | solution.py:75
  225.3 7.6 %collective-permute-start.26 = (bf16[64,2176]{1,0:T(8,128)(2,1)S(1)}, bf16[64,2176]{1,0:T(8,128)(2,1)S(1)}, u32[]{:S(2)}, u32[]{:S(2)}) collective-permute-start(bf16[64,2176]{1,0:T(8,128)(2,1)S(1)} %collective-permute-done.24), channel_id=1, source_target_pairs={{0,8},{8,16},{16,24},{24,28},{28,20},{20,12},{12,4},{4,0},{1,9},{9... | collective-permute-start | bytes 835592 | tf_op jit(solution)/shard_map/dispatch_gather/ppermute | solution.py:55
  225.6 7.6 %collective-permute-start.27 = (bf16[64,2176]{1,0:T(8,128)(2,1)S(1)}, bf16[64,2176]{1,0:T(8,128)(2,1)S(1)}, u32[]{:S(2)}, u32[]{:S(2)}) collective-permute-start(bf16[64,2176]{1,0:T(8,128)(2,1)S(1)} %collective-permute-done.25), channel_id=1, source_target_pairs={{0,4},{8,0},{16,8},{24,16},{28,24},{20,28},{12,20},{4,12},{1,5},{9... | collective-permute-start | bytes 835592 | tf_op jit(solution)/shard_map/dispatch_gather/ppermute | solution.py:55
  230.0 16.1 %collective-permute-start.38 = (bf16[64,2048]{1,0:T(8,128)(2,1)S(1)}, bf16[64,2048]{1,0:T(8,128)(2,1)S(1)}, u32[]{:S(2)}, u32[]{:S(2)}) collective-permute-start(bf16[64,2048]{1,0:T(8,128)(2,1)S(1)} %get-tuple-element.134), channel_id=1, source_target_pairs={{0,8},{8,16},{16,24},{24,28},{28,20},{20,12},{12,4},{4,0},{1,9},{9... | collective-permute-start | bytes 786440 | tf_op jit(solution)/shard_map/combine_return/ppermute | solution.py:75
  230.6 15.6 %collective-permute-start.39 = (bf16[64,2048]{1,0:T(8,128)(2,1)S(1)}, bf16[64,2048]{1,0:T(8,128)(2,1)}, u32[]{:S(2)}, u32[]{:S(2)}) collective-permute-start(bf16[64,2048]{1,0:T(8,128)(2,1)S(1)} %get-tuple-element.135), channel_id=1, source_target_pairs={{0,4},{8,0},{16,8},{24,16},{28,24},{20,28},{12,20},{4,12},{1,5},{9... | collective-permute-start | bytes 786440 | tf_op jit(solution)/shard_map/combine_return/ppermute | solution.py:75
  239.6 3.5 %copy-start.13 = (f32[256,1536]{1,0:T(8,128)S(1)}, f32[256,1536]{1,0:T(8,128)}, u32[]{:S(2)}) copy-start(f32[256,1536]{1,0:T(8,128)} %fusion.14) | copy-start | bytes 4718596
  247.2 7.5 %copy-start.6 = (f32[2048]{0:T(1024)S(1)}, f32[2048]{0:T(1024)}, u32[]{:S(2)}) copy-start(f32[2048]{0:T(1024)} %param.19) | copy-start | bytes 24580
  247.3 6.4 %collective-permute-start.40 = (bf16[64,2048]{1,0:T(8,128)(2,1)S(1)}, bf16[64,2048]{1,0:T(8,128)(2,1)S(1)}, u32[]{:S(2)}, u32[]{:S(2)}) collective-permute-start(bf16[64,2048]{1,0:T(8,128)(2,1)S(1)} %get-tuple-element.138), channel_id=1, source_target_pairs={{0,8},{8,16},{16,24},{24,28},{28,20},{20,12},{12,4},{4,0},{1,9},{9... | collective-permute-start | bytes 786440 | tf_op jit(solution)/shard_map/combine_return/ppermute | solution.py:75
  247.9 6.4 %collective-permute-start.41 = (bf16[64,2048]{1,0:T(8,128)(2,1)S(1)}, bf16[64,2048]{1,0:T(8,128)(2,1)S(1)}, u32[]{:S(2)}, u32[]{:S(2)}) collective-permute-start(bf16[64,2048]{1,0:T(8,128)(2,1)S(1)} %get-tuple-element.139), channel_id=1, source_target_pairs={{0,4},{8,0},{16,8},{24,16},{28,24},{20,28},{12,20},{4,12},{1,5},{9... | collective-permute-start | bytes 786440 | tf_op jit(solution)/shard_map/combine_return/ppermute | solution.py:75
  254.5 1.9 copy-start.1

commit v11 on v9

--- a/solution.py
+++ b/solution.py
@@ -115,13 +115,13 @@
             jnp.where(route_ids[:, :, None] == expert_ids, route_weight[:, :, None], 0.0), axis=1
         )
         dense_weight = dense_weight.reshape(row_count, ep_size, local_experts).transpose(1, 0, 2)
-        row_weights = lax.all_to_all(dense_weight, "ep", split_axis=0, concat_axis=0, tiled=True)
-        row_weights = row_weights.reshape(group_rows, local_experts)
 
     with jax.named_scope("out_projection"):
         columns = attn_out.reshape(row_count, ep_size, slice_width).transpose(1, 0, 2)
         columns = lax.all_to_all(columns, "ep", split_axis=0, concat_axis=0, tiled=True)
-        columns, row_weights = lax.optimization_barrier((columns, row_weights))
+        columns, dense_weight = lax.optimization_barrier((columns, dense_weight))
+        row_weights = lax.all_to_all(dense_weight, "ep", split_axis=0, concat_axis=0, tiled=True)
+        row_weights = row_weights.reshape(group_rows, local_experts)
         partial = jnp.dot(
             columns.reshape(group_rows, slice_width), out_weight, preferred_element_type=jnp.float32
         )

time: 220 us -> 230 us (1.045)
  waiting for transfers between devices: 69.3 us -> 81.7 us
  matrix products: 30.8 us -> 27.8 us
    ppermute x7, waiting for transfers between devices: 11.6 us -> 24.5 us  [ring_reduce_scatter(): lax.ppermute(send_fwd, 'ep', forward)]
    all_to_all x1, starting transfers between devices: 3.56 us -> 7.28 us  [body(): lax.all_to_all(columns, 'ep', split_axis=0, concat_axis=0, tiled=True)]
    dot_general x8, matrix products: 20.1 us -> 17.2 us  [expert_mix(): projected_up = jnp.dot(rows, gate_up[e], preferred_element_type=jnp.float32)]
    ppermute x7, starting transfers between devices: 7.13 us -> 9.89 us  [ring_reduce_scatter(): lax.ppermute(send_fwd, 'ep', forward)]
  transfers between devices with their start and end apart: 44 -> 44, of which waited for: 34 -> 31; matrix products, arithmetic and copies ran while one was open for 15% -> 13% of each run, Pallas kernels for 0% -> 0%
where the time goes in v11:
time: 230 us; the launch traced here: 229 us
  waiting for transfers between devices  81.7 us (36%)
  starting transfers between devices  57.3 us (25%)
  between operations  40.6 us (18%)
  matrix products  27.8 us (12%)
  other arithmetic  12.9 us (6%)
  local copies, waits for them, and re-layouts  8.69 us (4%)
    ppermute x7, waiting for transfers between devices, ring_reduce_scatter(): lax.ppermute(send_fwd, 'ep', forward)  24.5 us
    dot_general x8, matrix products, expert_mix(): projected_up = jnp.dot(rows, gate_up[e], preferred_element_type=jnp.float32)  17.2 us
    ppermute x7, waiting for transfers between devices, ring_reduce_scatter_steps(): lax.ppermute(send_fwd, 'ep', forward)  17 us
    ppermute x7, starting transfers between devices, ring_reduce_scatter_steps(): lax.ppermute(send_bwd, 'ep', backward)  10.9 us
    ppermute x7, starting transfers between devices, ring_reduce_scatter(): lax.ppermute(send_fwd, 'ep', forward)  9.89 us
    ppermute x7, waiting for transfers between devices, ring_all_gather(): lax.ppermute(got_fwd, 'ep', forward)  8.96 us
    all_to_all x1, waiting for transfers between devices, body(): lax.all_to_all(columns, 'ep', split_axis=0, concat_axis=0, tiled=True)  8.65 us
    dot_general x8, matrix products, expert_mix(): jnp.dot(activated, down[e], preferred_element_type=jnp.float32)  8.32 us
  transfers between devices with their start and end apart: 44, of which 31 were waited for; matrix products, arithmetic and copies ran while one was open for 13% of the time, Pallas kernels for 0%

profile of v11, /device:TPU:0, one launch (start us, length us, event | category | flops | bytes accessed | tf_op | source)
XLA Modules:
  0.0 229.2 jit_solution(3633635725612478928)
XLA Ops:
  0.7 2.4 %copy.20 = bf16[16,8,8,512]{3,2,0,1:T(8,128)(2,1)} copy(bf16[16,8,8,512]{3,2,1,0:T(8,128)(2,1)} %bitcast.252) | data formatting | bytes 2097152 | tf_op jit(solution)/shard_map/out_projection/reshape | solution.py:120
  3.1 7.3 %all-to-all-start = ((bf16[8,128,512]{2,1,0:T(8,128)(2,1)}), bf16[8,128,512]{2,1,0:T(8,128)(2,1)S(1)}, u32[]{:S(2)}, u32[]{:S(2)}) async-start(bf16[8,128,512]{2,1,0:T(8,128)(2,1)} %bitcast.251), calls=%async_computation | async-start | bytes 2097152 | tf_op jit(solution)/shard_map/out_projection/all_to_all | solution.py:121
  27.5 8.7 %all-to-all-done = bf16[8,128,512]{2,1,0:T(8,128)(2,1)S(1)} async-done(((bf16[8,128,512]{2,1,0:T(8,128)(2,1)}), bf16[8,128,512]{2,1,0:T(8,128)(2,1)S(1)}, u32[]{:S(2)}, u32[]{:S(2)}) %all-to-all-start) | async-done | bytes 1048608 | tf_op jit(solution)/shard_map/out_projection/all_to_all | solution.py:121
  36.2 2.3 %fusion.124 = f32[8,128,2048]{2,1,0:T(8,128)S(1)} fusion(bf16[8,128,512]{2,1,0:T(8,128)(2,1)S(1)} %all-to-all-done, bf16[512,2048]{1,0:T(8,128)(2,1)S(1)} %copy-done), kind=kOutput, calls=%fused_computation.68 | convolution fusion | flops 2147483648 | bytes 11534336 | tf_op jit(solution)/shard_map/out_projection/dot_general | solution.py:125
  38.5 3.4 %copy-done.2 = f32[8,128,2048]{2,1,0:T(8,128)} copy-done((f32[8,128,2048]{2,1,0:T(8,128)}, f32[8,128,2048]{2,1,0:T(8,128)S(1)}, u32[]{:S(2)}) %copy-start.2) | copy-done | bytes 8388632
  42.0 2.0 collective-permute-start.1
  47.8 1.2 collective-permute-done
  49.0 1.3 fusion.170
  50.3 1.6 collective-permute-start.2
  72.8 5.2 %all-to-all-start.1 = ((f32[8,128,2]{1,2,0:T(2,128)}), f32[8,128,2]{1,2,0:T(2,128)S(1)}, u32[]{:S(2)}, u32[]{:S(2)}) async-start(f32[8,128,2]{1,2,0:T(2,128)} %bitcast.2), calls=%async_computation.1 | async-start | bytes 16384 | tf_op jit(solution)/shard_map/out_projection/all_to_all | solution.py:123
  78.0 1.3 fusion.168
  79.3 2.1 collective-permute-start.4
  81.5 3.2 %all-to-all-done.1 = f32[8,128,2]{1,2,0:T(2,128)S(1)} async-done(((f32[8,128,2]{1,2,0:T(2,128)}), f32[8,128,2]{1,2,0:T(2,128)S(1)}, u32[]{:S(2)}, u32[]{:S(2)}) %all-to-all-start.1) | async-done | bytes 8224 | tf_op jit(solution)/shard_map/out_projection/all_to_all | solution.py:123
  85.8 2.0 collective-permute-done.5
  87.8 1.3 fusion.166
  89.1 1.5 collective-permute-start.6
  91.3 4.2 %collective-permute-done.6 = bf16[64,2048]{1,0:T(8,128)(2,1)S(1)} collective-permute-done((bf16[64,2048]{1,0:T(8,128)(2,1)S(1)}, bf16[64,2048]{1,0:T(8,128)(2,1)S(1)}, u32[]{:S(2)}, u32[]{:S(2)}) %collective-permute-start.6) | collective-permute-done | bytes 262176 | tf_op jit(solution)/shard_map/out_projection/ppermute | solution.py:37
  95.5 1.5 collective-permute-done.7
  97.0 1.5 fusion.164
  98.5 1.5 collective-permute-start.8
  100.6 4.9 %collective-permute-done.8 = bf16[64,2048]{1,0:T(8,128)(2,1)S(1)} collective-permute-done((bf16[64,2048]{1,0:T(8,128)(2,1)S(1)}, bf16[64,2048]{1,0:T(8,128)(2,1)S(1)}, u32[]{:S(2)}, u32[]{:S(2)}) %collective-permute-start.8) | collective-permute-done | bytes 262176 | tf_op jit(solution)/shard_map/out_projection/ppermute | solution.py:37
  105.5 1.8 collective-permute-done.9
  107.3 1.3 fusion.162
  108.6 2.6 %collective-permute-start.10 = (bf16[64,2048]{1,0:T(8,128)(2,1)S(1)}, bf16[64,2048]{1,0:T(8,128)(2,1)S(1)}, u32[]{:S(2)}, u32[]{:S(2)}) collective-permute-start(bf16[64,2048]{1,0:T(8,128)(2,1)S(1)} %get-tuple-element.95), channel_id=1, source_target_pairs={{0,8},{8,16},{16,24},{24,28},{28,20},{20,12},{12,4},{4,0},{1,9},{9... | collective-permute-start | bytes 786440 | tf_op jit(solution)/shard_map/out_projection/ppermute | solution.py:37
  111.3 6.5 %collective-permute-done.10 = bf16[64,2048]{1,0:T(8,128)(2,1)S(1)} collective-permute-done((bf16[64,2048]{1,0:T(8,128)(2,1)S(1)}, bf16[64,2048]{1,0:T(8,128)(2,1)S(1)}, u32[]{:S(2)}, u32[]{:S(2)}) %collective-permute-start.10) | collective-permute-done | bytes 262176 | tf_op jit(solution)/shard_map/out_projection/ppermute | solution.py:37
  117.7 2.2 collective-permute-done.11
  119.9 1.3 fusion.160
  121.9 1.5 collective-permute-start.13
  123.5 6.8 %collective-permute-done.12 = bf16[64,2048]{1,0:T(8,128)(2,1)S(1)} collective-permute-done((bf16[64,2048]{1,0:T(8,128)(2,1)S(1)}, bf16[64,2048]{1,0:T(8,128)(2,1)S(1)}, u32[]{:S(2)}, u32[]{:S(2)}) %collective-permute-start.12) | collective-permute-done | bytes 262176 | tf_op jit(solution)/shard_map/out_projection/ppermute | solution.py:37
  130.3 1.3 fusion.183
  132.5 1.7 collective-permute-start.14
  134.3 4.5 %collective-permute-done.15 = bf16[64,2048]{1,0:T(8,128)(2,1)S(1)} collective-permute-done((bf16[64,2048]{1,0:T(8,128)(2,1)S(1)}, bf16[64,2048]{1,0:T(8,128)(2,1)S(1)}, u32[]{:S(2)}, u32[]{:S(2)}) %collective-permute-start.15) | collective-permute-done | bytes 262176 | tf_op jit(solution)/shard_map/dispatch_gather/ppermute | solution.py:55
  138.9 2.4 %collective-permute-start.16 = (bf16[64,2048]{1,0:T(8,128)(2,1)S(1)}, bf16[64,2048]{1,0:T(8,128)(2,1)S(1)}, u32[]{:S(2)}, u32[]{:S(2)}) collective-permute-start(bf16[64,2048]{1,0:T(8,128)(2,1)S(1)} %collective-permute-done.14), channel_id=1, source_target_pairs={{0,8},{8,16},{16,24},{24,28},{28,20},{20,12},{12,4},{4,0},{1,9},{9... | collective-permute-start | bytes 786440 | tf_op jit(solution)/shard_map/dispatch_gather/ppermute | solution.py:55
  141.4 3.9 %collective-permute-done.16 = bf16[64,2048]{1,0:T(8,128)(2,1)S(1)} collective-permute-done((bf16[64,2048]{1,0:T(8,128)(2,1)S(1)}, bf16[64,2048]{1,0:T(8,128)(2,1)S(1)}, u32[]{:S(2)}, u32[]{:S(2)}) %collective-permute-start.16) | collective-permute-done | bytes 262176 | tf_op jit(solution)/shard_map/dispatch_gather/ppermute | solution.py:55
  145.3 2.4 %collective-permute-done.17 = bf16[64,2048]{1,0:T(8,128)(2,1)S(1)} collective-permute-done((bf16[64,2048]{1,0:T(8,128)(2,1)S(1)}, bf16[64,2048]{1,0:T(8,128)(2,1)S(1)}, u32[]{:S(2)}, u32[]{:S(2)}) %collective-permute-start.17) | collective-permute-done | bytes 262176 | tf_op jit(solution)/shard_map/dispatch_gather/ppermute | solution.py:55
  147.7 2.0 collective-permute-start.19
  149.8 4.7 %fusion = f32[256,1536]{1,0:T(8,128)S(1)} fusion(bf16[256,2048]{1,0:T(8,128)(2,1)S(1)} %constant_dynamic-update-slice_fusion.8, bf16[2,2048,1536]{2,1,0:T(8,128)(2,1)} %param.16), kind=kOutput, calls=%fused_computation | convolution fusion | flops 1610612736 | bytes 8912896 | tf_op jit(solution)/shard_map/local_experts/dot_general | solution.py:87
  154.6 1.8 fusion.8
  158.6 2.0 collective-permute-start.29
  160.8 2.0 collective-permute-start.21
  162.7 3.8 %collective-permute-done.28 = bf16[64,2048]{1,0:T(8,128)(2,1)S(1)} collective-permute-done((bf16[64,2048]{1,0:T(8,128)(2,1)S(1)}, bf16[64,2048]{1,0:T(8,128)(2,1)S(1)}, u32[]{:S(2)}, u32[]{:S(2)}) %collective-permute-start.28) | collective-permute-done | bytes 262176 | tf_op jit(solution)/shard_map/combine_return/ppermute | solution.py:75
  167.4 1.5 collective-permute-start.31
  169.0 1.7 collective-permute-done.20
  171.1 1.6 collective-permute-start.23
  172.7 1.8 fusion.2
  174.5 1.8 fusion.10
  178.9 1.7 collective-permute-start.32
  182.3 1.7 collective-permute-start.24
  184.3 3.8 %collective-permute-done.32 = bf16[64,2048]{1,0:T(8,128)(2,1)S(1)} collective-permute-done((bf16[64,2048]{1,0:T(8,128)(2,1)S(1)}, bf16[64,2048]{1,0:T(8,128)(2,1)S(1)}, u32[]{:S(2)}, u32[]{:S(2)}) %collective-permute-start.32) | collective-permute-done | bytes 262176 | tf_op jit(solution)/shard_map/combine_return/ppermute | solution.py:75
  189.9 1.5 collective-permute-start.35
  191.4 2.4 %collective-permute-done.24 = bf16[64,2048]{1,0:T(8,128)(2,1)S(1)} collective-permute-done((bf16[64,2048]{1,0:T(8,128)(2,1)S(1)}, bf16[64,2048]{1,0:T(8,128)(2,1)S(1)}, u32[]{:S(2)}, u32[]{:S(2)}) %collective-permute-start.24) | collective-permute-done | bytes 262176 | tf_op jit(solution)/shard_map/dispatch_gather/ppermute | solution.py:55
  194.6 1.7 collective-permute-start.27
  196.4 1.8 fusion.4
  198.2 1.8 fusion.12
  202.5 1.7 collective-permute-start.37
  204.3 1.8 fusion.6
  206.1 1.8 fusion.14
  207.9 3.1 %collective-permute-done.36 = bf16[64,2048]{1,0:T(8,128)(2,1)S(1)} collective-permute-done((bf16[64,2048]{1,0:T(8,128)(2,1)S(1)}, bf16[64,2048]{1,0:T(8,128)(2,1)S(1)}, u32[]{:S(2)}, u32[]{:S(2)}) %collective-permute-start.36) | collective-permute-done | bytes 262176 | tf_op jit(solution)/shard_map/combine_return/ppermute | solution.py:75
  211.2 2.4 %collective-permute-start.39 = (bf16[64,2048]{1,0:T(8,128)(2,1)S(1)}, bf16[64,2048]{1,0:T(8,128)(2,1)S(1)}, u32[]{:S(2)}, u32[]{:S(2)}) collective-permute-start(bf16[64,2048]{1,0:T(8,128)(2,1)S(1)} %get-tuple-element.139), channel_id=1, source_target_pairs={{0,4},{8,0},{16,8},{24,16},{28,24},{20,28},{12,20},{4,12},{1,5},{9... | collective-permute-start | bytes 786440 | tf_op jit(solution)/shard_map/combine_return/ppermute | solution.py:75
  215.7 2.0 collective-permute-done.38
  218.9 1.3 collective-permute-start.41
  220.2 4.3 %collective-permute-done.40 = bf16[64,2048]{1,0:T(8,128)(2,1)S(1)} collective-permute-done((bf16[64,2048]{1,0:T(8,128)(2,1)S(1)}, bf16[64,2048]{1,0:T(8,128)(2,1)S(1)}, u32[]{:S(2)}, u32[]{:S(2)}) %collective-permute-start.40) | collective-permute-done | bytes 262176 | tf_op jit(solution)/shard_map/combine_return/ppermute | solution.py:75
  224.5 2.5 %collective-permute-done.41 = bf16[64,2048]{1,0:T(8,128)(2,1)S(1)} collective-permute-done((bf16[64,2048]{1,0:T(8,128)(2,1)S(1)}, bf16[64,2048]{1,0:T(8,128)(2,1)S(1)}, u32[]{:S(2)}, u32[]{:S(2)}) %collective-permute-start.41) | collective-permute-done | bytes 262176 | tf_op jit(solution)/shard_map/combine_return/ppermute | solution.py:75
  227.4 1.2 multiply_convert_fusion
  (128 shorter events, 25.0 us)
Async XLA Ops:
  0.6 35.5 %copy-start = (bf16[512,2048]{1,0:T(8,128)(2,1)S(1)}, bf16[512,2048]{1,0:T(8,128)(2,1)}, u32[]{:S(2)}) copy-start(bf16[512,2048]{1,0:T(8,128)(2,1)} %param.14) | copy-start | bytes 6291460
  0.6 9.8 %copy-start.9 = (s32[8]{0:T(128)S(1)}, s32[8]{0:T(128)}, u32[]{:S(2)}) copy-start(s32[8]{0:T(128)} %constant.224.clone) | copy-start | bytes 100
  0.7 21.6 %copy-start.4 = (s32[8]{0:T(128)S(1)}, s32[8]{0:T(128)}, u32[]{:S(2)}) copy-start(s32[8]{0:T(128)} %constant.225.clone) | copy-start | bytes 100
  0.7 26.2 %copy-start.7 = (f32[128,8]{0,1:T(8,128)S(1)}, f32[128,8]{0,1:T(8,128)}, u32[]{:S(2)}) copy-start(f32[128,8]{0,1:T(8,128)} %param.19) | copy-start | bytes 12292
  0.7 26.2 %copy-start.8 = (s32[128,8]{0,1:T(8,128)S(1)}, s32[128,8]{0,1:T(8,128)}, u32[]{:S(2)}) copy-start(s32[128,8]{0,1:T(8,128)} %param.18) | copy-start | bytes 12292
  3.1 33.0 %all-to-all-start = ((bf16[8,128,512]{2,1,0:T(8,128)(2,1)}), bf16[8,128,512]{2,1,0:T(8,128)(2,1)S(1)}, u32[]{:S(2)}, u32[]{:S(2)}) async-start(bf16[8,128,512]{2,1,0:T(8,128)(2,1)} %bitcast.251), calls=%async_computation | async-start | bytes 2097152 | tf_op jit(solution)/shard_map/out_projection/all_to_all | solution.py:121
  38.5 3.4 %copy-start.2 = (f32[8,128,2048]{2,1,0:T(8,128)}, f32[8,128,2048]{2,1,0:T(8,128)S(1)}, u32[]{:S(2)}) copy-start(f32[8,128,2048]{2,1,0:T(8,128)S(1)} %fusion.124) | copy-start | bytes 25165828
  41.9 7.0 %collective-permute-start = (bf16[64,2048]{1,0:T(8,128)(2,1)S(1)}, bf16[64,2048]{1,0:T(8,128)(2,1)S(1)}, u32[]{:S(2)}, u32[]{:S(2)}) collective-permute-start(bf16[64,2048]{1,0:T(8,128)(2,1)S(1)} %get-tuple-element.75), channel_id=1, source_target_pairs={{0,8},{8,16},{16,24},{24,28},{28,20},{20,12},{12,4},{4,0},{1,9},{9... | collective-permute-start | bytes 786440 | tf_op jit(solution)/shard_map/out_projection/ppermute | solution.py:37
  42.0 6.9 %collective-permute-start.1 = (bf16[64,2048]{1,0:T(8,128)(2,1)S(1)}, bf16[64,2048]{1,0:T(8,128)(2,1)S(1)}, u32[]{:S(2)}, u32[]{:S(2)}) collective-permute-start(bf16[64,2048]{1,0:T(8,128)(2,1)S(1)} %get-tuple-element.76), channel_id=1, source_target_pairs={{0,4},{8,0},{16,8},{24,16},{28,24},{20,28},{12,20},{4,12},{1,5},{9... | collective-permute-start | bytes 786440 | tf_op jit(solution)/shard_map/out_projection/ppermute | solution.py:37
  50.3 27.7 %collective-permute-start.2 = (bf16[64,2048]{1,0:T(8,128)(2,1)S(1)}, bf16[64,2048]{1,0:T(8,128)(2,1)S(1)}, u32[]{:S(2)}, u32[]{:S(2)}) collective-permute-start(bf16[64,2048]{1,0:T(8,128)(2,1)S(1)} %get-tuple-element.79), channel_id=1, source_target_pairs={{0,8},{8,16},{16,24},{24,28},{28,20},{20,12},{12,4},{4,0},{1,9},{9... | collective-permute-start | bytes 786440 | tf_op jit(solution)/shard_map/out_projection/ppermute | solution.py:37
  51.8 26.2 %collective-permute-start.3 = (bf16[64,2048]{1,0:T(8,128)(2,1)S(1)}, bf16[64,2048]{1,0:T(8,128)(2,1)S(1)}, u32[]{:S(2)}, u32[]{:S(2)}) collective-permute-start(bf16[64,2048]{1,0:T(8,128)(2,1)S(1)} %get-tuple-element.80), channel_id=1, source_target_pairs={{0,4},{8,0},{16,8},{24,16},{28,24},{20,28},{12,20},{4,12},{1,5},{9... | collective-permute-start | bytes 786440 | tf_op jit(solution)/shard_map/out_projection/ppermute | solution.py:37
  72.8 11.8 %all-to-all-start.1 = ((f32[8,128,2]{1,2,0:T(2,128)}), f32[8,128,2]{1,2,0:T(2,128)S(1)}, u32[]{:S(2)}, u32[]{:S(2)}) async-start(f32[8,128,2]{1,2,0:T(2,128)} %bitcast.2), calls=%async_computation.1 | async-start | bytes 16384 | tf_op jit(solution)/shard_map/out_projection/all_to_all | solution.py:123
  79.3 6.4 %collective-permute-start.4 = (bf16[64,2048]{1,0:T(8,128)(2,1)S(1)}, bf16[64,2048]{1,0:T(8,128)(2,1)S(1)}, u32[]{:S(2)}, u32[]{:S(2)}) collective-permute-start(bf16[64,2048]{1,0:T(8,128)(2,1)S(1)} %get-tuple-element.83), channel_id=1, source_target_pairs={{0,8},{8,16},{16,24},{24,28},{28,20},{20,12},{12,4},{4,0},{1,9},{9... | collective-permute-start | bytes 786440 | tf_op jit(solution)/shard_map/out_projection/ppermute | solution.py:37
  81.4 6.4 %collective-permute-start.5 = (bf16[64,2048]{1,0:T(8,128)(2,1)S(1)}, bf16[64,2048]{1,0:T(8,128)(2,1)S(1)}, u32[]{:S(2)}, u32[]{:S(2)}) collective-permute-start(bf16[64,2048]{1,0:T(8,128)(2,1)S(1)} %get-tuple-element.84), channel_id=1, source_target_pairs={{0,4},{8,0},{16,8},{24,16},{28,24},{20,28},{12,20},{4,12},{1,5},{9... | collective-permute-start | bytes 786440 | tf_op jit(solution)/shard_map/out_projection/ppermute | solution.py:37
  89.1 6.4 %collective-permute-start.6 = (bf16[64,2048]{1,0:T(8,128)(2,1)S(1)}, bf16[64,2048]{1,0:T(8,128)(2,1)S(1)}, u32[]{:S(2)}, u32[]{:S(2)}) collective-permute-start(bf16[64,2048]{1,0:T(8,128)(2,1)S(1)} %get-tuple-element.87), channel_id=1, source_target_pairs={{0,8},{8,16},{16,24},{24,28},{28,20},{20,12},{12,4},{4,0},{1,9},{9... | collective-permute-start | bytes 786440 | tf_op jit(solution)/shard_map/out_projection/ppermute | solution.py:37
  90.6 6.4 %collective-permute-start.7 = (bf16[64,2048]{1,0:T(8,128)(2,1)S(1)}, bf16[64,2048]{1,0:T(8,128)(2,1)S(1)}, u32[]{:S(2)}, u32[]{:S(2)}) collective-permute-start(bf16[64,2048]{1,0:T(8,128)(2,1)S(1)} %get-tuple-element.88), channel_id=1, source_target_pairs={{0,4},{8,0},{16,8},{24,16},{28,24},{20,28},{12,20},{4,12},{1,5},{9... | collective-permute-start | bytes 786440 | tf_op jit(solution)/shard_map/out_projection/ppermute | solution.py:37
  97.0 57.6 %slice-start = ((s8[12582912]{0:T(1024)(128)(4,1)}), s8[4194304]{0:T(1024)(128)(4,1)S(1)}, s32[]{:S(2)}) async-start(s8[12582912]{0:T(1024)(128)(4,1)} %bitcast.261), calls=%async_computation.2 | async-start | bytes 8388608
  98.5 7.0 %collective-permute-start.8 = (bf16[64,2048]{1,0:T(8,128)(2,1)S(1)}, bf16[64,2048]{1,0:T(8,128)(2,1)S(1)}, u32[]{:S(2)}, u32[]{:S(2)}) collective-permute-start(bf16[64,2048]{1,0:T(8,128)(2,1)S(1)} %get-tuple-element.91), channel_id=1, source_target_pairs={{0,8},{8,16},{16,24},{24,28},{28,20},{20,12},{12,4},{4,0},{1,9},{9... | collective-permute-start | bytes 786440 | tf_op jit(solution)/shard_map/out_projection/ppermute | solution.py:37
  100.0 7.3 %collective-permute-start.9 = (bf16[64,2048]{1,0:T(8,128)(2,1)S(1)}, bf16[64,2048]{1,0:T(8,128)(2,1)S(1)}, u32[]{:S(2)}, u32[]{:S(2)}) collective-permute-start(bf16[64,2048]{1,0:T(8,128)(2,1)S(1)} %get-tuple-element.92), channel_id=1, source_target_pairs={{0,4},{8,0},{16,8},{24,16},{28,24},{20,28},{12,20},{4,12},{1,5},{9... | collective-permute-start | bytes 786440 | tf_op jit(solution)/shard_map/out_projection/ppermute | solution.py:37
  108.6 9.2 %collective-permute-start.10 = (bf16[64,2048]{1,0:T(8,128)(2,1)S(1)}, bf16[64,2048]{1,0:T(8,128)(2,1)S(1)}, u32[]{:S(2)}, u32[]{:S(2)}) collective-permute-start(bf16[64,2048]{1,0:T(8,128)(2,1)S(1)} %get-tuple-element.95), channel_id=1, source_target_pairs={{0,8},{8,16},{16,24},{24,28},{28,20},{20,12},{12,4},{4,0},{1,9},{9... | collective-permute-start | bytes 786440 | tf_op jit(solution)/shard_map/out_projection/ppermute | solution.py:37
  111.1 8.8 %collective-permute-start.11 = (bf16[64,2048]{1,0:T(8,128)(2,1)S(1)}, bf16[64,2048]{1,0:T(8,128)(2,1)S(1)}, u32[]{:S(2)}, u32[]{:S(2)}) collective-permute-start(bf16[64,2048]{1,0:T(8,128)(2,1)S(1)} %get-tuple-element.96), channel_id=1, source_target_pairs={{0,4},{8,0},{16,8},{24,16},{28,24},{20,28},{12,20},{4,12},{1,5},{9... | collective-permute-start | bytes 786440 | tf_op jit(solution)/shard_map/out_projection/ppermute | solution.py:37
  111.3 20.3 %copy-start.3 = (bf16[128,2048]{1,0:T(8,128)(2,1)S(1)}, bf16[128,2048]{1,0:T(8,128)(2,1)}, u32[]{:S(2)}) copy-start(bf16[128,2048]{1,0:T(8,128)(2,1)} %param.12) | copy-start | bytes 1572868
  121.3 9.0 %collective-permute-start.12 = (bf16[64,2048]{1,0:T(8,128)(2,1)S(1)}, bf16[64,2048]{1,0:T(8,128)(2,1)S(1)}, u32[]{:S(2)}, u32[]{:S(2)}) collective-permute-start(bf16[64,2048]{1,0:T(8,128)(2,1)S(1)} %get-tuple-element.99), channel_id=1, source_target_pairs={{0,8},{8,16},{16,24},{24,28},{28,20},{20,12},{12,4},{4,0},{1,9},{9... | collective-permute-start | bytes 786440 | tf_op jit(solution)/shard_map/out_projection/ppermute | solution.py:37
  121.9 8.4 %collective-permute-start.13 = (bf16[64,2048]{1,0:T(8,128)(2,1)S(1)}, bf16[64,2048]{1,0:T(8,128)(2,1)S(1)}, u32[]{:S(2)}, u32[]{:S(2)}) collective-permute-start(bf16[64,2048]{1,0:T(8,128)(2,1)S(1)} %get-tuple-element.100), channel_id=1, source_target_pairs={{0,4},{8,0},{16,8},{24,16},{28,24},{20,28},{12,20},{4,12},{1,5},{9... | collective-permute-start | bytes 786440 | tf_op jit(solution)/shard_map/out_projection/ppermute | solution.py:37
  123.5 8.4 %copy-start.5 = (f32[2048]{0:T(1024)S(1)}, f32[2048]{0:T(1024)}, u32[]{:S(2)}) copy-start(f32[2048]{0:T(1024)} %param.15) | copy-start | bytes 24580
  131.6 22.9 %slice-start.1 = ((s8[12582912]{0:T(1024)(128)(4,1)}), s8[4194304]{0:T(1024)(128)(4,1)S(1)}, s32[]{:S(2)}) async-start(s8[12582912]{0:T(1024)(128)(4,1)} %bitcast.261), calls=%async_computation.3 | async-start | bytes 8388608
  132.1 6.7 %collective-permute-start.15 = (bf16[64,2048]{1,0:T(8,128)(2,1)S(1)}, bf16[64,2048]{1,0:T(8,128)(2,1)S(1)}, u32[]{:S(2)}, u32[]{:S(2)}) collective-permute-start(bf16[64,2048]{1,0:T(8,128)(2,1)S(1)} %get-tuple-element.182), channel_id=1, source_target_pairs={{0,4},{8,0},{16,8},{24,16},{28,24},{20,28},{12,20},{4,12},{1,5},{9... | collective-permute-start | bytes 786440 | tf_op jit(solution)/shard_map/dispatch_gather/ppermute | solution.py:55
  132.5 6.4 %collective-permute-start.14 = (bf16[64,2048]{1,0:T(8,128)(2,1)S(1)}, bf16[64,2048]{1,0:T(8,128)(2,1)S(1)}, u32[]{:S(2)}, u32[]{:S(2)}) collective-permute-start(bf16[64,2048]{1,0:T(8,128)(2,1)S(1)} %get-tuple-element.183), channel_id=1, source_target_pairs={{0,8},{8,16},{16,24},{24,28},{28,20},{20,12},{12,4},{4,0},{1,9},{9... | collective-permute-start | bytes 786440 | tf_op jit(solution)/shard_map/dispatch_gather/ppermute | solution.py:55
  138.9 6.4 %collective-permute-start.16 = (bf16[64,2048]{1,0:T(8,128)(2,1)S(1)}, bf16[64,2048]{1,0:T(8,128)(2,1)S(1)}, u32[]{:S(2)}, u32[]{:S(2)}) collective-permute-start(bf16[64,2048]{1,0:T(8,128)(2,1)S(1)} %collective-permute-done.14), channel_id=1, source_target_pairs={{0,8},{8,16},{16,24},{24,28},{28,20},{20,12},{12,4},{4,0},{1,9},{9... | collective-permute-start | bytes 786440 | tf_op jit(solution)/shard_map/dispatch_gather/ppermute | solution.py:55
  141.3 6.4 %collective-permute-start.17 = (bf16[64,2048]{1,0:T(8,128)(2,1)S(1)}, bf16[64,2048]{1,0:T(8,128)(2,1)S(1)}, u32[]{:S(2)}, u32[]{:S(2)}) collective-permute-start(bf16[64,2048]{1,0:T(8,128)(2,1)S(1)} %collective-permute-done.15), channel_id=1, source_target_pairs={{0,4},{8,0},{16,8},{24,16},{28,24},{20,28},{12,20},{4,12},{1,5},{9... | collective-permute-start | bytes 786440 | tf_op jit(solution)/shard_map/dispatch_gather/ppermute | solution.py:55
  147.7 13.0 %collective-permute-start.18 = (bf16[64,2048]{1,0:T(8,128)(2,1)S(1)}, bf16[64,2048]{1,0:T(8,128)(2,1)S(1)}, u32[]{:S(2)}, u32[]{:S(2)}) collective-permute-start(bf16[64,2048]{1,0:T(8,128)(2,1)S(1)} %collective-permute-done.16), channel_id=1, source_target_pairs={{0,8},{8,16},{16,24},{24,28},{28,20},{20,12},{12,4},{4,0},{1,9},{9... | collective-permute-start | bytes 786440 | tf_op jit(solution)/shard_map/dispatch_gather/ppermute | solution.py:55
  147.7 13.0 %collective-permute-start.19 = (bf16[64,2048]{1,0:T(8,128)(2,1)S(1)}, bf16[64,2048]{1,0:T(8,128)(2,1)S(1)}, u32[]{:S(2)}, u32[]{:S(2)}) collective-permute-start(bf16[64,2048]{1,0:T(8,128)(2,1)S(1)} %collective-permute-done.17), channel_id=1, source_target_pairs={{0,4},{8,0},{16,8},{24,16},{28,24},{20,28},{12,20},{4,12},{1,5},{9... | collective-permute-start | bytes 786440 | tf_op jit(solution)/shard_map/dispatch_gather/ppermute | solution.py:55
  149.8 4.8 %slice-start.2 = ((s8[12582912]{0:T(1024)(128)(4,1)}), s8[4194304]{0:T(1024)(128)(4,1)S(1)}, s32[]{:S(2)}) async-start(s8[12582912]{0:T(1024)(128)(4,1)} %bitcast.261), calls=%async_computation.4 | async-start | bytes 8388608
  149.8 6.6 %slice-start.3 = ((s8[6291456]{0:T(1024)(128)(4,1)}), s8[4194304]{0:T(1024)(128)(4,1)S(1)}, s32[]{:S(2)}) async-start(s8[6291456]{0:T(1024)(128)(4,1)} %bitcast.263), calls=%async_computation.5 | async-start | bytes 8388608
  154.6 1.8 slice-start.4
  158.5 8.0 %collective-permute-start.28 = (bf16[64,2048]{1,0:T(8,128)(2,1)S(1)}, bf16[64,2048]{1,0:T(8,128)(2,1)S(1)}, u32[]{:S(2)}, u32[]{:S(2)}) collective-permute-start(bf16[64,2048]{1,0:T(8,128)(2,1)S(1)} %get-tuple-element.118), channel_id=1, source_target_pairs={{0,8},{8,16},{16,24},{24,28},{28,20},{20,12},{12,4},{4,0},{1,9},{9... | collective-permute-start | bytes 786440 | tf_op jit(solution)/shard_map/combine_return/ppermute | solution.py:75
  158.6 8.1 %collective-permute-start.29 = (bf16[64,2048]{1,0:T(8,128)(2,1)S(1)}, bf16[64,2048]{1,0:T(8,128)(2,1)S(1)}, u32[]{:S(2)}, u32[]{:S(2)}) collective-permute-start(bf16[64,2048]{1,0:T(8,128)(2,1)S(1)} %get-tuple-element.119), channel_id=1, source_target_pairs={{0,4},{8,0},{16,8},{24,16},{28,24},{20,28},{12,20},{4,12},{1,5},{9... | collective-permute-start | bytes 786440 | tf_op jit(solution)/shard_map/combine_return/ppermute | solution.py:75
  160.7 10.0 %collective-permute-start.20 = (bf16[64,2048]{1,0:T(8,128)(2,1)S(1)}, bf16[64,2048]{1,0:T(8,128)(2,1)S(1)}, u32[]{:S(2)}, u32[]{:S(2)}) collective-permute-start(bf16[64,2048]{1,0:T(8,128)(2,1)S(1)} %collective-permute-done.18), channel_id=1, source_target_pairs={{0,8},{8,16},{16,24},{24,28},{28,20},{20,12},{12,4},{4,0},{1,9},{9... | collective-permute-start | bytes 786440 | tf_op jit(solution)/shard_map/dispatch_gather/ppermute | solution.py:55
  160.8 9.9 %collective-permute-start.21 = (bf16[64,2048]{1,0:T(8,128)(2,1)S(1)}, bf16[64,2048]{1,0:T(8,128)(2,1)S(1)}, u32[]{:S(2)}, u32[]{:S(2)}) collective-permute-start(bf16[64,2048]{1,0:T(8,128)(2,1)S(1)} %collective-permute-done.19), channel_id=1, source_target_pairs={{0,4},{8,0},{16,8},{24,16},{28,24},{20,28},{12,20},{4,12},{1,5},{9... | collective-permute-start | bytes 786440 | tf_op jit(solution)/shard_map/dispatch_gather/ppermute | solution.py:55
  166.9 9.5 %collective-permute-start.30 = (bf16[64,2048]{1,0:T(8,128)(2,1)S(1)}, bf16[64,2048]{1,0:T(8,128)(2,1)S(1)}, u32[]{:S(2)}, u32[]{:S(2)}) collective-permute-start(bf16[64,2048]{1,0:T(8,128)(2,1)S(1)} %get-tuple-element.122), channel_id=1, source_target_pairs={{0,8},{8,16},{16,24},{24,28},{28,20},{20,12},{12,4},{4,0},{1,9},{9... | collective-permute-start | bytes 786440 | tf_op jit(solution)/shard_map/combine_return/ppermute | solution.py:75
  167.4 9.2 %collective-permute-start.31 = (bf16[64,2048]{1,0:T(8,128)(2,1)S(1)}, bf16[64,2048]{1,0:T(8,128)(2,1)S(1)}, u32[]{:S(2)}, u32[]{:S(2)}) collective-permute-start(bf16[64,2048]{1,0:T(8,128)(2,1)S(1)} %get-tuple-element.123), channel_id=1, source_target_pairs={{0,4},{8,0},{16,8},{24,16},{28,24},{20,28},{12,20},{4,12},{1,5},{9... | collective-permute-start | bytes 786440 | tf_op jit(solution)/shard_map/combine_return/ppermute | solution.py:75
  170.7 11.2 %collective-permute-start.22 = (bf16[64,2048]{1,0:T(8,128)(2,1)S(1)}, bf16[64,2048]{1,0:T(8,128)(2,1)S(1)}, u32[]{:S(2)}, u32[]{:S(2)}) collective-permute-start(bf16[64,2048]{1,0:T(8,128)(2,1)S(1)} %collective-permute-done.20), channel_id=1, source_target_pairs={{0,8},{8,16},{16,24},{24,28},{28,20},{20,12},{12,4},{4,0},{1,9},{9... | collective-permute-start | bytes 786440 | tf_op jit(solution)/shard_map/dispatch_gather/ppermute | solution.py:55
  171.1 11.2 %collective-permute-start.23 = (bf16[64,2048]{1,0:T(8,128)(2,1)S(1)}, bf16[64,2048]{1,0:T(8,128)(2,1)S(1)}, u32[]{:S(2)}, u32[]{:S(2)}) collective-permute-start(bf16[64,2048]{1,0:T(8,128)(2,1)S(1)} %collective-permute-done.21), channel_id=1, source_target_pairs={{0,4},{8,0},{16,8},{24,16},{28,24},{20,28},{12,20},{4,12},{1,5},{9... | collective-permute-start | bytes 786440 | tf_op jit(solution)/shard_map/dispatch_gather/ppermute | solution.py:55
  178.9 9.3 %collective-permute-start.32 = (bf16[64,2048]{1,0:T(8,128)(2,1)S(1)}, bf16[64,2048]{1,0:T(8,128)(2,1)S(1)}, u32[]{:S(2)}, u32[]{:S(2)}) collective-permute-start(bf16[64,2048]{1,0:T(8,128)(2,1)S(1)} %get-tuple-element.126), channel_id=1, source_target_pairs={{0,8},{8,16},{16,24},{24,28},{28,20},{20,12},{12,4},{4,0},{1,9},{9... | collective-permute-start | bytes 786440 | tf_op jit(solution)/shard_map/combine_return/ppermute | solution.py:75
  180.6 8.6 %collective-permute-start.33 = (bf16[64,2048]{1,0:T(8,128)(2,1)S(1)}, bf16[64,2048]{1,0:T(8,128)(2,1)S(1)}, u32[]{:S(2)}, u32[]{:S(2)}) collective-permute-start(bf16[64,2048]{1,0:T(8,128)(2,1)S(1)} %get-tuple-element.127), channel_id=1, source_target_pairs={{0,4},{8,0},{16,8},{24,16},{28,24},{20,28},{12,20},{4,12},{1,5},{9... | collective-permute-start | bytes 786440 | tf_op jit(solution)/shard_map/combine_return/ppermute | solution.py:75
  182.3 11.5 %collective-permute-start.24 = (bf16[64,2048]{1,0:T(8,128)(2,1)S(1)}, bf16[64,2048]{1,0:T(8,128)(2,1)S(1)}, u32[]{:S(2)}, u32[]{:S(2)}) collective-permute-start(bf16[64,2048]{1,0:T(8,128)(2,1)S(1)} %collective-permute-done.22), channel_id=1, source_target_pairs={{0,8},{8,16},{16,24},{24,28},{28,20},{20,12},{12,4},{4,0},{1,9},{9... | collective-permute-start | bytes 786440 | tf_op jit(solution)/shard_map/dispatch_gather/ppermute | solution.py:55
  183.9 10.4 %collective-permute-start.25 = (bf16[64,2048]{1,0:T(8,128)(2,1)S(1)}, bf16[64,2048]{1,0:T(8,128)(2,1)S(1)}, u32[]{:S(2)}, u32[]{:S(2)}) collective-permute-start(bf16[64,2048]{1,0:T(8,128)(2,1)S(1)} %collective-permute-done.23), channel_id=1, source_target_pairs={{0,4},{8,0},{16,8},{24,16},{28,24},{20,28},{12,20},{4,12},{1,5},{9... | collective-permute-start | bytes 786440 | tf_op jit(solution)/shard_map/dispatch_gather/ppermute | solution.py:55
  189.3 10.7 %collective-permute-start.34 = (bf16[64,2048]{1,0:T(8,128)(2,1)S(1)}, bf16[64,2048]{1,0:T(8,128)(2,1)S(1)}, u32[]{:S(2)}, u32[]{:S(2)}) collective-permute-start(bf16[64,2048]{1,0:T(8,128)(2,1)S(1)} %get-tuple-element.130), channel_id=1, source_target_pairs={{0,8},{8,16},{16,24},{24,28},{28,20},{20,12},{12,4},{4,0},{1,9},{9... | collective-permute-start | bytes 786440 | tf_op jit(solution)/shard_map/combine_return/ppermute | solution.py:75
  189.9 10.1 %collective-permute-start.35 = (bf16[64,2048]{1,0:T(8,128)(2,1)S(1)}, bf16[64,2048]{1,0:T(8,128)(2,1)S(1)}, u32[]{:S(2)}, u32[]{:S(2)}) collective-permute-start(bf16[64,2048]{1,0:T(8,128)(2,1)S(1)} %get-tuple-element.131), channel_id=1, source_target_pairs={{0,4},{8,0},{16,8},{24,16},{28,24},{20,28},{12,20},{4,12},{1,5},{9... | collective-permute-start | bytes 786440 | tf_op jit(solution)/shard_map/combine_return/ppermute | solution.py:75
  194.3 10.0 %collective-permute-start.26 = (bf16[64,2048]{1,0:T(8,128)(2,1)S(1)}, bf16[64,2048]{1,0:T(8,128)(2,1)S(1)}, u32[]{:S(2)}, u32[]{:S(2)}) collective-permute-start(bf16[64,2048]{1,0:T(8,128)(2,1)S(1)} %collective-permute-done.24), channel_id=1, source_target_pairs={{0,8},{8,16},{16,24},{24,28},{28,20},{20,12},{12,4},{4,0},{1,9},{9... | collective-permute-start | bytes 786440 | tf_op jit(solution)/shard_map/dispatch_gather/ppermute | solution.py:55
  194.6 9.7 %collective-permute-start.27 = (bf16[64,2048]{1,0:T(8,128)(2,1)S(1)}, bf16[64,2048]{1,0:T(8,128)(2,1)S(1)}, u32[]{:S(2)}, u32[]{:S(2)}) collective-permute-start(bf16[64,2048]{1,0:T(8,128)(2,1)S(1)} %collective-permute-done.25), channel_id=1, source_target_pairs={{0,4},{8,0},{16,8},{24,16},{28,24},{20,28},{12,20},{4,12},{1,5},{9... | collective-permute-start | bytes 786440 | tf_op jit(solution)/shard_map/dispatch_gather/ppermute | solution.py:55
  202.2 8.8 %collective-permute-start.36 = (bf16[64,2048]{1,0:T(8,128)(2,1)S(1)}, bf16[64,2048]{1,0:T(8,128)(2,1)S(1)}, u32[]{:S(2)}, u32[]{:S(2)}) collective-permute-start(bf16[64,2048]{1,0:T(8,128)(2,1)S(1)} %get-tuple-element.134), channel_id=1, source_target_pairs={{0,8},{8,16},{16,24},{24,28},{28,20},{20,12},{12,4},{4,0},{1,9},{9... | collective-permute-start | bytes 786440 | tf_op jit(solution)/shard_map/combine_return/ppermute | solution.py:75
  202.5 8.4 %collective-permute-start.37 = (bf16[64,2048]{1,0:T(8,128)(2,1)S(1)}, bf16[64,2048]{1,0:T(8,128)(2,1)S(1)}, u32[]{:S(2)}, u32[]{:S(2)}) collective-permute-start(bf16[64,2048]{1,0:T(8,128)(2,1)S(1)} %get-tuple-element.135), channel_id=1, source_target_pairs={{0,4},{8,0},{16,8},{24,16},{28,24},{20,28},{12,20},{4,12},{1,5},{9... | collective-permute-start | bytes 786440 | tf_op jit(solution)/shard_map/combine_return/ppermute | solution.py:75
  211.1 6.6 %collective-permute-start.38 = (bf16[64,2048]{1,0:T(8,128)(2,1)S(1)}, bf16[64,2048]{1,0:T(8,128)(2,1)S(1)}, u32[]{:S(2)}, u32[]{:S(2)}) collective-permute-start(bf16[64,2048]{1,0:T(8,128)(2,1)S(1)} %get-tuple-element.138), channel_id=1, source_target_pairs={{0,8},{8,16},{16,24},{24,28},{28,20},{20,12},{12,4},{4,0},{1,9},{9... | collective-permute-start | bytes 786440 | tf_op jit(solution)/shard_map/combine_return/ppermute | solution.py:75
  211.2 6.6 %collective-permute-start.39 = (bf16[64,2048]{1,0:T(8,128)(2,1)S(1)}, bf16[64,2048]{1,0:T(8,128)(2,1)S(1)}, u32[]{:S(2)}, u32[]{:S(2)}) collective-permute-start(bf16[64,2048]{1,0:T(8,128)(2,1)S(1)} %get-tuple-element.139), channel_id=1, source_target_pairs={{0,4},{8,0},{16,8},{24,16},{28,24},{20,28},{12,20},{4,12},{1,5},{9... | collective-permute-start | bytes 786440 | tf_op jit(solution)/shard_map/combine_return/ppermute | solution.py:75
  217.9 9.5 %copy-start.6 = (f32[2048]{0:T(1024)S(1)}, f32[2048]{0:T(1024)}, u32[]{:S(2)}) copy-start(f32[2048]{0:T(1024)} %param.20) | copy-start | bytes 24580
  217.9 6.6 %collective-permute-start.40 = (bf16[64,2048]{1,0:T(8,128)(2,1)S(1)}, bf16[64,2048]{1,0:T(8,128)(2,1)S(1)}, u32[]{:S(2)}, u32[]{:S(2)}) collective-permute-start(bf16[64,2048]{1,0:T(8,128)(2,1)S(1)} %get-tuple-element.142), channel_id=1, source_target_pairs={{0,8},{8,16},{16,24},{24,28},{28,20},{20,12},{12,4},{4,0},{1,9},{9... | collective-permute-start | bytes 786440 | tf_op jit(solution)/shard_map/combine_return/ppermute | solution.py:75
  218.9 8.1 %collective-permute-start.41 = (bf16[64,2048]{1,0:T(8,128)(2,1)S(1)}, bf16[64,2048]{1,0:T(8,128)(2,1)S(1)}, u32[]{:S(2)}, u32[]{:S(2)}) collective-permute-start(bf16[64,2048]{1,0:T(8,128)(2,1)S(1)} %get-tuple-element.143), channel_id=1, source_target_pairs={{0,4},{8,0},{16,8},{24,16},{28,24},{20,28},{12,20},{4,12},{1,5},{9... | collective-permute-start | bytes 786440 | tf_op jit(solution)/shard_map/combine_return/ppermute | solution.py:75
  227.2 2.0 copy-start.1

commit v12 on v11

--- a/solution.py
+++ b/solution.py
@@ -118,9 +118,13 @@
 
     with jax.named_scope("out_projection"):
         columns = attn_out.reshape(row_count, ep_size, slice_width).transpose(1, 0, 2)
-        columns = lax.all_to_all(columns, "ep", split_axis=0, concat_axis=0, tiled=True)
         columns, dense_weight = lax.optimization_barrier((columns, dense_weight))
-        row_weights = lax.all_to_all(dense_weight, "ep", split_axis=0, concat_axis=0, tiled=True)
+        columns, row_weights = lax.optimization_barrier(
+            (
+                lax.all_to_all(columns, "ep", split_axis=0, concat_axis=0, tiled=True),
+                lax.all_to_all(dense_weight, "ep", split_axis=0, concat_axis=0, tiled=True),
+            )
+        )
         row_weights = row_weights.reshape(group_rows, local_experts)
         partial = jnp.dot(
             columns.reshape(group_rows, slice_width), out_weight, preferred_element_type=jnp.float32

time: 230 us -> 233 us (1.013)
  blocking collectives: 0 us -> 13.6 us
  starting transfers between devices: 57.3 us -> 47.9 us
    all_to_all x0 -> x1, blocking collectives: none -> 13.6 us  [body(): lax.all_to_all(dense_weight, 'ep', split_axis=0, concat_axis=0, tiled=True)]
    all_to_all x1 -> x0, starting transfers between devices: 5.17 us -> none  [body(): lax.all_to_all(dense_weight, 'ep', split_axis=0, concat_axis=0, tiled=True)]
    all_to_all x1, starting transfers between devices: 7.28 us -> 3.56 us  [body(): lax.all_to_all(columns, 'ep', split_axis=0, concat_axis=0, tiled=True)]
    all_to_all x1 -> x0, waiting for transfers between devices: 3.18 us -> none  [body(): lax.all_to_all(dense_weight, 'ep', split_axis=0, concat_axis=0, tiled=True)]
    ppermute x7, starting transfers between devices: 4.29 us -> 6.99 us  [ring_reduce_scatter_steps(): lax.ppermute(send_fwd, 'ep', forward)]
    ppermute x7, starting transfers between devices: 9.89 us -> 7.38 us  [ring_reduce_scatter(): lax.ppermute(send_fwd, 'ep', forward)]
    ppermute x7, starting transfers between devices: 10.9 us -> 8.46 us  [ring_reduce_scatter_steps(): lax.ppermute(send_bwd, 'ep', backward)]
  transfers between devices with their start and end apart: 44 -> 43, of which waited for: 31 -> 30; matrix products, arithmetic and copies ran while one was open for 13% -> 12% of each run, Pallas kernels for 0% -> 0%
where the time goes in v12:
time: 233 us; the launch traced here: 232 us
  waiting for transfers between devices  80.9 us (35%)
  starting transfers between devices  47.9 us (21%)
  between operations  40.9 us (18%)
  matrix products  28.1 us (12%)
  blocking collectives  13.6 us (6%)
  other arithmetic  12.3 us (5%)
  local copies, waits for them, and re-layouts  8.68 us (4%)
    ppermute x7, waiting for transfers between devices, ring_reduce_scatter(): lax.ppermute(send_fwd, 'ep', forward)  25.7 us
    ppermute x7, waiting for transfers between devices, ring_reduce_scatter_steps(): lax.ppermute(send_fwd, 'ep', forward)  18.2 us
    dot_general x8, matrix products, expert_mix(): projected_up = jnp.dot(rows, gate_up[e], preferred_element_type=jnp.float32)  17.2 us
    all_to_all x1, blocking collectives, body(): lax.all_to_all(dense_weight, 'ep', split_axis=0, concat_axis=0, tiled=True)  13.6 us
    ppermute x7, waiting for transfers between devices, ring_all_gather(): lax.ppermute(got_fwd, 'ep', forward)  9.03 us
    dot_general x8, matrix products, expert_mix(): jnp.dot(activated, down[e], preferred_element_type=jnp.float32)  8.55 us
    ppermute x7, starting transfers between devices, ring_all_gather(): lax.ppermute(got_bwd, 'ep', backward)  8.52 us
    ppermute x7, starting transfers between devices, ring_reduce_scatter_steps(): lax.ppermute(send_bwd, 'ep', backward)  8.46 us
  transfers between devices with their start and end apart: 43, of which 30 were waited for; matrix products, arithmetic and copies ran while one was open for 12% of the time, Pallas kernels for 0%

profile of v12, /device:TPU:0, one launch (start us, length us, event | category | flops | bytes accessed | tf_op | source)
XLA Modules:
  0.0 232.4 jit_solution(13114970389647549617)
XLA Ops:
  0.7 2.4 %copy.20 = bf16[16,8,8,512]{3,2,0,1:T(8,128)(2,1)} copy(bf16[16,8,8,512]{3,2,1,0:T(8,128)(2,1)} %bitcast.252) | data formatting | bytes 2097152 | tf_op jit(solution)/shard_map/out_projection/reshape | solution.py:120
  3.2 13.6 %all_to_all.10 = f32[8,128,2]{1,2,0:T(2,128)S(1)} all-to-all(f32[8,128,2]{1,2,0:T(2,128)S(1)} %bitcast.253), channel_id=1, replica_groups=mesh['ep'=8,'rep'=4] {'ep'}, dimensions={0} | all-to-all | bytes 16384 | tf_op jit(solution)/shard_map/out_projection/all_to_all | solution.py:125
  16.7 3.6 %all-to-all-start = ((bf16[8,128,512]{2,1,0:T(8,128)(2,1)}), bf16[8,128,512]{2,1,0:T(8,128)(2,1)S(1)}, u32[]{:S(2)}, u32[]{:S(2)}) async-start(bf16[8,128,512]{2,1,0:T(8,128)(2,1)} %bitcast.251), calls=%async_computation | async-start | bytes 2097152 | tf_op jit(solution)/shard_map/out_projection/all_to_all | solution.py:124
  36.9 8.1 %all-to-all-done = bf16[8,128,512]{2,1,0:T(8,128)(2,1)S(1)} async-done(((bf16[8,128,512]{2,1,0:T(8,128)(2,1)}), bf16[8,128,512]{2,1,0:T(8,128)(2,1)S(1)}, u32[]{:S(2)}, u32[]{:S(2)}) %all-to-all-start) | async-done | bytes 1048608 | tf_op jit(solution)/shard_map/out_projection/all_to_all | solution.py:124
  45.0 2.3 %fusion.124 = f32[8,128,2048]{2,1,0:T(8,128)S(1)} fusion(bf16[8,128,512]{2,1,0:T(8,128)(2,1)S(1)} %all-to-all-done, bf16[512,2048]{1,0:T(8,128)(2,1)S(1)} %copy-done), kind=kOutput, calls=%fused_computation.68 | convolution fusion | flops 2147483648 | bytes 11534336 | tf_op jit(solution)/shard_map/out_projection/dot_general | solution.py:129
  47.4 3.4 %copy-done.2 = f32[8,128,2048]{2,1,0:T(8,128)} copy-done((f32[8,128,2048]{2,1,0:T(8,128)}, f32[8,128,2048]{2,1,0:T(8,128)S(1)}, u32[]{:S(2)}) %copy-start.2) | copy-done | bytes 8388632
  50.9 2.0 collective-permute-start.1
  57.5 1.3 fusion.170
  59.4 1.5 collective-permute-start.3
  81.5 1.3 fusion.168
  82.8 1.5 collective-permute-start.4
  85.0 4.3 %collective-permute-done.4 = bf16[64,2048]{1,0:T(8,128)(2,1)S(1)} collective-permute-done((bf16[64,2048]{1,0:T(8,128)(2,1)S(1)}, bf16[64,2048]{1,0:T(8,128)(2,1)S(1)}, u32[]{:S(2)}, u32[]{:S(2)}) %collective-permute-start.4) | collective-permute-done | bytes 262176 | tf_op jit(solution)/shard_map/out_projection/ppermute | solution.py:37
  89.2 1.6 collective-permute-done.5
  90.8 1.3 fusion.166
  92.1 2.0 collective-permute-start.6
  94.3 4.2 %collective-permute-done.6 = bf16[64,2048]{1,0:T(8,128)(2,1)S(1)} collective-permute-done((bf16[64,2048]{1,0:T(8,128)(2,1)S(1)}, bf16[64,2048]{1,0:T(8,128)(2,1)S(1)}, u32[]{:S(2)}, u32[]{:S(2)}) %collective-permute-start.6) | collective-permute-done | bytes 262176 | tf_op jit(solution)/shard_map/out_projection/ppermute | solution.py:37
  98.5 1.9 collective-permute-done.7
  100.4 1.5 fusion.164
  101.9 1.8 collective-permute-start.8
  104.0 4.4 %collective-permute-done.8 = bf16[64,2048]{1,0:T(8,128)(2,1)S(1)} collective-permute-done((bf16[64,2048]{1,0:T(8,128)(2,1)S(1)}, bf16[64,2048]{1,0:T(8,128)(2,1)S(1)}, u32[]{:S(2)}, u32[]{:S(2)}) %collective-permute-start.8) | collective-permute-done | bytes 262176 | tf_op jit(solution)/shard_map/out_projection/ppermute | solution.py:37
  108.5 2.8 %collective-permute-done.9 = bf16[64,2048]{1,0:T(8,128)(2,1)S(1)} collective-permute-done((bf16[64,2048]{1,0:T(8,128)(2,1)S(1)}, bf16[64,2048]{1,0:T(8,128)(2,1)S(1)}, u32[]{:S(2)}, u32[]{:S(2)}) %collective-permute-start.9) | collective-permute-done | bytes 262176 | tf_op jit(solution)/shard_map/out_projection/ppermute | solution.py:37
  111.2 1.3 fusion.162
  112.8 1.8 collective-permute-start.11
  114.8 6.6 %collective-permute-done.10 = bf16[64,2048]{1,0:T(8,128)(2,1)S(1)} collective-permute-done((bf16[64,2048]{1,0:T(8,128)(2,1)S(1)}, bf16[64,2048]{1,0:T(8,128)(2,1)S(1)}, u32[]{:S(2)}, u32[]{:S(2)}) %collective-permute-start.10) | collective-permute-done | bytes 262176 | tf_op jit(solution)/shard_map/out_projection/ppermute | solution.py:37
  121.5 1.3 fusion.160
  122.9 1.2 collective-permute-start.12
  125.2 5.5 %collective-permute-done.12 = bf16[64,2048]{1,0:T(8,128)(2,1)S(1)} collective-permute-done((bf16[64,2048]{1,0:T(8,128)(2,1)S(1)}, bf16[64,2048]{1,0:T(8,128)(2,1)S(1)}, u32[]{:S(2)}, u32[]{:S(2)}) %collective-permute-start.12) | collective-permute-done | bytes 262176 | tf_op jit(solution)/shard_map/out_projection/ppermute | solution.py:37
  130.7 1.2 collective-permute-done.13
  131.9 1.3 fusion.183
  133.8 2.0 collective-permute-start.15
  135.9 5.1 %collective-permute-done.15 = bf16[64,2048]{1,0:T(8,128)(2,1)S(1)} collective-permute-done((bf16[64,2048]{1,0:T(8,128)(2,1)S(1)}, bf16[64,2048]{1,0:T(8,128)(2,1)S(1)}, u32[]{:S(2)}, u32[]{:S(2)}) %collective-permute-start.15) | collective-permute-done | bytes 262176 | tf_op jit(solution)/shard_map/dispatch_gather/ppermute | solution.py:55
  141.0 1.6 collective-permute-done.14
  142.6 2.0 collective-permute-start.17
  144.7 4.3 %collective-permute-done.16 = bf16[64,2048]{1,0:T(8,128)(2,1)S(1)} collective-permute-done((bf16[64,2048]{1,0:T(8,128)(2,1)S(1)}, bf16[64,2048]{1,0:T(8,128)(2,1)S(1)}, u32[]{:S(2)}, u32[]{:S(2)}) %collective-permute-start.16) | collective-permute-done | bytes 262176 | tf_op jit(solution)/shard_map/dispatch_gather/ppermute | solution.py:55
  149.0 1.8 collective-permute-start.18
  151.1 4.7 %fusion = f32[256,1536]{1,0:T(8,128)S(1)} fusion(bf16[256,2048]{1,0:T(8,128)(2,1)S(1)} %constant_dynamic-update-slice_fusion.8, bf16[2,2048,1536]{2,1,0:T(8,128)(2,1)} %param.16), kind=kOutput, calls=%fused_computation | convolution fusion | flops 1610612736 | bytes 8912896 | tf_op jit(solution)/shard_map/local_experts/dot_general | solution.py:87
  155.8 1.8 fusion.8
  159.9 1.9 collective-permute-start.28
  162.1 1.8 collective-permute-start.20
  164.1 5.0 %collective-permute-done.28 = bf16[64,2048]{1,0:T(8,128)(2,1)S(1)} collective-permute-done((bf16[64,2048]{1,0:T(8,128)(2,1)S(1)}, bf16[64,2048]{1,0:T(8,128)(2,1)S(1)}, u32[]{:S(2)}, u32[]{:S(2)}) %collective-permute-start.28) | collective-permute-done | bytes 262176 | tf_op jit(solution)/shard_map/combine_return/ppermute | solution.py:75
  169.2 1.3 collective-permute-done.29
  171.0 1.7 collective-permute-start.31
  173.3 1.2 collective-permute-done.21
  174.8 1.7 collective-permute-start.23
  176.6 1.8 fusion.2
  178.3 1.8 fusion.10
  182.5 1.6 collective-permute-start.32
  185.9 1.5 collective-permute-start.24
  187.9 3.9 %collective-permute-done.32 = bf16[64,2048]{1,0:T(8,128)(2,1)S(1)} collective-permute-done((bf16[64,2048]{1,0:T(8,128)(2,1)S(1)}, bf16[64,2048]{1,0:T(8,128)(2,1)S(1)}, u32[]{:S(2)}, u32[]{:S(2)}) %collective-permute-start.32) | collective-permute-done | bytes 262176 | tf_op jit(solution)/shard_map/combine_return/ppermute | solution.py:75
  193.4 1.7 collective-permute-start.35
  195.1 1.7 collective-permute-done.24
  198.2 1.7 collective-permute-start.27
  200.0 1.8 fusion.4
  201.8 1.8 fusion.12
  206.2 1.7 collective-permute-start.37
  208.0 1.8 fusion.6
  209.8 1.8 fusion.14
  211.6 3.0 %collective-permute-done.36 = bf16[64,2048]{1,0:T(8,128)(2,1)S(1)} collective-permute-done((bf16[64,2048]{1,0:T(8,128)(2,1)S(1)}, bf16[64,2048]{1,0:T(8,128)(2,1)S(1)}, u32[]{:S(2)}, u32[]{:S(2)}) %collective-permute-start.36) | collective-permute-done | bytes 262176 | tf_op jit(solution)/shard_map/combine_return/ppermute | solution.py:75
  214.8 2.5 %collective-permute-start.39 = (bf16[64,2048]{1,0:T(8,128)(2,1)S(1)}, bf16[64,2048]{1,0:T(8,128)(2,1)S(1)}, u32[]{:S(2)}, u32[]{:S(2)}) collective-permute-start(bf16[64,2048]{1,0:T(8,128)(2,1)S(1)} %get-tuple-element.143), channel_id=1, source_target_pairs={{0,4},{8,0},{16,8},{24,16},{28,24},{20,28},{12,20},{4,12},{1,5},{9... | collective-permute-start | bytes 786440 | tf_op jit(solution)/shard_map/combine_return/ppermute | solution.py:75
  219.4 1.9 collective-permute-done.38
  221.6 2.3 %collective-permute-start.40 = (bf16[64,2048]{1,0:T(8,128)(2,1)S(1)}, bf16[64,2048]{1,0:T(8,128)(2,1)S(1)}, u32[]{:S(2)}, u32[]{:S(2)}) collective-permute-start(bf16[64,2048]{1,0:T(8,128)(2,1)S(1)} %get-tuple-element.146), channel_id=1, source_target_pairs={{0,8},{8,16},{16,24},{24,28},{28,20},{20,12},{12,4},{4,0},{1,9},{9... | collective-permute-start | bytes 786440 | tf_op jit(solution)/shard_map/combine_return/ppermute | solution.py:75
  223.9 4.3 %collective-permute-done.40 = bf16[64,2048]{1,0:T(8,128)(2,1)S(1)} collective-permute-done((bf16[64,2048]{1,0:T(8,128)(2,1)S(1)}, bf16[64,2048]{1,0:T(8,128)(2,1)S(1)}, u32[]{:S(2)}, u32[]{:S(2)}) %collective-permute-start.40) | collective-permute-done | bytes 262176 | tf_op jit(solution)/shard_map/combine_return/ppermute | solution.py:75
  228.2 2.0 collective-permute-done.41
  230.7 1.2 multiply_convert_fusion
  (127 shorter events, 24.8 us)
Async XLA Ops:
  0.6 44.4 %copy-start = (bf16[512,2048]{1,0:T(8,128)(2,1)S(1)}, bf16[512,2048]{1,0:T(8,128)(2,1)}, u32[]{:S(2)}) copy-start(bf16[512,2048]{1,0:T(8,128)(2,1)} %param.14) | copy-start | bytes 6291460
  0.6 2.5 %copy-start.7 = (f32[128,8]{0,1:T(8,128)S(1)}, f32[128,8]{0,1:T(8,128)}, u32[]{:S(2)}) copy-start(f32[128,8]{0,1:T(8,128)} %param.19) | copy-start | bytes 12292
  0.7 2.5 %copy-start.8 = (s32[128,8]{0,1:T(8,128)S(1)}, s32[128,8]{0,1:T(8,128)}, u32[]{:S(2)}) copy-start(s32[128,8]{0,1:T(8,128)} %param.18) | copy-start | bytes 12292
  0.7 19.6 %copy-start.9 = (s32[8]{0:T(128)S(1)}, s32[8]{0:T(128)}, u32[]{:S(2)}) copy-start(s32[8]{0:T(128)} %constant.224.clone) | copy-start | bytes 100
  0.7 31.5 %copy-start.4 = (s32[8]{0:T(128)S(1)}, s32[8]{0:T(128)}, u32[]{:S(2)}) copy-start(s32[8]{0:T(128)} %constant.225.clone) | copy-start | bytes 100
  16.7 28.3 %all-to-all-start = ((bf16[8,128,512]{2,1,0:T(8,128)(2,1)}), bf16[8,128,512]{2,1,0:T(8,128)(2,1)S(1)}, u32[]{:S(2)}, u32[]{:S(2)}) async-start(bf16[8,128,512]{2,1,0:T(8,128)(2,1)} %bitcast.251), calls=%async_computation | async-start | bytes 2097152 | tf_op jit(solution)/shard_map/out_projection/all_to_all | solution.py:124
  47.4 3.4 %copy-start.2 = (f32[8,128,2048]{2,1,0:T(8,128)}, f32[8,128,2048]{2,1,0:T(8,128)S(1)}, u32[]{:S(2)}) copy-start(f32[8,128,2048]{2,1,0:T(8,128)S(1)} %fusion.124) | copy-start | bytes 25165828
  50.8 6.6 %collective-permute-start = (bf16[64,2048]{1,0:T(8,128)(2,1)S(1)}, bf16[64,2048]{1,0:T(8,128)(2,1)S(1)}, u32[]{:S(2)}, u32[]{:S(2)}) collective-permute-start(bf16[64,2048]{1,0:T(8,128)(2,1)S(1)} %get-tuple-element.79), channel_id=1, source_target_pairs={{0,8},{8,16},{16,24},{24,28},{28,20},{20,12},{12,4},{4,0},{1,9},{9... | collective-permute-start | bytes 786440 | tf_op jit(solution)/shard_map/out_projection/ppermute | solution.py:37
  50.9 6.6 %collective-permute-start.1 = (bf16[64,2048]{1,0:T(8,128)(2,1)S(1)}, bf16[64,2048]{1,0:T(8,128)(2,1)S(1)}, u32[]{:S(2)}, u32[]{:S(2)}) collective-permute-start(bf16[64,2048]{1,0:T(8,128)(2,1)S(1)} %get-tuple-element.80), channel_id=1, source_target_pairs={{0,4},{8,0},{16,8},{24,16},{28,24},{20,28},{12,20},{4,12},{1,5},{9... | collective-permute-start | bytes 786440 | tf_op jit(solution)/shard_map/out_projection/ppermute | solution.py:37
  58.8 22.7 %collective-permute-start.2 = (bf16[64,2048]{1,0:T(8,128)(2,1)S(1)}, bf16[64,2048]{1,0:T(8,128)(2,1)S(1)}, u32[]{:S(2)}, u32[]{:S(2)}) collective-permute-start(bf16[64,2048]{1,0:T(8,128)(2,1)S(1)} %get-tuple-element.83), channel_id=1, source_target_pairs={{0,8},{8,16},{16,24},{24,28},{28,20},{20,12},{12,4},{4,0},{1,9},{9... | collective-permute-start | bytes 786440 | tf_op jit(solution)/shard_map/out_projection/ppermute | solution.py:37
  59.4 22.1 %collective-permute-start.3 = (bf16[64,2048]{1,0:T(8,128)(2,1)S(1)}, bf16[64,2048]{1,0:T(8,128)(2,1)S(1)}, u32[]{:S(2)}, u32[]{:S(2)}) collective-permute-start(bf16[64,2048]{1,0:T(8,128)(2,1)S(1)} %get-tuple-element.84), channel_id=1, source_target_pairs={{0,4},{8,0},{16,8},{24,16},{28,24},{20,28},{12,20},{4,12},{1,5},{9... | collective-permute-start | bytes 786440 | tf_op jit(solution)/shard_map/out_projection/ppermute | solution.py:37
  82.8 6.4 %collective-permute-start.4 = (bf16[64,2048]{1,0:T(8,128)(2,1)S(1)}, bf16[64,2048]{1,0:T(8,128)(2,1)S(1)}, u32[]{:S(2)}, u32[]{:S(2)}) collective-permute-start(bf16[64,2048]{1,0:T(8,128)(2,1)S(1)} %get-tuple-element.87), channel_id=1, source_target_pairs={{0,8},{8,16},{16,24},{24,28},{28,20},{20,12},{12,4},{4,0},{1,9},{9... | collective-permute-start | bytes 786440 | tf_op jit(solution)/shard_map/out_projection/ppermute | solution.py:37
  84.3 6.5 %collective-permute-start.5 = (bf16[64,2048]{1,0:T(8,128)(2,1)S(1)}, bf16[64,2048]{1,0:T(8,128)(2,1)S(1)}, u32[]{:S(2)}, u32[]{:S(2)}) collective-permute-start(bf16[64,2048]{1,0:T(8,128)(2,1)S(1)} %get-tuple-element.88), channel_id=1, source_target_pairs={{0,4},{8,0},{16,8},{24,16},{28,24},{20,28},{12,20},{4,12},{1,5},{9... | collective-permute-start | bytes 786440 | tf_op jit(solution)/shard_map/out_projection/ppermute | solution.py:37
  92.1 6.4 %collective-permute-start.6 = (bf16[64,2048]{1,0:T(8,128)(2,1)S(1)}, bf16[64,2048]{1,0:T(8,128)(2,1)S(1)}, u32[]{:S(2)}, u32[]{:S(2)}) collective-permute-start(bf16[64,2048]{1,0:T(8,128)(2,1)S(1)} %get-tuple-element.91), channel_id=1, source_target_pairs={{0,8},{8,16},{16,24},{24,28},{28,20},{20,12},{12,4},{4,0},{1,9},{9... | collective-permute-start | bytes 786440 | tf_op jit(solution)/shard_map/out_projection/ppermute | solution.py:37
  94.0 6.4 %collective-permute-start.7 = (bf16[64,2048]{1,0:T(8,128)(2,1)S(1)}, bf16[64,2048]{1,0:T(8,128)(2,1)S(1)}, u32[]{:S(2)}, u32[]{:S(2)}) collective-permute-start(bf16[64,2048]{1,0:T(8,128)(2,1)S(1)} %get-tuple-element.92), channel_id=1, source_target_pairs={{0,4},{8,0},{16,8},{24,16},{28,24},{20,28},{12,20},{4,12},{1,5},{9... | collective-permute-start | bytes 786440 | tf_op jit(solution)/shard_map/out_projection/ppermute | solution.py:37
  100.4 55.4 %slice-start = ((s8[12582912]{0:T(1024)(128)(4,1)}), s8[4194304]{0:T(1024)(128)(4,1)S(1)}, s32[]{:S(2)}) async-start(s8[12582912]{0:T(1024)(128)(4,1)} %bitcast.262), calls=%async_computation.2 | async-start | bytes 8388608
  101.9 6.6 %collective-permute-start.8 = (bf16[64,2048]{1,0:T(8,128)(2,1)S(1)}, bf16[64,2048]{1,0:T(8,128)(2,1)S(1)}, u32[]{:S(2)}, u32[]{:S(2)}) collective-permute-start(bf16[64,2048]{1,0:T(8,128)(2,1)S(1)} %get-tuple-element.95), channel_id=1, source_target_pairs={{0,8},{8,16},{16,24},{24,28},{28,20},{20,12},{12,4},{4,0},{1,9},{9... | collective-permute-start | bytes 786440 | tf_op jit(solution)/shard_map/out_projection/ppermute | solution.py:37
  103.7 7.6 %collective-permute-start.9 = (bf16[64,2048]{1,0:T(8,128)(2,1)S(1)}, bf16[64,2048]{1,0:T(8,128)(2,1)S(1)}, u32[]{:S(2)}, u32[]{:S(2)}) collective-permute-start(bf16[64,2048]{1,0:T(8,128)(2,1)S(1)} %get-tuple-element.96), channel_id=1, source_target_pairs={{0,4},{8,0},{16,8},{24,16},{28,24},{20,28},{12,20},{4,12},{1,5},{9... | collective-permute-start | bytes 786440 | tf_op jit(solution)/shard_map/out_projection/ppermute | solution.py:37
  112.5 8.8 %collective-permute-start.10 = (bf16[64,2048]{1,0:T(8,128)(2,1)S(1)}, bf16[64,2048]{1,0:T(8,128)(2,1)S(1)}, u32[]{:S(2)}, u32[]{:S(2)}) collective-permute-start(bf16[64,2048]{1,0:T(8,128)(2,1)S(1)} %get-tuple-element.99), channel_id=1, source_target_pairs={{0,8},{8,16},{16,24},{24,28},{28,20},{20,12},{12,4},{4,0},{1,9},{9... | collective-permute-start | bytes 786440 | tf_op jit(solution)/shard_map/out_projection/ppermute | solution.py:37
  112.8 8.7 %collective-permute-start.11 = (bf16[64,2048]{1,0:T(8,128)(2,1)S(1)}, bf16[64,2048]{1,0:T(8,128)(2,1)S(1)}, u32[]{:S(2)}, u32[]{:S(2)}) collective-permute-start(bf16[64,2048]{1,0:T(8,128)(2,1)S(1)} %get-tuple-element.100), channel_id=1, source_target_pairs={{0,4},{8,0},{16,8},{24,16},{28,24},{20,28},{12,20},{4,12},{1,5},{9... | collective-permute-start | bytes 786440 | tf_op jit(solution)/shard_map/out_projection/ppermute | solution.py:37
  114.8 18.5 %copy-start.3 = (bf16[128,2048]{1,0:T(8,128)(2,1)S(1)}, bf16[128,2048]{1,0:T(8,128)(2,1)}, u32[]{:S(2)}) copy-start(bf16[128,2048]{1,0:T(8,128)(2,1)} %param.12) | copy-start | bytes 1572868
  122.9 7.8 %collective-permute-start.12 = (bf16[64,2048]{1,0:T(8,128)(2,1)S(1)}, bf16[64,2048]{1,0:T(8,128)(2,1)S(1)}, u32[]{:S(2)}, u32[]{:S(2)}) collective-permute-start(bf16[64,2048]{1,0:T(8,128)(2,1)S(1)} %get-tuple-element.103), channel_id=1, source_target_pairs={{0,8},{8,16},{16,24},{24,28},{28,20},{20,12},{12,4},{4,0},{1,9},{9... | collective-permute-start | bytes 786440 | tf_op jit(solution)/shard_map/out_projection/ppermute | solution.py:37
  124.1 7.8 %collective-permute-start.13 = (bf16[64,2048]{1,0:T(8,128)(2,1)S(1)}, bf16[64,2048]{1,0:T(8,128)(2,1)S(1)}, u32[]{:S(2)}, u32[]{:S(2)}) collective-permute-start(bf16[64,2048]{1,0:T(8,128)(2,1)S(1)} %get-tuple-element.104), channel_id=1, source_target_pairs={{0,4},{8,0},{16,8},{24,16},{28,24},{20,28},{12,20},{4,12},{1,5},{9... | collective-permute-start | bytes 786440 | tf_op jit(solution)/shard_map/out_projection/ppermute | solution.py:37
  125.2 8.3 %copy-start.5 = (f32[2048]{0:T(1024)S(1)}, f32[2048]{0:T(1024)}, u32[]{:S(2)}) copy-start(f32[2048]{0:T(1024)} %param.15) | copy-start | bytes 24580
  133.3 22.6 %slice-start.1 = ((s8[12582912]{0:T(1024)(128)(4,1)}), s8[4194304]{0:T(1024)(128)(4,1)S(1)}, s32[]{:S(2)}) async-start(s8[12582912]{0:T(1024)(128)(4,1)} %bitcast.262), calls=%async_computation.3 | async-start | bytes 8388608
  133.8 7.3 %collective-permute-start.15 = (bf16[64,2048]{1,0:T(8,128)(2,1)S(1)}, bf16[64,2048]{1,0:T(8,128)(2,1)S(1)}, u32[]{:S(2)}, u32[]{:S(2)}) collective-permute-start(bf16[64,2048]{1,0:T(8,128)(2,1)S(1)} %get-tuple-element.186), channel_id=1, source_target_pairs={{0,4},{8,0},{16,8},{24,16},{28,24},{20,28},{12,20},{4,12},{1,5},{9... | collective-permute-start | bytes 786440 | tf_op jit(solution)/shard_map/dispatch_gather/ppermute | solution.py:55
  135.8 6.8 %collective-permute-start.14 = (bf16[64,2048]{1,0:T(8,128)(2,1)S(1)}, bf16[64,2048]{1,0:T(8,128)(2,1)S(1)}, u32[]{:S(2)}, u32[]{:S(2)}) collective-permute-start(bf16[64,2048]{1,0:T(8,128)(2,1)S(1)} %get-tuple-element.187), channel_id=1, source_target_pairs={{0,8},{8,16},{16,24},{24,28},{28,20},{20,12},{12,4},{4,0},{1,9},{9... | collective-permute-start | bytes 786440 | tf_op jit(solution)/shard_map/dispatch_gather/ppermute | solution.py:55
  142.6 6.4 %collective-permute-start.16 = (bf16[64,2048]{1,0:T(8,128)(2,1)S(1)}, bf16[64,2048]{1,0:T(8,128)(2,1)S(1)}, u32[]{:S(2)}, u32[]{:S(2)}) collective-permute-start(bf16[64,2048]{1,0:T(8,128)(2,1)S(1)} %collective-permute-done.14), channel_id=1, source_target_pairs={{0,8},{8,16},{16,24},{24,28},{28,20},{20,12},{12,4},{4,0},{1,9},{9... | collective-permute-start | bytes 786440 | tf_op jit(solution)/shard_map/dispatch_gather/ppermute | solution.py:55
  142.6 6.4 %collective-permute-start.17 = (bf16[64,2048]{1,0:T(8,128)(2,1)S(1)}, bf16[64,2048]{1,0:T(8,128)(2,1)S(1)}, u32[]{:S(2)}, u32[]{:S(2)}) collective-permute-start(bf16[64,2048]{1,0:T(8,128)(2,1)S(1)} %collective-permute-done.15), channel_id=1, source_target_pairs={{0,4},{8,0},{16,8},{24,16},{28,24},{20,28},{12,20},{4,12},{1,5},{9... | collective-permute-start | bytes 786440 | tf_op jit(solution)/shard_map/dispatch_gather/ppermute | solution.py:55
  149.0 13.1 %collective-permute-start.18 = (bf16[64,2048]{1,0:T(8,128)(2,1)S(1)}, bf16[64,2048]{1,0:T(8,128)(2,1)S(1)}, u32[]{:S(2)}, u32[]{:S(2)}) collective-permute-start(bf16[64,2048]{1,0:T(8,128)(2,1)S(1)} %collective-permute-done.16), channel_id=1, source_target_pairs={{0,8},{8,16},{16,24},{24,28},{28,20},{20,12},{12,4},{4,0},{1,9},{9... | collective-permute-start | bytes 786440 | tf_op jit(solution)/shard_map/dispatch_gather/ppermute | solution.py:55
  150.8 11.3 %collective-permute-start.19 = (bf16[64,2048]{1,0:T(8,128)(2,1)S(1)}, bf16[64,2048]{1,0:T(8,128)(2,1)S(1)}, u32[]{:S(2)}, u32[]{:S(2)}) collective-permute-start(bf16[64,2048]{1,0:T(8,128)(2,1)S(1)} %collective-permute-done.17), channel_id=1, source_target_pairs={{0,4},{8,0},{16,8},{24,16},{28,24},{20,28},{12,20},{4,12},{1,5},{9... | collective-permute-start | bytes 786440 | tf_op jit(solution)/shard_map/dispatch_gather/ppermute | solution.py:55
  151.0 4.8 %slice-start.2 = ((s8[12582912]{0:T(1024)(128)(4,1)}), s8[4194304]{0:T(1024)(128)(4,1)S(1)}, s32[]{:S(2)}) async-start(s8[12582912]{0:T(1024)(128)(4,1)} %bitcast.262), calls=%async_computation.4 | async-start | bytes 8388608
  151.1 6.6 %slice-start.3 = ((s8[6291456]{0:T(1024)(128)(4,1)}), s8[4194304]{0:T(1024)(128)(4,1)S(1)}, s32[]{:S(2)}) async-start(s8[6291456]{0:T(1024)(128)(4,1)} %bitcast.264), calls=%async_computation.5 | async-start | bytes 8388608
  155.8 1.8 slice-start.4
  159.9 9.3 %collective-permute-start.28 = (bf16[64,2048]{1,0:T(8,128)(2,1)S(1)}, bf16[64,2048]{1,0:T(8,128)(2,1)S(1)}, u32[]{:S(2)}, u32[]{:S(2)}) collective-permute-start(bf16[64,2048]{1,0:T(8,128)(2,1)S(1)} %get-tuple-element.122), channel_id=1, source_target_pairs={{0,8},{8,16},{16,24},{24,28},{28,20},{20,12},{12,4},{4,0},{1,9},{9... | collective-permute-start | bytes 786440 | tf_op jit(solution)/shard_map/combine_return/ppermute | solution.py:75
  161.7 8.7 %collective-permute-start.29 = (bf16[64,2048]{1,0:T(8,128)(2,1)S(1)}, bf16[64,2048]{1,0:T(8,128)(2,1)S(1)}, u32[]{:S(2)}, u32[]{:S(2)}) collective-permute-start(bf16[64,2048]{1,0:T(8,128)(2,1)S(1)} %get-tuple-element.123), channel_id=1, source_target_pairs={{0,4},{8,0},{16,8},{24,16},{28,24},{20,28},{12,20},{4,12},{1,5},{9... | collective-permute-start | bytes 786440 | tf_op jit(solution)/shard_map/combine_return/ppermute | solution.py:75
  162.1 11.2 %collective-permute-start.20 = (bf16[64,2048]{1,0:T(8,128)(2,1)S(1)}, bf16[64,2048]{1,0:T(8,128)(2,1)S(1)}, u32[]{:S(2)}, u32[]{:S(2)}) collective-permute-start(bf16[64,2048]{1,0:T(8,128)(2,1)S(1)} %collective-permute-done.18), channel_id=1, source_target_pairs={{0,8},{8,16},{16,24},{24,28},{28,20},{20,12},{12,4},{4,0},{1,9},{9... | collective-permute-start | bytes 786440 | tf_op jit(solution)/shard_map/dispatch_gather/ppermute | solution.py:55
  163.9 10.6 %collective-permute-start.21 = (bf16[64,2048]{1,0:T(8,128)(2,1)S(1)}, bf16[64,2048]{1,0:T(8,128)(2,1)S(1)}, u32[]{:S(2)}, u32[]{:S(2)}) collective-permute-start(bf16[64,2048]{1,0:T(8,128)(2,1)S(1)} %collective-permute-done.19), channel_id=1, source_target_pairs={{0,4},{8,0},{16,8},{24,16},{28,24},{20,28},{12,20},{4,12},{1,5},{9... | collective-permute-start | bytes 786440 | tf_op jit(solution)/shard_map/dispatch_gather/ppermute | solution.py:55
  170.6 9.5 %collective-permute-start.30 = (bf16[64,2048]{1,0:T(8,128)(2,1)S(1)}, bf16[64,2048]{1,0:T(8,128)(2,1)S(1)}, u32[]{:S(2)}, u32[]{:S(2)}) collective-permute-start(bf16[64,2048]{1,0:T(8,128)(2,1)S(1)} %get-tuple-element.126), channel_id=1, source_target_pairs={{0,8},{8,16},{16,24},{24,28},{28,20},{20,12},{12,4},{4,0},{1,9},{9... | collective-permute-start | bytes 786440 | tf_op jit(solution)/shard_map/combine_return/ppermute | solution.py:75
  171.0 9.2 %collective-permute-start.31 = (bf16[64,2048]{1,0:T(8,128)(2,1)S(1)}, bf16[64,2048]{1,0:T(8,128)(2,1)S(1)}, u32[]{:S(2)}, u32[]{:S(2)}) collective-permute-start(bf16[64,2048]{1,0:T(8,128)(2,1)S(1)} %get-tuple-element.127), channel_id=1, source_target_pairs={{0,4},{8,0},{16,8},{24,16},{28,24},{20,28},{12,20},{4,12},{1,5},{9... | collective-permute-start | bytes 786440 | tf_op jit(solution)/shard_map/combine_return/ppermute | solution.py:75
  174.5 11.0 %collective-permute-start.22 = (bf16[64,2048]{1,0:T(8,128)(2,1)S(1)}, bf16[64,2048]{1,0:T(8,128)(2,1)S(1)}, u32[]{:S(2)}, u32[]{:S(2)}) collective-permute-start(bf16[64,2048]{1,0:T(8,128)(2,1)S(1)} %collective-permute-done.20), channel_id=1, source_target_pairs={{0,8},{8,16},{16,24},{24,28},{28,20},{20,12},{12,4},{4,0},{1,9},{9... | collective-permute-start | bytes 786440 | tf_op jit(solution)/shard_map/dispatch_gather/ppermute | solution.py:55
  174.8 11.1 %collective-permute-start.23 = (bf16[64,2048]{1,0:T(8,128)(2,1)S(1)}, bf16[64,2048]{1,0:T(8,128)(2,1)S(1)}, u32[]{:S(2)}, u32[]{:S(2)}) collective-permute-start(bf16[64,2048]{1,0:T(8,128)(2,1)S(1)} %collective-permute-done.21), channel_id=1, source_target_pairs={{0,4},{8,0},{16,8},{24,16},{28,24},{20,28},{12,20},{4,12},{1,5},{9... | collective-permute-start | bytes 786440 | tf_op jit(solution)/shard_map/dispatch_gather/ppermute | solution.py:55
  182.5 9.3 %collective-permute-start.32 = (bf16[64,2048]{1,0:T(8,128)(2,1)S(1)}, bf16[64,2048]{1,0:T(8,128)(2,1)S(1)}, u32[]{:S(2)}, u32[]{:S(2)}) collective-permute-start(bf16[64,2048]{1,0:T(8,128)(2,1)S(1)} %get-tuple-element.130), channel_id=1, source_target_pairs={{0,8},{8,16},{16,24},{24,28},{28,20},{20,12},{12,4},{4,0},{1,9},{9... | collective-permute-start | bytes 786440 | tf_op jit(solution)/shard_map/combine_return/ppermute | solution.py:75
  184.1 8.8 %collective-permute-start.33 = (bf16[64,2048]{1,0:T(8,128)(2,1)S(1)}, bf16[64,2048]{1,0:T(8,128)(2,1)S(1)}, u32[]{:S(2)}, u32[]{:S(2)}) collective-permute-start(bf16[64,2048]{1,0:T(8,128)(2,1)S(1)} %get-tuple-element.131), channel_id=1, source_target_pairs={{0,4},{8,0},{16,8},{24,16},{28,24},{20,28},{12,20},{4,12},{1,5},{9... | collective-permute-start | bytes 786440 | tf_op jit(solution)/shard_map/combine_return/ppermute | solution.py:75
  185.9 11.0 %collective-permute-start.24 = (bf16[64,2048]{1,0:T(8,128)(2,1)S(1)}, bf16[64,2048]{1,0:T(8,128)(2,1)S(1)}, u32[]{:S(2)}, u32[]{:S(2)}) collective-permute-start(bf16[64,2048]{1,0:T(8,128)(2,1)S(1)} %collective-permute-done.22), channel_id=1, source_target_pairs={{0,8},{8,16},{16,24},{24,28},{28,20},{20,12},{12,4},{4,0},{1,9},{9... | collective-permute-start | bytes 786440 | tf_op jit(solution)/shard_map/dispatch_gather/ppermute | solution.py:55
  187.4 10.6 %collective-permute-start.25 = (bf16[64,2048]{1,0:T(8,128)(2,1)S(1)}, bf16[64,2048]{1,0:T(8,128)(2,1)S(1)}, u32[]{:S(2)}, u32[]{:S(2)}) collective-permute-start(bf16[64,2048]{1,0:T(8,128)(2,1)S(1)} %collective-permute-done.23), channel_id=1, source_target_pairs={{0,4},{8,0},{16,8},{24,16},{28,24},{20,28},{12,20},{4,12},{1,5},{9... | collective-permute-start | bytes 786440 | tf_op jit(solution)/shard_map/dispatch_gather/ppermute | solution.py:55
  193.0 10.6 %collective-permute-start.34 = (bf16[64,2048]{1,0:T(8,128)(2,1)S(1)}, bf16[64,2048]{1,0:T(8,128)(2,1)S(1)}, u32[]{:S(2)}, u32[]{:S(2)}) collective-permute-start(bf16[64,2048]{1,0:T(8,128)(2,1)S(1)} %get-tuple-element.134), channel_id=1, source_target_pairs={{0,8},{8,16},{16,24},{24,28},{28,20},{20,12},{12,4},{4,0},{1,9},{9... | collective-permute-start | bytes 786440 | tf_op jit(solution)/shard_map/combine_return/ppermute | solution.py:75
  193.4 10.2 %collective-permute-start.35 = (bf16[64,2048]{1,0:T(8,128)(2,1)S(1)}, bf16[64,2048]{1,0:T(8,128)(2,1)S(1)}, u32[]{:S(2)}, u32[]{:S(2)}) collective-permute-start(bf16[64,2048]{1,0:T(8,128)(2,1)S(1)} %get-tuple-element.135), channel_id=1, source_target_pairs={{0,4},{8,0},{16,8},{24,16},{28,24},{20,28},{12,20},{4,12},{1,5},{9... | collective-permute-start | bytes 786440 | tf_op jit(solution)/shard_map/combine_return/ppermute | solution.py:75
  198.0 10.0 %collective-permute-start.26 = (bf16[64,2048]{1,0:T(8,128)(2,1)S(1)}, bf16[64,2048]{1,0:T(8,128)(2,1)S(1)}, u32[]{:S(2)}, u32[]{:S(2)}) collective-permute-start(bf16[64,2048]{1,0:T(8,128)(2,1)S(1)} %collective-permute-done.24), channel_id=1, source_target_pairs={{0,8},{8,16},{16,24},{24,28},{28,20},{20,12},{12,4},{4,0},{1,9},{9... | collective-permute-start | bytes 786440 | tf_op jit(solution)/shard_map/dispatch_gather/ppermute | solution.py:55
  198.2 9.8 %collective-permute-start.27 = (bf16[64,2048]{1,0:T(8,128)(2,1)S(1)}, bf16[64,2048]{1,0:T(8,128)(2,1)S(1)}, u32[]{:S(2)}, u32[]{:S(2)}) collective-permute-start(bf16[64,2048]{1,0:T(8,128)(2,1)S(1)} %collective-permute-done.25), channel_id=1, source_target_pairs={{0,4},{8,0},{16,8},{24,16},{28,24},{20,28},{12,20},{4,12},{1,5},{9... | collective-permute-start | bytes 786440 | tf_op jit(solution)/shard_map/dispatch_gather/ppermute | solution.py:55
  205.9 8.7 %collective-permute-start.36 = (bf16[64,2048]{1,0:T(8,128)(2,1)S(1)}, bf16[64,2048]{1,0:T(8,128)(2,1)S(1)}, u32[]{:S(2)}, u32[]{:S(2)}) collective-permute-start(bf16[64,2048]{1,0:T(8,128)(2,1)S(1)} %get-tuple-element.138), channel_id=1, source_target_pairs={{0,8},{8,16},{16,24},{24,28},{28,20},{20,12},{12,4},{4,0},{1,9},{9... | collective-permute-start | bytes 786440 | tf_op jit(solution)/shard_map/combine_return/ppermute | solution.py:75
  206.2 8.3 %collective-permute-start.37 = (bf16[64,2048]{1,0:T(8,128)(2,1)S(1)}, bf16[64,2048]{1,0:T(8,128)(2,1)S(1)}, u32[]{:S(2)}, u32[]{:S(2)}) collective-permute-start(bf16[64,2048]{1,0:T(8,128)(2,1)S(1)} %get-tuple-element.139), channel_id=1, source_target_pairs={{0,4},{8,0},{16,8},{24,16},{28,24},{20,28},{12,20},{4,12},{1,5},{9... | collective-permute-start | bytes 786440 | tf_op jit(solution)/shard_map/combine_return/ppermute | solution.py:75
  214.7 6.7 %collective-permute-start.38 = (bf16[64,2048]{1,0:T(8,128)(2,1)S(1)}, bf16[64,2048]{1,0:T(8,128)(2,1)S(1)}, u32[]{:S(2)}, u32[]{:S(2)}) collective-permute-start(bf16[64,2048]{1,0:T(8,128)(2,1)S(1)} %get-tuple-element.142), channel_id=1, source_target_pairs={{0,8},{8,16},{16,24},{24,28},{28,20},{20,12},{12,4},{4,0},{1,9},{9... | collective-permute-start | bytes 786440 | tf_op jit(solution)/shard_map/combine_return/ppermute | solution.py:75
  214.8 6.6 %collective-permute-start.39 = (bf16[64,2048]{1,0:T(8,128)(2,1)S(1)}, bf16[64,2048]{1,0:T(8,128)(2,1)S(1)}, u32[]{:S(2)}, u32[]{:S(2)}) collective-permute-start(bf16[64,2048]{1,0:T(8,128)(2,1)S(1)} %get-tuple-element.143), channel_id=1, source_target_pairs={{0,4},{8,0},{16,8},{24,16},{28,24},{20,28},{12,20},{4,12},{1,5},{9... | collective-permute-start | bytes 786440 | tf_op jit(solution)/shard_map/combine_return/ppermute | solution.py:75
  221.5 9.1 %copy-start.6 = (f32[2048]{0:T(1024)S(1)}, f32[2048]{0:T(1024)}, u32[]{:S(2)}) copy-start(f32[2048]{0:T(1024)} %param.20) | copy-start | bytes 24580
  221.6 6.7 %collective-permute-start.40 = (bf16[64,2048]{1,0:T(8,128)(2,1)S(1)}, bf16[64,2048]{1,0:T(8,128)(2,1)S(1)}, u32[]{:S(2)}, u32[]{:S(2)}) collective-permute-start(bf16[64,2048]{1,0:T(8,128)(2,1)S(1)} %get-tuple-element.146), channel_id=1, source_target_pairs={{0,8},{8,16},{16,24},{24,28},{28,20},{20,12},{12,4},{4,0},{1,9},{9... | collective-permute-start | bytes 786440 | tf_op jit(solution)/shard_map/combine_return/ppermute | solution.py:75
  223.9 6.4 %collective-permute-start.41 = (bf16[64,2048]{1,0:T(8,128)(2,1)S(1)}, bf16[64,2048]{1,0:T(8,128)(2,1)S(1)}, u32[]{:S(2)}, u32[]{:S(2)}) collective-permute-start(bf16[64,2048]{1,0:T(8,128)(2,1)S(1)} %get-tuple-element.147), channel_id=1, source_target_pairs={{0,4},{8,0},{16,8},{24,16},{28,24},{20,28},{12,20},{4,12},{1,5},{9... | collective-permute-start | bytes 786440 | tf_op jit(solution)/shard_map/combine_return/ppermute | solution.py:75
  230.4 2.0 copy-start.1

commit v13 on v9

--- a/solution.py
+++ b/solution.py
@@ -145,7 +145,7 @@
 
     with jax.named_scope("local_experts"):
         steps_all = list(range(ep_size - 1))
-        chunks = [steps_all[i : i + 2] for i in range(0, ep_size - 1, 2)]
+        chunks = [[step] for step in steps_all]
         pieces = [None] * (ep_size - 1)
         own_part = None
         for c, steps in enumerate(chunks):

time: 220 us -> 230 us (1.045)
  waiting for transfers between devices: 69.3 us -> 77.4 us
  local copies, waits for them, and re-layouts: 8.18 us -> 10.5 us
    ppermute x7, waiting for transfers between devices: 11.6 us -> 29.6 us  [ring_reduce_scatter(): lax.ppermute(send_fwd, 'ep', forward)]
    ppermute x7, waiting for transfers between devices: 17.1 us -> 11 us  [ring_reduce_scatter_steps(): lax.ppermute(send_fwd, 'ep', forward)]
    ppermute x7, starting transfers between devices: 9.27 us -> 5.88 us  [ring_reduce_scatter_steps(): lax.ppermute(send_bwd, 'ep', backward)]
    dot_general x8 -> x14, matrix products: 8.31 us -> 9.56 us  [expert_mix(): jnp.dot(activated, down[e], preferred_element_type=jnp.float32)]
    dot_general x8 -> x14, matrix products: 20.1 us -> 18.9 us  [expert_mix(): projected_up = jnp.dot(rows, gate_up[e], preferred_element_type=jnp.float32)]
where the time goes in v13:
time: 230 us; the launch traced here: 229 us
  waiting for transfers between devices  77.4 us (34%)
  starting transfers between devices  55.4 us (24%)
  between operations  40.4 us (18%)
  matrix products  30.8 us (13%)
  other arithmetic  14.1 us (6%)
  local copies, waits for them, and re-layouts  10.5 us (5%)
    ppermute x7, waiting for transfers between devices, ring_reduce_scatter(): lax.ppermute(send_fwd, 'ep', forward)  29.6 us
    dot_general x14, matrix products, expert_mix(): projected_up = jnp.dot(rows, gate_up[e], preferred_element_type=jnp.float32)  18.9 us
    ppermute x7, waiting for transfers between devices, ring_reduce_scatter_steps(): lax.ppermute(send_fwd, 'ep', forward)  11 us
    dot_general x14, matrix products, expert_mix(): jnp.dot(activated, down[e], preferred_element_type=jnp.float32)  9.56 us
    ppermute x7, starting transfers between devices, ring_reduce_scatter_steps(): lax.ppermute(send_fwd, 'ep', forward)  8.66 us
    ppermute x7, waiting for transfers between devices, ring_all_gather(): lax.ppermute(got_bwd, 'ep', backward)  8.5 us
    convert_element_type x6, other arithmetic, ring_reduce_scatter(): send_bwd.astype(jnp.bfloat16)  8.11 us
    ppermute x7, starting transfers between devices, ring_all_gather(): lax.ppermute(got_bwd, 'ep', backward)  8.1 us
  transfers between devices with their start and end apart: 44, of which 34 were waited for; matrix products, arithmetic and copies ran while one was open for 15% of the time, Pallas kernels for 0%

profile of v13, /device:TPU:0, one launch (start us, length us, event | category | flops | bytes accessed | tf_op | source)
XLA Modules:
  0.0 228.6 jit_solution(9245168562540554587)
XLA Ops:
  0.6 1.5 select_reduce_fusion
  2.1 7.3 %all-to-all-start.1 = ((f32[8,128,2]{1,2,0:T(2,128)}), f32[8,128,2]{1,2,0:T(2,128)S(1)}, u32[]{:S(2)}, u32[]{:S(2)}) async-start(f32[8,128,2]{1,2,0:T(2,128)} %bitcast.2), calls=%async_computation.1 | async-start | bytes 16384 | tf_op jit(solution)/shard_map/route_weights/all_to_all | solution.py:118
  9.4 2.3 %copy.25 = bf16[16,8,8,512]{3,2,0,1:T(8,128)(2,1)} copy(bf16[16,8,8,512]{3,2,1,0:T(8,128)(2,1)} %bitcast.334) | data formatting | bytes 2097152 | tf_op jit(solution)/shard_map/out_projection/reshape | solution.py:122
  11.7 4.2 %all-to-all-done.1 = f32[8,128,2]{1,2,0:T(2,128)S(1)} async-done(((f32[8,128,2]{1,2,0:T(2,128)}), f32[8,128,2]{1,2,0:T(2,128)S(1)}, u32[]{:S(2)}, u32[]{:S(2)}) %all-to-all-start.1) | async-done | bytes 8224 | tf_op jit(solution)/shard_map/route_weights/all_to_all | solution.py:118
  15.9 3.6 %all-to-all-start = ((bf16[8,128,512]{2,1,0:T(8,128)(2,1)}), bf16[8,128,512]{2,1,0:T(8,128)(2,1)S(1)}, u32[]{:S(2)}, u32[]{:S(2)}) async-start(bf16[8,128,512]{2,1,0:T(8,128)(2,1)} %bitcast.332), calls=%async_computation | async-start | bytes 2097152 | tf_op jit(solution)/shard_map/out_projection/all_to_all | solution.py:123
  19.5 1.2 dynamic_slice.182
  32.0 2.0 fusion.343
  37.7 6.5 %all-to-all-done = bf16[8,128,512]{2,1,0:T(8,128)(2,1)S(1)} async-done(((bf16[8,128,512]{2,1,0:T(8,128)(2,1)}), bf16[8,128,512]{2,1,0:T(8,128)(2,1)S(1)}, u32[]{:S(2)}, u32[]{:S(2)}) %all-to-all-start) | async-done | bytes 1048608 | tf_op jit(solution)/shard_map/out_projection/all_to_all | solution.py:123
  44.2 2.3 %fusion.206 = f32[8,128,2048]{2,1,0:T(8,128)S(1)} fusion(bf16[8,128,512]{2,1,0:T(8,128)(2,1)S(1)} %all-to-all-done, bf16[512,2048]{1,0:T(8,128)(2,1)S(1)} %copy-done), kind=kOutput, calls=%fused_computation.106 | convolution fusion | flops 2147483648 | bytes 11534336 | tf_op jit(solution)/shard_map/out_projection/dot_general | solution.py:125
  46.6 3.3 %copy-done.2 = f32[8,128,2048]{2,1,0:T(8,128)} copy-done((f32[8,128,2048]{2,1,0:T(8,128)}, f32[8,128,2048]{2,1,0:T(8,128)S(1)}, u32[]{:S(2)}) %copy-start.2) | copy-done | bytes 8388632
  50.0 2.0 collective-permute-start.1
  76.3 1.3 fusion.266
  77.8 2.0 collective-permute-start.3
  79.8 4.3 %collective-permute-done.2 = bf16[64,2048]{1,0:T(8,128)(2,1)S(1)} collective-permute-done((bf16[64,2048]{1,0:T(8,128)(2,1)S(1)}, bf16[64,2048]{1,0:T(8,128)(2,1)S(1)}, u32[]{:S(2)}, u32[]{:S(2)}) %collective-permute-start.2) | collective-permute-done | bytes 262176 | tf_op jit(solution)/shard_map/out_projection/ppermute | solution.py:37
  84.1 1.3 fusion.264
  85.5 1.4 collective-permute-start.4
  87.6 4.3 %collective-permute-done.4 = bf16[64,2048]{1,0:T(8,128)(2,1)S(1)} collective-permute-done((bf16[64,2048]{1,0:T(8,128)(2,1)S(1)}, bf16[64,2048]{1,0:T(8,128)(2,1)S(1)}, u32[]{:S(2)}, u32[]{:S(2)}) %collective-permute-start.4) | collective-permute-done | bytes 262176 | tf_op jit(solution)/shard_map/out_projection/ppermute | solution.py:37
  91.9 1.3 collective-permute-done.5
  93.2 1.3 fusion.262
  94.5 1.8 collective-permute-start.6
  96.7 4.3 %collective-permute-done.6 = bf16[64,2048]{1,0:T(8,128)(2,1)S(1)} collective-permute-done((bf16[64,2048]{1,0:T(8,128)(2,1)S(1)}, bf16[64,2048]{1,0:T(8,128)(2,1)S(1)}, u32[]{:S(2)}, u32[]{:S(2)}) %collective-permute-start.6) | collective-permute-done | bytes 262176 | tf_op jit(solution)/shard_map/out_projection/ppermute | solution.py:37
  101.0 1.7 collective-permute-done.7
  102.7 1.5 fusion.260
  104.2 1.8 collective-permute-start.8
  106.4 4.6 %collective-permute-done.8 = bf16[64,2048]{1,0:T(8,128)(2,1)S(1)} collective-permute-done((bf16[64,2048]{1,0:T(8,128)(2,1)S(1)}, bf16[64,2048]{1,0:T(8,128)(2,1)S(1)}, u32[]{:S(2)}, u32[]{:S(2)}) %collective-permute-start.8) | collective-permute-done | bytes 262176 | tf_op jit(solution)/shard_map/out_projection/ppermute | solution.py:37
  110.9 2.8 %collective-permute-done.9 = bf16[64,2048]{1,0:T(8,128)(2,1)S(1)} collective-permute-done((bf16[64,2048]{1,0:T(8,128)(2,1)S(1)}, bf16[64,2048]{1,0:T(8,128)(2,1)S(1)}, u32[]{:S(2)}, u32[]{:S(2)}) %collective-permute-start.9) | collective-permute-done | bytes 262176 | tf_op jit(solution)/shard_map/out_projection/ppermute | solution.py:37
  113.7 1.3 fusion.258
  115.1 2.0 collective-permute-start.11
  117.2 6.7 %collective-permute-done.10 = bf16[64,2048]{1,0:T(8,128)(2,1)S(1)} collective-permute-done((bf16[64,2048]{1,0:T(8,128)(2,1)S(1)}, bf16[64,2048]{1,0:T(8,128)(2,1)S(1)}, u32[]{:S(2)}, u32[]{:S(2)}) %collective-permute-start.10) | collective-permute-done | bytes 262176 | tf_op jit(solution)/shard_map/out_projection/ppermute | solution.py:37
  124.0 1.3 fusion.256
  125.3 1.5 collective-permute-start.12
  127.8 5.5 %collective-permute-done.12 = bf16[64,2048]{1,0:T(8,128)(2,1)S(1)} collective-permute-done((bf16[64,2048]{1,0:T(8,128)(2,1)S(1)}, bf16[64,2048]{1,0:T(8,128)(2,1)S(1)}, u32[]{:S(2)}, u32[]{:S(2)}) %collective-permute-start.12) | collective-permute-done | bytes 262176 | tf_op jit(solution)/shard_map/out_projection/ppermute | solution.py:37
  134.3 1.3 fusion.279
  136.1 2.3 %collective-permute-start.15 = (bf16[64,2048]{1,0:T(8,128)(2,1)S(1)}, bf16[64,2048]{1,0:T(8,128)(2,1)S(1)}, u32[]{:S(2)}, u32[]{:S(2)}) collective-permute-start(bf16[64,2048]{1,0:T(8,128)(2,1)S(1)} %get-tuple-element.182), channel_id=1, source_target_pairs={{0,4},{8,0},{16,8},{24,16},{28,24},{20,28},{12,20},{4,12},{1,5},{9... | collective-permute-start | bytes 786440 | tf_op jit(solution)/shard_map/dispatch_gather/ppermute | solution.py:55
  138.5 5.3 %collective-permute-done.15 = bf16[64,2048]{1,0:T(8,128)(2,1)S(1)} collective-permute-done((bf16[64,2048]{1,0:T(8,128)(2,1)S(1)}, bf16[64,2048]{1,0:T(8,128)(2,1)S(1)}, u32[]{:S(2)}, u32[]{:S(2)}) %collective-permute-start.15) | collective-permute-done | bytes 262176 | tf_op jit(solution)/shard_map/dispatch_gather/ppermute | solution.py:55
  144.8 2.1 collective-permute-start.17
  147.0 3.9 %fusion = f32[128,1536]{1,0:T(8,128)S(1)} fusion(bf16[128,2048]{1,0:T(8,128)(2,1)S(1)} %constant_dynamic-update-slice_fusion.10, bf16[2,2048,1536]{2,1,0:T(8,128)(2,1)} %param.16), kind=kOutput, calls=%fused_computation | convolution fusion | flops 805306368 | bytes 7602176 | tf_op jit(solution)/shard_map/local_experts/dot_general | solution.py:87
  154.4 2.0 collective-permute-start.29
  156.5 2.2 collective-permute-start.19
  160.8 2.8 %collective-permute-done.28 = bf16[64,2048]{1,0:T(8,128)(2,1)S(1)} collective-permute-done((bf16[64,2048]{1,0:T(8,128)(2,1)S(1)}, bf16[64,2048]{1,0:T(8,128)(2,1)S(1)}, u32[]{:S(2)}, u32[]{:S(2)}) %collective-permute-start.28) | collective-permute-done | bytes 262176 | tf_op jit(solution)/shard_map/combine_return/ppermute | solution.py:75
  165.0 1.7 collective-permute-start.30
  167.1 2.1 collective-permute-done.18
  169.2 1.7 collective-permute-start.20
  173.5 1.4 collective-permute-done.30
  177.3 1.0 collective-permute-start.32
  179.3 1.1 collective-permute-done.20
  180.7 1.8 collective-permute-start.22
  184.9 1.7 collective-permute-done.32
  188.5 1.7 collective-permute-start.34
  190.6 1.6 collective-permute-done.22
  192.6 1.8 collective-permute-start.24
  196.0 1.0 fusion.22
  199.7 1.7 collective-permute-start.36
  201.8 1.5 collective-permute-done.24
  203.8 1.8 collective-permute-start.26
  209.4 1.8 collective-permute-start.38
  211.5 2.0 collective-permute-done.27
  213.5 1.8 fusion.12
  215.3 1.8 fusion.26
  217.7 1.1 fusion.74
  218.8 1.1 fusion.65
  220.7 1.4 collective-permute-start.41
  222.1 4.3 %collective-permute-done.40 = bf16[64,2048]{1,0:T(8,128)(2,1)S(1)} collective-permute-done((bf16[64,2048]{1,0:T(8,128)(2,1)S(1)}, bf16[64,2048]{1,0:T(8,128)(2,1)S(1)}, u32[]{:S(2)}, u32[]{:S(2)}) %collective-permute-start.40) | collective-permute-done | bytes 262176 | tf_op jit(solution)/shard_map/combine_return/ppermute | solution.py:75
  227.4 1.2 multiply_convert_fusion
  (133 shorter events, 36.0 us)
Async XLA Ops:
  0.6 43.6 %copy-start = (bf16[512,2048]{1,0:T(8,128)(2,1)S(1)}, bf16[512,2048]{1,0:T(8,128)(2,1)}, u32[]{:S(2)}) copy-start(bf16[512,2048]{1,0:T(8,128)(2,1)} %param.14) | copy-start | bytes 6291460
  2.1 13.8 %all-to-all-start.1 = ((f32[8,128,2]{1,2,0:T(2,128)}), f32[8,128,2]{1,2,0:T(2,128)S(1)}, u32[]{:S(2)}, u32[]{:S(2)}) async-start(f32[8,128,2]{1,2,0:T(2,128)} %bitcast.2), calls=%async_computation.1 | async-start | bytes 16384 | tf_op jit(solution)/shard_map/route_weights/all_to_all | solution.py:118
  15.9 28.3 %all-to-all-start = ((bf16[8,128,512]{2,1,0:T(8,128)(2,1)}), bf16[8,128,512]{2,1,0:T(8,128)(2,1)S(1)}, u32[]{:S(2)}, u32[]{:S(2)}) async-start(bf16[8,128,512]{2,1,0:T(8,128)(2,1)} %bitcast.332), calls=%async_computation | async-start | bytes 2097152 | tf_op jit(solution)/shard_map/out_projection/all_to_all | solution.py:123
  46.5 3.3 %copy-start.2 = (f32[8,128,2048]{2,1,0:T(8,128)}, f32[8,128,2048]{2,1,0:T(8,128)S(1)}, u32[]{:S(2)}) copy-start(f32[8,128,2048]{2,1,0:T(8,128)S(1)} %fusion.206) | copy-start | bytes 25165828
  49.9 26.4 %collective-permute-start = (bf16[64,2048]{1,0:T(8,128)(2,1)S(1)}, bf16[64,2048]{1,0:T(8,128)(2,1)S(1)}, u32[]{:S(2)}, u32[]{:S(2)}) collective-permute-start(bf16[64,2048]{1,0:T(8,128)(2,1)S(1)} %get-tuple-element.75), channel_id=1, source_target_pairs={{0,8},{8,16},{16,24},{24,28},{28,20},{20,12},{12,4},{4,0},{1,9},{9... | collective-permute-start | bytes 786440 | tf_op jit(solution)/shard_map/out_projection/ppermute | solution.py:37
  50.0 26.3 %collective-permute-start.1 = (bf16[64,2048]{1,0:T(8,128)(2,1)S(1)}, bf16[64,2048]{1,0:T(8,128)(2,1)S(1)}, u32[]{:S(2)}, u32[]{:S(2)}) collective-permute-start(bf16[64,2048]{1,0:T(8,128)(2,1)S(1)} %get-tuple-element.76), channel_id=1, source_target_pairs={{0,4},{8,0},{16,8},{24,16},{28,24},{20,28},{12,20},{4,12},{1,5},{9... | collective-permute-start | bytes 786440 | tf_op jit(solution)/shard_map/out_projection/ppermute | solution.py:37
  77.7 6.4 %collective-permute-start.2 = (bf16[64,2048]{1,0:T(8,128)(2,1)S(1)}, bf16[64,2048]{1,0:T(8,128)(2,1)S(1)}, u32[]{:S(2)}, u32[]{:S(2)}) collective-permute-start(bf16[64,2048]{1,0:T(8,128)(2,1)S(1)} %get-tuple-element.79), channel_id=1, source_target_pairs={{0,8},{8,16},{16,24},{24,28},{28,20},{20,12},{12,4},{4,0},{1,9},{9... | collective-permute-start | bytes 786440 | tf_op jit(solution)/shard_map/out_projection/ppermute | solution.py:37
  77.8 6.4 %collective-permute-start.3 = (bf16[64,2048]{1,0:T(8,128)(2,1)S(1)}, bf16[64,2048]{1,0:T(8,128)(2,1)S(1)}, u32[]{:S(2)}, u32[]{:S(2)}) collective-permute-start(bf16[64,2048]{1,0:T(8,128)(2,1)S(1)} %get-tuple-element.80), channel_id=1, source_target_pairs={{0,4},{8,0},{16,8},{24,16},{28,24},{20,28},{12,20},{4,12},{1,5},{9... | collective-permute-start | bytes 786440 | tf_op jit(solution)/shard_map/out_projection/ppermute | solution.py:37
  79.8 55.8 %copy-start.3 = (bf16[128,2048]{1,0:T(8,128)(2,1)S(1)}, bf16[128,2048]{1,0:T(8,128)(2,1)}, u32[]{:S(2)}) copy-start(bf16[128,2048]{1,0:T(8,128)(2,1)} %param.12) | copy-start | bytes 1572868
  85.5 6.4 %collective-permute-start.4 = (bf16[64,2048]{1,0:T(8,128)(2,1)S(1)}, bf16[64,2048]{1,0:T(8,128)(2,1)S(1)}, u32[]{:S(2)}, u32[]{:S(2)}) collective-permute-start(bf16[64,2048]{1,0:T(8,128)(2,1)S(1)} %get-tuple-element.83), channel_id=1, source_target_pairs={{0,8},{8,16},{16,24},{24,28},{28,20},{20,12},{12,4},{4,0},{1,9},{9... | collective-permute-start | bytes 786440 | tf_op jit(solution)/shard_map/out_projection/ppermute | solution.py:37
  86.8 6.4 %collective-permute-start.5 = (bf16[64,2048]{1,0:T(8,128)(2,1)S(1)}, bf16[64,2048]{1,0:T(8,128)(2,1)S(1)}, u32[]{:S(2)}, u32[]{:S(2)}) collective-permute-start(bf16[64,2048]{1,0:T(8,128)(2,1)S(1)} %get-tuple-element.84), channel_id=1, source_target_pairs={{0,4},{8,0},{16,8},{24,16},{28,24},{20,28},{12,20},{4,12},{1,5},{9... | collective-permute-start | bytes 786440 | tf_op jit(solution)/shard_map/out_projection/ppermute | solution.py:37
  87.6 48.2 %copy-start.4 = (f32[2048]{0:T(1024)S(1)}, f32[2048]{0:T(1024)}, u32[]{:S(2)}) copy-start(f32[2048]{0:T(1024)} %param.15) | copy-start | bytes 24580
  94.5 6.4 %collective-permute-start.6 = (bf16[64,2048]{1,0:T(8,128)(2,1)S(1)}, bf16[64,2048]{1,0:T(8,128)(2,1)S(1)}, u32[]{:S(2)}, u32[]{:S(2)}) collective-permute-start(bf16[64,2048]{1,0:T(8,128)(2,1)S(1)} %get-tuple-element.87), channel_id=1, source_target_pairs={{0,8},{8,16},{16,24},{24,28},{28,20},{20,12},{12,4},{4,0},{1,9},{9... | collective-permute-start | bytes 786440 | tf_op jit(solution)/shard_map/out_projection/ppermute | solution.py:37
  96.3 6.4 %collective-permute-start.7 = (bf16[64,2048]{1,0:T(8,128)(2,1)S(1)}, bf16[64,2048]{1,0:T(8,128)(2,1)S(1)}, u32[]{:S(2)}, u32[]{:S(2)}) collective-permute-start(bf16[64,2048]{1,0:T(8,128)(2,1)S(1)} %get-tuple-element.88), channel_id=1, source_target_pairs={{0,4},{8,0},{16,8},{24,16},{28,24},{20,28},{12,20},{4,12},{1,5},{9... | collective-permute-start | bytes 786440 | tf_op jit(solution)/shard_map/out_projection/ppermute | solution.py:37
  102.7 48.2 %slice-start = ((s8[12582912]{0:T(1024)(128)(4,1)}), s8[4194304]{0:T(1024)(128)(4,1)S(1)}, s32[]{:S(2)}) async-start(s8[12582912]{0:T(1024)(128)(4,1)} %bitcast.355), calls=%async_computation.2 | async-start | bytes 8388608
  104.2 6.7 %collective-permute-start.8 = (bf16[64,2048]{1,0:T(8,128)(2,1)S(1)}, bf16[64,2048]{1,0:T(8,128)(2,1)S(1)}, u32[]{:S(2)}, u32[]{:S(2)}) collective-permute-start(bf16[64,2048]{1,0:T(8,128)(2,1)S(1)} %get-tuple-element.91), channel_id=1, source_target_pairs={{0,8},{8,16},{16,24},{24,28},{28,20},{20,12},{12,4},{4,0},{1,9},{9... | collective-permute-start | bytes 786440 | tf_op jit(solution)/shard_map/out_projection/ppermute | solution.py:37
  106.0 7.7 %collective-permute-start.9 = (bf16[64,2048]{1,0:T(8,128)(2,1)S(1)}, bf16[64,2048]{1,0:T(8,128)(2,1)S(1)}, u32[]{:S(2)}, u32[]{:S(2)}) collective-permute-start(bf16[64,2048]{1,0:T(8,128)(2,1)S(1)} %get-tuple-element.92), channel_id=1, source_target_pairs={{0,4},{8,0},{16,8},{24,16},{28,24},{20,28},{12,20},{4,12},{1,5},{9... | collective-permute-start | bytes 786440 | tf_op jit(solution)/shard_map/out_projection/ppermute | solution.py:37
  115.0 8.9 %collective-permute-start.10 = (bf16[64,2048]{1,0:T(8,128)(2,1)S(1)}, bf16[64,2048]{1,0:T(8,128)(2,1)S(1)}, u32[]{:S(2)}, u32[]{:S(2)}) collective-permute-start(bf16[64,2048]{1,0:T(8,128)(2,1)S(1)} %get-tuple-element.95), channel_id=1, source_target_pairs={{0,8},{8,16},{16,24},{24,28},{28,20},{20,12},{12,4},{4,0},{1,9},{9... | collective-permute-start | bytes 786440 | tf_op jit(solution)/shard_map/out_projection/ppermute | solution.py:37
  115.1 8.9 %collective-permute-start.11 = (bf16[64,2048]{1,0:T(8,128)(2,1)S(1)}, bf16[64,2048]{1,0:T(8,128)(2,1)S(1)}, u32[]{:S(2)}, u32[]{:S(2)}) collective-permute-start(bf16[64,2048]{1,0:T(8,128)(2,1)S(1)} %get-tuple-element.96), channel_id=1, source_target_pairs={{0,4},{8,0},{16,8},{24,16},{28,24},{20,28},{12,20},{4,12},{1,5},{9... | collective-permute-start | bytes 786440 | tf_op jit(solution)/shard_map/out_projection/ppermute | solution.py:37
  125.3 8.0 %collective-permute-start.12 = (bf16[64,2048]{1,0:T(8,128)(2,1)S(1)}, bf16[64,2048]{1,0:T(8,128)(2,1)S(1)}, u32[]{:S(2)}, u32[]{:S(2)}) collective-permute-start(bf16[64,2048]{1,0:T(8,128)(2,1)S(1)} %get-tuple-element.99), channel_id=1, source_target_pairs={{0,8},{8,16},{16,24},{24,28},{28,20},{20,12},{12,4},{4,0},{1,9},{9... | collective-permute-start | bytes 786440 | tf_op jit(solution)/shard_map/out_projection/ppermute | solution.py:37
  126.8 7.4 %collective-permute-start.13 = (bf16[64,2048]{1,0:T(8,128)(2,1)S(1)}, bf16[64,2048]{1,0:T(8,128)(2,1)S(1)}, u32[]{:S(2)}, u32[]{:S(2)}) collective-permute-start(bf16[64,2048]{1,0:T(8,128)(2,1)S(1)} %get-tuple-element.100), channel_id=1, source_target_pairs={{0,4},{8,0},{16,8},{24,16},{28,24},{20,28},{12,20},{4,12},{1,5},{9... | collective-permute-start | bytes 786440 | tf_op jit(solution)/shard_map/out_projection/ppermute | solution.py:37
  127.8 23.2 %slice-start.1 = ((s8[12582912]{0:T(1024)(128)(4,1)}), s8[4194304]{0:T(1024)(128)(4,1)S(1)}, s32[]{:S(2)}) async-start(s8[12582912]{0:T(1024)(128)(4,1)} %bitcast.355), calls=%async_computation.3 | async-start | bytes 8388608
  136.1 7.7 %collective-permute-start.15 = (bf16[64,2048]{1,0:T(8,128)(2,1)S(1)}, bf16[64,2048]{1,0:T(8,128)(2,1)S(1)}, u32[]{:S(2)}, u32[]{:S(2)}) collective-permute-start(bf16[64,2048]{1,0:T(8,128)(2,1)S(1)} %get-tuple-element.182), channel_id=1, source_target_pairs={{0,4},{8,0},{16,8},{24,16},{28,24},{20,28},{12,20},{4,12},{1,5},{9... | collective-permute-start | bytes 786440 | tf_op jit(solution)/shard_map/dispatch_gather/ppermute | solution.py:55
  138.4 6.4 %collective-permute-start.14 = (bf16[64,2048]{1,0:T(8,128)(2,1)S(1)}, bf16[64,2048]{1,0:T(8,128)(2,1)S(1)}, u32[]{:S(2)}, u32[]{:S(2)}) collective-permute-start(bf16[64,2048]{1,0:T(8,128)(2,1)S(1)} %get-tuple-element.183), channel_id=1, source_target_pairs={{0,8},{8,16},{16,24},{24,28},{28,20},{20,12},{12,4},{4,0},{1,9},{9... | collective-permute-start | bytes 786440 | tf_op jit(solution)/shard_map/dispatch_gather/ppermute | solution.py:55
  144.8 11.6 %collective-permute-start.16 = (bf16[64,2048]{1,0:T(8,128)(2,1)S(1)}, bf16[64,2048]{1,0:T(8,128)(2,1)S(1)}, u32[]{:S(2)}, u32[]{:S(2)}) collective-permute-start(bf16[64,2048]{1,0:T(8,128)(2,1)S(1)} %collective-permute-done.14), channel_id=1, source_target_pairs={{0,8},{8,16},{16,24},{24,28},{28,20},{20,12},{12,4},{4,0},{1,9},{9... | collective-permute-start | bytes 786440 | tf_op jit(solution)/shard_map/dispatch_gather/ppermute | solution.py:55
  144.8 11.6 %collective-permute-start.17 = (bf16[64,2048]{1,0:T(8,128)(2,1)S(1)}, bf16[64,2048]{1,0:T(8,128)(2,1)S(1)}, u32[]{:S(2)}, u32[]{:S(2)}) collective-permute-start(bf16[64,2048]{1,0:T(8,128)(2,1)S(1)} %collective-permute-done.15), channel_id=1, source_target_pairs={{0,4},{8,0},{16,8},{24,16},{28,24},{20,28},{12,20},{4,12},{1,5},{9... | collective-permute-start | bytes 786440 | tf_op jit(solution)/shard_map/dispatch_gather/ppermute | solution.py:55
  146.9 4.0 %slice-start.2 = ((s8[12582912]{0:T(1024)(128)(4,1)}), s8[4194304]{0:T(1024)(128)(4,1)S(1)}, s32[]{:S(2)}) async-start(s8[12582912]{0:T(1024)(128)(4,1)} %bitcast.355), calls=%async_computation.4 | async-start | bytes 8388608
  147.0 5.3 %slice-start.3 = ((s8[6291456]{0:T(1024)(128)(4,1)}), s8[4194304]{0:T(1024)(128)(4,1)S(1)}, s32[]{:S(2)}) async-start(s8[6291456]{0:T(1024)(128)(4,1)} %bitcast.357), calls=%async_computation.5 | async-start | bytes 8388608
  150.9 2.1 slice-start.4
  154.3 9.3 %collective-permute-start.28 = (bf16[64,2048]{1,0:T(8,128)(2,1)S(1)}, bf16[64,2048]{1,0:T(8,128)(2,1)S(1)}, u32[]{:S(2)}, u32[]{:S(2)}) collective-permute-start(bf16[64,2048]{1,0:T(8,128)(2,1)S(1)} %get-tuple-element.118), channel_id=1, source_target_pairs={{0,8},{8,16},{16,24},{24,28},{28,20},{20,12},{12,4},{4,0},{1,9},{9... | collective-permute-start | bytes 786440 | tf_op jit(solution)/shard_map/combine_return/ppermute | solution.py:75
  154.4 9.3 %collective-permute-start.29 = (bf16[64,2048]{1,0:T(8,128)(2,1)S(1)}, bf16[64,2048]{1,0:T(8,128)(2,1)S(1)}, u32[]{:S(2)}, u32[]{:S(2)}) collective-permute-start(bf16[64,2048]{1,0:T(8,128)(2,1)S(1)} %get-tuple-element.119), channel_id=1, source_target_pairs={{0,4},{8,0},{16,8},{24,16},{28,24},{20,28},{12,20},{4,12},{1,5},{9... | collective-permute-start | bytes 786440 | tf_op jit(solution)/shard_map/combine_return/ppermute | solution.py:75
  156.4 12.8 %collective-permute-start.18 = (bf16[64,2048]{1,0:T(8,128)(2,1)S(1)}, bf16[64,2048]{1,0:T(8,128)(2,1)S(1)}, u32[]{:S(2)}, u32[]{:S(2)}) collective-permute-start(bf16[64,2048]{1,0:T(8,128)(2,1)S(1)} %collective-permute-done.16), channel_id=1, source_target_pairs={{0,8},{8,16},{16,24},{24,28},{28,20},{20,12},{12,4},{4,0},{1,9},{9... | collective-permute-start | bytes 786440 | tf_op jit(solution)/shard_map/dispatch_gather/ppermute | solution.py:55
  156.5 12.7 %collective-permute-start.19 = (bf16[64,2048]{1,0:T(8,128)(2,1)S(1)}, bf16[64,2048]{1,0:T(8,128)(2,1)S(1)}, u32[]{:S(2)}, u32[]{:S(2)}) collective-permute-start(bf16[64,2048]{1,0:T(8,128)(2,1)S(1)} %collective-permute-done.17), channel_id=1, source_target_pairs={{0,4},{8,0},{16,8},{24,16},{28,24},{20,28},{12,20},{4,12},{1,5},{9... | collective-permute-start | bytes 786440 | tf_op jit(solution)/shard_map/dispatch_gather/ppermute | solution.py:55
  165.0 9.8 %collective-permute-start.30 = (bf16[64,2048]{1,0:T(8,128)(2,1)S(1)}, bf16[64,2048]{1,0:T(8,128)(2,1)S(1)}, u32[]{:S(2)}, u32[]{:S(2)}) collective-permute-start(bf16[64,2048]{1,0:T(8,128)(2,1)S(1)} %get-tuple-element.122), channel_id=1, source_target_pairs={{0,8},{8,16},{16,24},{24,28},{28,20},{20,12},{12,4},{4,0},{1,9},{9... | collective-permute-start | bytes 786440 | tf_op jit(solution)/shard_map/combine_return/ppermute | solution.py:75
  166.7 9.2 %collective-permute-start.31 = (bf16[64,2048]{1,0:T(8,128)(2,1)S(1)}, bf16[64,2048]{1,0:T(8,128)(2,1)S(1)}, u32[]{:S(2)}, u32[]{:S(2)}) collective-permute-start(bf16[64,2048]{1,0:T(8,128)(2,1)S(1)} %get-tuple-element.123), channel_id=1, source_target_pairs={{0,4},{8,0},{16,8},{24,16},{28,24},{20,28},{12,20},{4,12},{1,5},{9... | collective-permute-start | bytes 786440 | tf_op jit(solution)/shard_map/combine_return/ppermute | solution.py:75
  169.2 11.2 %collective-permute-start.20 = (bf16[64,2048]{1,0:T(8,128)(2,1)S(1)}, bf16[64,2048]{1,0:T(8,128)(2,1)S(1)}, u32[]{:S(2)}, u32[]{:S(2)}) collective-permute-start(bf16[64,2048]{1,0:T(8,128)(2,1)S(1)} %collective-permute-done.18), channel_id=1, source_target_pairs={{0,8},{8,16},{16,24},{24,28},{28,20},{20,12},{12,4},{4,0},{1,9},{9... | collective-permute-start | bytes 786440 | tf_op jit(solution)/shard_map/dispatch_gather/ppermute | solution.py:55
  170.9 9.8 %collective-permute-start.21 = (bf16[64,2048]{1,0:T(8,128)(2,1)S(1)}, bf16[64,2048]{1,0:T(8,128)(2,1)S(1)}, u32[]{:S(2)}, u32[]{:S(2)}) collective-permute-start(bf16[64,2048]{1,0:T(8,128)(2,1)S(1)} %collective-permute-done.19), channel_id=1, source_target_pairs={{0,4},{8,0},{16,8},{24,16},{28,24},{20,28},{12,20},{4,12},{1,5},{9... | collective-permute-start | bytes 786440 | tf_op jit(solution)/shard_map/dispatch_gather/ppermute | solution.py:55
  177.3 9.3 %collective-permute-start.32 = (bf16[64,2048]{1,0:T(8,128)(2,1)S(1)}, bf16[64,2048]{1,0:T(8,128)(2,1)S(1)}, u32[]{:S(2)}, u32[]{:S(2)}) collective-permute-start(bf16[64,2048]{1,0:T(8,128)(2,1)S(1)} %get-tuple-element.126), channel_id=1, source_target_pairs={{0,8},{8,16},{16,24},{24,28},{28,20},{20,12},{12,4},{4,0},{1,9},{9... | collective-permute-start | bytes 786440 | tf_op jit(solution)/shard_map/combine_return/ppermute | solution.py:75
  178.3 8.8 %collective-permute-start.33 = (bf16[64,2048]{1,0:T(8,128)(2,1)S(1)}, bf16[64,2048]{1,0:T(8,128)(2,1)S(1)}, u32[]{:S(2)}, u32[]{:S(2)}) collective-permute-start(bf16[64,2048]{1,0:T(8,128)(2,1)S(1)} %get-tuple-element.127), channel_id=1, source_target_pairs={{0,4},{8,0},{16,8},{24,16},{28,24},{20,28},{12,20},{4,12},{1,5},{9... | collective-permute-start | bytes 786440 | tf_op jit(solution)/shard_map/combine_return/ppermute | solution.py:75
  180.7 11.5 %collective-permute-start.22 = (bf16[64,2048]{1,0:T(8,128)(2,1)S(1)}, bf16[64,2048]{1,0:T(8,128)(2,1)S(1)}, u32[]{:S(2)}, u32[]{:S(2)}) collective-permute-start(bf16[64,2048]{1,0:T(8,128)(2,1)S(1)} %collective-permute-done.20), channel_id=1, source_target_pairs={{0,8},{8,16},{16,24},{24,28},{28,20},{20,12},{12,4},{4,0},{1,9},{9... | collective-permute-start | bytes 786440 | tf_op jit(solution)/shard_map/dispatch_gather/ppermute | solution.py:55
  182.5 10.1 %collective-permute-start.23 = (bf16[64,2048]{1,0:T(8,128)(2,1)S(1)}, bf16[64,2048]{1,0:T(8,128)(2,1)S(1)}, u32[]{:S(2)}, u32[]{:S(2)}) collective-permute-start(bf16[64,2048]{1,0:T(8,128)(2,1)S(1)} %collective-permute-done.21), channel_id=1, source_target_pairs={{0,4},{8,0},{16,8},{24,16},{28,24},{20,28},{12,20},{4,12},{1,5},{9... | collective-permute-start | bytes 786440 | tf_op jit(solution)/shard_map/dispatch_gather/ppermute | solution.py:55
  188.5 9.3 %collective-permute-start.34 = (bf16[64,2048]{1,0:T(8,128)(2,1)S(1)}, bf16[64,2048]{1,0:T(8,128)(2,1)S(1)}, u32[]{:S(2)}, u32[]{:S(2)}) collective-permute-start(bf16[64,2048]{1,0:T(8,128)(2,1)S(1)} %get-tuple-element.130), channel_id=1, source_target_pairs={{0,8},{8,16},{16,24},{24,28},{28,20},{20,12},{12,4},{4,0},{1,9},{9... | collective-permute-start | bytes 786440 | tf_op jit(solution)/shard_map/combine_return/ppermute | solution.py:75
  190.2 8.2 %collective-permute-start.35 = (bf16[64,2048]{1,0:T(8,128)(2,1)S(1)}, bf16[64,2048]{1,0:T(8,128)(2,1)S(1)}, u32[]{:S(2)}, u32[]{:S(2)}) collective-permute-start(bf16[64,2048]{1,0:T(8,128)(2,1)S(1)} %get-tuple-element.131), channel_id=1, source_target_pairs={{0,4},{8,0},{16,8},{24,16},{28,24},{20,28},{12,20},{4,12},{1,5},{9... | collective-permute-start | bytes 786440 | tf_op jit(solution)/shard_map/combine_return/ppermute | solution.py:75
  192.6 10.7 %collective-permute-start.24 = (bf16[64,2048]{1,0:T(8,128)(2,1)S(1)}, bf16[64,2048]{1,0:T(8,128)(2,1)S(1)}, u32[]{:S(2)}, u32[]{:S(2)}) collective-permute-start(bf16[64,2048]{1,0:T(8,128)(2,1)S(1)} %collective-permute-done.22), channel_id=1, source_target_pairs={{0,8},{8,16},{16,24},{24,28},{28,20},{20,12},{12,4},{4,0},{1,9},{9... | collective-permute-start | bytes 786440 | tf_op jit(solution)/shard_map/dispatch_gather/ppermute | solution.py:55
  194.4 9.4 %collective-permute-start.25 = (bf16[64,2048]{1,0:T(8,128)(2,1)S(1)}, bf16[64,2048]{1,0:T(8,128)(2,1)S(1)}, u32[]{:S(2)}, u32[]{:S(2)}) collective-permute-start(bf16[64,2048]{1,0:T(8,128)(2,1)S(1)} %collective-permute-done.23), channel_id=1, source_target_pairs={{0,4},{8,0},{16,8},{24,16},{28,24},{20,28},{12,20},{4,12},{1,5},{9... | collective-permute-start | bytes 786440 | tf_op jit(solution)/shard_map/dispatch_gather/ppermute | solution.py:55
  199.7 8.3 %collective-permute-start.36 = (bf16[64,2048]{1,0:T(8,128)(2,1)S(1)}, bf16[64,2048]{1,0:T(8,128)(2,1)S(1)}, u32[]{:S(2)}, u32[]{:S(2)}) collective-permute-start(bf16[64,2048]{1,0:T(8,128)(2,1)S(1)} %get-tuple-element.134), channel_id=1, source_target_pairs={{0,8},{8,16},{16,24},{24,28},{28,20},{20,12},{12,4},{4,0},{1,9},{9... | collective-permute-start | bytes 786440 | tf_op jit(solution)/shard_map/combine_return/ppermute | solution.py:75
  201.4 6.6 %collective-permute-start.37 = (bf16[64,2048]{1,0:T(8,128)(2,1)S(1)}, bf16[64,2048]{1,0:T(8,128)(2,1)S(1)}, u32[]{:S(2)}, u32[]{:S(2)}) collective-permute-start(bf16[64,2048]{1,0:T(8,128)(2,1)S(1)} %get-tuple-element.135), channel_id=1, source_target_pairs={{0,4},{8,0},{16,8},{24,16},{28,24},{20,28},{12,20},{4,12},{1,5},{9... | collective-permute-start | bytes 786440 | tf_op jit(solution)/shard_map/combine_return/ppermute | solution.py:75
  203.8 7.7 %collective-permute-start.26 = (bf16[64,2048]{1,0:T(8,128)(2,1)S(1)}, bf16[64,2048]{1,0:T(8,128)(2,1)S(1)}, u32[]{:S(2)}, u32[]{:S(2)}) collective-permute-start(bf16[64,2048]{1,0:T(8,128)(2,1)S(1)} %collective-permute-done.24), channel_id=1, source_target_pairs={{0,8},{8,16},{16,24},{24,28},{28,20},{20,12},{12,4},{4,0},{1,9},{9... | collective-permute-start | bytes 786440 | tf_op jit(solution)/shard_map/dispatch_gather/ppermute | solution.py:55
  205.6 7.9 %collective-permute-start.27 = (bf16[64,2048]{1,0:T(8,128)(2,1)S(1)}, bf16[64,2048]{1,0:T(8,128)(2,1)S(1)}, u32[]{:S(2)}, u32[]{:S(2)}) collective-permute-start(bf16[64,2048]{1,0:T(8,128)(2,1)S(1)} %collective-permute-done.25), channel_id=1, source_target_pairs={{0,4},{8,0},{16,8},{24,16},{28,24},{20,28},{12,20},{4,12},{1,5},{9... | collective-permute-start | bytes 786440 | tf_op jit(solution)/shard_map/dispatch_gather/ppermute | solution.py:55
  209.4 7.7 %collective-permute-start.38 = (bf16[64,2048]{1,0:T(8,128)(2,1)S(1)}, bf16[64,2048]{1,0:T(8,128)(2,1)S(1)}, u32[]{:S(2)}, u32[]{:S(2)}) collective-permute-start(bf16[64,2048]{1,0:T(8,128)(2,1)S(1)} %get-tuple-element.138), channel_id=1, source_target_pairs={{0,8},{8,16},{16,24},{24,28},{28,20},{20,12},{12,4},{4,0},{1,9},{9... | collective-permute-start | bytes 786440 | tf_op jit(solution)/shard_map/combine_return/ppermute | solution.py:75
  211.3 6.4 %collective-permute-start.39 = (bf16[64,2048]{1,0:T(8,128)(2,1)S(1)}, bf16[64,2048]{1,0:T(8,128)(2,1)S(1)}, u32[]{:S(2)}, u32[]{:S(2)}) collective-permute-start(bf16[64,2048]{1,0:T(8,128)(2,1)S(1)} %get-tuple-element.139), channel_id=1, source_target_pairs={{0,4},{8,0},{16,8},{24,16},{28,24},{20,28},{12,20},{4,12},{1,5},{9... | collective-permute-start | bytes 786440 | tf_op jit(solution)/shard_map/combine_return/ppermute | solution.py:75
  218.7 8.7 %copy-start.5 = (f32[2048]{0:T(1024)S(1)}, f32[2048]{0:T(1024)}, u32[]{:S(2)}) copy-start(f32[2048]{0:T(1024)} %param.20) | copy-start | bytes 24580
  218.7 9.8 %copy-start.1 = (bf16[512,2048]{1,0:T(8,128)(2,1)S(1)}, bf16[512,2048]{1,0:T(8,128)(2,1)}, u32[]{:S(2)}) copy-start(bf16[512,2048]{1,0:T(8,128)(2,1)} %param.14) | copy-start | bytes 6291460
  220.0 6.4 %collective-permute-start.40 = (bf16[64,2048]{1,0:T(8,128)(2,1)S(1)}, bf16[64,2048]{1,0:T(8,128)(2,1)S(1)}, u32[]{:S(2)}, u32[]{:S(2)}) collective-permute-start(bf16[64,2048]{1,0:T(8,128)(2,1)S(1)} %get-tuple-element.142), channel_id=1, source_target_pairs={{0,8},{8,16},{16,24},{24,28},{28,20},{20,12},{12,4},{4,0},{1,9},{9... | collective-permute-start | bytes 786440 | tf_op jit(solution)/shard_map/combine_return/ppermute | solution.py:75
  220.7 6.4 %collective-permute-start.41 = (bf16[64,2048]{1,0:T(8,128)(2,1)S(1)}, bf16[64,2048]{1,0:T(8,128)(2,1)S(1)}, u32[]{:S(2)}, u32[]{:S(2)}) collective-permute-start(bf16[64,2048]{1,0:T(8,128)(2,1)S(1)} %get-tuple-element.143), channel_id=1, source_target_pairs={{0,4},{8,0},{16,8},{24,16},{28,24},{20,28},{12,20},{4,12},{1,5},{9... | collective-permute-start | bytes 786440 | tf_op jit(solution)/shard_map/combine_return/ppermute | solution.py:75

commit v14 on v13

--- a/solution.py
+++ b/solution.py
@@ -145,7 +145,7 @@
 
     with jax.named_scope("local_experts"):
         steps_all = list(range(ep_size - 1))
-        chunks = [[step] for step in steps_all]
+        chunks = [steps_all[:1]] + [steps_all[i : i + 2] for i in range(1, ep_size - 1, 2)]
         pieces = [None] * (ep_size - 1)
         own_part = None
         for c, steps in enumerate(chunks):

time: 230 us -> 224 us (0.974)
  waiting for transfers between devices: 77.4 us -> 68.2 us
  matrix products: 30.8 us -> 35.7 us
    ppermute x7, waiting for transfers between devices: 29.6 us -> 11.8 us  [ring_reduce_scatter(): lax.ppermute(send_fwd, 'ep', forward)]
    ppermute x7, waiting for transfers between devices: 11 us -> 19 us  [ring_reduce_scatter_steps(): lax.ppermute(send_fwd, 'ep', forward)]
    dot_general x14 -> x8, matrix products: 18.9 us -> 24.7 us  [expert_mix(): projected_up = jnp.dot(rows, gate_up[e], preferred_element_type=jnp.float32)]
    ppermute x7, starting transfers between devices: 7.11 us -> 3.27 us  [ring_all_gather(): lax.ppermute(got_fwd, 'ep', forward)]
    ppermute x7, starting transfers between devices: 8.1 us -> 11.1 us  [ring_all_gather(): lax.ppermute(got_bwd, 'ep', backward)]
    ppermute x7, waiting for transfers between devices: 7.3 us -> 4.74 us  [ring_all_gather(): lax.ppermute(got_fwd, 'ep', forward)]
    dot_general x14 -> x8, matrix products: 9.56 us -> 8.63 us  [expert_mix(): jnp.dot(activated, down[e], preferred_element_type=jnp.float32)]
    unnamed x29 -> x42, local copies, waits for them, and re-layouts: 4.54 us -> 4.66 us
  transfers between devices with their start and end apart: 44 -> 44, of which waited for: 34 -> 32; matrix products, arithmetic and copies ran while one was open for 15% -> 17% of each run, Pallas kernels for 0% -> 0%
where the time goes in v14:
time: 224 us; the launch traced here: 223 us
  waiting for transfers between devices  68.2 us (30%)
  starting transfers between devices  54.3 us (24%)
  between operations  40.4 us (18%)
  matrix products  35.7 us (16%)
  other arithmetic  15.5 us (7%)
  local copies, waits for them, and re-layouts  8.77 us (4%)
    dot_general x8, matrix products, expert_mix(): projected_up = jnp.dot(rows, gate_up[e], preferred_element_type=jnp.float32)  24.7 us
    ppermute x7, waiting for transfers between devices, ring_reduce_scatter_steps(): lax.ppermute(send_fwd, 'ep', forward)  19 us
    ppermute x7, waiting for transfers between devices, ring_reduce_scatter(): lax.ppermute(send_fwd, 'ep', forward)  11.8 us
    ppermute x7, starting transfers between devices, ring_all_gather(): lax.ppermute(got_bwd, 'ep', backward)  11.1 us
    dot_general x8, matrix products, expert_mix(): jnp.dot(activated, down[e], preferred_element_type=jnp.float32)  8.63 us
    all_to_all x1, waiting for transfers between devices, body(): lax.all_to_all(columns, 'ep', split_axis=0, concat_axis=0, tiled=True)  8.62 us
    ppermute x7, starting transfers between devices, ring_reduce_scatter(): lax.ppermute(send_bwd, 'ep', backward)  7.99 us
    ppermute x7, starting transfers between devices, ring_reduce_scatter_steps(): lax.ppermute(send_bwd, 'ep', backward)  7.82 us
  transfers between devices with their start and end apart: 44, of which 32 were waited for; matrix products, arithmetic and copies ran while one was open for 17% of the time, Pallas kernels for 0%

profile of v14, /device:TPU:0, one launch (start us, length us, event | category | flops | bytes accessed | tf_op | source)
XLA Modules:
  0.0 222.8 jit_solution(12853325713738210929)
XLA Ops:
  0.7 1.5 select_reduce_fusion
  2.1 7.3 %all-to-all-start.1 = ((f32[8,128,2]{1,2,0:T(2,128)}), f32[8,128,2]{1,2,0:T(2,128)S(1)}, u32[]{:S(2)}, u32[]{:S(2)}) async-start(f32[8,128,2]{1,2,0:T(2,128)} %bitcast.2), calls=%async_computation.1 | async-start | bytes 16384 | tf_op jit(solution)/shard_map/route_weights/all_to_all | solution.py:118
  9.4 2.3 %copy.25 = bf16[16,8,8,512]{3,2,0,1:T(8,128)(2,1)} copy(bf16[16,8,8,512]{3,2,1,0:T(8,128)(2,1)} %bitcast.238) | data formatting | bytes 2097152 | tf_op jit(solution)/shard_map/out_projection/reshape | solution.py:122
  11.7 4.2 %all-to-all-done.1 = f32[8,128,2]{1,2,0:T(2,128)S(1)} async-done(((f32[8,128,2]{1,2,0:T(2,128)}), f32[8,128,2]{1,2,0:T(2,128)S(1)}, u32[]{:S(2)}, u32[]{:S(2)}) %all-to-all-start.1) | async-done | bytes 8224 | tf_op jit(solution)/shard_map/route_weights/all_to_all | solution.py:118
  15.9 3.6 %all-to-all-start = ((bf16[8,128,512]{2,1,0:T(8,128)(2,1)}), bf16[8,128,512]{2,1,0:T(8,128)(2,1)S(1)}, u32[]{:S(2)}, u32[]{:S(2)}) async-start(bf16[8,128,512]{2,1,0:T(8,128)(2,1)} %bitcast.236), calls=%async_computation | async-start | bytes 2097152 | tf_op jit(solution)/shard_map/out_projection/all_to_all | solution.py:123
  35.6 8.6 %all-to-all-done = bf16[8,128,512]{2,1,0:T(8,128)(2,1)S(1)} async-done(((bf16[8,128,512]{2,1,0:T(8,128)(2,1)}), bf16[8,128,512]{2,1,0:T(8,128)(2,1)S(1)}, u32[]{:S(2)}, u32[]{:S(2)}) %all-to-all-start) | async-done | bytes 1048608 | tf_op jit(solution)/shard_map/out_projection/all_to_all | solution.py:123
  44.2 2.3 %fusion.114 = f32[8,128,2048]{2,1,0:T(8,128)S(1)} fusion(bf16[8,128,512]{2,1,0:T(8,128)(2,1)S(1)} %all-to-all-done, bf16[512,2048]{1,0:T(8,128)(2,1)S(1)} %copy-done), kind=kOutput, calls=%fused_computation.65 | convolution fusion | flops 2147483648 | bytes 11534336 | tf_op jit(solution)/shard_map/out_projection/dot_general | solution.py:125
  46.6 3.3 %copy-done.2 = f32[8,128,2048]{2,1,0:T(8,128)} copy-done((f32[8,128,2048]{2,1,0:T(8,128)}, f32[8,128,2048]{2,1,0:T(8,128)S(1)}, u32[]{:S(2)}) %copy-start.2) | copy-done | bytes 8388632
  50.0 2.0 collective-permute-start.1
  56.6 1.3 fusion.162
  58.5 1.5 collective-permute-start.3
  64.4 2.1 collective-permute-done.3
  66.5 1.3 fusion.160
  67.8 1.8 collective-permute-start.4
  74.2 1.8 collective-permute-done.5
  76.0 1.3 fusion.158
  77.3 1.8 collective-permute-start.6
  83.7 1.9 collective-permute-done.7
  85.6 1.3 fusion.156
  87.5 1.5 collective-permute-start.9
  92.7 1.9 collective-permute-done.8
  95.2 1.3 fusion.154
  97.1 1.5 collective-permute-start.11
  102.4 3.1 %collective-permute-done.10 = bf16[64,2048]{1,0:T(8,128)(2,1)S(1)} collective-permute-done((bf16[64,2048]{1,0:T(8,128)(2,1)S(1)}, bf16[64,2048]{1,0:T(8,128)(2,1)S(1)}, u32[]{:S(2)}, u32[]{:S(2)}) %collective-permute-start.10) | collective-permute-done | bytes 262176 | tf_op jit(solution)/shard_map/out_projection/ppermute | solution.py:37
  106.3 1.3 fusion.152
  107.6 1.2 collective-permute-start.12
  111.6 4.4 %collective-permute-done.12 = bf16[64,2048]{1,0:T(8,128)(2,1)S(1)} collective-permute-done((bf16[64,2048]{1,0:T(8,128)(2,1)S(1)}, bf16[64,2048]{1,0:T(8,128)(2,1)S(1)}, u32[]{:S(2)}, u32[]{:S(2)}) %collective-permute-start.12) | collective-permute-done | bytes 262176 | tf_op jit(solution)/shard_map/out_projection/ppermute | solution.py:37
  116.5 1.3 fusion.175
  118.3 1.5 collective-permute-start.15
  120.5 5.3 %collective-permute-done.15 = bf16[64,2048]{1,0:T(8,128)(2,1)S(1)} collective-permute-done((bf16[64,2048]{1,0:T(8,128)(2,1)S(1)}, bf16[64,2048]{1,0:T(8,128)(2,1)S(1)}, u32[]{:S(2)}, u32[]{:S(2)}) %collective-permute-start.15) | collective-permute-done | bytes 262176 | tf_op jit(solution)/shard_map/dispatch_gather/ppermute | solution.py:55
  126.8 1.5 collective-permute-start.17
  128.4 3.9 %fusion = f32[128,1536]{1,0:T(8,128)S(1)} fusion(bf16[128,2048]{1,0:T(8,128)(2,1)S(1)} %constant_dynamic-update-slice_fusion.13, bf16[2,2048,1536]{2,1,0:T(8,128)(2,1)} %param.16), kind=kOutput, calls=%fused_computation | convolution fusion | flops 805306368 | bytes 7602176 | tf_op jit(solution)/shard_map/local_experts/dot_general | solution.py:87
  132.3 3.9 %fusion.8 = f32[128,1536]{1,0:T(8,128)S(1)} fusion(bf16[128,2048]{1,0:T(8,128)(2,1)S(1)} %constant_dynamic-update-slice_fusion.13, bf16[2,2048,1536]{2,1,0:T(8,128)(2,1)} %param.16), kind=kOutput, calls=%fused_computation.8 | convolution fusion | flops 805306368 | bytes 7602176 | tf_op jit(solution)/shard_map/local_experts/dot_general | solution.py:87
  138.3 1.4 collective-permute-start.29
  140.4 1.4 collective-permute-start.19
  141.8 5.0 %collective-permute-done.28 = bf16[64,2048]{1,0:T(8,128)(2,1)S(1)} collective-permute-done((bf16[64,2048]{1,0:T(8,128)(2,1)S(1)}, bf16[64,2048]{1,0:T(8,128)(2,1)S(1)}, u32[]{:S(2)}, u32[]{:S(2)}) %collective-permute-start.28) | collective-permute-done | bytes 262176 | tf_op jit(solution)/shard_map/combine_return/ppermute | solution.py:75
  147.5 2.9 %collective-permute-done.18 = bf16[64,2048]{1,0:T(8,128)(2,1)S(1)} collective-permute-done((bf16[64,2048]{1,0:T(8,128)(2,1)S(1)}, bf16[64,2048]{1,0:T(8,128)(2,1)S(1)}, u32[]{:S(2)}, u32[]{:S(2)}) %collective-permute-start.18) | collective-permute-done | bytes 262176 | tf_op jit(solution)/shard_map/dispatch_gather/ppermute | solution.py:55
  151.5 1.6 collective-permute-start.21
  153.2 1.8 fusion.2
  155.0 1.8 fusion.10
  159.6 1.6 collective-permute-start.31
  161.8 1.6 collective-permute-start.23
  163.4 3.1 %collective-permute-done.30 = bf16[64,2048]{1,0:T(8,128)(2,1)S(1)} collective-permute-done((bf16[64,2048]{1,0:T(8,128)(2,1)S(1)}, bf16[64,2048]{1,0:T(8,128)(2,1)S(1)}, u32[]{:S(2)}, u32[]{:S(2)}) %collective-permute-start.30) | collective-permute-done | bytes 262176 | tf_op jit(solution)/shard_map/combine_return/ppermute | solution.py:75
  167.8 1.6 collective-permute-start.33
  169.4 1.3 collective-permute-done.22
  170.7 1.2 collective-permute-done.23
  172.1 1.9 collective-permute-start.25
  174.0 1.8 fusion.4
  175.8 1.8 fusion.12
  181.1 1.7 collective-permute-start.35
  183.7 1.6 collective-permute-start.27
  185.3 2.2 collective-permute-done.34
  188.9 1.6 collective-permute-start.36
  192.3 4.8 %fusion.6 = f32[384,1536]{1,0:T(8,128)S(1)} fusion(bf16[384,2048]{1,0:T(8,128)(2,1)S(1)} %constant_dynamic-update-slice_fusion, bf16[2,2048,1536]{2,1,0:T(8,128)(2,1)} %param.16), kind=kOutput, calls=%fused_computation.6 | convolution fusion | flops 2415919104 | bytes 10223616 | tf_op jit(solution)/shard_map/local_experts/dot_general | solution.py:87
  197.1 4.8 %fusion.14 = f32[384,1536]{1,0:T(8,128)S(1)} fusion(bf16[384,2048]{1,0:T(8,128)(2,1)S(1)} %constant_dynamic-update-slice_fusion, bf16[2,2048,1536]{2,1,0:T(8,128)(2,1)} %param.16), kind=kOutput, calls=%fused_computation.14 | convolution fusion | flops 2415919104 | bytes 10223616 | tf_op jit(solution)/shard_map/local_experts/dot_general | solution.py:87
  202.0 1.4 fusion.40
  203.5 1.5 multiply_add_fusion
  205.2 1.6 collective-permute-start.38
  207.3 4.3 %collective-permute-done.38 = bf16[64,2048]{1,0:T(8,128)(2,1)S(1)} collective-permute-done((bf16[64,2048]{1,0:T(8,128)(2,1)S(1)}, bf16[64,2048]{1,0:T(8,128)(2,1)S(1)}, u32[]{:S(2)}, u32[]{:S(2)}) %collective-permute-start.38) | collective-permute-done | bytes 262176 | tf_op jit(solution)/shard_map/combine_return/ppermute | solution.py:75
  211.6 1.5 collective-permute-done.39
  213.3 1.5 collective-permute-start.40
  215.4 4.3 %collective-permute-done.40 = bf16[64,2048]{1,0:T(8,128)(2,1)S(1)} collective-permute-done((bf16[64,2048]{1,0:T(8,128)(2,1)S(1)}, bf16[64,2048]{1,0:T(8,128)(2,1)S(1)}, u32[]{:S(2)}, u32[]{:S(2)}) %collective-permute-start.40) | collective-permute-done | bytes 262176 | tf_op jit(solution)/shard_map/combine_return/ppermute | solution.py:75
  219.7 1.5 collective-permute-done.41
  221.5 1.2 multiply_convert_fusion
  (127 shorter events, 30.2 us)
Async XLA Ops:
  0.6 43.6 %copy-start = (bf16[512,2048]{1,0:T(8,128)(2,1)S(1)}, bf16[512,2048]{1,0:T(8,128)(2,1)}, u32[]{:S(2)}) copy-start(bf16[512,2048]{1,0:T(8,128)(2,1)} %param.14) | copy-start | bytes 6291460
  0.6 18.9 %copy-start.7 = (s32[8]{0:T(128)S(1)}, s32[8]{0:T(128)}, u32[]{:S(2)}) copy-start(s32[8]{0:T(128)} %constant.226.clone) | copy-start | bytes 100
  0.7 30.7 %copy-start.4 = (s32[8]{0:T(128)S(1)}, s32[8]{0:T(128)}, u32[]{:S(2)}) copy-start(s32[8]{0:T(128)} %constant.227.clone) | copy-start | bytes 100
  2.1 13.8 %all-to-all-start.1 = ((f32[8,128,2]{1,2,0:T(2,128)}), f32[8,128,2]{1,2,0:T(2,128)S(1)}, u32[]{:S(2)}, u32[]{:S(2)}) async-start(f32[8,128,2]{1,2,0:T(2,128)} %bitcast.2), calls=%async_computation.1 | async-start | bytes 16384 | tf_op jit(solution)/shard_map/route_weights/all_to_all | solution.py:118
  15.9 28.3 %all-to-all-start = ((bf16[8,128,512]{2,1,0:T(8,128)(2,1)}), bf16[8,128,512]{2,1,0:T(8,128)(2,1)S(1)}, u32[]{:S(2)}, u32[]{:S(2)}) async-start(bf16[8,128,512]{2,1,0:T(8,128)(2,1)} %bitcast.236), calls=%async_computation | async-start | bytes 2097152 | tf_op jit(solution)/shard_map/out_projection/all_to_all | solution.py:123
  46.6 3.3 %copy-start.2 = (f32[8,128,2048]{2,1,0:T(8,128)}, f32[8,128,2048]{2,1,0:T(8,128)S(1)}, u32[]{:S(2)}) copy-start(f32[8,128,2048]{2,1,0:T(8,128)S(1)} %fusion.114) | copy-start | bytes 25165828
  50.0 6.6 %collective-permute-start = (bf16[64,2048]{1,0:T(8,128)(2,1)S(1)}, bf16[64,2048]{1,0:T(8,128)(2,1)S(1)}, u32[]{:S(2)}, u32[]{:S(2)}) collective-permute-start(bf16[64,2048]{1,0:T(8,128)(2,1)S(1)} %get-tuple-element.75), channel_id=1, source_target_pairs={{0,8},{8,16},{16,24},{24,28},{28,20},{20,12},{12,4},{4,0},{1,9},{9... | collective-permute-start | bytes 786440 | tf_op jit(solution)/shard_map/out_projection/ppermute | solution.py:37
  50.0 6.6 %collective-permute-start.1 = (bf16[64,2048]{1,0:T(8,128)(2,1)S(1)}, bf16[64,2048]{1,0:T(8,128)(2,1)S(1)}, u32[]{:S(2)}, u32[]{:S(2)}) collective-permute-start(bf16[64,2048]{1,0:T(8,128)(2,1)S(1)} %get-tuple-element.76), channel_id=1, source_target_pairs={{0,4},{8,0},{16,8},{24,16},{28,24},{20,28},{12,20},{4,12},{1,5},{9... | collective-permute-start | bytes 786440 | tf_op jit(solution)/shard_map/out_projection/ppermute | solution.py:37
  57.9 6.4 %collective-permute-start.2 = (bf16[64,2048]{1,0:T(8,128)(2,1)S(1)}, bf16[64,2048]{1,0:T(8,128)(2,1)S(1)}, u32[]{:S(2)}, u32[]{:S(2)}) collective-permute-start(bf16[64,2048]{1,0:T(8,128)(2,1)S(1)} %get-tuple-element.79), channel_id=1, source_target_pairs={{0,8},{8,16},{16,24},{24,28},{28,20},{20,12},{12,4},{4,0},{1,9},{9... | collective-permute-start | bytes 786440 | tf_op jit(solution)/shard_map/out_projection/ppermute | solution.py:37
  58.5 7.9 %collective-permute-start.3 = (bf16[64,2048]{1,0:T(8,128)(2,1)S(1)}, bf16[64,2048]{1,0:T(8,128)(2,1)S(1)}, u32[]{:S(2)}, u32[]{:S(2)}) collective-permute-start(bf16[64,2048]{1,0:T(8,128)(2,1)S(1)} %get-tuple-element.80), channel_id=1, source_target_pairs={{0,4},{8,0},{16,8},{24,16},{28,24},{20,28},{12,20},{4,12},{1,5},{9... | collective-permute-start | bytes 786440 | tf_op jit(solution)/shard_map/out_projection/ppermute | solution.py:37
  67.8 6.4 %collective-permute-start.4 = (bf16[64,2048]{1,0:T(8,128)(2,1)S(1)}, bf16[64,2048]{1,0:T(8,128)(2,1)S(1)}, u32[]{:S(2)}, u32[]{:S(2)}) collective-permute-start(bf16[64,2048]{1,0:T(8,128)(2,1)S(1)} %get-tuple-element.83), channel_id=1, source_target_pairs={{0,8},{8,16},{16,24},{24,28},{28,20},{20,12},{12,4},{4,0},{1,9},{9... | collective-permute-start | bytes 786440 | tf_op jit(solution)/shard_map/out_projection/ppermute | solution.py:37
  69.6 6.4 %collective-permute-start.5 = (bf16[64,2048]{1,0:T(8,128)(2,1)S(1)}, bf16[64,2048]{1,0:T(8,128)(2,1)S(1)}, u32[]{:S(2)}, u32[]{:S(2)}) collective-permute-start(bf16[64,2048]{1,0:T(8,128)(2,1)S(1)} %get-tuple-element.84), channel_id=1, source_target_pairs={{0,4},{8,0},{16,8},{24,16},{28,24},{20,28},{12,20},{4,12},{1,5},{9... | collective-permute-start | bytes 786440 | tf_op jit(solution)/shard_map/out_projection/ppermute | solution.py:37
  77.3 6.4 %collective-permute-start.6 = (bf16[64,2048]{1,0:T(8,128)(2,1)S(1)}, bf16[64,2048]{1,0:T(8,128)(2,1)S(1)}, u32[]{:S(2)}, u32[]{:S(2)}) collective-permute-start(bf16[64,2048]{1,0:T(8,128)(2,1)S(1)} %get-tuple-element.87), channel_id=1, source_target_pairs={{0,8},{8,16},{16,24},{24,28},{28,20},{20,12},{12,4},{4,0},{1,9},{9... | collective-permute-start | bytes 786440 | tf_op jit(solution)/shard_map/out_projection/ppermute | solution.py:37
  79.1 6.6 %collective-permute-start.7 = (bf16[64,2048]{1,0:T(8,128)(2,1)S(1)}, bf16[64,2048]{1,0:T(8,128)(2,1)S(1)}, u32[]{:S(2)}, u32[]{:S(2)}) collective-permute-start(bf16[64,2048]{1,0:T(8,128)(2,1)S(1)} %get-tuple-element.88), channel_id=1, source_target_pairs={{0,4},{8,0},{16,8},{24,16},{28,24},{20,28},{12,20},{4,12},{1,5},{9... | collective-permute-start | bytes 786440 | tf_op jit(solution)/shard_map/out_projection/ppermute | solution.py:37
  86.9 7.7 %collective-permute-start.8 = (bf16[64,2048]{1,0:T(8,128)(2,1)S(1)}, bf16[64,2048]{1,0:T(8,128)(2,1)S(1)}, u32[]{:S(2)}, u32[]{:S(2)}) collective-permute-start(bf16[64,2048]{1,0:T(8,128)(2,1)S(1)} %get-tuple-element.91), channel_id=1, source_target_pairs={{0,8},{8,16},{16,24},{24,28},{28,20},{20,12},{12,4},{4,0},{1,9},{9... | collective-permute-start | bytes 786440 | tf_op jit(solution)/shard_map/out_projection/ppermute | solution.py:37
  87.5 7.8 %collective-permute-start.9 = (bf16[64,2048]{1,0:T(8,128)(2,1)S(1)}, bf16[64,2048]{1,0:T(8,128)(2,1)S(1)}, u32[]{:S(2)}, u32[]{:S(2)}) collective-permute-start(bf16[64,2048]{1,0:T(8,128)(2,1)S(1)} %get-tuple-element.92), channel_id=1, source_target_pairs={{0,4},{8,0},{16,8},{24,16},{28,24},{20,28},{12,20},{4,12},{1,5},{9... | collective-permute-start | bytes 786440 | tf_op jit(solution)/shard_map/out_projection/ppermute | solution.py:37
  96.5 9.0 %collective-permute-start.10 = (bf16[64,2048]{1,0:T(8,128)(2,1)S(1)}, bf16[64,2048]{1,0:T(8,128)(2,1)S(1)}, u32[]{:S(2)}, u32[]{:S(2)}) collective-permute-start(bf16[64,2048]{1,0:T(8,128)(2,1)S(1)} %get-tuple-element.95), channel_id=1, source_target_pairs={{0,8},{8,16},{16,24},{24,28},{28,20},{20,12},{12,4},{4,0},{1,9},{9... | collective-permute-start | bytes 786440 | tf_op jit(solution)/shard_map/out_projection/ppermute | solution.py:37
  97.1 9.2 %collective-permute-start.11 = (bf16[64,2048]{1,0:T(8,128)(2,1)S(1)}, bf16[64,2048]{1,0:T(8,128)(2,1)S(1)}, u32[]{:S(2)}, u32[]{:S(2)}) collective-permute-start(bf16[64,2048]{1,0:T(8,128)(2,1)S(1)} %get-tuple-element.96), channel_id=1, source_target_pairs={{0,4},{8,0},{16,8},{24,16},{28,24},{20,28},{12,20},{4,12},{1,5},{9... | collective-permute-start | bytes 786440 | tf_op jit(solution)/shard_map/out_projection/ppermute | solution.py:37
  102.4 15.4 %copy-start.3 = (bf16[128,2048]{1,0:T(8,128)(2,1)S(1)}, bf16[128,2048]{1,0:T(8,128)(2,1)}, u32[]{:S(2)}) copy-start(bf16[128,2048]{1,0:T(8,128)(2,1)} %param.12) | copy-start | bytes 1572868
  107.6 8.4 %collective-permute-start.12 = (bf16[64,2048]{1,0:T(8,128)(2,1)S(1)}, bf16[64,2048]{1,0:T(8,128)(2,1)S(1)}, u32[]{:S(2)}, u32[]{:S(2)}) collective-permute-start(bf16[64,2048]{1,0:T(8,128)(2,1)S(1)} %get-tuple-element.99), channel_id=1, source_target_pairs={{0,8},{8,16},{16,24},{24,28},{28,20},{20,12},{12,4},{4,0},{1,9},{9... | collective-permute-start | bytes 786440 | tf_op jit(solution)/shard_map/out_projection/ppermute | solution.py:37
  108.7 7.7 %collective-permute-start.13 = (bf16[64,2048]{1,0:T(8,128)(2,1)S(1)}, bf16[64,2048]{1,0:T(8,128)(2,1)S(1)}, u32[]{:S(2)}, u32[]{:S(2)}) collective-permute-start(bf16[64,2048]{1,0:T(8,128)(2,1)S(1)} %get-tuple-element.100), channel_id=1, source_target_pairs={{0,4},{8,0},{16,8},{24,16},{28,24},{20,28},{12,20},{4,12},{1,5},{9... | collective-permute-start | bytes 786440 | tf_op jit(solution)/shard_map/out_projection/ppermute | solution.py:37
  111.6 6.5 %copy-start.5 = (f32[2048]{0:T(1024)S(1)}, f32[2048]{0:T(1024)}, u32[]{:S(2)}) copy-start(f32[2048]{0:T(1024)} %param.15) | copy-start | bytes 24580
  118.3 7.4 %collective-permute-start.15 = (bf16[64,2048]{1,0:T(8,128)(2,1)S(1)}, bf16[64,2048]{1,0:T(8,128)(2,1)S(1)}, u32[]{:S(2)}, u32[]{:S(2)}) collective-permute-start(bf16[64,2048]{1,0:T(8,128)(2,1)S(1)} %get-tuple-element.184), channel_id=1, source_target_pairs={{0,4},{8,0},{16,8},{24,16},{28,24},{20,28},{12,20},{4,12},{1,5},{9... | collective-permute-start | bytes 786440 | tf_op jit(solution)/shard_map/dispatch_gather/ppermute | solution.py:55
  119.9 6.4 %collective-permute-start.14 = (bf16[64,2048]{1,0:T(8,128)(2,1)S(1)}, bf16[64,2048]{1,0:T(8,128)(2,1)S(1)}, u32[]{:S(2)}, u32[]{:S(2)}) collective-permute-start(bf16[64,2048]{1,0:T(8,128)(2,1)S(1)} %get-tuple-element.185), channel_id=1, source_target_pairs={{0,8},{8,16},{16,24},{24,28},{28,20},{20,12},{12,4},{4,0},{1,9},{9... | collective-permute-start | bytes 786440 | tf_op jit(solution)/shard_map/dispatch_gather/ppermute | solution.py:55
  126.2 13.5 %collective-permute-start.16 = (bf16[64,2048]{1,0:T(8,128)(2,1)S(1)}, bf16[64,2048]{1,0:T(8,128)(2,1)S(1)}, u32[]{:S(2)}, u32[]{:S(2)}) collective-permute-start(bf16[64,2048]{1,0:T(8,128)(2,1)S(1)} %collective-permute-done.14), channel_id=1, source_target_pairs={{0,8},{8,16},{16,24},{24,28},{28,20},{20,12},{12,4},{4,0},{1,9},{9... | collective-permute-start | bytes 786440 | tf_op jit(solution)/shard_map/dispatch_gather/ppermute | solution.py:55
  126.8 9.5 %slice-start.3 = ((s8[6291456]{0:T(1024)(128)(4,1)}), s8[4194304]{0:T(1024)(128)(4,1)S(1)}, s32[]{:S(2)}) async-start(s8[6291456]{0:T(1024)(128)(4,1)} %bitcast.263), calls=%async_computation.5 | async-start | bytes 8388608
  126.8 12.9 %collective-permute-start.17 = (bf16[64,2048]{1,0:T(8,128)(2,1)S(1)}, bf16[64,2048]{1,0:T(8,128)(2,1)S(1)}, u32[]{:S(2)}, u32[]{:S(2)}) collective-permute-start(bf16[64,2048]{1,0:T(8,128)(2,1)S(1)} %collective-permute-done.15), channel_id=1, source_target_pairs={{0,4},{8,0},{16,8},{24,16},{28,24},{20,28},{12,20},{4,12},{1,5},{9... | collective-permute-start | bytes 786440 | tf_op jit(solution)/shard_map/dispatch_gather/ppermute | solution.py:55
  128.4 7.9 %slice-start.4 = ((s8[6291456]{0:T(1024)(128)(4,1)}), s8[2097152]{0:T(1024)(128)(4,1)S(1)}, s32[]{:S(2)}) async-start(s8[6291456]{0:T(1024)(128)(4,1)} %bitcast.263), calls=%async_computation.6 | async-start | bytes 4194304
  132.3 20.8 %slice-start = ((s8[12582912]{0:T(1024)(128)(4,1)}), s8[4194304]{0:T(1024)(128)(4,1)S(1)}, s32[]{:S(2)}) async-start(s8[12582912]{0:T(1024)(128)(4,1)} %bitcast.261), calls=%async_computation.2 | async-start | bytes 8388608
  132.3 20.8 %slice-start.1 = ((s8[12582912]{0:T(1024)(128)(4,1)}), s8[4194304]{0:T(1024)(128)(4,1)S(1)}, s32[]{:S(2)}) async-start(s8[12582912]{0:T(1024)(128)(4,1)} %bitcast.261), calls=%async_computation.3 | async-start | bytes 8388608
  136.9 16.3 %slice-start.2 = ((s8[12582912]{0:T(1024)(128)(4,1)}), s8[4194304]{0:T(1024)(128)(4,1)S(1)}, s32[]{:S(2)}) async-start(s8[12582912]{0:T(1024)(128)(4,1)} %bitcast.261), calls=%async_computation.4 | async-start | bytes 8388608
  137.6 9.2 %collective-permute-start.28 = (bf16[64,2048]{1,0:T(8,128)(2,1)S(1)}, bf16[64,2048]{1,0:T(8,128)(2,1)S(1)}, u32[]{:S(2)}, u32[]{:S(2)}) collective-permute-start(bf16[64,2048]{1,0:T(8,128)(2,1)S(1)} %get-tuple-element.118), channel_id=1, source_target_pairs={{0,8},{8,16},{16,24},{24,28},{28,20},{20,12},{12,4},{4,0},{1,9},{9... | collective-permute-start | bytes 786440 | tf_op jit(solution)/shard_map/combine_return/ppermute | solution.py:75
  138.3 9.1 %collective-permute-start.29 = (bf16[64,2048]{1,0:T(8,128)(2,1)S(1)}, bf16[64,2048]{1,0:T(8,128)(2,1)S(1)}, u32[]{:S(2)}, u32[]{:S(2)}) collective-permute-start(bf16[64,2048]{1,0:T(8,128)(2,1)S(1)} %get-tuple-element.119), channel_id=1, source_target_pairs={{0,4},{8,0},{16,8},{24,16},{28,24},{20,28},{12,20},{4,12},{1,5},{9... | collective-permute-start | bytes 786440 | tf_op jit(solution)/shard_map/combine_return/ppermute | solution.py:75
  139.7 10.7 %collective-permute-start.18 = (bf16[64,2048]{1,0:T(8,128)(2,1)S(1)}, bf16[64,2048]{1,0:T(8,128)(2,1)S(1)}, u32[]{:S(2)}, u32[]{:S(2)}) collective-permute-start(bf16[64,2048]{1,0:T(8,128)(2,1)S(1)} %collective-permute-done.16), channel_id=1, source_target_pairs={{0,8},{8,16},{16,24},{24,28},{28,20},{20,12},{12,4},{4,0},{1,9},{9... | collective-permute-start | bytes 786440 | tf_op jit(solution)/shard_map/dispatch_gather/ppermute | solution.py:55
  140.4 10.6 %collective-permute-start.19 = (bf16[64,2048]{1,0:T(8,128)(2,1)S(1)}, bf16[64,2048]{1,0:T(8,128)(2,1)S(1)}, u32[]{:S(2)}, u32[]{:S(2)}) collective-permute-start(bf16[64,2048]{1,0:T(8,128)(2,1)S(1)} %collective-permute-done.17), channel_id=1, source_target_pairs={{0,4},{8,0},{16,8},{24,16},{28,24},{20,28},{12,20},{4,12},{1,5},{9... | collective-permute-start | bytes 786440 | tf_op jit(solution)/shard_map/dispatch_gather/ppermute | solution.py:55
  151.1 10.2 %collective-permute-start.20 = (bf16[64,2048]{1,0:T(8,128)(2,1)S(1)}, bf16[64,2048]{1,0:T(8,128)(2,1)S(1)}, u32[]{:S(2)}, u32[]{:S(2)}) collective-permute-start(bf16[64,2048]{1,0:T(8,128)(2,1)S(1)} %collective-permute-done.18), channel_id=1, source_target_pairs={{0,8},{8,16},{16,24},{24,28},{28,20},{20,12},{12,4},{4,0},{1,9},{9... | collective-permute-start | bytes 786440 | tf_op jit(solution)/shard_map/dispatch_gather/ppermute | solution.py:55
  151.5 9.8 %collective-permute-start.21 = (bf16[64,2048]{1,0:T(8,128)(2,1)S(1)}, bf16[64,2048]{1,0:T(8,128)(2,1)S(1)}, u32[]{:S(2)}, u32[]{:S(2)}) collective-permute-start(bf16[64,2048]{1,0:T(8,128)(2,1)S(1)} %collective-permute-done.19), channel_id=1, source_target_pairs={{0,4},{8,0},{16,8},{24,16},{28,24},{20,28},{12,20},{4,12},{1,5},{9... | collective-permute-start | bytes 786440 | tf_op jit(solution)/shard_map/dispatch_gather/ppermute | solution.py:55
  159.1 7.4 %collective-permute-start.30 = (bf16[64,2048]{1,0:T(8,128)(2,1)S(1)}, bf16[64,2048]{1,0:T(8,128)(2,1)S(1)}, u32[]{:S(2)}, u32[]{:S(2)}) collective-permute-start(bf16[64,2048]{1,0:T(8,128)(2,1)S(1)} %get-tuple-element.122), channel_id=1, source_target_pairs={{0,8},{8,16},{16,24},{24,28},{28,20},{20,12},{12,4},{4,0},{1,9},{9... | collective-permute-start | bytes 786440 | tf_op jit(solution)/shard_map/combine_return/ppermute | solution.py:75
  159.6 7.5 %collective-permute-start.31 = (bf16[64,2048]{1,0:T(8,128)(2,1)S(1)}, bf16[64,2048]{1,0:T(8,128)(2,1)S(1)}, u32[]{:S(2)}, u32[]{:S(2)}) collective-permute-start(bf16[64,2048]{1,0:T(8,128)(2,1)S(1)} %get-tuple-element.123), channel_id=1, source_target_pairs={{0,4},{8,0},{16,8},{24,16},{28,24},{20,28},{12,20},{4,12},{1,5},{9... | collective-permute-start | bytes 786440 | tf_op jit(solution)/shard_map/combine_return/ppermute | solution.py:75
  161.3 9.4 %collective-permute-start.22 = (bf16[64,2048]{1,0:T(8,128)(2,1)S(1)}, bf16[64,2048]{1,0:T(8,128)(2,1)S(1)}, u32[]{:S(2)}, u32[]{:S(2)}) collective-permute-start(bf16[64,2048]{1,0:T(8,128)(2,1)S(1)} %collective-permute-done.20), channel_id=1, source_target_pairs={{0,8},{8,16},{16,24},{24,28},{28,20},{20,12},{12,4},{4,0},{1,9},{9... | collective-permute-start | bytes 786440 | tf_op jit(solution)/shard_map/dispatch_gather/ppermute | solution.py:55
  161.8 10.1 %collective-permute-start.23 = (bf16[64,2048]{1,0:T(8,128)(2,1)S(1)}, bf16[64,2048]{1,0:T(8,128)(2,1)S(1)}, u32[]{:S(2)}, u32[]{:S(2)}) collective-permute-start(bf16[64,2048]{1,0:T(8,128)(2,1)S(1)} %collective-permute-done.21), channel_id=1, source_target_pairs={{0,4},{8,0},{16,8},{24,16},{28,24},{20,28},{12,20},{4,12},{1,5},{9... | collective-permute-start | bytes 786440 | tf_op jit(solution)/shard_map/dispatch_gather/ppermute | solution.py:55
  167.3 10.4 %collective-permute-start.32 = (bf16[64,2048]{1,0:T(8,128)(2,1)S(1)}, bf16[64,2048]{1,0:T(8,128)(2,1)S(1)}, u32[]{:S(2)}, u32[]{:S(2)}) collective-permute-start(bf16[64,2048]{1,0:T(8,128)(2,1)S(1)} %get-tuple-element.126), channel_id=1, source_target_pairs={{0,8},{8,16},{16,24},{24,28},{28,20},{20,12},{12,4},{4,0},{1,9},{9... | collective-permute-start | bytes 786440 | tf_op jit(solution)/shard_map/combine_return/ppermute | solution.py:75
  167.8 9.9 %collective-permute-start.33 = (bf16[64,2048]{1,0:T(8,128)(2,1)S(1)}, bf16[64,2048]{1,0:T(8,128)(2,1)S(1)}, u32[]{:S(2)}, u32[]{:S(2)}) collective-permute-start(bf16[64,2048]{1,0:T(8,128)(2,1)S(1)} %get-tuple-element.127), channel_id=1, source_target_pairs={{0,4},{8,0},{16,8},{24,16},{28,24},{20,28},{12,20},{4,12},{1,5},{9... | collective-permute-start | bytes 786440 | tf_op jit(solution)/shard_map/combine_return/ppermute | solution.py:75
  172.0 11.0 %collective-permute-start.24 = (bf16[64,2048]{1,0:T(8,128)(2,1)S(1)}, bf16[64,2048]{1,0:T(8,128)(2,1)S(1)}, u32[]{:S(2)}, u32[]{:S(2)}) collective-permute-start(bf16[64,2048]{1,0:T(8,128)(2,1)S(1)} %collective-permute-done.22), channel_id=1, source_target_pairs={{0,8},{8,16},{16,24},{24,28},{28,20},{20,12},{12,4},{4,0},{1,9},{9... | collective-permute-start | bytes 786440 | tf_op jit(solution)/shard_map/dispatch_gather/ppermute | solution.py:55
  172.1 11.2 %collective-permute-start.25 = (bf16[64,2048]{1,0:T(8,128)(2,1)S(1)}, bf16[64,2048]{1,0:T(8,128)(2,1)}, u32[]{:S(2)}, u32[]{:S(2)}) collective-permute-start(bf16[64,2048]{1,0:T(8,128)(2,1)S(1)} %collective-permute-done.23), channel_id=1, source_target_pairs={{0,4},{8,0},{16,8},{24,16},{28,24},{20,28},{12,20},{4,12},{1,5},{9... | collective-permute-start | bytes 786440 | tf_op jit(solution)/shard_map/dispatch_gather/ppermute | solution.py:55
  180.8 6.7 %collective-permute-start.34 = (bf16[64,2048]{1,0:T(8,128)(2,1)}, bf16[64,2048]{1,0:T(8,128)(2,1)}, u32[]{:S(2)}, u32[]{:S(2)}) collective-permute-start(bf16[64,2048]{1,0:T(8,128)(2,1)} %get-tuple-element.130), channel_id=1, source_target_pairs={{0,8},{8,16},{16,24},{24,28},{28,20},{20,12},{12,4},{4,0},{1,9},{9... | collective-permute-start | bytes 786440 | tf_op jit(solution)/shard_map/combine_return/ppermute | solution.py:75
  181.1 6.7 %collective-permute-start.35 = (bf16[64,2048]{1,0:T(8,128)(2,1)}, bf16[64,2048]{1,0:T(8,128)(2,1)}, u32[]{:S(2)}, u32[]{:S(2)}) collective-permute-start(bf16[64,2048]{1,0:T(8,128)(2,1)} %get-tuple-element.131), channel_id=1, source_target_pairs={{0,4},{8,0},{16,8},{24,16},{28,24},{20,28},{12,20},{4,12},{1,5},{9... | collective-permute-start | bytes 786440 | tf_op jit(solution)/shard_map/combine_return/ppermute | solution.py:75
  183.3 8.7 %collective-permute-start.26 = (bf16[64,2048]{1,0:T(8,128)(2,1)S(1)}, bf16[64,2048]{1,0:T(8,128)(2,1)S(1)}, u32[]{:S(2)}, u32[]{:S(2)}) collective-permute-start(bf16[64,2048]{1,0:T(8,128)(2,1)S(1)} %collective-permute-done.24), channel_id=1, source_target_pairs={{0,8},{8,16},{16,24},{24,28},{28,20},{20,12},{12,4},{4,0},{1,9},{9... | collective-permute-start | bytes 786440 | tf_op jit(solution)/shard_map/dispatch_gather/ppermute | solution.py:55
  183.7 8.3 %collective-permute-start.27 = (bf16[64,2048]{1,0:T(8,128)(2,1)}, bf16[64,2048]{1,0:T(8,128)(2,1)S(1)}, u32[]{:S(2)}, u32[]{:S(2)}) collective-permute-start(bf16[64,2048]{1,0:T(8,128)(2,1)} %collective-permute-done.25), channel_id=1, source_target_pairs={{0,4},{8,0},{16,8},{24,16},{28,24},{20,28},{12,20},{4,12},{1,5},{9... | collective-permute-start | bytes 786440 | tf_op jit(solution)/shard_map/dispatch_gather/ppermute | solution.py:55
  188.9 13.0 %collective-permute-start.36 = (bf16[64,2048]{1,0:T(8,128)(2,1)S(1)}, bf16[64,2048]{1,0:T(8,128)(2,1)S(1)}, u32[]{:S(2)}, u32[]{:S(2)}) collective-permute-start(bf16[64,2048]{1,0:T(8,128)(2,1)S(1)} %get-tuple-element.134), channel_id=1, source_target_pairs={{0,8},{8,16},{16,24},{24,28},{28,20},{20,12},{12,4},{4,0},{1,9},{9... | collective-permute-start | bytes 786440 | tf_op jit(solution)/shard_map/combine_return/ppermute | solution.py:75
  190.5 11.5 %collective-permute-start.37 = (bf16[64,2048]{1,0:T(8,128)(2,1)S(1)}, bf16[64,2048]{1,0:T(8,128)(2,1)S(1)}, u32[]{:S(2)}, u32[]{:S(2)}) collective-permute-start(bf16[64,2048]{1,0:T(8,128)(2,1)S(1)} %get-tuple-element.135), channel_id=1, source_target_pairs={{0,4},{8,0},{16,8},{24,16},{28,24},{20,28},{12,20},{4,12},{1,5},{9... | collective-permute-start | bytes 786440 | tf_op jit(solution)/shard_map/combine_return/ppermute | solution.py:75
  192.3 9.7 %slice-start.5 = ((s8[6291456]{0:T(1024)(128)(4,1)}), s8[4194304]{0:T(1024)(128)(4,1)S(1)}, s32[]{:S(2)}) async-start(s8[6291456]{0:T(1024)(128)(4,1)} %bitcast.265), calls=%async_computation.7 | async-start | bytes 8388608
  197.1 4.9 %slice-start.6 = ((s8[6291456]{0:T(1024)(128)(4,1)}), s8[2097152]{0:T(1024)(128)(4,1)S(1)}, s32[]{:S(2)}) async-start(s8[6291456]{0:T(1024)(128)(4,1)} %bitcast.265), calls=%async_computation.8 | async-start | bytes 4194304
  205.2 6.4 %collective-permute-start.38 = (bf16[64,2048]{1,0:T(8,128)(2,1)S(1)}, bf16[64,2048]{1,0:T(8,128)(2,1)S(1)}, u32[]{:S(2)}, u32[]{:S(2)}) collective-permute-start(bf16[64,2048]{1,0:T(8,128)(2,1)S(1)} %get-tuple-element.138), channel_id=1, source_target_pairs={{0,8},{8,16},{16,24},{24,28},{28,20},{20,12},{12,4},{4,0},{1,9},{9... | collective-permute-start | bytes 786440 | tf_op jit(solution)/shard_map/combine_return/ppermute | solution.py:75
  206.8 6.4 %collective-permute-start.39 = (bf16[64,2048]{1,0:T(8,128)(2,1)S(1)}, bf16[64,2048]{1,0:T(8,128)(2,1)S(1)}, u32[]{:S(2)}, u32[]{:S(2)}) collective-permute-start(bf16[64,2048]{1,0:T(8,128)(2,1)S(1)} %get-tuple-element.139), channel_id=1, source_target_pairs={{0,4},{8,0},{16,8},{24,16},{28,24},{20,28},{12,20},{4,12},{1,5},{9... | collective-permute-start | bytes 786440 | tf_op jit(solution)/shard_map/combine_return/ppermute | solution.py:75
  213.3 8.3 %copy-start.6 = (f32[2048]{0:T(1024)S(1)}, f32[2048]{0:T(1024)}, u32[]{:S(2)}) copy-start(f32[2048]{0:T(1024)} %param.20) | copy-start | bytes 24580
  213.3 6.4 %collective-permute-start.40 = (bf16[64,2048]{1,0:T(8,128)(2,1)S(1)}, bf16[64,2048]{1,0:T(8,128)(2,1)S(1)}, u32[]{:S(2)}, u32[]{:S(2)}) collective-permute-start(bf16[64,2048]{1,0:T(8,128)(2,1)S(1)} %get-tuple-element.142), channel_id=1, source_target_pairs={{0,8},{8,16},{16,24},{24,28},{28,20},{20,12},{12,4},{4,0},{1,9},{9... | collective-permute-start | bytes 786440 | tf_op jit(solution)/shard_map/combine_return/ppermute | solution.py:75
  214.8 6.4 %collective-permute-start.41 = (bf16[64,2048]{1,0:T(8,128)(2,1)S(1)}, bf16[64,2048]{1,0:T(8,128)(2,1)S(1)}, u32[]{:S(2)}, u32[]{:S(2)}) collective-permute-start(bf16[64,2048]{1,0:T(8,128)(2,1)S(1)} %get-tuple-element.143), channel_id=1, source_target_pairs={{0,4},{8,0},{16,8},{24,16},{28,24},{20,28},{12,20},{4,12},{1,5},{9... | collective-permute-start | bytes 786440 | tf_op jit(solution)/shard_map/combine_return/ppermute | solution.py:75
  221.2 1.6 copy-start.1

commit v15 on v9

--- a/solution.py
+++ b/solution.py
@@ -122,10 +122,27 @@
         columns = attn_out.reshape(row_count, ep_size, slice_width).transpose(1, 0, 2)
         columns = lax.all_to_all(columns, "ep", split_axis=0, concat_axis=0, tiled=True)
         columns, row_weights = lax.optimization_barrier((columns, row_weights))
-        partial = jnp.dot(
-            columns.reshape(group_rows, slice_width), out_weight, preferred_element_type=jnp.float32
-        )
-        projected = ring_reduce_scatter(partial.reshape(ep_size, row_count, model_width), ring, pos)
+        ring_index = jnp.array(ring, dtype=jnp.int32)
+        half = row_count // 2
+        pieces = []
+        for step in range(ep_size - 1):
+            owner_fwd = ring_index[(pos - 1 - step) % ep_size]
+            owner_bwd = ring_index[(pos + 1 + step) % ep_size]
+            rows_in = jnp.concatenate(
+                [
+                    lax.dynamic_index_in_dim(columns, owner_fwd, 0, keepdims=False)[:half],
+                    lax.dynamic_index_in_dim(columns, owner_bwd, 0, keepdims=False)[half:],
+                ],
+                axis=0,
+            )
+            part = jnp.dot(rows_in, out_weight, preferred_element_type=jnp.float32)
+            pieces.append((part[:half], part[half:]))
+        own_part = jnp.dot(
+            lax.dynamic_index_in_dim(columns, me, 0, keepdims=False),
+            out_weight,
+            preferred_element_type=jnp.float32,
+        )
+        projected = ring_reduce_scatter_steps(pieces, own_part, ring)
         middle = (residual.astype(jnp.float32) + projected).astype(jnp.bfloat16)
 
     normed = rms_scale(middle.astype(jnp.float32), post_gain).astype(jnp.bfloat16)

time: 220 us -> 226 us (1.027)
  waiting for transfers between devices: 69.3 us -> 93.2 us
  other arithmetic: 13.6 us -> 5.13 us
  matrix products: 30.8 us -> 27 us
  between operations: 40.4 us -> 37 us
  local copies, waits for them, and re-layouts: 8.18 us -> 5.16 us
    ppermute x7 -> x14, waiting for transfers between devices: 17.1 us -> 50.6 us  [ring_reduce_scatter_steps(): lax.ppermute(send_fwd, 'ep', forward)]
    ppermute x14 -> x0, waiting for transfers between devices: 19.4 us -> none  [the longest x7 11.6 us: ring_reduce_scatter(): lax.ppermute(send_fwd, 'ep', forward)]
    ppermute x14 -> x0, starting transfers between devices: 14.5 us -> none  [the longest x7 7.41 us: ring_reduce_scatter(): lax.ppermute(send_bwd, 'ep', backward)]
    ppermute x7 -> x14, starting transfers between devices: 6.45 us -> 18.8 us  [ring_reduce_scatter_steps(): lax.ppermute(send_fwd, 'ep', forward)]
    ppermute x7 -> x14, waiting for transfers between devices: 3.89 us -> 14.5 us  [ring_reduce_scatter_steps(): lax.ppermute(send_bwd, 'ep', backward)]
    ppermute x7, waiting for transfers between devices: 9.08 us -> 17.8 us  [ring_all_gather(): lax.ppermute(got_fwd, 'ep', forward)]
    all_to_all x1, waiting for transfers between devices: 8.34 us -> 0.01 us  [body(): lax.all_to_all(columns, 'ep', split_axis=0, concat_axis=0, tiled=True)]
    convert_element_type x6 -> x0, other arithmetic: 7.85 us -> none  [ring_reduce_scatter(): send_bwd.astype(jnp.bfloat16)]
  transfers between devices with their start and end apart: 44 -> 44, of which waited for: 34 -> 32; matrix products, arithmetic and copies ran while one was open for 15% -> 12% of each run, Pallas kernels for 0% -> 0%
where the time goes in v15:
time: 226 us; the launch traced here: 225 us
  waiting for transfers between devices  93.2 us (41%)
  starting transfers between devices  57.5 us (25%)
  between operations  37 us (16%)
  matrix products  27 us (12%)
  local copies, waits for them, and re-layouts  5.16 us (2%)
  other arithmetic  5.13 us (2%)
    ppermute x14, waiting for transfers between devices, ring_reduce_scatter_steps(): lax.ppermute(send_fwd, 'ep', forward)  50.6 us
    ppermute x14, starting transfers between devices, ring_reduce_scatter_steps(): lax.ppermute(send_fwd, 'ep', forward)  18.8 us
    ppermute x7, waiting for transfers between devices, ring_all_gather(): lax.ppermute(got_fwd, 'ep', forward)  17.8 us
    ppermute x14, waiting for transfers between devices, ring_reduce_scatter_steps(): lax.ppermute(send_bwd, 'ep', backward)  14.5 us
    dot_general x8, matrix products, expert_mix(): projected_up = jnp.dot(rows, gate_up[e], preferred_element_type=jnp.float32)  14.2 us
    ppermute x14, starting transfers between devices, ring_reduce_scatter_steps(): lax.ppermute(send_bwd, 'ep', backward)  11 us
    ppermute x7, starting transfers between devices, ring_all_gather(): lax.ppermute(got_fwd, 'ep', forward)  10.1 us
    dot_general x8, matrix products, expert_mix(): jnp.dot(activated, down[e], preferred_element_type=jnp.float32)  8.53 us
  transfers between devices with their start and end apart: 44, of which 32 were waited for; matrix products, arithmetic and copies ran while one was open for 12% of the time, Pallas kernels for 0%

profile of v15, /device:TPU:0, one launch (start us, length us, event | category | flops | bytes accessed | tf_op | source)
XLA Modules:
  0.0 225.0 jit_solution(15467788622411045310)
XLA Ops:
  0.6 1.5 select_reduce_fusion
  2.1 7.3 %all-to-all-start.1 = ((f32[8,128,2]{1,2,0:T(2,128)}), f32[8,128,2]{1,2,0:T(2,128)S(1)}, u32[]{:S(2)}, u32[]{:S(2)}) async-start(f32[8,128,2]{1,2,0:T(2,128)} %bitcast.3), calls=%async_computation.1 | async-start | bytes 16384 | tf_op jit(solution)/shard_map/route_weights/all_to_all | solution.py:118
  9.4 2.3 %copy.43 = bf16[128,4096]{0,1:T(8,128)(2,1)} copy(bf16[128,4096]{1,0:T(8,128)(2,1)} %param.13) | data formatting | bytes 2097152 | tf_op args[1]
  11.7 4.2 %all-to-all-done.1 = f32[8,128,2]{1,2,0:T(2,128)S(1)} async-done(((f32[8,128,2]{1,2,0:T(2,128)}), f32[8,128,2]{1,2,0:T(2,128)S(1)}, u32[]{:S(2)}, u32[]{:S(2)}) %all-to-all-start.1) | async-done | bytes 8224 | tf_op jit(solution)/shard_map/route_weights/all_to_all | solution.py:118
  15.9 3.6 %all-to-all-start = ((bf16[8,128,512]{1,2,0:T(8,128)(2,1)}), bf16[8,128,512]{1,2,0:T(8,128)(2,1)S(1)}, u32[]{:S(2)}, u32[]{:S(2)}) async-start(bf16[8,128,512]{1,2,0:T(8,128)(2,1)} %bitcast.204), calls=%async_computation | async-start | bytes 2097152 | tf_op jit(solution)/shard_map/out_projection/all_to_all | solution.py:123
  58.2 2.0 collective-permute-start
  61.0 3.9 %collective-permute-done = bf16[64,2048]{1,0:T(8,128)(2,1)S(1)} collective-permute-done((bf16[64,2048]{1,0:T(8,128)(2,1)S(1)}, bf16[64,2048]{1,0:T(8,128)(2,1)S(1)}, u32[]{:S(2)}, u32[]{:S(2)}) %collective-permute-start) | collective-permute-done | bytes 262176 | tf_op jit(solution)/shard_map/out_projection/ppermute | solution.py:75
  64.9 1.7 collective-permute-done.1
  66.7 1.5 collective-permute-start.2
  69.3 3.8 %collective-permute-done.2 = bf16[64,2048]{1,0:T(8,128)(2,1)S(1)} collective-permute-done((bf16[64,2048]{1,0:T(8,128)(2,1)S(1)}, bf16[64,2048]{1,0:T(8,128)(2,1)S(1)}, u32[]{:S(2)}, u32[]{:S(2)}) %collective-permute-start.2) | collective-permute-done | bytes 262176 | tf_op jit(solution)/shard_map/out_projection/ppermute | solution.py:75
  73.1 1.6 collective-permute-done.3
  74.8 1.5 collective-permute-start.4
  77.4 5.0 %collective-permute-done.4 = bf16[64,2048]{1,0:T(8,128)(2,1)S(1)} collective-permute-done((bf16[64,2048]{1,0:T(8,128)(2,1)S(1)}, bf16[64,2048]{1,0:T(8,128)(2,1)S(1)}, u32[]{:S(2)}, u32[]{:S(2)}) %collective-permute-start.4) | collective-permute-done | bytes 262176 | tf_op jit(solution)/shard_map/out_projection/ppermute | solution.py:75
  82.4 3.0 %collective-permute-done.5 = bf16[64,2048]{1,0:T(8,128)(2,1)S(1)} collective-permute-done((bf16[64,2048]{1,0:T(8,128)(2,1)S(1)}, bf16[64,2048]{1,0:T(8,128)(2,1)S(1)}, u32[]{:S(2)}, u32[]{:S(2)}) %collective-permute-start.5) | collective-permute-done | bytes 262176 | tf_op jit(solution)/shard_map/out_projection/ppermute | solution.py:75
  85.5 2.6 %collective-permute-start.6 = (bf16[64,2048]{1,0:T(8,128)(2,1)S(1)}, bf16[64,2048]{1,0:T(8,128)(2,1)S(1)}, u32[]{:S(2)}, u32[]{:S(2)}) collective-permute-start(bf16[64,2048]{1,0:T(8,128)(2,1)S(1)} %get-tuple-element.87), channel_id=1, source_target_pairs={{0,8},{8,16},{16,24},{24,28},{28,20},{20,12},{12,4},{4,0},{1,9},{9... | collective-permute-start | bytes 786440 | tf_op jit(solution)/shard_map/out_projection/ppermute | solution.py:75
  88.7 5.6 %collective-permute-done.6 = bf16[64,2048]{1,0:T(8,128)(2,1)S(1)} collective-permute-done((bf16[64,2048]{1,0:T(8,128)(2,1)S(1)}, bf16[64,2048]{1,0:T(8,128)(2,1)S(1)}, u32[]{:S(2)}, u32[]{:S(2)}) %collective-permute-start.6) | collective-permute-done | bytes 262176 | tf_op jit(solution)/shard_map/out_projection/ppermute | solution.py:75
  94.3 1.9 collective-permute-done.7
  97.1 1.3 collective-permute-start.9
  98.9 4.6 %collective-permute-done.8 = bf16[64,2048]{1,0:T(8,128)(2,1)S(1)} collective-permute-done((bf16[64,2048]{1,0:T(8,128)(2,1)S(1)}, bf16[64,2048]{1,0:T(8,128)(2,1)S(1)}, u32[]{:S(2)}, u32[]{:S(2)}) %collective-permute-start.8) | collective-permute-done | bytes 262176 | tf_op jit(solution)/shard_map/out_projection/ppermute | solution.py:75
  104.7 1.4 collective-permute-start.11
  106.7 3.8 %collective-permute-done.10 = bf16[64,2048]{1,0:T(8,128)(2,1)S(1)} collective-permute-done((bf16[64,2048]{1,0:T(8,128)(2,1)S(1)}, bf16[64,2048]{1,0:T(8,128)(2,1)S(1)}, u32[]{:S(2)}, u32[]{:S(2)}) %collective-permute-start.10) | collective-permute-done | bytes 262176 | tf_op jit(solution)/shard_map/out_projection/ppermute | solution.py:75
  111.8 1.5 collective-permute-start.13
  113.4 5.5 %collective-permute-done.12 = bf16[64,2048]{1,0:T(8,128)(2,1)S(1)} collective-permute-done((bf16[64,2048]{1,0:T(8,128)(2,1)S(1)}, bf16[64,2048]{1,0:T(8,128)(2,1)S(1)}, u32[]{:S(2)}, u32[]{:S(2)}) %collective-permute-start.12) | collective-permute-done | bytes 262176 | tf_op jit(solution)/shard_map/out_projection/ppermute | solution.py:75
  119.9 2.1 collective-permute-start.15
  122.1 4.2 %collective-permute-done.14 = bf16[64,2048]{1,0:T(8,128)(2,1)S(1)} collective-permute-done((bf16[64,2048]{1,0:T(8,128)(2,1)S(1)}, bf16[64,2048]{1,0:T(8,128)(2,1)S(1)}, u32[]{:S(2)}, u32[]{:S(2)}) %collective-permute-start.14) | collective-permute-done | bytes 262176 | tf_op jit(solution)/shard_map/dispatch_gather/ppermute | solution.py:55
  126.5 1.9 collective-permute-start.17
  128.4 6.2 %collective-permute-done.16 = bf16[64,2048]{1,0:T(8,128)(2,1)S(1)} collective-permute-done((bf16[64,2048]{1,0:T(8,128)(2,1)S(1)}, bf16[64,2048]{1,0:T(8,128)(2,1)S(1)}, u32[]{:S(2)}, u32[]{:S(2)}) %collective-permute-start.16) | collective-permute-done | bytes 262176 | tf_op jit(solution)/shard_map/dispatch_gather/ppermute | solution.py:55
  135.1 1.8 fusion
  136.9 1.8 fusion.8
  138.7 2.3 %collective-permute-start.18 = (bf16[64,2048]{1,0:T(8,128)(2,1)S(1)}, bf16[64,2048]{1,0:T(8,128)(2,1)S(1)}, u32[]{:S(2)}, u32[]{:S(2)}) collective-permute-start(bf16[64,2048]{1,0:T(8,128)(2,1)S(1)} %collective-permute-done.16), channel_id=1, source_target_pairs={{0,8},{8,16},{16,24},{24,28},{28,20},{20,12},{12,4},{4,0},{1,9},{9... | collective-permute-start | bytes 786440 | tf_op jit(solution)/shard_map/dispatch_gather/ppermute | solution.py:55
  141.2 1.0 fusion.121
  142.3 1.1 fusion.242
  143.4 2.3 %collective-permute-start.28 = (bf16[64,2048]{1,0:T(8,128)(2,1)S(1)}, bf16[64,2048]{1,0:T(8,128)(2,1)S(1)}, u32[]{:S(2)}, u32[]{:S(2)}) collective-permute-start(bf16[64,2048]{1,0:T(8,128)(2,1)S(1)} %get-tuple-element.118), channel_id=1, source_target_pairs={{0,8},{8,16},{16,24},{24,28},{28,20},{20,12},{12,4},{4,0},{1,9},{9... | collective-permute-start | bytes 786440 | tf_op jit(solution)/shard_map/combine_return/ppermute | solution.py:75
  145.8 4.7 %collective-permute-done.28 = bf16[64,2048]{1,0:T(8,128)(2,1)S(1)} collective-permute-done((bf16[64,2048]{1,0:T(8,128)(2,1)S(1)}, bf16[64,2048]{1,0:T(8,128)(2,1)S(1)}, u32[]{:S(2)}, u32[]{:S(2)}) %collective-permute-start.28) | collective-permute-done | bytes 262176 | tf_op jit(solution)/shard_map/combine_return/ppermute | solution.py:75
  150.5 2.6 %collective-permute-done.29 = bf16[64,2048]{1,0:T(8,128)(2,1)S(1)} collective-permute-done((bf16[64,2048]{1,0:T(8,128)(2,1)S(1)}, bf16[64,2048]{1,0:T(8,128)(2,1)S(1)}, u32[]{:S(2)}, u32[]{:S(2)}) %collective-permute-start.29) | collective-permute-done | bytes 262176 | tf_op jit(solution)/shard_map/combine_return/ppermute | solution.py:75
  153.1 3.7 %collective-permute-start.20 = (bf16[64,2048]{1,0:T(8,128)(2,1)S(1)}, bf16[64,2048]{1,0:T(8,128)(2,1)S(1)}, u32[]{:S(2)}, u32[]{:S(2)}) collective-permute-start(bf16[64,2048]{1,0:T(8,128)(2,1)S(1)} %collective-permute-done.18), channel_id=1, source_target_pairs={{0,8},{8,16},{16,24},{24,28},{28,20},{20,12},{12,4},{4,0},{1,9},{9... | collective-permute-start | bytes 786440 | tf_op jit(solution)/shard_map/dispatch_gather/ppermute | solution.py:55
  157.0 2.1 collective-permute-start.30
  159.1 2.6 %collective-permute-done.20 = bf16[64,2048]{1,0:T(8,128)(2,1)S(1)} collective-permute-done((bf16[64,2048]{1,0:T(8,128)(2,1)S(1)}, bf16[64,2048]{1,0:T(8,128)(2,1)S(1)}, u32[]{:S(2)}, u32[]{:S(2)}) %collective-permute-start.20) | collective-permute-done | bytes 262176 | tf_op jit(solution)/shard_map/dispatch_gather/ppermute | solution.py:55
  161.7 2.8 %collective-permute-done.21 = bf16[64,2048]{1,0:T(8,128)(2,1)S(1)} collective-permute-done((bf16[64,2048]{1,0:T(8,128)(2,1)S(1)}, bf16[64,2048]{1,0:T(8,128)(2,1)S(1)}, u32[]{:S(2)}, u32[]{:S(2)}) %collective-permute-start.21) | collective-permute-done | bytes 262176 | tf_op jit(solution)/shard_map/dispatch_gather/ppermute | solution.py:55
  164.5 1.8 fusion.2
  166.3 1.8 fusion.10
  168.9 1.3 collective-permute-start.23
  170.2 1.0 fusion.112
  171.3 1.1 fusion.73
  173.5 1.1 collective-permute-start.33
  174.7 7.1 %collective-permute-done.32 = bf16[64,2048]{1,0:T(8,128)(2,1)S(1)} collective-permute-done((bf16[64,2048]{1,0:T(8,128)(2,1)S(1)}, bf16[64,2048]{1,0:T(8,128)(2,1)S(1)}, u32[]{:S(2)}, u32[]{:S(2)}) %collective-permute-start.32) | collective-permute-done | bytes 262176 | tf_op jit(solution)/shard_map/combine_return/ppermute | solution.py:75
  182.8 2.0 collective-permute-start.24
  184.9 2.1 collective-permute-start.34
  187.0 4.7 %collective-permute-done.24 = bf16[64,2048]{1,0:T(8,128)(2,1)S(1)} collective-permute-done((bf16[64,2048]{1,0:T(8,128)(2,1)S(1)}, bf16[64,2048]{1,0:T(8,128)(2,1)S(1)}, u32[]{:S(2)}, u32[]{:S(2)}) %collective-permute-start.24) | collective-permute-done | bytes 262176 | tf_op jit(solution)/shard_map/dispatch_gather/ppermute | solution.py:55
  191.8 2.1 collective-permute-done.25
  193.9 1.8 fusion.4
  195.7 1.8 fusion.12
  198.5 1.1 collective-permute-start.27
  199.6 1.0 fusion.103
  200.6 1.1 fusion.61
  202.8 1.1 collective-permute-start.37
  204.8 1.8 fusion.14
  206.6 1.8 fusion.6
  209.7 1.7 collective-permute-start.39
  212.4 1.1 fusion.49
  213.5 2.2 collective-permute-done.38
  216.5 1.7 collective-permute-start.41
  218.3 4.3 %collective-permute-done.40 = bf16[64,2048]{1,0:T(8,128)(2,1)S(1)} collective-permute-done((bf16[64,2048]{1,0:T(8,128)(2,1)S(1)}, bf16[64,2048]{1,0:T(8,128)(2,1)S(1)}, u32[]{:S(2)}, u32[]{:S(2)}) %collective-permute-start.40) | collective-permute-done | bytes 262176 | tf_op jit(solution)/shard_map/combine_return/ppermute | solution.py:75
  223.3 1.2 multiply_convert_fusion
  (125 shorter events, 24.0 us)
Async XLA Ops:
  0.6 56.0 %copy-start = (bf16[512,2048]{1,0:T(8,128)(2,1)S(1)}, bf16[512,2048]{1,0:T(8,128)(2,1)}, u32[]{:S(2)}) copy-start(bf16[512,2048]{1,0:T(8,128)(2,1)} %param.14) | copy-start | bytes 6291460
  2.1 13.8 %all-to-all-start.1 = ((f32[8,128,2]{1,2,0:T(2,128)}), f32[8,128,2]{1,2,0:T(2,128)S(1)}, u32[]{:S(2)}, u32[]{:S(2)}) async-start(f32[8,128,2]{1,2,0:T(2,128)} %bitcast.3), calls=%async_computation.1 | async-start | bytes 16384 | tf_op jit(solution)/shard_map/route_weights/all_to_all | solution.py:118
  9.4 10.1 %copy-start.6 = (s32[8]{0:T(128)S(1)}, s32[8]{0:T(128)}, u32[]{:S(2)}) copy-start(s32[8]{0:T(128)} %constant.239.clone) | copy-start | bytes 100
  9.4 20.0 %copy-start.3 = (s32[8]{0:T(128)S(1)}, s32[8]{0:T(128)}, u32[]{:S(2)}) copy-start(s32[8]{0:T(128)} %constant.240.clone) | copy-start | bytes 100
  15.9 40.7 %all-to-all-start = ((bf16[8,128,512]{1,2,0:T(8,128)(2,1)}), bf16[8,128,512]{1,2,0:T(8,128)(2,1)S(1)}, u32[]{:S(2)}, u32[]{:S(2)}) async-start(bf16[8,128,512]{1,2,0:T(8,128)(2,1)} %bitcast.204), calls=%async_computation | async-start | bytes 2097152 | tf_op jit(solution)/shard_map/out_projection/all_to_all | solution.py:123
  58.2 6.7 %collective-permute-start = (bf16[64,2048]{1,0:T(8,128)(2,1)S(1)}, bf16[64,2048]{1,0:T(8,128)(2,1)S(1)}, u32[]{:S(2)}, u32[]{:S(2)}) collective-permute-start(bf16[64,2048]{1,0:T(8,128)(2,1)S(1)} %get-tuple-element.75), channel_id=1, source_target_pairs={{0,8},{8,16},{16,24},{24,28},{28,20},{20,12},{12,4},{4,0},{1,9},{9... | collective-permute-start | bytes 786440 | tf_op jit(solution)/shard_map/out_projection/ppermute | solution.py:75
  60.2 6.4 %collective-permute-start.1 = (bf16[64,2048]{1,0:T(8,128)(2,1)S(1)}, bf16[64,2048]{1,0:T(8,128)(2,1)S(1)}, u32[]{:S(2)}, u32[]{:S(2)}) collective-permute-start(bf16[64,2048]{1,0:T(8,128)(2,1)S(1)} %get-tuple-element.76), channel_id=1, source_target_pairs={{0,4},{8,0},{16,8},{24,16},{28,24},{20,28},{12,20},{4,12},{1,5},{9... | collective-permute-start | bytes 786440 | tf_op jit(solution)/shard_map/out_projection/ppermute | solution.py:75
  66.7 6.4 %collective-permute-start.2 = (bf16[64,2048]{1,0:T(8,128)(2,1)S(1)}, bf16[64,2048]{1,0:T(8,128)(2,1)S(1)}, u32[]{:S(2)}, u32[]{:S(2)}) collective-permute-start(bf16[64,2048]{1,0:T(8,128)(2,1)S(1)} %get-tuple-element.79), channel_id=1, source_target_pairs={{0,8},{8,16},{16,24},{24,28},{28,20},{20,12},{12,4},{4,0},{1,9},{9... | collective-permute-start | bytes 786440 | tf_op jit(solution)/shard_map/out_projection/ppermute | solution.py:75
  68.2 6.5 %collective-permute-start.3 = (bf16[64,2048]{1,0:T(8,128)(2,1)S(1)}, bf16[64,2048]{1,0:T(8,128)(2,1)S(1)}, u32[]{:S(2)}, u32[]{:S(2)}) collective-permute-start(bf16[64,2048]{1,0:T(8,128)(2,1)S(1)} %get-tuple-element.80), channel_id=1, source_target_pairs={{0,4},{8,0},{16,8},{24,16},{28,24},{20,28},{12,20},{4,12},{1,5},{9... | collective-permute-start | bytes 786440 | tf_op jit(solution)/shard_map/out_projection/ppermute | solution.py:75
  74.8 7.6 %collective-permute-start.4 = (bf16[64,2048]{1,0:T(8,128)(2,1)S(1)}, bf16[64,2048]{1,0:T(8,128)(2,1)S(1)}, u32[]{:S(2)}, u32[]{:S(2)}) collective-permute-start(bf16[64,2048]{1,0:T(8,128)(2,1)S(1)} %get-tuple-element.83), channel_id=1, source_target_pairs={{0,8},{8,16},{16,24},{24,28},{28,20},{20,12},{12,4},{4,0},{1,9},{9... | collective-permute-start | bytes 786440 | tf_op jit(solution)/shard_map/out_projection/ppermute | solution.py:75
  76.3 9.1 %collective-permute-start.5 = (bf16[64,2048]{1,0:T(8,128)(2,1)S(1)}, bf16[64,2048]{1,0:T(8,128)(2,1)S(1)}, u32[]{:S(2)}, u32[]{:S(2)}) collective-permute-start(bf16[64,2048]{1,0:T(8,128)(2,1)S(1)} %get-tuple-element.84), channel_id=1, source_target_pairs={{0,4},{8,0},{16,8},{24,16},{28,24},{20,28},{12,20},{4,12},{1,5},{9... | collective-permute-start | bytes 786440 | tf_op jit(solution)/shard_map/out_projection/ppermute | solution.py:75
  85.5 8.7 %collective-permute-start.6 = (bf16[64,2048]{1,0:T(8,128)(2,1)S(1)}, bf16[64,2048]{1,0:T(8,128)(2,1)S(1)}, u32[]{:S(2)}, u32[]{:S(2)}) collective-permute-start(bf16[64,2048]{1,0:T(8,128)(2,1)S(1)} %get-tuple-element.87), channel_id=1, source_target_pairs={{0,8},{8,16},{16,24},{24,28},{28,20},{20,12},{12,4},{4,0},{1,9},{9... | collective-permute-start | bytes 786440 | tf_op jit(solution)/shard_map/out_projection/ppermute | solution.py:75
  88.1 8.0 %collective-permute-start.7 = (bf16[64,2048]{1,0:T(8,128)(2,1)S(1)}, bf16[64,2048]{1,0:T(8,128)(2,1)S(1)}, u32[]{:S(2)}, u32[]{:S(2)}) collective-permute-start(bf16[64,2048]{1,0:T(8,128)(2,1)S(1)} %get-tuple-element.88), channel_id=1, source_target_pairs={{0,4},{8,0},{16,8},{24,16},{28,24},{20,28},{12,20},{4,12},{1,5},{9... | collective-permute-start | bytes 786440 | tf_op jit(solution)/shard_map/out_projection/ppermute | solution.py:75
  88.1 46.9 %slice-start = ((s8[12582912]{0:T(1024)(128)(4,1)}), s8[4194304]{0:T(1024)(128)(4,1)S(1)}, s32[]{:S(2)}) async-start(s8[12582912]{0:T(1024)(128)(4,1)} %bitcast.231), calls=%async_computation.2 | async-start | bytes 8388608
  96.3 7.2 %collective-permute-start.8 = (bf16[64,2048]{1,0:T(8,128)(2,1)S(1)}, bf16[64,2048]{1,0:T(8,128)(2,1)S(1)}, u32[]{:S(2)}, u32[]{:S(2)}) collective-permute-start(bf16[64,2048]{1,0:T(8,128)(2,1)S(1)} %get-tuple-element.91), channel_id=1, source_target_pairs={{0,8},{8,16},{16,24},{24,28},{28,20},{20,12},{12,4},{4,0},{1,9},{9... | collective-permute-start | bytes 786440 | tf_op jit(solution)/shard_map/out_projection/ppermute | solution.py:75
  97.1 6.9 %collective-permute-start.9 = (bf16[64,2048]{1,0:T(8,128)(2,1)S(1)}, bf16[64,2048]{1,0:T(8,128)(2,1)S(1)}, u32[]{:S(2)}, u32[]{:S(2)}) collective-permute-start(bf16[64,2048]{1,0:T(8,128)(2,1)S(1)} %get-tuple-element.92), channel_id=1, source_target_pairs={{0,4},{8,0},{16,8},{24,16},{28,24},{20,28},{12,20},{4,12},{1,5},{9... | collective-permute-start | bytes 786440 | tf_op jit(solution)/shard_map/out_projection/ppermute | solution.py:75
  98.3 36.7 %slice-start.1 = ((s8[12582912]{0:T(1024)(128)(4,1)}), s8[4194304]{0:T(1024)(128)(4,1)S(1)}, s32[]{:S(2)}) async-start(s8[12582912]{0:T(1024)(128)(4,1)} %bitcast.231), calls=%async_computation.3 | async-start | bytes 8388608
  104.1 6.4 %collective-permute-start.10 = (bf16[64,2048]{1,0:T(8,128)(2,1)S(1)}, bf16[64,2048]{1,0:T(8,128)(2,1)S(1)}, u32[]{:S(2)}, u32[]{:S(2)}) collective-permute-start(bf16[64,2048]{1,0:T(8,128)(2,1)S(1)} %get-tuple-element.95), channel_id=1, source_target_pairs={{0,8},{8,16},{16,24},{24,28},{28,20},{20,12},{12,4},{4,0},{1,9},{9... | collective-permute-start | bytes 786440 | tf_op jit(solution)/shard_map/out_projection/ppermute | solution.py:75
  104.7 6.4 %collective-permute-start.11 = (bf16[64,2048]{1,0:T(8,128)(2,1)S(1)}, bf16[64,2048]{1,0:T(8,128)(2,1)S(1)}, u32[]{:S(2)}, u32[]{:S(2)}) collective-permute-start(bf16[64,2048]{1,0:T(8,128)(2,1)S(1)} %get-tuple-element.96), channel_id=1, source_target_pairs={{0,4},{8,0},{16,8},{24,16},{28,24},{20,28},{12,20},{4,12},{1,5},{9... | collective-permute-start | bytes 786440 | tf_op jit(solution)/shard_map/out_projection/ppermute | solution.py:75
  106.7 12.6 %copy-start.2 = (bf16[128,2048]{1,0:T(8,128)(2,1)S(1)}, bf16[128,2048]{1,0:T(8,128)(2,1)}, u32[]{:S(2)}) copy-start(bf16[128,2048]{1,0:T(8,128)(2,1)} %param.12) | copy-start | bytes 1572868
  111.2 7.7 %collective-permute-start.12 = (bf16[64,2048]{1,0:T(8,128)(2,1)S(1)}, bf16[64,2048]{1,0:T(8,128)(2,1)S(1)}, u32[]{:S(2)}, u32[]{:S(2)}) collective-permute-start(bf16[64,2048]{1,0:T(8,128)(2,1)S(1)} %get-tuple-element.99), channel_id=1, source_target_pairs={{0,8},{8,16},{16,24},{24,28},{28,20},{20,12},{12,4},{4,0},{1,9},{9... | collective-permute-start | bytes 786440 | tf_op jit(solution)/shard_map/out_projection/ppermute | solution.py:75
  111.8 7.3 %collective-permute-start.13 = (bf16[64,2048]{1,0:T(8,128)(2,1)S(1)}, bf16[64,2048]{1,0:T(8,128)(2,1)S(1)}, u32[]{:S(2)}, u32[]{:S(2)}) collective-permute-start(bf16[64,2048]{1,0:T(8,128)(2,1)S(1)} %get-tuple-element.100), channel_id=1, source_target_pairs={{0,4},{8,0},{16,8},{24,16},{28,24},{20,28},{12,20},{4,12},{1,5},{9... | collective-permute-start | bytes 786440 | tf_op jit(solution)/shard_map/out_projection/ppermute | solution.py:75
  113.4 6.2 %copy-start.4 = (f32[2048]{0:T(1024)S(1)}, f32[2048]{0:T(1024)}, u32[]{:S(2)}) copy-start(f32[2048]{0:T(1024)} %param.15) | copy-start | bytes 24580
  113.4 21.7 %slice-start.2 = ((s8[12582912]{0:T(1024)(128)(4,1)}), s8[4194304]{0:T(1024)(128)(4,1)S(1)}, s32[]{:S(2)}) async-start(s8[12582912]{0:T(1024)(128)(4,1)} %bitcast.231), calls=%async_computation.4 | async-start | bytes 8388608
  119.8 6.5 %collective-permute-start.14 = (bf16[64,2048]{1,0:T(8,128)(2,1)S(1)}, bf16[64,2048]{1,0:T(8,128)(2,1)S(1)}, u32[]{:S(2)}, u32[]{:S(2)}) collective-permute-start(bf16[64,2048]{1,0:T(8,128)(2,1)S(1)} %get-tuple-element.195), channel_id=1, source_target_pairs={{0,8},{8,16},{16,24},{24,28},{28,20},{20,12},{12,4},{4,0},{1,9},{9... | collective-permute-start | bytes 786440 | tf_op jit(solution)/shard_map/dispatch_gather/ppermute | solution.py:55
  119.9 6.4 %collective-permute-start.15 = (bf16[64,2048]{1,0:T(8,128)(2,1)S(1)}, bf16[64,2048]{1,0:T(8,128)(2,1)S(1)}, u32[]{:S(2)}, u32[]{:S(2)}) collective-permute-start(bf16[64,2048]{1,0:T(8,128)(2,1)S(1)} %get-tuple-element.194), channel_id=1, source_target_pairs={{0,4},{8,0},{16,8},{24,16},{28,24},{20,28},{12,20},{4,12},{1,5},{9... | collective-permute-start | bytes 786440 | tf_op jit(solution)/shard_map/dispatch_gather/ppermute | solution.py:55
  126.3 8.4 %collective-permute-start.16 = (bf16[64,2048]{1,0:T(8,128)(2,1)S(1)}, bf16[64,2048]{1,0:T(8,128)(2,1)S(1)}, u32[]{:S(2)}, u32[]{:S(2)}) collective-permute-start(bf16[64,2048]{1,0:T(8,128)(2,1)S(1)} %collective-permute-done.14), channel_id=1, source_target_pairs={{0,8},{8,16},{16,24},{24,28},{28,20},{20,12},{12,4},{4,0},{1,9},{9... | collective-permute-start | bytes 786440 | tf_op jit(solution)/shard_map/dispatch_gather/ppermute | solution.py:55
  126.5 8.5 %collective-permute-start.17 = (bf16[64,2048]{1,0:T(8,128)(2,1)S(1)}, bf16[64,2048]{1,0:T(8,128)(2,1)S(1)}, u32[]{:S(2)}, u32[]{:S(2)}) collective-permute-start(bf16[64,2048]{1,0:T(8,128)(2,1)S(1)} %collective-permute-done.15), channel_id=1, source_target_pairs={{0,4},{8,0},{16,8},{24,16},{28,24},{20,28},{12,20},{4,12},{1,5},{9... | collective-permute-start | bytes 786440 | tf_op jit(solution)/shard_map/dispatch_gather/ppermute | solution.py:55
  135.1 6.2 %slice-start.3 = ((s8[6291456]{0:T(1024)(128)(4,1)}), s8[4194304]{0:T(1024)(128)(4,1)S(1)}, s32[]{:S(2)}) async-start(s8[6291456]{0:T(1024)(128)(4,1)} %bitcast.233), calls=%async_computation.5 | async-start | bytes 8388608
  136.9 4.4 %slice-start.4 = ((s8[6291456]{0:T(1024)(128)(4,1)}), s8[2097152]{0:T(1024)(128)(4,1)S(1)}, s32[]{:S(2)}) async-start(s8[6291456]{0:T(1024)(128)(4,1)} %bitcast.233), calls=%async_computation.6 | async-start | bytes 4194304
  138.7 14.4 %collective-permute-start.18 = (bf16[64,2048]{1,0:T(8,128)(2,1)S(1)}, bf16[64,2048]{1,0:T(8,128)(2,1)S(1)}, u32[]{:S(2)}, u32[]{:S(2)}) collective-permute-start(bf16[64,2048]{1,0:T(8,128)(2,1)S(1)} %collective-permute-done.16), channel_id=1, source_target_pairs={{0,8},{8,16},{16,24},{24,28},{28,20},{20,12},{12,4},{4,0},{1,9},{9... | collective-permute-start | bytes 786440 | tf_op jit(solution)/shard_map/dispatch_gather/ppermute | solution.py:55
  141.0 12.1 %collective-permute-start.19 = (bf16[64,2048]{1,0:T(8,128)(2,1)S(1)}, bf16[64,2048]{1,0:T(8,128)(2,1)S(1)}, u32[]{:S(2)}, u32[]{:S(2)}) collective-permute-start(bf16[64,2048]{1,0:T(8,128)(2,1)S(1)} %collective-permute-done.17), channel_id=1, source_target_pairs={{0,4},{8,0},{16,8},{24,16},{28,24},{20,28},{12,20},{4,12},{1,5},{9... | collective-permute-start | bytes 786440 | tf_op jit(solution)/shard_map/dispatch_gather/ppermute | solution.py:55
  143.4 7.1 %collective-permute-start.28 = (bf16[64,2048]{1,0:T(8,128)(2,1)S(1)}, bf16[64,2048]{1,0:T(8,128)(2,1)S(1)}, u32[]{:S(2)}, u32[]{:S(2)}) collective-permute-start(bf16[64,2048]{1,0:T(8,128)(2,1)S(1)} %get-tuple-element.118), channel_id=1, source_target_pairs={{0,8},{8,16},{16,24},{24,28},{28,20},{20,12},{12,4},{4,0},{1,9},{9... | collective-permute-start | bytes 786440 | tf_op jit(solution)/shard_map/combine_return/ppermute | solution.py:75
  145.7 7.4 %collective-permute-start.29 = (bf16[64,2048]{1,0:T(8,128)(2,1)S(1)}, bf16[64,2048]{1,0:T(8,128)(2,1)S(1)}, u32[]{:S(2)}, u32[]{:S(2)}) collective-permute-start(bf16[64,2048]{1,0:T(8,128)(2,1)S(1)} %get-tuple-element.119), channel_id=1, source_target_pairs={{0,4},{8,0},{16,8},{24,16},{28,24},{20,28},{12,20},{4,12},{1,5},{9... | collective-permute-start | bytes 786440 | tf_op jit(solution)/shard_map/combine_return/ppermute | solution.py:75
  153.1 8.6 %collective-permute-start.20 = (bf16[64,2048]{1,0:T(8,128)(2,1)S(1)}, bf16[64,2048]{1,0:T(8,128)(2,1)S(1)}, u32[]{:S(2)}, u32[]{:S(2)}) collective-permute-start(bf16[64,2048]{1,0:T(8,128)(2,1)S(1)} %collective-permute-done.18), channel_id=1, source_target_pairs={{0,8},{8,16},{16,24},{24,28},{28,20},{20,12},{12,4},{4,0},{1,9},{9... | collective-permute-start | bytes 786440 | tf_op jit(solution)/shard_map/dispatch_gather/ppermute | solution.py:55
  156.8 7.7 %collective-permute-start.21 = (bf16[64,2048]{1,0:T(8,128)(2,1)S(1)}, bf16[64,2048]{1,0:T(8,128)(2,1)S(1)}, u32[]{:S(2)}, u32[]{:S(2)}) collective-permute-start(bf16[64,2048]{1,0:T(8,128)(2,1)S(1)} %collective-permute-done.19), channel_id=1, source_target_pairs={{0,4},{8,0},{16,8},{24,16},{28,24},{20,28},{12,20},{4,12},{1,5},{9... | collective-permute-start | bytes 786440 | tf_op jit(solution)/shard_map/dispatch_gather/ppermute | solution.py:55
  157.0 13.2 %collective-permute-start.30 = (bf16[64,2048]{1,0:T(8,128)(2,1)S(1)}, bf16[64,2048]{1,0:T(8,128)(2,1)S(1)}, u32[]{:S(2)}, u32[]{:S(2)}) collective-permute-start(bf16[64,2048]{1,0:T(8,128)(2,1)S(1)} %get-tuple-element.122), channel_id=1, source_target_pairs={{0,8},{8,16},{16,24},{24,28},{28,20},{20,12},{12,4},{4,0},{1,9},{9... | collective-permute-start | bytes 786440 | tf_op jit(solution)/shard_map/combine_return/ppermute | solution.py:75
  159.1 11.1 %collective-permute-start.31 = (bf16[64,2048]{1,0:T(8,128)(2,1)S(1)}, bf16[64,2048]{1,0:T(8,128)(2,1)S(1)}, u32[]{:S(2)}, u32[]{:S(2)}) collective-permute-start(bf16[64,2048]{1,0:T(8,128)(2,1)S(1)} %get-tuple-element.123), channel_id=1, source_target_pairs={{0,4},{8,0},{16,8},{24,16},{28,24},{20,28},{12,20},{4,12},{1,5},{9... | collective-permute-start | bytes 786440 | tf_op jit(solution)/shard_map/combine_return/ppermute | solution.py:75
  168.1 14.6 %collective-permute-start.22 = (bf16[64,2048]{1,0:T(8,128)(2,1)S(1)}, bf16[64,2048]{1,0:T(8,128)(2,1)S(1)}, u32[]{:S(2)}, u32[]{:S(2)}) collective-permute-start(bf16[64,2048]{1,0:T(8,128)(2,1)S(1)} %collective-permute-done.20), channel_id=1, source_target_pairs={{0,8},{8,16},{16,24},{24,28},{28,20},{20,12},{12,4},{4,0},{1,9},{9... | collective-permute-start | bytes 786440 | tf_op jit(solution)/shard_map/dispatch_gather/ppermute | solution.py:55
  168.9 13.8 %collective-permute-start.23 = (bf16[64,2048]{1,0:T(8,128)(2,1)S(1)}, bf16[64,2048]{1,0:T(8,128)(2,1)S(1)}, u32[]{:S(2)}, u32[]{:S(2)}) collective-permute-start(bf16[64,2048]{1,0:T(8,128)(2,1)S(1)} %collective-permute-done.21), channel_id=1, source_target_pairs={{0,4},{8,0},{16,8},{24,16},{28,24},{20,28},{12,20},{4,12},{1,5},{9... | collective-permute-start | bytes 786440 | tf_op jit(solution)/shard_map/dispatch_gather/ppermute | solution.py:55
  172.5 9.3 %collective-permute-start.32 = (bf16[64,2048]{1,0:T(8,128)(2,1)S(1)}, bf16[64,2048]{1,0:T(8,128)(2,1)S(1)}, u32[]{:S(2)}, u32[]{:S(2)}) collective-permute-start(bf16[64,2048]{1,0:T(8,128)(2,1)S(1)} %get-tuple-element.126), channel_id=1, source_target_pairs={{0,8},{8,16},{16,24},{24,28},{28,20},{20,12},{12,4},{4,0},{1,9},{9... | collective-permute-start | bytes 786440 | tf_op jit(solution)/shard_map/combine_return/ppermute | solution.py:75
  173.5 9.2 %collective-permute-start.33 = (bf16[64,2048]{1,0:T(8,128)(2,1)S(1)}, bf16[64,2048]{1,0:T(8,128)(2,1)S(1)}, u32[]{:S(2)}, u32[]{:S(2)}) collective-permute-start(bf16[64,2048]{1,0:T(8,128)(2,1)S(1)} %get-tuple-element.127), channel_id=1, source_target_pairs={{0,4},{8,0},{16,8},{24,16},{28,24},{20,28},{12,20},{4,12},{1,5},{9... | collective-permute-start | bytes 786440 | tf_op jit(solution)/shard_map/combine_return/ppermute | solution.py:75
  182.8 9.0 %collective-permute-start.24 = (bf16[64,2048]{1,0:T(8,128)(2,1)S(1)}, bf16[64,2048]{1,0:T(8,128)(2,1)S(1)}, u32[]{:S(2)}, u32[]{:S(2)}) collective-permute-start(bf16[64,2048]{1,0:T(8,128)(2,1)S(1)} %collective-permute-done.22), channel_id=1, source_target_pairs={{0,8},{8,16},{16,24},{24,28},{28,20},{20,12},{12,4},{4,0},{1,9},{9... | collective-permute-start | bytes 786440 | tf_op jit(solution)/shard_map/dispatch_gather/ppermute | solution.py:55
  184.8 9.1 %collective-permute-start.25 = (bf16[64,2048]{1,0:T(8,128)(2,1)S(1)}, bf16[64,2048]{1,0:T(8,128)(2,1)S(1)}, u32[]{:S(2)}, u32[]{:S(2)}) collective-permute-start(bf16[64,2048]{1,0:T(8,128)(2,1)S(1)} %collective-permute-done.23), channel_id=1, source_target_pairs={{0,4},{8,0},{16,8},{24,16},{28,24},{20,28},{12,20},{4,12},{1,5},{9... | collective-permute-start | bytes 786440 | tf_op jit(solution)/shard_map/dispatch_gather/ppermute | solution.py:55
  184.9 14.6 %collective-permute-start.34 = (bf16[64,2048]{1,0:T(8,128)(2,1)S(1)}, bf16[64,2048]{1,0:T(8,128)(2,1)S(1)}, u32[]{:S(2)}, u32[]{:S(2)}) collective-permute-start(bf16[64,2048]{1,0:T(8,128)(2,1)S(1)} %get-tuple-element.130), channel_id=1, source_target_pairs={{0,8},{8,16},{16,24},{24,28},{28,20},{20,12},{12,4},{4,0},{1,9},{9... | collective-permute-start | bytes 786440 | tf_op jit(solution)/shard_map/combine_return/ppermute | solution.py:75
  187.0 12.6 %collective-permute-start.35 = (bf16[64,2048]{1,0:T(8,128)(2,1)S(1)}, bf16[64,2048]{1,0:T(8,128)(2,1)S(1)}, u32[]{:S(2)}, u32[]{:S(2)}) collective-permute-start(bf16[64,2048]{1,0:T(8,128)(2,1)S(1)} %get-tuple-element.131), channel_id=1, source_target_pairs={{0,4},{8,0},{16,8},{24,16},{28,24},{20,28},{12,20},{4,12},{1,5},{9... | collective-permute-start | bytes 786440 | tf_op jit(solution)/shard_map/combine_return/ppermute | solution.py:75
  197.5 6.4 %collective-permute-start.26 = (bf16[64,2048]{1,0:T(8,128)(2,1)S(1)}, bf16[64,2048]{1,0:T(8,128)(2,1)S(1)}, u32[]{:S(2)}, u32[]{:S(2)}) collective-permute-start(bf16[64,2048]{1,0:T(8,128)(2,1)S(1)} %collective-permute-done.24), channel_id=1, source_target_pairs={{0,8},{8,16},{16,24},{24,28},{28,20},{20,12},{12,4},{4,0},{1,9},{9... | collective-permute-start | bytes 786440 | tf_op jit(solution)/shard_map/dispatch_gather/ppermute | solution.py:55
  198.5 6.4 %collective-permute-start.27 = (bf16[64,2048]{1,0:T(8,128)(2,1)S(1)}, bf16[64,2048]{1,0:T(8,128)(2,1)S(1)}, u32[]{:S(2)}, u32[]{:S(2)}) collective-permute-start(bf16[64,2048]{1,0:T(8,128)(2,1)S(1)} %collective-permute-done.25), channel_id=1, source_target_pairs={{0,4},{8,0},{16,8},{24,16},{28,24},{20,28},{12,20},{4,12},{1,5},{9... | collective-permute-start | bytes 786440 | tf_op jit(solution)/shard_map/dispatch_gather/ppermute | solution.py:55
  201.9 6.5 %collective-permute-start.36 = (bf16[64,2048]{1,0:T(8,128)(2,1)S(1)}, bf16[64,2048]{1,0:T(8,128)(2,1)S(1)}, u32[]{:S(2)}, u32[]{:S(2)}) collective-permute-start(bf16[64,2048]{1,0:T(8,128)(2,1)S(1)} %get-tuple-element.134), channel_id=1, source_target_pairs={{0,8},{8,16},{16,24},{24,28},{28,20},{20,12},{12,4},{4,0},{1,9},{9... | collective-permute-start | bytes 786440 | tf_op jit(solution)/shard_map/combine_return/ppermute | solution.py:75
  202.8 6.4 %collective-permute-start.37 = (bf16[64,2048]{1,0:T(8,128)(2,1)S(1)}, bf16[64,2048]{1,0:T(8,128)(2,1)S(1)}, u32[]{:S(2)}, u32[]{:S(2)}) collective-permute-start(bf16[64,2048]{1,0:T(8,128)(2,1)S(1)} %get-tuple-element.135), channel_id=1, source_target_pairs={{0,4},{8,0},{16,8},{24,16},{28,24},{20,28},{12,20},{4,12},{1,5},{9... | collective-permute-start | bytes 786440 | tf_op jit(solution)/shard_map/combine_return/ppermute | solution.py:75
  209.3 6.4 %collective-permute-start.38 = (bf16[64,2048]{1,0:T(8,128)(2,1)S(1)}, bf16[64,2048]{1,0:T(8,128)(2,1)S(1)}, u32[]{:S(2)}, u32[]{:S(2)}) collective-permute-start(bf16[64,2048]{1,0:T(8,128)(2,1)S(1)} %get-tuple-element.138), channel_id=1, source_target_pairs={{0,8},{8,16},{16,24},{24,28},{28,20},{20,12},{12,4},{4,0},{1,9},{9... | collective-permute-start | bytes 786440 | tf_op jit(solution)/shard_map/combine_return/ppermute | solution.py:75
  209.7 6.4 %collective-permute-start.39 = (bf16[64,2048]{1,0:T(8,128)(2,1)S(1)}, bf16[64,2048]{1,0:T(8,128)(2,1)S(1)}, u32[]{:S(2)}, u32[]{:S(2)}) collective-permute-start(bf16[64,2048]{1,0:T(8,128)(2,1)S(1)} %get-tuple-element.139), channel_id=1, source_target_pairs={{0,4},{8,0},{16,8},{24,16},{28,24},{20,28},{12,20},{4,12},{1,5},{9... | collective-permute-start | bytes 786440 | tf_op jit(solution)/shard_map/combine_return/ppermute | solution.py:75
  216.2 7.1 %copy-start.5 = (f32[2048]{0:T(1024)S(1)}, f32[2048]{0:T(1024)}, u32[]{:S(2)}) copy-start(f32[2048]{0:T(1024)} %param.20) | copy-start | bytes 24580
  216.2 6.4 %collective-permute-start.40 = (bf16[64,2048]{1,0:T(8,128)(2,1)S(1)}, bf16[64,2048]{1,0:T(8,128)(2,1)S(1)}, u32[]{:S(2)}, u32[]{:S(2)}) collective-permute-start(bf16[64,2048]{1,0:T(8,128)(2,1)S(1)} %get-tuple-element.142), channel_id=1, source_target_pairs={{0,8},{8,16},{16,24},{24,28},{28,20},{20,12},{12,4},{4,0},{1,9},{9... | collective-permute-start | bytes 786440 | tf_op jit(solution)/shard_map/combine_return/ppermute | solution.py:75
  216.5 6.4 %collective-permute-start.41 = (bf16[64,2048]{1,0:T(8,128)(2,1)S(1)}, bf16[64,2048]{1,0:T(8,128)(2,1)S(1)}, u32[]{:S(2)}, u32[]{:S(2)}) collective-permute-start(bf16[64,2048]{1,0:T(8,128)(2,1)S(1)} %get-tuple-element.143), channel_id=1, source_target_pairs={{0,4},{8,0},{16,8},{24,16},{28,24},{20,28},{12,20},{4,12},{1,5},{9... | collective-permute-start | bytes 786440 | tf_op jit(solution)/shard_map/combine_return/ppermute | solution.py:75
  223.0 2.0 copy-start.1

commit v16 on v9

--- a/solution.py
+++ b/solution.py
@@ -154,17 +154,15 @@
             for step in steps:
                 rows_in += list(arrived[step])
                 weights_in += list(step_weights(step))
-            if c == len(chunks) - 1:
-                rows_in.append(normed)
-                weights_in.append(lax.dynamic_index_in_dim(weight_blocks, me, 0, keepdims=False))
             mixed = expert_mix(
                 jnp.concatenate(rows_in, axis=0), jnp.concatenate(weights_in, axis=0), gate_up, down
             )
             for i, step in enumerate(steps):
                 pieces[step] = (mixed[(2 * i) * half : (2 * i + 1) * half],
                                 mixed[(2 * i + 1) * half : (2 * i + 2) * half])
-            if c == len(chunks) - 1:
-                own_part = mixed[2 * len(steps) * half :]
+        own_part = expert_mix(
+            normed, lax.dynamic_index_in_dim(weight_blocks, me, 0, keepdims=False), gate_up, down
+        )
 
     with jax.named_scope("combine_return"):
         combined = ring_reduce_scatter_steps(pieces, own_part, ring)

time: 220 us -> 230 us (1.045)
  waiting for transfers between devices: 69.3 us -> 82.8 us
    ppermute x7, waiting for transfers between devices: 11.6 us -> 26.2 us  [ring_reduce_scatter(): lax.ppermute(send_fwd, 'ep', forward)]
    ppermute x7, starting transfers between devices: 9.27 us -> 5.1 us  [ring_reduce_scatter_steps(): lax.ppermute(send_bwd, 'ep', backward)]
    ppermute x7, waiting for transfers between devices: 3.89 us -> 7.86 us  [ring_reduce_scatter_steps(): lax.ppermute(send_bwd, 'ep', backward)]
    ppermute x7, starting transfers between devices: 6.45 us -> 10.1 us  [ring_reduce_scatter_steps(): lax.ppermute(send_fwd, 'ep', forward)]
    ppermute x7, starting transfers between devices: 8.58 us -> 6.12 us  [ring_all_gather(): lax.ppermute(got_bwd, 'ep', backward)]
    dot_general x8 -> x10, matrix products: 20.1 us -> 17.8 us  [expert_mix(): projected_up = jnp.dot(rows, gate_up[e], preferred_element_type=jnp.float32)]
    dot_general x8 -> x10, matrix products: 8.31 us -> 8.94 us  [expert_mix(): jnp.dot(activated, down[e], preferred_element_type=jnp.float32)]
  transfers between devices with their start and end apart: 44 -> 44, of which waited for: 34 -> 34; matrix products, arithmetic and copies ran while one was open for 15% -> 14% of each run, Pallas kernels for 0% -> 0%
where the time goes in v16:
time: 230 us; the launch traced here: 229 us
  waiting for transfers between devices  82.8 us (36%)
  starting transfers between devices  55.1 us (24%)
  between operations  40.8 us (18%)
  matrix products  29.1 us (13%)
  other arithmetic  13.8 us (6%)
  local copies, waits for them, and re-layouts  7.65 us (3%)
    ppermute x7, waiting for transfers between devices, ring_reduce_scatter(): lax.ppermute(send_fwd, 'ep', forward)  26.2 us
    dot_general x10, matrix products, expert_mix(): projected_up = jnp.dot(rows, gate_up[e], preferred_element_type=jnp.float32)  17.8 us
    ppermute x7, waiting for transfers between devices, ring_reduce_scatter_steps(): lax.ppermute(send_fwd, 'ep', forward)  15.5 us
    ppermute x7, starting transfers between devices, ring_reduce_scatter_steps(): lax.ppermute(send_fwd, 'ep', forward)  10.1 us
    dot_general x10, matrix products, expert_mix(): jnp.dot(activated, down[e], preferred_element_type=jnp.float32)  8.94 us
    all_to_all x1, waiting for transfers between devices, body(): lax.all_to_all(columns, 'ep', split_axis=0, concat_axis=0, tiled=True)  8.37 us
    ppermute x7, starting transfers between devices, ring_all_gather(): lax.ppermute(got_fwd, 'ep', forward)  8.27 us
    convert_element_type x6, other arithmetic, ring_reduce_scatter(): send_bwd.astype(jnp.bfloat16)  8.04 us
  transfers between devices with their start and end apart: 44, of which 34 were waited for; matrix products, arithmetic and copies ran while one was open for 14% of the time, Pallas kernels for 0%

profile of v16, /device:TPU:0, one launch (start us, length us, event | category | flops | bytes accessed | tf_op | source)
XLA Modules:
  0.0 229.3 jit_solution(6744657563431022842)
XLA Ops:
  0.7 1.5 select_reduce_fusion
  2.1 7.3 %all-to-all-start.1 = ((f32[8,128,2]{1,2,0:T(2,128)}), f32[8,128,2]{1,2,0:T(2,128)S(1)}, u32[]{:S(2)}, u32[]{:S(2)}) async-start(f32[8,128,2]{1,2,0:T(2,128)} %bitcast.2), calls=%async_computation.1 | async-start | bytes 16384 | tf_op jit(solution)/shard_map/route_weights/all_to_all | solution.py:118
  9.4 2.3 %copy.25 = bf16[16,8,8,512]{3,2,0,1:T(8,128)(2,1)} copy(bf16[16,8,8,512]{3,2,1,0:T(8,128)(2,1)} %bitcast.276) | data formatting | bytes 2097152 | tf_op jit(solution)/shard_map/out_projection/reshape | solution.py:122
  11.7 4.2 %all-to-all-done.1 = f32[8,128,2]{1,2,0:T(2,128)S(1)} async-done(((f32[8,128,2]{1,2,0:T(2,128)}), f32[8,128,2]{1,2,0:T(2,128)S(1)}, u32[]{:S(2)}, u32[]{:S(2)}) %all-to-all-start.1) | async-done | bytes 8224 | tf_op jit(solution)/shard_map/route_weights/all_to_all | solution.py:118
  15.9 3.6 %all-to-all-start = ((bf16[8,128,512]{2,1,0:T(8,128)(2,1)}), bf16[8,128,512]{2,1,0:T(8,128)(2,1)S(1)}, u32[]{:S(2)}, u32[]{:S(2)}) async-start(bf16[8,128,512]{2,1,0:T(8,128)(2,1)} %bitcast.274), calls=%async_computation | async-start | bytes 2097152 | tf_op jit(solution)/shard_map/out_projection/all_to_all | solution.py:123
  35.8 8.4 %all-to-all-done = bf16[8,128,512]{2,1,0:T(8,128)(2,1)S(1)} async-done(((bf16[8,128,512]{2,1,0:T(8,128)(2,1)}), bf16[8,128,512]{2,1,0:T(8,128)(2,1)S(1)}, u32[]{:S(2)}, u32[]{:S(2)}) %all-to-all-start) | async-done | bytes 1048608 | tf_op jit(solution)/shard_map/out_projection/all_to_all | solution.py:123
  44.2 2.4 %fusion.155 = f32[8,128,2048]{2,1,0:T(8,128)S(1)} fusion(bf16[8,128,512]{2,1,0:T(8,128)(2,1)S(1)} %all-to-all-done, bf16[512,2048]{1,0:T(8,128)(2,1)S(1)} %copy-done), kind=kOutput, calls=%fused_computation.85 | convolution fusion | flops 2147483648 | bytes 11534336 | tf_op jit(solution)/shard_map/out_projection/dot_general | solution.py:125
  46.6 3.3 %copy-done.2 = f32[8,128,2048]{2,1,0:T(8,128)} copy-done((f32[8,128,2048]{2,1,0:T(8,128)}, f32[8,128,2048]{2,1,0:T(8,128)S(1)}, u32[]{:S(2)}) %copy-start.2) | copy-done | bytes 8388632
  50.1 2.0 collective-permute-start.1
  56.6 1.3 fusion.201
  58.6 1.5 collective-permute-start.3
  81.2 1.3 fusion.199
  82.5 1.5 collective-permute-start.4
  84.6 4.3 %collective-permute-done.4 = bf16[64,2048]{1,0:T(8,128)(2,1)S(1)} collective-permute-done((bf16[64,2048]{1,0:T(8,128)(2,1)S(1)}, bf16[64,2048]{1,0:T(8,128)(2,1)S(1)}, u32[]{:S(2)}, u32[]{:S(2)}) %collective-permute-start.4) | collective-permute-done | bytes 262176 | tf_op jit(solution)/shard_map/out_projection/ppermute | solution.py:37
  88.9 1.6 collective-permute-done.5
  90.5 1.3 fusion.197
  91.8 1.9 collective-permute-start.6
  94.0 4.3 %collective-permute-done.6 = bf16[64,2048]{1,0:T(8,128)(2,1)S(1)} collective-permute-done((bf16[64,2048]{1,0:T(8,128)(2,1)S(1)}, bf16[64,2048]{1,0:T(8,128)(2,1)S(1)}, u32[]{:S(2)}, u32[]{:S(2)}) %collective-permute-start.6) | collective-permute-done | bytes 262176 | tf_op jit(solution)/shard_map/out_projection/ppermute | solution.py:37
  98.2 1.9 collective-permute-done.7
  100.1 1.5 fusion.195
  101.6 1.8 collective-permute-start.8
  103.8 4.4 %collective-permute-done.8 = bf16[64,2048]{1,0:T(8,128)(2,1)S(1)} collective-permute-done((bf16[64,2048]{1,0:T(8,128)(2,1)S(1)}, bf16[64,2048]{1,0:T(8,128)(2,1)S(1)}, u32[]{:S(2)}, u32[]{:S(2)}) %collective-permute-start.8) | collective-permute-done | bytes 262176 | tf_op jit(solution)/shard_map/out_projection/ppermute | solution.py:37
  108.2 2.8 %collective-permute-done.9 = bf16[64,2048]{1,0:T(8,128)(2,1)S(1)} collective-permute-done((bf16[64,2048]{1,0:T(8,128)(2,1)S(1)}, bf16[64,2048]{1,0:T(8,128)(2,1)S(1)}, u32[]{:S(2)}, u32[]{:S(2)}) %collective-permute-start.9) | collective-permute-done | bytes 262176 | tf_op jit(solution)/shard_map/out_projection/ppermute | solution.py:37
  110.9 1.3 fusion.193
  112.5 1.8 collective-permute-start.11
  114.4 6.6 %collective-permute-done.10 = bf16[64,2048]{1,0:T(8,128)(2,1)S(1)} collective-permute-done((bf16[64,2048]{1,0:T(8,128)(2,1)S(1)}, bf16[64,2048]{1,0:T(8,128)(2,1)S(1)}, u32[]{:S(2)}, u32[]{:S(2)}) %collective-permute-start.10) | collective-permute-done | bytes 262176 | tf_op jit(solution)/shard_map/out_projection/ppermute | solution.py:37
  121.2 1.3 fusion.191
  124.8 5.5 %collective-permute-done.12 = bf16[64,2048]{1,0:T(8,128)(2,1)S(1)} collective-permute-done((bf16[64,2048]{1,0:T(8,128)(2,1)S(1)}, bf16[64,2048]{1,0:T(8,128)(2,1)S(1)}, u32[]{:S(2)}, u32[]{:S(2)}) %collective-permute-start.12) | collective-permute-done | bytes 262176 | tf_op jit(solution)/shard_map/out_projection/ppermute | solution.py:37
  130.4 1.3 collective-permute-done.13
  131.6 1.3 fusion.214
  133.5 2.0 collective-permute-start.15
  135.6 3.9 %fusion.8 = f32[128,1536]{1,0:T(8,128)S(1)} fusion(bf16[128,2048]{1,0:T(8,128)(2,1)S(1)} %fusion.169, bf16[2,2048,1536]{2,1,0:T(8,128)(2,1)} %param.16), kind=kOutput, calls=%fused_computation.8 | convolution fusion | flops 805306368 | bytes 7602176 | tf_op jit(solution)/shard_map/local_experts/dot_general | solution.py:87
  140.7 1.7 collective-permute-done.14
  142.4 2.0 collective-permute-start.17
  144.5 4.3 %collective-permute-done.16 = bf16[64,2048]{1,0:T(8,128)(2,1)S(1)} collective-permute-done((bf16[64,2048]{1,0:T(8,128)(2,1)S(1)}, bf16[64,2048]{1,0:T(8,128)(2,1)S(1)}, u32[]{:S(2)}, u32[]{:S(2)}) %collective-permute-start.16) | collective-permute-done | bytes 262176 | tf_op jit(solution)/shard_map/dispatch_gather/ppermute | solution.py:55
  148.8 1.6 collective-permute-start.18
  151.1 1.8 fusion
  152.9 1.8 fusion.10
  157.0 2.8 %collective-permute-start.28 = (bf16[64,2048]{1,0:T(8,128)(2,1)S(1)}, bf16[64,2048]{1,0:T(8,128)(2,1)S(1)}, u32[]{:S(2)}, u32[]{:S(2)}) collective-permute-start(bf16[64,2048]{1,0:T(8,128)(2,1)S(1)} %get-tuple-element.118), channel_id=1, source_target_pairs={{0,8},{8,16},{16,24},{24,28},{28,20},{20,12},{12,4},{4,0},{1,9},{9... | collective-permute-start | bytes 786440 | tf_op jit(solution)/shard_map/combine_return/ppermute | solution.py:75
  160.9 2.0 collective-permute-start.20
  163.0 2.7 %collective-permute-done.28 = bf16[64,2048]{1,0:T(8,128)(2,1)S(1)} collective-permute-done((bf16[64,2048]{1,0:T(8,128)(2,1)S(1)}, bf16[64,2048]{1,0:T(8,128)(2,1)S(1)}, u32[]{:S(2)}, u32[]{:S(2)}) %collective-permute-start.28) | collective-permute-done | bytes 262176 | tf_op jit(solution)/shard_map/combine_return/ppermute | solution.py:75
  165.7 1.5 collective-permute-done.29
  167.3 1.4 collective-permute-start.30
  169.7 1.9 collective-permute-done.21
  171.6 2.0 collective-permute-start.22
  173.7 1.8 fusion.2
  175.5 1.8 fusion.12
  180.2 1.4 collective-permute-start.32
  183.6 1.3 collective-permute-start.24
  185.6 2.6 %collective-permute-done.32 = bf16[64,2048]{1,0:T(8,128)(2,1)S(1)} collective-permute-done((bf16[64,2048]{1,0:T(8,128)(2,1)S(1)}, bf16[64,2048]{1,0:T(8,128)(2,1)S(1)}, u32[]{:S(2)}, u32[]{:S(2)}) %collective-permute-start.32) | collective-permute-done | bytes 262176 | tf_op jit(solution)/shard_map/combine_return/ppermute | solution.py:75
  188.2 1.5 collective-permute-done.33
  189.8 1.4 collective-permute-start.34
  192.8 1.8 collective-permute-done.25
  194.6 1.3 collective-permute-start.26
  196.7 1.8 fusion.4
  198.5 1.8 fusion.14
  202.6 1.4 collective-permute-start.36
  207.0 3.4 %collective-permute-done.36 = bf16[64,2048]{1,0:T(8,128)(2,1)S(1)} collective-permute-done((bf16[64,2048]{1,0:T(8,128)(2,1)S(1)}, bf16[64,2048]{1,0:T(8,128)(2,1)S(1)}, u32[]{:S(2)}, u32[]{:S(2)}) %collective-permute-start.36) | collective-permute-done | bytes 262176 | tf_op jit(solution)/shard_map/combine_return/ppermute | solution.py:75
  210.4 2.6 %collective-permute-done.37 = bf16[64,2048]{1,0:T(8,128)(2,1)S(1)} collective-permute-done((bf16[64,2048]{1,0:T(8,128)(2,1)S(1)}, bf16[64,2048]{1,0:T(8,128)(2,1)S(1)}, u32[]{:S(2)}, u32[]{:S(2)}) %collective-permute-start.37) | collective-permute-done | bytes 262176 | tf_op jit(solution)/shard_map/combine_return/ppermute | solution.py:75
  213.2 2.0 collective-permute-start.39
  216.4 3.1 %collective-permute-done.38 = bf16[64,2048]{1,0:T(8,128)(2,1)S(1)} collective-permute-done((bf16[64,2048]{1,0:T(8,128)(2,1)S(1)}, bf16[64,2048]{1,0:T(8,128)(2,1)S(1)}, u32[]{:S(2)}, u32[]{:S(2)}) %collective-permute-start.38) | collective-permute-done | bytes 262176 | tf_op jit(solution)/shard_map/combine_return/ppermute | solution.py:75
  219.7 1.7 collective-permute-start.40
  222.4 3.7 %collective-permute-done.40 = bf16[64,2048]{1,0:T(8,128)(2,1)S(1)} collective-permute-done((bf16[64,2048]{1,0:T(8,128)(2,1)S(1)}, bf16[64,2048]{1,0:T(8,128)(2,1)S(1)}, u32[]{:S(2)}, u32[]{:S(2)}) %collective-permute-start.40) | collective-permute-done | bytes 262176 | tf_op jit(solution)/shard_map/combine_return/ppermute | solution.py:75
  226.1 1.6 collective-permute-done.41
  (126 shorter events, 31.6 us)
Async XLA Ops:
  0.6 43.6 %copy-start = (bf16[512,2048]{1,0:T(8,128)(2,1)S(1)}, bf16[512,2048]{1,0:T(8,128)(2,1)}, u32[]{:S(2)}) copy-start(bf16[512,2048]{1,0:T(8,128)(2,1)} %param.14) | copy-start | bytes 6291460
  0.6 18.9 %copy-start.7 = (s32[8]{0:T(128)S(1)}, s32[8]{0:T(128)}, u32[]{:S(2)}) copy-start(s32[8]{0:T(128)} %constant.227.clone) | copy-start | bytes 100
  0.7 30.7 %copy-start.4 = (s32[8]{0:T(128)S(1)}, s32[8]{0:T(128)}, u32[]{:S(2)}) copy-start(s32[8]{0:T(128)} %constant.228.clone) | copy-start | bytes 100
  2.1 13.8 %all-to-all-start.1 = ((f32[8,128,2]{1,2,0:T(2,128)}), f32[8,128,2]{1,2,0:T(2,128)S(1)}, u32[]{:S(2)}, u32[]{:S(2)}) async-start(f32[8,128,2]{1,2,0:T(2,128)} %bitcast.2), calls=%async_computation.1 | async-start | bytes 16384 | tf_op jit(solution)/shard_map/route_weights/all_to_all | solution.py:118
  15.9 28.3 %all-to-all-start = ((bf16[8,128,512]{2,1,0:T(8,128)(2,1)}), bf16[8,128,512]{2,1,0:T(8,128)(2,1)S(1)}, u32[]{:S(2)}, u32[]{:S(2)}) async-start(bf16[8,128,512]{2,1,0:T(8,128)(2,1)} %bitcast.274), calls=%async_computation | async-start | bytes 2097152 | tf_op jit(solution)/shard_map/out_projection/all_to_all | solution.py:123
  46.6 3.3 %copy-start.2 = (f32[8,128,2048]{2,1,0:T(8,128)}, f32[8,128,2048]{2,1,0:T(8,128)S(1)}, u32[]{:S(2)}) copy-start(f32[8,128,2048]{2,1,0:T(8,128)S(1)} %fusion.155) | copy-start | bytes 25165828
  50.0 6.6 %collective-permute-start = (bf16[64,2048]{1,0:T(8,128)(2,1)S(1)}, bf16[64,2048]{1,0:T(8,128)(2,1)S(1)}, u32[]{:S(2)}, u32[]{:S(2)}) collective-permute-start(bf16[64,2048]{1,0:T(8,128)(2,1)S(1)} %get-tuple-element.75), channel_id=1, source_target_pairs={{0,8},{8,16},{16,24},{24,28},{28,20},{20,12},{12,4},{4,0},{1,9},{9... | collective-permute-start | bytes 786440 | tf_op jit(solution)/shard_map/out_projection/ppermute | solution.py:37
  50.1 6.6 %collective-permute-start.1 = (bf16[64,2048]{1,0:T(8,128)(2,1)S(1)}, bf16[64,2048]{1,0:T(8,128)(2,1)S(1)}, u32[]{:S(2)}, u32[]{:S(2)}) collective-permute-start(bf16[64,2048]{1,0:T(8,128)(2,1)S(1)} %get-tuple-element.76), channel_id=1, source_target_pairs={{0,4},{8,0},{16,8},{24,16},{28,24},{20,28},{12,20},{4,12},{1,5},{9... | collective-permute-start | bytes 786440 | tf_op jit(solution)/shard_map/out_projection/ppermute | solution.py:37
  58.0 23.2 %collective-permute-start.2 = (bf16[64,2048]{1,0:T(8,128)(2,1)S(1)}, bf16[64,2048]{1,0:T(8,128)(2,1)S(1)}, u32[]{:S(2)}, u32[]{:S(2)}) collective-permute-start(bf16[64,2048]{1,0:T(8,128)(2,1)S(1)} %get-tuple-element.79), channel_id=1, source_target_pairs={{0,8},{8,16},{16,24},{24,28},{28,20},{20,12},{12,4},{4,0},{1,9},{9... | collective-permute-start | bytes 786440 | tf_op jit(solution)/shard_map/out_projection/ppermute | solution.py:37
  58.6 22.6 %collective-permute-start.3 = (bf16[64,2048]{1,0:T(8,128)(2,1)S(1)}, bf16[64,2048]{1,0:T(8,128)(2,1)S(1)}, u32[]{:S(2)}, u32[]{:S(2)}) collective-permute-start(bf16[64,2048]{1,0:T(8,128)(2,1)S(1)} %get-tuple-element.80), channel_id=1, source_target_pairs={{0,4},{8,0},{16,8},{24,16},{28,24},{20,28},{12,20},{4,12},{1,5},{9... | collective-permute-start | bytes 786440 | tf_op jit(solution)/shard_map/out_projection/ppermute | solution.py:37
  82.5 6.4 %collective-permute-start.4 = (bf16[64,2048]{1,0:T(8,128)(2,1)S(1)}, bf16[64,2048]{1,0:T(8,128)(2,1)S(1)}, u32[]{:S(2)}, u32[]{:S(2)}) collective-permute-start(bf16[64,2048]{1,0:T(8,128)(2,1)S(1)} %get-tuple-element.83), channel_id=1, source_target_pairs={{0,8},{8,16},{16,24},{24,28},{28,20},{20,12},{12,4},{4,0},{1,9},{9... | collective-permute-start | bytes 786440 | tf_op jit(solution)/shard_map/out_projection/ppermute | solution.py:37
  84.0 6.5 %collective-permute-start.5 = (bf16[64,2048]{1,0:T(8,128)(2,1)S(1)}, bf16[64,2048]{1,0:T(8,128)(2,1)S(1)}, u32[]{:S(2)}, u32[]{:S(2)}) collective-permute-start(bf16[64,2048]{1,0:T(8,128)(2,1)S(1)} %get-tuple-element.84), channel_id=1, source_target_pairs={{0,4},{8,0},{16,8},{24,16},{28,24},{20,28},{12,20},{4,12},{1,5},{9... | collective-permute-start | bytes 786440 | tf_op jit(solution)/shard_map/out_projection/ppermute | solution.py:37
  91.8 6.4 %collective-permute-start.6 = (bf16[64,2048]{1,0:T(8,128)(2,1)S(1)}, bf16[64,2048]{1,0:T(8,128)(2,1)S(1)}, u32[]{:S(2)}, u32[]{:S(2)}) collective-permute-start(bf16[64,2048]{1,0:T(8,128)(2,1)S(1)} %get-tuple-element.87), channel_id=1, source_target_pairs={{0,8},{8,16},{16,24},{24,28},{28,20},{20,12},{12,4},{4,0},{1,9},{9... | collective-permute-start | bytes 786440 | tf_op jit(solution)/shard_map/out_projection/ppermute | solution.py:37
  93.7 6.4 %collective-permute-start.7 = (bf16[64,2048]{1,0:T(8,128)(2,1)S(1)}, bf16[64,2048]{1,0:T(8,128)(2,1)S(1)}, u32[]{:S(2)}, u32[]{:S(2)}) collective-permute-start(bf16[64,2048]{1,0:T(8,128)(2,1)S(1)} %get-tuple-element.88), channel_id=1, source_target_pairs={{0,4},{8,0},{16,8},{24,16},{28,24},{20,28},{12,20},{4,12},{1,5},{9... | collective-permute-start | bytes 786440 | tf_op jit(solution)/shard_map/out_projection/ppermute | solution.py:37
  100.1 50.9 %slice-start = ((s8[12582912]{0:T(1024)(128)(4,1)}), s8[4194304]{0:T(1024)(128)(4,1)S(1)}, s32[]{:S(2)}) async-start(s8[12582912]{0:T(1024)(128)(4,1)} %bitcast.301), calls=%async_computation.2 | async-start | bytes 8388608
  101.6 6.6 %collective-permute-start.8 = (bf16[64,2048]{1,0:T(8,128)(2,1)S(1)}, bf16[64,2048]{1,0:T(8,128)(2,1)S(1)}, u32[]{:S(2)}, u32[]{:S(2)}) collective-permute-start(bf16[64,2048]{1,0:T(8,128)(2,1)S(1)} %get-tuple-element.91), channel_id=1, source_target_pairs={{0,8},{8,16},{16,24},{24,28},{28,20},{20,12},{12,4},{4,0},{1,9},{9... | collective-permute-start | bytes 786440 | tf_op jit(solution)/shard_map/out_projection/ppermute | solution.py:37
  103.4 7.5 %collective-permute-start.9 = (bf16[64,2048]{1,0:T(8,128)(2,1)S(1)}, bf16[64,2048]{1,0:T(8,128)(2,1)S(1)}, u32[]{:S(2)}, u32[]{:S(2)}) collective-permute-start(bf16[64,2048]{1,0:T(8,128)(2,1)S(1)} %get-tuple-element.92), channel_id=1, source_target_pairs={{0,4},{8,0},{16,8},{24,16},{28,24},{20,28},{12,20},{4,12},{1,5},{9... | collective-permute-start | bytes 786440 | tf_op jit(solution)/shard_map/out_projection/ppermute | solution.py:37
  103.8 29.2 %copy-start.3 = (bf16[128,2048]{1,0:T(8,128)(2,1)S(1)}, bf16[128,2048]{1,0:T(8,128)(2,1)}, u32[]{:S(2)}) copy-start(bf16[128,2048]{1,0:T(8,128)(2,1)} %param.12) | copy-start | bytes 1572868
  112.3 8.8 %collective-permute-start.10 = (bf16[64,2048]{1,0:T(8,128)(2,1)S(1)}, bf16[64,2048]{1,0:T(8,128)(2,1)S(1)}, u32[]{:S(2)}, u32[]{:S(2)}) collective-permute-start(bf16[64,2048]{1,0:T(8,128)(2,1)S(1)} %get-tuple-element.95), channel_id=1, source_target_pairs={{0,8},{8,16},{16,24},{24,28},{28,20},{20,12},{12,4},{4,0},{1,9},{9... | collective-permute-start | bytes 786440 | tf_op jit(solution)/shard_map/out_projection/ppermute | solution.py:37
  112.5 8.7 %collective-permute-start.11 = (bf16[64,2048]{1,0:T(8,128)(2,1)S(1)}, bf16[64,2048]{1,0:T(8,128)(2,1)S(1)}, u32[]{:S(2)}, u32[]{:S(2)}) collective-permute-start(bf16[64,2048]{1,0:T(8,128)(2,1)S(1)} %get-tuple-element.96), channel_id=1, source_target_pairs={{0,4},{8,0},{16,8},{24,16},{28,24},{20,28},{12,20},{4,12},{1,5},{9... | collective-permute-start | bytes 786440 | tf_op jit(solution)/shard_map/out_projection/ppermute | solution.py:37
  114.4 18.8 %copy-start.5 = (f32[2048]{0:T(1024)S(1)}, f32[2048]{0:T(1024)}, u32[]{:S(2)}) copy-start(f32[2048]{0:T(1024)} %param.15) | copy-start | bytes 24580
  122.6 7.8 %collective-permute-start.12 = (bf16[64,2048]{1,0:T(8,128)(2,1)S(1)}, bf16[64,2048]{1,0:T(8,128)(2,1)S(1)}, u32[]{:S(2)}, u32[]{:S(2)}) collective-permute-start(bf16[64,2048]{1,0:T(8,128)(2,1)S(1)} %get-tuple-element.99), channel_id=1, source_target_pairs={{0,8},{8,16},{16,24},{24,28},{28,20},{20,12},{12,4},{4,0},{1,9},{9... | collective-permute-start | bytes 786440 | tf_op jit(solution)/shard_map/out_projection/ppermute | solution.py:37
  123.8 7.9 %collective-permute-start.13 = (bf16[64,2048]{1,0:T(8,128)(2,1)S(1)}, bf16[64,2048]{1,0:T(8,128)(2,1)S(1)}, u32[]{:S(2)}, u32[]{:S(2)}) collective-permute-start(bf16[64,2048]{1,0:T(8,128)(2,1)S(1)} %get-tuple-element.100), channel_id=1, source_target_pairs={{0,4},{8,0},{16,8},{24,16},{28,24},{20,28},{12,20},{4,12},{1,5},{9... | collective-permute-start | bytes 786440 | tf_op jit(solution)/shard_map/out_projection/ppermute | solution.py:37
  124.8 26.2 %slice-start.1 = ((s8[12582912]{0:T(1024)(128)(4,1)}), s8[4194304]{0:T(1024)(128)(4,1)S(1)}, s32[]{:S(2)}) async-start(s8[12582912]{0:T(1024)(128)(4,1)} %bitcast.301), calls=%async_computation.3 | async-start | bytes 8388608
  133.5 7.2 %collective-permute-start.15 = (bf16[64,2048]{1,0:T(8,128)(2,1)S(1)}, bf16[64,2048]{1,0:T(8,128)(2,1)S(1)}, u32[]{:S(2)}, u32[]{:S(2)}) collective-permute-start(bf16[64,2048]{1,0:T(8,128)(2,1)S(1)} %get-tuple-element.182), channel_id=1, source_target_pairs={{0,4},{8,0},{16,8},{24,16},{28,24},{20,28},{12,20},{4,12},{1,5},{9... | collective-permute-start | bytes 786440 | tf_op jit(solution)/shard_map/dispatch_gather/ppermute | solution.py:55
  135.5 15.5 %slice-start.2 = ((s8[12582912]{0:T(1024)(128)(4,1)}), s8[4194304]{0:T(1024)(128)(4,1)S(1)}, s32[]{:S(2)}) async-start(s8[12582912]{0:T(1024)(128)(4,1)} %bitcast.301), calls=%async_computation.4 | async-start | bytes 8388608
  135.5 6.9 %collective-permute-start.14 = (bf16[64,2048]{1,0:T(8,128)(2,1)S(1)}, bf16[64,2048]{1,0:T(8,128)(2,1)S(1)}, u32[]{:S(2)}, u32[]{:S(2)}) collective-permute-start(bf16[64,2048]{1,0:T(8,128)(2,1)S(1)} %get-tuple-element.183), channel_id=1, source_target_pairs={{0,8},{8,16},{16,24},{24,28},{28,20},{20,12},{12,4},{4,0},{1,9},{9... | collective-permute-start | bytes 786440 | tf_op jit(solution)/shard_map/dispatch_gather/ppermute | solution.py:55
  142.4 6.4 %collective-permute-start.16 = (bf16[64,2048]{1,0:T(8,128)(2,1)S(1)}, bf16[64,2048]{1,0:T(8,128)(2,1)S(1)}, u32[]{:S(2)}, u32[]{:S(2)}) collective-permute-start(bf16[64,2048]{1,0:T(8,128)(2,1)S(1)} %collective-permute-done.14), channel_id=1, source_target_pairs={{0,8},{8,16},{16,24},{24,28},{28,20},{20,12},{12,4},{4,0},{1,9},{9... | collective-permute-start | bytes 786440 | tf_op jit(solution)/shard_map/dispatch_gather/ppermute | solution.py:55
  142.4 6.4 %collective-permute-start.17 = (bf16[64,2048]{1,0:T(8,128)(2,1)S(1)}, bf16[64,2048]{1,0:T(8,128)(2,1)S(1)}, u32[]{:S(2)}, u32[]{:S(2)}) collective-permute-start(bf16[64,2048]{1,0:T(8,128)(2,1)S(1)} %collective-permute-done.15), channel_id=1, source_target_pairs={{0,4},{8,0},{16,8},{24,16},{28,24},{20,28},{12,20},{4,12},{1,5},{9... | collective-permute-start | bytes 786440 | tf_op jit(solution)/shard_map/dispatch_gather/ppermute | solution.py:55
  148.8 12.0 %collective-permute-start.18 = (bf16[64,2048]{1,0:T(8,128)(2,1)S(1)}, bf16[64,2048]{1,0:T(8,128)(2,1)S(1)}, u32[]{:S(2)}, u32[]{:S(2)}) collective-permute-start(bf16[64,2048]{1,0:T(8,128)(2,1)S(1)} %collective-permute-done.16), channel_id=1, source_target_pairs={{0,8},{8,16},{16,24},{24,28},{28,20},{20,12},{12,4},{4,0},{1,9},{9... | collective-permute-start | bytes 786440 | tf_op jit(solution)/shard_map/dispatch_gather/ppermute | solution.py:55
  150.4 10.5 %collective-permute-start.19 = (bf16[64,2048]{1,0:T(8,128)(2,1)S(1)}, bf16[64,2048]{1,0:T(8,128)(2,1)S(1)}, u32[]{:S(2)}, u32[]{:S(2)}) collective-permute-start(bf16[64,2048]{1,0:T(8,128)(2,1)S(1)} %collective-permute-done.17), channel_id=1, source_target_pairs={{0,4},{8,0},{16,8},{24,16},{28,24},{20,28},{12,20},{4,12},{1,5},{9... | collective-permute-start | bytes 786440 | tf_op jit(solution)/shard_map/dispatch_gather/ppermute | solution.py:55
  151.1 3.6 %slice-start.3 = ((s8[6291456]{0:T(1024)(128)(4,1)}), s8[4194304]{0:T(1024)(128)(4,1)S(1)}, s32[]{:S(2)}) async-start(s8[6291456]{0:T(1024)(128)(4,1)} %bitcast.303), calls=%async_computation.5 | async-start | bytes 8388608
  152.9 1.8 slice-start.4
  157.0 8.7 %collective-permute-start.28 = (bf16[64,2048]{1,0:T(8,128)(2,1)S(1)}, bf16[64,2048]{1,0:T(8,128)(2,1)S(1)}, u32[]{:S(2)}, u32[]{:S(2)}) collective-permute-start(bf16[64,2048]{1,0:T(8,128)(2,1)S(1)} %get-tuple-element.118), channel_id=1, source_target_pairs={{0,8},{8,16},{16,24},{24,28},{28,20},{20,12},{12,4},{4,0},{1,9},{9... | collective-permute-start | bytes 786440 | tf_op jit(solution)/shard_map/combine_return/ppermute | solution.py:75
  159.8 7.4 %collective-permute-start.29 = (bf16[64,2048]{1,0:T(8,128)(2,1)S(1)}, bf16[64,2048]{1,0:T(8,128)(2,1)S(1)}, u32[]{:S(2)}, u32[]{:S(2)}) collective-permute-start(bf16[64,2048]{1,0:T(8,128)(2,1)S(1)} %get-tuple-element.119), channel_id=1, source_target_pairs={{0,4},{8,0},{16,8},{24,16},{28,24},{20,28},{12,20},{4,12},{1,5},{9... | collective-permute-start | bytes 786440 | tf_op jit(solution)/shard_map/combine_return/ppermute | solution.py:75
  160.9 8.7 %collective-permute-start.20 = (bf16[64,2048]{1,0:T(8,128)(2,1)S(1)}, bf16[64,2048]{1,0:T(8,128)(2,1)S(1)}, u32[]{:S(2)}, u32[]{:S(2)}) collective-permute-start(bf16[64,2048]{1,0:T(8,128)(2,1)S(1)} %collective-permute-done.18), channel_id=1, source_target_pairs={{0,8},{8,16},{16,24},{24,28},{28,20},{20,12},{12,4},{4,0},{1,9},{9... | collective-permute-start | bytes 786440 | tf_op jit(solution)/shard_map/dispatch_gather/ppermute | solution.py:55
  162.9 8.7 %collective-permute-start.21 = (bf16[64,2048]{1,0:T(8,128)(2,1)S(1)}, bf16[64,2048]{1,0:T(8,128)(2,1)S(1)}, u32[]{:S(2)}, u32[]{:S(2)}) collective-permute-start(bf16[64,2048]{1,0:T(8,128)(2,1)S(1)} %collective-permute-done.19), channel_id=1, source_target_pairs={{0,4},{8,0},{16,8},{24,16},{28,24},{20,28},{12,20},{4,12},{1,5},{9... | collective-permute-start | bytes 786440 | tf_op jit(solution)/shard_map/dispatch_gather/ppermute | solution.py:55
  167.3 10.0 %collective-permute-start.30 = (bf16[64,2048]{1,0:T(8,128)(2,1)S(1)}, bf16[64,2048]{1,0:T(8,128)(2,1)S(1)}, u32[]{:S(2)}, u32[]{:S(2)}) collective-permute-start(bf16[64,2048]{1,0:T(8,128)(2,1)S(1)} %get-tuple-element.122), channel_id=1, source_target_pairs={{0,8},{8,16},{16,24},{24,28},{28,20},{20,12},{12,4},{4,0},{1,9},{9... | collective-permute-start | bytes 786440 | tf_op jit(solution)/shard_map/combine_return/ppermute | solution.py:75
  168.7 9.2 %collective-permute-start.31 = (bf16[64,2048]{1,0:T(8,128)(2,1)S(1)}, bf16[64,2048]{1,0:T(8,128)(2,1)S(1)}, u32[]{:S(2)}, u32[]{:S(2)}) collective-permute-start(bf16[64,2048]{1,0:T(8,128)(2,1)S(1)} %get-tuple-element.123), channel_id=1, source_target_pairs={{0,4},{8,0},{16,8},{24,16},{28,24},{20,28},{12,20},{4,12},{1,5},{9... | collective-permute-start | bytes 786440 | tf_op jit(solution)/shard_map/combine_return/ppermute | solution.py:75
  171.6 11.4 %collective-permute-start.22 = (bf16[64,2048]{1,0:T(8,128)(2,1)S(1)}, bf16[64,2048]{1,0:T(8,128)(2,1)S(1)}, u32[]{:S(2)}, u32[]{:S(2)}) collective-permute-start(bf16[64,2048]{1,0:T(8,128)(2,1)S(1)} %collective-permute-done.20), channel_id=1, source_target_pairs={{0,8},{8,16},{16,24},{24,28},{28,20},{20,12},{12,4},{4,0},{1,9},{9... | collective-permute-start | bytes 786440 | tf_op jit(solution)/shard_map/dispatch_gather/ppermute | solution.py:55
  173.6 9.9 %collective-permute-start.23 = (bf16[64,2048]{1,0:T(8,128)(2,1)S(1)}, bf16[64,2048]{1,0:T(8,128)(2,1)S(1)}, u32[]{:S(2)}, u32[]{:S(2)}) collective-permute-start(bf16[64,2048]{1,0:T(8,128)(2,1)S(1)} %collective-permute-done.21), channel_id=1, source_target_pairs={{0,4},{8,0},{16,8},{24,16},{28,24},{20,28},{12,20},{4,12},{1,5},{9... | collective-permute-start | bytes 786440 | tf_op jit(solution)/shard_map/dispatch_gather/ppermute | solution.py:55
  180.2 7.9 %collective-permute-start.32 = (bf16[64,2048]{1,0:T(8,128)(2,1)S(1)}, bf16[64,2048]{1,0:T(8,128)(2,1)S(1)}, u32[]{:S(2)}, u32[]{:S(2)}) collective-permute-start(bf16[64,2048]{1,0:T(8,128)(2,1)S(1)} %get-tuple-element.126), channel_id=1, source_target_pairs={{0,8},{8,16},{16,24},{24,28},{28,20},{20,12},{12,4},{4,0},{1,9},{9... | collective-permute-start | bytes 786440 | tf_op jit(solution)/shard_map/combine_return/ppermute | solution.py:75
  181.7 8.0 %collective-permute-start.33 = (bf16[64,2048]{1,0:T(8,128)(2,1)S(1)}, bf16[64,2048]{1,0:T(8,128)(2,1)S(1)}, u32[]{:S(2)}, u32[]{:S(2)}) collective-permute-start(bf16[64,2048]{1,0:T(8,128)(2,1)S(1)} %get-tuple-element.127), channel_id=1, source_target_pairs={{0,4},{8,0},{16,8},{24,16},{28,24},{20,28},{12,20},{4,12},{1,5},{9... | collective-permute-start | bytes 786440 | tf_op jit(solution)/shard_map/combine_return/ppermute | solution.py:75
  183.6 9.2 %collective-permute-start.24 = (bf16[64,2048]{1,0:T(8,128)(2,1)S(1)}, bf16[64,2048]{1,0:T(8,128)(2,1)S(1)}, u32[]{:S(2)}, u32[]{:S(2)}) collective-permute-start(bf16[64,2048]{1,0:T(8,128)(2,1)S(1)} %collective-permute-done.22), channel_id=1, source_target_pairs={{0,8},{8,16},{16,24},{24,28},{28,20},{20,12},{12,4},{4,0},{1,9},{9... | collective-permute-start | bytes 786440 | tf_op jit(solution)/shard_map/dispatch_gather/ppermute | solution.py:55
  184.8 9.7 %collective-permute-start.25 = (bf16[64,2048]{1,0:T(8,128)(2,1)S(1)}, bf16[64,2048]{1,0:T(8,128)(2,1)S(1)}, u32[]{:S(2)}, u32[]{:S(2)}) collective-permute-start(bf16[64,2048]{1,0:T(8,128)(2,1)S(1)} %collective-permute-done.23), channel_id=1, source_target_pairs={{0,4},{8,0},{16,8},{24,16},{28,24},{20,28},{12,20},{4,12},{1,5},{9... | collective-permute-start | bytes 786440 | tf_op jit(solution)/shard_map/dispatch_gather/ppermute | solution.py:55
  189.8 10.5 %collective-permute-start.34 = (bf16[64,2048]{1,0:T(8,128)(2,1)S(1)}, bf16[64,2048]{1,0:T(8,128)(2,1)S(1)}, u32[]{:S(2)}, u32[]{:S(2)}) collective-permute-start(bf16[64,2048]{1,0:T(8,128)(2,1)S(1)} %get-tuple-element.130), channel_id=1, source_target_pairs={{0,8},{8,16},{16,24},{24,28},{28,20},{20,12},{12,4},{4,0},{1,9},{9... | collective-permute-start | bytes 786440 | tf_op jit(solution)/shard_map/combine_return/ppermute | solution.py:75
  191.2 9.1 %collective-permute-start.35 = (bf16[64,2048]{1,0:T(8,128)(2,1)S(1)}, bf16[64,2048]{1,0:T(8,128)(2,1)S(1)}, u32[]{:S(2)}, u32[]{:S(2)}) collective-permute-start(bf16[64,2048]{1,0:T(8,128)(2,1)S(1)} %get-tuple-element.131), channel_id=1, source_target_pairs={{0,4},{8,0},{16,8},{24,16},{28,24},{20,28},{12,20},{4,12},{1,5},{9... | collective-permute-start | bytes 786440 | tf_op jit(solution)/shard_map/combine_return/ppermute | solution.py:75
  194.6 10.1 %collective-permute-start.26 = (bf16[64,2048]{1,0:T(8,128)(2,1)S(1)}, bf16[64,2048]{1,0:T(8,128)(2,1)S(1)}, u32[]{:S(2)}, u32[]{:S(2)}) collective-permute-start(bf16[64,2048]{1,0:T(8,128)(2,1)S(1)} %collective-permute-done.24), channel_id=1, source_target_pairs={{0,8},{8,16},{16,24},{24,28},{28,20},{20,12},{12,4},{4,0},{1,9},{9... | collective-permute-start | bytes 786440 | tf_op jit(solution)/shard_map/dispatch_gather/ppermute | solution.py:55
  195.9 8.9 %collective-permute-start.27 = (bf16[64,2048]{1,0:T(8,128)(2,1)S(1)}, bf16[64,2048]{1,0:T(8,128)(2,1)S(1)}, u32[]{:S(2)}, u32[]{:S(2)}) collective-permute-start(bf16[64,2048]{1,0:T(8,128)(2,1)S(1)} %collective-permute-done.25), channel_id=1, source_target_pairs={{0,4},{8,0},{16,8},{24,16},{28,24},{20,28},{12,20},{4,12},{1,5},{9... | collective-permute-start | bytes 786440 | tf_op jit(solution)/shard_map/dispatch_gather/ppermute | solution.py:55
  202.6 7.8 %collective-permute-start.36 = (bf16[64,2048]{1,0:T(8,128)(2,1)S(1)}, bf16[64,2048]{1,0:T(8,128)(2,1)S(1)}, u32[]{:S(2)}, u32[]{:S(2)}) collective-permute-start(bf16[64,2048]{1,0:T(8,128)(2,1)S(1)} %get-tuple-element.134), channel_id=1, source_target_pairs={{0,8},{8,16},{16,24},{24,28},{28,20},{20,12},{12,4},{4,0},{1,9},{9... | collective-permute-start | bytes 786440 | tf_op jit(solution)/shard_map/combine_return/ppermute | solution.py:75
  204.0 9.0 %collective-permute-start.37 = (bf16[64,2048]{1,0:T(8,128)(2,1)S(1)}, bf16[64,2048]{1,0:T(8,128)(2,1)S(1)}, u32[]{:S(2)}, u32[]{:S(2)}) collective-permute-start(bf16[64,2048]{1,0:T(8,128)(2,1)S(1)} %get-tuple-element.135), channel_id=1, source_target_pairs={{0,4},{8,0},{16,8},{24,16},{28,24},{20,28},{12,20},{4,12},{1,5},{9... | collective-permute-start | bytes 786440 | tf_op jit(solution)/shard_map/combine_return/ppermute | solution.py:75
  213.1 6.4 %collective-permute-start.38 = (bf16[64,2048]{1,0:T(8,128)(2,1)S(1)}, bf16[64,2048]{1,0:T(8,128)(2,1)S(1)}, u32[]{:S(2)}, u32[]{:S(2)}) collective-permute-start(bf16[64,2048]{1,0:T(8,128)(2,1)S(1)} %get-tuple-element.138), channel_id=1, source_target_pairs={{0,8},{8,16},{16,24},{24,28},{28,20},{20,12},{12,4},{4,0},{1,9},{9... | collective-permute-start | bytes 786440 | tf_op jit(solution)/shard_map/combine_return/ppermute | solution.py:75
  213.2 6.4 %collective-permute-start.39 = (bf16[64,2048]{1,0:T(8,128)(2,1)S(1)}, bf16[64,2048]{1,0:T(8,128)(2,1)S(1)}, u32[]{:S(2)}, u32[]{:S(2)}) collective-permute-start(bf16[64,2048]{1,0:T(8,128)(2,1)S(1)} %get-tuple-element.139), channel_id=1, source_target_pairs={{0,4},{8,0},{16,8},{24,16},{28,24},{20,28},{12,20},{4,12},{1,5},{9... | collective-permute-start | bytes 786440 | tf_op jit(solution)/shard_map/combine_return/ppermute | solution.py:75
  219.7 6.4 %collective-permute-start.40 = (bf16[64,2048]{1,0:T(8,128)(2,1)S(1)}, bf16[64,2048]{1,0:T(8,128)(2,1)S(1)}, u32[]{:S(2)}, u32[]{:S(2)}) collective-permute-start(bf16[64,2048]{1,0:T(8,128)(2,1)S(1)} %get-tuple-element.142), channel_id=1, source_target_pairs={{0,8},{8,16},{16,24},{24,28},{28,20},{20,12},{12,4},{4,0},{1,9},{9... | collective-permute-start | bytes 786440 | tf_op jit(solution)/shard_map/combine_return/ppermute | solution.py:75
  221.3 6.4 %collective-permute-start.41 = (bf16[64,2048]{1,0:T(8,128)(2,1)S(1)}, bf16[64,2048]{1,0:T(8,128)(2,1)S(1)}, u32[]{:S(2)}, u32[]{:S(2)}) collective-permute-start(bf16[64,2048]{1,0:T(8,128)(2,1)S(1)} %get-tuple-element.143), channel_id=1, source_target_pairs={{0,4},{8,0},{16,8},{24,16},{28,24},{20,28},{12,20},{4,12},{1,5},{9... | collective-permute-start | bytes 786440 | tf_op jit(solution)/shard_map/combine_return/ppermute | solution.py:75
  221.8 7.5 %copy-start.1 = (bf16[512,2048]{1,0:T(8,128)(2,1)S(1)}, bf16[512,2048]{1,0:T(8,128)(2,1)}, u32[]{:S(2)}) copy-start(bf16[512,2048]{1,0:T(8,128)(2,1)} %param.14) | copy-start | bytes 6291460
  222.4 5.7 %copy-start.6 = (f32[2048]{0:T(1024)S(1)}, f32[2048]{0:T(1024)}, u32[]{:S(2)}) copy-start(f32[2048]{0:T(1024)} %param.20) | copy-start | bytes 24580

commit v17 on v9

--- a/solution.py
+++ b/solution.py
@@ -27,6 +27,8 @@
         owner_bwd = ring_index[(pos + 1 + step) % n]
         send_fwd = lax.dynamic_index_in_dim(blocks, owner_fwd, 0, keepdims=False)[:half]
         send_bwd = lax.dynamic_index_in_dim(blocks, owner_bwd, 0, keepdims=False)[half:]
+        send_fwd = send_fwd.astype(jnp.float32)
+        send_bwd = send_bwd.astype(jnp.float32)
         if step:
             send_fwd = send_fwd + got_fwd
             send_bwd = send_bwd + got_bwd
@@ -39,7 +41,7 @@
         got_fwd = got_fwd.astype(jnp.float32)
         got_bwd = got_bwd.astype(jnp.float32)
     me = ring_index[pos]
-    own = lax.dynamic_index_in_dim(blocks, me, 0, keepdims=False)
+    own = lax.dynamic_index_in_dim(blocks, me, 0, keepdims=False).astype(jnp.float32)
     return jnp.concatenate([own[:half] + got_fwd, own[half:] + got_bwd], axis=0)
 
 
@@ -124,7 +126,7 @@
         columns, row_weights = lax.optimization_barrier((columns, row_weights))
         partial = jnp.dot(
             columns.reshape(group_rows, slice_width), out_weight, preferred_element_type=jnp.float32
-        )
+        ).astype(jnp.bfloat16)
         projected = ring_reduce_scatter(partial.reshape(ep_size, row_count, model_width), ring, pos)
         middle = (residual.astype(jnp.float32) + projected).astype(jnp.bfloat16)
 

time: 220 us -> 227 us (1.032)
  waiting for transfers between devices: 69.3 us -> 78 us
    ppermute x7, waiting for transfers between devices: 9.08 us -> 17.9 us  [ring_all_gather(): lax.ppermute(got_fwd, 'ep', forward)]
    ppermute x7, waiting for transfers between devices: 17.1 us -> 19.9 us  [ring_reduce_scatter_steps(): lax.ppermute(send_fwd, 'ep', forward)]
    ppermute x7, waiting for transfers between devices: 7.35 us -> 4.82 us  [ring_all_gather(): lax.ppermute(got_bwd, 'ep', backward)]
    reshape x1 -> x0, local copies, waits for them, and re-layouts: 2.34 us -> none  [body(): attn_out.reshape(row_count, ep_size, slice_width).transpose(1, 0, 2)]
    unnamed x36 -> x37, local copies, waits for them, and re-layouts: 4.14 us -> 5.09 us
  transfers between devices with their start and end apart: 44 -> 44, of which waited for: 34 -> 31; matrix products, arithmetic and copies ran while one was open for 15% -> 11% of each run, Pallas kernels for 0% -> 0%
where the time goes in v17:
time: 227 us; the launch traced here: 226 us
  waiting for transfers between devices  78 us (34%)
  starting transfers between devices  54.3 us (24%)
  between operations  40.8 us (18%)
  matrix products  32 us (14%)
  other arithmetic  12.7 us (6%)
  local copies, waits for them, and re-layouts  8.08 us (4%)
    dot_general x8, matrix products, expert_mix(): projected_up = jnp.dot(rows, gate_up[e], preferred_element_type=jnp.float32)  20.1 us
    ppermute x7, waiting for transfers between devices, ring_reduce_scatter_steps(): lax.ppermute(send_fwd, 'ep', forward)  19.9 us
    ppermute x7, waiting for transfers between devices, ring_all_gather(): lax.ppermute(got_fwd, 'ep', forward)  17.9 us
    ppermute x7, waiting for transfers between devices, ring_reduce_scatter(): lax.ppermute(send_fwd, 'ep', forward)  13.7 us
    ppermute x7, starting transfers between devices, ring_reduce_scatter_steps(): lax.ppermute(send_bwd, 'ep', backward)  9.24 us
    ppermute x7, starting transfers between devices, ring_reduce_scatter(): lax.ppermute(send_bwd, 'ep', backward)  8.63 us
    all_to_all x1, waiting for transfers between devices, body(): lax.all_to_all(columns, 'ep', split_axis=0, concat_axis=0, tiled=True)  8.35 us
    dot_general x8, matrix products, expert_mix(): jnp.dot(activated, down[e], preferred_element_type=jnp.float32)  8.32 us
  transfers between devices with their start and end apart: 44, of which 31 were waited for; matrix products, arithmetic and copies ran while one was open for 11% of the time, Pallas kernels for 0%

profile of v17, /device:TPU:0, one launch (start us, length us, event | category | flops | bytes accessed | tf_op | source)
XLA Modules:
  0.0 225.8 jit_solution(1342953369706329603)
XLA Ops:
  0.6 1.5 select_reduce_fusion
  2.1 7.3 %all-to-all-start.1 = ((f32[8,128,2]{1,2,0:T(2,128)}), f32[8,128,2]{1,2,0:T(2,128)S(1)}, u32[]{:S(2)}, u32[]{:S(2)}) async-start(f32[8,128,2]{1,2,0:T(2,128)} %bitcast.3), calls=%async_computation.1 | async-start | bytes 16384 | tf_op jit(solution)/shard_map/route_weights/all_to_all | solution.py:120
  9.4 2.3 %copy.22 = bf16[128,4096]{0,1:T(8,128)(2,1)} copy(bf16[128,4096]{1,0:T(8,128)(2,1)} %param.13) | data formatting | bytes 2097152 | tf_op args[1]
  11.7 4.2 %all-to-all-done.1 = f32[8,128,2]{1,2,0:T(2,128)S(1)} async-done(((f32[8,128,2]{1,2,0:T(2,128)}), f32[8,128,2]{1,2,0:T(2,128)S(1)}, u32[]{:S(2)}, u32[]{:S(2)}) %all-to-all-start.1) | async-done | bytes 8224 | tf_op jit(solution)/shard_map/route_weights/all_to_all | solution.py:120
  15.9 3.6 %all-to-all-start = ((bf16[8,128,512]{1,2,0:T(8,128)(2,1)}), bf16[8,128,512]{1,2,0:T(8,128)(2,1)S(1)}, u32[]{:S(2)}, u32[]{:S(2)}) async-start(bf16[8,128,512]{1,2,0:T(8,128)(2,1)} %bitcast.1), calls=%async_computation | async-start | bytes 2097152 | tf_op jit(solution)/shard_map/out_projection/all_to_all | solution.py:125
  35.9 8.3 %all-to-all-done = bf16[8,128,512]{1,2,0:T(8,128)(2,1)S(1)} async-done(((bf16[8,128,512]{1,2,0:T(8,128)(2,1)}), bf16[8,128,512]{1,2,0:T(8,128)(2,1)S(1)}, u32[]{:S(2)}, u32[]{:S(2)}) %all-to-all-start) | async-done | bytes 1048608 | tf_op jit(solution)/shard_map/out_projection/all_to_all | solution.py:125
  44.2 1.3 copy.23
  45.5 3.6 %convolution_convert_fusion = bf16[1024,2048]{1,0:T(8,128)(2,1)S(1)} fusion(bf16[1024,512]{1,0:T(8,128)(2,1)} %bitcast.236, bf16[512,2048]{1,0:T(8,128)(2,1)S(1)} %copy-done), kind=kOutput, calls=%fused_computation.24 | convolution fusion | flops 2149580800 | bytes 7340032 | tf_op jit(solution)/shard_map/out_projection/dot_general | solution.py:127
  49.1 2.0 copy-done.2
  51.2 2.0 collective-permute-start.1
  57.8 1.2 fusion.163
  59.5 1.5 collective-permute-start.3
  65.4 2.1 collective-permute-done.3
  67.5 1.2 fusion.162
  68.6 1.8 collective-permute-start.4
  75.0 1.8 collective-permute-done.5
  76.8 1.2 fusion.161
  78.0 1.8 collective-permute-start.6
  84.4 2.1 collective-permute-done.7
  86.5 1.2 fusion.160
  88.2 1.5 collective-permute-start.9
  99.2 1.2 fusion.159
  100.9 1.5 collective-permute-start.11
  102.5 6.8 %collective-permute-done.10 = bf16[64,2048]{1,0:T(8,128)(2,1)S(1)} collective-permute-done((bf16[64,2048]{1,0:T(8,128)(2,1)S(1)}, bf16[64,2048]{1,0:T(8,128)(2,1)S(1)}, u32[]{:S(2)}, u32[]{:S(2)}) %collective-permute-start.10) | collective-permute-done | bytes 262176 | tf_op jit(solution)/shard_map/out_projection/ppermute | solution.py:39
  109.7 1.2 fusion.158
  111.4 1.6 collective-permute-start.13
  113.0 1.2 dynamic-slice_convert_fusion
  114.3 4.5 %collective-permute-done.12 = bf16[64,2048]{1,0:T(8,128)(2,1)S(1)} collective-permute-done((bf16[64,2048]{1,0:T(8,128)(2,1)S(1)}, bf16[64,2048]{1,0:T(8,128)(2,1)S(1)}, u32[]{:S(2)}, u32[]{:S(2)}) %collective-permute-start.12) | collective-permute-done | bytes 262176 | tf_op jit(solution)/shard_map/out_projection/ppermute | solution.py:39
  119.6 1.1 collective-permute-start.14
  121.8 4.3 %collective-permute-done.14 = bf16[64,2048]{1,0:T(8,128)(2,1)S(1)} collective-permute-done((bf16[64,2048]{1,0:T(8,128)(2,1)S(1)}, bf16[64,2048]{1,0:T(8,128)(2,1)S(1)}, u32[]{:S(2)}, u32[]{:S(2)}) %collective-permute-start.14) | collective-permute-done | bytes 262176 | tf_op jit(solution)/shard_map/dispatch_gather/ppermute | solution.py:57
  127.4 1.7 collective-permute-start.17
  129.2 4.3 %collective-permute-done.16 = bf16[64,2048]{1,0:T(8,128)(2,1)S(1)} collective-permute-done((bf16[64,2048]{1,0:T(8,128)(2,1)S(1)}, bf16[64,2048]{1,0:T(8,128)(2,1)S(1)}, u32[]{:S(2)}, u32[]{:S(2)}) %collective-permute-start.16) | collective-permute-done | bytes 262176 | tf_op jit(solution)/shard_map/dispatch_gather/ppermute | solution.py:57
  133.9 4.7 %fusion = f32[256,1536]{1,0:T(8,128)S(1)} fusion(bf16[256,2048]{1,0:T(8,128)(2,1)S(1)} %constant_dynamic-update-slice_fusion.8, bf16[2,2048,1536]{2,1,0:T(8,128)(2,1)} %param.16), kind=kOutput, calls=%fused_computation | convolution fusion | flops 1610612736 | bytes 8912896 | tf_op jit(solution)/shard_map/local_experts/dot_general | solution.py:89
  138.6 4.7 %fusion.8 = f32[256,1536]{1,0:T(8,128)S(1)} fusion(bf16[256,2048]{1,0:T(8,128)(2,1)S(1)} %constant_dynamic-update-slice_fusion.8, bf16[2,2048,1536]{2,1,0:T(8,128)(2,1)} %param.16), kind=kOutput, calls=%fused_computation.8 | convolution fusion | flops 1610612736 | bytes 8912896 | tf_op jit(solution)/shard_map/local_experts/dot_general | solution.py:89
  144.0 1.5 collective-permute-start.19
  148.2 1.5 collective-permute-start.29
  149.7 6.4 %collective-permute-done.28 = bf16[64,2048]{1,0:T(8,128)(2,1)S(1)} collective-permute-done((bf16[64,2048]{1,0:T(8,128)(2,1)S(1)}, bf16[64,2048]{1,0:T(8,128)(2,1)S(1)}, u32[]{:S(2)}, u32[]{:S(2)}) %collective-permute-start.28) | collective-permute-done | bytes 262176 | tf_op jit(solution)/shard_map/combine_return/ppermute | solution.py:77
  156.1 1.2 collective-permute-done.29
  157.3 1.9 collective-permute-start.20
  159.5 2.0 collective-permute-start.30
  161.6 4.8 %collective-permute-done.20 = bf16[64,2048]{1,0:T(8,128)(2,1)S(1)} collective-permute-done((bf16[64,2048]{1,0:T(8,128)(2,1)S(1)}, bf16[64,2048]{1,0:T(8,128)(2,1)S(1)}, u32[]{:S(2)}, u32[]{:S(2)}) %collective-permute-start.20) | collective-permute-done | bytes 262176 | tf_op jit(solution)/shard_map/dispatch_gather/ppermute | solution.py:57
  166.4 1.2 collective-permute-done.21
  167.7 1.8 fusion.2
  169.5 1.8 fusion.10
  172.0 1.3 collective-permute-start.23
  176.3 1.3 collective-permute-start.33
  177.7 6.9 %collective-permute-done.32 = bf16[64,2048]{1,0:T(8,128)(2,1)S(1)} collective-permute-done((bf16[64,2048]{1,0:T(8,128)(2,1)S(1)}, bf16[64,2048]{1,0:T(8,128)(2,1)S(1)}, u32[]{:S(2)}, u32[]{:S(2)}) %collective-permute-start.32) | collective-permute-done | bytes 262176 | tf_op jit(solution)/shard_map/combine_return/ppermute | solution.py:77
  185.5 1.1 collective-permute-start.24
  187.7 1.2 collective-permute-start.34
  189.8 2.2 collective-permute-done.24
  192.0 1.4 collective-permute-done.25
  193.5 1.8 fusion.4
  195.2 1.8 fusion.12
  197.7 1.4 collective-permute-start.27
  202.0 1.4 collective-permute-start.37
  203.4 2.4 %collective-permute-done.26 = bf16[64,2048]{1,0:T(8,128)(2,1)S(1)} collective-permute-done((bf16[64,2048]{1,0:T(8,128)(2,1)S(1)}, bf16[64,2048]{1,0:T(8,128)(2,1)S(1)}, u32[]{:S(2)}, u32[]{:S(2)}) %collective-permute-start.26) | collective-permute-done | bytes 262176 | tf_op jit(solution)/shard_map/dispatch_gather/ppermute | solution.py:57
  206.6 1.8 fusion.14
  208.4 1.8 fusion.6
  210.4 2.0 collective-permute-start.39
  213.5 1.1 fusion.49
  214.5 2.2 collective-permute-done.38
  217.3 2.0 collective-permute-start.41
  219.3 4.3 %collective-permute-done.40 = bf16[64,2048]{1,0:T(8,128)(2,1)S(1)} collective-permute-done((bf16[64,2048]{1,0:T(8,128)(2,1)S(1)}, bf16[64,2048]{1,0:T(8,128)(2,1)S(1)}, u32[]{:S(2)}, u32[]{:S(2)}) %collective-permute-start.40) | collective-permute-done | bytes 262176 | tf_op jit(solution)/shard_map/combine_return/ppermute | solution.py:77
  224.1 1.2 multiply_convert_fusion
  (121 shorter events, 28.6 us)
Async XLA Ops:
  0.6 44.9 %copy-start = (bf16[512,2048]{1,0:T(8,128)(2,1)S(1)}, bf16[512,2048]{1,0:T(8,128)(2,1)}, u32[]{:S(2)}) copy-start(bf16[512,2048]{1,0:T(8,128)(2,1)} %param.14) | copy-start | bytes 6291460
  2.1 13.8 %all-to-all-start.1 = ((f32[8,128,2]{1,2,0:T(2,128)}), f32[8,128,2]{1,2,0:T(2,128)S(1)}, u32[]{:S(2)}, u32[]{:S(2)}) async-start(f32[8,128,2]{1,2,0:T(2,128)} %bitcast.3), calls=%async_computation.1 | async-start | bytes 16384 | tf_op jit(solution)/shard_map/route_weights/all_to_all | solution.py:120
  9.4 10.1 %copy-start.7 = (s32[8]{0:T(128)S(1)}, s32[8]{0:T(128)}, u32[]{:S(2)}) copy-start(s32[8]{0:T(128)} %constant.224.clone) | copy-start | bytes 100
  9.4 21.9 %copy-start.4 = (s32[8]{0:T(128)S(1)}, s32[8]{0:T(128)}, u32[]{:S(2)}) copy-start(s32[8]{0:T(128)} %constant.225.clone) | copy-start | bytes 100
  15.9 28.3 %all-to-all-start = ((bf16[8,128,512]{1,2,0:T(8,128)(2,1)}), bf16[8,128,512]{1,2,0:T(8,128)(2,1)S(1)}, u32[]{:S(2)}, u32[]{:S(2)}) async-start(bf16[8,128,512]{1,2,0:T(8,128)(2,1)} %bitcast.1), calls=%async_computation | async-start | bytes 2097152 | tf_op jit(solution)/shard_map/out_projection/all_to_all | solution.py:125
  49.1 2.0 copy-start.2
  51.1 6.6 %collective-permute-start = (bf16[64,2048]{1,0:T(8,128)(2,1)S(1)}, bf16[64,2048]{1,0:T(8,128)(2,1)S(1)}, u32[]{:S(2)}, u32[]{:S(2)}) collective-permute-start(bf16[64,2048]{1,0:T(8,128)(2,1)S(1)} %get-tuple-element.75), channel_id=1, source_target_pairs={{0,8},{8,16},{16,24},{24,28},{28,20},{20,12},{12,4},{4,0},{1,9},{9... | collective-permute-start | bytes 786440 | tf_op jit(solution)/shard_map/out_projection/ppermute | solution.py:39
  51.2 6.6 %collective-permute-start.1 = (bf16[64,2048]{1,0:T(8,128)(2,1)S(1)}, bf16[64,2048]{1,0:T(8,128)(2,1)S(1)}, u32[]{:S(2)}, u32[]{:S(2)}) collective-permute-start(bf16[64,2048]{1,0:T(8,128)(2,1)S(1)} %get-tuple-element.76), channel_id=1, source_target_pairs={{0,4},{8,0},{16,8},{24,16},{28,24},{20,28},{12,20},{4,12},{1,5},{9... | collective-permute-start | bytes 786440 | tf_op jit(solution)/shard_map/out_projection/ppermute | solution.py:39
  58.9 6.4 %collective-permute-start.2 = (bf16[64,2048]{1,0:T(8,128)(2,1)S(1)}, bf16[64,2048]{1,0:T(8,128)(2,1)S(1)}, u32[]{:S(2)}, u32[]{:S(2)}) collective-permute-start(bf16[64,2048]{1,0:T(8,128)(2,1)S(1)} %get-tuple-element.79), channel_id=1, source_target_pairs={{0,8},{8,16},{16,24},{24,28},{28,20},{20,12},{12,4},{4,0},{1,9},{9... | collective-permute-start | bytes 786440 | tf_op jit(solution)/shard_map/out_projection/ppermute | solution.py:39
  59.5 7.9 %collective-permute-start.3 = (bf16[64,2048]{1,0:T(8,128)(2,1)S(1)}, bf16[64,2048]{1,0:T(8,128)(2,1)S(1)}, u32[]{:S(2)}, u32[]{:S(2)}) collective-permute-start(bf16[64,2048]{1,0:T(8,128)(2,1)S(1)} %get-tuple-element.80), channel_id=1, source_target_pairs={{0,4},{8,0},{16,8},{24,16},{28,24},{20,28},{12,20},{4,12},{1,5},{9... | collective-permute-start | bytes 786440 | tf_op jit(solution)/shard_map/out_projection/ppermute | solution.py:39
  68.6 6.4 %collective-permute-start.4 = (bf16[64,2048]{1,0:T(8,128)(2,1)S(1)}, bf16[64,2048]{1,0:T(8,128)(2,1)S(1)}, u32[]{:S(2)}, u32[]{:S(2)}) collective-permute-start(bf16[64,2048]{1,0:T(8,128)(2,1)S(1)} %get-tuple-element.83), channel_id=1, source_target_pairs={{0,8},{8,16},{16,24},{24,28},{28,20},{20,12},{12,4},{4,0},{1,9},{9... | collective-permute-start | bytes 786440 | tf_op jit(solution)/shard_map/out_projection/ppermute | solution.py:39
  70.4 6.4 %collective-permute-start.5 = (bf16[64,2048]{1,0:T(8,128)(2,1)S(1)}, bf16[64,2048]{1,0:T(8,128)(2,1)S(1)}, u32[]{:S(2)}, u32[]{:S(2)}) collective-permute-start(bf16[64,2048]{1,0:T(8,128)(2,1)S(1)} %get-tuple-element.84), channel_id=1, source_target_pairs={{0,4},{8,0},{16,8},{24,16},{28,24},{20,28},{12,20},{4,12},{1,5},{9... | collective-permute-start | bytes 786440 | tf_op jit(solution)/shard_map/out_projection/ppermute | solution.py:39
  78.0 6.4 %collective-permute-start.6 = (bf16[64,2048]{1,0:T(8,128)(2,1)S(1)}, bf16[64,2048]{1,0:T(8,128)(2,1)S(1)}, u32[]{:S(2)}, u32[]{:S(2)}) collective-permute-start(bf16[64,2048]{1,0:T(8,128)(2,1)S(1)} %get-tuple-element.87), channel_id=1, source_target_pairs={{0,8},{8,16},{16,24},{24,28},{28,20},{20,12},{12,4},{4,0},{1,9},{9... | collective-permute-start | bytes 786440 | tf_op jit(solution)/shard_map/out_projection/ppermute | solution.py:39
  79.8 6.7 %collective-permute-start.7 = (bf16[64,2048]{1,0:T(8,128)(2,1)S(1)}, bf16[64,2048]{1,0:T(8,128)(2,1)S(1)}, u32[]{:S(2)}, u32[]{:S(2)}) collective-permute-start(bf16[64,2048]{1,0:T(8,128)(2,1)S(1)} %get-tuple-element.88), channel_id=1, source_target_pairs={{0,4},{8,0},{16,8},{24,16},{28,24},{20,28},{12,20},{4,12},{1,5},{9... | collective-permute-start | bytes 786440 | tf_op jit(solution)/shard_map/out_projection/ppermute | solution.py:39
  87.6 11.5 %collective-permute-start.8 = (bf16[64,2048]{1,0:T(8,128)(2,1)S(1)}, bf16[64,2048]{1,0:T(8,128)(2,1)S(1)}, u32[]{:S(2)}, u32[]{:S(2)}) collective-permute-start(bf16[64,2048]{1,0:T(8,128)(2,1)S(1)} %get-tuple-element.91), channel_id=1, source_target_pairs={{0,8},{8,16},{16,24},{24,28},{28,20},{20,12},{12,4},{4,0},{1,9},{9... | collective-permute-start | bytes 786440 | tf_op jit(solution)/shard_map/out_projection/ppermute | solution.py:39
  88.2 11.0 %collective-permute-start.9 = (bf16[64,2048]{1,0:T(8,128)(2,1)S(1)}, bf16[64,2048]{1,0:T(8,128)(2,1)S(1)}, u32[]{:S(2)}, u32[]{:S(2)}) collective-permute-start(bf16[64,2048]{1,0:T(8,128)(2,1)S(1)} %get-tuple-element.92), channel_id=1, source_target_pairs={{0,4},{8,0},{16,8},{24,16},{28,24},{20,28},{12,20},{4,12},{1,5},{9... | collective-permute-start | bytes 786440 | tf_op jit(solution)/shard_map/out_projection/ppermute | solution.py:39
  100.3 8.9 %collective-permute-start.10 = (bf16[64,2048]{1,0:T(8,128)(2,1)S(1)}, bf16[64,2048]{1,0:T(8,128)(2,1)S(1)}, u32[]{:S(2)}, u32[]{:S(2)}) collective-permute-start(bf16[64,2048]{1,0:T(8,128)(2,1)S(1)} %get-tuple-element.95), channel_id=1, source_target_pairs={{0,8},{8,16},{16,24},{24,28},{28,20},{20,12},{12,4},{4,0},{1,9},{9... | collective-permute-start | bytes 786440 | tf_op jit(solution)/shard_map/out_projection/ppermute | solution.py:39
  100.9 8.8 %collective-permute-start.11 = (bf16[64,2048]{1,0:T(8,128)(2,1)S(1)}, bf16[64,2048]{1,0:T(8,128)(2,1)S(1)}, u32[]{:S(2)}, u32[]{:S(2)}) collective-permute-start(bf16[64,2048]{1,0:T(8,128)(2,1)S(1)} %get-tuple-element.96), channel_id=1, source_target_pairs={{0,4},{8,0},{16,8},{24,16},{28,24},{20,28},{12,20},{4,12},{1,5},{9... | collective-permute-start | bytes 786440 | tf_op jit(solution)/shard_map/out_projection/ppermute | solution.py:39
  110.9 7.9 %collective-permute-start.12 = (bf16[64,2048]{1,0:T(8,128)(2,1)S(1)}, bf16[64,2048]{1,0:T(8,128)(2,1)S(1)}, u32[]{:S(2)}, u32[]{:S(2)}) collective-permute-start(bf16[64,2048]{1,0:T(8,128)(2,1)S(1)} %get-tuple-element.99), channel_id=1, source_target_pairs={{0,8},{8,16},{16,24},{24,28},{28,20},{20,12},{12,4},{4,0},{1,9},{9... | collective-permute-start | bytes 786440 | tf_op jit(solution)/shard_map/out_projection/ppermute | solution.py:39
  111.4 7.6 %collective-permute-start.13 = (bf16[64,2048]{1,0:T(8,128)(2,1)S(1)}, bf16[64,2048]{1,0:T(8,128)(2,1)S(1)}, u32[]{:S(2)}, u32[]{:S(2)}) collective-permute-start(bf16[64,2048]{1,0:T(8,128)(2,1)S(1)} %get-tuple-element.100), channel_id=1, source_target_pairs={{0,4},{8,0},{16,8},{24,16},{28,24},{20,28},{12,20},{4,12},{1,5},{9... | collective-permute-start | bytes 786440 | tf_op jit(solution)/shard_map/out_projection/ppermute | solution.py:39
  113.0 6.1 %copy-start.3 = (bf16[128,2048]{1,0:T(8,128)(2,1)S(1)}, bf16[128,2048]{1,0:T(8,128)(2,1)}, u32[]{:S(2)}) copy-start(bf16[128,2048]{1,0:T(8,128)(2,1)} %param.12) | copy-start | bytes 1572868
  114.2 5.1 %copy-start.5 = (f32[2048]{0:T(1024)S(1)}, f32[2048]{0:T(1024)}, u32[]{:S(2)}) copy-start(f32[2048]{0:T(1024)} %param.15) | copy-start | bytes 24580
  119.6 6.4 %collective-permute-start.14 = (bf16[64,2048]{1,0:T(8,128)(2,1)S(1)}, bf16[64,2048]{1,0:T(8,128)(2,1)S(1)}, u32[]{:S(2)}, u32[]{:S(2)}) collective-permute-start(bf16[64,2048]{1,0:T(8,128)(2,1)S(1)} %get-tuple-element.183), channel_id=1, source_target_pairs={{0,8},{8,16},{16,24},{24,28},{28,20},{20,12},{12,4},{4,0},{1,9},{9... | collective-permute-start | bytes 786440 | tf_op jit(solution)/shard_map/dispatch_gather/ppermute | solution.py:57
  120.7 6.4 %collective-permute-start.15 = (bf16[64,2048]{1,0:T(8,128)(2,1)S(1)}, bf16[64,2048]{1,0:T(8,128)(2,1)S(1)}, u32[]{:S(2)}, u32[]{:S(2)}) collective-permute-start(bf16[64,2048]{1,0:T(8,128)(2,1)S(1)} %get-tuple-element.182), channel_id=1, source_target_pairs={{0,4},{8,0},{16,8},{24,16},{28,24},{20,28},{12,20},{4,12},{1,5},{9... | collective-permute-start | bytes 786440 | tf_op jit(solution)/shard_map/dispatch_gather/ppermute | solution.py:57
  127.1 6.4 %collective-permute-start.16 = (bf16[64,2048]{1,0:T(8,128)(2,1)S(1)}, bf16[64,2048]{1,0:T(8,128)(2,1)S(1)}, u32[]{:S(2)}, u32[]{:S(2)}) collective-permute-start(bf16[64,2048]{1,0:T(8,128)(2,1)S(1)} %collective-permute-done.14), channel_id=1, source_target_pairs={{0,8},{8,16},{16,24},{24,28},{28,20},{20,12},{12,4},{4,0},{1,9},{9... | collective-permute-start | bytes 786440 | tf_op jit(solution)/shard_map/dispatch_gather/ppermute | solution.py:57
  127.4 6.4 %collective-permute-start.17 = (bf16[64,2048]{1,0:T(8,128)(2,1)S(1)}, bf16[64,2048]{1,0:T(8,128)(2,1)S(1)}, u32[]{:S(2)}, u32[]{:S(2)}) collective-permute-start(bf16[64,2048]{1,0:T(8,128)(2,1)S(1)} %collective-permute-done.15), channel_id=1, source_target_pairs={{0,4},{8,0},{16,8},{24,16},{28,24},{20,28},{12,20},{4,12},{1,5},{9... | collective-permute-start | bytes 786440 | tf_op jit(solution)/shard_map/dispatch_gather/ppermute | solution.py:57
  133.9 11.6 %slice-start.3 = ((s8[6291456]{0:T(1024)(128)(4,1)}), s8[4194304]{0:T(1024)(128)(4,1)S(1)}, s32[]{:S(2)}) async-start(s8[6291456]{0:T(1024)(128)(4,1)} %bitcast.265), calls=%async_computation.5 | async-start | bytes 8388608
  138.6 6.8 %slice-start.4 = ((s8[6291456]{0:T(1024)(128)(4,1)}), s8[2097152]{0:T(1024)(128)(4,1)S(1)}, s32[]{:S(2)}) async-start(s8[6291456]{0:T(1024)(128)(4,1)} %bitcast.265), calls=%async_computation.6 | async-start | bytes 4194304
  143.4 14.0 %collective-permute-start.18 = (bf16[64,2048]{1,0:T(8,128)(2,1)S(1)}, bf16[64,2048]{1,0:T(8,128)(2,1)S(1)}, u32[]{:S(2)}, u32[]{:S(2)}) collective-permute-start(bf16[64,2048]{1,0:T(8,128)(2,1)S(1)} %collective-permute-done.16), channel_id=1, source_target_pairs={{0,8},{8,16},{16,24},{24,28},{28,20},{20,12},{12,4},{4,0},{1,9},{9... | collective-permute-start | bytes 786440 | tf_op jit(solution)/shard_map/dispatch_gather/ppermute | solution.py:57
  144.0 13.4 %collective-permute-start.19 = (bf16[64,2048]{1,0:T(8,128)(2,1)S(1)}, bf16[64,2048]{1,0:T(8,128)(2,1)S(1)}, u32[]{:S(2)}, u32[]{:S(2)}) collective-permute-start(bf16[64,2048]{1,0:T(8,128)(2,1)S(1)} %collective-permute-done.17), channel_id=1, source_target_pairs={{0,4},{8,0},{16,8},{24,16},{28,24},{20,28},{12,20},{4,12},{1,5},{9... | collective-permute-start | bytes 786440 | tf_op jit(solution)/shard_map/dispatch_gather/ppermute | solution.py:57
  145.4 22.2 %slice-start = ((s8[12582912]{0:T(1024)(128)(4,1)}), s8[4194304]{0:T(1024)(128)(4,1)S(1)}, s32[]{:S(2)}) async-start(s8[12582912]{0:T(1024)(128)(4,1)} %bitcast.263), calls=%async_computation.2 | async-start | bytes 8388608
  145.4 22.2 %slice-start.1 = ((s8[12582912]{0:T(1024)(128)(4,1)}), s8[4194304]{0:T(1024)(128)(4,1)S(1)}, s32[]{:S(2)}) async-start(s8[12582912]{0:T(1024)(128)(4,1)} %bitcast.263), calls=%async_computation.3 | async-start | bytes 8388608
  146.5 21.2 %slice-start.2 = ((s8[12582912]{0:T(1024)(128)(4,1)}), s8[4194304]{0:T(1024)(128)(4,1)S(1)}, s32[]{:S(2)}) async-start(s8[12582912]{0:T(1024)(128)(4,1)} %bitcast.263), calls=%async_computation.4 | async-start | bytes 8388608
  147.6 8.5 %collective-permute-start.28 = (bf16[64,2048]{1,0:T(8,128)(2,1)S(1)}, bf16[64,2048]{1,0:T(8,128)(2,1)S(1)}, u32[]{:S(2)}, u32[]{:S(2)}) collective-permute-start(bf16[64,2048]{1,0:T(8,128)(2,1)S(1)} %get-tuple-element.118), channel_id=1, source_target_pairs={{0,8},{8,16},{16,24},{24,28},{28,20},{20,12},{12,4},{4,0},{1,9},{9... | collective-permute-start | bytes 786440 | tf_op jit(solution)/shard_map/combine_return/ppermute | solution.py:77
  148.2 9.1 %collective-permute-start.29 = (bf16[64,2048]{1,0:T(8,128)(2,1)S(1)}, bf16[64,2048]{1,0:T(8,128)(2,1)S(1)}, u32[]{:S(2)}, u32[]{:S(2)}) collective-permute-start(bf16[64,2048]{1,0:T(8,128)(2,1)S(1)} %get-tuple-element.119), channel_id=1, source_target_pairs={{0,4},{8,0},{16,8},{24,16},{28,24},{20,28},{12,20},{4,12},{1,5},{9... | collective-permute-start | bytes 786440 | tf_op jit(solution)/shard_map/combine_return/ppermute | solution.py:77
  157.3 9.1 %collective-permute-start.20 = (bf16[64,2048]{1,0:T(8,128)(2,1)S(1)}, bf16[64,2048]{1,0:T(8,128)(2,1)S(1)}, u32[]{:S(2)}, u32[]{:S(2)}) collective-permute-start(bf16[64,2048]{1,0:T(8,128)(2,1)S(1)} %collective-permute-done.18), channel_id=1, source_target_pairs={{0,8},{8,16},{16,24},{24,28},{28,20},{20,12},{12,4},{4,0},{1,9},{9... | collective-permute-start | bytes 786440 | tf_op jit(solution)/shard_map/dispatch_gather/ppermute | solution.py:57
  159.2 8.4 %collective-permute-start.21 = (bf16[64,2048]{1,0:T(8,128)(2,1)S(1)}, bf16[64,2048]{1,0:T(8,128)(2,1)S(1)}, u32[]{:S(2)}, u32[]{:S(2)}) collective-permute-start(bf16[64,2048]{1,0:T(8,128)(2,1)S(1)} %collective-permute-done.19), channel_id=1, source_target_pairs={{0,4},{8,0},{16,8},{24,16},{28,24},{20,28},{12,20},{4,12},{1,5},{9... | collective-permute-start | bytes 786440 | tf_op jit(solution)/shard_map/dispatch_gather/ppermute | solution.py:57
  159.5 13.8 %collective-permute-start.30 = (bf16[64,2048]{1,0:T(8,128)(2,1)S(1)}, bf16[64,2048]{1,0:T(8,128)(2,1)S(1)}, u32[]{:S(2)}, u32[]{:S(2)}) collective-permute-start(bf16[64,2048]{1,0:T(8,128)(2,1)S(1)} %get-tuple-element.122), channel_id=1, source_target_pairs={{0,8},{8,16},{16,24},{24,28},{28,20},{20,12},{12,4},{4,0},{1,9},{9... | collective-permute-start | bytes 786440 | tf_op jit(solution)/shard_map/combine_return/ppermute | solution.py:77
  161.5 11.9 %collective-permute-start.31 = (bf16[64,2048]{1,0:T(8,128)(2,1)S(1)}, bf16[64,2048]{1,0:T(8,128)(2,1)S(1)}, u32[]{:S(2)}, u32[]{:S(2)}) collective-permute-start(bf16[64,2048]{1,0:T(8,128)(2,1)S(1)} %get-tuple-element.123), channel_id=1, source_target_pairs={{0,4},{8,0},{16,8},{24,16},{28,24},{20,28},{12,20},{4,12},{1,5},{9... | collective-permute-start | bytes 786440 | tf_op jit(solution)/shard_map/combine_return/ppermute | solution.py:77
  171.3 14.2 %collective-permute-start.22 = (bf16[64,2048]{1,0:T(8,128)(2,1)S(1)}, bf16[64,2048]{1,0:T(8,128)(2,1)S(1)}, u32[]{:S(2)}, u32[]{:S(2)}) collective-permute-start(bf16[64,2048]{1,0:T(8,128)(2,1)S(1)} %collective-permute-done.20), channel_id=1, source_target_pairs={{0,8},{8,16},{16,24},{24,28},{28,20},{20,12},{12,4},{4,0},{1,9},{9... | collective-permute-start | bytes 786440 | tf_op jit(solution)/shard_map/dispatch_gather/ppermute | solution.py:57
  172.0 13.5 %collective-permute-start.23 = (bf16[64,2048]{1,0:T(8,128)(2,1)S(1)}, bf16[64,2048]{1,0:T(8,128)(2,1)S(1)}, u32[]{:S(2)}, u32[]{:S(2)}) collective-permute-start(bf16[64,2048]{1,0:T(8,128)(2,1)S(1)} %collective-permute-done.21), channel_id=1, source_target_pairs={{0,4},{8,0},{16,8},{24,16},{28,24},{20,28},{12,20},{4,12},{1,5},{9... | collective-permute-start | bytes 786440 | tf_op jit(solution)/shard_map/dispatch_gather/ppermute | solution.py:57
  175.5 9.1 %collective-permute-start.32 = (bf16[64,2048]{1,0:T(8,128)(2,1)S(1)}, bf16[64,2048]{1,0:T(8,128)(2,1)S(1)}, u32[]{:S(2)}, u32[]{:S(2)}) collective-permute-start(bf16[64,2048]{1,0:T(8,128)(2,1)S(1)} %get-tuple-element.126), channel_id=1, source_target_pairs={{0,8},{8,16},{16,24},{24,28},{28,20},{20,12},{12,4},{4,0},{1,9},{9... | collective-permute-start | bytes 786440 | tf_op jit(solution)/shard_map/combine_return/ppermute | solution.py:77
  176.3 9.2 %collective-permute-start.33 = (bf16[64,2048]{1,0:T(8,128)(2,1)S(1)}, bf16[64,2048]{1,0:T(8,128)(2,1)S(1)}, u32[]{:S(2)}, u32[]{:S(2)}) collective-permute-start(bf16[64,2048]{1,0:T(8,128)(2,1)S(1)} %get-tuple-element.127), channel_id=1, source_target_pairs={{0,4},{8,0},{16,8},{24,16},{28,24},{20,28},{12,20},{4,12},{1,5},{9... | collective-permute-start | bytes 786440 | tf_op jit(solution)/shard_map/combine_return/ppermute | solution.py:77
  185.5 6.5 %collective-permute-start.24 = (bf16[64,2048]{1,0:T(8,128)(2,1)S(1)}, bf16[64,2048]{1,0:T(8,128)(2,1)S(1)}, u32[]{:S(2)}, u32[]{:S(2)}) collective-permute-start(bf16[64,2048]{1,0:T(8,128)(2,1)S(1)} %collective-permute-done.22), channel_id=1, source_target_pairs={{0,8},{8,16},{16,24},{24,28},{28,20},{20,12},{12,4},{4,0},{1,9},{9... | collective-permute-start | bytes 786440 | tf_op jit(solution)/shard_map/dispatch_gather/ppermute | solution.py:57
  186.6 6.8 %collective-permute-start.25 = (bf16[64,2048]{1,0:T(8,128)(2,1)S(1)}, bf16[64,2048]{1,0:T(8,128)(2,1)S(1)}, u32[]{:S(2)}, u32[]{:S(2)}) collective-permute-start(bf16[64,2048]{1,0:T(8,128)(2,1)S(1)} %collective-permute-done.23), channel_id=1, source_target_pairs={{0,4},{8,0},{16,8},{24,16},{28,24},{20,28},{12,20},{4,12},{1,5},{9... | collective-permute-start | bytes 786440 | tf_op jit(solution)/shard_map/dispatch_gather/ppermute | solution.py:57
  187.7 11.4 %collective-permute-start.34 = (bf16[64,2048]{1,0:T(8,128)(2,1)S(1)}, bf16[64,2048]{1,0:T(8,128)(2,1)S(1)}, u32[]{:S(2)}, u32[]{:S(2)}) collective-permute-start(bf16[64,2048]{1,0:T(8,128)(2,1)S(1)} %get-tuple-element.130), channel_id=1, source_target_pairs={{0,8},{8,16},{16,24},{24,28},{28,20},{20,12},{12,4},{4,0},{1,9},{9... | collective-permute-start | bytes 786440 | tf_op jit(solution)/shard_map/combine_return/ppermute | solution.py:77
  188.9 10.2 %collective-permute-start.35 = (bf16[64,2048]{1,0:T(8,128)(2,1)S(1)}, bf16[64,2048]{1,0:T(8,128)(2,1)S(1)}, u32[]{:S(2)}, u32[]{:S(2)}) collective-permute-start(bf16[64,2048]{1,0:T(8,128)(2,1)S(1)} %get-tuple-element.131), channel_id=1, source_target_pairs={{0,4},{8,0},{16,8},{24,16},{28,24},{20,28},{12,20},{4,12},{1,5},{9... | collective-permute-start | bytes 786440 | tf_op jit(solution)/shard_map/combine_return/ppermute | solution.py:77
  197.0 8.8 %collective-permute-start.26 = (bf16[64,2048]{1,0:T(8,128)(2,1)S(1)}, bf16[64,2048]{1,0:T(8,128)(2,1)S(1)}, u32[]{:S(2)}, u32[]{:S(2)}) collective-permute-start(bf16[64,2048]{1,0:T(8,128)(2,1)S(1)} %collective-permute-done.24), channel_id=1, source_target_pairs={{0,8},{8,16},{16,24},{24,28},{28,20},{20,12},{12,4},{4,0},{1,9},{9... | collective-permute-start | bytes 786440 | tf_op jit(solution)/shard_map/dispatch_gather/ppermute | solution.py:57
  197.7 8.9 %collective-permute-start.27 = (bf16[64,2048]{1,0:T(8,128)(2,1)S(1)}, bf16[64,2048]{1,0:T(8,128)(2,1)S(1)}, u32[]{:S(2)}, u32[]{:S(2)}) collective-permute-start(bf16[64,2048]{1,0:T(8,128)(2,1)S(1)} %collective-permute-done.25), channel_id=1, source_target_pairs={{0,4},{8,0},{16,8},{24,16},{28,24},{20,28},{12,20},{4,12},{1,5},{9... | collective-permute-start | bytes 786440 | tf_op jit(solution)/shard_map/dispatch_gather/ppermute | solution.py:57
  201.4 8.9 %collective-permute-start.36 = (bf16[64,2048]{1,0:T(8,128)(2,1)S(1)}, bf16[64,2048]{1,0:T(8,128)(2,1)S(1)}, u32[]{:S(2)}, u32[]{:S(2)}) collective-permute-start(bf16[64,2048]{1,0:T(8,128)(2,1)S(1)} %get-tuple-element.134), channel_id=1, source_target_pairs={{0,8},{8,16},{16,24},{24,28},{28,20},{20,12},{12,4},{4,0},{1,9},{9... | collective-permute-start | bytes 786440 | tf_op jit(solution)/shard_map/combine_return/ppermute | solution.py:77
  202.0 8.2 %collective-permute-start.37 = (bf16[64,2048]{1,0:T(8,128)(2,1)S(1)}, bf16[64,2048]{1,0:T(8,128)(2,1)S(1)}, u32[]{:S(2)}, u32[]{:S(2)}) collective-permute-start(bf16[64,2048]{1,0:T(8,128)(2,1)S(1)} %get-tuple-element.135), channel_id=1, source_target_pairs={{0,4},{8,0},{16,8},{24,16},{28,24},{20,28},{12,20},{4,12},{1,5},{9... | collective-permute-start | bytes 786440 | tf_op jit(solution)/shard_map/combine_return/ppermute | solution.py:77
  210.4 6.4 %collective-permute-start.38 = (bf16[64,2048]{1,0:T(8,128)(2,1)S(1)}, bf16[64,2048]{1,0:T(8,128)(2,1)S(1)}, u32[]{:S(2)}, u32[]{:S(2)}) collective-permute-start(bf16[64,2048]{1,0:T(8,128)(2,1)S(1)} %get-tuple-element.138), channel_id=1, source_target_pairs={{0,8},{8,16},{16,24},{24,28},{28,20},{20,12},{12,4},{4,0},{1,9},{9... | collective-permute-start | bytes 786440 | tf_op jit(solution)/shard_map/combine_return/ppermute | solution.py:77
  210.4 6.6 %collective-permute-start.39 = (bf16[64,2048]{1,0:T(8,128)(2,1)S(1)}, bf16[64,2048]{1,0:T(8,128)(2,1)S(1)}, u32[]{:S(2)}, u32[]{:S(2)}) collective-permute-start(bf16[64,2048]{1,0:T(8,128)(2,1)S(1)} %get-tuple-element.139), channel_id=1, source_target_pairs={{0,4},{8,0},{16,8},{24,16},{28,24},{20,28},{12,20},{4,12},{1,5},{9... | collective-permute-start | bytes 786440 | tf_op jit(solution)/shard_map/combine_return/ppermute | solution.py:77
  217.2 6.9 %copy-start.6 = (f32[2048]{0:T(1024)S(1)}, f32[2048]{0:T(1024)}, u32[]{:S(2)}) copy-start(f32[2048]{0:T(1024)} %param.20) | copy-start | bytes 24580
  217.2 6.4 %collective-permute-start.40 = (bf16[64,2048]{1,0:T(8,128)(2,1)S(1)}, bf16[64,2048]{1,0:T(8,128)(2,1)S(1)}, u32[]{:S(2)}, u32[]{:S(2)}) collective-permute-start(bf16[64,2048]{1,0:T(8,128)(2,1)S(1)} %get-tuple-element.142), channel_id=1, source_target_pairs={{0,8},{8,16},{16,24},{24,28},{28,20},{20,12},{12,4},{4,0},{1,9},{9... | collective-permute-start | bytes 786440 | tf_op jit(solution)/shard_map/combine_return/ppermute | solution.py:77
  217.3 6.4 %collective-permute-start.41 = (bf16[64,2048]{1,0:T(8,128)(2,1)S(1)}, bf16[64,2048]{1,0:T(8,128)(2,1)S(1)}, u32[]{:S(2)}, u32[]{:S(2)}) collective-permute-start(bf16[64,2048]{1,0:T(8,128)(2,1)S(1)} %get-tuple-element.143), channel_id=1, source_target_pairs={{0,4},{8,0},{16,8},{24,16},{28,24},{20,28},{12,20},{4,12},{1,5},{9... | collective-permute-start | bytes 786440 | tf_op jit(solution)/shard_map/combine_return/ppermute | solution.py:77
  223.9 2.0 copy-start.1

commit v18 on v9

--- a/solution.py
+++ b/solution.py
@@ -146,6 +146,8 @@
     with jax.named_scope("local_experts"):
         steps_all = list(range(ep_size - 1))
         chunks = [steps_all[i : i + 2] for i in range(0, ep_size - 1, 2)]
+        if len(chunks) > 2:
+            chunks = chunks[:-2] + [chunks[-2] + chunks[-1]]
         pieces = [None] * (ep_size - 1)
         own_part = None
         for c, steps in enumerate(chunks):

time: 220 us -> 232 us (1.055)
  waiting for transfers between devices: 69.3 us -> 77.6 us
    ppermute x7, waiting for transfers between devices: 17.1 us -> 26.1 us  [ring_reduce_scatter_steps(): lax.ppermute(send_fwd, 'ep', forward)]
    dot_general x8 -> x6, matrix products: 20.1 us -> 22.1 us  [expert_mix(): projected_up = jnp.dot(rows, gate_up[e], preferred_element_type=jnp.float32)]
    unnamed x36 -> x49, local copies, waits for them, and re-layouts: 4.14 us -> 5.75 us
    dot_general x8 -> x6, matrix products: 8.31 us -> 8.05 us  [expert_mix(): jnp.dot(activated, down[e], preferred_element_type=jnp.float32)]
  transfers between devices with their start and end apart: 44 -> 44, of which waited for: 34 -> 39; matrix products, arithmetic and copies ran while one was open for 15% -> 11% of each run, Pallas kernels for 0% -> 0%
where the time goes in v18:
time: 232 us; the launch traced here: 230 us
  waiting for transfers between devices  77.6 us (33%)
  starting transfers between devices  54.4 us (23%)
  between operations  40.9 us (18%)
  matrix products  32.5 us (14%)
  other arithmetic  15.3 us (7%)
  local copies, waits for them, and re-layouts  9.83 us (4%)
    ppermute x7, waiting for transfers between devices, ring_reduce_scatter_steps(): lax.ppermute(send_fwd, 'ep', forward)  26.1 us
    dot_general x6, matrix products, expert_mix(): projected_up = jnp.dot(rows, gate_up[e], preferred_element_type=jnp.float32)  22.1 us
    ppermute x7, waiting for transfers between devices, ring_reduce_scatter(): lax.ppermute(send_fwd, 'ep', forward)  11.7 us
    ppermute x7, waiting for transfers between devices, ring_all_gather(): lax.ppermute(got_fwd, 'ep', forward)  8.46 us
    all_to_all x1, waiting for transfers between devices, body(): lax.all_to_all(columns, 'ep', split_axis=0, concat_axis=0, tiled=True)  8.35 us
    dot_general x6, matrix products, expert_mix(): jnp.dot(activated, down[e], preferred_element_type=jnp.float32)  8.05 us
    ppermute x7, starting transfers between devices, ring_reduce_scatter(): lax.ppermute(send_bwd, 'ep', backward)  8 us
    ppermute x7, starting transfers between devices, ring_all_gather(): lax.ppermute(got_bwd, 'ep', backward)  7.87 us
  transfers between devices with their start and end apart: 44, of which 39 were waited for; matrix products, arithmetic and copies ran while one was open for 11% of the time, Pallas kernels for 0%

profile of v18, /device:TPU:0, one launch (start us, length us, event | category | flops | bytes accessed | tf_op | source)
XLA Modules:
  0.0 230.5 jit_solution(17844080154696490029)
XLA Ops:
  0.6 1.5 select_reduce_fusion
  2.1 7.3 %all-to-all-start.1 = ((f32[8,128,2]{1,2,0:T(2,128)}), f32[8,128,2]{1,2,0:T(2,128)S(1)}, u32[]{:S(2)}, u32[]{:S(2)}) async-start(f32[8,128,2]{1,2,0:T(2,128)} %bitcast.2), calls=%async_computation.1 | async-start | bytes 16384 | tf_op jit(solution)/shard_map/route_weights/all_to_all | solution.py:118
  9.4 2.3 copy.25
  11.7 4.2 %all-to-all-done.1 = f32[8,128,2]{1,2,0:T(2,128)S(1)} async-done(((f32[8,128,2]{1,2,0:T(2,128)}), f32[8,128,2]{1,2,0:T(2,128)S(1)}, u32[]{:S(2)}, u32[]{:S(2)}) %all-to-all-start.1) | async-done | bytes 8224 | tf_op jit(solution)/shard_map/route_weights/all_to_all | solution.py:118
  15.9 3.6 %all-to-all-start = ((bf16[8,128,512]{2,1,0:T(8,128)(2,1)}), bf16[8,128,512]{2,1,0:T(8,128)(2,1)S(1)}, u32[]{:S(2)}, u32[]{:S(2)}) async-start(bf16[8,128,512]{2,1,0:T(8,128)(2,1)} %bitcast.210), calls=%async_computation | async-start | bytes 2097152 | tf_op jit(solution)/shard_map/out_projection/all_to_all | solution.py:123
  35.8 8.3 %all-to-all-done = bf16[8,128,512]{2,1,0:T(8,128)(2,1)S(1)} async-done(((bf16[8,128,512]{2,1,0:T(8,128)(2,1)}), bf16[8,128,512]{2,1,0:T(8,128)(2,1)S(1)}, u32[]{:S(2)}, u32[]{:S(2)}) %all-to-all-start) | async-done | bytes 1048608 | tf_op jit(solution)/shard_map/out_projection/all_to_all | solution.py:123
  44.2 2.3 %fusion.86 = f32[8,128,2048]{2,1,0:T(8,128)S(1)} fusion(bf16[8,128,512]{2,1,0:T(8,128)(2,1)S(1)} %all-to-all-done, bf16[512,2048]{1,0:T(8,128)(2,1)S(1)} %copy-done), kind=kOutput, calls=%fused_computation.53 | convolution fusion | flops 2147483648 | bytes 11534336 | tf_op jit(solution)/shard_map/out_projection/dot_general | solution.py:125
  46.6 3.4 %copy-done.2 = f32[8,128,2048]{2,1,0:T(8,128)} copy-done((f32[8,128,2048]{2,1,0:T(8,128)}, f32[8,128,2048]{2,1,0:T(8,128)S(1)}, u32[]{:S(2)}) %copy-start.2) | copy-done | bytes 8388632
  50.0 2.0 collective-permute-start.1
  56.6 1.3 fusion.126
  58.5 1.5 collective-permute-start.3
  64.4 2.1 collective-permute-done.3
  66.5 1.3 fusion.124
  67.8 1.8 collective-permute-start.4
  74.2 1.8 collective-permute-done.5
  75.9 1.3 fusion.122
  77.3 1.8 collective-permute-start.6
  83.7 1.9 collective-permute-done.7
  85.6 1.3 fusion.120
  87.5 1.5 collective-permute-start.9
  93.0 1.6 collective-permute-done.8
  95.2 1.3 fusion.118
  97.1 1.5 collective-permute-start.11
  102.3 3.2 %collective-permute-done.10 = bf16[64,2048]{1,0:T(8,128)(2,1)S(1)} collective-permute-done((bf16[64,2048]{1,0:T(8,128)(2,1)S(1)}, bf16[64,2048]{1,0:T(8,128)(2,1)S(1)}, u32[]{:S(2)}, u32[]{:S(2)}) %collective-permute-start.10) | collective-permute-done | bytes 262176 | tf_op jit(solution)/shard_map/out_projection/ppermute | solution.py:37
  106.3 1.3 fusion.116
  107.6 1.2 collective-permute-start.12
  111.8 4.1 %collective-permute-done.12 = bf16[64,2048]{1,0:T(8,128)(2,1)S(1)} collective-permute-done((bf16[64,2048]{1,0:T(8,128)(2,1)S(1)}, bf16[64,2048]{1,0:T(8,128)(2,1)S(1)}, u32[]{:S(2)}, u32[]{:S(2)}) %collective-permute-start.12) | collective-permute-done | bytes 262176 | tf_op jit(solution)/shard_map/out_projection/ppermute | solution.py:37
  116.5 1.3 fusion.139
  118.3 1.5 collective-permute-start.15
  120.5 5.2 %collective-permute-done.15 = bf16[64,2048]{1,0:T(8,128)(2,1)S(1)} collective-permute-done((bf16[64,2048]{1,0:T(8,128)(2,1)S(1)}, bf16[64,2048]{1,0:T(8,128)(2,1)S(1)}, u32[]{:S(2)}, u32[]{:S(2)}) %collective-permute-start.15) | collective-permute-done | bytes 262176 | tf_op jit(solution)/shard_map/dispatch_gather/ppermute | solution.py:55
  126.9 1.5 collective-permute-start.17
  128.4 4.3 %collective-permute-done.16 = bf16[64,2048]{1,0:T(8,128)(2,1)S(1)} collective-permute-done((bf16[64,2048]{1,0:T(8,128)(2,1)S(1)}, bf16[64,2048]{1,0:T(8,128)(2,1)S(1)}, u32[]{:S(2)}, u32[]{:S(2)}) %collective-permute-start.16) | collective-permute-done | bytes 262176 | tf_op jit(solution)/shard_map/dispatch_gather/ppermute | solution.py:55
  133.7 2.0 collective-permute-start.18
  135.8 4.7 %fusion = f32[256,1536]{1,0:T(8,128)S(1)} fusion(bf16[256,2048]{1,0:T(8,128)(2,1)S(1)} %constant_dynamic-update-slice_fusion.11, bf16[2,2048,1536]{2,1,0:T(8,128)(2,1)} %param.16), kind=kOutput, calls=%fused_computation | convolution fusion | flops 1610612736 | bytes 8912896 | tf_op jit(solution)/shard_map/local_experts/dot_general | solution.py:87
  140.5 4.7 %fusion.6 = f32[256,1536]{1,0:T(8,128)S(1)} fusion(bf16[256,2048]{1,0:T(8,128)(2,1)S(1)} %constant_dynamic-update-slice_fusion.11, bf16[2,2048,1536]{2,1,0:T(8,128)(2,1)} %param.16), kind=kOutput, calls=%fused_computation.6 | convolution fusion | flops 1610612736 | bytes 8912896 | tf_op jit(solution)/shard_map/local_experts/dot_general | solution.py:87
  147.5 2.1 collective-permute-start.28
  149.7 2.1 collective-permute-start.20
  151.8 4.2 %collective-permute-done.28 = bf16[64,2048]{1,0:T(8,128)(2,1)S(1)} collective-permute-done((bf16[64,2048]{1,0:T(8,128)(2,1)S(1)}, bf16[64,2048]{1,0:T(8,128)(2,1)S(1)}, u32[]{:S(2)}, u32[]{:S(2)}) %collective-permute-start.28) | collective-permute-done | bytes 262176 | tf_op jit(solution)/shard_map/combine_return/ppermute | solution.py:75
  156.5 1.9 collective-permute-start.31
  159.2 2.0 collective-permute-start.23
  161.3 1.8 fusion.2
  163.1 1.8 fusion.8
  166.7 1.1 fusion.47
  168.8 1.2 collective-permute-start.32
  171.4 1.2 collective-permute-start.24
  173.4 4.9 %collective-permute-done.32 = bf16[64,2048]{1,0:T(8,128)(2,1)} collective-permute-done((bf16[64,2048]{1,0:T(8,128)(2,1)}, bf16[64,2048]{1,0:T(8,128)(2,1)}, u32[]{:S(2)}, u32[]{:S(2)}) %collective-permute-start.32) | collective-permute-done | bytes 262176 | tf_op jit(solution)/shard_map/combine_return/ppermute | solution.py:75
  178.7 1.1 fusion.105
  180.0 1.9 collective-permute-start.35
  183.1 1.9 collective-permute-start.27
  185.1 1.3 collective-permute-done.34
  186.4 2.9 %collective-permute-done.26 = bf16[64,2048]{1,0:T(8,128)(2,1)S(1)} collective-permute-done((bf16[64,2048]{1,0:T(8,128)(2,1)S(1)}, bf16[64,2048]{1,0:T(8,128)(2,1)S(1)}, u32[]{:S(2)}, u32[]{:S(2)}) %collective-permute-start.26) | collective-permute-done | bytes 262176 | tf_op jit(solution)/shard_map/dispatch_gather/ppermute | solution.py:55
  189.8 5.7 %fusion.4 = f32[512,1536]{1,0:T(8,128)S(1)} fusion(bf16[512,2048]{1,0:T(8,128)(2,1)S(1)} %constant_dynamic-update-slice_fusion, bf16[2,2048,1536]{2,1,0:T(8,128)(2,1)} %param.16), kind=kOutput, calls=%fused_computation.4 | convolution fusion | flops 3221225472 | bytes 11534336 | tf_op jit(solution)/shard_map/local_experts/dot_general | solution.py:87
  196.1 3.4 %fusion.10 = f32[512,1536]{1,0:T(8,128)S(1)} fusion(bf16[512,2048]{1,0:T(8,128)(2,1)S(1)} %constant_dynamic-update-slice_fusion, bf16[2,2048,1536]{2,1,0:T(8,128)(2,1)S(1)} %bitcast.240), kind=kOutput, calls=%fused_computation.10 | convolution fusion | flops 3221225472 | bytes 11534336 | tf_op jit(solution)/shard_map/local_experts/dot_general | solution.py:87
  199.5 1.8 fusion.30
  201.3 1.9 multiply_add_fusion
  203.3 1.3 collective-permute-start.36
  205.4 6.5 %collective-permute-done.36 = bf16[64,2048]{1,0:T(8,128)(2,1)S(1)} collective-permute-done((bf16[64,2048]{1,0:T(8,128)(2,1)S(1)}, bf16[64,2048]{1,0:T(8,128)(2,1)S(1)}, u32[]{:S(2)}, u32[]{:S(2)}) %collective-permute-start.36) | collective-permute-done | bytes 262176 | tf_op jit(solution)/shard_map/combine_return/ppermute | solution.py:75
  211.9 1.1 collective-permute-done.37
  213.1 1.8 collective-permute-start.38
  215.2 4.3 %collective-permute-done.38 = bf16[64,2048]{1,0:T(8,128)(2,1)S(1)} collective-permute-done((bf16[64,2048]{1,0:T(8,128)(2,1)S(1)}, bf16[64,2048]{1,0:T(8,128)(2,1)S(1)}, u32[]{:S(2)}, u32[]{:S(2)}) %collective-permute-start.38) | collective-permute-done | bytes 262176 | tf_op jit(solution)/shard_map/combine_return/ppermute | solution.py:75
  219.6 1.7 collective-permute-done.39
  222.0 1.5 collective-permute-start.41
  223.5 4.3 %collective-permute-done.40 = bf16[64,2048]{1,0:T(8,128)(2,1)S(1)} collective-permute-done((bf16[64,2048]{1,0:T(8,128)(2,1)S(1)}, bf16[64,2048]{1,0:T(8,128)(2,1)S(1)}, u32[]{:S(2)}, u32[]{:S(2)}) %collective-permute-start.40) | collective-permute-done | bytes 262176 | tf_op jit(solution)/shard_map/combine_return/ppermute | solution.py:75
  228.8 1.2 multiply_convert_fusion
  (128 shorter events, 27.6 us)
Async XLA Ops:
  0.6 43.6 %copy-start = (bf16[512,2048]{1,0:T(8,128)(2,1)S(1)}, bf16[512,2048]{1,0:T(8,128)(2,1)}, u32[]{:S(2)}) copy-start(bf16[512,2048]{1,0:T(8,128)(2,1)} %param.14) | copy-start | bytes 6291460
  2.1 13.8 %all-to-all-start.1 = ((f32[8,128,2]{1,2,0:T(2,128)}), f32[8,128,2]{1,2,0:T(2,128)S(1)}, u32[]{:S(2)}, u32[]{:S(2)}) async-start(f32[8,128,2]{1,2,0:T(2,128)} %bitcast.2), calls=%async_computation.1 | async-start | bytes 16384 | tf_op jit(solution)/shard_map/route_weights/all_to_all | solution.py:118
  9.4 10.1 %copy-start.7 = (s32[8]{0:T(128)S(1)}, s32[8]{0:T(128)}, u32[]{:S(2)}) copy-start(s32[8]{0:T(128)} %constant.223.clone) | copy-start | bytes 100
  9.4 21.9 %copy-start.4 = (s32[8]{0:T(128)S(1)}, s32[8]{0:T(128)}, u32[]{:S(2)}) copy-start(s32[8]{0:T(128)} %constant.224.clone) | copy-start | bytes 100
  15.9 28.3 %all-to-all-start = ((bf16[8,128,512]{2,1,0:T(8,128)(2,1)}), bf16[8,128,512]{2,1,0:T(8,128)(2,1)S(1)}, u32[]{:S(2)}, u32[]{:S(2)}) async-start(bf16[8,128,512]{2,1,0:T(8,128)(2,1)} %bitcast.210), calls=%async_computation | async-start | bytes 2097152 | tf_op jit(solution)/shard_map/out_projection/all_to_all | solution.py:123
  46.5 3.4 %copy-start.2 = (f32[8,128,2048]{2,1,0:T(8,128)}, f32[8,128,2048]{2,1,0:T(8,128)S(1)}, u32[]{:S(2)}) copy-start(f32[8,128,2048]{2,1,0:T(8,128)S(1)} %fusion.86) | copy-start | bytes 25165828
  50.0 6.6 %collective-permute-start = (bf16[64,2048]{1,0:T(8,128)(2,1)S(1)}, bf16[64,2048]{1,0:T(8,128)(2,1)S(1)}, u32[]{:S(2)}, u32[]{:S(2)}) collective-permute-start(bf16[64,2048]{1,0:T(8,128)(2,1)S(1)} %get-tuple-element.75), channel_id=1, source_target_pairs={{0,8},{8,16},{16,24},{24,28},{28,20},{20,12},{12,4},{4,0},{1,9},{9... | collective-permute-start | bytes 786440 | tf_op jit(solution)/shard_map/out_projection/ppermute | solution.py:37
  50.0 6.6 %collective-permute-start.1 = (bf16[64,2048]{1,0:T(8,128)(2,1)S(1)}, bf16[64,2048]{1,0:T(8,128)(2,1)S(1)}, u32[]{:S(2)}, u32[]{:S(2)}) collective-permute-start(bf16[64,2048]{1,0:T(8,128)(2,1)S(1)} %get-tuple-element.76), channel_id=1, source_target_pairs={{0,4},{8,0},{16,8},{24,16},{28,24},{20,28},{12,20},{4,12},{1,5},{9... | collective-permute-start | bytes 786440 | tf_op jit(solution)/shard_map/out_projection/ppermute | solution.py:37
  57.9 6.4 %collective-permute-start.2 = (bf16[64,2048]{1,0:T(8,128)(2,1)S(1)}, bf16[64,2048]{1,0:T(8,128)(2,1)S(1)}, u32[]{:S(2)}, u32[]{:S(2)}) collective-permute-start(bf16[64,2048]{1,0:T(8,128)(2,1)S(1)} %get-tuple-element.79), channel_id=1, source_target_pairs={{0,8},{8,16},{16,24},{24,28},{28,20},{20,12},{12,4},{4,0},{1,9},{9... | collective-permute-start | bytes 786440 | tf_op jit(solution)/shard_map/out_projection/ppermute | solution.py:37
  58.5 7.9 %collective-permute-start.3 = (bf16[64,2048]{1,0:T(8,128)(2,1)S(1)}, bf16[64,2048]{1,0:T(8,128)(2,1)S(1)}, u32[]{:S(2)}, u32[]{:S(2)}) collective-permute-start(bf16[64,2048]{1,0:T(8,128)(2,1)S(1)} %get-tuple-element.80), channel_id=1, source_target_pairs={{0,4},{8,0},{16,8},{24,16},{28,24},{20,28},{12,20},{4,12},{1,5},{9... | collective-permute-start | bytes 786440 | tf_op jit(solution)/shard_map/out_projection/ppermute | solution.py:37
  67.8 6.4 %collective-permute-start.4 = (bf16[64,2048]{1,0:T(8,128)(2,1)S(1)}, bf16[64,2048]{1,0:T(8,128)(2,1)S(1)}, u32[]{:S(2)}, u32[]{:S(2)}) collective-permute-start(bf16[64,2048]{1,0:T(8,128)(2,1)S(1)} %get-tuple-element.83), channel_id=1, source_target_pairs={{0,8},{8,16},{16,24},{24,28},{28,20},{20,12},{12,4},{4,0},{1,9},{9... | collective-permute-start | bytes 786440 | tf_op jit(solution)/shard_map/out_projection/ppermute | solution.py:37
  69.6 6.4 %collective-permute-start.5 = (bf16[64,2048]{1,0:T(8,128)(2,1)S(1)}, bf16[64,2048]{1,0:T(8,128)(2,1)S(1)}, u32[]{:S(2)}, u32[]{:S(2)}) collective-permute-start(bf16[64,2048]{1,0:T(8,128)(2,1)S(1)} %get-tuple-element.84), channel_id=1, source_target_pairs={{0,4},{8,0},{16,8},{24,16},{28,24},{20,28},{12,20},{4,12},{1,5},{9... | collective-permute-start | bytes 786440 | tf_op jit(solution)/shard_map/out_projection/ppermute | solution.py:37
  77.3 6.4 %collective-permute-start.6 = (bf16[64,2048]{1,0:T(8,128)(2,1)S(1)}, bf16[64,2048]{1,0:T(8,128)(2,1)S(1)}, u32[]{:S(2)}, u32[]{:S(2)}) collective-permute-start(bf16[64,2048]{1,0:T(8,128)(2,1)S(1)} %get-tuple-element.87), channel_id=1, source_target_pairs={{0,8},{8,16},{16,24},{24,28},{28,20},{20,12},{12,4},{4,0},{1,9},{9... | collective-permute-start | bytes 786440 | tf_op jit(solution)/shard_map/out_projection/ppermute | solution.py:37
  79.1 6.6 %collective-permute-start.7 = (bf16[64,2048]{1,0:T(8,128)(2,1)S(1)}, bf16[64,2048]{1,0:T(8,128)(2,1)S(1)}, u32[]{:S(2)}, u32[]{:S(2)}) collective-permute-start(bf16[64,2048]{1,0:T(8,128)(2,1)S(1)} %get-tuple-element.88), channel_id=1, source_target_pairs={{0,4},{8,0},{16,8},{24,16},{28,24},{20,28},{12,20},{4,12},{1,5},{9... | collective-permute-start | bytes 786440 | tf_op jit(solution)/shard_map/out_projection/ppermute | solution.py:37
  86.9 7.7 %collective-permute-start.8 = (bf16[64,2048]{1,0:T(8,128)(2,1)S(1)}, bf16[64,2048]{1,0:T(8,128)(2,1)S(1)}, u32[]{:S(2)}, u32[]{:S(2)}) collective-permute-start(bf16[64,2048]{1,0:T(8,128)(2,1)S(1)} %get-tuple-element.91), channel_id=1, source_target_pairs={{0,8},{8,16},{16,24},{24,28},{28,20},{20,12},{12,4},{4,0},{1,9},{9... | collective-permute-start | bytes 786440 | tf_op jit(solution)/shard_map/out_projection/ppermute | solution.py:37
  87.5 7.8 %collective-permute-start.9 = (bf16[64,2048]{1,0:T(8,128)(2,1)S(1)}, bf16[64,2048]{1,0:T(8,128)(2,1)S(1)}, u32[]{:S(2)}, u32[]{:S(2)}) collective-permute-start(bf16[64,2048]{1,0:T(8,128)(2,1)S(1)} %get-tuple-element.92), channel_id=1, source_target_pairs={{0,4},{8,0},{16,8},{24,16},{28,24},{20,28},{12,20},{4,12},{1,5},{9... | collective-permute-start | bytes 786440 | tf_op jit(solution)/shard_map/out_projection/ppermute | solution.py:37
  96.5 9.0 %collective-permute-start.10 = (bf16[64,2048]{1,0:T(8,128)(2,1)S(1)}, bf16[64,2048]{1,0:T(8,128)(2,1)S(1)}, u32[]{:S(2)}, u32[]{:S(2)}) collective-permute-start(bf16[64,2048]{1,0:T(8,128)(2,1)S(1)} %get-tuple-element.95), channel_id=1, source_target_pairs={{0,8},{8,16},{16,24},{24,28},{28,20},{20,12},{12,4},{4,0},{1,9},{9... | collective-permute-start | bytes 786440 | tf_op jit(solution)/shard_map/out_projection/ppermute | solution.py:37
  97.1 9.2 %collective-permute-start.11 = (bf16[64,2048]{1,0:T(8,128)(2,1)S(1)}, bf16[64,2048]{1,0:T(8,128)(2,1)S(1)}, u32[]{:S(2)}, u32[]{:S(2)}) collective-permute-start(bf16[64,2048]{1,0:T(8,128)(2,1)S(1)} %get-tuple-element.96), channel_id=1, source_target_pairs={{0,4},{8,0},{16,8},{24,16},{28,24},{20,28},{12,20},{4,12},{1,5},{9... | collective-permute-start | bytes 786440 | tf_op jit(solution)/shard_map/out_projection/ppermute | solution.py:37
  102.3 15.5 %copy-start.3 = (bf16[128,2048]{1,0:T(8,128)(2,1)S(1)}, bf16[128,2048]{1,0:T(8,128)(2,1)}, u32[]{:S(2)}) copy-start(bf16[128,2048]{1,0:T(8,128)(2,1)} %param.12) | copy-start | bytes 1572868
  107.6 8.4 %collective-permute-start.12 = (bf16[64,2048]{1,0:T(8,128)(2,1)S(1)}, bf16[64,2048]{1,0:T(8,128)(2,1)S(1)}, u32[]{:S(2)}, u32[]{:S(2)}) collective-permute-start(bf16[64,2048]{1,0:T(8,128)(2,1)S(1)} %get-tuple-element.99), channel_id=1, source_target_pairs={{0,8},{8,16},{16,24},{24,28},{28,20},{20,12},{12,4},{4,0},{1,9},{9... | collective-permute-start | bytes 786440 | tf_op jit(solution)/shard_map/out_projection/ppermute | solution.py:37
  108.7 7.7 %collective-permute-start.13 = (bf16[64,2048]{1,0:T(8,128)(2,1)S(1)}, bf16[64,2048]{1,0:T(8,128)(2,1)S(1)}, u32[]{:S(2)}, u32[]{:S(2)}) collective-permute-start(bf16[64,2048]{1,0:T(8,128)(2,1)S(1)} %get-tuple-element.100), channel_id=1, source_target_pairs={{0,4},{8,0},{16,8},{24,16},{28,24},{20,28},{12,20},{4,12},{1,5},{9... | collective-permute-start | bytes 786440 | tf_op jit(solution)/shard_map/out_projection/ppermute | solution.py:37
  111.8 6.2 %copy-start.5 = (f32[2048]{0:T(1024)S(1)}, f32[2048]{0:T(1024)}, u32[]{:S(2)}) copy-start(f32[2048]{0:T(1024)} %param.15) | copy-start | bytes 24580
  118.3 7.4 %collective-permute-start.15 = (bf16[64,2048]{1,0:T(8,128)(2,1)S(1)}, bf16[64,2048]{1,0:T(8,128)(2,1)S(1)}, u32[]{:S(2)}, u32[]{:S(2)}) collective-permute-start(bf16[64,2048]{1,0:T(8,128)(2,1)S(1)} %get-tuple-element.182), channel_id=1, source_target_pairs={{0,4},{8,0},{16,8},{24,16},{28,24},{20,28},{12,20},{4,12},{1,5},{9... | collective-permute-start | bytes 786440 | tf_op jit(solution)/shard_map/dispatch_gather/ppermute | solution.py:55
  119.9 6.4 %collective-permute-start.14 = (bf16[64,2048]{1,0:T(8,128)(2,1)S(1)}, bf16[64,2048]{1,0:T(8,128)(2,1)S(1)}, u32[]{:S(2)}, u32[]{:S(2)}) collective-permute-start(bf16[64,2048]{1,0:T(8,128)(2,1)S(1)} %get-tuple-element.183), channel_id=1, source_target_pairs={{0,8},{8,16},{16,24},{24,28},{28,20},{20,12},{12,4},{4,0},{1,9},{9... | collective-permute-start | bytes 786440 | tf_op jit(solution)/shard_map/dispatch_gather/ppermute | solution.py:55
  126.2 6.5 %collective-permute-start.16 = (bf16[64,2048]{1,0:T(8,128)(2,1)S(1)}, bf16[64,2048]{1,0:T(8,128)(2,1)S(1)}, u32[]{:S(2)}, u32[]{:S(2)}) collective-permute-start(bf16[64,2048]{1,0:T(8,128)(2,1)S(1)} %collective-permute-done.14), channel_id=1, source_target_pairs={{0,8},{8,16},{16,24},{24,28},{28,20},{20,12},{12,4},{4,0},{1,9},{9... | collective-permute-start | bytes 786440 | tf_op jit(solution)/shard_map/dispatch_gather/ppermute | solution.py:55
  126.9 6.8 %collective-permute-start.17 = (bf16[64,2048]{1,0:T(8,128)(2,1)S(1)}, bf16[64,2048]{1,0:T(8,128)(2,1)S(1)}, u32[]{:S(2)}, u32[]{:S(2)}) collective-permute-start(bf16[64,2048]{1,0:T(8,128)(2,1)S(1)} %collective-permute-done.15), channel_id=1, source_target_pairs={{0,4},{8,0},{16,8},{24,16},{28,24},{20,28},{12,20},{4,12},{1,5},{9... | collective-permute-start | bytes 786440 | tf_op jit(solution)/shard_map/dispatch_gather/ppermute | solution.py:55
  133.7 16.0 %collective-permute-start.18 = (bf16[64,2048]{1,0:T(8,128)(2,1)S(1)}, bf16[64,2048]{1,0:T(8,128)(2,1)S(1)}, u32[]{:S(2)}, u32[]{:S(2)}) collective-permute-start(bf16[64,2048]{1,0:T(8,128)(2,1)S(1)} %collective-permute-done.16), channel_id=1, source_target_pairs={{0,8},{8,16},{16,24},{24,28},{28,20},{20,12},{12,4},{4,0},{1,9},{9... | collective-permute-start | bytes 786440 | tf_op jit(solution)/shard_map/dispatch_gather/ppermute | solution.py:55
  135.7 14.0 %collective-permute-start.19 = (bf16[64,2048]{1,0:T(8,128)(2,1)S(1)}, bf16[64,2048]{1,0:T(8,128)(2,1)S(1)}, u32[]{:S(2)}, u32[]{:S(2)}) collective-permute-start(bf16[64,2048]{1,0:T(8,128)(2,1)S(1)} %collective-permute-done.17), channel_id=1, source_target_pairs={{0,4},{8,0},{16,8},{24,16},{28,24},{20,28},{12,20},{4,12},{1,5},{9... | collective-permute-start | bytes 786440 | tf_op jit(solution)/shard_map/dispatch_gather/ppermute | solution.py:55
  135.8 9.5 %slice-start.6 = ((s8[6291456]{0:T(1024)(128)(4,1)}), s8[4194304]{0:T(1024)(128)(4,1)S(1)}, s32[]{:S(2)}) async-start(s8[6291456]{0:T(1024)(128)(4,1)} %bitcast.241), calls=%async_computation.8 | async-start | bytes 8388608
  140.5 4.7 %slice-start.7 = ((s8[6291456]{0:T(1024)(128)(4,1)}), s8[2097152]{0:T(1024)(128)(4,1)S(1)}, s32[]{:S(2)}) async-start(s8[6291456]{0:T(1024)(128)(4,1)} %bitcast.241), calls=%async_computation.9 | async-start | bytes 4194304
  145.3 16.0 %slice-start = ((s8[12582912]{0:T(1024)(128)(4,1)}), s8[4194304]{0:T(1024)(128)(4,1)S(1)}, s32[]{:S(2)}) async-start(s8[12582912]{0:T(1024)(128)(4,1)} %bitcast.237), calls=%async_computation.2 | async-start | bytes 8388608
  145.3 16.0 %slice-start.1 = ((s8[12582912]{0:T(1024)(128)(4,1)}), s8[4194304]{0:T(1024)(128)(4,1)S(1)}, s32[]{:S(2)}) async-start(s8[12582912]{0:T(1024)(128)(4,1)} %bitcast.237), calls=%async_computation.3 | async-start | bytes 8388608
  146.4 14.9 %slice-start.2 = ((s8[12582912]{0:T(1024)(128)(4,1)}), s8[4194304]{0:T(1024)(128)(4,1)S(1)}, s32[]{:S(2)}) async-start(s8[12582912]{0:T(1024)(128)(4,1)} %bitcast.237), calls=%async_computation.4 | async-start | bytes 8388608
  147.5 8.4 %collective-permute-start.28 = (bf16[64,2048]{1,0:T(8,128)(2,1)S(1)}, bf16[64,2048]{1,0:T(8,128)(2,1)S(1)}, u32[]{:S(2)}, u32[]{:S(2)}) collective-permute-start(bf16[64,2048]{1,0:T(8,128)(2,1)S(1)} %get-tuple-element.118), channel_id=1, source_target_pairs={{0,8},{8,16},{16,24},{24,28},{28,20},{20,12},{12,4},{4,0},{1,9},{9... | collective-permute-start | bytes 786440 | tf_op jit(solution)/shard_map/combine_return/ppermute | solution.py:75
  149.6 6.5 %collective-permute-start.29 = (bf16[64,2048]{1,0:T(8,128)(2,1)S(1)}, bf16[64,2048]{1,0:T(8,128)(2,1)S(1)}, u32[]{:S(2)}, u32[]{:S(2)}) collective-permute-start(bf16[64,2048]{1,0:T(8,128)(2,1)S(1)} %get-tuple-element.119), channel_id=1, source_target_pairs={{0,4},{8,0},{16,8},{24,16},{28,24},{20,28},{12,20},{4,12},{1,5},{9... | collective-permute-start | bytes 786440 | tf_op jit(solution)/shard_map/combine_return/ppermute | solution.py:75
  149.7 9.1 %collective-permute-start.20 = (bf16[64,2048]{1,0:T(8,128)(2,1)S(1)}, bf16[64,2048]{1,0:T(8,128)(2,1)S(1)}, u32[]{:S(2)}, u32[]{:S(2)}) collective-permute-start(bf16[64,2048]{1,0:T(8,128)(2,1)S(1)} %collective-permute-done.18), channel_id=1, source_target_pairs={{0,8},{8,16},{16,24},{24,28},{28,20},{20,12},{12,4},{4,0},{1,9},{9... | collective-permute-start | bytes 786440 | tf_op jit(solution)/shard_map/dispatch_gather/ppermute | solution.py:55
  151.8 7.4 %collective-permute-start.21 = (bf16[64,2048]{1,0:T(8,128)(2,1)S(1)}, bf16[64,2048]{1,0:T(8,128)(2,1)S(1)}, u32[]{:S(2)}, u32[]{:S(2)}) collective-permute-start(bf16[64,2048]{1,0:T(8,128)(2,1)S(1)} %collective-permute-done.19), channel_id=1, source_target_pairs={{0,4},{8,0},{16,8},{24,16},{28,24},{20,28},{12,20},{4,12},{1,5},{9... | collective-permute-start | bytes 786440 | tf_op jit(solution)/shard_map/dispatch_gather/ppermute | solution.py:55
  156.3 9.3 %collective-permute-start.30 = (bf16[64,2048]{1,0:T(8,128)(2,1)S(1)}, bf16[64,2048]{1,0:T(8,128)(2,1)S(1)}, u32[]{:S(2)}, u32[]{:S(2)}) collective-permute-start(bf16[64,2048]{1,0:T(8,128)(2,1)S(1)} %get-tuple-element.122), channel_id=1, source_target_pairs={{0,8},{8,16},{16,24},{24,28},{28,20},{20,12},{12,4},{4,0},{1,9},{9... | collective-permute-start | bytes 786440 | tf_op jit(solution)/shard_map/combine_return/ppermute | solution.py:75
  156.5 9.2 %collective-permute-start.31 = (bf16[64,2048]{1,0:T(8,128)(2,1)S(1)}, bf16[64,2048]{1,0:T(8,128)(2,1)S(1)}, u32[]{:S(2)}, u32[]{:S(2)}) collective-permute-start(bf16[64,2048]{1,0:T(8,128)(2,1)S(1)} %get-tuple-element.123), channel_id=1, source_target_pairs={{0,4},{8,0},{16,8},{24,16},{28,24},{20,28},{12,20},{4,12},{1,5},{9... | collective-permute-start | bytes 786440 | tf_op jit(solution)/shard_map/combine_return/ppermute | solution.py:75
  159.2 12.0 %collective-permute-start.22 = (bf16[64,2048]{1,0:T(8,128)(2,1)S(1)}, bf16[64,2048]{1,0:T(8,128)(2,1)S(1)}, u32[]{:S(2)}, u32[]{:S(2)}) collective-permute-start(bf16[64,2048]{1,0:T(8,128)(2,1)S(1)} %collective-permute-done.20), channel_id=1, source_target_pairs={{0,8},{8,16},{16,24},{24,28},{28,20},{20,12},{12,4},{4,0},{1,9},{9... | collective-permute-start | bytes 786440 | tf_op jit(solution)/shard_map/dispatch_gather/ppermute | solution.py:55
  159.2 12.2 %collective-permute-start.23 = (bf16[64,2048]{1,0:T(8,128)(2,1)S(1)}, bf16[64,2048]{1,0:T(8,128)(2,1)}, u32[]{:S(2)}, u32[]{:S(2)}) collective-permute-start(bf16[64,2048]{1,0:T(8,128)(2,1)S(1)} %collective-permute-done.21), channel_id=1, source_target_pairs={{0,4},{8,0},{16,8},{24,16},{28,24},{20,28},{12,20},{4,12},{1,5},{9... | collective-permute-start | bytes 786440 | tf_op jit(solution)/shard_map/dispatch_gather/ppermute | solution.py:55
  168.8 9.6 %collective-permute-start.32 = (bf16[64,2048]{1,0:T(8,128)(2,1)}, bf16[64,2048]{1,0:T(8,128)(2,1)}, u32[]{:S(2)}, u32[]{:S(2)}) collective-permute-start(bf16[64,2048]{1,0:T(8,128)(2,1)} %get-tuple-element.126), channel_id=1, source_target_pairs={{0,8},{8,16},{16,24},{24,28},{28,20},{20,12},{12,4},{4,0},{1,9},{9... | collective-permute-start | bytes 786440 | tf_op jit(solution)/shard_map/combine_return/ppermute | solution.py:75
  170.0 8.8 %collective-permute-start.33 = (bf16[64,2048]{1,0:T(8,128)(2,1)}, bf16[64,2048]{1,0:T(8,128)(2,1)}, u32[]{:S(2)}, u32[]{:S(2)}) collective-permute-start(bf16[64,2048]{1,0:T(8,128)(2,1)} %get-tuple-element.127), channel_id=1, source_target_pairs={{0,4},{8,0},{16,8},{24,16},{28,24},{20,28},{12,20},{4,12},{1,5},{9... | collective-permute-start | bytes 786440 | tf_op jit(solution)/shard_map/combine_return/ppermute | solution.py:75
  171.4 11.5 %collective-permute-start.24 = (bf16[64,2048]{1,0:T(8,128)(2,1)S(1)}, bf16[64,2048]{1,0:T(8,128)(2,1)S(1)}, u32[]{:S(2)}, u32[]{:S(2)}) collective-permute-start(bf16[64,2048]{1,0:T(8,128)(2,1)S(1)} %collective-permute-done.22), channel_id=1, source_target_pairs={{0,8},{8,16},{16,24},{24,28},{28,20},{20,12},{12,4},{4,0},{1,9},{9... | collective-permute-start | bytes 786440 | tf_op jit(solution)/shard_map/dispatch_gather/ppermute | solution.py:55
  172.6 10.4 %collective-permute-start.25 = (bf16[64,2048]{1,0:T(8,128)(2,1)}, bf16[64,2048]{1,0:T(8,128)(2,1)S(1)}, u32[]{:S(2)}, u32[]{:S(2)}) collective-permute-start(bf16[64,2048]{1,0:T(8,128)(2,1)} %collective-permute-done.23), channel_id=1, source_target_pairs={{0,4},{8,0},{16,8},{24,16},{28,24},{20,28},{12,20},{4,12},{1,5},{9... | collective-permute-start | bytes 786440 | tf_op jit(solution)/shard_map/dispatch_gather/ppermute | solution.py:55
  179.9 6.4 %collective-permute-start.34 = (bf16[64,2048]{1,0:T(8,128)(2,1)S(1)}, bf16[64,2048]{1,0:T(8,128)(2,1)S(1)}, u32[]{:S(2)}, u32[]{:S(2)}) collective-permute-start(bf16[64,2048]{1,0:T(8,128)(2,1)S(1)} %get-tuple-element.130), channel_id=1, source_target_pairs={{0,8},{8,16},{16,24},{24,28},{28,20},{20,12},{12,4},{4,0},{1,9},{9... | collective-permute-start | bytes 786440 | tf_op jit(solution)/shard_map/combine_return/ppermute | solution.py:75
  180.0 6.4 %collective-permute-start.35 = (bf16[64,2048]{1,0:T(8,128)(2,1)S(1)}, bf16[64,2048]{1,0:T(8,128)(2,1)S(1)}, u32[]{:S(2)}, u32[]{:S(2)}) collective-permute-start(bf16[64,2048]{1,0:T(8,128)(2,1)S(1)} %get-tuple-element.131), channel_id=1, source_target_pairs={{0,4},{8,0},{16,8},{24,16},{28,24},{20,28},{12,20},{4,12},{1,5},{9... | collective-permute-start | bytes 786440 | tf_op jit(solution)/shard_map/combine_return/ppermute | solution.py:75
  183.0 6.4 %collective-permute-start.26 = (bf16[64,2048]{1,0:T(8,128)(2,1)S(1)}, bf16[64,2048]{1,0:T(8,128)(2,1)S(1)}, u32[]{:S(2)}, u32[]{:S(2)}) collective-permute-start(bf16[64,2048]{1,0:T(8,128)(2,1)S(1)} %collective-permute-done.24), channel_id=1, source_target_pairs={{0,8},{8,16},{16,24},{24,28},{28,20},{20,12},{12,4},{4,0},{1,9},{9... | collective-permute-start | bytes 786440 | tf_op jit(solution)/shard_map/dispatch_gather/ppermute | solution.py:55
  183.1 6.4 %collective-permute-start.27 = (bf16[64,2048]{1,0:T(8,128)(2,1)S(1)}, bf16[64,2048]{1,0:T(8,128)(2,1)S(1)}, u32[]{:S(2)}, u32[]{:S(2)}) collective-permute-start(bf16[64,2048]{1,0:T(8,128)(2,1)S(1)} %collective-permute-done.25), channel_id=1, source_target_pairs={{0,4},{8,0},{16,8},{24,16},{28,24},{20,28},{12,20},{4,12},{1,5},{9... | collective-permute-start | bytes 786440 | tf_op jit(solution)/shard_map/dispatch_gather/ppermute | solution.py:55
  189.5 6.0 %slice-start.3 = ((s8[12582912]{0:T(1024)(128)(4,1)}), s8[4194304]{0:T(1024)(128)(4,1)S(1)}, s32[]{:S(2)}) async-start(s8[12582912]{0:T(1024)(128)(4,1)} %bitcast.239), calls=%async_computation.5 | async-start | bytes 8388608
  189.7 5.7 %slice-start.4 = ((s8[12582912]{0:T(1024)(128)(4,1)}), s8[4194304]{0:T(1024)(128)(4,1)S(1)}, s32[]{:S(2)}) async-start(s8[12582912]{0:T(1024)(128)(4,1)} %bitcast.239), calls=%async_computation.6 | async-start | bytes 8388608
  189.7 6.3 %slice-start.5 = ((s8[12582912]{0:T(1024)(128)(4,1)}), s8[4194304]{0:T(1024)(128)(4,1)S(1)}, s32[]{:S(2)}) async-start(s8[12582912]{0:T(1024)(128)(4,1)} %bitcast.239), calls=%async_computation.7 | async-start | bytes 8388608
  189.8 9.7 %slice-start.8 = ((s8[6291456]{0:T(1024)(128)(4,1)}), s8[4194304]{0:T(1024)(128)(4,1)S(1)}, s32[]{:S(2)}) async-start(s8[6291456]{0:T(1024)(128)(4,1)} %bitcast.243), calls=%async_computation.10 | async-start | bytes 8388608
  196.1 3.4 %slice-start.9 = ((s8[6291456]{0:T(1024)(128)(4,1)}), s8[2097152]{0:T(1024)(128)(4,1)S(1)}, s32[]{:S(2)}) async-start(s8[6291456]{0:T(1024)(128)(4,1)} %bitcast.243), calls=%async_computation.11 | async-start | bytes 4194304
  203.3 8.5 %collective-permute-start.36 = (bf16[64,2048]{1,0:T(8,128)(2,1)S(1)}, bf16[64,2048]{1,0:T(8,128)(2,1)S(1)}, u32[]{:S(2)}, u32[]{:S(2)}) collective-permute-start(bf16[64,2048]{1,0:T(8,128)(2,1)S(1)} %get-tuple-element.134), channel_id=1, source_target_pairs={{0,8},{8,16},{16,24},{24,28},{28,20},{20,12},{12,4},{4,0},{1,9},{9... | collective-permute-start | bytes 786440 | tf_op jit(solution)/shard_map/combine_return/ppermute | solution.py:75
  204.6 8.4 %collective-permute-start.37 = (bf16[64,2048]{1,0:T(8,128)(2,1)S(1)}, bf16[64,2048]{1,0:T(8,128)(2,1)S(1)}, u32[]{:S(2)}, u32[]{:S(2)}) collective-permute-start(bf16[64,2048]{1,0:T(8,128)(2,1)S(1)} %get-tuple-element.135), channel_id=1, source_target_pairs={{0,4},{8,0},{16,8},{24,16},{28,24},{20,28},{12,20},{4,12},{1,5},{9... | collective-permute-start | bytes 786440 | tf_op jit(solution)/shard_map/combine_return/ppermute | solution.py:75
  213.1 6.4 %collective-permute-start.38 = (bf16[64,2048]{1,0:T(8,128)(2,1)S(1)}, bf16[64,2048]{1,0:T(8,128)(2,1)S(1)}, u32[]{:S(2)}, u32[]{:S(2)}) collective-permute-start(bf16[64,2048]{1,0:T(8,128)(2,1)S(1)} %get-tuple-element.138), channel_id=1, source_target_pairs={{0,8},{8,16},{16,24},{24,28},{28,20},{20,12},{12,4},{4,0},{1,9},{9... | collective-permute-start | bytes 786440 | tf_op jit(solution)/shard_map/combine_return/ppermute | solution.py:75
  214.9 6.4 %collective-permute-start.39 = (bf16[64,2048]{1,0:T(8,128)(2,1)S(1)}, bf16[64,2048]{1,0:T(8,128)(2,1)S(1)}, u32[]{:S(2)}, u32[]{:S(2)}) collective-permute-start(bf16[64,2048]{1,0:T(8,128)(2,1)S(1)} %get-tuple-element.139), channel_id=1, source_target_pairs={{0,4},{8,0},{16,8},{24,16},{28,24},{20,28},{12,20},{4,12},{1,5},{9... | collective-permute-start | bytes 786440 | tf_op jit(solution)/shard_map/combine_return/ppermute | solution.py:75
  221.4 7.4 %copy-start.6 = (f32[2048]{0:T(1024)S(1)}, f32[2048]{0:T(1024)}, u32[]{:S(2)}) copy-start(f32[2048]{0:T(1024)} %param.20) | copy-start | bytes 24580
  221.4 6.4 %collective-permute-start.40 = (bf16[64,2048]{1,0:T(8,128)(2,1)S(1)}, bf16[64,2048]{1,0:T(8,128)(2,1)S(1)}, u32[]{:S(2)}, u32[]{:S(2)}) collective-permute-start(bf16[64,2048]{1,0:T(8,128)(2,1)S(1)} %get-tuple-element.142), channel_id=1, source_target_pairs={{0,8},{8,16},{16,24},{24,28},{28,20},{20,12},{12,4},{4,0},{1,9},{9... | collective-permute-start | bytes 786440 | tf_op jit(solution)/shard_map/combine_return/ppermute | solution.py:75
  222.0 6.4 %collective-permute-start.41 = (bf16[64,2048]{1,0:T(8,128)(2,1)S(1)}, bf16[64,2048]{1,0:T(8,128)(2,1)S(1)}, u32[]{:S(2)}, u32[]{:S(2)}) collective-permute-start(bf16[64,2048]{1,0:T(8,128)(2,1)S(1)} %get-tuple-element.143), channel_id=1, source_target_pairs={{0,4},{8,0},{16,8},{24,16},{28,24},{20,28},{12,20},{4,12},{1,5},{9... | collective-permute-start | bytes 786440 | tf_op jit(solution)/shard_map/combine_return/ppermute | solution.py:75
  228.5 1.9 copy-start.1

commit v19 on v9

--- a/solution.py
+++ b/solution.py
@@ -154,7 +154,7 @@
             for step in steps:
                 rows_in += list(arrived[step])
                 weights_in += list(step_weights(step))
-            if c == len(chunks) - 1:
+            if c == 0:
                 rows_in.append(normed)
                 weights_in.append(lax.dynamic_index_in_dim(weight_blocks, me, 0, keepdims=False))
             mixed = expert_mix(
@@ -163,7 +163,7 @@
             for i, step in enumerate(steps):
                 pieces[step] = (mixed[(2 * i) * half : (2 * i + 1) * half],
                                 mixed[(2 * i + 1) * half : (2 * i + 2) * half])
-            if c == len(chunks) - 1:
+            if c == 0:
                 own_part = mixed[2 * len(steps) * half :]
 
     with jax.named_scope("combine_return"):

time: 220 us -> 225 us (1.023)
  waiting for transfers between devices: 69.3 us -> 79.4 us
  matrix products: 30.8 us -> 27.3 us
    ppermute x7, waiting for transfers between devices: 9.08 us -> 17.9 us  [ring_all_gather(): lax.ppermute(got_fwd, 'ep', forward)]
    ppermute x7, waiting for transfers between devices: 17.1 us -> 21.4 us  [ring_reduce_scatter_steps(): lax.ppermute(send_fwd, 'ep', forward)]
    ppermute x7, waiting for transfers between devices: 7.35 us -> 3.4 us  [ring_all_gather(): lax.ppermute(got_bwd, 'ep', backward)]
    dot_general x8, matrix products: 20.1 us -> 16.6 us  [expert_mix(): projected_up = jnp.dot(rows, gate_up[e], preferred_element_type=jnp.float32)]
  transfers between devices with their start and end apart: 44 -> 44, of which waited for: 34 -> 35; matrix products, arithmetic and copies ran while one was open for 15% -> 10% of each run, Pallas kernels for 0% -> 0%
where the time goes in v19:
time: 225 us; the launch traced here: 224 us
  waiting for transfers between devices  79.4 us (35%)
  starting transfers between devices  54.5 us (24%)
  between operations  40.7 us (18%)
  matrix products  27.3 us (12%)
  other arithmetic  13.8 us (6%)
  local copies, waits for them, and re-layouts  8.18 us (4%)
    ppermute x7, waiting for transfers between devices, ring_reduce_scatter_steps(): lax.ppermute(send_fwd, 'ep', forward)  21.4 us
    ppermute x7, waiting for transfers between devices, ring_all_gather(): lax.ppermute(got_fwd, 'ep', forward)  17.9 us
    dot_general x8, matrix products, expert_mix(): projected_up = jnp.dot(rows, gate_up[e], preferred_element_type=jnp.float32)  16.6 us
    ppermute x7, waiting for transfers between devices, ring_reduce_scatter(): lax.ppermute(send_fwd, 'ep', forward)  11.8 us
    all_to_all x1, waiting for transfers between devices, body(): lax.all_to_all(columns, 'ep', split_axis=0, concat_axis=0, tiled=True)  8.41 us
    dot_general x8, matrix products, expert_mix(): jnp.dot(activated, down[e], preferred_element_type=jnp.float32)  8.35 us
    ppermute x7, waiting for transfers between devices, ring_reduce_scatter(): lax.ppermute(send_bwd, 'ep', backward)  7.92 us
    convert_element_type x6, other arithmetic, ring_reduce_scatter(): send_bwd.astype(jnp.bfloat16)  7.86 us
  transfers between devices with their start and end apart: 44, of which 35 were waited for; matrix products, arithmetic and copies ran while one was open for 10% of the time, Pallas kernels for 0%

profile of v19, /device:TPU:0, one launch (start us, length us, event | category | flops | bytes accessed | tf_op | source)
XLA Modules:
  0.0 223.9 jit_solution(633161206171203779)
XLA Ops:
  0.7 1.5 select_reduce_fusion
  2.1 7.3 %all-to-all-start.1 = ((f32[8,128,2]{1,2,0:T(2,128)}), f32[8,128,2]{1,2,0:T(2,128)S(1)}, u32[]{:S(2)}, u32[]{:S(2)}) async-start(f32[8,128,2]{1,2,0:T(2,128)} %bitcast.2), calls=%async_computation.1 | async-start | bytes 16384 | tf_op jit(solution)/shard_map/route_weights/all_to_all | solution.py:118
  9.4 2.3 %copy.25 = bf16[16,8,8,512]{3,2,0,1:T(8,128)(2,1)} copy(bf16[16,8,8,512]{3,2,1,0:T(8,128)(2,1)} %bitcast.238) | data formatting | bytes 2097152 | tf_op jit(solution)/shard_map/out_projection/reshape | solution.py:122
  11.7 4.2 %all-to-all-done.1 = f32[8,128,2]{1,2,0:T(2,128)S(1)} async-done(((f32[8,128,2]{1,2,0:T(2,128)}), f32[8,128,2]{1,2,0:T(2,128)S(1)}, u32[]{:S(2)}, u32[]{:S(2)}) %all-to-all-start.1) | async-done | bytes 8224 | tf_op jit(solution)/shard_map/route_weights/all_to_all | solution.py:118
  15.9 3.6 %all-to-all-start = ((bf16[8,128,512]{2,1,0:T(8,128)(2,1)}), bf16[8,128,512]{2,1,0:T(8,128)(2,1)S(1)}, u32[]{:S(2)}, u32[]{:S(2)}) async-start(bf16[8,128,512]{2,1,0:T(8,128)(2,1)} %bitcast.236), calls=%async_computation | async-start | bytes 2097152 | tf_op jit(solution)/shard_map/out_projection/all_to_all | solution.py:123
  35.8 8.4 %all-to-all-done = bf16[8,128,512]{2,1,0:T(8,128)(2,1)S(1)} async-done(((bf16[8,128,512]{2,1,0:T(8,128)(2,1)}), bf16[8,128,512]{2,1,0:T(8,128)(2,1)S(1)}, u32[]{:S(2)}, u32[]{:S(2)}) %all-to-all-start) | async-done | bytes 1048608 | tf_op jit(solution)/shard_map/out_projection/all_to_all | solution.py:123
  44.2 2.4 %fusion.111 = f32[8,128,2048]{2,1,0:T(8,128)S(1)} fusion(bf16[8,128,512]{2,1,0:T(8,128)(2,1)S(1)} %all-to-all-done, bf16[512,2048]{1,0:T(8,128)(2,1)S(1)} %copy-done), kind=kOutput, calls=%fused_computation.64 | convolution fusion | flops 2147483648 | bytes 11534336 | tf_op jit(solution)/shard_map/out_projection/dot_general | solution.py:125
  46.6 3.3 %copy-done.2 = f32[8,128,2048]{2,1,0:T(8,128)} copy-done((f32[8,128,2048]{2,1,0:T(8,128)}, f32[8,128,2048]{2,1,0:T(8,128)S(1)}, u32[]{:S(2)}) %copy-start.2) | copy-done | bytes 8388632
  50.0 2.0 collective-permute-start.1
  56.6 1.3 fusion.159
  58.5 1.5 collective-permute-start.3
  64.4 2.1 collective-permute-done.3
  66.5 1.3 fusion.157
  67.8 1.8 collective-permute-start.4
  74.2 1.8 collective-permute-done.5
  76.0 1.3 fusion.155
  77.3 1.8 collective-permute-start.6
  83.7 1.9 collective-permute-done.7
  85.6 1.3 fusion.153
  87.5 1.5 collective-permute-start.9
  92.7 1.9 collective-permute-done.8
  95.2 1.3 fusion.151
  97.1 1.5 collective-permute-start.11
  105.9 1.3 fusion.149
  107.2 1.6 collective-permute-start.12
  109.6 6.7 %collective-permute-done.12 = bf16[64,2048]{1,0:T(8,128)(2,1)S(1)} collective-permute-done((bf16[64,2048]{1,0:T(8,128)(2,1)S(1)}, bf16[64,2048]{1,0:T(8,128)(2,1)S(1)}, u32[]{:S(2)}, u32[]{:S(2)}) %collective-permute-start.12) | collective-permute-done | bytes 262176 | tf_op jit(solution)/shard_map/out_projection/ppermute | solution.py:37
  117.1 1.3 fusion.172
  119.6 1.4 collective-permute-start.15
  121.1 4.3 %collective-permute-done.14 = bf16[64,2048]{1,0:T(8,128)(2,1)S(1)} collective-permute-done((bf16[64,2048]{1,0:T(8,128)(2,1)S(1)}, bf16[64,2048]{1,0:T(8,128)(2,1)S(1)}, u32[]{:S(2)}, u32[]{:S(2)}) %collective-permute-start.14) | collective-permute-done | bytes 262176 | tf_op jit(solution)/shard_map/dispatch_gather/ppermute | solution.py:55
  126.3 1.7 collective-permute-start.17
  128.0 4.3 %collective-permute-done.16 = bf16[64,2048]{1,0:T(8,128)(2,1)S(1)} collective-permute-done((bf16[64,2048]{1,0:T(8,128)(2,1)S(1)}, bf16[64,2048]{1,0:T(8,128)(2,1)S(1)}, u32[]{:S(2)}, u32[]{:S(2)}) %collective-permute-start.16) | collective-permute-done | bytes 262176 | tf_op jit(solution)/shard_map/dispatch_gather/ppermute | solution.py:55
  133.0 4.8 %fusion.14 = f32[384,1536]{1,0:T(8,128)S(1)} fusion(bf16[384,2048]{1,0:T(8,128)(2,1)S(1)} %constant_dynamic-update-slice_fusion, bf16[2,2048,1536]{2,1,0:T(8,128)(2,1)} %param.16), kind=kOutput, calls=%fused_computation.14 | convolution fusion | flops 2415919104 | bytes 10223616 | tf_op jit(solution)/shard_map/local_experts/dot_general | solution.py:87
  138.3 2.6 %fusion.6 = f32[384,1536]{1,0:T(8,128)S(1)} fusion(bf16[384,2048]{1,0:T(8,128)(2,1)S(1)} %constant_dynamic-update-slice_fusion, bf16[2,2048,1536]{2,1,0:T(8,128)(2,1)S(1)} %bitcast.262), kind=kOutput, calls=%fused_computation.6 | convolution fusion | flops 2415919104 | bytes 10223616 | tf_op jit(solution)/shard_map/local_experts/dot_general | solution.py:87
  140.9 1.7 collective-permute-start.18
  142.9 1.4 fusion.40
  144.4 1.5 fusion.204
  145.9 1.8 collective-permute-start.28
  148.3 6.3 %collective-permute-done.28 = bf16[64,2048]{1,0:T(8,128)(2,1)S(1)} collective-permute-done((bf16[64,2048]{1,0:T(8,128)(2,1)S(1)}, bf16[64,2048]{1,0:T(8,128)(2,1)S(1)}, u32[]{:S(2)}, u32[]{:S(2)}) %collective-permute-start.28) | collective-permute-done | bytes 262176 | tf_op jit(solution)/shard_map/combine_return/ppermute | solution.py:75
  154.6 1.4 collective-permute-done.29
  156.1 1.7 collective-permute-start.20
  158.2 1.8 collective-permute-start.30
  160.3 4.8 %collective-permute-done.20 = bf16[64,2048]{1,0:T(8,128)(2,1)S(1)} collective-permute-done((bf16[64,2048]{1,0:T(8,128)(2,1)S(1)}, bf16[64,2048]{1,0:T(8,128)(2,1)S(1)}, u32[]{:S(2)}, u32[]{:S(2)}) %collective-permute-start.20) | collective-permute-done | bytes 262176 | tf_op jit(solution)/shard_map/dispatch_gather/ppermute | solution.py:55
  165.1 1.5 collective-permute-done.21
  166.7 1.8 fusion
  168.4 1.8 fusion.8
  170.2 1.2 collective-permute-start.22
  173.3 1.0 fusion.69
  174.5 1.2 collective-permute-start.32
  176.7 6.9 %collective-permute-done.32 = bf16[64,2048]{1,0:T(8,128)(2,1)S(1)} collective-permute-done((bf16[64,2048]{1,0:T(8,128)(2,1)S(1)}, bf16[64,2048]{1,0:T(8,128)(2,1)S(1)}, u32[]{:S(2)}, u32[]{:S(2)}) %collective-permute-start.32) | collective-permute-done | bytes 262176 | tf_op jit(solution)/shard_map/combine_return/ppermute | solution.py:75
  183.6 1.3 collective-permute-done.33
  185.5 1.4 collective-permute-start.25
  187.8 1.4 collective-permute-start.35
  189.2 3.1 %collective-permute-done.24 = bf16[64,2048]{1,0:T(8,128)(2,1)S(1)} collective-permute-done((bf16[64,2048]{1,0:T(8,128)(2,1)S(1)}, bf16[64,2048]{1,0:T(8,128)(2,1)S(1)}, u32[]{:S(2)}, u32[]{:S(2)}) %collective-permute-start.24) | collective-permute-done | bytes 262176 | tf_op jit(solution)/shard_map/dispatch_gather/ppermute | solution.py:55
  193.3 1.8 fusion.2
  195.1 1.8 fusion.10
  197.3 1.7 collective-permute-start.27
  200.0 1.1 fusion.57
  201.6 1.7 collective-permute-start.37
  203.3 1.5 collective-permute-done.26
  208.9 1.3 collective-permute-start.39
  211.5 3.0 %collective-permute-done.38 = bf16[64,2048]{1,0:T(8,128)(2,1)S(1)} collective-permute-done((bf16[64,2048]{1,0:T(8,128)(2,1)S(1)}, bf16[64,2048]{1,0:T(8,128)(2,1)S(1)}, u32[]{:S(2)}, u32[]{:S(2)}) %collective-permute-start.38) | collective-permute-done | bytes 262176 | tf_op jit(solution)/shard_map/combine_return/ppermute | solution.py:75
  215.9 1.5 collective-permute-start.41
  217.5 4.3 %collective-permute-done.40 = bf16[64,2048]{1,0:T(8,128)(2,1)S(1)} collective-permute-done((bf16[64,2048]{1,0:T(8,128)(2,1)S(1)}, bf16[64,2048]{1,0:T(8,128)(2,1)S(1)}, u32[]{:S(2)}, u32[]{:S(2)}) %collective-permute-start.40) | collective-permute-done | bytes 262176 | tf_op jit(solution)/shard_map/combine_return/ppermute | solution.py:75
  222.7 1.2 multiply_convert_fusion
  (122 shorter events, 29.9 us)
Async XLA Ops:
  0.6 43.6 %copy-start = (bf16[512,2048]{1,0:T(8,128)(2,1)S(1)}, bf16[512,2048]{1,0:T(8,128)(2,1)}, u32[]{:S(2)}) copy-start(bf16[512,2048]{1,0:T(8,128)(2,1)} %param.14) | copy-start | bytes 6291460
  0.6 18.9 %copy-start.7 = (s32[8]{0:T(128)S(1)}, s32[8]{0:T(128)}, u32[]{:S(2)}) copy-start(s32[8]{0:T(128)} %constant.226.clone) | copy-start | bytes 100
  0.7 30.7 %copy-start.4 = (s32[8]{0:T(128)S(1)}, s32[8]{0:T(128)}, u32[]{:S(2)}) copy-start(s32[8]{0:T(128)} %constant.227.clone) | copy-start | bytes 100
  2.1 13.8 %all-to-all-start.1 = ((f32[8,128,2]{1,2,0:T(2,128)}), f32[8,128,2]{1,2,0:T(2,128)S(1)}, u32[]{:S(2)}, u32[]{:S(2)}) async-start(f32[8,128,2]{1,2,0:T(2,128)} %bitcast.2), calls=%async_computation.1 | async-start | bytes 16384 | tf_op jit(solution)/shard_map/route_weights/all_to_all | solution.py:118
  15.9 28.3 %all-to-all-start = ((bf16[8,128,512]{2,1,0:T(8,128)(2,1)}), bf16[8,128,512]{2,1,0:T(8,128)(2,1)S(1)}, u32[]{:S(2)}, u32[]{:S(2)}) async-start(bf16[8,128,512]{2,1,0:T(8,128)(2,1)} %bitcast.236), calls=%async_computation | async-start | bytes 2097152 | tf_op jit(solution)/shard_map/out_projection/all_to_all | solution.py:123
  46.6 3.3 %copy-start.2 = (f32[8,128,2048]{2,1,0:T(8,128)}, f32[8,128,2048]{2,1,0:T(8,128)S(1)}, u32[]{:S(2)}) copy-start(f32[8,128,2048]{2,1,0:T(8,128)S(1)} %fusion.111) | copy-start | bytes 25165828
  50.0 6.6 %collective-permute-start = (bf16[64,2048]{1,0:T(8,128)(2,1)S(1)}, bf16[64,2048]{1,0:T(8,128)(2,1)S(1)}, u32[]{:S(2)}, u32[]{:S(2)}) collective-permute-start(bf16[64,2048]{1,0:T(8,128)(2,1)S(1)} %get-tuple-element.75), channel_id=1, source_target_pairs={{0,8},{8,16},{16,24},{24,28},{28,20},{20,12},{12,4},{4,0},{1,9},{9... | collective-permute-start | bytes 786440 | tf_op jit(solution)/shard_map/out_projection/ppermute | solution.py:37
  50.0 6.6 %collective-permute-start.1 = (bf16[64,2048]{1,0:T(8,128)(2,1)S(1)}, bf16[64,2048]{1,0:T(8,128)(2,1)S(1)}, u32[]{:S(2)}, u32[]{:S(2)}) collective-permute-start(bf16[64,2048]{1,0:T(8,128)(2,1)S(1)} %get-tuple-element.76), channel_id=1, source_target_pairs={{0,4},{8,0},{16,8},{24,16},{28,24},{20,28},{12,20},{4,12},{1,5},{9... | collective-permute-start | bytes 786440 | tf_op jit(solution)/shard_map/out_projection/ppermute | solution.py:37
  57.9 6.4 %collective-permute-start.2 = (bf16[64,2048]{1,0:T(8,128)(2,1)S(1)}, bf16[64,2048]{1,0:T(8,128)(2,1)S(1)}, u32[]{:S(2)}, u32[]{:S(2)}) collective-permute-start(bf16[64,2048]{1,0:T(8,128)(2,1)S(1)} %get-tuple-element.79), channel_id=1, source_target_pairs={{0,8},{8,16},{16,24},{24,28},{28,20},{20,12},{12,4},{4,0},{1,9},{9... | collective-permute-start | bytes 786440 | tf_op jit(solution)/shard_map/out_projection/ppermute | solution.py:37
  58.5 7.9 %collective-permute-start.3 = (bf16[64,2048]{1,0:T(8,128)(2,1)S(1)}, bf16[64,2048]{1,0:T(8,128)(2,1)S(1)}, u32[]{:S(2)}, u32[]{:S(2)}) collective-permute-start(bf16[64,2048]{1,0:T(8,128)(2,1)S(1)} %get-tuple-element.80), channel_id=1, source_target_pairs={{0,4},{8,0},{16,8},{24,16},{28,24},{20,28},{12,20},{4,12},{1,5},{9... | collective-permute-start | bytes 786440 | tf_op jit(solution)/shard_map/out_projection/ppermute | solution.py:37
  67.8 6.4 %collective-permute-start.4 = (bf16[64,2048]{1,0:T(8,128)(2,1)S(1)}, bf16[64,2048]{1,0:T(8,128)(2,1)S(1)}, u32[]{:S(2)}, u32[]{:S(2)}) collective-permute-start(bf16[64,2048]{1,0:T(8,128)(2,1)S(1)} %get-tuple-element.83), channel_id=1, source_target_pairs={{0,8},{8,16},{16,24},{24,28},{28,20},{20,12},{12,4},{4,0},{1,9},{9... | collective-permute-start | bytes 786440 | tf_op jit(solution)/shard_map/out_projection/ppermute | solution.py:37
  69.6 6.4 %collective-permute-start.5 = (bf16[64,2048]{1,0:T(8,128)(2,1)S(1)}, bf16[64,2048]{1,0:T(8,128)(2,1)S(1)}, u32[]{:S(2)}, u32[]{:S(2)}) collective-permute-start(bf16[64,2048]{1,0:T(8,128)(2,1)S(1)} %get-tuple-element.84), channel_id=1, source_target_pairs={{0,4},{8,0},{16,8},{24,16},{28,24},{20,28},{12,20},{4,12},{1,5},{9... | collective-permute-start | bytes 786440 | tf_op jit(solution)/shard_map/out_projection/ppermute | solution.py:37
  77.3 6.4 %collective-permute-start.6 = (bf16[64,2048]{1,0:T(8,128)(2,1)S(1)}, bf16[64,2048]{1,0:T(8,128)(2,1)S(1)}, u32[]{:S(2)}, u32[]{:S(2)}) collective-permute-start(bf16[64,2048]{1,0:T(8,128)(2,1)S(1)} %get-tuple-element.87), channel_id=1, source_target_pairs={{0,8},{8,16},{16,24},{24,28},{28,20},{20,12},{12,4},{4,0},{1,9},{9... | collective-permute-start | bytes 786440 | tf_op jit(solution)/shard_map/out_projection/ppermute | solution.py:37
  79.1 6.6 %collective-permute-start.7 = (bf16[64,2048]{1,0:T(8,128)(2,1)S(1)}, bf16[64,2048]{1,0:T(8,128)(2,1)S(1)}, u32[]{:S(2)}, u32[]{:S(2)}) collective-permute-start(bf16[64,2048]{1,0:T(8,128)(2,1)S(1)} %get-tuple-element.88), channel_id=1, source_target_pairs={{0,4},{8,0},{16,8},{24,16},{28,24},{20,28},{12,20},{4,12},{1,5},{9... | collective-permute-start | bytes 786440 | tf_op jit(solution)/shard_map/out_projection/ppermute | solution.py:37
  86.9 7.7 %collective-permute-start.8 = (bf16[64,2048]{1,0:T(8,128)(2,1)S(1)}, bf16[64,2048]{1,0:T(8,128)(2,1)S(1)}, u32[]{:S(2)}, u32[]{:S(2)}) collective-permute-start(bf16[64,2048]{1,0:T(8,128)(2,1)S(1)} %get-tuple-element.91), channel_id=1, source_target_pairs={{0,8},{8,16},{16,24},{24,28},{28,20},{20,12},{12,4},{4,0},{1,9},{9... | collective-permute-start | bytes 786440 | tf_op jit(solution)/shard_map/out_projection/ppermute | solution.py:37
  87.5 7.7 %collective-permute-start.9 = (bf16[64,2048]{1,0:T(8,128)(2,1)S(1)}, bf16[64,2048]{1,0:T(8,128)(2,1)S(1)}, u32[]{:S(2)}, u32[]{:S(2)}) collective-permute-start(bf16[64,2048]{1,0:T(8,128)(2,1)S(1)} %get-tuple-element.92), channel_id=1, source_target_pairs={{0,4},{8,0},{16,8},{24,16},{28,24},{20,28},{12,20},{4,12},{1,5},{9... | collective-permute-start | bytes 786440 | tf_op jit(solution)/shard_map/out_projection/ppermute | solution.py:37
  96.5 8.7 %collective-permute-start.10 = (bf16[64,2048]{1,0:T(8,128)(2,1)S(1)}, bf16[64,2048]{1,0:T(8,128)(2,1)S(1)}, u32[]{:S(2)}, u32[]{:S(2)}) collective-permute-start(bf16[64,2048]{1,0:T(8,128)(2,1)S(1)} %get-tuple-element.95), channel_id=1, source_target_pairs={{0,8},{8,16},{16,24},{24,28},{28,20},{20,12},{12,4},{4,0},{1,9},{9... | collective-permute-start | bytes 786440 | tf_op jit(solution)/shard_map/out_projection/ppermute | solution.py:37
  97.1 8.8 %collective-permute-start.11 = (bf16[64,2048]{1,0:T(8,128)(2,1)S(1)}, bf16[64,2048]{1,0:T(8,128)(2,1)S(1)}, u32[]{:S(2)}, u32[]{:S(2)}) collective-permute-start(bf16[64,2048]{1,0:T(8,128)(2,1)S(1)} %get-tuple-element.96), channel_id=1, source_target_pairs={{0,4},{8,0},{16,8},{24,16},{28,24},{20,28},{12,20},{4,12},{1,5},{9... | collective-permute-start | bytes 786440 | tf_op jit(solution)/shard_map/out_projection/ppermute | solution.py:37
  104.4 14.1 %copy-start.3 = (bf16[128,2048]{1,0:T(8,128)(2,1)S(1)}, bf16[128,2048]{1,0:T(8,128)(2,1)}, u32[]{:S(2)}) copy-start(bf16[128,2048]{1,0:T(8,128)(2,1)} %param.12) | copy-start | bytes 1572868
  107.2 9.0 %collective-permute-start.12 = (bf16[64,2048]{1,0:T(8,128)(2,1)S(1)}, bf16[64,2048]{1,0:T(8,128)(2,1)S(1)}, u32[]{:S(2)}, u32[]{:S(2)}) collective-permute-start(bf16[64,2048]{1,0:T(8,128)(2,1)S(1)} %get-tuple-element.99), channel_id=1, source_target_pairs={{0,8},{8,16},{16,24},{24,28},{28,20},{20,12},{12,4},{4,0},{1,9},{9... | collective-permute-start | bytes 786440 | tf_op jit(solution)/shard_map/out_projection/ppermute | solution.py:37
  108.8 8.3 %collective-permute-start.13 = (bf16[64,2048]{1,0:T(8,128)(2,1)S(1)}, bf16[64,2048]{1,0:T(8,128)(2,1)S(1)}, u32[]{:S(2)}, u32[]{:S(2)}) collective-permute-start(bf16[64,2048]{1,0:T(8,128)(2,1)S(1)} %get-tuple-element.100), channel_id=1, source_target_pairs={{0,4},{8,0},{16,8},{24,16},{28,24},{20,28},{12,20},{4,12},{1,5},{9... | collective-permute-start | bytes 786440 | tf_op jit(solution)/shard_map/out_projection/ppermute | solution.py:37
  109.5 9.2 %copy-start.5 = (f32[2048]{0:T(1024)S(1)}, f32[2048]{0:T(1024)}, u32[]{:S(2)}) copy-start(f32[2048]{0:T(1024)} %param.15) | copy-start | bytes 24580
  118.4 19.4 %slice-start = ((s8[12582912]{0:T(1024)(128)(4,1)}), s8[4194304]{0:T(1024)(128)(4,1)S(1)}, s32[]{:S(2)}) async-start(s8[12582912]{0:T(1024)(128)(4,1)} %bitcast.261), calls=%async_computation.2 | async-start | bytes 8388608
  118.9 6.4 %collective-permute-start.14 = (bf16[64,2048]{1,0:T(8,128)(2,1)S(1)}, bf16[64,2048]{1,0:T(8,128)(2,1)S(1)}, u32[]{:S(2)}, u32[]{:S(2)}) collective-permute-start(bf16[64,2048]{1,0:T(8,128)(2,1)S(1)} %get-tuple-element.185), channel_id=1, source_target_pairs={{0,8},{8,16},{16,24},{24,28},{28,20},{20,12},{12,4},{4,0},{1,9},{9... | collective-permute-start | bytes 786440 | tf_op jit(solution)/shard_map/dispatch_gather/ppermute | solution.py:55
  119.6 6.4 %collective-permute-start.15 = (bf16[64,2048]{1,0:T(8,128)(2,1)S(1)}, bf16[64,2048]{1,0:T(8,128)(2,1)S(1)}, u32[]{:S(2)}, u32[]{:S(2)}) collective-permute-start(bf16[64,2048]{1,0:T(8,128)(2,1)S(1)} %get-tuple-element.184), channel_id=1, source_target_pairs={{0,4},{8,0},{16,8},{24,16},{28,24},{20,28},{12,20},{4,12},{1,5},{9... | collective-permute-start | bytes 786440 | tf_op jit(solution)/shard_map/dispatch_gather/ppermute | solution.py:55
  126.0 6.4 %collective-permute-start.16 = (bf16[64,2048]{1,0:T(8,128)(2,1)S(1)}, bf16[64,2048]{1,0:T(8,128)(2,1)S(1)}, u32[]{:S(2)}, u32[]{:S(2)}) collective-permute-start(bf16[64,2048]{1,0:T(8,128)(2,1)S(1)} %collective-permute-done.14), channel_id=1, source_target_pairs={{0,8},{8,16},{16,24},{24,28},{28,20},{20,12},{12,4},{4,0},{1,9},{9... | collective-permute-start | bytes 786440 | tf_op jit(solution)/shard_map/dispatch_gather/ppermute | solution.py:55
  126.3 6.4 %collective-permute-start.17 = (bf16[64,2048]{1,0:T(8,128)(2,1)S(1)}, bf16[64,2048]{1,0:T(8,128)(2,1)S(1)}, u32[]{:S(2)}, u32[]{:S(2)}) collective-permute-start(bf16[64,2048]{1,0:T(8,128)(2,1)S(1)} %collective-permute-done.15), channel_id=1, source_target_pairs={{0,4},{8,0},{16,8},{24,16},{28,24},{20,28},{12,20},{4,12},{1,5},{9... | collective-permute-start | bytes 786440 | tf_op jit(solution)/shard_map/dispatch_gather/ppermute | solution.py:55
  132.9 4.9 %slice-start.1 = ((s8[12582912]{0:T(1024)(128)(4,1)}), s8[4194304]{0:T(1024)(128)(4,1)S(1)}, s32[]{:S(2)}) async-start(s8[12582912]{0:T(1024)(128)(4,1)} %bitcast.261), calls=%async_computation.3 | async-start | bytes 8388608
  133.0 5.3 %slice-start.2 = ((s8[12582912]{0:T(1024)(128)(4,1)}), s8[4194304]{0:T(1024)(128)(4,1)S(1)}, s32[]{:S(2)}) async-start(s8[12582912]{0:T(1024)(128)(4,1)} %bitcast.261), calls=%async_computation.4 | async-start | bytes 8388608
  133.0 10.0 %slice-start.3 = ((s8[6291456]{0:T(1024)(128)(4,1)}), s8[4194304]{0:T(1024)(128)(4,1)S(1)}, s32[]{:S(2)}) async-start(s8[6291456]{0:T(1024)(128)(4,1)} %bitcast.263), calls=%async_computation.5 | async-start | bytes 8388608
  138.3 4.7 %slice-start.4 = ((s8[6291456]{0:T(1024)(128)(4,1)}), s8[2097152]{0:T(1024)(128)(4,1)S(1)}, s32[]{:S(2)}) async-start(s8[6291456]{0:T(1024)(128)(4,1)} %bitcast.263), calls=%async_computation.6 | async-start | bytes 4194304
  140.9 15.2 %collective-permute-start.18 = (bf16[64,2048]{1,0:T(8,128)(2,1)S(1)}, bf16[64,2048]{1,0:T(8,128)(2,1)S(1)}, u32[]{:S(2)}, u32[]{:S(2)}) collective-permute-start(bf16[64,2048]{1,0:T(8,128)(2,1)S(1)} %collective-permute-done.16), channel_id=1, source_target_pairs={{0,8},{8,16},{16,24},{24,28},{28,20},{20,12},{12,4},{4,0},{1,9},{9... | collective-permute-start | bytes 786440 | tf_op jit(solution)/shard_map/dispatch_gather/ppermute | solution.py:55
  142.5 13.5 %collective-permute-start.19 = (bf16[64,2048]{1,0:T(8,128)(2,1)S(1)}, bf16[64,2048]{1,0:T(8,128)(2,1)S(1)}, u32[]{:S(2)}, u32[]{:S(2)}) collective-permute-start(bf16[64,2048]{1,0:T(8,128)(2,1)S(1)} %collective-permute-done.17), channel_id=1, source_target_pairs={{0,4},{8,0},{16,8},{24,16},{28,24},{20,28},{12,20},{4,12},{1,5},{9... | collective-permute-start | bytes 786440 | tf_op jit(solution)/shard_map/dispatch_gather/ppermute | solution.py:55
  145.9 8.7 %collective-permute-start.28 = (bf16[64,2048]{1,0:T(8,128)(2,1)S(1)}, bf16[64,2048]{1,0:T(8,128)(2,1)S(1)}, u32[]{:S(2)}, u32[]{:S(2)}) collective-permute-start(bf16[64,2048]{1,0:T(8,128)(2,1)S(1)} %get-tuple-element.118), channel_id=1, source_target_pairs={{0,8},{8,16},{16,24},{24,28},{28,20},{20,12},{12,4},{4,0},{1,9},{9... | collective-permute-start | bytes 786440 | tf_op jit(solution)/shard_map/combine_return/ppermute | solution.py:75
  147.8 8.3 %collective-permute-start.29 = (bf16[64,2048]{1,0:T(8,128)(2,1)S(1)}, bf16[64,2048]{1,0:T(8,128)(2,1)S(1)}, u32[]{:S(2)}, u32[]{:S(2)}) collective-permute-start(bf16[64,2048]{1,0:T(8,128)(2,1)S(1)} %get-tuple-element.119), channel_id=1, source_target_pairs={{0,4},{8,0},{16,8},{24,16},{28,24},{20,28},{12,20},{4,12},{1,5},{9... | collective-permute-start | bytes 786440 | tf_op jit(solution)/shard_map/combine_return/ppermute | solution.py:75
  156.1 9.1 %collective-permute-start.20 = (bf16[64,2048]{1,0:T(8,128)(2,1)S(1)}, bf16[64,2048]{1,0:T(8,128)(2,1)S(1)}, u32[]{:S(2)}, u32[]{:S(2)}) collective-permute-start(bf16[64,2048]{1,0:T(8,128)(2,1)S(1)} %collective-permute-done.18), channel_id=1, source_target_pairs={{0,8},{8,16},{16,24},{24,28},{28,20},{20,12},{12,4},{4,0},{1,9},{9... | collective-permute-start | bytes 786440 | tf_op jit(solution)/shard_map/dispatch_gather/ppermute | solution.py:55
  157.7 8.9 %collective-permute-start.21 = (bf16[64,2048]{1,0:T(8,128)(2,1)S(1)}, bf16[64,2048]{1,0:T(8,128)(2,1)S(1)}, u32[]{:S(2)}, u32[]{:S(2)}) collective-permute-start(bf16[64,2048]{1,0:T(8,128)(2,1)S(1)} %collective-permute-done.19), channel_id=1, source_target_pairs={{0,4},{8,0},{16,8},{24,16},{28,24},{20,28},{12,20},{4,12},{1,5},{9... | collective-permute-start | bytes 786440 | tf_op jit(solution)/shard_map/dispatch_gather/ppermute | solution.py:55
  158.2 14.1 %collective-permute-start.30 = (bf16[64,2048]{1,0:T(8,128)(2,1)S(1)}, bf16[64,2048]{1,0:T(8,128)(2,1)S(1)}, u32[]{:S(2)}, u32[]{:S(2)}) collective-permute-start(bf16[64,2048]{1,0:T(8,128)(2,1)S(1)} %get-tuple-element.122), channel_id=1, source_target_pairs={{0,8},{8,16},{16,24},{24,28},{28,20},{20,12},{12,4},{4,0},{1,9},{9... | collective-permute-start | bytes 786440 | tf_op jit(solution)/shard_map/combine_return/ppermute | solution.py:75
  160.0 12.3 %collective-permute-start.31 = (bf16[64,2048]{1,0:T(8,128)(2,1)S(1)}, bf16[64,2048]{1,0:T(8,128)(2,1)S(1)}, u32[]{:S(2)}, u32[]{:S(2)}) collective-permute-start(bf16[64,2048]{1,0:T(8,128)(2,1)S(1)} %get-tuple-element.123), channel_id=1, source_target_pairs={{0,4},{8,0},{16,8},{24,16},{28,24},{20,28},{12,20},{4,12},{1,5},{9... | collective-permute-start | bytes 786440 | tf_op jit(solution)/shard_map/combine_return/ppermute | solution.py:75
  170.2 14.7 %collective-permute-start.22 = (bf16[64,2048]{1,0:T(8,128)(2,1)S(1)}, bf16[64,2048]{1,0:T(8,128)(2,1)S(1)}, u32[]{:S(2)}, u32[]{:S(2)}) collective-permute-start(bf16[64,2048]{1,0:T(8,128)(2,1)S(1)} %collective-permute-done.20), channel_id=1, source_target_pairs={{0,8},{8,16},{16,24},{24,28},{28,20},{20,12},{12,4},{4,0},{1,9},{9... | collective-permute-start | bytes 786440 | tf_op jit(solution)/shard_map/dispatch_gather/ppermute | solution.py:55
  171.5 13.5 %collective-permute-start.23 = (bf16[64,2048]{1,0:T(8,128)(2,1)S(1)}, bf16[64,2048]{1,0:T(8,128)(2,1)S(1)}, u32[]{:S(2)}, u32[]{:S(2)}) collective-permute-start(bf16[64,2048]{1,0:T(8,128)(2,1)S(1)} %collective-permute-done.21), channel_id=1, source_target_pairs={{0,4},{8,0},{16,8},{24,16},{28,24},{20,28},{12,20},{4,12},{1,5},{9... | collective-permute-start | bytes 786440 | tf_op jit(solution)/shard_map/dispatch_gather/ppermute | solution.py:55
  174.5 9.1 %collective-permute-start.32 = (bf16[64,2048]{1,0:T(8,128)(2,1)S(1)}, bf16[64,2048]{1,0:T(8,128)(2,1)S(1)}, u32[]{:S(2)}, u32[]{:S(2)}) collective-permute-start(bf16[64,2048]{1,0:T(8,128)(2,1)S(1)} %get-tuple-element.126), channel_id=1, source_target_pairs={{0,8},{8,16},{16,24},{24,28},{28,20},{20,12},{12,4},{4,0},{1,9},{9... | collective-permute-start | bytes 786440 | tf_op jit(solution)/shard_map/combine_return/ppermute | solution.py:75
  175.8 9.2 %collective-permute-start.33 = (bf16[64,2048]{1,0:T(8,128)(2,1)S(1)}, bf16[64,2048]{1,0:T(8,128)(2,1)S(1)}, u32[]{:S(2)}, u32[]{:S(2)}) collective-permute-start(bf16[64,2048]{1,0:T(8,128)(2,1)S(1)} %get-tuple-element.127), channel_id=1, source_target_pairs={{0,4},{8,0},{16,8},{24,16},{28,24},{20,28},{12,20},{4,12},{1,5},{9... | collective-permute-start | bytes 786440 | tf_op jit(solution)/shard_map/combine_return/ppermute | solution.py:75
  184.9 7.4 %collective-permute-start.24 = (bf16[64,2048]{1,0:T(8,128)(2,1)S(1)}, bf16[64,2048]{1,0:T(8,128)(2,1)S(1)}, u32[]{:S(2)}, u32[]{:S(2)}) collective-permute-start(bf16[64,2048]{1,0:T(8,128)(2,1)S(1)} %collective-permute-done.22), channel_id=1, source_target_pairs={{0,8},{8,16},{16,24},{24,28},{28,20},{20,12},{12,4},{4,0},{1,9},{9... | collective-permute-start | bytes 786440 | tf_op jit(solution)/shard_map/dispatch_gather/ppermute | solution.py:55
  185.5 7.7 %collective-permute-start.25 = (bf16[64,2048]{1,0:T(8,128)(2,1)S(1)}, bf16[64,2048]{1,0:T(8,128)(2,1)S(1)}, u32[]{:S(2)}, u32[]{:S(2)}) collective-permute-start(bf16[64,2048]{1,0:T(8,128)(2,1)S(1)} %collective-permute-done.23), channel_id=1, source_target_pairs={{0,4},{8,0},{16,8},{24,16},{28,24},{20,28},{12,20},{4,12},{1,5},{9... | collective-permute-start | bytes 786440 | tf_op jit(solution)/shard_map/dispatch_gather/ppermute | solution.py:55
  187.1 11.8 %collective-permute-start.34 = (bf16[64,2048]{1,0:T(8,128)(2,1)S(1)}, bf16[64,2048]{1,0:T(8,128)(2,1)S(1)}, u32[]{:S(2)}, u32[]{:S(2)}) collective-permute-start(bf16[64,2048]{1,0:T(8,128)(2,1)S(1)} %get-tuple-element.130), channel_id=1, source_target_pairs={{0,8},{8,16},{16,24},{24,28},{28,20},{20,12},{12,4},{4,0},{1,9},{9... | collective-permute-start | bytes 786440 | tf_op jit(solution)/shard_map/combine_return/ppermute | solution.py:75
  187.8 11.1 %collective-permute-start.35 = (bf16[64,2048]{1,0:T(8,128)(2,1)S(1)}, bf16[64,2048]{1,0:T(8,128)(2,1)S(1)}, u32[]{:S(2)}, u32[]{:S(2)}) collective-permute-start(bf16[64,2048]{1,0:T(8,128)(2,1)S(1)} %get-tuple-element.131), channel_id=1, source_target_pairs={{0,4},{8,0},{16,8},{24,16},{28,24},{20,28},{12,20},{4,12},{1,5},{9... | collective-permute-start | bytes 786440 | tf_op jit(solution)/shard_map/combine_return/ppermute | solution.py:75
  196.8 7.9 %collective-permute-start.26 = (bf16[64,2048]{1,0:T(8,128)(2,1)S(1)}, bf16[64,2048]{1,0:T(8,128)(2,1)S(1)}, u32[]{:S(2)}, u32[]{:S(2)}) collective-permute-start(bf16[64,2048]{1,0:T(8,128)(2,1)S(1)} %collective-permute-done.24), channel_id=1, source_target_pairs={{0,8},{8,16},{16,24},{24,28},{28,20},{20,12},{12,4},{4,0},{1,9},{9... | collective-permute-start | bytes 786440 | tf_op jit(solution)/shard_map/dispatch_gather/ppermute | solution.py:55
  197.3 7.5 %collective-permute-start.27 = (bf16[64,2048]{1,0:T(8,128)(2,1)S(1)}, bf16[64,2048]{1,0:T(8,128)(2,1)S(1)}, u32[]{:S(2)}, u32[]{:S(2)}) collective-permute-start(bf16[64,2048]{1,0:T(8,128)(2,1)S(1)} %collective-permute-done.25), channel_id=1, source_target_pairs={{0,4},{8,0},{16,8},{24,16},{28,24},{20,28},{12,20},{4,12},{1,5},{9... | collective-permute-start | bytes 786440 | tf_op jit(solution)/shard_map/dispatch_gather/ppermute | solution.py:55
  201.2 6.4 %collective-permute-start.36 = (bf16[64,2048]{1,0:T(8,128)(2,1)S(1)}, bf16[64,2048]{1,0:T(8,128)(2,1)S(1)}, u32[]{:S(2)}, u32[]{:S(2)}) collective-permute-start(bf16[64,2048]{1,0:T(8,128)(2,1)S(1)} %get-tuple-element.134), channel_id=1, source_target_pairs={{0,8},{8,16},{16,24},{24,28},{28,20},{20,12},{12,4},{4,0},{1,9},{9... | collective-permute-start | bytes 786440 | tf_op jit(solution)/shard_map/combine_return/ppermute | solution.py:75
  201.6 6.4 %collective-permute-start.37 = (bf16[64,2048]{1,0:T(8,128)(2,1)S(1)}, bf16[64,2048]{1,0:T(8,128)(2,1)S(1)}, u32[]{:S(2)}, u32[]{:S(2)}) collective-permute-start(bf16[64,2048]{1,0:T(8,128)(2,1)S(1)} %get-tuple-element.135), channel_id=1, source_target_pairs={{0,4},{8,0},{16,8},{24,16},{28,24},{20,28},{12,20},{4,12},{1,5},{9... | collective-permute-start | bytes 786440 | tf_op jit(solution)/shard_map/combine_return/ppermute | solution.py:75
  208.1 6.4 %collective-permute-start.38 = (bf16[64,2048]{1,0:T(8,128)(2,1)S(1)}, bf16[64,2048]{1,0:T(8,128)(2,1)S(1)}, u32[]{:S(2)}, u32[]{:S(2)}) collective-permute-start(bf16[64,2048]{1,0:T(8,128)(2,1)S(1)} %get-tuple-element.138), channel_id=1, source_target_pairs={{0,8},{8,16},{16,24},{24,28},{28,20},{20,12},{12,4},{4,0},{1,9},{9... | collective-permute-start | bytes 786440 | tf_op jit(solution)/shard_map/combine_return/ppermute | solution.py:75
  208.9 6.4 %collective-permute-start.39 = (bf16[64,2048]{1,0:T(8,128)(2,1)S(1)}, bf16[64,2048]{1,0:T(8,128)(2,1)S(1)}, u32[]{:S(2)}, u32[]{:S(2)}) collective-permute-start(bf16[64,2048]{1,0:T(8,128)(2,1)S(1)} %get-tuple-element.139), channel_id=1, source_target_pairs={{0,4},{8,0},{16,8},{24,16},{28,24},{20,28},{12,20},{4,12},{1,5},{9... | collective-permute-start | bytes 786440 | tf_op jit(solution)/shard_map/combine_return/ppermute | solution.py:75
  215.4 7.3 %copy-start.6 = (f32[2048]{0:T(1024)S(1)}, f32[2048]{0:T(1024)}, u32[]{:S(2)}) copy-start(f32[2048]{0:T(1024)} %param.20) | copy-start | bytes 24580
  215.4 6.4 %collective-permute-start.40 = (bf16[64,2048]{1,0:T(8,128)(2,1)S(1)}, bf16[64,2048]{1,0:T(8,128)(2,1)S(1)}, u32[]{:S(2)}, u32[]{:S(2)}) collective-permute-start(bf16[64,2048]{1,0:T(8,128)(2,1)S(1)} %get-tuple-element.142), channel_id=1, source_target_pairs={{0,8},{8,16},{16,24},{24,28},{28,20},{20,12},{12,4},{4,0},{1,9},{9... | collective-permute-start | bytes 786440 | tf_op jit(solution)/shard_map/combine_return/ppermute | solution.py:75
  215.9 6.4 %collective-permute-start.41 = (bf16[64,2048]{1,0:T(8,128)(2,1)S(1)}, bf16[64,2048]{1,0:T(8,128)(2,1)S(1)}, u32[]{:S(2)}, u32[]{:S(2)}) collective-permute-start(bf16[64,2048]{1,0:T(8,128)(2,1)S(1)} %get-tuple-element.143), channel_id=1, source_target_pairs={{0,4},{8,0},{16,8},{24,16},{28,24},{20,28},{12,20},{4,12},{1,5},{9... | collective-permute-start | bytes 786440 | tf_op jit(solution)/shard_map/combine_return/ppermute | solution.py:75
  222.3 1.6 copy-start.1

commit v20 on v19

--- a/solution.py
+++ b/solution.py
@@ -154,7 +154,7 @@
             for step in steps:
                 rows_in += list(arrived[step])
                 weights_in += list(step_weights(step))
-            if c == 0:
+            if c == 1:
                 rows_in.append(normed)
                 weights_in.append(lax.dynamic_index_in_dim(weight_blocks, me, 0, keepdims=False))
             mixed = expert_mix(
@@ -163,7 +163,7 @@
             for i, step in enumerate(steps):
                 pieces[step] = (mixed[(2 * i) * half : (2 * i + 1) * half],
                                 mixed[(2 * i + 1) * half : (2 * i + 2) * half])
-            if c == 0:
+            if c == 1:
                 own_part = mixed[2 * len(steps) * half :]
 
     with jax.named_scope("combine_return"):

time: 225 us -> 229 us (1.018)
  matrix products: 27.3 us -> 30.8 us
    dot_general x8, matrix products: 16.6 us -> 20.2 us  [expert_mix(): projected_up = jnp.dot(rows, gate_up[e], preferred_element_type=jnp.float32)]
  transfers between devices with their start and end apart: 44 -> 44, of which waited for: 35 -> 34; matrix products, arithmetic and copies ran while one was open for 10% -> 11% of each run, Pallas kernels for 0% -> 0%
where the time goes in v20:
time: 229 us; the launch traced here: 228 us
  waiting for transfers between devices  79.9 us (35%)
  starting transfers between devices  54.7 us (24%)
  between operations  40.8 us (18%)
  matrix products  30.8 us (13%)
  other arithmetic  13.6 us (6%)
  local copies, waits for them, and re-layouts  7.85 us (3%)
    ppermute x7, waiting for transfers between devices, ring_reduce_scatter_steps(): lax.ppermute(send_fwd, 'ep', forward)  22.5 us
    dot_general x8, matrix products, expert_mix(): projected_up = jnp.dot(rows, gate_up[e], preferred_element_type=jnp.float32)  20.2 us
    ppermute x7, waiting for transfers between devices, ring_all_gather(): lax.ppermute(got_fwd, 'ep', forward)  16.6 us
    ppermute x7, waiting for transfers between devices, ring_reduce_scatter(): lax.ppermute(send_fwd, 'ep', forward)  11.9 us
    all_to_all x1, waiting for transfers between devices, body(): lax.all_to_all(columns, 'ep', split_axis=0, concat_axis=0, tiled=True)  8.41 us
    dot_general x8, matrix products, expert_mix(): jnp.dot(activated, down[e], preferred_element_type=jnp.float32)  8.27 us
    ppermute x7, starting transfers between devices, ring_reduce_scatter_steps(): lax.ppermute(send_bwd, 'ep', backward)  8.15 us
    ppermute x7, waiting for transfers between devices, ring_reduce_scatter(): lax.ppermute(send_bwd, 'ep', backward)  7.84 us
  transfers between devices with their start and end apart: 44, of which 34 were waited for; matrix products, arithmetic and copies ran while one was open for 11% of the time, Pallas kernels for 0%

profile of v20, /device:TPU:0, one launch (start us, length us, event | category | flops | bytes accessed | tf_op | source)
XLA Modules:
  0.0 227.7 jit_solution(6504214417173777643)
XLA Ops:
  0.7 1.5 select_reduce_fusion
  2.1 7.3 %all-to-all-start.1 = ((f32[8,128,2]{1,2,0:T(2,128)}), f32[8,128,2]{1,2,0:T(2,128)S(1)}, u32[]{:S(2)}, u32[]{:S(2)}) async-start(f32[8,128,2]{1,2,0:T(2,128)} %bitcast.2), calls=%async_computation.1 | async-start | bytes 16384 | tf_op jit(solution)/shard_map/route_weights/all_to_all | solution.py:118
  9.4 2.3 %copy.25 = bf16[16,8,8,512]{3,2,0,1:T(8,128)(2,1)} copy(bf16[16,8,8,512]{3,2,1,0:T(8,128)(2,1)} %bitcast.238) | data formatting | bytes 2097152 | tf_op jit(solution)/shard_map/out_projection/reshape | solution.py:122
  11.7 4.2 %all-to-all-done.1 = f32[8,128,2]{1,2,0:T(2,128)S(1)} async-done(((f32[8,128,2]{1,2,0:T(2,128)}), f32[8,128,2]{1,2,0:T(2,128)S(1)}, u32[]{:S(2)}, u32[]{:S(2)}) %all-to-all-start.1) | async-done | bytes 8224 | tf_op jit(solution)/shard_map/route_weights/all_to_all | solution.py:118
  15.9 3.6 %all-to-all-start = ((bf16[8,128,512]{2,1,0:T(8,128)(2,1)}), bf16[8,128,512]{2,1,0:T(8,128)(2,1)S(1)}, u32[]{:S(2)}, u32[]{:S(2)}) async-start(bf16[8,128,512]{2,1,0:T(8,128)(2,1)} %bitcast.236), calls=%async_computation | async-start | bytes 2097152 | tf_op jit(solution)/shard_map/out_projection/all_to_all | solution.py:123
  35.8 8.4 %all-to-all-done = bf16[8,128,512]{2,1,0:T(8,128)(2,1)S(1)} async-done(((bf16[8,128,512]{2,1,0:T(8,128)(2,1)}), bf16[8,128,512]{2,1,0:T(8,128)(2,1)S(1)}, u32[]{:S(2)}, u32[]{:S(2)}) %all-to-all-start) | async-done | bytes 1048608 | tf_op jit(solution)/shard_map/out_projection/all_to_all | solution.py:123
  44.2 2.4 %fusion.111 = f32[8,128,2048]{2,1,0:T(8,128)S(1)} fusion(bf16[8,128,512]{2,1,0:T(8,128)(2,1)S(1)} %all-to-all-done, bf16[512,2048]{1,0:T(8,128)(2,1)S(1)} %copy-done), kind=kOutput, calls=%fused_computation.64 | convolution fusion | flops 2147483648 | bytes 11534336 | tf_op jit(solution)/shard_map/out_projection/dot_general | solution.py:125
  46.6 3.3 %copy-done.2 = f32[8,128,2048]{2,1,0:T(8,128)} copy-done((f32[8,128,2048]{2,1,0:T(8,128)}, f32[8,128,2048]{2,1,0:T(8,128)S(1)}, u32[]{:S(2)}) %copy-start.2) | copy-done | bytes 8388632
  50.0 2.0 collective-permute-start.1
  56.6 1.3 fusion.159
  58.5 1.5 collective-permute-start.3
  64.4 2.1 collective-permute-done.3
  66.5 1.3 fusion.157
  67.8 1.8 collective-permute-start.4
  74.2 1.8 collective-permute-done.5
  76.0 1.3 fusion.155
  77.3 1.8 collective-permute-start.6
  83.7 1.9 collective-permute-done.7
  85.6 1.3 fusion.153
  87.5 1.5 collective-permute-start.9
  92.7 1.9 collective-permute-done.8
  95.2 1.3 fusion.151
  97.1 1.5 collective-permute-start.11
  106.0 1.3 fusion.149
  107.3 1.5 collective-permute-start.12
  109.6 6.6 %collective-permute-done.12 = bf16[64,2048]{1,0:T(8,128)(2,1)S(1)} collective-permute-done((bf16[64,2048]{1,0:T(8,128)(2,1)S(1)}, bf16[64,2048]{1,0:T(8,128)(2,1)S(1)}, u32[]{:S(2)}, u32[]{:S(2)}) %collective-permute-start.12) | collective-permute-done | bytes 262176 | tf_op jit(solution)/shard_map/out_projection/ppermute | solution.py:37
  117.0 1.3 fusion.172
  119.6 1.3 collective-permute-start.15
  120.9 4.3 %collective-permute-done.14 = bf16[64,2048]{1,0:T(8,128)(2,1)S(1)} collective-permute-done((bf16[64,2048]{1,0:T(8,128)(2,1)S(1)}, bf16[64,2048]{1,0:T(8,128)(2,1)S(1)}, u32[]{:S(2)}, u32[]{:S(2)}) %collective-permute-start.14) | collective-permute-done | bytes 262176 | tf_op jit(solution)/shard_map/dispatch_gather/ppermute | solution.py:55
  126.3 1.7 collective-permute-start.17
  128.0 4.3 %collective-permute-done.16 = bf16[64,2048]{1,0:T(8,128)(2,1)S(1)} collective-permute-done((bf16[64,2048]{1,0:T(8,128)(2,1)S(1)}, bf16[64,2048]{1,0:T(8,128)(2,1)S(1)}, u32[]{:S(2)}, u32[]{:S(2)}) %collective-permute-start.16) | collective-permute-done | bytes 262176 | tf_op jit(solution)/shard_map/dispatch_gather/ppermute | solution.py:55
  132.7 4.7 %fusion = f32[256,1536]{1,0:T(8,128)S(1)} fusion(bf16[256,2048]{1,0:T(8,128)(2,1)S(1)} %constant_dynamic-update-slice_fusion.11, bf16[2,2048,1536]{2,1,0:T(8,128)(2,1)} %param.16), kind=kOutput, calls=%fused_computation | convolution fusion | flops 1610612736 | bytes 8912896 | tf_op jit(solution)/shard_map/local_experts/dot_general | solution.py:87
  137.5 4.7 %fusion.8 = f32[256,1536]{1,0:T(8,128)S(1)} fusion(bf16[256,2048]{1,0:T(8,128)(2,1)S(1)} %constant_dynamic-update-slice_fusion.11, bf16[2,2048,1536]{2,1,0:T(8,128)(2,1)} %param.16), kind=kOutput, calls=%fused_computation.8 | convolution fusion | flops 1610612736 | bytes 8912896 | tf_op jit(solution)/shard_map/local_experts/dot_general | solution.py:87
  142.2 1.6 collective-permute-start.18
  145.3 1.0 fusion.204
  146.4 1.6 collective-permute-start.28
  148.6 6.4 %collective-permute-done.28 = bf16[64,2048]{1,0:T(8,128)(2,1)S(1)} collective-permute-done((bf16[64,2048]{1,0:T(8,128)(2,1)S(1)}, bf16[64,2048]{1,0:T(8,128)(2,1)S(1)}, u32[]{:S(2)}, u32[]{:S(2)}) %collective-permute-start.28) | collective-permute-done | bytes 262176 | tf_op jit(solution)/shard_map/combine_return/ppermute | solution.py:75
  155.0 1.4 collective-permute-done.29
  156.5 1.4 collective-permute-start.20
  158.7 1.5 collective-permute-start.30
  160.8 3.5 %collective-permute-done.20 = bf16[64,2048]{1,0:T(8,128)(2,1)S(1)} collective-permute-done((bf16[64,2048]{1,0:T(8,128)(2,1)S(1)}, bf16[64,2048]{1,0:T(8,128)(2,1)S(1)}, u32[]{:S(2)}, u32[]{:S(2)}) %collective-permute-start.20) | collective-permute-done | bytes 262176 | tf_op jit(solution)/shard_map/dispatch_gather/ppermute | solution.py:55
  164.2 2.1 collective-permute-done.21
  166.6 2.6 %fusion.14 = f32[384,1536]{1,0:T(8,128)S(1)} fusion(bf16[384,2048]{1,0:T(8,128)(2,1)S(1)} %constant_dynamic-update-slice_fusion, bf16[2,2048,1536]{2,1,0:T(8,128)(2,1)S(1)} %bitcast.262), kind=kOutput, calls=%fused_computation.14 | convolution fusion | flops 2415919104 | bytes 10223616 | tf_op jit(solution)/shard_map/local_experts/dot_general | solution.py:87
  169.2 2.6 %fusion.6 = f32[384,1536]{1,0:T(8,128)S(1)} fusion(bf16[384,2048]{1,0:T(8,128)(2,1)S(1)} %constant_dynamic-update-slice_fusion, bf16[2,2048,1536]{2,1,0:T(8,128)(2,1)S(1)} %bitcast.262), kind=kOutput, calls=%fused_computation.6 | convolution fusion | flops 2415919104 | bytes 10223616 | tf_op jit(solution)/shard_map/local_experts/dot_general | solution.py:87
  171.8 1.8 collective-permute-start.22
  173.9 1.4 fusion.40
  175.3 1.5 multiply_add_fusion
  176.9 1.8 collective-permute-start.32
  179.1 7.1 %collective-permute-done.32 = bf16[64,2048]{1,0:T(8,128)(2,1)S(1)} collective-permute-done((bf16[64,2048]{1,0:T(8,128)(2,1)S(1)}, bf16[64,2048]{1,0:T(8,128)(2,1)S(1)}, u32[]{:S(2)}, u32[]{:S(2)}) %collective-permute-start.32) | collective-permute-done | bytes 262176 | tf_op jit(solution)/shard_map/combine_return/ppermute | solution.py:75
  186.2 1.8 collective-permute-done.33
  188.1 1.9 collective-permute-start.25
  190.4 1.9 collective-permute-start.35
  192.2 4.6 %collective-permute-done.24 = bf16[64,2048]{1,0:T(8,128)(2,1)S(1)} collective-permute-done((bf16[64,2048]{1,0:T(8,128)(2,1)S(1)}, bf16[64,2048]{1,0:T(8,128)(2,1)S(1)}, u32[]{:S(2)}, u32[]{:S(2)}) %collective-permute-start.24) | collective-permute-done | bytes 262176 | tf_op jit(solution)/shard_map/dispatch_gather/ppermute | solution.py:55
  197.1 1.8 fusion.2
  198.9 1.8 fusion.10
  201.6 1.4 collective-permute-start.27
  204.0 1.0 fusion.57
  205.9 1.6 collective-permute-start.37
  210.0 1.6 collective-permute-done.36
  212.7 1.7 collective-permute-start.39
  215.7 3.1 %collective-permute-done.38 = bf16[64,2048]{1,0:T(8,128)(2,1)S(1)} collective-permute-done((bf16[64,2048]{1,0:T(8,128)(2,1)S(1)}, bf16[64,2048]{1,0:T(8,128)(2,1)S(1)}, u32[]{:S(2)}, u32[]{:S(2)}) %collective-permute-start.38) | collective-permute-done | bytes 262176 | tf_op jit(solution)/shard_map/combine_return/ppermute | solution.py:75
  219.6 1.6 collective-permute-start.41
  221.3 4.3 %collective-permute-done.40 = bf16[64,2048]{1,0:T(8,128)(2,1)S(1)} collective-permute-done((bf16[64,2048]{1,0:T(8,128)(2,1)S(1)}, bf16[64,2048]{1,0:T(8,128)(2,1)S(1)}, u32[]{:S(2)}, u32[]{:S(2)}) %collective-permute-start.40) | collective-permute-done | bytes 262176 | tf_op jit(solution)/shard_map/combine_return/ppermute | solution.py:75
  226.4 1.2 multiply_convert_fusion
  (122 shorter events, 27.5 us)
Async XLA Ops:
  0.6 43.6 %copy-start = (bf16[512,2048]{1,0:T(8,128)(2,1)S(1)}, bf16[512,2048]{1,0:T(8,128)(2,1)}, u32[]{:S(2)}) copy-start(bf16[512,2048]{1,0:T(8,128)(2,1)} %param.14) | copy-start | bytes 6291460
  0.6 18.9 %copy-start.7 = (s32[8]{0:T(128)S(1)}, s32[8]{0:T(128)}, u32[]{:S(2)}) copy-start(s32[8]{0:T(128)} %constant.226.clone) | copy-start | bytes 100
  0.7 30.7 %copy-start.4 = (s32[8]{0:T(128)S(1)}, s32[8]{0:T(128)}, u32[]{:S(2)}) copy-start(s32[8]{0:T(128)} %constant.227.clone) | copy-start | bytes 100
  2.1 13.8 %all-to-all-start.1 = ((f32[8,128,2]{1,2,0:T(2,128)}), f32[8,128,2]{1,2,0:T(2,128)S(1)}, u32[]{:S(2)}, u32[]{:S(2)}) async-start(f32[8,128,2]{1,2,0:T(2,128)} %bitcast.2), calls=%async_computation.1 | async-start | bytes 16384 | tf_op jit(solution)/shard_map/route_weights/all_to_all | solution.py:118
  15.9 28.3 %all-to-all-start = ((bf16[8,128,512]{2,1,0:T(8,128)(2,1)}), bf16[8,128,512]{2,1,0:T(8,128)(2,1)S(1)}, u32[]{:S(2)}, u32[]{:S(2)}) async-start(bf16[8,128,512]{2,1,0:T(8,128)(2,1)} %bitcast.236), calls=%async_computation | async-start | bytes 2097152 | tf_op jit(solution)/shard_map/out_projection/all_to_all | solution.py:123
  46.6 3.3 %copy-start.2 = (f32[8,128,2048]{2,1,0:T(8,128)}, f32[8,128,2048]{2,1,0:T(8,128)S(1)}, u32[]{:S(2)}) copy-start(f32[8,128,2048]{2,1,0:T(8,128)S(1)} %fusion.111) | copy-start | bytes 25165828
  50.0 6.6 %collective-permute-start = (bf16[64,2048]{1,0:T(8,128)(2,1)S(1)}, bf16[64,2048]{1,0:T(8,128)(2,1)S(1)}, u32[]{:S(2)}, u32[]{:S(2)}) collective-permute-start(bf16[64,2048]{1,0:T(8,128)(2,1)S(1)} %get-tuple-element.75), channel_id=1, source_target_pairs={{0,8},{8,16},{16,24},{24,28},{28,20},{20,12},{12,4},{4,0},{1,9},{9... | collective-permute-start | bytes 786440 | tf_op jit(solution)/shard_map/out_projection/ppermute | solution.py:37
  50.0 6.6 %collective-permute-start.1 = (bf16[64,2048]{1,0:T(8,128)(2,1)S(1)}, bf16[64,2048]{1,0:T(8,128)(2,1)S(1)}, u32[]{:S(2)}, u32[]{:S(2)}) collective-permute-start(bf16[64,2048]{1,0:T(8,128)(2,1)S(1)} %get-tuple-element.76), channel_id=1, source_target_pairs={{0,4},{8,0},{16,8},{24,16},{28,24},{20,28},{12,20},{4,12},{1,5},{9... | collective-permute-start | bytes 786440 | tf_op jit(solution)/shard_map/out_projection/ppermute | solution.py:37
  57.9 6.4 %collective-permute-start.2 = (bf16[64,2048]{1,0:T(8,128)(2,1)S(1)}, bf16[64,2048]{1,0:T(8,128)(2,1)S(1)}, u32[]{:S(2)}, u32[]{:S(2)}) collective-permute-start(bf16[64,2048]{1,0:T(8,128)(2,1)S(1)} %get-tuple-element.79), channel_id=1, source_target_pairs={{0,8},{8,16},{16,24},{24,28},{28,20},{20,12},{12,4},{4,0},{1,9},{9... | collective-permute-start | bytes 786440 | tf_op jit(solution)/shard_map/out_projection/ppermute | solution.py:37
  58.5 7.9 %collective-permute-start.3 = (bf16[64,2048]{1,0:T(8,128)(2,1)S(1)}, bf16[64,2048]{1,0:T(8,128)(2,1)S(1)}, u32[]{:S(2)}, u32[]{:S(2)}) collective-permute-start(bf16[64,2048]{1,0:T(8,128)(2,1)S(1)} %get-tuple-element.80), channel_id=1, source_target_pairs={{0,4},{8,0},{16,8},{24,16},{28,24},{20,28},{12,20},{4,12},{1,5},{9... | collective-permute-start | bytes 786440 | tf_op jit(solution)/shard_map/out_projection/ppermute | solution.py:37
  67.8 6.4 %collective-permute-start.4 = (bf16[64,2048]{1,0:T(8,128)(2,1)S(1)}, bf16[64,2048]{1,0:T(8,128)(2,1)S(1)}, u32[]{:S(2)}, u32[]{:S(2)}) collective-permute-start(bf16[64,2048]{1,0:T(8,128)(2,1)S(1)} %get-tuple-element.83), channel_id=1, source_target_pairs={{0,8},{8,16},{16,24},{24,28},{28,20},{20,12},{12,4},{4,0},{1,9},{9... | collective-permute-start | bytes 786440 | tf_op jit(solution)/shard_map/out_projection/ppermute | solution.py:37
  69.6 6.4 %collective-permute-start.5 = (bf16[64,2048]{1,0:T(8,128)(2,1)S(1)}, bf16[64,2048]{1,0:T(8,128)(2,1)S(1)}, u32[]{:S(2)}, u32[]{:S(2)}) collective-permute-start(bf16[64,2048]{1,0:T(8,128)(2,1)S(1)} %get-tuple-element.84), channel_id=1, source_target_pairs={{0,4},{8,0},{16,8},{24,16},{28,24},{20,28},{12,20},{4,12},{1,5},{9... | collective-permute-start | bytes 786440 | tf_op jit(solution)/shard_map/out_projection/ppermute | solution.py:37
  77.3 6.4 %collective-permute-start.6 = (bf16[64,2048]{1,0:T(8,128)(2,1)S(1)}, bf16[64,2048]{1,0:T(8,128)(2,1)S(1)}, u32[]{:S(2)}, u32[]{:S(2)}) collective-permute-start(bf16[64,2048]{1,0:T(8,128)(2,1)S(1)} %get-tuple-element.87), channel_id=1, source_target_pairs={{0,8},{8,16},{16,24},{24,28},{28,20},{20,12},{12,4},{4,0},{1,9},{9... | collective-permute-start | bytes 786440 | tf_op jit(solution)/shard_map/out_projection/ppermute | solution.py:37
  79.1 6.6 %collective-permute-start.7 = (bf16[64,2048]{1,0:T(8,128)(2,1)S(1)}, bf16[64,2048]{1,0:T(8,128)(2,1)S(1)}, u32[]{:S(2)}, u32[]{:S(2)}) collective-permute-start(bf16[64,2048]{1,0:T(8,128)(2,1)S(1)} %get-tuple-element.88), channel_id=1, source_target_pairs={{0,4},{8,0},{16,8},{24,16},{28,24},{20,28},{12,20},{4,12},{1,5},{9... | collective-permute-start | bytes 786440 | tf_op jit(solution)/shard_map/out_projection/ppermute | solution.py:37
  86.9 7.7 %collective-permute-start.8 = (bf16[64,2048]{1,0:T(8,128)(2,1)S(1)}, bf16[64,2048]{1,0:T(8,128)(2,1)S(1)}, u32[]{:S(2)}, u32[]{:S(2)}) collective-permute-start(bf16[64,2048]{1,0:T(8,128)(2,1)S(1)} %get-tuple-element.91), channel_id=1, source_target_pairs={{0,8},{8,16},{16,24},{24,28},{28,20},{20,12},{12,4},{4,0},{1,9},{9... | collective-permute-start | bytes 786440 | tf_op jit(solution)/shard_map/out_projection/ppermute | solution.py:37
  87.5 7.8 %collective-permute-start.9 = (bf16[64,2048]{1,0:T(8,128)(2,1)S(1)}, bf16[64,2048]{1,0:T(8,128)(2,1)S(1)}, u32[]{:S(2)}, u32[]{:S(2)}) collective-permute-start(bf16[64,2048]{1,0:T(8,128)(2,1)S(1)} %get-tuple-element.92), channel_id=1, source_target_pairs={{0,4},{8,0},{16,8},{24,16},{28,24},{20,28},{12,20},{4,12},{1,5},{9... | collective-permute-start | bytes 786440 | tf_op jit(solution)/shard_map/out_projection/ppermute | solution.py:37
  96.5 8.8 %collective-permute-start.10 = (bf16[64,2048]{1,0:T(8,128)(2,1)S(1)}, bf16[64,2048]{1,0:T(8,128)(2,1)S(1)}, u32[]{:S(2)}, u32[]{:S(2)}) collective-permute-start(bf16[64,2048]{1,0:T(8,128)(2,1)S(1)} %get-tuple-element.95), channel_id=1, source_target_pairs={{0,8},{8,16},{16,24},{24,28},{28,20},{20,12},{12,4},{4,0},{1,9},{9... | collective-permute-start | bytes 786440 | tf_op jit(solution)/shard_map/out_projection/ppermute | solution.py:37
  97.1 8.9 %collective-permute-start.11 = (bf16[64,2048]{1,0:T(8,128)(2,1)S(1)}, bf16[64,2048]{1,0:T(8,128)(2,1)S(1)}, u32[]{:S(2)}, u32[]{:S(2)}) collective-permute-start(bf16[64,2048]{1,0:T(8,128)(2,1)S(1)} %get-tuple-element.96), channel_id=1, source_target_pairs={{0,4},{8,0},{16,8},{24,16},{28,24},{20,28},{12,20},{4,12},{1,5},{9... | collective-permute-start | bytes 786440 | tf_op jit(solution)/shard_map/out_projection/ppermute | solution.py:37
  104.4 13.9 %copy-start.3 = (bf16[128,2048]{1,0:T(8,128)(2,1)S(1)}, bf16[128,2048]{1,0:T(8,128)(2,1)}, u32[]{:S(2)}) copy-start(bf16[128,2048]{1,0:T(8,128)(2,1)} %param.12) | copy-start | bytes 1572868
  107.3 8.9 %collective-permute-start.12 = (bf16[64,2048]{1,0:T(8,128)(2,1)S(1)}, bf16[64,2048]{1,0:T(8,128)(2,1)S(1)}, u32[]{:S(2)}, u32[]{:S(2)}) collective-permute-start(bf16[64,2048]{1,0:T(8,128)(2,1)S(1)} %get-tuple-element.99), channel_id=1, source_target_pairs={{0,8},{8,16},{16,24},{24,28},{28,20},{20,12},{12,4},{4,0},{1,9},{9... | collective-permute-start | bytes 786440 | tf_op jit(solution)/shard_map/out_projection/ppermute | solution.py:37
  108.8 8.2 %collective-permute-start.13 = (bf16[64,2048]{1,0:T(8,128)(2,1)S(1)}, bf16[64,2048]{1,0:T(8,128)(2,1)S(1)}, u32[]{:S(2)}, u32[]{:S(2)}) collective-permute-start(bf16[64,2048]{1,0:T(8,128)(2,1)S(1)} %get-tuple-element.100), channel_id=1, source_target_pairs={{0,4},{8,0},{16,8},{24,16},{28,24},{20,28},{12,20},{4,12},{1,5},{9... | collective-permute-start | bytes 786440 | tf_op jit(solution)/shard_map/out_projection/ppermute | solution.py:37
  109.6 8.9 %copy-start.5 = (f32[2048]{0:T(1024)S(1)}, f32[2048]{0:T(1024)}, u32[]{:S(2)}) copy-start(f32[2048]{0:T(1024)} %param.15) | copy-start | bytes 24580
  118.8 6.4 %collective-permute-start.14 = (bf16[64,2048]{1,0:T(8,128)(2,1)S(1)}, bf16[64,2048]{1,0:T(8,128)(2,1)S(1)}, u32[]{:S(2)}, u32[]{:S(2)}) collective-permute-start(bf16[64,2048]{1,0:T(8,128)(2,1)S(1)} %get-tuple-element.185), channel_id=1, source_target_pairs={{0,8},{8,16},{16,24},{24,28},{28,20},{20,12},{12,4},{4,0},{1,9},{9... | collective-permute-start | bytes 786440 | tf_op jit(solution)/shard_map/dispatch_gather/ppermute | solution.py:55
  119.6 6.4 %collective-permute-start.15 = (bf16[64,2048]{1,0:T(8,128)(2,1)S(1)}, bf16[64,2048]{1,0:T(8,128)(2,1)S(1)}, u32[]{:S(2)}, u32[]{:S(2)}) collective-permute-start(bf16[64,2048]{1,0:T(8,128)(2,1)S(1)} %get-tuple-element.184), channel_id=1, source_target_pairs={{0,4},{8,0},{16,8},{24,16},{28,24},{20,28},{12,20},{4,12},{1,5},{9... | collective-permute-start | bytes 786440 | tf_op jit(solution)/shard_map/dispatch_gather/ppermute | solution.py:55
  126.0 6.4 %collective-permute-start.16 = (bf16[64,2048]{1,0:T(8,128)(2,1)S(1)}, bf16[64,2048]{1,0:T(8,128)(2,1)S(1)}, u32[]{:S(2)}, u32[]{:S(2)}) collective-permute-start(bf16[64,2048]{1,0:T(8,128)(2,1)S(1)} %collective-permute-done.14), channel_id=1, source_target_pairs={{0,8},{8,16},{16,24},{24,28},{28,20},{20,12},{12,4},{4,0},{1,9},{9... | collective-permute-start | bytes 786440 | tf_op jit(solution)/shard_map/dispatch_gather/ppermute | solution.py:55
  126.3 6.4 %collective-permute-start.17 = (bf16[64,2048]{1,0:T(8,128)(2,1)S(1)}, bf16[64,2048]{1,0:T(8,128)(2,1)S(1)}, u32[]{:S(2)}, u32[]{:S(2)}) collective-permute-start(bf16[64,2048]{1,0:T(8,128)(2,1)S(1)} %collective-permute-done.15), channel_id=1, source_target_pairs={{0,4},{8,0},{16,8},{24,16},{28,24},{20,28},{12,20},{4,12},{1,5},{9... | collective-permute-start | bytes 786440 | tf_op jit(solution)/shard_map/dispatch_gather/ppermute | solution.py:55
  132.7 11.6 %slice-start.3 = ((s8[6291456]{0:T(1024)(128)(4,1)}), s8[4194304]{0:T(1024)(128)(4,1)S(1)}, s32[]{:S(2)}) async-start(s8[6291456]{0:T(1024)(128)(4,1)} %bitcast.263), calls=%async_computation.5 | async-start | bytes 8388608
  137.5 6.8 %slice-start.4 = ((s8[6291456]{0:T(1024)(128)(4,1)}), s8[2097152]{0:T(1024)(128)(4,1)S(1)}, s32[]{:S(2)}) async-start(s8[6291456]{0:T(1024)(128)(4,1)} %bitcast.263), calls=%async_computation.6 | async-start | bytes 4194304
  142.2 14.3 %collective-permute-start.18 = (bf16[64,2048]{1,0:T(8,128)(2,1)S(1)}, bf16[64,2048]{1,0:T(8,128)(2,1)S(1)}, u32[]{:S(2)}, u32[]{:S(2)}) collective-permute-start(bf16[64,2048]{1,0:T(8,128)(2,1)S(1)} %collective-permute-done.16), channel_id=1, source_target_pairs={{0,8},{8,16},{16,24},{24,28},{28,20},{20,12},{12,4},{4,0},{1,9},{9... | collective-permute-start | bytes 786440 | tf_op jit(solution)/shard_map/dispatch_gather/ppermute | solution.py:55
  143.8 12.7 %collective-permute-start.19 = (bf16[64,2048]{1,0:T(8,128)(2,1)S(1)}, bf16[64,2048]{1,0:T(8,128)(2,1)S(1)}, u32[]{:S(2)}, u32[]{:S(2)}) collective-permute-start(bf16[64,2048]{1,0:T(8,128)(2,1)S(1)} %collective-permute-done.17), channel_id=1, source_target_pairs={{0,4},{8,0},{16,8},{24,16},{28,24},{20,28},{12,20},{4,12},{1,5},{9... | collective-permute-start | bytes 786440 | tf_op jit(solution)/shard_map/dispatch_gather/ppermute | solution.py:55
  144.3 22.3 %slice-start = ((s8[12582912]{0:T(1024)(128)(4,1)}), s8[4194304]{0:T(1024)(128)(4,1)S(1)}, s32[]{:S(2)}) async-start(s8[12582912]{0:T(1024)(128)(4,1)} %bitcast.261), calls=%async_computation.2 | async-start | bytes 8388608
  144.3 22.3 %slice-start.1 = ((s8[12582912]{0:T(1024)(128)(4,1)}), s8[4194304]{0:T(1024)(128)(4,1)S(1)}, s32[]{:S(2)}) async-start(s8[12582912]{0:T(1024)(128)(4,1)} %bitcast.261), calls=%async_computation.3 | async-start | bytes 8388608
  145.3 21.3 %slice-start.2 = ((s8[12582912]{0:T(1024)(128)(4,1)}), s8[4194304]{0:T(1024)(128)(4,1)S(1)}, s32[]{:S(2)}) async-start(s8[12582912]{0:T(1024)(128)(4,1)} %bitcast.261), calls=%async_computation.4 | async-start | bytes 8388608
  146.4 8.6 %collective-permute-start.28 = (bf16[64,2048]{1,0:T(8,128)(2,1)S(1)}, bf16[64,2048]{1,0:T(8,128)(2,1)S(1)}, u32[]{:S(2)}, u32[]{:S(2)}) collective-permute-start(bf16[64,2048]{1,0:T(8,128)(2,1)S(1)} %get-tuple-element.118), channel_id=1, source_target_pairs={{0,8},{8,16},{16,24},{24,28},{28,20},{20,12},{12,4},{4,0},{1,9},{9... | collective-permute-start | bytes 786440 | tf_op jit(solution)/shard_map/combine_return/ppermute | solution.py:75
  148.1 8.4 %collective-permute-start.29 = (bf16[64,2048]{1,0:T(8,128)(2,1)S(1)}, bf16[64,2048]{1,0:T(8,128)(2,1)S(1)}, u32[]{:S(2)}, u32[]{:S(2)}) collective-permute-start(bf16[64,2048]{1,0:T(8,128)(2,1)S(1)} %get-tuple-element.119), channel_id=1, source_target_pairs={{0,4},{8,0},{16,8},{24,16},{28,24},{20,28},{12,20},{4,12},{1,5},{9... | collective-permute-start | bytes 786440 | tf_op jit(solution)/shard_map/combine_return/ppermute | solution.py:75
  156.5 7.7 %collective-permute-start.20 = (bf16[64,2048]{1,0:T(8,128)(2,1)S(1)}, bf16[64,2048]{1,0:T(8,128)(2,1)S(1)}, u32[]{:S(2)}, u32[]{:S(2)}) collective-permute-start(bf16[64,2048]{1,0:T(8,128)(2,1)S(1)} %collective-permute-done.18), channel_id=1, source_target_pairs={{0,8},{8,16},{16,24},{24,28},{28,20},{20,12},{12,4},{4,0},{1,9},{9... | collective-permute-start | bytes 786440 | tf_op jit(solution)/shard_map/dispatch_gather/ppermute | solution.py:55
  157.9 8.4 %collective-permute-start.21 = (bf16[64,2048]{1,0:T(8,128)(2,1)S(1)}, bf16[64,2048]{1,0:T(8,128)(2,1)S(1)}, u32[]{:S(2)}, u32[]{:S(2)}) collective-permute-start(bf16[64,2048]{1,0:T(8,128)(2,1)S(1)} %collective-permute-done.19), channel_id=1, source_target_pairs={{0,4},{8,0},{16,8},{24,16},{28,24},{20,28},{12,20},{4,12},{1,5},{9... | collective-permute-start | bytes 786440 | tf_op jit(solution)/shard_map/dispatch_gather/ppermute | solution.py:55
  158.7 15.2 %collective-permute-start.30 = (bf16[64,2048]{1,0:T(8,128)(2,1)S(1)}, bf16[64,2048]{1,0:T(8,128)(2,1)S(1)}, u32[]{:S(2)}, u32[]{:S(2)}) collective-permute-start(bf16[64,2048]{1,0:T(8,128)(2,1)S(1)} %get-tuple-element.122), channel_id=1, source_target_pairs={{0,8},{8,16},{16,24},{24,28},{28,20},{20,12},{12,4},{4,0},{1,9},{9... | collective-permute-start | bytes 786440 | tf_op jit(solution)/shard_map/combine_return/ppermute | solution.py:75
  160.1 13.8 %collective-permute-start.31 = (bf16[64,2048]{1,0:T(8,128)(2,1)S(1)}, bf16[64,2048]{1,0:T(8,128)(2,1)S(1)}, u32[]{:S(2)}, u32[]{:S(2)}) collective-permute-start(bf16[64,2048]{1,0:T(8,128)(2,1)S(1)} %get-tuple-element.123), channel_id=1, source_target_pairs={{0,4},{8,0},{16,8},{24,16},{28,24},{20,28},{12,20},{4,12},{1,5},{9... | collective-permute-start | bytes 786440 | tf_op jit(solution)/shard_map/combine_return/ppermute | solution.py:75
  171.8 16.1 %collective-permute-start.22 = (bf16[64,2048]{1,0:T(8,128)(2,1)S(1)}, bf16[64,2048]{1,0:T(8,128)(2,1)S(1)}, u32[]{:S(2)}, u32[]{:S(2)}) collective-permute-start(bf16[64,2048]{1,0:T(8,128)(2,1)S(1)} %collective-permute-done.20), channel_id=1, source_target_pairs={{0,8},{8,16},{16,24},{24,28},{28,20},{20,12},{12,4},{4,0},{1,9},{9... | collective-permute-start | bytes 786440 | tf_op jit(solution)/shard_map/dispatch_gather/ppermute | solution.py:55
  173.6 14.4 %collective-permute-start.23 = (bf16[64,2048]{1,0:T(8,128)(2,1)S(1)}, bf16[64,2048]{1,0:T(8,128)(2,1)S(1)}, u32[]{:S(2)}, u32[]{:S(2)}) collective-permute-start(bf16[64,2048]{1,0:T(8,128)(2,1)S(1)} %collective-permute-done.21), channel_id=1, source_target_pairs={{0,4},{8,0},{16,8},{24,16},{28,24},{20,28},{12,20},{4,12},{1,5},{9... | collective-permute-start | bytes 786440 | tf_op jit(solution)/shard_map/dispatch_gather/ppermute | solution.py:55
  176.9 9.2 %collective-permute-start.32 = (bf16[64,2048]{1,0:T(8,128)(2,1)S(1)}, bf16[64,2048]{1,0:T(8,128)(2,1)S(1)}, u32[]{:S(2)}, u32[]{:S(2)}) collective-permute-start(bf16[64,2048]{1,0:T(8,128)(2,1)S(1)} %get-tuple-element.126), channel_id=1, source_target_pairs={{0,8},{8,16},{16,24},{24,28},{28,20},{20,12},{12,4},{4,0},{1,9},{9... | collective-permute-start | bytes 786440 | tf_op jit(solution)/shard_map/combine_return/ppermute | solution.py:75
  178.7 9.2 %collective-permute-start.33 = (bf16[64,2048]{1,0:T(8,128)(2,1)S(1)}, bf16[64,2048]{1,0:T(8,128)(2,1)S(1)}, u32[]{:S(2)}, u32[]{:S(2)}) collective-permute-start(bf16[64,2048]{1,0:T(8,128)(2,1)S(1)} %get-tuple-element.127), channel_id=1, source_target_pairs={{0,4},{8,0},{16,8},{24,16},{28,24},{20,28},{12,20},{4,12},{1,5},{9... | collective-permute-start | bytes 786440 | tf_op jit(solution)/shard_map/combine_return/ppermute | solution.py:75
  188.0 8.9 %collective-permute-start.24 = (bf16[64,2048]{1,0:T(8,128)(2,1)S(1)}, bf16[64,2048]{1,0:T(8,128)(2,1)S(1)}, u32[]{:S(2)}, u32[]{:S(2)}) collective-permute-start(bf16[64,2048]{1,0:T(8,128)(2,1)S(1)} %collective-permute-done.22), channel_id=1, source_target_pairs={{0,8},{8,16},{16,24},{24,28},{28,20},{20,12},{12,4},{4,0},{1,9},{9... | collective-permute-start | bytes 786440 | tf_op jit(solution)/shard_map/dispatch_gather/ppermute | solution.py:55
  188.1 8.9 %collective-permute-start.25 = (bf16[64,2048]{1,0:T(8,128)(2,1)S(1)}, bf16[64,2048]{1,0:T(8,128)(2,1)S(1)}, u32[]{:S(2)}, u32[]{:S(2)}) collective-permute-start(bf16[64,2048]{1,0:T(8,128)(2,1)S(1)} %collective-permute-done.23), channel_id=1, source_target_pairs={{0,4},{8,0},{16,8},{24,16},{28,24},{20,28},{12,20},{4,12},{1,5},{9... | collective-permute-start | bytes 786440 | tf_op jit(solution)/shard_map/dispatch_gather/ppermute | solution.py:55
  190.1 12.8 %collective-permute-start.34 = (bf16[64,2048]{1,0:T(8,128)(2,1)S(1)}, bf16[64,2048]{1,0:T(8,128)(2,1)S(1)}, u32[]{:S(2)}, u32[]{:S(2)}) collective-permute-start(bf16[64,2048]{1,0:T(8,128)(2,1)S(1)} %get-tuple-element.130), channel_id=1, source_target_pairs={{0,8},{8,16},{16,24},{24,28},{28,20},{20,12},{12,4},{4,0},{1,9},{9... | collective-permute-start | bytes 786440 | tf_op jit(solution)/shard_map/combine_return/ppermute | solution.py:75
  190.4 12.6 %collective-permute-start.35 = (bf16[64,2048]{1,0:T(8,128)(2,1)S(1)}, bf16[64,2048]{1,0:T(8,128)(2,1)S(1)}, u32[]{:S(2)}, u32[]{:S(2)}) collective-permute-start(bf16[64,2048]{1,0:T(8,128)(2,1)S(1)} %get-tuple-element.131), channel_id=1, source_target_pairs={{0,4},{8,0},{16,8},{24,16},{28,24},{20,28},{12,20},{4,12},{1,5},{9... | collective-permute-start | bytes 786440 | tf_op jit(solution)/shard_map/combine_return/ppermute | solution.py:75
  200.7 6.8 %collective-permute-start.26 = (bf16[64,2048]{1,0:T(8,128)(2,1)S(1)}, bf16[64,2048]{1,0:T(8,128)(2,1)S(1)}, u32[]{:S(2)}, u32[]{:S(2)}) collective-permute-start(bf16[64,2048]{1,0:T(8,128)(2,1)S(1)} %collective-permute-done.24), channel_id=1, source_target_pairs={{0,8},{8,16},{16,24},{24,28},{28,20},{20,12},{12,4},{4,0},{1,9},{9... | collective-permute-start | bytes 786440 | tf_op jit(solution)/shard_map/dispatch_gather/ppermute | solution.py:55
  201.6 6.4 %collective-permute-start.27 = (bf16[64,2048]{1,0:T(8,128)(2,1)S(1)}, bf16[64,2048]{1,0:T(8,128)(2,1)S(1)}, u32[]{:S(2)}, u32[]{:S(2)}) collective-permute-start(bf16[64,2048]{1,0:T(8,128)(2,1)S(1)} %collective-permute-done.25), channel_id=1, source_target_pairs={{0,4},{8,0},{16,8},{24,16},{28,24},{20,28},{12,20},{4,12},{1,5},{9... | collective-permute-start | bytes 786440 | tf_op jit(solution)/shard_map/dispatch_gather/ppermute | solution.py:55
  205.1 6.4 %collective-permute-start.36 = (bf16[64,2048]{1,0:T(8,128)(2,1)S(1)}, bf16[64,2048]{1,0:T(8,128)(2,1)S(1)}, u32[]{:S(2)}, u32[]{:S(2)}) collective-permute-start(bf16[64,2048]{1,0:T(8,128)(2,1)S(1)} %get-tuple-element.134), channel_id=1, source_target_pairs={{0,8},{8,16},{16,24},{24,28},{28,20},{20,12},{12,4},{4,0},{1,9},{9... | collective-permute-start | bytes 786440 | tf_op jit(solution)/shard_map/combine_return/ppermute | solution.py:75
  205.9 6.4 %collective-permute-start.37 = (bf16[64,2048]{1,0:T(8,128)(2,1)S(1)}, bf16[64,2048]{1,0:T(8,128)(2,1)S(1)}, u32[]{:S(2)}, u32[]{:S(2)}) collective-permute-start(bf16[64,2048]{1,0:T(8,128)(2,1)S(1)} %get-tuple-element.135), channel_id=1, source_target_pairs={{0,4},{8,0},{16,8},{24,16},{28,24},{20,28},{12,20},{4,12},{1,5},{9... | collective-permute-start | bytes 786440 | tf_op jit(solution)/shard_map/combine_return/ppermute | solution.py:75
  212.3 6.4 %collective-permute-start.38 = (bf16[64,2048]{1,0:T(8,128)(2,1)S(1)}, bf16[64,2048]{1,0:T(8,128)(2,1)S(1)}, u32[]{:S(2)}, u32[]{:S(2)}) collective-permute-start(bf16[64,2048]{1,0:T(8,128)(2,1)S(1)} %get-tuple-element.138), channel_id=1, source_target_pairs={{0,8},{8,16},{16,24},{24,28},{28,20},{20,12},{12,4},{4,0},{1,9},{9... | collective-permute-start | bytes 786440 | tf_op jit(solution)/shard_map/combine_return/ppermute | solution.py:75
  212.7 6.4 %collective-permute-start.39 = (bf16[64,2048]{1,0:T(8,128)(2,1)S(1)}, bf16[64,2048]{1,0:T(8,128)(2,1)S(1)}, u32[]{:S(2)}, u32[]{:S(2)}) collective-permute-start(bf16[64,2048]{1,0:T(8,128)(2,1)S(1)} %get-tuple-element.139), channel_id=1, source_target_pairs={{0,4},{8,0},{16,8},{24,16},{28,24},{20,28},{12,20},{4,12},{1,5},{9... | collective-permute-start | bytes 786440 | tf_op jit(solution)/shard_map/combine_return/ppermute | solution.py:75
  219.2 7.2 %copy-start.6 = (f32[2048]{0:T(1024)S(1)}, f32[2048]{0:T(1024)}, u32[]{:S(2)}) copy-start(f32[2048]{0:T(1024)} %param.20) | copy-start | bytes 24580
  219.2 6.4 %collective-permute-start.40 = (bf16[64,2048]{1,0:T(8,128)(2,1)S(1)}, bf16[64,2048]{1,0:T(8,128)(2,1)S(1)}, u32[]{:S(2)}, u32[]{:S(2)}) collective-permute-start(bf16[64,2048]{1,0:T(8,128)(2,1)S(1)} %get-tuple-element.142), channel_id=1, source_target_pairs={{0,8},{8,16},{16,24},{24,28},{28,20},{20,12},{12,4},{4,0},{1,9},{9... | collective-permute-start | bytes 786440 | tf_op jit(solution)/shard_map/combine_return/ppermute | solution.py:75
  219.6 6.4 %collective-permute-start.41 = (bf16[64,2048]{1,0:T(8,128)(2,1)S(1)}, bf16[64,2048]{1,0:T(8,128)(2,1)S(1)}, u32[]{:S(2)}, u32[]{:S(2)}) collective-permute-start(bf16[64,2048]{1,0:T(8,128)(2,1)S(1)} %get-tuple-element.143), channel_id=1, source_target_pairs={{0,4},{8,0},{16,8},{24,16},{28,24},{20,28},{12,20},{4,12},{1,5},{9... | collective-permute-start | bytes 786440 | tf_op jit(solution)/shard_map/combine_return/ppermute | solution.py:75
  226.0 1.7 copy-start.1
